TPU v7x, 32 devices: a whole 2x2x4 slice. The times are simulated.
32 devices in a mesh: pp: 2 (over y), ep: 16 (over z, x, core).
Axes of the slice: x: 2, y: 2, z: 4, core: 2. Of those that a mesh axis runs over, the one named last changes fastest.
Arguments:
- fwd_input: bfloat16 [2, 512, 7168], P('pp', 'ep'), may hold values from -6 to 6
- fwd_experts: int32 [2, 512, 2], P('pp', 'ep'), may hold values from 0 to 3, all different within a row; in each aligned block of 32 rows (0 to 31, 32 to 63, ..., all dimensions but the last counted through in order) at most 24 rows name the same one
- fwd_gates: float32 [2, 512, 2], P('pp', 'ep'), may hold values from 0.1 to 1
- bwd_input: bfloat16 [2, 512, 7168], P('pp', 'ep'), may hold values from -6 to 6
- bwd_grad: bfloat16 [2, 512, 7168], P('pp', 'ep'), may hold values from -6 to 6
- bwd_experts: int32 [2, 512, 2], P('pp', 'ep'), may hold values from 0 to 3, all different within a row; in each aligned block of 32 rows (0 to 31, 32 to 63, ..., all dimensions but the last counted through in order) at most 24 rows name the same one
- bwd_gates: float32 [2, 512, 2], P('pp', 'ep'), may hold values from 0.1 to 1
- gate_proj: bfloat16 [2, 7168, 4096], P('pp', None, 'ep'), may hold values from -0.0625 to 0.0625
- up_proj: bfloat16 [2, 7168, 4096], P('pp', None, 'ep'), may hold values from -0.0625 to 0.0625
- down_proj: bfloat16 [2, 4096, 7168], P('pp', 'ep'), may hold values from -0.1875 to 0.1875
Outputs:
- next_section_input: bfloat16 [2, 512, 7168], P('pp', 'ep')
- prev_section_grad: bfloat16 [2, 512, 7168], P('pp', 'ep')
Inputs may be any that keep to these rules, and one draw needn't show every extreme that they name: `fwd_experts`: each token names 2 different experts; in each device's aligned block of 32 tokens no expert is named more than 24 times, a bound that some block reaches. `bwd_experts`: each token names 2 different experts; in each device's aligned block of 32 tokens no expert is named more than 24 times, a bound that some block reaches.
All inputs are finite; a program needn't handle non-finite values.
Results may differ from a plain program's by a relative error of at most 0.0075.
Values may be sent and summed in bfloat16 or wider, within the bound.
No kernel may reach another device: no remote copies, remote signals or barrier semaphores. Data moves between devices by JAX's collectives and lax.ppermute only.
A program may use at most 128 MiB of HBM per device.

v0:
```python
import jax
import jax.numpy as jnp
from jax import lax
from jax.sharding import PartitionSpec as P

GROUP = 4
TOPK = 2


def from_partner(block, axis, apart):
    count = lax.axis_size(axis)
    route = []
    for low in range(count):
        high = low | 1 << apart
        if high != low and high < count:
            route += [(low, high), (high, low)]
    return lax.ppermute(block, axis, route)


def passed_along(value, axis, steps):
    count = lax.axis_size(axis)
    pairs = [(source, (source + steps) % count) for source in range(count)]
    return lax.ppermute(value, axis, pairs)


def routing(ids, gates, experts, capacity):
    pairs = ids.reshape(-1)
    hot = (pairs[:, None] == jnp.arange(experts, dtype=jnp.int32)[None, :]).astype(jnp.int32)
    before = jnp.cumsum(hot, axis=0) - hot
    slot = jnp.sum(hot * before, axis=1)
    target = (pairs * capacity + slot).reshape(ids.shape)
    columns = jnp.arange(experts * capacity, dtype=jnp.int32)
    match = (target[:, :, None] == columns[None, None, :]).astype(jnp.float32)
    select = jnp.sum(match, axis=1).astype(jnp.bfloat16)
    weights = jnp.sum(gates[:, :, None] * match, axis=1)
    return (select, weights)


def into_slots(select, rows_in):
    placed = lax.dot_general(
        select, rows_in, (((0,), (0,)), ((), ())), preferred_element_type=jnp.float32
    )
    return placed.astype(jnp.bfloat16)


def make_forward(w_gate, w_up, w_down):

    def forward_rows(received):
        lead, count, width = received.shape
        rows_in = received.reshape(lead * count, width)
        g = jnp.dot(rows_in, w_gate, preferred_element_type=jnp.float32)
        u = jnp.dot(rows_in, w_up, preferred_element_type=jnp.float32)
        hidden = (g * jax.nn.sigmoid(g) * u).astype(jnp.bfloat16)
        part = jnp.dot(hidden, w_down, preferred_element_type=jnp.float32).astype(jnp.bfloat16)
        return part.reshape(lead, count, w_down.shape[1])

    return forward_rows


def make_backward(w_gate, w_up, w_down):
    width = w_gate.shape[0]

    def backward_rows(received):
        lead, count, _ = received.shape
        rows_all = received.reshape(lead * count, 2 * width)
        rows_in = rows_all[:, :width]
        rows_grad = rows_all[:, width:]
        g = jnp.dot(rows_in, w_gate, preferred_element_type=jnp.float32)
        u = jnp.dot(rows_in, w_up, preferred_element_type=jnp.float32)
        dh = lax.dot_general(
            rows_grad, w_down, (((1,), (1,)), ((), ())), preferred_element_type=jnp.float32
        )
        sig = jax.nn.sigmoid(g)
        grad_gate = (dh * u * sig * (1.0 + g * (1.0 - sig))).astype(jnp.bfloat16)
        grad_up = (dh * g * sig).astype(jnp.bfloat16)
        part = lax.dot_general(
            grad_gate, w_gate, (((1,), (1,)), ((), ())), preferred_element_type=jnp.float32
        )
        part = part + lax.dot_general(
            grad_up, w_up, (((1,), (1,)), ((), ())), preferred_element_type=jnp.float32
        )
        return part.astype(jnp.bfloat16).reshape(lead, count, width)

    return backward_rows


def fill_group(shares, backward):
    index = lax.axis_index("ep")
    gathered = shares[:, None]
    for bit in range(GROUP.bit_length() - 1):
        if backward:
            other = from_partner(gathered, "ep", bit)
        else:
            other = from_partner(gathered, "ep", bit)
        upper = index >> bit & 1 == 1
        gathered = jnp.where(
            upper,
            jnp.concatenate([other, gathered], axis=1),
            jnp.concatenate([gathered, other], axis=1),
        )
    lead = gathered.shape[0]
    return gathered.reshape(lead, -1, gathered.shape[3])


def body(
    fwd_input,
    fwd_experts,
    fwd_gates,
    bwd_input,
    bwd_grad,
    bwd_experts,
    bwd_gates,
    gate_proj,
    up_proj,
    down_proj,
):
    devices = lax.axis_size("ep")
    experts = devices // GROUP
    tokens = fwd_input.shape[1]
    width = fwd_input.shape[2]
    capacity = min(tokens, 3 * tokens * TOPK // (2 * experts))
    w_gate = gate_proj[0]
    w_up = up_proj[0]
    w_down = down_proj[0]
    forward_rows = make_forward(w_gate, w_up, w_down)
    backward_rows = make_backward(w_gate, w_up, w_down)
    f_select, f_weights = routing(fwd_experts[0], fwd_gates[0], experts, capacity)
    b_select, b_weights = routing(bwd_experts[0], bwd_gates[0], experts, capacity)
    f_slots = into_slots(f_select, fwd_input[0]).reshape(experts, capacity, width)
    b_joined = jnp.concatenate([bwd_input[0], bwd_grad[0]], axis=1)
    b_slots = into_slots(b_select, b_joined).reshape(experts, capacity, 2 * width)
    f_shares = lax.all_to_all(
        f_slots.reshape(devices, capacity // GROUP, width),
        "ep",
        split_axis=0,
        concat_axis=0,
        tiled=True,
    )
    f_partial = forward_rows(fill_group(f_shares, False))
    b_shares = lax.all_to_all(
        b_slots.reshape(devices, capacity // GROUP, 2 * width),
        "ep",
        split_axis=0,
        concat_axis=0,
        tiled=True,
    )
    b_partial = backward_rows(fill_group(b_shares, True))
    f_back = lax.all_to_all(f_partial, "ep", split_axis=0, concat_axis=0, tiled=True)
    f_out = jnp.sum(
        f_back.reshape(experts, GROUP, capacity, width).astype(jnp.float32), axis=1
    ).astype(jnp.bfloat16)
    b_back = lax.all_to_all(b_partial, "ep", split_axis=0, concat_axis=0, tiled=True)
    b_out = jnp.sum(
        b_back.reshape(experts, GROUP, capacity, width).astype(jnp.float32), axis=1
    ).astype(jnp.bfloat16)
    high = lax.Precision.HIGHEST
    f_mixed = jnp.dot(
        f_weights, f_out.reshape(experts * capacity, width).astype(jnp.float32), precision=high
    )
    f_result = (fwd_input[0].astype(jnp.float32) + f_mixed).astype(jnp.bfloat16)
    b_mixed = jnp.dot(
        b_weights, b_out.reshape(experts * capacity, width).astype(jnp.float32), precision=high
    )
    b_result = (bwd_grad[0].astype(jnp.float32) + b_mixed).astype(jnp.bfloat16)
    next_section_input = passed_along(f_result[None], "pp", 1)
    prev_section_grad = passed_along(b_result[None], "pp", -1)
    return (next_section_input, prev_section_grad)


def solution(mesh):
    in_specs = (
        P("pp", "ep", None),
        P("pp", "ep", None),
        P("pp", "ep", None),
        P("pp", "ep", None),
        P("pp", "ep", None),
        P("pp", "ep", None),
        P("pp", "ep", None),
        P("pp", None, "ep"),
        P("pp", None, "ep"),
        P("pp", "ep", None),
    )
    out_specs = (P("pp", "ep", None), P("pp", "ep", None))
    return jax.shard_map(body, mesh=mesh, in_specs=in_specs, out_specs=out_specs, check_vma=False)
```

profile of v0, /device:TPU:16, one launch (start us, length us, event | category | flops | bytes accessed | tf_op | source)
XLA Modules:
  0.0 561.8 jit_solution(15178722693794301228)
XLA Ops:
  0.6 0.8 copy.52
  1.4 0.1 eq.64
  1.7 0.2 select_reduce_fusion.3
  1.9 0.1 reduce_sum.83
  2.0 0.7 bitcast_add_fusion.1
  2.7 0.8 convert_reduce_fusion.1
  3.5 1.6 convolution_convert_fusion.2
  5.1 1.5 reshape_reshape.8
  6.6 6.2 %all-to-all-start = ((bf16[16,6,7168]{2,1,0:T(8,128)(2,1)}), bf16[16,6,7168]{2,1,0:T(8,128)(2,1)S(1)}, u32[]{:S(2)}, u32[]{:S(2)}) async-start(bf16[16,6,7168]{2,1,0:T(8,128)(2,1)} %reshape_reshape.8), calls=%async_computation | async-start | bytes 3670016 | tf_op jit(solution)/shard_map/all_to_all | solution.py:132
  12.9 0.1 eq.73
  13.1 0.1 reduce_window_sum.18
  13.2 0.2 select_reduce_fusion.1
  13.4 0.1 reduce_sum.88
  13.7 2.5 convolution_convert_fusion
  16.1 4.6 reshape_reshape.9
  20.8 34.1 %all-to-all-done = bf16[16,6,7168]{2,1,0:T(8,128)(2,1)S(1)} async-done(((bf16[16,6,7168]{2,1,0:T(8,128)(2,1)}), bf16[16,6,7168]{2,1,0:T(8,128)(2,1)S(1)}, u32[]{:S(2)}, u32[]{:S(2)}) %all-to-all-start) | async-done | bytes 1376288 | tf_op jit(solution)/shard_map/all_to_all | solution.py:132
  54.8 5.3 all-to-all-start.2
  60.2 1.9 copy.54
  62.0 0.1 collective-permute-start
  62.2 3.2 collective-permute-done
  65.4 0.8 copy.55
  66.2 1.0 maximum_select_fusion.3
  67.2 1.8 copy-done.1
  69.0 3.1 copy.57
  72.1 1.5 collective-permute-start.1
  73.5 68.1 %all-to-all-done.2 = bf16[16,6,14336]{2,1,0:T(8,128)(2,1)} async-done(((bf16[16,6,14336]{2,1,0:T(8,128)(2,1)}), bf16[16,6,14336]{2,1,0:T(8,128)(2,1)}, u32[]{:S(2)}, u32[]{:S(2)}) %all-to-all-start.2) | async-done | bytes 2752544 | tf_op jit(solution)/shard_map/all_to_all | solution.py:140
  141.7 5.1 copy.63
  146.8 14.4 %collective-permute-done.1 = bf16[16,2,6,7168]{3,0,2,1:T(8,128)(2,1)} collective-permute-done((bf16[16,2,6,7168]{3,0,2,1:T(8,128)(2,1)}, bf16[16,2,6,7168]{3,0,2,1:T(8,128)(2,1)}, u32[]{:S(2)}, u32[]{:S(2)}) %collective-permute-start.1) | collective-permute-done | bytes 2752544 | tf_op jit(solution)/shard_map/ppermute | solution.py:17
  161.2 3.3 copy.58
  164.5 3.2 maximum_select_fusion.1
  167.6 3.6 copy.60
  171.2 8.6 %select_n.54 = bf16[384,7168]{1,0:T(8,128)(2,1)} reshape(bf16[16,4,6,7168]{3,2,1,0:T(8,128)(2,1)} %copy.60) | data formatting | bytes 11010048 | tf_op jit(solution)/shard_map/jit(_where)/select_n | solution.py:96
  179.8 5.3 fusion.19
  185.1 1.5 copy.64
  186.6 5.8 %maximum_select_fusion.2 = bf16[16,2,6,14336]{3,2,0,1:T(8,128)(2,1)S(1)} fusion(bf16[16,1,6,14336]{3,2,0,1:T(8,128)(2,1)} %bitcast.15, bf16[16,1,6,14336]{3,2,0,1:T(8,128)(2,1)S(1)} %copy.64, pred[]{:T(512)S(6)} %eq.72), kind=kLoop, calls=%fused_computation.12 | loop fusion | flops 8257536 | bytes 11010049 | tf_op jit(solution)/shard_map/jit(_where)/select_n | solution.py:96
  192.5 5.4 copy.66
  197.9 0.2 copy-done
  198.1 0.6 collective-permute-start.4
  198.7 1.6 fusion.44
  200.3 4.0 convolution_convert_fusion.1
  204.2 6.6 %all-to-all-start.1 = ((bf16[16,24,7168]{2,1,0:T(8,128)(2,1)}), bf16[16,24,7168]{2,1,0:T(8,128)(2,1)}, u32[]{:S(2)}, u32[]{:S(2)}) async-start(bf16[16,24,7168]{2,1,0:T(8,128)(2,1)} %bitcast.71), calls=%async_computation.1 | async-start | bytes 11010048 | tf_op jit(solution)/shard_map/all_to_all | solution.py:148
  210.9 153.3 %collective-permute-done.4 = bf16[16,2,6,14336]{3,0,2,1:T(8,128)(2,1)} collective-permute-done((bf16[16,2,6,14336]{3,0,2,1:T(8,128)(2,1)}, bf16[16,2,6,14336]{3,0,2,1:T(8,128)(2,1)}, u32[]{:S(2)}, u32[]{:S(2)}) %collective-permute-start.4) | collective-permute-done | bytes 5505056 | tf_op jit(solution)/shard_map/ppermute | solution.py:17
  364.2 5.6 %copy.67 = bf16[16,2,6,14336]{3,2,0,1:T(8,128)(2,1)S(1)} copy(bf16[16,2,6,14336]{3,0,2,1:T(8,128)(2,1)} %collective-permute-done.4) | data formatting | bytes 11010048 | tf_op jit(solution)/shard_map/ppermute | solution.py:17
  369.9 6.3 %maximum_select_fusion = bf16[16,4,6,14336]{3,2,0,1:T(8,128)(2,1)S(1)} fusion(bf16[16,2,6,14336]{3,2,0,1:T(8,128)(2,1)S(1)} %bitcast.69, bf16[16,2,6,14336]{3,2,0,1:T(8,128)(2,1)S(1)} %copy.67, pred[]{:T(512)S(6)} %eq.71), kind=kLoop, calls=%fused_computation.1 | loop fusion | flops 16515072 | bytes 22020096 | tf_op jit(solution)/shard_map/jit(_where)/select_n | solution.py:96
  376.1 6.6 %copy.69 = bf16[16,4,6,14336]{3,2,1,0:T(8,128)(2,1)} copy(bf16[16,4,6,14336]{3,2,0,1:T(8,128)(2,1)S(1)} %maximum_select_fusion) | data formatting | bytes 22020096 | tf_op jit(solution)/shard_map/jit(_where)/select_n | solution.py:96
  382.7 16.5 %select_n.59 = bf16[384,14336]{1,0:T(8,128)(2,1)} reshape(bf16[16,4,6,14336]{3,2,1,0:T(8,128)(2,1)} %copy.69) | data formatting | bytes 22020096 | tf_op jit(solution)/shard_map/jit(_where)/select_n | solution.py:96
  399.3 5.4 fusion.4
  404.7 1.4 copy-done.3
  406.0 3.8 fusion.6
  409.9 1.6 fusion.39
  411.5 0.4 copy-done.4
  411.9 1.6 fusion.16
  413.5 4.1 add_convert_fusion
  417.6 5.2 all-to-all-start.3
  422.8 3.6 bitcast_reduce_fusion.1
  426.4 0.7 fusion.3
  427.1 1.6 collective-permute-start.2
  428.7 114.9 %all-to-all-done.3 = bf16[16,24,7168]{2,1,0:T(8,128)(2,1)} async-done(((bf16[16,24,7168]{2,1,0:T(8,128)(2,1)}), bf16[16,24,7168]{2,1,0:T(8,128)(2,1)}, u32[]{:S(2)}, u32[]{:S(2)}) %all-to-all-start.3) | async-done | bytes 5505056 | tf_op jit(solution)/shard_map/all_to_all | solution.py:152
  543.6 3.5 bitcast_reduce_fusion
  547.2 0.7 fusion.2
  547.8 1.6 collective-permute-start.5
  549.4 10.5 %collective-permute-done.5 = bf16[1,32,7168]{2,1,0:T(8,128)(2,1)S(1)} collective-permute-done((bf16[1,32,7168]{2,1,0:T(8,128)(2,1)S(1)}, bf16[1,32,7168]{2,1,0:T(8,128)(2,1)S(1)}, u32[]{:S(2)}, u32[]{:S(2)}) %collective-permute-start.5) | collective-permute-done | bytes 458784 | tf_op jit(solution)/shard_map/ppermute | solution.py:23
  560.0 0.8 copy.72
  560.7 0.8 copy.73
  (46 shorter events, 0.7 us)
Async XLA Ops:
  5.1 7.7 %copy-start.12 = (s32[1,32,2]{1,2,0:T(2,128)S(1)}, s32[1,32,2]{1,2,0:T(2,128)}, u32[]{:S(2)}) copy-start(s32[1,32,2]{1,2,0:T(2,128)} %param.15) | copy-start | bytes 772
  5.1 8.5 %copy-start.13 = (f32[1,32,2]{1,2,0:T(2,128)S(1)}, f32[1,32,2]{1,2,0:T(2,128)}, u32[]{:S(2)}) copy-start(f32[1,32,2]{1,2,0:T(2,128)} %param.16) | copy-start | bytes 772
  5.1 8.6 %copy-start.9 = (bf16[1,32,7168]{2,1,0:T(8,128)(2,1)S(1)}, bf16[1,32,7168]{2,1,0:T(8,128)(2,1)}, u32[]{:S(2)}) copy-start(bf16[1,32,7168]{2,1,0:T(8,128)(2,1)} %param.14) | copy-start | bytes 1376260
  5.1 8.6 %copy-start.11 = (bf16[1,32,7168]{2,1,0:T(8,128)(2,1)S(1)}, bf16[1,32,7168]{2,1,0:T(8,128)(2,1)}, u32[]{:S(2)}) copy-start(bf16[1,32,7168]{2,1,0:T(8,128)(2,1)} %param.13) | copy-start | bytes 1376260
  6.6 48.2 %all-to-all-start = ((bf16[16,6,7168]{2,1,0:T(8,128)(2,1)}), bf16[16,6,7168]{2,1,0:T(8,128)(2,1)S(1)}, u32[]{:S(2)}, u32[]{:S(2)}) async-start(bf16[16,6,7168]{2,1,0:T(8,128)(2,1)} %reshape_reshape.8), calls=%async_computation | async-start | bytes 3670016 | tf_op jit(solution)/shard_map/all_to_all | solution.py:132
  54.8 86.8 %all-to-all-start.2 = ((bf16[16,6,14336]{2,1,0:T(8,128)(2,1)}), bf16[16,6,14336]{2,1,0:T(8,128)(2,1)}, u32[]{:S(2)}, u32[]{:S(2)}) async-start(bf16[16,6,14336]{2,1,0:T(8,128)(2,1)} %reshape_reshape.9), calls=%async_computation.2 | async-start | bytes 7340032 | tf_op jit(solution)/shard_map/all_to_all | solution.py:140
  62.0 3.3 collective-permute-start
  67.1 1.8 copy-start.1
  72.1 89.1 %collective-permute-start.1 = (bf16[16,2,6,7168]{3,0,2,1:T(8,128)(2,1)}, bf16[16,2,6,7168]{3,0,2,1:T(8,128)(2,1)}, u32[]{:S(2)}, u32[]{:S(2)}) collective-permute-start(bf16[16,2,6,7168]{3,0,2,1:T(8,128)(2,1)} %copy.57), channel_id=1, source_target_pairs={{0,2},{2,0},{1,3},{3,1},{4,6},{6,4},{5,7},{7,5},{8,10},{10,8},{9,1... | collective-permute-start | bytes 8257544 | tf_op jit(solution)/shard_map/ppermute | solution.py:17
  146.8 38.3 %collective-permute-start.3 = (bf16[16,1,6,14336]{3,0,2,1:T(8,128)(2,1)}, bf16[16,1,6,14336]{3,0,2,1:T(8,128)(2,1)S(1)}, u32[]{:S(2)}, u32[]{:S(2)}) collective-permute-start(bf16[16,1,6,14336]{3,0,2,1:T(8,128)(2,1)} %copy.63), channel_id=1, source_target_pairs={{0,1},{1,0},{2,3},{3,2},{4,5},{5,4},{6,7},{7,6},{8,9},{9,8},{10,11... | collective-permute-start | bytes 8257544 | tf_op jit(solution)/shard_map/ppermute | solution.py:17
  146.8 17.7 %copy-start.2 = (bf16[16,2,6,7168]{3,2,0,1:T(8,128)(2,1)S(1)}, bf16[16,2,6,7168]{3,2,0,1:T(8,128)(2,1)}, u32[]{:S(2)}) copy-start(bf16[16,2,6,7168]{3,2,0,1:T(8,128)(2,1)} %copy-done.1) | copy-start | bytes 8257540
  185.1 13.6 %slice-start.2 = ((s8[5505024]{0:T(1024)(128)(4,1)}), s8[4194304]{0:T(1024)(128)(4,1)S(1)}, s32[]{:S(2)}) async-start(s8[5505024]{0:T(1024)(128)(4,1)} %bitcast.74), calls=%async_computation.6 | async-start | bytes 8388608
  186.6 12.0 %slice-start.3 = ((s8[5505024]{0:T(1024)(128)(4,1)}), s8[1310720]{0:T(1024)(128)(4,1)S(1)}, s32[]{:S(2)}) async-start(s8[5505024]{0:T(1024)(128)(4,1)} %bitcast.74), calls=%async_computation.7 | async-start | bytes 2621440
  192.5 5.6 copy-start
  192.5 6.2 %copy-start.5 = (bf16[1,7168,256]{2,1,0:T(8,128)(2,1)S(1)}, bf16[1,7168,256]{2,1,0:T(8,128)(2,1)}, u32[]{:S(2)}) copy-start(bf16[1,7168,256]{2,1,0:T(8,128)(2,1)} %param.18) | copy-start | bytes 11010052
  198.1 2.2 copy-start.7
  198.1 166.1 %collective-permute-start.4 = (bf16[16,2,6,14336]{3,0,2,1:T(8,128)(2,1)}, bf16[16,2,6,14336]{3,0,2,1:T(8,128)(2,1)}, u32[]{:S(2)}, u32[]{:S(2)}) collective-permute-start(bf16[16,2,6,14336]{3,0,2,1:T(8,128)(2,1)} %copy.66), channel_id=1, source_target_pairs={{0,2},{2,0},{1,3},{3,1},{4,6},{6,4},{5,7},{7,5},{8,10},{10,8},{9,1... | collective-permute-start | bytes 16515080 | tf_op jit(solution)/shard_map/ppermute | solution.py:17
  204.2 165.6 %slice-start = ((s8[7340032]{0:T(1024)(128)(4,1)}), s8[3145728]{0:T(1024)(128)(4,1)S(1)}, s32[]{:S(2)}) async-start(s8[7340032]{0:T(1024)(128)(4,1)} %bitcast.68), calls=%async_computation.4 | async-start | bytes 6291456
  204.2 213.4 %all-to-all-start.1 = ((bf16[16,24,7168]{2,1,0:T(8,128)(2,1)}), bf16[16,24,7168]{2,1,0:T(8,128)(2,1)}, u32[]{:S(2)}, u32[]{:S(2)}) async-start(bf16[16,24,7168]{2,1,0:T(8,128)(2,1)} %bitcast.71), calls=%async_computation.1 | async-start | bytes 11010048 | tf_op jit(solution)/shard_map/all_to_all | solution.py:148
  210.9 159.0 %slice-start.1 = ((s8[7340032]{0:T(1024)(128)(4,1)}), s8[4194304]{0:T(1024)(128)(4,1)S(1)}, s32[]{:S(2)}) async-start(s8[7340032]{0:T(1024)(128)(4,1)} %bitcast.68), calls=%async_computation.5 | async-start | bytes 8388608
  399.3 6.8 %copy-start.3 = (bf16[384,14336]{1,0:T(8,128)(2,1)S(1)}, bf16[384,14336]{1,0:T(8,128)(2,1)}, u32[]{:S(2)}) copy-start(bf16[384,14336]{1,0:T(8,128)(2,1)} %select_n.59) | copy-start | bytes 33030148
  406.0 3.8 copy-start.6
  409.9 2.0 copy-start.4
  417.6 126.0 %all-to-all-start.3 = ((bf16[16,24,7168]{2,1,0:T(8,128)(2,1)}), bf16[16,24,7168]{2,1,0:T(8,128)(2,1)}, u32[]{:S(2)}, u32[]{:S(2)}) async-start(bf16[16,24,7168]{2,1,0:T(8,128)(2,1)} %bitcast.70), calls=%async_computation.3 | async-start | bytes 11010048 | tf_op jit(solution)/shard_map/all_to_all | solution.py:152
  422.8 3.6 copy-start.8
  427.1 120.0 %copy-start.10 = (bf16[1,32,7168]{2,1,0:T(8,128)(2,1)S(1)}, bf16[1,32,7168]{2,1,0:T(8,128)(2,1)}, u32[]{:S(2)}) copy-start(bf16[1,32,7168]{2,1,0:T(8,128)(2,1)} %param.14) | copy-start | bytes 1376260
  427.1 122.3 %collective-permute-start.2 = (bf16[1,32,7168]{2,1,0:T(8,128)(2,1)S(1)}, bf16[1,32,7168]{2,1,0:T(8,128)(2,1)S(1)}, u32[]{:S(2)}, u32[]{:S(2)}) collective-permute-start(bf16[1,32,7168]{2,1,0:T(8,128)(2,1)S(1)} %fusion.3), channel_id=1, source_target_pairs={{0,16},{16,0},{1,17},{17,1},{2,18},{18,2},{3,19},{19,3},{4,20},{20... | collective-permute-start | bytes 1376264 | tf_op jit(solution)/shard_map/ppermute | solution.py:23
  547.8 12.1 %collective-permute-start.5 = (bf16[1,32,7168]{2,1,0:T(8,128)(2,1)S(1)}, bf16[1,32,7168]{2,1,0:T(8,128)(2,1)S(1)}, u32[]{:S(2)}, u32[]{:S(2)}) collective-permute-start(bf16[1,32,7168]{2,1,0:T(8,128)(2,1)S(1)} %fusion.2), channel_id=1, source_target_pairs={{0,16},{16,0},{1,17},{17,1},{2,18},{18,2},{3,19},{19,3},{4,20},{20... | collective-permute-start | bytes 1376264 | tf_op jit(solution)/shard_map/ppermute | solution.py:23
where the time goes:
time: 566 us; the launch traced here: 562 us
  waiting for transfers between devices  399 us (70%)
  local copies, waits for them, and re-layouts  74.9 us (13%)
  matrix products  32.7 us (6%)
  starting transfers between devices  28.7 us (5%)
  other arithmetic  25.6 us (5%)
    ppermute x4, waiting for transfers between devices, from_partner(): return lax.ppermute(block, axis, route)  171 us
    all_to_all x1, waiting for transfers between devices, body(): lax.all_to_all(b_partial, 'ep', split_axis=0, concat_axis=0, tiled=True)  115 us
    all_to_all x1, waiting for transfers between devices, body(): lax.all_to_all(b_slots.reshape(devices, capacity // GROUP, 2 * width), 'e...  68.1 us
    select_n x6, local copies, waits for them, and re-layouts, fill_group(): jnp.where(upper, jnp.concatenate([other, gathered], axis=1), jnp.concaten...  43.7 us
    all_to_all x1, waiting for transfers between devices, body(): lax.all_to_all(f_slots.reshape(devices, capacity // GROUP, width), 'ep',...  34.1 us
    select_n x4, other arithmetic, fill_group(): jnp.where(upper, jnp.concatenate([other, gathered], axis=1), jnp.concaten...  16.3 us
  transfers between devices with their start and end apart: 10, of which 7 were waited for; matrix products, arithmetic and copies ran while one was open for 19% of the time, Pallas kernels for 0%

commit v1 on v0

v1 whole, which is shorter than its diff:
```python
import jax
import jax.numpy as jnp
from jax import lax
from jax.sharding import Mesh
from jax.sharding import PartitionSpec as P

GROUP = 4
TOPK = 2
EP = ("z", "x", "c")


def swap(value, axis):
    return lax.ppermute(value, axis, [(0, 1), (1, 0)])


def passed_along(value, axis, steps):
    count = lax.axis_size(axis)
    pairs = [(source, (source + steps) % count) for source in range(count)]
    return lax.ppermute(value, axis, pairs)


def routing(ids, gates, experts, capacity):
    pairs = ids.reshape(-1)
    hot = (pairs[:, None] == jnp.arange(experts, dtype=jnp.int32)[None, :]).astype(jnp.int32)
    before = jnp.cumsum(hot, axis=0) - hot
    slot = jnp.sum(hot * before, axis=1)
    target = (pairs * capacity + slot).reshape(ids.shape)
    columns = jnp.arange(experts * capacity, dtype=jnp.int32)
    match = (target[:, :, None] == columns[None, None, :]).astype(jnp.float32)
    select = jnp.sum(match, axis=1).astype(jnp.bfloat16)
    weights = jnp.sum(gates[:, :, None] * match, axis=1)
    return (select, weights)


def into_slots(select, rows_in):
    placed = lax.dot_general(
        select, rows_in, (((0,), (0,)), ((), ())), preferred_element_type=jnp.float32
    )
    return placed.astype(jnp.bfloat16)


def forward_rows(rows_in, w_gate, w_up, w_down):
    g = jnp.dot(rows_in, w_gate, preferred_element_type=jnp.float32)
    u = jnp.dot(rows_in, w_up, preferred_element_type=jnp.float32)
    hidden = (g * jax.nn.sigmoid(g) * u).astype(jnp.bfloat16)
    return jnp.dot(hidden, w_down, preferred_element_type=jnp.float32).astype(jnp.bfloat16)


def backward_rows(rows_all, w_gate, w_up, w_down):
    width = w_gate.shape[0]
    rows_in = rows_all[:, :width]
    rows_grad = rows_all[:, width:]
    g = jnp.dot(rows_in, w_gate, preferred_element_type=jnp.float32)
    u = jnp.dot(rows_in, w_up, preferred_element_type=jnp.float32)
    dh = lax.dot_general(
        rows_grad, w_down, (((1,), (1,)), ((), ())), preferred_element_type=jnp.float32
    )
    sig = jax.nn.sigmoid(g)
    grad_gate = (dh * u * sig * (1.0 + g * (1.0 - sig))).astype(jnp.bfloat16)
    grad_up = (dh * g * sig).astype(jnp.bfloat16)
    part = lax.dot_general(
        grad_gate, w_gate, (((1,), (1,)), ((), ())), preferred_element_type=jnp.float32
    )
    part = part + lax.dot_general(
        grad_up, w_up, (((1,), (1,)), ((), ())), preferred_element_type=jnp.float32
    )
    return part.astype(jnp.bfloat16)


def dispatch(slots):
    received = lax.all_to_all(slots, "z", 0, 0, tiled=True)
    across = jnp.stack([received, swap(received, "x")])
    return jnp.stack([across, swap(across, "c")])


def combine(partial):
    from_core = swap(partial[1], "c")
    chip_sum = partial[0].astype(jnp.float32) + from_core.astype(jnp.float32)
    from_x = swap(chip_sum[1].astype(jnp.bfloat16), "x")
    total = (chip_sum[0] + from_x.astype(jnp.float32)).astype(jnp.bfloat16)
    return lax.all_to_all(total, "z", 0, 0, tiled=True)


def body(
    fwd_input,
    fwd_experts,
    fwd_gates,
    bwd_input,
    bwd_grad,
    bwd_experts,
    bwd_gates,
    gate_proj,
    up_proj,
    down_proj,
):
    experts = lax.axis_size("z")
    tokens = fwd_input.shape[1]
    width = fwd_input.shape[2]
    capacity = min(tokens, 3 * tokens * TOPK // (2 * experts))
    w_gate = gate_proj[0]
    w_up = up_proj[0]
    w_down = down_proj[0]
    f_select, f_weights = routing(fwd_experts[0], fwd_gates[0], experts, capacity)
    b_select, b_weights = routing(bwd_experts[0], bwd_gates[0], experts, capacity)
    f_slots = into_slots(f_select, fwd_input[0]).reshape(experts, capacity, width)
    b_joined = jnp.concatenate([bwd_input[0], bwd_grad[0]], axis=1)
    b_slots = into_slots(b_select, b_joined).reshape(experts, capacity, 2 * width)
    f_rows = dispatch(f_slots)
    b_rows = dispatch(b_slots)
    f_partial = forward_rows(f_rows.reshape(-1, width), w_gate, w_up, w_down)
    b_partial = backward_rows(b_rows.reshape(-1, 2 * width), w_gate, w_up, w_down)
    f_out = combine(f_partial.reshape(2, 2, experts, capacity, width))
    b_out = combine(b_partial.reshape(2, 2, experts, capacity, width))
    high = lax.Precision.HIGHEST
    f_mixed = jnp.dot(
        f_weights, f_out.reshape(experts * capacity, width).astype(jnp.float32), precision=high
    )
    f_result = (fwd_input[0].astype(jnp.float32) + f_mixed).astype(jnp.bfloat16)
    b_mixed = jnp.dot(
        b_weights, b_out.reshape(experts * capacity, width).astype(jnp.float32), precision=high
    )
    b_result = (bwd_grad[0].astype(jnp.float32) + b_mixed).astype(jnp.bfloat16)
    next_section_input = passed_along(f_result[None], "pp", 1)
    prev_section_grad = passed_along(b_result[None], "pp", -1)
    return (next_section_input, prev_section_grad)


def solution(mesh):
    sections = mesh.shape["pp"]
    devices = mesh.shape["ep"]
    grid = mesh.devices.reshape(sections, devices // GROUP, 2, 2)
    split = Mesh(grid, ("pp",) + EP)
    rows = P("pp", EP, None)
    columns = P("pp", None, EP)
    in_specs = (rows, rows, rows, rows, rows, rows, rows, columns, columns, rows)
    out_specs = (rows, rows)
    return jax.shard_map(body, mesh=split, in_specs=in_specs, out_specs=out_specs, check_vma=False)
```

time: 566 us -> 337 us (0.60)
  waiting for transfers between devices: 399 us -> 231 us
  local copies, waits for them, and re-layouts: 74.9 us -> 12.3 us
  starting transfers between devices: 28.7 us -> 34.4 us
    all_to_all x4, waiting for transfers between devices: 217 us -> 113 us  [the longest x2 84 us: dispatch(): received = lax.all_to_all(slots, 'z', 0, 0, tiled=True)]
    ppermute x4 -> x8, waiting for transfers between devices: 171 us -> 108 us  [swap(): return lax.ppermute(value, axis, [(0, 1), (1, 0)])]
    select_n x6 -> x0, local copies, waits for them, and re-layouts: 43.7 us -> none  [fill_group(): jnp.where(upper, jnp.concatenate([other, gathered], axis=1), jnp.concaten...]
    select_n x4 -> x0, other arithmetic: 16.3 us -> none  [fill_group(): jnp.where(upper, jnp.concatenate([other, gathered], axis=1), jnp.concaten...]
    another operation x0 -> x4, other arithmetic: none -> 14.7 us  [dispatch(): return jnp.stack([across, swap(across, 'c')])]
    ppermute x4 -> x0, local copies, waits for them, and re-layouts: 11.3 us -> none  [from_partner(): return lax.ppermute(block, axis, route)]
    reduce_sum x2 -> x0, other arithmetic: 7.12 us -> none  [the longest x1 3.59 us: body(): jnp.sum(f_back.reshape(experts, GROUP, capacity, width).astype(jnp.float3...]
    broadcast_in_dim x2 -> x0, local copies, waits for them, and re-layouts: 6.96 us -> none  [fill_group(): gathered = shares[:, None]]
  transfers between devices with their start and end apart: 10 -> 14, of which waited for: 7 -> 8; matrix products, arithmetic and copies ran while one was open for 19% -> 16% of each run, Pallas kernels for 0% -> 0%
where the time goes in v1:
time: 337 us; the launch traced here: 332 us
  waiting for transfers between devices  231 us (69%)
  starting transfers between devices  34.4 us (10%)
  matrix products  28.3 us (8%)
  other arithmetic  24.8 us (7%)
  local copies, waits for them, and re-layouts  12.3 us (4%)
    ppermute x8, waiting for transfers between devices, swap(): return lax.ppermute(value, axis, [(0, 1), (1, 0)])  108 us
    all_to_all x2, waiting for transfers between devices, dispatch(): received = lax.all_to_all(slots, 'z', 0, 0, tiled=True)  84 us
    all_to_all x2, waiting for transfers between devices, combine(): return lax.all_to_all(total, 'z', 0, 0, tiled=True)  29.2 us
    another operation x4, other arithmetic, dispatch(): return jnp.stack([across, swap(across, 'c')])  14.7 us
    all_to_all x2, starting transfers between devices, dispatch(): received = lax.all_to_all(slots, 'z', 0, 0, tiled=True)  12.9 us
    all_to_all x2, starting transfers between devices, combine(): return lax.all_to_all(total, 'z', 0, 0, tiled=True)  11.9 us
    ppermute x2, waiting for transfers between devices, passed_along(): return lax.ppermute(value, axis, pairs)  9.99 us
    unnamed x24, local copies, waits for them, and re-layouts  7.18 us
  transfers between devices with their start and end apart: 14, of which 8 were waited for; matrix products, arithmetic and copies ran while one was open for 16% of the time, Pallas kernels for 0%

profile of v1, /device:TPU:16, one launch (start us, length us, event | category | flops | bytes accessed | tf_op | source)
XLA Modules:
  0.0 331.7 jit_solution(7819792813356321197)
XLA Ops:
  0.6 0.8 copy.30
  1.4 0.1 eq.63
  1.6 0.1 reduce_window_sum.18
  1.7 0.2 select_reduce_fusion.1
  1.9 0.1 reduce_sum.63
  2.0 0.7 bitcast_add_fusion
  2.7 0.8 convert_reduce_fusion
  3.5 3.6 %convolution_convert_fusion = bf16[96,14336]{1,0:T(8,128)(2,1)} fusion(bf16[32,7168]{1,0:T(8,128)(2,1)} %bitcast.104, bf16[32,7168]{1,0:T(8,128)(2,1)} %bitcast.106, bf16[32,96]{1,0:T(8,128)(2,1)S(1)} %get-tuple-element.2), kind=kOutput, calls=%fused_computation | convolution fusion | flops 91291648 | bytes 3676160 | tf_op jit(solution)/shard_map/dot_general | solution.py:36
  7.1 5.3 %all-to-all-start.2 = ((bf16[4,24,14336]{2,1,0:T(8,128)(2,1)}), bf16[4,24,14336]{2,1,0:T(8,128)(2,1)S(1)}, u32[]{:S(2)}, u32[]{:S(2)}) async-start(bf16[4,24,14336]{2,1,0:T(8,128)(2,1)} %bitcast.22), calls=%async_computation.2 | async-start | bytes 5505024 | tf_op jit(solution)/shard_map/all_to_all | solution.py:71
  12.4 0.1 copy.28
  12.5 0.1 eq.56
  12.7 0.1 reduce_window_sum.17
  12.8 0.2 select_reduce_fusion.3
  13.0 0.1 reduce_sum.59
  13.2 0.1 convert_reduce_fusion.1
  13.3 1.6 convolution_convert_fusion.2
  14.9 56.5 %all-to-all-done.2 = bf16[4,24,14336]{2,1,0:T(8,128)(2,1)S(1)} async-done(((bf16[4,24,14336]{2,1,0:T(8,128)(2,1)}), bf16[4,24,14336]{2,1,0:T(8,128)(2,1)S(1)}, u32[]{:S(2)}, u32[]{:S(2)}) %all-to-all-start.2) | async-done | bytes 2752544 | tf_op jit(solution)/shard_map/all_to_all | solution.py:71
  71.4 7.5 %all-to-all-start = ((bf16[4,24,7168]{2,1,0:T(8,128)(2,1)}), bf16[4,24,7168]{2,1,0:T(8,128)(2,1)}, u32[]{:S(2)}, u32[]{:S(2)}) async-start(bf16[4,24,7168]{2,1,0:T(8,128)(2,1)} %bitcast.102), calls=%async_computation | async-start | bytes 2752512 | tf_op jit(solution)/shard_map/all_to_all | solution.py:71
  79.0 1.5 collective-permute-start.5
  80.4 27.5 %all-to-all-done = bf16[4,24,7168]{2,1,0:T(8,128)(2,1)} async-done(((bf16[4,24,7168]{2,1,0:T(8,128)(2,1)}), bf16[4,24,7168]{2,1,0:T(8,128)(2,1)}, u32[]{:S(2)}, u32[]{:S(2)}) %all-to-all-start) | async-done | bytes 1376288 | tf_op jit(solution)/shard_map/all_to_all | solution.py:71
  107.9 1.5 collective-permute-start
  109.4 59.4 %collective-permute-done = bf16[4,24,7168]{2,1,0:T(8,128)(2,1)S(1)} collective-permute-done((bf16[4,24,7168]{2,1,0:T(8,128)(2,1)}, bf16[4,24,7168]{2,1,0:T(8,128)(2,1)S(1)}, u32[]{:S(2)}, u32[]{:S(2)}) %collective-permute-start) | collective-permute-done | bytes 1376288 | tf_op jit(solution)/shard_map/ppermute | solution.py:13
  168.8 3.3 %fusion.60 = (bf16[1,2,4,24,7168]{4,3,2,1,0:T(8,128)(2,1)S(1)}, bf16[2,4,24,7168]{3,2,1,0:T(8,128)(2,1)}) fusion(bf16[1,4,24,7168]{3,2,1,0:T(8,128)(2,1)S(1)} %bitcast.105, bf16[1,4,24,7168]{3,2,1,0:T(8,128)(2,1)} %bitcast.4), kind=kLoop, calls=%fused_computation.75 | loop fusion | flops 1376256 | bytes 8257536 | tf_op jit(solution)/shard_map/stack | solution.py:73
  172.1 4.9 %fusion.61 = (bf16[1,2,4,24,14336]{4,3,2,1,0:T(8,128)(2,1)S(1)}, bf16[2,4,24,14336]{3,2,1,0:T(8,128)(2,1)}) fusion(bf16[1,4,24,14336]{3,2,1,0:T(8,128)(2,1)} %bitcast.24, bf16[1,4,24,14336]{3,2,1,0:T(8,128)(2,1)S(1)} %bitcast.96), kind=kLoop, calls=%fused_computation.76 | loop fusion | flops 2752512 | bytes 16515072 | tf_op jit(solution)/shard_map/stack | solution.py:73
  177.1 0.5 collective-permute-start.6
  177.6 4.9 %pad_maximum_fusion.1 = bf16[2,2,4,24,7168]{4,3,2,1,0:T(8,128)(2,1)} fusion(bf16[1,2,4,24,7168]{4,3,2,1,0:T(8,128)(2,1)} %bitcast.7, bf16[1,2,4,24,7168]{4,3,2,1,0:T(8,128)(2,1)S(1)} %get-tuple-element.12), kind=kLoop, calls=%fused_computation.13 | loop fusion | flops 2752512 | bytes 11010048 | tf_op jit(solution)/shard_map/stack | solution.py:73
  182.5 4.3 %fusion.14 = f32[384,256]{1,0:T(8,128)S(1)} fusion(bf16[384,7168]{1,0:T(8,128)(2,1)} %bitcast.98, bf16[1,7168,256]{2,1,0:T(8,128)(2,1)S(1)} %copy-done.4), kind=kOutput, calls=%fused_computation.25 | convolution fusion | flops 1409286144 | bytes 9568256 | tf_op jit(solution)/shard_map/dot_general | solution.py:44
  186.8 0.9 copy-done.3
  187.8 1.6 fusion.19
  189.4 0.4 copy-done.5
  189.8 1.6 convolution_convert_fusion.1
  191.4 2.8 fusion.63
  194.3 0.2 collective-permute-start.2
  194.4 1.6 pad_maximum_fusion
  196.1 3.7 %fusion.4 = f32[384,256]{1,0:T(8,128)S(1)} fusion(bf16[384,14336]{1,0:T(8,128)(2,1)S(1)} %bitcast.91, bf16[1,256,7168]{2,1,0:T(8,128)(2,1)} %param.19), kind=kOutput, calls=%fused_computation.11 | convolution fusion | flops 1409286144 | bytes 9568256 | tf_op jit(solution)/shard_map/dot_general | solution.py:55
  199.7 1.6 fusion.6
  201.4 1.6 fusion.42
  203.0 1.6 fusion.16
  204.6 3.9 %add_convert_fusion = bf16[384,7168]{1,0:T(8,128)(2,1)S(1)} fusion(f32[384,7168]{1,0:T(8,128)S(1)} %fusion.16, bf16[1,7168,256]{2,1,0:T(8,128)(2,1)} %param.18, f32[384,256]{1,0:T(8,128)S(1)} %fusion.4, f32[384,256]{1,0:T(8,128)} %copy-done.7), kind=kOutput, calls=%fused_computation.2 | convolution fusion | flops 1415380992 | bytes 20971520 | tf_op jit(solution)/shard_map/dot_general | solution.py:64
  208.5 0.4 fusion.62
  208.9 0.4 collective-permute-start.7
  209.3 1.0 copy-done.1
  210.3 2.5 convert_add_fusion.1
  212.8 0.2 fusion.25
  213.0 1.5 collective-permute-start.3
  214.5 0.7 convert_add_fusion
  215.3 2.4 copy-done
  217.7 1.2 fusion.26
  218.9 1.0 collective-permute-start.8
  219.9 26.1 %collective-permute-done.3 = bf16[4,24,7168]{2,1,0:T(8,128)(2,1)S(1)} collective-permute-done((bf16[4,24,7168]{2,1,0:T(8,128)(2,1)S(1)}, bf16[4,24,7168]{2,1,0:T(8,128)(2,1)S(1)}, u32[]{:S(2)}, u32[]{:S(2)}) %collective-permute-start.3) | collective-permute-done | bytes 1376288 | tf_op jit(solution)/shard_map/ppermute | solution.py:13
  246.0 1.4 fusion.24
  247.5 5.1 %all-to-all-start.1 = ((bf16[4,24,7168]{2,1,0:T(8,128)(2,1)}), bf16[4,24,7168]{2,1,0:T(8,128)(2,1)S(1)}, u32[]{:S(2)}, u32[]{:S(2)}) async-start(bf16[4,24,7168]{2,1,0:T(8,128)(2,1)} %fusion.24), calls=%async_computation.1 | async-start | bytes 2752512 | tf_op jit(solution)/shard_map/all_to_all | solution.py:81
  252.6 22.4 %collective-permute-done.8 = bf16[4,24,7168]{2,1,0:T(8,128)(2,1)S(1)} collective-permute-done((bf16[4,24,7168]{2,1,0:T(8,128)(2,1)}, bf16[4,24,7168]{2,1,0:T(8,128)(2,1)S(1)}, u32[]{:S(2)}, u32[]{:S(2)}) %collective-permute-start.8) | collective-permute-done | bytes 1376288 | tf_op jit(solution)/shard_map/ppermute | solution.py:13
  275.0 3.1 fusion.22
  278.1 3.1 all-to-all-done.1
  281.2 6.8 %all-to-all-start.3 = ((bf16[4,24,7168]{2,1,0:T(8,128)(2,1)}), bf16[4,24,7168]{2,1,0:T(8,128)(2,1)S(1)}, u32[]{:S(2)}, u32[]{:S(2)}) async-start(bf16[4,24,7168]{2,1,0:T(8,128)(2,1)} %fusion.22), calls=%async_computation.3 | async-start | bytes 2752512 | tf_op jit(solution)/shard_map/all_to_all | solution.py:81
  288.0 1.4 fusion.3
  289.5 1.5 collective-permute-start.4
  290.9 26.1 %all-to-all-done.3 = bf16[4,24,7168]{2,1,0:T(8,128)(2,1)S(1)} async-done(((bf16[4,24,7168]{2,1,0:T(8,128)(2,1)}), bf16[4,24,7168]{2,1,0:T(8,128)(2,1)S(1)}, u32[]{:S(2)}, u32[]{:S(2)}) %all-to-all-start.3) | async-done | bytes 1376288 | tf_op jit(solution)/shard_map/all_to_all | solution.py:81
  317.0 1.7 fusion.2
  318.7 1.5 collective-permute-start.9
  320.2 10.0 %collective-permute-done.9 = bf16[1,32,7168]{2,1,0:T(8,128)(2,1)S(1)} collective-permute-done((bf16[1,32,7168]{2,1,0:T(8,128)(2,1)S(1)}, bf16[1,32,7168]{2,1,0:T(8,128)(2,1)S(1)}, u32[]{:S(2)}, u32[]{:S(2)}) %collective-permute-start.9) | collective-permute-done | bytes 458784 | tf_op jit(solution)/shard_map/ppermute | solution.py:19
  330.2 0.8 copy.34
  331.0 0.8 copy.35
  (28 shorter events, 0.4 us)
Async XLA Ops:
  7.1 5.3 %copy-start.8 = (s32[1,32,2]{1,2,0:T(2,128)S(1)}, s32[1,32,2]{1,2,0:T(2,128)}, u32[]{:S(2)}) copy-start(s32[1,32,2]{1,2,0:T(2,128)} %param.11) | copy-start | bytes 772
  7.1 6.1 %copy-start.9 = (f32[1,32,2]{1,2,0:T(2,128)S(1)}, f32[1,32,2]{1,2,0:T(2,128)}, u32[]{:S(2)}) copy-start(f32[1,32,2]{1,2,0:T(2,128)} %param.12) | copy-start | bytes 772
  7.1 6.2 %copy-start.6 = (bf16[1,32,7168]{2,1,0:T(8,128)(2,1)S(1)}, bf16[1,32,7168]{2,1,0:T(8,128)(2,1)}, u32[]{:S(2)}) copy-start(bf16[1,32,7168]{2,1,0:T(8,128)(2,1)} %param.10) | copy-start | bytes 1376260
  7.1 64.3 %all-to-all-start.2 = ((bf16[4,24,14336]{2,1,0:T(8,128)(2,1)}), bf16[4,24,14336]{2,1,0:T(8,128)(2,1)S(1)}, u32[]{:S(2)}, u32[]{:S(2)}) async-start(bf16[4,24,14336]{2,1,0:T(8,128)(2,1)} %bitcast.22), calls=%async_computation.2 | async-start | bytes 5505024 | tf_op jit(solution)/shard_map/all_to_all | solution.py:71
  71.4 36.5 %all-to-all-start = ((bf16[4,24,7168]{2,1,0:T(8,128)(2,1)}), bf16[4,24,7168]{2,1,0:T(8,128)(2,1)}, u32[]{:S(2)}, u32[]{:S(2)}) async-start(bf16[4,24,7168]{2,1,0:T(8,128)(2,1)} %bitcast.102), calls=%async_computation | async-start | bytes 2752512 | tf_op jit(solution)/shard_map/all_to_all | solution.py:71
  79.0 93.2 %collective-permute-start.5 = (bf16[4,24,14336]{2,1,0:T(8,128)(2,1)S(1)}, bf16[4,24,14336]{2,1,0:T(8,128)(2,1)}, u32[]{:S(2)}, u32[]{:S(2)}) collective-permute-start(bf16[4,24,14336]{2,1,0:T(8,128)(2,1)S(1)} %all-to-all-done.2), channel_id=1, source_target_pairs={{0,2},{2,0},{1,3},{3,1},{4,6},{6,4},{5,7},{7,5},{8,10},{10,8},{9,1... | collective-permute-start | bytes 8257544 | tf_op jit(solution)/shard_map/ppermute | solution.py:13
  107.9 60.9 %collective-permute-start = (bf16[4,24,7168]{2,1,0:T(8,128)(2,1)}, bf16[4,24,7168]{2,1,0:T(8,128)(2,1)S(1)}, u32[]{:S(2)}, u32[]{:S(2)}) collective-permute-start(bf16[4,24,7168]{2,1,0:T(8,128)(2,1)} %all-to-all-done), channel_id=1, source_target_pairs={{0,2},{2,0},{1,3},{3,1},{4,6},{6,4},{5,7},{7,5},{8,10},{10,8},{9,1... | collective-permute-start | bytes 4128776 | tf_op jit(solution)/shard_map/ppermute | solution.py:13
  172.1 5.4 %collective-permute-start.1 = (bf16[2,4,24,7168]{3,2,1,0:T(8,128)(2,1)}, bf16[2,4,24,7168]{3,2,1,0:T(8,128)(2,1)}, u32[]{:S(2)}, u32[]{:S(2)}) collective-permute-start(bf16[2,4,24,7168]{3,2,1,0:T(8,128)(2,1)} %get-tuple-element.13), channel_id=1, source_target_pairs={{0,1},{1,0},{2,3},{3,2},{4,5},{5,4},{6,7},{7,6},{8,9},{9,8},{10,11... | collective-permute-start | bytes 8257544 | tf_op jit(solution)/shard_map/ppermute | solution.py:13
  177.1 17.4 %collective-permute-start.6 = (bf16[2,4,24,14336]{3,2,1,0:T(8,128)(2,1)}, bf16[2,4,24,14336]{3,2,1,0:T(8,128)(2,1)S(1)}, u32[]{:S(2)}, u32[]{:S(2)}) collective-permute-start(bf16[2,4,24,14336]{3,2,1,0:T(8,128)(2,1)} %get-tuple-element.9), channel_id=1, source_target_pairs={{0,1},{1,0},{2,3},{3,2},{4,5},{5,4},{6,7},{7,6},{8,9},{9,8},{10,11... | collective-permute-start | bytes 16515080 | tf_op jit(solution)/shard_map/ppermute | solution.py:13
  177.6 4.9 %copy-start.4 = (bf16[1,7168,256]{2,1,0:T(8,128)(2,1)S(1)}, bf16[1,7168,256]{2,1,0:T(8,128)(2,1)}, u32[]{:S(2)}) copy-start(bf16[1,7168,256]{2,1,0:T(8,128)(2,1)} %param.18) | copy-start | bytes 11010052
  182.5 4.3 %copy-start.2 = (bf16[2,2,4,24,7168]{4,3,2,1,0:T(8,128)(2,1)S(1)}, bf16[2,2,4,24,7168]{4,3,2,1,0:T(8,128)(2,1)}, u32[]{:S(2)}) copy-start(bf16[2,2,4,24,7168]{4,3,2,1,0:T(8,128)(2,1)} %pad_maximum_fusion.1) | copy-start | bytes 16515076
  182.5 5.3 %copy-start.3 = (bf16[1,7168,256]{2,1,0:T(8,128)(2,1)S(1)}, bf16[1,7168,256]{2,1,0:T(8,128)(2,1)}, u32[]{:S(2)}) copy-start(bf16[1,7168,256]{2,1,0:T(8,128)(2,1)} %param.17) | copy-start | bytes 11010052
  187.8 2.0 copy-start.5
  194.3 15.0 %collective-permute-start.2 = (bf16[2,4,24,7168]{3,2,1,0:T(8,128)(2,1)}, bf16[2,4,24,7168]{3,2,1,0:T(8,128)(2,1)}, u32[]{:S(2)}, u32[]{:S(2)}) collective-permute-start(bf16[2,4,24,7168]{3,2,1,0:T(8,128)(2,1)} %bitcast.13), channel_id=1, source_target_pairs={{0,1},{1,0},{2,3},{3,2},{4,5},{5,4},{6,7},{7,6},{8,9},{9,8},{10,11... | collective-permute-start | bytes 8257544 | tf_op jit(solution)/shard_map/ppermute | solution.py:13
  201.3 1.6 copy-start.7
  208.5 1.8 copy-start.1
  208.9 5.6 %collective-permute-start.7 = (bf16[2,4,24,7168]{3,2,1,0:T(8,128)(2,1)S(1)}, bf16[2,4,24,7168]{3,2,1,0:T(8,128)(2,1)S(1)}, u32[]{:S(2)}, u32[]{:S(2)}) collective-permute-start(bf16[2,4,24,7168]{3,2,1,0:T(8,128)(2,1)S(1)} %bitcast.103), channel_id=1, source_target_pairs={{0,1},{1,0},{2,3},{3,2},{4,5},{5,4},{6,7},{7,6},{8,9},{9,8},{10,11... | collective-permute-start | bytes 8257544 | tf_op jit(solution)/shard_map/ppermute | solution.py:13
  213.0 33.1 %collective-permute-start.3 = (bf16[4,24,7168]{2,1,0:T(8,128)(2,1)S(1)}, bf16[4,24,7168]{2,1,0:T(8,128)(2,1)S(1)}, u32[]{:S(2)}, u32[]{:S(2)}) collective-permute-start(bf16[4,24,7168]{2,1,0:T(8,128)(2,1)S(1)} %fusion.25), channel_id=1, source_target_pairs={{0,2},{2,0},{1,3},{3,1},{4,6},{6,4},{5,7},{7,5},{8,10},{10,8},{9,1... | collective-permute-start | bytes 4128776 | tf_op jit(solution)/shard_map/ppermute | solution.py:13
  215.3 2.4 copy-start
  218.9 56.0 %collective-permute-start.8 = (bf16[4,24,7168]{2,1,0:T(8,128)(2,1)}, bf16[4,24,7168]{2,1,0:T(8,128)(2,1)S(1)}, u32[]{:S(2)}, u32[]{:S(2)}) collective-permute-start(bf16[4,24,7168]{2,1,0:T(8,128)(2,1)} %fusion.26), channel_id=1, source_target_pairs={{0,2},{2,0},{1,3},{3,1},{4,6},{6,4},{5,7},{7,5},{8,10},{10,8},{9,1... | collective-permute-start | bytes 4128776 | tf_op jit(solution)/shard_map/ppermute | solution.py:13
  247.5 33.7 %all-to-all-start.1 = ((bf16[4,24,7168]{2,1,0:T(8,128)(2,1)}), bf16[4,24,7168]{2,1,0:T(8,128)(2,1)S(1)}, u32[]{:S(2)}, u32[]{:S(2)}) async-start(bf16[4,24,7168]{2,1,0:T(8,128)(2,1)} %fusion.24), calls=%async_computation.1 | async-start | bytes 2752512 | tf_op jit(solution)/shard_map/all_to_all | solution.py:81
  281.2 35.8 %all-to-all-start.3 = ((bf16[4,24,7168]{2,1,0:T(8,128)(2,1)}), bf16[4,24,7168]{2,1,0:T(8,128)(2,1)S(1)}, u32[]{:S(2)}, u32[]{:S(2)}) async-start(bf16[4,24,7168]{2,1,0:T(8,128)(2,1)} %fusion.22), calls=%async_computation.3 | async-start | bytes 2752512 | tf_op jit(solution)/shard_map/all_to_all | solution.py:81
  289.5 30.8 %collective-permute-start.4 = (bf16[1,32,7168]{2,1,0:T(8,128)(2,1)}, bf16[1,32,7168]{2,1,0:T(8,128)(2,1)S(1)}, u32[]{:S(2)}, u32[]{:S(2)}) collective-permute-start(bf16[1,32,7168]{2,1,0:T(8,128)(2,1)} %fusion.3), channel_id=1, source_target_pairs={{0,16},{16,0},{1,17},{17,1},{2,18},{18,2},{3,19},{19,3},{4,20},{20... | collective-permute-start | bytes 1376264 | tf_op jit(solution)/shard_map/ppermute | solution.py:19
  318.7 11.5 %collective-permute-start.9 = (bf16[1,32,7168]{2,1,0:T(8,128)(2,1)S(1)}, bf16[1,32,7168]{2,1,0:T(8,128)(2,1)S(1)}, u32[]{:S(2)}, u32[]{:S(2)}) collective-permute-start(bf16[1,32,7168]{2,1,0:T(8,128)(2,1)S(1)} %fusion.2), channel_id=1, source_target_pairs={{0,16},{16,0},{1,17},{17,1},{2,18},{18,2},{3,19},{19,3},{4,20},{20... | collective-permute-start | bytes 1376264 | tf_op jit(solution)/shard_map/ppermute | solution.py:19

commit v2 on v1

--- a/solution.py
+++ b/solution.py
@@ -67,8 +67,17 @@
     return part.astype(jnp.bfloat16)
 
 
+def exchange(chunks):
+    count = lax.axis_size("z")
+    out = [chunks[0]]
+    for d in range(1, count):
+        pairs = [(i, i ^ d) for i in range(count)]
+        out.append(lax.ppermute(chunks[d], "z", pairs))
+    return jnp.stack(out)
+
+
 def dispatch(slots):
-    received = lax.all_to_all(slots, "z", 0, 0, tiled=True)
+    received = exchange(slots)
     across = jnp.stack([received, swap(received, "x")])
     return jnp.stack([across, swap(across, "c")])
 
@@ -78,7 +87,7 @@
     chip_sum = partial[0].astype(jnp.float32) + from_core.astype(jnp.float32)
     from_x = swap(chip_sum[1].astype(jnp.bfloat16), "x")
     total = (chip_sum[0] + from_x.astype(jnp.float32)).astype(jnp.bfloat16)
-    return lax.all_to_all(total, "z", 0, 0, tiled=True)
+    return exchange(total)
 
 
 def body(
@@ -100,8 +109,9 @@
     w_gate = gate_proj[0]
     w_up = up_proj[0]
     w_down = down_proj[0]
-    f_select, f_weights = routing(fwd_experts[0], fwd_gates[0], experts, capacity)
-    b_select, b_weights = routing(bwd_experts[0], bwd_gates[0], experts, capacity)
+    here = lax.axis_index("z")
+    f_select, f_weights = routing(fwd_experts[0] ^ here, fwd_gates[0], experts, capacity)
+    b_select, b_weights = routing(bwd_experts[0] ^ here, bwd_gates[0], experts, capacity)
     f_slots = into_slots(f_select, fwd_input[0]).reshape(experts, capacity, width)
     b_joined = jnp.concatenate([bwd_input[0], bwd_grad[0]], axis=1)
     b_slots = into_slots(b_select, b_joined).reshape(experts, capacity, 2 * width)

time: 337 us -> 321 us (0.953); the launches traced: 332 us -> 321 us
  waiting for transfers between devices: 231 us -> 246 us
  starting transfers between devices: 34.4 us -> 23.8 us
  matrix products: 28.3 us -> 19 us
  other arithmetic: 24.8 us -> 19.1 us
    ppermute x0 -> x12, waiting for transfers between devices: none -> 116 us  [exchange(): out.append(lax.ppermute(chunks[d], 'z', pairs))]
    all_to_all x4 -> x0, waiting for transfers between devices: 113 us -> none  [the longest x2 84 us: dispatch(): received = lax.all_to_all(slots, 'z', 0, 0, tiled=True)]
    all_to_all x4 -> x0, starting transfers between devices: 24.8 us -> none  [the longest x2 12.9 us: dispatch(): received = lax.all_to_all(slots, 'z', 0, 0, tiled=True)]
    ppermute x0 -> x12, starting transfers between devices: none -> 14.2 us  [exchange(): out.append(lax.ppermute(chunks[d], 'z', pairs))]
    ppermute x8, waiting for transfers between devices: 108 us -> 122 us  [swap(): return lax.ppermute(value, axis, [(0, 1), (1, 0)])]
    another operation x4, other arithmetic: 14.7 us -> 8.7 us  [dispatch(): return jnp.stack([across, swap(across, 'c')])]
    unnamed x24 -> x28, local copies, waits for them, and re-layouts: 7.18 us -> 6.82 us
  transfers between devices with their start and end apart: 14 -> 22, of which waited for: 8 -> 15; matrix products, arithmetic and copies ran while one was open for 16% -> 11% of each run, Pallas kernels for 0% -> 0%
where the time goes in v2:
time: 321 us
  waiting for transfers between devices  246 us (77%)
  starting transfers between devices  23.8 us (7%)
  other arithmetic  19.1 us (6%)
  matrix products  19 us (6%)
  local copies, waits for them, and re-layouts  11.9 us (4%)
    ppermute x8, waiting for transfers between devices, swap(): return lax.ppermute(value, axis, [(0, 1), (1, 0)])  122 us
    ppermute x12, waiting for transfers between devices, exchange(): out.append(lax.ppermute(chunks[d], 'z', pairs))  116 us
    ppermute x12, starting transfers between devices, exchange(): out.append(lax.ppermute(chunks[d], 'z', pairs))  14.2 us
    another operation x4, other arithmetic, dispatch(): return jnp.stack([across, swap(across, 'c')])  8.7 us
    ppermute x2, waiting for transfers between devices, passed_along(): return lax.ppermute(value, axis, pairs)  8.57 us
    unnamed x28, local copies, waits for them, and re-layouts  6.82 us
  transfers between devices with their start and end apart: 22, of which 15 were waited for; matrix products, arithmetic and copies ran while one was open for 11% of the time, Pallas kernels for 0%

profile of v2, /device:TPU:16, one launch (start us, length us, event | category | flops | bytes accessed | tf_op | source)
XLA Modules:
  0.0 320.8 jit_solution(7409144364705143746)
XLA Ops:
  0.6 0.7 broadcast_xor_fusion
  2.1 0.8 convert_reduce_fusion.1
  2.9 1.6 convolution_convert_fusion.2
  4.6 1.6 collective-permute-start
  6.6 1.6 collective-permute-start.2
  8.1 11.4 %collective-permute-done = bf16[24,7168]{1,0:T(8,128)(2,1)S(1)} collective-permute-done((bf16[24,7168]{1,0:T(8,128)(2,1)S(1)}, bf16[24,7168]{1,0:T(8,128)(2,1)S(1)}, u32[]{:S(2)}, u32[]{:S(2)}) %collective-permute-start) | collective-permute-done | bytes 344096 | tf_op jit(solution)/shard_map/ppermute | solution.py:75
  19.6 10.2 %collective-permute-done.1 = bf16[24,7168]{1,0:T(8,128)(2,1)S(1)} collective-permute-done((bf16[24,7168]{1,0:T(8,128)(2,1)S(1)}, bf16[24,7168]{1,0:T(8,128)(2,1)S(1)}, u32[]{:S(2)}, u32[]{:S(2)}) %collective-permute-start.1) | collective-permute-done | bytes 344096 | tf_op jit(solution)/shard_map/ppermute | solution.py:75
  29.8 8.0 %collective-permute-done.2 = bf16[24,7168]{1,0:T(8,128)(2,1)S(1)} collective-permute-done((bf16[24,7168]{1,0:T(8,128)(2,1)S(1)}, bf16[24,7168]{1,0:T(8,128)(2,1)S(1)}, u32[]{:S(2)}, u32[]{:S(2)}) %collective-permute-start.2) | collective-permute-done | bytes 344096 | tf_op jit(solution)/shard_map/ppermute | solution.py:75
  37.8 1.3 fusion.61
  39.1 1.5 collective-permute-start.3
  41.5 0.9 convolution_convert_fusion
  42.4 27.8 %collective-permute-done.3 = bf16[4,24,7168]{2,1,0:T(8,128)(2,1)} collective-permute-done((bf16[4,24,7168]{2,1,0:T(8,128)(2,1)}, bf16[4,24,7168]{2,1,0:T(8,128)(2,1)}, u32[]{:S(2)}, u32[]{:S(2)}) %collective-permute-start.3) | collective-permute-done | bytes 1376288 | tf_op jit(solution)/shard_map/ppermute | solution.py:13
  70.2 1.7 fusion.60
  72.2 1.9 collective-permute-start.12
  74.2 1.6 collective-permute-start.13
  75.7 25.7 %collective-permute-done.11 = bf16[24,14336]{1,0:T(8,128)(2,1)S(1)} collective-permute-done((bf16[24,14336]{1,0:T(8,128)(2,1)S(1)}, bf16[24,14336]{1,0:T(8,128)(2,1)S(1)}, u32[]{:S(2)}, u32[]{:S(2)}) %collective-permute-start.11) | collective-permute-done | bytes 688160 | tf_op jit(solution)/shard_map/ppermute | solution.py:75
  101.4 18.1 %collective-permute-done.12 = bf16[24,14336]{1,0:T(8,128)(2,1)S(1)} collective-permute-done((bf16[24,14336]{1,0:T(8,128)(2,1)S(1)}, bf16[24,14336]{1,0:T(8,128)(2,1)S(1)}, u32[]{:S(2)}, u32[]{:S(2)}) %collective-permute-start.12) | collective-permute-done | bytes 688160 | tf_op jit(solution)/shard_map/ppermute | solution.py:75
  119.5 16.1 %collective-permute-done.13 = bf16[24,14336]{1,0:T(8,128)(2,1)S(1)} collective-permute-done((bf16[24,14336]{1,0:T(8,128)(2,1)S(1)}, bf16[24,14336]{1,0:T(8,128)(2,1)S(1)}, u32[]{:S(2)}, u32[]{:S(2)}) %collective-permute-start.13) | collective-permute-done | bytes 688160 | tf_op jit(solution)/shard_map/ppermute | solution.py:75
  135.5 0.5 fusion.63
  136.0 1.6 collective-permute-start.14
  137.6 0.5 pad_maximum_fusion.1
  138.1 1.5 copy-done.3
  139.6 1.6 fusion.14
  141.2 0.4 copy-done.1
  141.7 1.6 fusion.19
  143.3 0.4 copy-done.5
  143.7 1.6 convolution_convert_fusion.1
  145.3 1.9 fusion.65
  147.2 49.8 %collective-permute-done.14 = bf16[4,24,14336]{2,1,0:T(8,128)(2,1)S(1)} collective-permute-done((bf16[4,24,14336]{2,1,0:T(8,128)(2,1)S(1)}, bf16[4,24,14336]{2,1,0:T(8,128)(2,1)S(1)}, u32[]{:S(2)}, u32[]{:S(2)}) %collective-permute-start.14) | collective-permute-done | bytes 2752544 | tf_op jit(solution)/shard_map/ppermute | solution.py:13
  197.1 1.6 copy-done.7
  198.7 4.9 %fusion.62 = (bf16[1,2,4,24,14336]{4,3,2,1,0:T(8,128)(2,1)S(1)}, bf16[2,4,24,14336]{3,2,1,0:T(8,128)(2,1)}) fusion(bf16[1,4,24,14336]{3,2,1,0:T(8,128)(2,1)} %bitcast.131, bf16[1,4,24,14336]{3,2,1,0:T(8,128)(2,1)S(1)} %get-tuple-element.12), kind=kLoop, calls=%fused_computation.91 | loop fusion | flops 2752512 | bytes 16515072 | tf_op jit(solution)/shard_map/stack | solution.py:82
  203.6 2.5 convert_add_fusion.1
  206.1 1.4 fusion.25
  207.5 1.5 collective-permute-start.6
  209.0 3.8 %collective-permute-done.15 = bf16[2,4,24,14336]{3,2,1,0:T(8,128)(2,1)S(1)} collective-permute-done((bf16[2,4,24,14336]{3,2,1,0:T(8,128)(2,1)}, bf16[2,4,24,14336]{3,2,1,0:T(8,128)(2,1)S(1)}, u32[]{:S(2)}, u32[]{:S(2)}) %collective-permute-start.15) | collective-permute-done | bytes 5505056 | tf_op jit(solution)/shard_map/ppermute | solution.py:13
  212.8 1.6 pad_maximum_fusion
  214.5 0.4 copy-done.6
  214.9 1.6 fusion.4
  216.5 0.4 copy-done.2
  216.9 1.6 fusion.6
  218.5 0.4 copy-done.4
  218.9 1.6 fusion.42
  220.6 1.6 fusion.16
  222.2 3.9 %add_convert_fusion = bf16[384,7168]{1,0:T(8,128)(2,1)S(1)} fusion(f32[384,7168]{1,0:T(8,128)S(1)} %fusion.16, bf16[1,7168,256]{2,1,0:T(8,128)(2,1)} %param.18, f32[384,256]{1,0:T(8,128)S(1)} %fusion.4, f32[384,256]{1,0:T(8,128)} %copy-done.11), kind=kOutput, calls=%fused_computation.2 | convolution fusion | flops 1415380992 | bytes 20971520 | tf_op jit(solution)/shard_map/dot_general | solution.py:64
  226.1 0.4 fusion.64
  226.7 13.8 %collective-permute-done.6 = bf16[4,24,7168]{2,1,0:T(8,128)(2,1)} collective-permute-done((bf16[4,24,7168]{2,1,0:T(8,128)(2,1)}, bf16[4,24,7168]{2,1,0:T(8,128)(2,1)}, u32[]{:S(2)}, u32[]{:S(2)}) %collective-permute-start.6) | collective-permute-done | bytes 1376288 | tf_op jit(solution)/shard_map/ppermute | solution.py:13
  240.4 2.4 fusion.24
  242.9 0.7 convert_add_fusion
  243.8 1.6 collective-permute-start.17
  245.5 1.9 collective-permute-start.8
  247.4 1.6 collective-permute-start.9
  249.0 26.7 %collective-permute-done.17 = bf16[4,24,7168]{2,1,0:T(8,128)(2,1)S(1)} collective-permute-done((bf16[4,24,7168]{2,1,0:T(8,128)(2,1)S(1)}, bf16[4,24,7168]{2,1,0:T(8,128)(2,1)S(1)}, u32[]{:S(2)}, u32[]{:S(2)}) %collective-permute-start.17) | collective-permute-done | bytes 1376288 | tf_op jit(solution)/shard_map/ppermute | solution.py:13
  276.1 1.9 collective-permute-start.19
  278.0 1.6 collective-permute-start.20
  279.8 0.7 fusion.3
  280.5 1.6 collective-permute-start.10
  282.1 6.2 %collective-permute-done.18 = bf16[24,7168]{1,0:T(8,128)(2,1)S(1)} collective-permute-done((bf16[24,7168]{1,0:T(8,128)(2,1)S(1)}, bf16[24,7168]{1,0:T(8,128)(2,1)S(1)}, u32[]{:S(2)}, u32[]{:S(2)}) %collective-permute-start.18) | collective-permute-done | bytes 344096 | tf_op jit(solution)/shard_map/ppermute | solution.py:75
  288.3 13.0 %collective-permute-done.19 = bf16[24,7168]{1,0:T(8,128)(2,1)S(1)} collective-permute-done((bf16[24,7168]{1,0:T(8,128)(2,1)S(1)}, bf16[24,7168]{1,0:T(8,128)(2,1)S(1)}, u32[]{:S(2)}, u32[]{:S(2)}) %collective-permute-start.19) | collective-permute-done | bytes 344096 | tf_op jit(solution)/shard_map/ppermute | solution.py:75
  301.3 7.0 %collective-permute-done.20 = bf16[24,7168]{1,0:T(8,128)(2,1)S(1)} collective-permute-done((bf16[24,7168]{1,0:T(8,128)(2,1)S(1)}, bf16[24,7168]{1,0:T(8,128)(2,1)S(1)}, u32[]{:S(2)}, u32[]{:S(2)}) %collective-permute-start.20) | collective-permute-done | bytes 344096 | tf_op jit(solution)/shard_map/ppermute | solution.py:75
  308.4 0.7 fusion.2
  309.1 1.6 collective-permute-start.21
  310.7 8.6 %collective-permute-done.21 = bf16[1,32,7168]{2,1,0:T(8,128)(2,1)S(1)} collective-permute-done((bf16[1,32,7168]{2,1,0:T(8,128)(2,1)S(1)}, bf16[1,32,7168]{2,1,0:T(8,128)(2,1)S(1)}, u32[]{:S(2)}, u32[]{:S(2)}) %collective-permute-start.21) | collective-permute-done | bytes 458784 | tf_op jit(solution)/shard_map/ppermute | solution.py:19
  319.3 0.8 copy.34
  320.1 0.8 copy.35
  (59 shorter events, 3.7 us)
Async XLA Ops:
  4.5 36.8 %copy-start.12 = (f32[1,32,2]{1,2,0:T(2,128)S(1)}, f32[1,32,2]{1,2,0:T(2,128)}, u32[]{:S(2)}) copy-start(f32[1,32,2]{1,2,0:T(2,128)} %param.16) | copy-start | bytes 772
  4.5 36.9 %copy-start.9 = (bf16[1,32,7168]{2,1,0:T(8,128)(2,1)S(1)}, bf16[1,32,7168]{2,1,0:T(8,128)(2,1)}, u32[]{:S(2)}) copy-start(bf16[1,32,7168]{2,1,0:T(8,128)(2,1)} %param.14) | copy-start | bytes 1376260
  4.6 36.9 %copy-start.10 = (bf16[1,32,7168]{2,1,0:T(8,128)(2,1)S(1)}, bf16[1,32,7168]{2,1,0:T(8,128)(2,1)}, u32[]{:S(2)}) copy-start(bf16[1,32,7168]{2,1,0:T(8,128)(2,1)} %param.13) | copy-start | bytes 1376260
  4.6 15.0 %collective-permute-start = (bf16[24,7168]{1,0:T(8,128)(2,1)S(1)}, bf16[24,7168]{1,0:T(8,128)(2,1)S(1)}, u32[]{:S(2)}, u32[]{:S(2)}) collective-permute-start(bf16[24,7168]{1,0:T(8,128)(2,1)S(1)} %get-tuple-element.33), channel_id=1, source_target_pairs={{0,4},{4,0},{8,12},{12,8},{1,5},{5,1},{9,13},{13,9},{2,6},{6,2},{1... | collective-permute-start | bytes 1032200 | tf_op jit(solution)/shard_map/ppermute | solution.py:75
  6.2 23.6 %collective-permute-start.1 = (bf16[24,7168]{1,0:T(8,128)(2,1)S(1)}, bf16[24,7168]{1,0:T(8,128)(2,1)S(1)}, u32[]{:S(2)}, u32[]{:S(2)}) collective-permute-start(bf16[24,7168]{1,0:T(8,128)(2,1)S(1)} %get-tuple-element.32), channel_id=1, source_target_pairs={{0,8},{4,12},{8,0},{12,4},{1,9},{5,13},{9,1},{13,5},{2,10},{6,14},... | collective-permute-start | bytes 1032200 | tf_op jit(solution)/shard_map/ppermute | solution.py:75
  6.6 31.2 %collective-permute-start.2 = (bf16[24,7168]{1,0:T(8,128)(2,1)S(1)}, bf16[24,7168]{1,0:T(8,128)(2,1)S(1)}, u32[]{:S(2)}, u32[]{:S(2)}) collective-permute-start(bf16[24,7168]{1,0:T(8,128)(2,1)S(1)} %get-tuple-element.31), channel_id=1, source_target_pairs={{0,12},{4,8},{8,4},{12,0},{1,13},{5,9},{9,5},{13,1},{2,14},{6,10},... | collective-permute-start | bytes 1032200 | tf_op jit(solution)/shard_map/ppermute | solution.py:75
  39.1 31.1 %collective-permute-start.3 = (bf16[4,24,7168]{2,1,0:T(8,128)(2,1)}, bf16[4,24,7168]{2,1,0:T(8,128)(2,1)}, u32[]{:S(2)}, u32[]{:S(2)}) collective-permute-start(bf16[4,24,7168]{2,1,0:T(8,128)(2,1)} %get-tuple-element.29), channel_id=1, source_target_pairs={{0,2},{2,0},{1,3},{3,1},{4,6},{6,4},{5,7},{7,5},{8,10},{10,8},{9,1... | collective-permute-start | bytes 4128776 | tf_op jit(solution)/shard_map/ppermute | solution.py:13
  71.9 65.7 %collective-permute-start.4 = (bf16[2,4,24,7168]{3,2,1,0:T(8,128)(2,1)S(1)}, bf16[2,4,24,7168]{3,2,1,0:T(8,128)(2,1)S(1)}, u32[]{:S(2)}, u32[]{:S(2)}) collective-permute-start(bf16[2,4,24,7168]{3,2,1,0:T(8,128)(2,1)S(1)} %get-tuple-element.19), channel_id=1, source_target_pairs={{0,1},{1,0},{2,3},{3,2},{4,5},{5,4},{6,7},{7,6},{8,9},{9,8},{10,11... | collective-permute-start | bytes 8257544 | tf_op jit(solution)/shard_map/ppermute | solution.py:13
  72.2 29.2 %collective-permute-start.11 = (bf16[24,14336]{1,0:T(8,128)(2,1)S(1)}, bf16[24,14336]{1,0:T(8,128)(2,1)S(1)}, u32[]{:S(2)}, u32[]{:S(2)}) collective-permute-start(bf16[24,14336]{1,0:T(8,128)(2,1)S(1)} %get-tuple-element.17), channel_id=1, source_target_pairs={{0,4},{4,0},{8,12},{12,8},{1,5},{5,1},{9,13},{13,9},{2,6},{6,2},{1... | collective-permute-start | bytes 2064392 | tf_op jit(solution)/shard_map/ppermute | solution.py:75
  72.2 47.2 %collective-permute-start.12 = (bf16[24,14336]{1,0:T(8,128)(2,1)S(1)}, bf16[24,14336]{1,0:T(8,128)(2,1)S(1)}, u32[]{:S(2)}, u32[]{:S(2)}) collective-permute-start(bf16[24,14336]{1,0:T(8,128)(2,1)S(1)} %get-tuple-element.16), channel_id=1, source_target_pairs={{0,8},{4,12},{8,0},{12,4},{1,9},{5,13},{9,1},{13,5},{2,10},{6,14},... | collective-permute-start | bytes 2064392 | tf_op jit(solution)/shard_map/ppermute | solution.py:75
  74.2 61.4 %collective-permute-start.13 = (bf16[24,14336]{1,0:T(8,128)(2,1)S(1)}, bf16[24,14336]{1,0:T(8,128)(2,1)S(1)}, u32[]{:S(2)}, u32[]{:S(2)}) collective-permute-start(bf16[24,14336]{1,0:T(8,128)(2,1)S(1)} %get-tuple-element.15), channel_id=1, source_target_pairs={{0,12},{4,8},{8,4},{12,0},{1,13},{5,9},{9,5},{13,1},{2,14},{6,10},... | collective-permute-start | bytes 2064392 | tf_op jit(solution)/shard_map/ppermute | solution.py:75
  136.0 61.0 %collective-permute-start.14 = (bf16[4,24,14336]{2,1,0:T(8,128)(2,1)S(1)}, bf16[4,24,14336]{2,1,0:T(8,128)(2,1)S(1)}, u32[]{:S(2)}, u32[]{:S(2)}) collective-permute-start(bf16[4,24,14336]{2,1,0:T(8,128)(2,1)S(1)} %get-tuple-element.13), channel_id=1, source_target_pairs={{0,2},{2,0},{1,3},{3,1},{4,6},{6,4},{5,7},{7,5},{8,10},{10,8},{9,1... | collective-permute-start | bytes 8257544 | tf_op jit(solution)/shard_map/ppermute | solution.py:13
  137.6 2.0 copy-start.3
  139.6 2.0 copy-start.1
  141.7 2.0 copy-start.5
  147.2 56.3 %collective-permute-start.5 = (bf16[2,4,24,7168]{3,2,1,0:T(8,128)(2,1)}, bf16[2,4,24,7168]{3,2,1,0:T(8,128)(2,1)}, u32[]{:S(2)}, u32[]{:S(2)}) collective-permute-start(bf16[2,4,24,7168]{3,2,1,0:T(8,128)(2,1)} %bitcast.16), channel_id=1, source_target_pairs={{0,1},{1,0},{2,3},{3,2},{4,5},{5,4},{6,7},{7,6},{8,9},{9,8},{10,11... | collective-permute-start | bytes 8257544 | tf_op jit(solution)/shard_map/ppermute | solution.py:13
  197.1 1.6 copy-start.7
  203.6 9.2 %collective-permute-start.15 = (bf16[2,4,24,14336]{3,2,1,0:T(8,128)(2,1)}, bf16[2,4,24,14336]{3,2,1,0:T(8,128)(2,1)S(1)}, u32[]{:S(2)}, u32[]{:S(2)}) collective-permute-start(bf16[2,4,24,14336]{3,2,1,0:T(8,128)(2,1)} %get-tuple-element.9), channel_id=1, source_target_pairs={{0,1},{1,0},{2,3},{3,2},{4,5},{5,4},{6,7},{7,6},{8,9},{9,8},{10,11... | collective-permute-start | bytes 16515080 | tf_op jit(solution)/shard_map/ppermute | solution.py:13
  206.1 8.4 %copy-start = (f32[2,4,24,7168]{3,2,1,0:T(8,128)}, f32[2,4,24,7168]{3,2,1,0:T(8,128)S(1)}, u32[]{:S(2)}) copy-start(f32[2,4,24,7168]{3,2,1,0:T(8,128)S(1)} %convert_add_fusion.1) | copy-start | bytes 16515076
  207.5 32.9 %collective-permute-start.6 = (bf16[4,24,7168]{2,1,0:T(8,128)(2,1)}, bf16[4,24,7168]{2,1,0:T(8,128)(2,1)}, u32[]{:S(2)}, u32[]{:S(2)}) collective-permute-start(bf16[4,24,7168]{2,1,0:T(8,128)(2,1)} %fusion.25), channel_id=1, source_target_pairs={{0,2},{2,0},{1,3},{3,1},{4,6},{6,4},{5,7},{7,5},{8,10},{10,8},{9,1... | collective-permute-start | bytes 4128776 | tf_op jit(solution)/shard_map/ppermute | solution.py:13
  212.8 2.0 copy-start.6
  214.9 2.0 copy-start.2
  216.9 2.0 copy-start.4
  218.9 1.6 copy-start.11
  226.5 16.4 %collective-permute-start.16 = (bf16[2,4,24,7168]{3,2,1,0:T(8,128)(2,1)S(1)}, bf16[2,4,24,7168]{3,2,1,0:T(8,128)(2,1)S(1)}, u32[]{:S(2)}, u32[]{:S(2)}) collective-permute-start(bf16[2,4,24,7168]{3,2,1,0:T(8,128)(2,1)S(1)} %bitcast.130), channel_id=1, source_target_pairs={{0,1},{1,0},{2,3},{3,2},{4,5},{5,4},{6,7},{7,6},{8,9},{9,8},{10,11... | collective-permute-start | bytes 8257544 | tf_op jit(solution)/shard_map/ppermute | solution.py:13
  243.8 31.9 %collective-permute-start.17 = (bf16[4,24,7168]{2,1,0:T(8,128)(2,1)S(1)}, bf16[4,24,7168]{2,1,0:T(8,128)(2,1)S(1)}, u32[]{:S(2)}, u32[]{:S(2)}) collective-permute-start(bf16[4,24,7168]{2,1,0:T(8,128)(2,1)S(1)} %fusion.26), channel_id=1, source_target_pairs={{0,2},{2,0},{1,3},{3,1},{4,6},{6,4},{5,7},{7,5},{8,10},{10,8},{9,1... | collective-permute-start | bytes 4128776 | tf_op jit(solution)/shard_map/ppermute | solution.py:13
  245.5 32.6 %collective-permute-start.7 = (bf16[24,7168]{1,0:T(8,128)(2,1)S(1)}, bf16[24,7168]{1,0:T(8,128)(2,1)S(1)}, u32[]{:S(2)}, u32[]{:S(2)}) collective-permute-start(bf16[24,7168]{1,0:T(8,128)(2,1)S(1)} %get-tuple-element.27), channel_id=1, source_target_pairs={{0,4},{4,0},{8,12},{12,8},{1,5},{5,1},{9,13},{13,9},{2,6},{6,2},{1... | collective-permute-start | bytes 1032200 | tf_op jit(solution)/shard_map/ppermute | solution.py:75
  245.5 34.1 %collective-permute-start.8 = (bf16[24,7168]{1,0:T(8,128)(2,1)S(1)}, bf16[24,7168]{1,0:T(8,128)(2,1)S(1)}, u32[]{:S(2)}, u32[]{:S(2)}) collective-permute-start(bf16[24,7168]{1,0:T(8,128)(2,1)S(1)} %get-tuple-element.26), channel_id=1, source_target_pairs={{0,8},{4,12},{8,0},{12,4},{1,9},{5,13},{9,1},{13,5},{2,10},{6,14},... | collective-permute-start | bytes 1032200 | tf_op jit(solution)/shard_map/ppermute | solution.py:75
  247.4 32.2 %collective-permute-start.9 = (bf16[24,7168]{1,0:T(8,128)(2,1)S(1)}, bf16[24,7168]{1,0:T(8,128)(2,1)S(1)}, u32[]{:S(2)}, u32[]{:S(2)}) collective-permute-start(bf16[24,7168]{1,0:T(8,128)(2,1)S(1)} %get-tuple-element.25), channel_id=1, source_target_pairs={{0,12},{4,8},{8,4},{12,0},{1,13},{5,9},{9,5},{13,1},{2,14},{6,10},... | collective-permute-start | bytes 1032200 | tf_op jit(solution)/shard_map/ppermute | solution.py:75
  275.9 3.9 %copy-start.8 = (bf16[1,32,7168]{2,1,0:T(8,128)(2,1)S(1)}, bf16[1,32,7168]{2,1,0:T(8,128)(2,1)}, u32[]{:S(2)}) copy-start(bf16[1,32,7168]{2,1,0:T(8,128)(2,1)} %param.10) | copy-start | bytes 1376260
  276.1 12.2 %collective-permute-start.18 = (bf16[24,7168]{1,0:T(8,128)(2,1)S(1)}, bf16[24,7168]{1,0:T(8,128)(2,1)S(1)}, u32[]{:S(2)}, u32[]{:S(2)}) collective-permute-start(bf16[24,7168]{1,0:T(8,128)(2,1)S(1)} %get-tuple-element.23), channel_id=1, source_target_pairs={{0,4},{4,0},{8,12},{12,8},{1,5},{5,1},{9,13},{13,9},{2,6},{6,2},{1... | collective-permute-start | bytes 1032200 | tf_op jit(solution)/shard_map/ppermute | solution.py:75
  276.1 25.2 %collective-permute-start.19 = (bf16[24,7168]{1,0:T(8,128)(2,1)S(1)}, bf16[24,7168]{1,0:T(8,128)(2,1)S(1)}, u32[]{:S(2)}, u32[]{:S(2)}) collective-permute-start(bf16[24,7168]{1,0:T(8,128)(2,1)S(1)} %get-tuple-element.22), channel_id=1, source_target_pairs={{0,8},{4,12},{8,0},{12,4},{1,9},{5,13},{9,1},{13,5},{2,10},{6,14},... | collective-permute-start | bytes 1032200 | tf_op jit(solution)/shard_map/ppermute | solution.py:75
  278.0 30.2 %collective-permute-start.20 = (bf16[24,7168]{1,0:T(8,128)(2,1)S(1)}, bf16[24,7168]{1,0:T(8,128)(2,1)S(1)}, u32[]{:S(2)}, u32[]{:S(2)}) collective-permute-start(bf16[24,7168]{1,0:T(8,128)(2,1)S(1)} %get-tuple-element.21), channel_id=1, source_target_pairs={{0,12},{4,8},{8,4},{12,0},{1,13},{5,9},{9,5},{13,1},{2,14},{6,10},... | collective-permute-start | bytes 1032200 | tf_op jit(solution)/shard_map/ppermute | solution.py:75
  280.5 30.2 %collective-permute-start.10 = (bf16[1,32,7168]{2,1,0:T(8,128)(2,1)S(1)}, bf16[1,32,7168]{2,1,0:T(8,128)(2,1)S(1)}, u32[]{:S(2)}, u32[]{:S(2)}) collective-permute-start(bf16[1,32,7168]{2,1,0:T(8,128)(2,1)S(1)} %fusion.3), channel_id=1, source_target_pairs={{0,16},{16,0},{1,17},{17,1},{2,18},{18,2},{3,19},{19,3},{4,20},{20... | collective-permute-start | bytes 1376264 | tf_op jit(solution)/shard_map/ppermute | solution.py:19
  309.1 10.2 %collective-permute-start.21 = (bf16[1,32,7168]{2,1,0:T(8,128)(2,1)S(1)}, bf16[1,32,7168]{2,1,0:T(8,128)(2,1)S(1)}, u32[]{:S(2)}, u32[]{:S(2)}) collective-permute-start(bf16[1,32,7168]{2,1,0:T(8,128)(2,1)S(1)} %fusion.2), channel_id=1, source_target_pairs={{0,16},{16,0},{1,17},{17,1},{2,18},{18,2},{3,19},{19,3},{4,20},{20... | collective-permute-start | bytes 1376264 | tf_op jit(solution)/shard_map/ppermute | solution.py:19

commit v3 on v2

--- a/solution.py
+++ b/solution.py
@@ -77,9 +77,16 @@
 
 
 def dispatch(slots):
-    received = exchange(slots)
-    across = jnp.stack([received, swap(received, "x")])
-    return jnp.stack([across, swap(across, "c")])
+    count = lax.axis_size("z")
+    pieces = []
+    for d in range(count):
+        if d == 0:
+            received = slots[0]
+        else:
+            received = lax.ppermute(slots[d], "z", [(i, i ^ d) for i in range(count)])
+        across = jnp.stack([received, swap(received, "x")])
+        pieces.append(jnp.stack([across, swap(across, "c")]))
+    return jnp.stack(pieces, axis=2)
 
 
 def combine(partial):

time: 321 us -> 308 us (0.960)
  waiting for transfers between devices: 246 us -> 229 us
    ppermute x12 -> x6, waiting for transfers between devices: 116 us -> 26.5 us  [exchange(): out.append(lax.ppermute(chunks[d], 'z', pairs))]
    ppermute x0 -> x6, waiting for transfers between devices: none -> 79.8 us  [dispatch(): received = lax.ppermute(slots[d], 'z', [(i, i ^ d) for i in range(count)])]
    ppermute x8 -> x20, waiting for transfers between devices: 122 us -> 114 us  [swap(): return lax.ppermute(value, axis, [(0, 1), (1, 0)])]
    ppermute x12 -> x6, starting transfers between devices: 14.2 us -> 7.09 us  [exchange(): out.append(lax.ppermute(chunks[d], 'z', pairs))]
    ppermute x0 -> x6, starting transfers between devices: none -> 7.06 us  [dispatch(): received = lax.ppermute(slots[d], 'z', [(i, i ^ d) for i in range(count)])]
    another operation x6 -> x18, other arithmetic: 10.5 us -> 13.7 us  [the longest x10 9.3 us: dispatch(): return jnp.stack(pieces, axis=2)]
    ppermute x8 -> x20, starting transfers between devices: 6.4 us -> 8.56 us  [swap(): return lax.ppermute(value, axis, [(0, 1), (1, 0)])]
    unnamed x28 -> x20, local copies, waits for them, and re-layouts: 6.82 us -> 5.26 us
  transfers between devices with their start and end apart: 22 -> 34, of which waited for: 15 -> 15; matrix products, arithmetic and copies ran while one was open for 11% -> 14% of each run, Pallas kernels for 0% -> 0%
where the time goes in v3:
time: 308 us
  waiting for transfers between devices  229 us (74%)
  starting transfers between devices  25.9 us (8%)
  other arithmetic  20.2 us (7%)
  matrix products  18.9 us (6%)
  local copies, waits for them, and re-layouts  12.6 us (4%)
    ppermute x20, waiting for transfers between devices, swap(): return lax.ppermute(value, axis, [(0, 1), (1, 0)])  114 us
    ppermute x6, waiting for transfers between devices, dispatch(): received = lax.ppermute(slots[d], 'z', [(i, i ^ d) for i in range(count)])  79.8 us
    ppermute x6, waiting for transfers between devices, exchange(): out.append(lax.ppermute(chunks[d], 'z', pairs))  26.5 us
    another operation x10, other arithmetic, dispatch(): return jnp.stack(pieces, axis=2)  9.3 us
    ppermute x2, waiting for transfers between devices, passed_along(): return lax.ppermute(value, axis, pairs)  8.92 us
    ppermute x20, starting transfers between devices, swap(): return lax.ppermute(value, axis, [(0, 1), (1, 0)])  8.56 us
    ppermute x6, starting transfers between devices, exchange(): out.append(lax.ppermute(chunks[d], 'z', pairs))  7.09 us
    ppermute x6, starting transfers between devices, dispatch(): received = lax.ppermute(slots[d], 'z', [(i, i ^ d) for i in range(count)])  7.06 us
  transfers between devices with their start and end apart: 34, of which 15 were waited for; matrix products, arithmetic and copies ran while one was open for 14% of the time, Pallas kernels for 0%

profile of v3, /device:TPU:16, one launch (start us, length us, event | category | flops | bytes accessed | tf_op | source)
XLA Modules:
  0.0 307.8 jit_solution(10163734195277690473)
XLA Ops:
  0.7 0.8 broadcast_xor_fusion
  2.2 0.8 convert_reduce_fusion.1
  3.0 1.6 convolution_convert_fusion.2
  4.7 1.6 collective-permute-start
  7.1 0.9 convolution_convert_fusion
  8.4 1.6 collective-permute-start.19
  10.3 1.6 collective-permute-start.25
  11.9 0.5 collective-permute-start.17
  12.5 3.2 %collective-permute-done = bf16[24,7168]{1,0:T(8,128)(2,1)S(1)} collective-permute-done((bf16[24,7168]{1,0:T(8,128)(2,1)S(1)}, bf16[24,7168]{1,0:T(8,128)(2,1)S(1)}, u32[]{:S(2)}, u32[]{:S(2)}) %collective-permute-start) | collective-permute-done | bytes 344096 | tf_op jit(solution)/shard_map/ppermute | solution.py:13
  15.7 0.8 collective-permute-start.2
  16.6 45.7 %collective-permute-done.2 = bf16[24,7168]{1,0:T(8,128)(2,1)S(1)} collective-permute-done((bf16[24,7168]{1,0:T(8,128)(2,1)S(1)}, bf16[24,7168]{1,0:T(8,128)(2,1)S(1)}, u32[]{:S(2)}, u32[]{:S(2)}) %collective-permute-start.2) | collective-permute-done | bytes 344096 | tf_op jit(solution)/shard_map/ppermute | solution.py:86
  63.1 20.5 %collective-permute-done.5 = bf16[24,7168]{1,0:T(8,128)(2,1)S(1)} collective-permute-done((bf16[24,7168]{1,0:T(8,128)(2,1)S(1)}, bf16[24,7168]{1,0:T(8,128)(2,1)S(1)}, u32[]{:S(2)}, u32[]{:S(2)}) %collective-permute-start.5) | collective-permute-done | bytes 344096 | tf_op jit(solution)/shard_map/ppermute | solution.py:86
  83.6 2.5 collective-permute-start.8
  86.1 0.5 collective-permute-start.6
  86.7 13.6 %collective-permute-done.8 = bf16[24,7168]{1,0:T(8,128)(2,1)S(1)} collective-permute-done((bf16[24,7168]{1,0:T(8,128)(2,1)S(1)}, bf16[24,7168]{1,0:T(8,128)(2,1)S(1)}, u32[]{:S(2)}, u32[]{:S(2)}) %collective-permute-start.8) | collective-permute-done | bytes 344096 | tf_op jit(solution)/shard_map/ppermute | solution.py:86
  100.3 0.5 collective-permute-start.9
  101.0 9.9 %collective-permute-done.9 = bf16[24,7168]{1,0:T(8,128)(2,1)S(1)} collective-permute-done((bf16[24,7168]{1,0:T(8,128)(2,1)S(1)}, bf16[24,7168]{1,0:T(8,128)(2,1)S(1)}, u32[]{:S(2)}, u32[]{:S(2)}) %collective-permute-start.9) | collective-permute-done | bytes 344096 | tf_op jit(solution)/shard_map/ppermute | solution.py:13
  110.9 0.6 collective-permute-start.4
  111.5 0.5 collective-permute-start.20
  112.2 16.7 %collective-permute-done.20 = bf16[24,14336]{1,0:T(8,128)(2,1)S(1)} collective-permute-done((bf16[24,14336]{1,0:T(8,128)(2,1)S(1)}, bf16[24,14336]{1,0:T(8,128)(2,1)S(1)}, u32[]{:S(2)}, u32[]{:S(2)}) %collective-permute-start.20) | collective-permute-done | bytes 688160 | tf_op jit(solution)/shard_map/ppermute | solution.py:13
  128.9 0.5 collective-permute-start.23
  129.5 1.3 fusion.70
  130.7 14.8 %collective-permute-done.23 = bf16[24,14336]{1,0:T(8,128)(2,1)S(1)} collective-permute-done((bf16[24,14336]{1,0:T(8,128)(2,1)S(1)}, bf16[24,14336]{1,0:T(8,128)(2,1)S(1)}, u32[]{:S(2)}, u32[]{:S(2)}) %collective-permute-start.23) | collective-permute-done | bytes 688160 | tf_op jit(solution)/shard_map/ppermute | solution.py:13
  146.0 1.3 fusion.69
  147.3 13.9 %collective-permute-done.26 = bf16[24,14336]{1,0:T(8,128)(2,1)S(1)} collective-permute-done((bf16[24,14336]{1,0:T(8,128)(2,1)S(1)}, bf16[24,14336]{1,0:T(8,128)(2,1)S(1)}, u32[]{:S(2)}, u32[]{:S(2)}) %collective-permute-start.26) | collective-permute-done | bytes 688160 | tf_op jit(solution)/shard_map/ppermute | solution.py:13
  161.2 1.3 fusion.68
  163.5 0.9 pad_maximum_fusion.1
  164.9 1.6 copy-done.1
  166.5 1.6 fusion.19
  168.5 1.6 fusion.50
  170.6 1.6 convolution_convert_fusion.1
  172.2 2.8 fusion.73
  175.5 1.6 maximum_bitcast_fusion
  177.1 1.6 maximum_bitcast_fusion.1
  178.7 1.6 maximum_bitcast_fusion.2
  180.3 1.6 maximum_bitcast_fusion.3
  181.9 1.5 pad_maximum_fusion
  183.4 2.1 copy.35
  185.5 1.6 fusion.4
  187.1 1.6 fusion.6
  188.7 1.6 fusion.45
  190.3 1.6 fusion.16
  191.9 3.8 %add_convert_fusion = bf16[384,7168]{1,0:T(8,128)(2,1)S(1)} fusion(f32[384,7168]{1,0:T(8,128)S(1)} %fusion.16, bf16[1,7168,256]{2,1,0:T(8,128)(2,1)} %param.18, f32[384,256]{1,0:T(8,128)S(1)} %fusion.4, f32[384,256]{1,0:T(8,128)S(1)} %fusion.6), kind=kOutput, calls=%fused_computation.2 | convolution fusion | flops 1415380992 | bytes 20971520 | tf_op jit(solution)/shard_map/dot_general | solution.py:64
  196.2 1.3 copy-done
  197.5 2.5 convert_add_fusion.1
  200.2 0.6 collective-permute-start.12
  201.3 0.7 convert_add_fusion
  202.2 1.1 collective-permute-start.29
  203.3 30.0 %collective-permute-done.12 = bf16[4,24,7168]{2,1,0:T(8,128)(2,1)S(1)} collective-permute-done((bf16[4,24,7168]{2,1,0:T(8,128)(2,1)S(1)}, bf16[4,24,7168]{2,1,0:T(8,128)(2,1)S(1)}, u32[]{:S(2)}, u32[]{:S(2)}) %collective-permute-start.12) | collective-permute-done | bytes 1376288 | tf_op jit(solution)/shard_map/ppermute | solution.py:13
  233.7 2.0 collective-permute-start.14
  235.7 1.5 collective-permute-start.15
  237.2 24.6 %collective-permute-done.29 = bf16[4,24,7168]{2,1,0:T(8,128)(2,1)S(1)} collective-permute-done((bf16[4,24,7168]{2,1,0:T(8,128)(2,1)S(1)}, bf16[4,24,7168]{2,1,0:T(8,128)(2,1)S(1)}, u32[]{:S(2)}, u32[]{:S(2)}) %collective-permute-start.29) | collective-permute-done | bytes 1376288 | tf_op jit(solution)/shard_map/ppermute | solution.py:13
  262.4 2.0 collective-permute-start.31
  264.4 1.5 collective-permute-start.32
  266.1 0.7 fusion.3
  266.7 1.6 collective-permute-start.16
  268.3 6.7 %collective-permute-done.30 = bf16[24,7168]{1,0:T(8,128)(2,1)S(1)} collective-permute-done((bf16[24,7168]{1,0:T(8,128)(2,1)S(1)}, bf16[24,7168]{1,0:T(8,128)(2,1)S(1)}, u32[]{:S(2)}, u32[]{:S(2)}) %collective-permute-start.30) | collective-permute-done | bytes 344096 | tf_op jit(solution)/shard_map/ppermute | solution.py:75
  275.1 12.6 %collective-permute-done.31 = bf16[24,7168]{1,0:T(8,128)(2,1)S(1)} collective-permute-done((bf16[24,7168]{1,0:T(8,128)(2,1)S(1)}, bf16[24,7168]{1,0:T(8,128)(2,1)S(1)}, u32[]{:S(2)}, u32[]{:S(2)}) %collective-permute-start.31) | collective-permute-done | bytes 344096 | tf_op jit(solution)/shard_map/ppermute | solution.py:75
  287.7 7.2 %collective-permute-done.32 = bf16[24,7168]{1,0:T(8,128)(2,1)S(1)} collective-permute-done((bf16[24,7168]{1,0:T(8,128)(2,1)S(1)}, bf16[24,7168]{1,0:T(8,128)(2,1)S(1)}, u32[]{:S(2)}, u32[]{:S(2)}) %collective-permute-start.32) | collective-permute-done | bytes 344096 | tf_op jit(solution)/shard_map/ppermute | solution.py:75
  295.0 0.7 fusion.2
  295.7 1.6 collective-permute-start.33
  297.3 8.9 %collective-permute-done.33 = bf16[1,32,7168]{2,1,0:T(8,128)(2,1)S(1)} collective-permute-done((bf16[1,32,7168]{2,1,0:T(8,128)(2,1)S(1)}, bf16[1,32,7168]{2,1,0:T(8,128)(2,1)S(1)}, u32[]{:S(2)}, u32[]{:S(2)}) %collective-permute-start.33) | collective-permute-done | bytes 458784 | tf_op jit(solution)/shard_map/ppermute | solution.py:19
  306.2 0.8 copy.38
  307.0 0.8 copy.39
  (89 shorter events, 9.6 us)
Async XLA Ops:
  0.6 6.4 %copy-start.8 = (f32[1,32,2]{1,2,0:T(2,128)S(1)}, f32[1,32,2]{1,2,0:T(2,128)}, u32[]{:S(2)}) copy-start(f32[1,32,2]{1,2,0:T(2,128)} %param.16) | copy-start | bytes 772
  0.6 6.5 %copy-start.6 = (bf16[1,32,7168]{2,1,0:T(8,128)(2,1)S(1)}, bf16[1,32,7168]{2,1,0:T(8,128)(2,1)}, u32[]{:S(2)}) copy-start(bf16[1,32,7168]{2,1,0:T(8,128)(2,1)} %param.14) | copy-start | bytes 1376260
  0.7 6.5 %copy-start.7 = (bf16[1,32,7168]{2,1,0:T(8,128)(2,1)S(1)}, bf16[1,32,7168]{2,1,0:T(8,128)(2,1)}, u32[]{:S(2)}) copy-start(bf16[1,32,7168]{2,1,0:T(8,128)(2,1)} %param.13) | copy-start | bytes 1376260
  4.7 11.0 %collective-permute-start = (bf16[24,7168]{1,0:T(8,128)(2,1)S(1)}, bf16[24,7168]{1,0:T(8,128)(2,1)S(1)}, u32[]{:S(2)}, u32[]{:S(2)}) collective-permute-start(bf16[24,7168]{1,0:T(8,128)(2,1)S(1)} %get-tuple-element.35), channel_id=1, source_target_pairs={{0,2},{2,0},{1,3},{3,1},{4,6},{6,4},{5,7},{7,5},{8,10},{10,8},{9,1... | collective-permute-start | bytes 1032200 | tf_op jit(solution)/shard_map/ppermute | solution.py:13
  8.4 102.6 %collective-permute-start.19 = (bf16[24,14336]{1,0:T(8,128)(2,1)S(1)}, bf16[24,14336]{1,0:T(8,128)(2,1)S(1)}, u32[]{:S(2)}, u32[]{:S(2)}) collective-permute-start(bf16[24,14336]{1,0:T(8,128)(2,1)S(1)} %get-tuple-element.13), channel_id=1, source_target_pairs={{0,4},{4,0},{8,12},{12,8},{1,5},{5,1},{9,13},{13,9},{2,6},{6,2},{1... | collective-permute-start | bytes 2064392 | tf_op jit(solution)/shard_map/ppermute | solution.py:86
  10.0 102.1 %collective-permute-start.22 = (bf16[24,14336]{1,0:T(8,128)(2,1)S(1)}, bf16[24,14336]{1,0:T(8,128)(2,1)S(1)}, u32[]{:S(2)}, u32[]{:S(2)}) collective-permute-start(bf16[24,14336]{1,0:T(8,128)(2,1)S(1)} %get-tuple-element.12), channel_id=1, source_target_pairs={{0,8},{4,12},{8,0},{12,4},{1,9},{5,13},{9,1},{13,5},{2,10},{6,14},... | collective-permute-start | bytes 2064392 | tf_op jit(solution)/shard_map/ppermute | solution.py:86
  10.3 120.4 %collective-permute-start.25 = (bf16[24,14336]{1,0:T(8,128)(2,1)S(1)}, bf16[24,14336]{1,0:T(8,128)(2,1)S(1)}, u32[]{:S(2)}, u32[]{:S(2)}) collective-permute-start(bf16[24,14336]{1,0:T(8,128)(2,1)S(1)} %get-tuple-element.11), channel_id=1, source_target_pairs={{0,12},{4,8},{8,4},{12,0},{1,13},{5,9},{9,5},{13,1},{2,14},{6,10},... | collective-permute-start | bytes 2064392 | tf_op jit(solution)/shard_map/ppermute | solution.py:86
  11.9 50.6 %collective-permute-start.17 = (bf16[24,14336]{1,0:T(8,128)(2,1)S(1)}, bf16[24,14336]{1,0:T(8,128)(2,1)S(1)}, u32[]{:S(2)}, u32[]{:S(2)}) collective-permute-start(bf16[24,14336]{1,0:T(8,128)(2,1)S(1)} %get-tuple-element.14), channel_id=1, source_target_pairs={{0,2},{2,0},{1,3},{3,1},{4,6},{6,4},{5,7},{7,5},{8,10},{10,8},{9,1... | collective-permute-start | bytes 2064392 | tf_op jit(solution)/shard_map/ppermute | solution.py:13
  15.7 46.6 %collective-permute-start.2 = (bf16[24,7168]{1,0:T(8,128)(2,1)S(1)}, bf16[24,7168]{1,0:T(8,128)(2,1)S(1)}, u32[]{:S(2)}, u32[]{:S(2)}) collective-permute-start(bf16[24,7168]{1,0:T(8,128)(2,1)S(1)} %get-tuple-element.34), channel_id=1, source_target_pairs={{0,4},{4,0},{8,12},{12,8},{1,5},{5,1},{9,13},{13,9},{2,6},{6,2},{1... | collective-permute-start | bytes 1032200 | tf_op jit(solution)/shard_map/ppermute | solution.py:86
  62.3 21.3 %collective-permute-start.5 = (bf16[24,7168]{1,0:T(8,128)(2,1)S(1)}, bf16[24,7168]{1,0:T(8,128)(2,1)S(1)}, u32[]{:S(2)}, u32[]{:S(2)}) collective-permute-start(bf16[24,7168]{1,0:T(8,128)(2,1)S(1)} %get-tuple-element.33), channel_id=1, source_target_pairs={{0,8},{4,12},{8,0},{12,4},{1,9},{5,13},{9,1},{13,5},{2,10},{6,14},... | collective-permute-start | bytes 1032200 | tf_op jit(solution)/shard_map/ppermute | solution.py:86
  62.5 23.6 %collective-permute-start.3 = (bf16[24,7168]{1,0:T(8,128)(2,1)S(1)}, bf16[24,7168]{1,0:T(8,128)(2,1)S(1)}, u32[]{:S(2)}, u32[]{:S(2)}) collective-permute-start(bf16[24,7168]{1,0:T(8,128)(2,1)S(1)} %collective-permute-done.2), channel_id=1, source_target_pairs={{0,2},{2,0},{1,3},{3,1},{4,6},{6,4},{5,7},{7,5},{8,10},{10,8},{9,1... | collective-permute-start | bytes 1032200 | tf_op jit(solution)/shard_map/ppermute | solution.py:13
  83.6 16.8 %collective-permute-start.8 = (bf16[24,7168]{1,0:T(8,128)(2,1)S(1)}, bf16[24,7168]{1,0:T(8,128)(2,1)S(1)}, u32[]{:S(2)}, u32[]{:S(2)}) collective-permute-start(bf16[24,7168]{1,0:T(8,128)(2,1)S(1)} %get-tuple-element.32), channel_id=1, source_target_pairs={{0,12},{4,8},{8,4},{12,0},{1,13},{5,9},{9,5},{13,1},{2,14},{6,10},... | collective-permute-start | bytes 1032200 | tf_op jit(solution)/shard_map/ppermute | solution.py:86
  86.1 14.3 %collective-permute-start.6 = (bf16[24,7168]{1,0:T(8,128)(2,1)S(1)}, bf16[24,7168]{1,0:T(8,128)(2,1)S(1)}, u32[]{:S(2)}, u32[]{:S(2)}) collective-permute-start(bf16[24,7168]{1,0:T(8,128)(2,1)S(1)} %collective-permute-done.5), channel_id=1, source_target_pairs={{0,2},{2,0},{1,3},{3,1},{4,6},{6,4},{5,7},{7,5},{8,10},{10,8},{9,1... | collective-permute-start | bytes 1032200 | tf_op jit(solution)/shard_map/ppermute | solution.py:13
  100.3 11.2 %collective-permute-start.1 = (bf16[2,24,7168]{2,1,0:T(8,128)(2,1)S(1)}, bf16[2,24,7168]{2,1,0:T(8,128)(2,1)S(1)}, u32[]{:S(2)}, u32[]{:S(2)}) collective-permute-start(bf16[2,24,7168]{2,1,0:T(8,128)(2,1)S(1)} %get-tuple-element.37), channel_id=1, source_target_pairs={{0,1},{1,0},{2,3},{3,2},{4,5},{5,4},{6,7},{7,6},{8,9},{9,8},{10,11... | collective-permute-start | bytes 2064392 | tf_op jit(solution)/shard_map/ppermute | solution.py:13
  100.3 10.5 %collective-permute-start.9 = (bf16[24,7168]{1,0:T(8,128)(2,1)S(1)}, bf16[24,7168]{1,0:T(8,128)(2,1)S(1)}, u32[]{:S(2)}, u32[]{:S(2)}) collective-permute-start(bf16[24,7168]{1,0:T(8,128)(2,1)S(1)} %collective-permute-done.8), channel_id=1, source_target_pairs={{0,2},{2,0},{1,3},{3,1},{4,6},{6,4},{5,7},{7,5},{8,10},{10,8},{9,1... | collective-permute-start | bytes 1032200 | tf_op jit(solution)/shard_map/ppermute | solution.py:13
  110.8 64.6 %collective-permute-start.18 = (bf16[2,24,14336]{2,1,0:T(8,128)(2,1)S(1)}, bf16[2,24,14336]{2,1,0:T(8,128)(2,1)}, u32[]{:S(2)}, u32[]{:S(2)}) collective-permute-start(bf16[2,24,14336]{2,1,0:T(8,128)(2,1)S(1)} %get-tuple-element.20), channel_id=1, source_target_pairs={{0,1},{1,0},{2,3},{3,2},{4,5},{5,4},{6,7},{7,6},{8,9},{9,8},{10,11... | collective-permute-start | bytes 4128776 | tf_op jit(solution)/shard_map/ppermute | solution.py:13
  110.9 51.6 %collective-permute-start.4 = (bf16[2,24,7168]{2,1,0:T(8,128)(2,1)S(1)}, bf16[2,24,7168]{2,1,0:T(8,128)(2,1)S(1)}, u32[]{:S(2)}, u32[]{:S(2)}) collective-permute-start(bf16[2,24,7168]{2,1,0:T(8,128)(2,1)S(1)} %get-tuple-element.39), channel_id=1, source_target_pairs={{0,1},{1,0},{2,3},{3,2},{4,5},{5,4},{6,7},{7,6},{8,9},{9,8},{10,11... | collective-permute-start | bytes 2064392 | tf_op jit(solution)/shard_map/ppermute | solution.py:13
  111.5 17.4 %collective-permute-start.20 = (bf16[24,14336]{1,0:T(8,128)(2,1)S(1)}, bf16[24,14336]{1,0:T(8,128)(2,1)S(1)}, u32[]{:S(2)}, u32[]{:S(2)}) collective-permute-start(bf16[24,14336]{1,0:T(8,128)(2,1)S(1)} %collective-permute-done.19), channel_id=1, source_target_pairs={{0,2},{2,0},{1,3},{3,1},{4,6},{6,4},{5,7},{7,5},{8,10},{10,8},{9,1... | collective-permute-start | bytes 2064392 | tf_op jit(solution)/shard_map/ppermute | solution.py:13
  112.2 51.0 %collective-permute-start.7 = (bf16[2,24,7168]{2,1,0:T(8,128)(2,1)S(1)}, bf16[2,24,7168]{2,1,0:T(8,128)(2,1)S(1)}, u32[]{:S(2)}, u32[]{:S(2)}) collective-permute-start(bf16[2,24,7168]{2,1,0:T(8,128)(2,1)S(1)} %get-tuple-element.41), channel_id=1, source_target_pairs={{0,1},{1,0},{2,3},{3,2},{4,5},{5,4},{6,7},{7,6},{8,9},{9,8},{10,11... | collective-permute-start | bytes 2064392 | tf_op jit(solution)/shard_map/ppermute | solution.py:13
  128.9 16.6 %collective-permute-start.23 = (bf16[24,14336]{1,0:T(8,128)(2,1)S(1)}, bf16[24,14336]{1,0:T(8,128)(2,1)S(1)}, u32[]{:S(2)}, u32[]{:S(2)}) collective-permute-start(bf16[24,14336]{1,0:T(8,128)(2,1)S(1)} %collective-permute-done.22), channel_id=1, source_target_pairs={{0,2},{2,0},{1,3},{3,1},{4,6},{6,4},{5,7},{7,5},{8,10},{10,8},{9,1... | collective-permute-start | bytes 2064392 | tf_op jit(solution)/shard_map/ppermute | solution.py:13
  130.7 32.6 %collective-permute-start.10 = (bf16[2,24,7168]{2,1,0:T(8,128)(2,1)S(1)}, bf16[2,24,7168]{2,1,0:T(8,128)(2,1)S(1)}, u32[]{:S(2)}, u32[]{:S(2)}) collective-permute-start(bf16[2,24,7168]{2,1,0:T(8,128)(2,1)S(1)} %get-tuple-element.43), channel_id=1, source_target_pairs={{0,1},{1,0},{2,3},{3,2},{4,5},{5,4},{6,7},{7,6},{8,9},{9,8},{10,11... | collective-permute-start | bytes 2064392 | tf_op jit(solution)/shard_map/ppermute | solution.py:13
  145.5 15.7 %collective-permute-start.26 = (bf16[24,14336]{1,0:T(8,128)(2,1)S(1)}, bf16[24,14336]{1,0:T(8,128)(2,1)S(1)}, u32[]{:S(2)}, u32[]{:S(2)}) collective-permute-start(bf16[24,14336]{1,0:T(8,128)(2,1)S(1)} %collective-permute-done.25), channel_id=1, source_target_pairs={{0,2},{2,0},{1,3},{3,1},{4,6},{6,4},{5,7},{7,5},{8,10},{10,8},{9,1... | collective-permute-start | bytes 2064392 | tf_op jit(solution)/shard_map/ppermute | solution.py:13
  161.2 15.9 %collective-permute-start.21 = (bf16[2,24,14336]{2,1,0:T(8,128)(2,1)}, bf16[2,24,14336]{2,1,0:T(8,128)(2,1)}, u32[]{:S(2)}, u32[]{:S(2)}) collective-permute-start(bf16[2,24,14336]{2,1,0:T(8,128)(2,1)} %get-tuple-element.22), channel_id=1, source_target_pairs={{0,1},{1,0},{2,3},{3,2},{4,5},{5,4},{6,7},{7,6},{8,9},{9,8},{10,11... | collective-permute-start | bytes 4128776 | tf_op jit(solution)/shard_map/ppermute | solution.py:13
  162.5 16.2 %collective-permute-start.24 = (bf16[2,24,14336]{2,1,0:T(8,128)(2,1)}, bf16[2,24,14336]{2,1,0:T(8,128)(2,1)}, u32[]{:S(2)}, u32[]{:S(2)}) collective-permute-start(bf16[2,24,14336]{2,1,0:T(8,128)(2,1)} %get-tuple-element.24), channel_id=1, source_target_pairs={{0,1},{1,0},{2,3},{3,2},{4,5},{5,4},{6,7},{7,6},{8,9},{9,8},{10,11... | collective-permute-start | bytes 4128776 | tf_op jit(solution)/shard_map/ppermute | solution.py:13
  163.2 17.1 %collective-permute-start.27 = (bf16[2,24,14336]{2,1,0:T(8,128)(2,1)}, bf16[2,24,14336]{2,1,0:T(8,128)(2,1)}, u32[]{:S(2)}, u32[]{:S(2)}) collective-permute-start(bf16[2,24,14336]{2,1,0:T(8,128)(2,1)} %get-tuple-element.26), channel_id=1, source_target_pairs={{0,1},{1,0},{2,3},{3,2},{4,5},{5,4},{6,7},{7,6},{8,9},{9,8},{10,11... | collective-permute-start | bytes 4128776 | tf_op jit(solution)/shard_map/ppermute | solution.py:13
  164.5 2.0 copy-start.1
  166.5 2.0 copy-start.2
  168.5 2.0 copy-start.3
  175.0 21.2 %collective-permute-start.11 = (bf16[2,4,24,7168]{3,2,1,0:T(8,128)(2,1)}, bf16[2,4,24,7168]{3,2,1,0:T(8,128)(2,1)}, u32[]{:S(2)}, u32[]{:S(2)}) collective-permute-start(bf16[2,4,24,7168]{3,2,1,0:T(8,128)(2,1)} %bitcast.28), channel_id=1, source_target_pairs={{0,1},{1,0},{2,3},{3,2},{4,5},{5,4},{6,7},{7,6},{8,9},{9,8},{10,11... | collective-permute-start | bytes 8257544 | tf_op jit(solution)/shard_map/ppermute | solution.py:13
  183.4 2.1 copy-start.4
  195.7 1.8 copy-start
  196.1 5.2 %collective-permute-start.28 = (bf16[2,4,24,7168]{3,2,1,0:T(8,128)(2,1)S(1)}, bf16[2,4,24,7168]{3,2,1,0:T(8,128)(2,1)S(1)}, u32[]{:S(2)}, u32[]{:S(2)}) collective-permute-start(bf16[2,4,24,7168]{3,2,1,0:T(8,128)(2,1)S(1)} %bitcast.169), channel_id=1, source_target_pairs={{0,1},{1,0},{2,3},{3,2},{4,5},{5,4},{6,7},{7,6},{8,9},{9,8},{10,11... | collective-permute-start | bytes 8257544 | tf_op jit(solution)/shard_map/ppermute | solution.py:13
  200.2 33.1 %collective-permute-start.12 = (bf16[4,24,7168]{2,1,0:T(8,128)(2,1)S(1)}, bf16[4,24,7168]{2,1,0:T(8,128)(2,1)S(1)}, u32[]{:S(2)}, u32[]{:S(2)}) collective-permute-start(bf16[4,24,7168]{2,1,0:T(8,128)(2,1)S(1)} %fusion.25), channel_id=1, source_target_pairs={{0,2},{2,0},{1,3},{3,1},{4,6},{6,4},{5,7},{7,5},{8,10},{10,8},{9,1... | collective-permute-start | bytes 4128776 | tf_op jit(solution)/shard_map/ppermute | solution.py:13
  202.2 59.7 %collective-permute-start.29 = (bf16[4,24,7168]{2,1,0:T(8,128)(2,1)S(1)}, bf16[4,24,7168]{2,1,0:T(8,128)(2,1)S(1)}, u32[]{:S(2)}, u32[]{:S(2)}) collective-permute-start(bf16[4,24,7168]{2,1,0:T(8,128)(2,1)S(1)} %fusion.26), channel_id=1, source_target_pairs={{0,2},{2,0},{1,3},{3,1},{4,6},{6,4},{5,7},{7,5},{8,10},{10,8},{9,1... | collective-permute-start | bytes 4128776 | tf_op jit(solution)/shard_map/ppermute | solution.py:13
  233.7 30.7 %collective-permute-start.13 = (bf16[24,7168]{1,0:T(8,128)(2,1)S(1)}, bf16[24,7168]{1,0:T(8,128)(2,1)S(1)}, u32[]{:S(2)}, u32[]{:S(2)}) collective-permute-start(bf16[24,7168]{1,0:T(8,128)(2,1)S(1)} %get-tuple-element.30), channel_id=1, source_target_pairs={{0,4},{4,0},{8,12},{12,8},{1,5},{5,1},{9,13},{13,9},{2,6},{6,2},{1... | collective-permute-start | bytes 1032200 | tf_op jit(solution)/shard_map/ppermute | solution.py:75
  233.7 32.1 %collective-permute-start.14 = (bf16[24,7168]{1,0:T(8,128)(2,1)S(1)}, bf16[24,7168]{1,0:T(8,128)(2,1)S(1)}, u32[]{:S(2)}, u32[]{:S(2)}) collective-permute-start(bf16[24,7168]{1,0:T(8,128)(2,1)S(1)} %get-tuple-element.29), channel_id=1, source_target_pairs={{0,8},{4,12},{8,0},{12,4},{1,9},{5,13},{9,1},{13,5},{2,10},{6,14},... | collective-permute-start | bytes 1032200 | tf_op jit(solution)/shard_map/ppermute | solution.py:75
  235.7 30.1 %collective-permute-start.15 = (bf16[24,7168]{1,0:T(8,128)(2,1)S(1)}, bf16[24,7168]{1,0:T(8,128)(2,1)S(1)}, u32[]{:S(2)}, u32[]{:S(2)}) collective-permute-start(bf16[24,7168]{1,0:T(8,128)(2,1)S(1)} %get-tuple-element.28), channel_id=1, source_target_pairs={{0,12},{4,8},{8,4},{12,0},{1,13},{5,9},{9,5},{13,1},{2,14},{6,10},... | collective-permute-start | bytes 1032200 | tf_op jit(solution)/shard_map/ppermute | solution.py:75
  262.2 3.9 %copy-start.5 = (bf16[1,32,7168]{2,1,0:T(8,128)(2,1)S(1)}, bf16[1,32,7168]{2,1,0:T(8,128)(2,1)}, u32[]{:S(2)}) copy-start(bf16[1,32,7168]{2,1,0:T(8,128)(2,1)} %param.10) | copy-start | bytes 1376260
  262.3 12.8 %collective-permute-start.30 = (bf16[24,7168]{1,0:T(8,128)(2,1)S(1)}, bf16[24,7168]{1,0:T(8,128)(2,1)S(1)}, u32[]{:S(2)}, u32[]{:S(2)}) collective-permute-start(bf16[24,7168]{1,0:T(8,128)(2,1)S(1)} %get-tuple-element.18), channel_id=1, source_target_pairs={{0,4},{4,0},{8,12},{12,8},{1,5},{5,1},{9,13},{13,9},{2,6},{6,2},{1... | collective-permute-start | bytes 1032200 | tf_op jit(solution)/shard_map/ppermute | solution.py:75
  262.4 25.3 %collective-permute-start.31 = (bf16[24,7168]{1,0:T(8,128)(2,1)S(1)}, bf16[24,7168]{1,0:T(8,128)(2,1)S(1)}, u32[]{:S(2)}, u32[]{:S(2)}) collective-permute-start(bf16[24,7168]{1,0:T(8,128)(2,1)S(1)} %get-tuple-element.17), channel_id=1, source_target_pairs={{0,8},{4,12},{8,0},{12,4},{1,9},{5,13},{9,1},{13,5},{2,10},{6,14},... | collective-permute-start | bytes 1032200 | tf_op jit(solution)/shard_map/ppermute | solution.py:75
  264.4 30.5 %collective-permute-start.32 = (bf16[24,7168]{1,0:T(8,128)(2,1)S(1)}, bf16[24,7168]{1,0:T(8,128)(2,1)S(1)}, u32[]{:S(2)}, u32[]{:S(2)}) collective-permute-start(bf16[24,7168]{1,0:T(8,128)(2,1)S(1)} %get-tuple-element.16), channel_id=1, source_target_pairs={{0,12},{4,8},{8,4},{12,0},{1,13},{5,9},{9,5},{13,1},{2,14},{6,10},... | collective-permute-start | bytes 1032200 | tf_op jit(solution)/shard_map/ppermute | solution.py:75
  266.7 30.6 %collective-permute-start.16 = (bf16[1,32,7168]{2,1,0:T(8,128)(2,1)S(1)}, bf16[1,32,7168]{2,1,0:T(8,128)(2,1)S(1)}, u32[]{:S(2)}, u32[]{:S(2)}) collective-permute-start(bf16[1,32,7168]{2,1,0:T(8,128)(2,1)S(1)} %fusion.3), channel_id=1, source_target_pairs={{0,16},{16,0},{1,17},{17,1},{2,18},{18,2},{3,19},{19,3},{4,20},{20... | collective-permute-start | bytes 1376264 | tf_op jit(solution)/shard_map/ppermute | solution.py:19
  295.7 10.5 %collective-permute-start.33 = (bf16[1,32,7168]{2,1,0:T(8,128)(2,1)S(1)}, bf16[1,32,7168]{2,1,0:T(8,128)(2,1)S(1)}, u32[]{:S(2)}, u32[]{:S(2)}) collective-permute-start(bf16[1,32,7168]{2,1,0:T(8,128)(2,1)S(1)} %fusion.2), channel_id=1, source_target_pairs={{0,16},{16,0},{1,17},{17,1},{2,18},{18,2},{3,19},{19,3},{4,20},{20... | collective-permute-start | bytes 1376264 | tf_op jit(solution)/shard_map/ppermute | solution.py:19

commit v4 on v2

--- a/solution.py
+++ b/solution.py
@@ -67,27 +67,22 @@
     return part.astype(jnp.bfloat16)
 
 
-def exchange(chunks):
+def to_group(chunk, d):
     count = lax.axis_size("z")
-    out = [chunks[0]]
-    for d in range(1, count):
-        pairs = [(i, i ^ d) for i in range(count)]
-        out.append(lax.ppermute(chunks[d], "z", pairs))
-    return jnp.stack(out)
-
-
-def dispatch(slots):
-    received = exchange(slots)
+    received = chunk if d == 0 else lax.ppermute(chunk, "z", [(i, i ^ d) for i in range(count)])
     across = jnp.stack([received, swap(received, "x")])
     return jnp.stack([across, swap(across, "c")])
 
 
-def combine(partial):
+def from_group(partial, d):
+    count = lax.axis_size("z")
     from_core = swap(partial[1], "c")
     chip_sum = partial[0].astype(jnp.float32) + from_core.astype(jnp.float32)
     from_x = swap(chip_sum[1].astype(jnp.bfloat16), "x")
     total = (chip_sum[0] + from_x.astype(jnp.float32)).astype(jnp.bfloat16)
-    return exchange(total)
+    if d == 0:
+        return total
+    return lax.ppermute(total, "z", [(i, i ^ d) for i in range(count)])
 
 
 def body(
@@ -115,12 +110,16 @@
     f_slots = into_slots(f_select, fwd_input[0]).reshape(experts, capacity, width)
     b_joined = jnp.concatenate([bwd_input[0], bwd_grad[0]], axis=1)
     b_slots = into_slots(b_select, b_joined).reshape(experts, capacity, 2 * width)
-    f_rows = dispatch(f_slots)
-    b_rows = dispatch(b_slots)
-    f_partial = forward_rows(f_rows.reshape(-1, width), w_gate, w_up, w_down)
-    b_partial = backward_rows(b_rows.reshape(-1, 2 * width), w_gate, w_up, w_down)
-    f_out = combine(f_partial.reshape(2, 2, experts, capacity, width))
-    b_out = combine(b_partial.reshape(2, 2, experts, capacity, width))
+    f_outs, b_outs = [], []
+    for d in range(experts):
+        f_rows = to_group(f_slots[d], d)
+        b_rows = to_group(b_slots[d], d)
+        f_partial = forward_rows(f_rows.reshape(-1, width), w_gate, w_up, w_down)
+        b_partial = backward_rows(b_rows.reshape(-1, 2 * width), w_gate, w_up, w_down)
+        f_outs.append(from_group(f_partial.reshape(2, 2, capacity, width), d))
+        b_outs.append(from_group(b_partial.reshape(2, 2, capacity, width), d))
+    f_out = jnp.stack(f_outs)
+    b_out = jnp.stack(b_outs)
     high = lax.Precision.HIGHEST
     f_mixed = jnp.dot(
         f_weights, f_out.reshape(experts * capacity, width).astype(jnp.float32), precision=high

time: 321 us -> 392 us (1.22); the launches traced: 321 us -> 387 us
  matrix products: 19 us -> 94.9 us
  waiting for transfers between devices: 246 us -> 191 us
  other arithmetic: 19.1 us -> 40.2 us
  starting transfers between devices: 23.8 us -> 37.7 us
  local copies, waits for them, and re-layouts: 11.9 us -> 21.9 us
    ppermute x8 -> x32, waiting for transfers between devices: 122 us -> 81.4 us  [swap(): return lax.ppermute(value, axis, [(0, 1), (1, 0)])]
    dot_general x1 -> x4, matrix products: 1.63 us -> 30 us  [backward_rows(): lax.dot_general(grad_gate, w_gate, (((1,), (1,)), ((), ())), preferred_el...]
    dot_general x1 -> x4, matrix products: 1.61 us -> 21.2 us  [forward_rows(): jnp.dot(hidden, w_down, preferred_element_type=jnp.float32)]
    another operation x8 -> x20, other arithmetic: 10.8 us -> 30 us  [the longest x16 25.6 us: to_group(): return jnp.stack([across, swap(across, 'c')])]
    ppermute x12, waiting for transfers between devices: 116 us -> 98.3 us  [the longest x6 75.8 us: to_group(): lax.ppermute(chunk, 'z', [(i, i ^ d) for i in range(count)])]
    ppermute x8 -> x32, starting transfers between devices: 6.4 us -> 21.3 us  [swap(): return lax.ppermute(value, axis, [(0, 1), (1, 0)])]
    dot_general x1 -> x4, matrix products: 1.6 us -> 14.6 us  [backward_rows(): g = jnp.dot(rows_in, w_gate, preferred_element_type=jnp.float32)]
    dot_general x1 -> x4, matrix products: 3.9 us -> 16.6 us  [backward_rows(): lax.dot_general(grad_up, w_up, (((1,), (1,)), ((), ())), preferred_elemen...]
  transfers between devices with their start and end apart: 22 -> 46, of which waited for: 15 -> 17; matrix products, arithmetic and copies ran while one was open for 11% -> 37% of each run, Pallas kernels for 0% -> 0%
where the time goes in v4:
time: 392 us; the launch traced here: 387 us
  waiting for transfers between devices  191 us (49%)
  matrix products  94.9 us (24%)
  other arithmetic  40.2 us (10%)
  starting transfers between devices  37.7 us (10%)
  local copies, waits for them, and re-layouts  21.9 us (6%)
    ppermute x32, waiting for transfers between devices, swap(): return lax.ppermute(value, axis, [(0, 1), (1, 0)])  81.4 us
    ppermute x6, waiting for transfers between devices, to_group(): lax.ppermute(chunk, 'z', [(i, i ^ d) for i in range(count)])  75.8 us
    dot_general x4, matrix products, backward_rows(): lax.dot_general(grad_gate, w_gate, (((1,), (1,)), ((), ())), preferred_el...  30 us
    another operation x16, other arithmetic, to_group(): return jnp.stack([across, swap(across, 'c')])  25.6 us
    ppermute x6, waiting for transfers between devices, from_group(): return lax.ppermute(total, 'z', [(i, i ^ d) for i in range(count)])  22.5 us
    ppermute x32, starting transfers between devices, swap(): return lax.ppermute(value, axis, [(0, 1), (1, 0)])  21.3 us
    dot_general x4, matrix products, forward_rows(): jnp.dot(hidden, w_down, preferred_element_type=jnp.float32)  21.2 us
    dot_general x4, matrix products, backward_rows(): lax.dot_general(grad_up, w_up, (((1,), (1,)), ((), ())), preferred_elemen...  16.6 us
  transfers between devices with their start and end apart: 46, of which 17 were waited for; matrix products, arithmetic and copies ran while one was open for 37% of the time, Pallas kernels for 0%

profile of v4, /device:TPU:16, one launch (start us, length us, event | category | flops | bytes accessed | tf_op | source)
XLA Modules:
  0.0 387.2 jit_solution(6547407015742531543)
XLA Ops:
  2.1 1.4 convert_reduce_fusion.1
  3.5 1.6 convolution_convert_fusion.5
  5.2 1.5 collective-permute-start
  8.6 1.3 slice_bitcast_fusion.9
  10.4 1.6 collective-permute-start.27
  12.4 1.6 collective-permute-start.39
  13.9 2.3 collective-permute-done
  16.3 1.6 collective-permute-start.4
  17.9 46.3 %collective-permute-done.4 = bf16[24,7168]{1,0:T(8,128)(2,1)S(1)} collective-permute-done((bf16[24,7168]{1,0:T(8,128)(2,1)S(1)}, bf16[24,7168]{1,0:T(8,128)(2,1)S(1)}, u32[]{:S(2)}, u32[]{:S(2)}) %collective-permute-start.4) | collective-permute-done | bytes 344096 | tf_op jit(solution)/shard_map/ppermute | solution.py:72
  64.3 1.6 collective-permute-start.5
  66.0 1.7 fusion.266
  67.7 18.0 %collective-permute-done.10 = bf16[24,7168]{1,0:T(8,128)(2,1)S(1)} collective-permute-done((bf16[24,7168]{1,0:T(8,128)(2,1)S(1)}, bf16[24,7168]{1,0:T(8,128)(2,1)S(1)}, u32[]{:S(2)}, u32[]{:S(2)}) %collective-permute-start.10) | collective-permute-done | bytes 344096 | tf_op jit(solution)/shard_map/ppermute | solution.py:72
  85.7 2.6 collective-permute-start.16
  88.3 1.5 collective-permute-start.11
  90.8 11.5 %collective-permute-done.16 = bf16[24,7168]{1,0:T(8,128)(2,1)S(1)} collective-permute-done((bf16[24,7168]{1,0:T(8,128)(2,1)S(1)}, bf16[24,7168]{1,0:T(8,128)(2,1)S(1)}, u32[]{:S(2)}, u32[]{:S(2)}) %collective-permute-start.16) | collective-permute-done | bytes 344096 | tf_op jit(solution)/shard_map/ppermute | solution.py:72
  102.3 1.5 collective-permute-start.17
  104.9 7.8 %collective-permute-done.17 = bf16[24,7168]{1,0:T(8,128)(2,1)S(1)} collective-permute-done((bf16[24,7168]{1,0:T(8,128)(2,1)S(1)}, bf16[24,7168]{1,0:T(8,128)(2,1)S(1)}, u32[]{:S(2)}, u32[]{:S(2)}) %collective-permute-start.17) | collective-permute-done | bytes 344096 | tf_op jit(solution)/shard_map/ppermute | solution.py:13
  116.0 5.3 %convolution_convert_fusion.4 = bf16[96,7168]{1,0:T(8,128)(2,1)S(1)} fusion(bf16[1,256,7168]{2,1,0:T(8,128)(2,1)} %param.19, f32[96,256]{1,0:T(8,128)S(1)} %fusion.38, bf16[96,7168]{1,0:T(8,128)(2,1)S(1)} %bitcast.321, bf16[1,7168,256]{2,1,0:T(8,128)(2,1)} %param.17), kind=kOutput, calls=%fused_computation.12 | convolution fusion | flops 705478656 | bytes 10190848 | tf_op jit(solution)/shard_map/dot_general | solution.py:46
  125.0 5.3 %convolution_convert_fusion.3 = bf16[96,7168]{1,0:T(8,128)(2,1)S(1)} fusion(bf16[1,256,7168]{2,1,0:T(8,128)(2,1)} %param.19, f32[96,256]{1,0:T(8,128)S(1)} %fusion.36, bf16[96,7168]{1,0:T(8,128)(2,1)S(1)} %bitcast.323, bf16[1,7168,256]{2,1,0:T(8,128)(2,1)} %param.17), kind=kOutput, calls=%fused_computation.11 | convolution fusion | flops 705478656 | bytes 10190848 | tf_op jit(solution)/shard_map/dot_general | solution.py:46
  131.7 1.5 collective-permute-start.28
  133.7 1.5 collective-permute-start.40
  135.2 1.4 pad_maximum_fusion.6
  137.4 5.3 %convolution_convert_fusion.2 = bf16[96,7168]{1,0:T(8,128)(2,1)S(1)} fusion(bf16[1,256,7168]{2,1,0:T(8,128)(2,1)} %param.19, f32[96,256]{1,0:T(8,128)S(1)} %fusion.34, bf16[96,7168]{1,0:T(8,128)(2,1)S(1)} %bitcast.325, bf16[1,7168,256]{2,1,0:T(8,128)(2,1)} %param.17), kind=kOutput, calls=%fused_computation.10 | convolution fusion | flops 705478656 | bytes 10190848 | tf_op jit(solution)/shard_map/dot_general | solution.py:46
  143.9 6.4 %collective-permute-done.28 = bf16[24,14336]{1,0:T(8,128)(2,1)} collective-permute-done((bf16[24,14336]{1,0:T(8,128)(2,1)}, bf16[24,14336]{1,0:T(8,128)(2,1)}, u32[]{:S(2)}, u32[]{:S(2)}) %collective-permute-start.28) | collective-permute-done | bytes 688160 | tf_op jit(solution)/shard_map/ppermute | solution.py:13
  150.3 3.3 fusion.265
  153.6 11.4 %collective-permute-done.34 = bf16[24,14336]{1,0:T(8,128)(2,1)} collective-permute-done((bf16[24,14336]{1,0:T(8,128)(2,1)}, bf16[24,14336]{1,0:T(8,128)(2,1)}, u32[]{:S(2)}, u32[]{:S(2)}) %collective-permute-start.34) | collective-permute-done | bytes 688160 | tf_op jit(solution)/shard_map/ppermute | solution.py:13
  165.1 3.1 fusion.264
  168.2 10.8 %collective-permute-done.40 = bf16[24,14336]{1,0:T(8,128)(2,1)} collective-permute-done((bf16[24,14336]{1,0:T(8,128)(2,1)}, bf16[24,14336]{1,0:T(8,128)(2,1)}, u32[]{:S(2)}, u32[]{:S(2)}) %collective-permute-start.40) | collective-permute-done | bytes 688160 | tf_op jit(solution)/shard_map/ppermute | solution.py:13
  179.0 3.2 fusion.263
  184.7 5.3 %convolution_convert_fusion.1 = bf16[96,7168]{1,0:T(8,128)(2,1)S(1)} fusion(bf16[1,256,7168]{2,1,0:T(8,128)(2,1)} %param.19, f32[96,256]{1,0:T(8,128)S(1)} %fusion.32, bf16[96,7168]{1,0:T(8,128)(2,1)S(1)} %bitcast.327, bf16[1,7168,256]{2,1,0:T(8,128)(2,1)} %param.17), kind=kOutput, calls=%fused_computation.9 | convolution fusion | flops 705478656 | bytes 10190848 | tf_op jit(solution)/shard_map/dot_general | solution.py:46
  191.4 1.4 convert_add_fusion.7
  193.5 1.5 collective-permute-start.3
  195.1 1.7 pad_maximum_fusion
  199.6 1.4 fusion.54
  200.9 7.4 %fusion.52 = f32[96,7168]{1,0:T(8,128)} fusion(bf16[1,7168,256]{2,1,0:T(8,128)(2,1)} %param.17, f32[96,256]{1,0:T(8,128)S(1)} %fusion.14, bf16[1,7168,256]{2,1,0:T(8,128)(2,1)} %param.18, bf16[96,14336]{1,0:T(8,128)(2,1)S(1)} %bitcast.319, f32[96,256]{1,0:T(8,128)} %fusion.54), kind=kOutput, calls=%fused_computation.64 | convolution fusion | flops 704888832 | bytes 11665408 | tf_op jit(solution)/shard_map/dot_general | solution.py:61
  208.3 4.2 %fusion = bf16[96,7168]{1,0:T(8,128)(2,1)S(1)} fusion(f32[96,7168]{1,0:T(8,128)} %fusion.52, bf16[1,7168,256]{2,1,0:T(8,128)(2,1)} %param.18, f32[96,256]{1,0:T(8,128)S(1)} %fusion.14, f32[96,256]{1,0:T(8,128)} %fusion.54), kind=kOutput, calls=%fused_computation.5 | convolution fusion | flops 353845248 | bytes 7995392 | tf_op jit(solution)/shard_map/dot_general | solution.py:64
  214.0 1.8 fusion.192
  215.9 1.3 convert_add_fusion.6
  219.0 9.0 %collective-permute-done.8 = bf16[24,7168]{1,0:T(8,128)(2,1)S(1)} collective-permute-done((bf16[24,7168]{1,0:T(8,128)(2,1)S(1)}, bf16[24,7168]{1,0:T(8,128)(2,1)S(1)}, u32[]{:S(2)}, u32[]{:S(2)}) %collective-permute-start.8) | collective-permute-done | bytes 344096 | tf_op jit(solution)/shard_map/ppermute | solution.py:13
  229.5 7.7 %collective-permute-done.14 = bf16[24,7168]{1,0:T(8,128)(2,1)S(1)} collective-permute-done((bf16[24,7168]{1,0:T(8,128)(2,1)S(1)}, bf16[24,7168]{1,0:T(8,128)(2,1)S(1)}, u32[]{:S(2)}, u32[]{:S(2)}) %collective-permute-start.14) | collective-permute-done | bytes 344096 | tf_op jit(solution)/shard_map/ppermute | solution.py:13
  238.9 6.6 %collective-permute-done.20 = bf16[24,7168]{1,0:T(8,128)(2,1)S(1)} collective-permute-done((bf16[24,7168]{1,0:T(8,128)(2,1)S(1)}, bf16[24,7168]{1,0:T(8,128)(2,1)S(1)}, u32[]{:S(2)}, u32[]{:S(2)}) %collective-permute-start.20) | collective-permute-done | bytes 344096 | tf_op jit(solution)/shard_map/ppermute | solution.py:13
  246.3 1.9 collective-permute-start.15
  248.3 1.7 pad_maximum_fusion.1
  250.0 1.6 collective-permute-start.21
  251.6 1.7 pad_maximum_fusion.2
  258.1 11.0 %fusion.46 = f32[96,256]{1,0:T(8,128)} fusion(bf16[1,7168,256]{2,1,0:T(8,128)(2,1)S(1)} %copy-done.1, bf16[96,14336]{1,0:T(8,128)(2,1)S(1)} %bitcast.309), kind=kOutput, calls=%fused_computation.58 | convolution fusion | flops 352321536 | bytes 5144576 | tf_op jit(solution)/shard_map/dot_general | solution.py:53
  269.2 1.6 pad_maximum_fusion.3
  270.8 1.5 fusion.42
  272.3 1.9 fusion.8
  277.3 7.8 %fusion.48 = f32[96,7168]{1,0:T(8,128)} fusion(bf16[1,7168,256]{2,1,0:T(8,128)(2,1)} %param.17, f32[96,256]{1,0:T(8,128)S(1)} %fusion.12, bf16[1,7168,256]{2,1,0:T(8,128)(2,1)} %param.18, bf16[96,14336]{1,0:T(8,128)(2,1)} %bitcast.313, f32[96,256]{1,0:T(8,128)S(1)} %fusion.50), kind=kOutput, calls=%fused_computation.60 | convolution fusion | flops 704888832 | bytes 11665408 | tf_op jit(solution)/shard_map/dot_general | solution.py:61
  285.1 4.1 %fusion.1 = bf16[96,7168]{1,0:T(8,128)(2,1)S(1)} fusion(f32[96,7168]{1,0:T(8,128)} %fusion.48, bf16[1,7168,256]{2,1,0:T(8,128)(2,1)} %param.18, f32[96,256]{1,0:T(8,128)S(1)} %fusion.12, f32[96,256]{1,0:T(8,128)S(1)} %fusion.50), kind=kOutput, calls=%fused_computation.6 | convolution fusion | flops 353845248 | bytes 7995392 | tf_op jit(solution)/shard_map/dot_general | solution.py:64
  290.2 7.4 %fusion.44 = f32[96,7168]{1,0:T(8,128)} fusion(bf16[1,7168,256]{2,1,0:T(8,128)(2,1)} %param.17, f32[96,256]{1,0:T(8,128)S(1)} %fusion.10, bf16[1,7168,256]{2,1,0:T(8,128)(2,1)} %param.18, bf16[96,14336]{1,0:T(8,128)(2,1)S(1)} %bitcast.310, f32[96,256]{1,0:T(8,128)} %fusion.46), kind=kOutput, calls=%fused_computation.56 | convolution fusion | flops 704888832 | bytes 11665408 | tf_op jit(solution)/shard_map/dot_general | solution.py:61
  297.6 4.2 %fusion.2 = bf16[96,7168]{1,0:T(8,128)(2,1)S(1)} fusion(f32[96,7168]{1,0:T(8,128)} %fusion.44, bf16[1,7168,256]{2,1,0:T(8,128)(2,1)} %param.18, f32[96,256]{1,0:T(8,128)S(1)} %fusion.10, f32[96,256]{1,0:T(8,128)} %fusion.46), kind=kOutput, calls=%fused_computation.7 | convolution fusion | flops 353845248 | bytes 7995392 | tf_op jit(solution)/shard_map/dot_general | solution.py:64
  304.1 7.4 %fusion.40 = f32[96,7168]{1,0:T(8,128)} fusion(bf16[1,7168,256]{2,1,0:T(8,128)(2,1)} %param.17, f32[96,256]{1,0:T(8,128)} %fusion.8, bf16[1,7168,256]{2,1,0:T(8,128)(2,1)} %param.18, bf16[96,14336]{1,0:T(8,128)(2,1)S(1)} %bitcast.316, f32[96,256]{1,0:T(8,128)} %fusion.42), kind=kOutput, calls=%fused_computation.52 | convolution fusion | flops 704888832 | bytes 11665408 | tf_op jit(solution)/shard_map/dot_general | solution.py:61
  311.5 4.2 %fusion.3 = bf16[96,7168]{1,0:T(8,128)(2,1)S(1)} fusion(f32[96,7168]{1,0:T(8,128)} %fusion.40, bf16[1,7168,256]{2,1,0:T(8,128)(2,1)} %param.18, f32[96,256]{1,0:T(8,128)} %fusion.8, f32[96,256]{1,0:T(8,128)S(1)} %copy-done.28), kind=kOutput, calls=%fused_computation.8 | convolution fusion | flops 353845248 | bytes 7995392 | tf_op jit(solution)/shard_map/dot_general | solution.py:64
  317.3 1.4 pad_maximum_fusion.8
  319.4 1.5 collective-permute-start.22
  321.0 1.3 convert_add_fusion.2
  325.9 7.3 %collective-permute-done.31 = bf16[24,7168]{1,0:T(8,128)(2,1)S(1)} collective-permute-done((bf16[24,7168]{1,0:T(8,128)(2,1)S(1)}, bf16[24,7168]{1,0:T(8,128)(2,1)S(1)}, u32[]{:S(2)}, u32[]{:S(2)}) %collective-permute-start.31) | collective-permute-done | bytes 344096 | tf_op jit(solution)/shard_map/ppermute | solution.py:13
  334.4 6.3 %collective-permute-done.37 = bf16[24,7168]{1,0:T(8,128)(2,1)S(1)} collective-permute-done((bf16[24,7168]{1,0:T(8,128)(2,1)S(1)}, bf16[24,7168]{1,0:T(8,128)(2,1)S(1)}, u32[]{:S(2)}, u32[]{:S(2)}) %collective-permute-start.37) | collective-permute-done | bytes 344096 | tf_op jit(solution)/shard_map/ppermute | solution.py:13
  341.7 5.6 %collective-permute-done.43 = bf16[24,7168]{1,0:T(8,128)(2,1)S(1)} collective-permute-done((bf16[24,7168]{1,0:T(8,128)(2,1)S(1)}, bf16[24,7168]{1,0:T(8,128)(2,1)S(1)}, u32[]{:S(2)}, u32[]{:S(2)}) %collective-permute-start.43) | collective-permute-done | bytes 344096 | tf_op jit(solution)/shard_map/ppermute | solution.py:13
  349.4 14.3 %collective-permute-done.38 = bf16[24,7168]{1,0:T(8,128)(2,1)S(1)} collective-permute-done((bf16[24,7168]{1,0:T(8,128)(2,1)S(1)}, bf16[24,7168]{1,0:T(8,128)(2,1)S(1)}, u32[]{:S(2)}, u32[]{:S(2)}) %collective-permute-start.38) | collective-permute-done | bytes 344096 | tf_op jit(solution)/shard_map/ppermute | solution.py:85
  363.7 8.2 %collective-permute-done.44 = bf16[24,7168]{1,0:T(8,128)(2,1)S(1)} collective-permute-done((bf16[24,7168]{1,0:T(8,128)(2,1)S(1)}, bf16[24,7168]{1,0:T(8,128)(2,1)S(1)}, u32[]{:S(2)}, u32[]{:S(2)}) %collective-permute-start.44) | collective-permute-done | bytes 344096 | tf_op jit(solution)/shard_map/ppermute | solution.py:85
  374.2 11.3 %collective-permute-done.45 = bf16[1,32,7168]{2,1,0:T(8,128)(2,1)S(1)} collective-permute-done((bf16[1,32,7168]{2,1,0:T(8,128)(2,1)S(1)}, bf16[1,32,7168]{2,1,0:T(8,128)(2,1)S(1)}, u32[]{:S(2)}, u32[]{:S(2)}) %collective-permute-start.45) | collective-permute-done | bytes 458784 | tf_op jit(solution)/shard_map/ppermute | solution.py:19
  (199 shorter events, 57.0 us)
Async XLA Ops:
  5.0 2.5 copy-start.34
  5.0 2.6 copy-start.25
  5.1 2.6 copy-start.32
  5.2 11.0 %collective-permute-start = (bf16[24,7168]{1,0:T(8,128)(2,1)S(1)}, bf16[24,7168]{1,0:T(8,128)(2,1)S(1)}, u32[]{:S(2)}, u32[]{:S(2)}) collective-permute-start(bf16[24,7168]{1,0:T(8,128)(2,1)S(1)} %get-tuple-element.33), channel_id=1, source_target_pairs={{0,2},{2,0},{1,3},{3,1},{4,6},{6,4},{5,7},{7,5},{8,10},{10,8},{9,1... | collective-permute-start | bytes 1032200 | tf_op jit(solution)/shard_map/ppermute | solution.py:13
  9.9 54.4 %collective-permute-start.23 = (bf16[24,14336]{1,0:T(8,128)(2,1)S(1)}, bf16[24,14336]{1,0:T(8,128)(2,1)S(1)}, u32[]{:S(2)}, u32[]{:S(2)}) collective-permute-start(bf16[24,14336]{1,0:T(8,128)(2,1)S(1)} %get-tuple-element.10), channel_id=1, source_target_pairs={{0,2},{2,0},{1,3},{3,1},{4,6},{6,4},{5,7},{7,5},{8,10},{10,8},{9,1... | collective-permute-start | bytes 2064392 | tf_op jit(solution)/shard_map/ppermute | solution.py:13
  10.4 120.8 %collective-permute-start.27 = (bf16[24,14336]{1,0:T(8,128)(2,1)}, bf16[24,14336]{1,0:T(8,128)(2,1)}, u32[]{:S(2)}, u32[]{:S(2)}) collective-permute-start(bf16[24,14336]{1,0:T(8,128)(2,1)} %get-tuple-element.9), channel_id=1, source_target_pairs={{0,4},{4,0},{8,12},{12,8},{1,5},{5,1},{9,13},{13,9},{2,6},{6,2},{1... | collective-permute-start | bytes 2064392 | tf_op jit(solution)/shard_map/ppermute | solution.py:72
  12.0 119.7 %collective-permute-start.33 = (bf16[24,14336]{1,0:T(8,128)(2,1)}, bf16[24,14336]{1,0:T(8,128)(2,1)}, u32[]{:S(2)}, u32[]{:S(2)}) collective-permute-start(bf16[24,14336]{1,0:T(8,128)(2,1)} %get-tuple-element.8), channel_id=1, source_target_pairs={{0,8},{4,12},{8,0},{12,4},{1,9},{5,13},{9,1},{13,5},{2,10},{6,14},... | collective-permute-start | bytes 2064392 | tf_op jit(solution)/shard_map/ppermute | solution.py:72
  12.4 120.8 %collective-permute-start.39 = (bf16[24,14336]{1,0:T(8,128)(2,1)}, bf16[24,14336]{1,0:T(8,128)(2,1)}, u32[]{:S(2)}, u32[]{:S(2)}) collective-permute-start(bf16[24,14336]{1,0:T(8,128)(2,1)} %get-tuple-element.7), channel_id=1, source_target_pairs={{0,12},{4,8},{8,4},{12,0},{1,13},{5,9},{9,5},{13,1},{2,14},{6,10},... | collective-permute-start | bytes 2064392 | tf_op jit(solution)/shard_map/ppermute | solution.py:72
  16.3 48.0 %collective-permute-start.4 = (bf16[24,7168]{1,0:T(8,128)(2,1)S(1)}, bf16[24,7168]{1,0:T(8,128)(2,1)S(1)}, u32[]{:S(2)}, u32[]{:S(2)}) collective-permute-start(bf16[24,7168]{1,0:T(8,128)(2,1)S(1)} %get-tuple-element.32), channel_id=1, source_target_pairs={{0,4},{4,0},{8,12},{12,8},{1,5},{5,1},{9,13},{13,9},{2,6},{6,2},{1... | collective-permute-start | bytes 1032200 | tf_op jit(solution)/shard_map/ppermute | solution.py:72
  64.2 21.4 %collective-permute-start.10 = (bf16[24,7168]{1,0:T(8,128)(2,1)S(1)}, bf16[24,7168]{1,0:T(8,128)(2,1)S(1)}, u32[]{:S(2)}, u32[]{:S(2)}) collective-permute-start(bf16[24,7168]{1,0:T(8,128)(2,1)S(1)} %get-tuple-element.31), channel_id=1, source_target_pairs={{0,8},{4,12},{8,0},{12,4},{1,9},{5,13},{9,1},{13,5},{2,10},{6,14},... | collective-permute-start | bytes 1032200 | tf_op jit(solution)/shard_map/ppermute | solution.py:72
  64.3 24.0 %collective-permute-start.5 = (bf16[24,7168]{1,0:T(8,128)(2,1)S(1)}, bf16[24,7168]{1,0:T(8,128)(2,1)S(1)}, u32[]{:S(2)}, u32[]{:S(2)}) collective-permute-start(bf16[24,7168]{1,0:T(8,128)(2,1)S(1)} %collective-permute-done.4), channel_id=1, source_target_pairs={{0,2},{2,0},{1,3},{3,1},{4,6},{6,4},{5,7},{7,5},{8,10},{10,8},{9,1... | collective-permute-start | bytes 1032200 | tf_op jit(solution)/shard_map/ppermute | solution.py:13
  85.7 16.6 %collective-permute-start.16 = (bf16[24,7168]{1,0:T(8,128)(2,1)S(1)}, bf16[24,7168]{1,0:T(8,128)(2,1)S(1)}, u32[]{:S(2)}, u32[]{:S(2)}) collective-permute-start(bf16[24,7168]{1,0:T(8,128)(2,1)S(1)} %get-tuple-element.30), channel_id=1, source_target_pairs={{0,12},{4,8},{8,4},{12,0},{1,13},{5,9},{9,5},{13,1},{2,14},{6,10},... | collective-permute-start | bytes 1032200 | tf_op jit(solution)/shard_map/ppermute | solution.py:72
  88.3 14.0 %collective-permute-start.11 = (bf16[24,7168]{1,0:T(8,128)(2,1)S(1)}, bf16[24,7168]{1,0:T(8,128)(2,1)S(1)}, u32[]{:S(2)}, u32[]{:S(2)}) collective-permute-start(bf16[24,7168]{1,0:T(8,128)(2,1)S(1)} %collective-permute-done.10), channel_id=1, source_target_pairs={{0,2},{2,0},{1,3},{3,1},{4,6},{6,4},{5,7},{7,5},{8,10},{10,8},{9,1... | collective-permute-start | bytes 1032200 | tf_op jit(solution)/shard_map/ppermute | solution.py:13
  102.3 11.7 %collective-permute-start.1 = (bf16[2,24,7168]{2,1,0:T(8,128)(2,1)S(1)}, bf16[2,24,7168]{2,1,0:T(8,128)(2,1)S(1)}, u32[]{:S(2)}, u32[]{:S(2)}) collective-permute-start(bf16[2,24,7168]{2,1,0:T(8,128)(2,1)S(1)} %get-tuple-element.41), channel_id=1, source_target_pairs={{0,1},{1,0},{2,3},{3,2},{4,5},{5,4},{6,7},{7,6},{8,9},{9,8},{10,11... | collective-permute-start | bytes 2064392 | tf_op jit(solution)/shard_map/ppermute | solution.py:13
  102.3 10.5 %collective-permute-start.17 = (bf16[24,7168]{1,0:T(8,128)(2,1)S(1)}, bf16[24,7168]{1,0:T(8,128)(2,1)S(1)}, u32[]{:S(2)}, u32[]{:S(2)}) collective-permute-start(bf16[24,7168]{1,0:T(8,128)(2,1)S(1)} %collective-permute-done.16), channel_id=1, source_target_pairs={{0,2},{2,0},{1,3},{3,1},{4,6},{6,4},{5,7},{7,5},{8,10},{10,8},{9,1... | collective-permute-start | bytes 1032200 | tf_op jit(solution)/shard_map/ppermute | solution.py:13
  112.7 80.8 %collective-permute-start.24 = (bf16[2,24,14336]{2,1,0:T(8,128)(2,1)}, bf16[2,24,14336]{2,1,0:T(8,128)(2,1)}, u32[]{:S(2)}, u32[]{:S(2)}) collective-permute-start(bf16[2,24,14336]{2,1,0:T(8,128)(2,1)} %get-tuple-element.14), channel_id=1, source_target_pairs={{0,1},{1,0},{2,3},{3,2},{4,5},{5,4},{6,7},{7,6},{8,9},{9,8},{10,11... | collective-permute-start | bytes 4128776 | tf_op jit(solution)/shard_map/ppermute | solution.py:13
  112.7 2.5 copy-start.2
  114.0 8.5 %collective-permute-start.6 = (bf16[2,24,7168]{2,1,0:T(8,128)(2,1)}, bf16[2,24,7168]{2,1,0:T(8,128)(2,1)}, u32[]{:S(2)}, u32[]{:S(2)}) collective-permute-start(bf16[2,24,7168]{2,1,0:T(8,128)(2,1)} %get-tuple-element.43), channel_id=1, source_target_pairs={{0,1},{1,0},{2,3},{3,2},{4,5},{5,4},{6,7},{7,6},{8,9},{9,8},{10,11... | collective-permute-start | bytes 2064392 | tf_op jit(solution)/shard_map/ppermute | solution.py:13
  121.3 2.9 copy-start.3
  122.5 11.2 %collective-permute-start.12 = (bf16[2,24,7168]{2,1,0:T(8,128)(2,1)}, bf16[2,24,7168]{2,1,0:T(8,128)(2,1)}, u32[]{:S(2)}, u32[]{:S(2)}) collective-permute-start(bf16[2,24,7168]{2,1,0:T(8,128)(2,1)} %get-tuple-element.45), channel_id=1, source_target_pairs={{0,1},{1,0},{2,3},{3,2},{4,5},{5,4},{6,7},{7,6},{8,9},{9,8},{10,11... | collective-permute-start | bytes 2064392 | tf_op jit(solution)/shard_map/ppermute | solution.py:13
  130.3 6.4 %copy-start.4 = (bf16[1,7168,256]{2,1,0:T(8,128)(2,1)S(1)}, bf16[1,7168,256]{2,1,0:T(8,128)(2,1)}, u32[]{:S(2)}) copy-start(bf16[1,7168,256]{2,1,0:T(8,128)(2,1)} %param.18) | copy-start | bytes 11010052
  131.3 50.9 %collective-permute-start.18 = (bf16[2,24,7168]{2,1,0:T(8,128)(2,1)}, bf16[2,24,7168]{2,1,0:T(8,128)(2,1)}, u32[]{:S(2)}, u32[]{:S(2)}) collective-permute-start(bf16[2,24,7168]{2,1,0:T(8,128)(2,1)} %get-tuple-element.47), channel_id=1, source_target_pairs={{0,1},{1,0},{2,3},{3,2},{4,5},{5,4},{6,7},{7,6},{8,9},{9,8},{10,11... | collective-permute-start | bytes 2064392 | tf_op jit(solution)/shard_map/ppermute | solution.py:13
  131.7 18.6 %collective-permute-start.28 = (bf16[24,14336]{1,0:T(8,128)(2,1)}, bf16[24,14336]{1,0:T(8,128)(2,1)}, u32[]{:S(2)}, u32[]{:S(2)}) collective-permute-start(bf16[24,14336]{1,0:T(8,128)(2,1)} %collective-permute-done.27), channel_id=1, source_target_pairs={{0,2},{2,0},{1,3},{3,1},{4,6},{6,4},{5,7},{7,5},{8,10},{10,8},{9,1... | collective-permute-start | bytes 2064392 | tf_op jit(solution)/shard_map/ppermute | solution.py:13
  133.2 31.8 %collective-permute-start.34 = (bf16[24,14336]{1,0:T(8,128)(2,1)}, bf16[24,14336]{1,0:T(8,128)(2,1)}, u32[]{:S(2)}, u32[]{:S(2)}) collective-permute-start(bf16[24,14336]{1,0:T(8,128)(2,1)} %collective-permute-done.33), channel_id=1, source_target_pairs={{0,2},{2,0},{1,3},{3,1},{4,6},{6,4},{5,7},{7,5},{8,10},{10,8},{9,1... | collective-permute-start | bytes 2064392 | tf_op jit(solution)/shard_map/ppermute | solution.py:13
  133.7 45.2 %collective-permute-start.40 = (bf16[24,14336]{1,0:T(8,128)(2,1)}, bf16[24,14336]{1,0:T(8,128)(2,1)}, u32[]{:S(2)}, u32[]{:S(2)}) collective-permute-start(bf16[24,14336]{1,0:T(8,128)(2,1)} %collective-permute-done.39), channel_id=1, source_target_pairs={{0,2},{2,0},{1,3},{3,1},{4,6},{6,4},{5,7},{7,5},{8,10},{10,8},{9,1... | collective-permute-start | bytes 2064392 | tf_op jit(solution)/shard_map/ppermute | solution.py:13
  150.3 40.9 %collective-permute-start.2 = (bf16[2,24,7168]{2,1,0:T(8,128)(2,1)}, bf16[2,24,7168]{2,1,0:T(8,128)(2,1)}, u32[]{:S(2)}, u32[]{:S(2)}) collective-permute-start(bf16[2,24,7168]{2,1,0:T(8,128)(2,1)} %bitcast.12), channel_id=1, source_target_pairs={{0,1},{1,0},{2,3},{3,2},{4,5},{5,4},{6,7},{7,6},{8,9},{9,8},{10,11... | collective-permute-start | bytes 2064392 | tf_op jit(solution)/shard_map/ppermute | solution.py:13
  165.0 81.3 %collective-permute-start.29 = (bf16[2,24,14336]{2,1,0:T(8,128)(2,1)}, bf16[2,24,14336]{2,1,0:T(8,128)(2,1)}, u32[]{:S(2)}, u32[]{:S(2)}) collective-permute-start(bf16[2,24,14336]{2,1,0:T(8,128)(2,1)} %get-tuple-element.18), channel_id=1, source_target_pairs={{0,1},{1,0},{2,3},{3,2},{4,5},{5,4},{6,7},{7,6},{8,9},{9,8},{10,11... | collective-permute-start | bytes 4128776 | tf_op jit(solution)/shard_map/ppermute | solution.py:13
  165.1 17.7 %copy-start.19 = (bf16[1,2,24,7168]{3,2,1,0:T(8,128)(2,1)S(1)}, bf16[1,2,24,7168]{3,2,1,0:T(8,128)(2,1)}, u32[]{:S(2)}) copy-start(bf16[1,2,24,7168]{3,2,1,0:T(8,128)(2,1)} %get-tuple-element.46) | copy-start | bytes 2064388
  179.0 71.0 %collective-permute-start.35 = (bf16[2,24,14336]{2,1,0:T(8,128)(2,1)}, bf16[2,24,14336]{2,1,0:T(8,128)(2,1)}, u32[]{:S(2)}, u32[]{:S(2)}) collective-permute-start(bf16[2,24,14336]{2,1,0:T(8,128)(2,1)} %get-tuple-element.22), channel_id=1, source_target_pairs={{0,1},{1,0},{2,3},{3,2},{4,5},{5,4},{6,7},{7,6},{8,9},{9,8},{10,11... | collective-permute-start | bytes 4128776 | tf_op jit(solution)/shard_map/ppermute | solution.py:13
  179.0 5.0 %copy-start.5 = (bf16[1,7168,256]{2,1,0:T(8,128)(2,1)S(1)}, bf16[1,7168,256]{2,1,0:T(8,128)(2,1)}, u32[]{:S(2)}) copy-start(bf16[1,7168,256]{2,1,0:T(8,128)(2,1)} %param.18) | copy-start | bytes 11010052
  182.2 87.0 %collective-permute-start.41 = (bf16[2,24,14336]{2,1,0:T(8,128)(2,1)}, bf16[2,24,14336]{2,1,0:T(8,128)(2,1)}, u32[]{:S(2)}, u32[]{:S(2)}) collective-permute-start(bf16[2,24,14336]{2,1,0:T(8,128)(2,1)} %get-tuple-element.26), channel_id=1, source_target_pairs={{0,1},{1,0},{2,3},{3,2},{4,5},{5,4},{6,7},{7,6},{8,9},{9,8},{10,11... | collective-permute-start | bytes 4128776 | tf_op jit(solution)/shard_map/ppermute | solution.py:13
  191.2 24.6 %collective-permute-start.7 = (bf16[2,24,7168]{2,1,0:T(8,128)(2,1)}, bf16[2,24,7168]{2,1,0:T(8,128)(2,1)}, u32[]{:S(2)}, u32[]{:S(2)}) collective-permute-start(bf16[2,24,7168]{2,1,0:T(8,128)(2,1)} %bitcast.22), channel_id=1, source_target_pairs={{0,1},{1,0},{2,3},{3,2},{4,5},{5,4},{6,7},{7,6},{8,9},{9,8},{10,11... | collective-permute-start | bytes 2064392 | tf_op jit(solution)/shard_map/ppermute | solution.py:13
  191.4 3.7 copy-start.11
  193.5 19.0 %collective-permute-start.3 = (bf16[24,7168]{1,0:T(8,128)(2,1)}, bf16[24,7168]{1,0:T(8,128)(2,1)}, u32[]{:S(2)}, u32[]{:S(2)}) collective-permute-start(bf16[24,7168]{1,0:T(8,128)(2,1)} %fusion.193), channel_id=1, source_target_pairs={{0,2},{2,0},{1,3},{3,1},{4,6},{6,4},{5,7},{7,5},{8,10},{10,8},{9,1... | collective-permute-start | bytes 1032200 | tf_op jit(solution)/shard_map/ppermute | solution.py:13
  195.1 2.5 copy-start.6
  212.6 3.2 copy-start.30
  213.6 3.7 collective-permute-start.13
  215.8 2.1 collective-permute-start.19
  217.2 57.0 %collective-permute-start.25 = (bf16[2,24,7168]{2,1,0:T(8,128)(2,1)S(1)}, bf16[2,24,7168]{2,1,0:T(8,128)(2,1)S(1)}, u32[]{:S(2)}, u32[]{:S(2)}) collective-permute-start(bf16[2,24,7168]{2,1,0:T(8,128)(2,1)S(1)} %bitcast.339), channel_id=1, source_target_pairs={{0,1},{1,0},{2,3},{3,2},{4,5},{5,4},{6,7},{7,6},{8,9},{9,8},{10,11... | collective-permute-start | bytes 2064392 | tf_op jit(solution)/shard_map/ppermute | solution.py:13
  218.0 10.1 %collective-permute-start.8 = (bf16[24,7168]{1,0:T(8,128)(2,1)S(1)}, bf16[24,7168]{1,0:T(8,128)(2,1)S(1)}, u32[]{:S(2)}, u32[]{:S(2)}) collective-permute-start(bf16[24,7168]{1,0:T(8,128)(2,1)S(1)} %fusion.194), channel_id=1, source_target_pairs={{0,2},{2,0},{1,3},{3,1},{4,6},{6,4},{5,7},{7,5},{8,10},{10,8},{9,1... | collective-permute-start | bytes 1032200 | tf_op jit(solution)/shard_map/ppermute | solution.py:13
  228.1 9.2 %collective-permute-start.14 = (bf16[24,7168]{1,0:T(8,128)(2,1)S(1)}, bf16[24,7168]{1,0:T(8,128)(2,1)S(1)}, u32[]{:S(2)}, u32[]{:S(2)}) collective-permute-start(bf16[24,7168]{1,0:T(8,128)(2,1)S(1)} %fusion.195), channel_id=1, source_target_pairs={{0,2},{2,0},{1,3},{3,1},{4,6},{6,4},{5,7},{7,5},{8,10},{10,8},{9,1... | collective-permute-start | bytes 1032200 | tf_op jit(solution)/shard_map/ppermute | solution.py:13
  229.5 18.7 %copy-start.12 = (bf16[1,2,24,14336]{3,2,1,0:T(8,128)(2,1)S(1)}, bf16[1,2,24,14336]{3,2,1,0:T(8,128)(2,1)}, u32[]{:S(2)}) copy-start(bf16[1,2,24,14336]{3,2,1,0:T(8,128)(2,1)} %get-tuple-element.17) | copy-start | bytes 4128772
  237.3 8.3 %collective-permute-start.20 = (bf16[24,7168]{1,0:T(8,128)(2,1)S(1)}, bf16[24,7168]{1,0:T(8,128)(2,1)S(1)}, u32[]{:S(2)}, u32[]{:S(2)}) collective-permute-start(bf16[24,7168]{1,0:T(8,128)(2,1)S(1)} %fusion.196), channel_id=1, source_target_pairs={{0,2},{2,0},{1,3},{3,1},{4,6},{6,4},{5,7},{7,5},{8,10},{10,8},{9,1... | collective-permute-start | bytes 1032200 | tf_op jit(solution)/shard_map/ppermute | solution.py:13
  245.5 70.2 %collective-permute-start.9 = (bf16[24,7168]{1,0:T(8,128)(2,1)}, bf16[24,7168]{1,0:T(8,128)(2,1)}, u32[]{:S(2)}, u32[]{:S(2)}) collective-permute-start(bf16[24,7168]{1,0:T(8,128)(2,1)} %fusion.188), channel_id=1, source_target_pairs={{0,4},{4,0},{8,12},{12,8},{1,5},{5,1},{9,13},{13,9},{2,6},{6,2},{1... | collective-permute-start | bytes 1032200 | tf_op jit(solution)/shard_map/ppermute | solution.py:85
  246.3 70.9 %collective-permute-start.15 = (bf16[24,7168]{1,0:T(8,128)(2,1)}, bf16[24,7168]{1,0:T(8,128)(2,1)}, u32[]{:S(2)}, u32[]{:S(2)}) collective-permute-start(bf16[24,7168]{1,0:T(8,128)(2,1)} %fusion.186), channel_id=1, source_target_pairs={{0,8},{4,12},{8,0},{12,4},{1,9},{5,13},{9,1},{13,5},{2,10},{6,14},... | collective-permute-start | bytes 1032200 | tf_op jit(solution)/shard_map/ppermute | solution.py:85
  248.3 3.4 copy-start.13
  250.0 5.4 %copy-start.8 = (bf16[2,2,24,14336]{3,2,1,0:T(8,128)(2,1)}, bf16[2,2,24,14336]{3,2,1,0:T(8,128)(2,1)S(1)}, u32[]{:S(2)}) copy-start(bf16[2,2,24,14336]{3,2,1,0:T(8,128)(2,1)S(1)} %pad_maximum_fusion.1) | copy-start | bytes 8257540
  250.0 67.3 %collective-permute-start.21 = (bf16[24,7168]{1,0:T(8,128)(2,1)}, bf16[24,7168]{1,0:T(8,128)(2,1)}, u32[]{:S(2)}, u32[]{:S(2)}) collective-permute-start(bf16[24,7168]{1,0:T(8,128)(2,1)} %fusion.184), channel_id=1, source_target_pairs={{0,12},{4,8},{8,4},{12,0},{1,13},{5,9},{9,5},{13,1},{2,14},{6,10},... | collective-permute-start | bytes 1032200 | tf_op jit(solution)/shard_map/ppermute | solution.py:85
  251.6 2.5 copy-start.7
  258.1 11.0 %copy-start.14 = (bf16[1,2,24,14336]{3,2,1,0:T(8,128)(2,1)S(1)}, bf16[1,2,24,14336]{3,2,1,0:T(8,128)(2,1)}, u32[]{:S(2)}) copy-start(bf16[1,2,24,14336]{3,2,1,0:T(8,128)(2,1)} %get-tuple-element.25) | copy-start | bytes 4128772
  276.2 72.1 %collective-permute-start.26 = (bf16[24,7168]{1,0:T(8,128)(2,1)}, bf16[24,7168]{1,0:T(8,128)(2,1)}, u32[]{:S(2)}, u32[]{:S(2)}) collective-permute-start(bf16[24,7168]{1,0:T(8,128)(2,1)} %fusion.198), channel_id=1, source_target_pairs={{0,2},{2,0},{1,3},{3,1},{4,6},{6,4},{5,7},{7,5},{8,10},{10,8},{9,1... | collective-permute-start | bytes 1032200 | tf_op jit(solution)/shard_map/ppermute | solution.py:13
  290.2 30.8 %collective-permute-start.30 = (bf16[2,24,7168]{2,1,0:T(8,128)(2,1)}, bf16[2,24,7168]{2,1,0:T(8,128)(2,1)}, u32[]{:S(2)}, u32[]{:S(2)}) collective-permute-start(bf16[2,24,7168]{2,1,0:T(8,128)(2,1)} %bitcast.68), channel_id=1, source_target_pairs={{0,1},{1,0},{2,3},{3,2},{4,5},{5,4},{6,7},{7,6},{8,9},{9,8},{10,11... | collective-permute-start | bytes 2064392 | tf_op jit(solution)/shard_map/ppermute | solution.py:13
  304.1 7.4 %copy-start.28 = (f32[96,256]{1,0:T(8,128)S(1)}, f32[96,256]{1,0:T(8,128)}, u32[]{:S(2)}) copy-start(f32[96,256]{1,0:T(8,128)} %fusion.42) | copy-start | bytes 294916
  316.8 6.6 %collective-permute-start.36 = (bf16[2,24,7168]{2,1,0:T(8,128)(2,1)S(1)}, bf16[2,24,7168]{2,1,0:T(8,128)(2,1)S(1)}, u32[]{:S(2)}, u32[]{:S(2)}) collective-permute-start(bf16[2,24,7168]{2,1,0:T(8,128)(2,1)S(1)} %bitcast.343), channel_id=1, source_target_pairs={{0,1},{1,0},{2,3},{3,2},{4,5},{5,4},{6,7},{7,6},{8,9},{9,8},{10,11... | collective-permute-start | bytes 2064392 | tf_op jit(solution)/shard_map/ppermute | solution.py:13
  317.3 7.4 %collective-permute-start.42 = (bf16[2,24,7168]{2,1,0:T(8,128)(2,1)S(1)}, bf16[2,24,7168]{2,1,0:T(8,128)(2,1)S(1)}, u32[]{:S(2)}, u32[]{:S(2)}) collective-permute-start(bf16[2,24,7168]{2,1,0:T(8,128)(2,1)S(1)} %bitcast.342), channel_id=1, source_target_pairs={{0,1},{1,0},{2,3},{3,2},{4,5},{5,4},{6,7},{7,6},{8,9},{9,8},{10,11... | collective-permute-start | bytes 2064392 | tf_op jit(solution)/shard_map/ppermute | solution.py:13
  319.4 54.8 %collective-permute-start.22 = (bf16[1,32,7168]{2,1,0:T(8,128)(2,1)S(1)}, bf16[1,32,7168]{2,1,0:T(8,128)(2,1)S(1)}, u32[]{:S(2)}, u32[]{:S(2)}) collective-permute-start(bf16[1,32,7168]{2,1,0:T(8,128)(2,1)S(1)} %fusion.7), channel_id=1, source_target_pairs={{0,16},{16,0},{1,17},{17,1},{2,18},{18,2},{3,19},{19,3},{4,20},{20... | collective-permute-start | bytes 1376264 | tf_op jit(solution)/shard_map/ppermute | solution.py:19
  322.3 11.0 %collective-permute-start.31 = (bf16[24,7168]{1,0:T(8,128)(2,1)S(1)}, bf16[24,7168]{1,0:T(8,128)(2,1)S(1)}, u32[]{:S(2)}, u32[]{:S(2)}) collective-permute-start(bf16[24,7168]{1,0:T(8,128)(2,1)S(1)} %fusion.199), channel_id=1, source_target_pairs={{0,2},{2,0},{1,3},{3,1},{4,6},{6,4},{5,7},{7,5},{8,10},{10,8},{9,1... | collective-permute-start | bytes 1032200 | tf_op jit(solution)/shard_map/ppermute | solution.py:13
  323.6 17.1 %collective-permute-start.37 = (bf16[24,7168]{1,0:T(8,128)(2,1)S(1)}, bf16[24,7168]{1,0:T(8,128)(2,1)S(1)}, u32[]{:S(2)}, u32[]{:S(2)}) collective-permute-start(bf16[24,7168]{1,0:T(8,128)(2,1)S(1)} %fusion.200), channel_id=1, source_target_pairs={{0,2},{2,0},{1,3},{3,1},{4,6},{6,4},{5,7},{7,5},{8,10},{10,8},{9,1... | collective-permute-start | bytes 1032200 | tf_op jit(solution)/shard_map/ppermute | solution.py:13
  324.9 22.4 %collective-permute-start.43 = (bf16[24,7168]{1,0:T(8,128)(2,1)S(1)}, bf16[24,7168]{1,0:T(8,128)(2,1)S(1)}, u32[]{:S(2)}, u32[]{:S(2)}) collective-permute-start(bf16[24,7168]{1,0:T(8,128)(2,1)S(1)} %fusion.201), channel_id=1, source_target_pairs={{0,2},{2,0},{1,3},{3,1},{4,6},{6,4},{5,7},{7,5},{8,10},{10,8},{9,1... | collective-permute-start | bytes 1032200 | tf_op jit(solution)/shard_map/ppermute | solution.py:13
  333.4 15.0 %copy-start.16 = (f32[2,24,7168]{2,1,0:T(8,128)S(1)}, f32[2,24,7168]{2,1,0:T(8,128)}, u32[]{:S(2)}) copy-start(f32[2,24,7168]{2,1,0:T(8,128)} %copy-done.15) | copy-start | bytes 4128772
  333.4 16.0 %collective-permute-start.32 = (bf16[24,7168]{1,0:T(8,128)(2,1)S(1)}, bf16[24,7168]{1,0:T(8,128)(2,1)S(1)}, u32[]{:S(2)}, u32[]{:S(2)}) collective-permute-start(bf16[24,7168]{1,0:T(8,128)(2,1)S(1)} %fusion.180), channel_id=1, source_target_pairs={{0,4},{4,0},{8,12},{12,8},{1,5},{5,1},{9,13},{13,9},{2,6},{6,2},{1... | collective-permute-start | bytes 1032200 | tf_op jit(solution)/shard_map/ppermute | solution.py:85
  340.8 22.9 %collective-permute-start.38 = (bf16[24,7168]{1,0:T(8,128)(2,1)S(1)}, bf16[24,7168]{1,0:T(8,128)(2,1)S(1)}, u32[]{:S(2)}, u32[]{:S(2)}) collective-permute-start(bf16[24,7168]{1,0:T(8,128)(2,1)S(1)} %fusion.178), channel_id=1, source_target_pairs={{0,8},{4,12},{8,0},{12,4},{1,9},{5,13},{9,1},{13,5},{2,10},{6,14},... | collective-permute-start | bytes 1032200 | tf_op jit(solution)/shard_map/ppermute | solution.py:85
  347.4 24.5 %collective-permute-start.44 = (bf16[24,7168]{1,0:T(8,128)(2,1)S(1)}, bf16[24,7168]{1,0:T(8,128)(2,1)S(1)}, u32[]{:S(2)}, u32[]{:S(2)}) collective-permute-start(bf16[24,7168]{1,0:T(8,128)(2,1)S(1)} %fusion.176), channel_id=1, source_target_pairs={{0,12},{4,8},{8,4},{12,0},{1,13},{5,9},{9,5},{13,1},{2,14},{6,10},... | collective-permute-start | bytes 1032200 | tf_op jit(solution)/shard_map/ppermute | solution.py:85
  373.6 11.9 %collective-permute-start.45 = (bf16[1,32,7168]{2,1,0:T(8,128)(2,1)S(1)}, bf16[1,32,7168]{2,1,0:T(8,128)(2,1)S(1)}, u32[]{:S(2)}, u32[]{:S(2)}) collective-permute-start(bf16[1,32,7168]{2,1,0:T(8,128)(2,1)S(1)} %fusion.6), channel_id=1, source_target_pairs={{0,16},{16,0},{1,17},{17,1},{2,18},{18,2},{3,19},{19,3},{4,20},{20... | collective-permute-start | bytes 1376264 | tf_op jit(solution)/shard_map/ppermute | solution.py:19
  (17 other events, 27.3 us)

commit v5 on v3

--- a/solution.py
+++ b/solution.py
@@ -67,15 +67,6 @@
     return part.astype(jnp.bfloat16)
 
 
-def exchange(chunks):
-    count = lax.axis_size("z")
-    out = [chunks[0]]
-    for d in range(1, count):
-        pairs = [(i, i ^ d) for i in range(count)]
-        out.append(lax.ppermute(chunks[d], "z", pairs))
-    return jnp.stack(out)
-
-
 def dispatch(slots):
     count = lax.axis_size("z")
     pieces = []
@@ -89,12 +80,22 @@
     return jnp.stack(pieces, axis=2)
 
 
-def combine(partial):
+def reduce_group(partial):
     from_core = swap(partial[1], "c")
     chip_sum = partial[0].astype(jnp.float32) + from_core.astype(jnp.float32)
-    from_x = swap(chip_sum[1].astype(jnp.bfloat16), "x")
-    total = (chip_sum[0] + from_x.astype(jnp.float32)).astype(jnp.bfloat16)
-    return exchange(total)
+    totals = []
+    for d in range(chip_sum.shape[1]):
+        from_x = swap(chip_sum[1, d].astype(jnp.bfloat16), "x")
+        totals.append((chip_sum[0, d] + from_x.astype(jnp.float32)).astype(jnp.bfloat16))
+    return totals
+
+
+def returned(totals):
+    count = lax.axis_size("z")
+    out = [totals[0]]
+    for d in range(1, count):
+        out.append(lax.ppermute(totals[d], "z", [(i, i ^ d) for i in range(count)]))
+    return jnp.stack(out)
 
 
 def body(
@@ -125,9 +126,11 @@
     f_rows = dispatch(f_slots)
     b_rows = dispatch(b_slots)
     f_partial = forward_rows(f_rows.reshape(-1, width), w_gate, w_up, w_down)
+    f_totals = reduce_group(f_partial.reshape(2, 2, experts, capacity, width))
+    b_rows, f_totals = lax.optimization_barrier((b_rows, f_totals))
+    f_out = returned(f_totals)
     b_partial = backward_rows(b_rows.reshape(-1, 2 * width), w_gate, w_up, w_down)
-    f_out = combine(f_partial.reshape(2, 2, experts, capacity, width))
-    b_out = combine(b_partial.reshape(2, 2, experts, capacity, width))
+    b_out = returned(reduce_group(b_partial.reshape(2, 2, experts, capacity, width)))
     high = lax.Precision.HIGHEST
     f_mixed = jnp.dot(
         f_weights, f_out.reshape(experts * capacity, width).astype(jnp.float32), precision=high

time: 308 us -> 275 us (0.89)
  waiting for transfers between devices: 229 us -> 187 us
  starting transfers between devices: 25.9 us -> 38.8 us
  local copies, waits for them, and re-layouts: 12.6 us -> 9.07 us
    ppermute x6, waiting for transfers between devices: 79.8 us -> 37.3 us  [dispatch(): received = lax.ppermute(slots[d], 'z', [(i, i ^ d) for i in range(count)])]
    ppermute x20 -> x26, starting transfers between devices: 8.56 us -> 21.4 us  [swap(): return lax.ppermute(value, axis, [(0, 1), (1, 0)])]
    ppermute x20 -> x26, waiting for transfers between devices: 114 us -> 105 us  [swap(): return lax.ppermute(value, axis, [(0, 1), (1, 0)])]
    ppermute x6, waiting for transfers between devices: 26.5 us -> 33.3 us  [returned(): out.append(lax.ppermute(totals[d], 'z', [(i, i ^ d) for i in range(count)]))]
    another operation x10, other arithmetic: 9.3 us -> 5.26 us  [dispatch(): return jnp.stack(pieces, axis=2)]
    another operation x8, other arithmetic: 4.39 us -> 8.09 us  [dispatch(): pieces.append(jnp.stack([across, swap(across, 'c')]))]
    add x2 -> x0, other arithmetic: 3.25 us -> none  [combine(): chip_sum = partial[0].astype(jnp.float32) + from_core.astype(jnp.float32)]
  transfers between devices with their start and end apart: 34 -> 40, of which waited for: 15 -> 25; matrix products, arithmetic and copies ran while one was open for 14% -> 8% of each run, Pallas kernels for 0% -> 0%
where the time goes in v5:
time: 275 us; the launch traced here: 274 us
  waiting for transfers between devices  187 us (68%)
  starting transfers between devices  38.8 us (14%)
  other arithmetic  19.5 us (7%)
  matrix products  18.9 us (7%)
  local copies, waits for them, and re-layouts  9.07 us (3%)
    ppermute x26, waiting for transfers between devices, swap(): return lax.ppermute(value, axis, [(0, 1), (1, 0)])  105 us
    ppermute x6, waiting for transfers between devices, dispatch(): received = lax.ppermute(slots[d], 'z', [(i, i ^ d) for i in range(count)])  37.3 us
    ppermute x6, waiting for transfers between devices, returned(): out.append(lax.ppermute(totals[d], 'z', [(i, i ^ d) for i in range(count)]))  33.3 us
    ppermute x26, starting transfers between devices, swap(): return lax.ppermute(value, axis, [(0, 1), (1, 0)])  21.4 us
    ppermute x2, waiting for transfers between devices, passed_along(): return lax.ppermute(value, axis, pairs)  10.9 us
    another operation x8, other arithmetic, dispatch(): pieces.append(jnp.stack([across, swap(across, 'c')]))  8.09 us
    ppermute x6, starting transfers between devices, dispatch(): received = lax.ppermute(slots[d], 'z', [(i, i ^ d) for i in range(count)])  7.38 us
    ppermute x6, starting transfers between devices, returned(): out.append(lax.ppermute(totals[d], 'z', [(i, i ^ d) for i in range(count)]))  6.8 us
  transfers between devices with their start and end apart: 40, of which 25 were waited for; matrix products, arithmetic and copies ran while one was open for 8% of the time, Pallas kernels for 0%

profile of v5, /device:TPU:16, one launch (start us, length us, event | category | flops | bytes accessed | tf_op | source)
XLA Modules:
  0.0 274.0 jit_solution(8737271713579528966)
XLA Ops:
  3.0 1.6 convolution_convert_fusion.2
  4.7 1.6 collective-permute-start.13
  6.7 1.6 collective-permute-start.19
  8.3 1.5 collective-permute-start.11
  11.9 2.5 collective-permute-start.2
  14.4 2.9 %collective-permute-done.11 = bf16[24,7168]{1,0:T(8,128)(2,1)} collective-permute-done((bf16[24,7168]{1,0:T(8,128)(2,1)S(1)}, bf16[24,7168]{1,0:T(8,128)(2,1)}, u32[]{:S(2)}, u32[]{:S(2)}) %collective-permute-start.11) | collective-permute-done | bytes 344096 | tf_op jit(solution)/shard_map/ppermute | solution.py:13
  17.3 1.5 collective-permute-start
  18.8 1.1 fusion.78
  19.9 1.5 collective-permute-done.13
  22.3 10.5 %collective-permute-done = bf16[24,14336]{1,0:T(8,128)(2,1)S(1)} collective-permute-done((bf16[24,14336]{1,0:T(8,128)(2,1)S(1)}, bf16[24,14336]{1,0:T(8,128)(2,1)S(1)}, u32[]{:S(2)}, u32[]{:S(2)}) %collective-permute-start) | collective-permute-done | bytes 688160 | tf_op jit(solution)/shard_map/ppermute | solution.py:13
  32.8 1.5 collective-permute-start.14
  34.3 1.3 fusion.84
  36.0 5.1 %collective-permute-done.14 = bf16[24,7168]{1,0:T(8,128)(2,1)S(1)} collective-permute-done((bf16[24,7168]{1,0:T(8,128)(2,1)}, bf16[24,7168]{1,0:T(8,128)(2,1)S(1)}, u32[]{:S(2)}, u32[]{:S(2)}) %collective-permute-start.14) | collective-permute-done | bytes 344096 | tf_op jit(solution)/shard_map/ppermute | solution.py:13
  41.1 1.5 collective-permute-start.17
  42.6 1.1 fusion.77
  43.8 6.0 %collective-permute-done.17 = bf16[24,7168]{1,0:T(8,128)(2,1)S(1)} collective-permute-done((bf16[24,7168]{1,0:T(8,128)(2,1)S(1)}, bf16[24,7168]{1,0:T(8,128)(2,1)S(1)}, u32[]{:S(2)}, u32[]{:S(2)}) %collective-permute-start.17) | collective-permute-done | bytes 344096 | tf_op jit(solution)/shard_map/ppermute | solution.py:13
  49.8 1.6 collective-permute-start.20
  51.5 5.5 %collective-permute-done.20 = bf16[24,7168]{1,0:T(8,128)(2,1)S(1)} collective-permute-done((bf16[24,7168]{1,0:T(8,128)(2,1)S(1)}, bf16[24,7168]{1,0:T(8,128)(2,1)S(1)}, u32[]{:S(2)}, u32[]{:S(2)}) %collective-permute-start.20) | collective-permute-done | bytes 344096 | tf_op jit(solution)/shard_map/ppermute | solution.py:13
  57.8 1.3 collective-permute-done.15
  59.9 21.7 %collective-permute-done.5 = bf16[24,14336]{1,0:T(8,128)(2,1)} collective-permute-done((bf16[24,14336]{1,0:T(8,128)(2,1)S(1)}, bf16[24,14336]{1,0:T(8,128)(2,1)}, u32[]{:S(2)}, u32[]{:S(2)}) %collective-permute-start.5) | collective-permute-done | bytes 688160 | tf_op jit(solution)/shard_map/ppermute | solution.py:77
  81.6 1.5 collective-permute-start.3
  83.1 14.0 %collective-permute-done.8 = bf16[24,14336]{1,0:T(8,128)(2,1)} collective-permute-done((bf16[24,14336]{1,0:T(8,128)(2,1)S(1)}, bf16[24,14336]{1,0:T(8,128)(2,1)}, u32[]{:S(2)}, u32[]{:S(2)}) %collective-permute-start.8) | collective-permute-done | bytes 688160 | tf_op jit(solution)/shard_map/ppermute | solution.py:77
  97.1 1.5 collective-permute-start.6
  100.8 1.6 copy-done
  102.4 1.6 fusion.19
  104.4 1.6 fusion.44
  106.5 1.6 convolution_convert_fusion.1
  108.5 1.5 fusion.83
  110.6 5.2 %collective-permute-done.6 = bf16[24,14336]{1,0:T(8,128)(2,1)} collective-permute-done((bf16[24,14336]{1,0:T(8,128)(2,1)}, bf16[24,14336]{1,0:T(8,128)(2,1)}, u32[]{:S(2)}, u32[]{:S(2)}) %collective-permute-start.6) | collective-permute-done | bytes 688160 | tf_op jit(solution)/shard_map/ppermute | solution.py:13
  115.8 1.5 fusion.82
  117.4 10.8 %collective-permute-done.9 = bf16[24,14336]{1,0:T(8,128)(2,1)} collective-permute-done((bf16[24,14336]{1,0:T(8,128)(2,1)}, bf16[24,14336]{1,0:T(8,128)(2,1)}, u32[]{:S(2)}, u32[]{:S(2)}) %collective-permute-start.9) | collective-permute-done | bytes 688160 | tf_op jit(solution)/shard_map/ppermute | solution.py:13
  128.2 1.5 fusion.81
  129.8 1.6 maximum_bitcast_fusion
  134.3 1.6 collective-permute-start.23
  136.4 1.5 collective-permute-start.25
  138.4 1.5 pad_maximum_fusion
  139.9 5.4 %collective-permute-done.23 = bf16[24,7168]{1,0:T(8,128)(2,1)S(1)} collective-permute-done((bf16[24,7168]{1,0:T(8,128)(2,1)S(1)}, bf16[24,7168]{1,0:T(8,128)(2,1)S(1)}, u32[]{:S(2)}, u32[]{:S(2)}) %collective-permute-start.23) | collective-permute-done | bytes 344096 | tf_op jit(solution)/shard_map/ppermute | solution.py:13
  145.3 7.4 %collective-permute-done.24 = bf16[24,7168]{1,0:T(8,128)(2,1)S(1)} collective-permute-done((bf16[24,7168]{1,0:T(8,128)(2,1)S(1)}, bf16[24,7168]{1,0:T(8,128)(2,1)S(1)}, u32[]{:S(2)}, u32[]{:S(2)}) %collective-permute-start.24) | collective-permute-done | bytes 344096 | tf_op jit(solution)/shard_map/ppermute | solution.py:13
  152.6 7.4 %collective-permute-done.25 = bf16[24,7168]{1,0:T(8,128)(2,1)S(1)} collective-permute-done((bf16[24,7168]{1,0:T(8,128)(2,1)S(1)}, bf16[24,7168]{1,0:T(8,128)(2,1)S(1)}, u32[]{:S(2)}, u32[]{:S(2)}) %collective-permute-start.25) | collective-permute-done | bytes 344096 | tf_op jit(solution)/shard_map/ppermute | solution.py:13
  160.0 6.6 %collective-permute-done.26 = bf16[24,7168]{1,0:T(8,128)(2,1)S(1)} collective-permute-done((bf16[24,7168]{1,0:T(8,128)(2,1)S(1)}, bf16[24,7168]{1,0:T(8,128)(2,1)S(1)}, u32[]{:S(2)}, u32[]{:S(2)}) %collective-permute-start.26) | collective-permute-done | bytes 344096 | tf_op jit(solution)/shard_map/ppermute | solution.py:13
  166.6 1.1 fusion.59
  167.7 1.9 copy.35
  169.7 1.6 fusion.4
  171.3 1.6 fusion.6
  173.4 1.6 fusion.39
  175.0 1.6 fusion.16
  176.6 3.8 %add_convert_fusion = bf16[384,7168]{1,0:T(8,128)(2,1)S(1)} fusion(f32[384,7168]{1,0:T(8,128)S(1)} %fusion.16, bf16[1,7168,256]{2,1,0:T(8,128)(2,1)} %param.18, f32[384,256]{1,0:T(8,128)S(1)} %fusion.4, f32[384,256]{1,0:T(8,128)S(1)} %fusion.6), kind=kOutput, calls=%fused_computation.2 | convolution fusion | flops 1415380992 | bytes 20971520 | tf_op jit(solution)/shard_map/dot_general | solution.py:64
  180.9 5.1 %collective-permute-done.31 = bf16[2,4,24,7168]{3,2,1,0:T(8,128)(2,1)S(1)} collective-permute-done((bf16[2,4,24,7168]{3,2,1,0:T(8,128)(2,1)S(1)}, bf16[2,4,24,7168]{3,2,1,0:T(8,128)(2,1)S(1)}, u32[]{:S(2)}, u32[]{:S(2)}) %collective-permute-start.31) | collective-permute-done | bytes 2752544 | tf_op jit(solution)/shard_map/ppermute | solution.py:13
  187.1 1.6 collective-permute-start.32
  189.2 1.5 collective-permute-start.35
  191.3 1.5 collective-permute-start.27
  192.7 5.4 %collective-permute-done.32 = bf16[24,7168]{1,0:T(8,128)(2,1)S(1)} collective-permute-done((bf16[24,7168]{1,0:T(8,128)(2,1)S(1)}, bf16[24,7168]{1,0:T(8,128)(2,1)S(1)}, u32[]{:S(2)}, u32[]{:S(2)}) %collective-permute-start.32) | collective-permute-done | bytes 344096 | tf_op jit(solution)/shard_map/ppermute | solution.py:13
  198.1 1.3 collective-permute-start.28
  199.5 6.0 %collective-permute-done.33 = bf16[24,7168]{1,0:T(8,128)(2,1)S(1)} collective-permute-done((bf16[24,7168]{1,0:T(8,128)(2,1)S(1)}, bf16[24,7168]{1,0:T(8,128)(2,1)S(1)}, u32[]{:S(2)}, u32[]{:S(2)}) %collective-permute-start.33) | collective-permute-done | bytes 344096 | tf_op jit(solution)/shard_map/ppermute | solution.py:13
  205.9 6.9 %collective-permute-done.35 = bf16[24,7168]{1,0:T(8,128)(2,1)S(1)} collective-permute-done((bf16[24,7168]{1,0:T(8,128)(2,1)S(1)}, bf16[24,7168]{1,0:T(8,128)(2,1)S(1)}, u32[]{:S(2)}, u32[]{:S(2)}) %collective-permute-start.35) | collective-permute-done | bytes 344096 | tf_op jit(solution)/shard_map/ppermute | solution.py:13
  212.9 6.6 %collective-permute-done.37 = bf16[24,7168]{1,0:T(8,128)(2,1)S(1)} collective-permute-done((bf16[24,7168]{1,0:T(8,128)(2,1)S(1)}, bf16[24,7168]{1,0:T(8,128)(2,1)S(1)}, u32[]{:S(2)}, u32[]{:S(2)}) %collective-permute-start.37) | collective-permute-done | bytes 344096 | tf_op jit(solution)/shard_map/ppermute | solution.py:13
  219.7 1.5 collective-permute-start.34
  221.7 1.6 collective-permute-start.38
  223.3 21.1 %collective-permute-done.29 = bf16[24,7168]{1,0:T(8,128)(2,1)S(1)} collective-permute-done((bf16[24,7168]{1,0:T(8,128)(2,1)S(1)}, bf16[24,7168]{1,0:T(8,128)(2,1)S(1)}, u32[]{:S(2)}, u32[]{:S(2)}) %collective-permute-start.29) | collective-permute-done | bytes 344096 | tf_op jit(solution)/shard_map/ppermute | solution.py:97
  245.3 1.6 collective-permute-start.30
  247.0 4.0 %collective-permute-done.36 = bf16[24,7168]{1,0:T(8,128)(2,1)S(1)} collective-permute-done((bf16[24,7168]{1,0:T(8,128)(2,1)S(1)}, bf16[24,7168]{1,0:T(8,128)(2,1)S(1)}, u32[]{:S(2)}, u32[]{:S(2)}) %collective-permute-start.36) | collective-permute-done | bytes 344096 | tf_op jit(solution)/shard_map/ppermute | solution.py:97
  251.0 8.1 %collective-permute-done.38 = bf16[24,7168]{1,0:T(8,128)(2,1)S(1)} collective-permute-done((bf16[24,7168]{1,0:T(8,128)(2,1)S(1)}, bf16[24,7168]{1,0:T(8,128)(2,1)S(1)}, u32[]{:S(2)}, u32[]{:S(2)}) %collective-permute-start.38) | collective-permute-done | bytes 344096 | tf_op jit(solution)/shard_map/ppermute | solution.py:97
  260.0 1.6 collective-permute-start.39
  261.6 10.9 %collective-permute-done.39 = bf16[1,32,7168]{2,1,0:T(8,128)(2,1)S(1)} collective-permute-done((bf16[1,32,7168]{2,1,0:T(8,128)(2,1)S(1)}, bf16[1,32,7168]{2,1,0:T(8,128)(2,1)S(1)}, u32[]{:S(2)}, u32[]{:S(2)}) %collective-permute-start.39) | collective-permute-done | bytes 458784 | tf_op jit(solution)/shard_map/ppermute | solution.py:19
  (107 shorter events, 23.4 us)
Async XLA Ops:
  0.6 9.9 %copy-start.12 = (f32[1,32,2]{1,2,0:T(2,128)S(1)}, f32[1,32,2]{1,2,0:T(2,128)}, u32[]{:S(2)}) copy-start(f32[1,32,2]{1,2,0:T(2,128)} %param.16) | copy-start | bytes 772
  0.6 10.0 %copy-start.8 = (bf16[1,32,7168]{2,1,0:T(8,128)(2,1)S(1)}, bf16[1,32,7168]{2,1,0:T(8,128)(2,1)}, u32[]{:S(2)}) copy-start(bf16[1,32,7168]{2,1,0:T(8,128)(2,1)} %param.13) | copy-start | bytes 1376260
  0.7 10.0 %copy-start.6 = (bf16[1,32,7168]{2,1,0:T(8,128)(2,1)S(1)}, bf16[1,32,7168]{2,1,0:T(8,128)(2,1)}, u32[]{:S(2)}) copy-start(bf16[1,32,7168]{2,1,0:T(8,128)(2,1)} %param.14) | copy-start | bytes 1376260
  4.7 16.7 %collective-permute-start.13 = (bf16[24,7168]{1,0:T(8,128)(2,1)S(1)}, bf16[24,7168]{1,0:T(8,128)(2,1)}, u32[]{:S(2)}, u32[]{:S(2)}) collective-permute-start(bf16[24,7168]{1,0:T(8,128)(2,1)S(1)} %get-tuple-element.48), channel_id=1, source_target_pairs={{0,4},{4,0},{8,12},{12,8},{1,5},{5,1},{9,13},{13,9},{2,6},{6,2},{1... | collective-permute-start | bytes 1032200 | tf_op jit(solution)/shard_map/ppermute | solution.py:77
  6.4 29.2 %collective-permute-start.16 = (bf16[24,7168]{1,0:T(8,128)(2,1)S(1)}, bf16[24,7168]{1,0:T(8,128)(2,1)S(1)}, u32[]{:S(2)}, u32[]{:S(2)}) collective-permute-start(bf16[24,7168]{1,0:T(8,128)(2,1)S(1)} %get-tuple-element.47), channel_id=1, source_target_pairs={{0,8},{4,12},{8,0},{12,4},{1,9},{5,13},{9,1},{13,5},{2,10},{6,14},... | collective-permute-start | bytes 1032200 | tf_op jit(solution)/shard_map/ppermute | solution.py:77
  6.7 37.0 %collective-permute-start.19 = (bf16[24,7168]{1,0:T(8,128)(2,1)S(1)}, bf16[24,7168]{1,0:T(8,128)(2,1)S(1)}, u32[]{:S(2)}, u32[]{:S(2)}) collective-permute-start(bf16[24,7168]{1,0:T(8,128)(2,1)S(1)} %get-tuple-element.46), channel_id=1, source_target_pairs={{0,12},{4,8},{8,4},{12,0},{1,13},{5,9},{9,5},{13,1},{2,14},{6,10},... | collective-permute-start | bytes 1032200 | tf_op jit(solution)/shard_map/ppermute | solution.py:77
  8.3 9.1 %collective-permute-start.11 = (bf16[24,7168]{1,0:T(8,128)(2,1)S(1)}, bf16[24,7168]{1,0:T(8,128)(2,1)}, u32[]{:S(2)}, u32[]{:S(2)}) collective-permute-start(bf16[24,7168]{1,0:T(8,128)(2,1)S(1)} %get-tuple-element.49), channel_id=1, source_target_pairs={{0,2},{2,0},{1,3},{3,1},{4,6},{6,4},{5,7},{7,5},{8,10},{10,8},{9,1... | collective-permute-start | bytes 1032200 | tf_op jit(solution)/shard_map/ppermute | solution.py:13
  11.9 47.6 %collective-permute-start.2 = (bf16[24,14336]{1,0:T(8,128)(2,1)S(1)}, bf16[24,14336]{1,0:T(8,128)(2,1)}, u32[]{:S(2)}, u32[]{:S(2)}) collective-permute-start(bf16[24,14336]{1,0:T(8,128)(2,1)S(1)} %get-tuple-element.43), channel_id=1, source_target_pairs={{0,4},{4,0},{8,12},{12,8},{1,5},{5,1},{9,13},{13,9},{2,6},{6,2},{1... | collective-permute-start | bytes 2064392 | tf_op jit(solution)/shard_map/ppermute | solution.py:77
  17.3 15.4 %collective-permute-start = (bf16[24,14336]{1,0:T(8,128)(2,1)S(1)}, bf16[24,14336]{1,0:T(8,128)(2,1)S(1)}, u32[]{:S(2)}, u32[]{:S(2)}) collective-permute-start(bf16[24,14336]{1,0:T(8,128)(2,1)S(1)} %get-tuple-element.44), channel_id=1, source_target_pairs={{0,2},{2,0},{1,3},{3,1},{4,6},{6,4},{5,7},{7,5},{8,10},{10,8},{9,1... | collective-permute-start | bytes 2064392 | tf_op jit(solution)/shard_map/ppermute | solution.py:13
  21.5 60.2 %collective-permute-start.5 = (bf16[24,14336]{1,0:T(8,128)(2,1)S(1)}, bf16[24,14336]{1,0:T(8,128)(2,1)}, u32[]{:S(2)}, u32[]{:S(2)}) collective-permute-start(bf16[24,14336]{1,0:T(8,128)(2,1)S(1)} %get-tuple-element.42), channel_id=1, source_target_pairs={{0,8},{4,12},{8,0},{12,4},{1,9},{5,13},{9,1},{13,5},{2,10},{6,14},... | collective-permute-start | bytes 2064392 | tf_op jit(solution)/shard_map/ppermute | solution.py:77
  32.8 8.4 %collective-permute-start.14 = (bf16[24,7168]{1,0:T(8,128)(2,1)}, bf16[24,7168]{1,0:T(8,128)(2,1)S(1)}, u32[]{:S(2)}, u32[]{:S(2)}) collective-permute-start(bf16[24,7168]{1,0:T(8,128)(2,1)} %collective-permute-done.13), channel_id=1, source_target_pairs={{0,2},{2,0},{1,3},{3,1},{4,6},{6,4},{5,7},{7,5},{8,10},{10,8},{9,1... | collective-permute-start | bytes 1032200 | tf_op jit(solution)/shard_map/ppermute | solution.py:13
  35.6 61.5 %collective-permute-start.8 = (bf16[24,14336]{1,0:T(8,128)(2,1)S(1)}, bf16[24,14336]{1,0:T(8,128)(2,1)}, u32[]{:S(2)}, u32[]{:S(2)}) collective-permute-start(bf16[24,14336]{1,0:T(8,128)(2,1)S(1)} %get-tuple-element.41), channel_id=1, source_target_pairs={{0,12},{4,8},{8,4},{12,0},{1,13},{5,9},{9,5},{13,1},{2,14},{6,10},... | collective-permute-start | bytes 2064392 | tf_op jit(solution)/shard_map/ppermute | solution.py:77
  41.1 8.7 %collective-permute-start.17 = (bf16[24,7168]{1,0:T(8,128)(2,1)S(1)}, bf16[24,7168]{1,0:T(8,128)(2,1)S(1)}, u32[]{:S(2)}, u32[]{:S(2)}) collective-permute-start(bf16[24,7168]{1,0:T(8,128)(2,1)S(1)} %collective-permute-done.16), channel_id=1, source_target_pairs={{0,2},{2,0},{1,3},{3,1},{4,6},{6,4},{5,7},{7,5},{8,10},{10,8},{9,1... | collective-permute-start | bytes 1032200 | tf_op jit(solution)/shard_map/ppermute | solution.py:13
  43.7 13.4 %collective-permute-start.12 = (bf16[2,24,7168]{2,1,0:T(8,128)(2,1)S(1)}, bf16[2,24,7168]{2,1,0:T(8,128)(2,1)S(1)}, u32[]{:S(2)}, u32[]{:S(2)}) collective-permute-start(bf16[2,24,7168]{2,1,0:T(8,128)(2,1)S(1)} %get-tuple-element.59), channel_id=1, source_target_pairs={{0,1},{1,0},{2,3},{3,2},{4,5},{5,4},{6,7},{7,6},{8,9},{9,8},{10,11... | collective-permute-start | bytes 2064392 | tf_op jit(solution)/shard_map/ppermute | solution.py:13
  49.8 7.2 %collective-permute-start.20 = (bf16[24,7168]{1,0:T(8,128)(2,1)S(1)}, bf16[24,7168]{1,0:T(8,128)(2,1)S(1)}, u32[]{:S(2)}, u32[]{:S(2)}) collective-permute-start(bf16[24,7168]{1,0:T(8,128)(2,1)S(1)} %collective-permute-done.19), channel_id=1, source_target_pairs={{0,2},{2,0},{1,3},{3,1},{4,6},{6,4},{5,7},{7,5},{8,10},{10,8},{9,1... | collective-permute-start | bytes 1032200 | tf_op jit(solution)/shard_map/ppermute | solution.py:13
  57.0 2.1 collective-permute-start.15
  57.1 41.5 %collective-permute-start.18 = (bf16[2,24,7168]{2,1,0:T(8,128)(2,1)S(1)}, bf16[2,24,7168]{2,1,0:T(8,128)(2,1)S(1)}, u32[]{:S(2)}, u32[]{:S(2)}) collective-permute-start(bf16[2,24,7168]{2,1,0:T(8,128)(2,1)S(1)} %get-tuple-element.63), channel_id=1, source_target_pairs={{0,1},{1,0},{2,3},{3,2},{4,5},{5,4},{6,7},{7,6},{8,9},{9,8},{10,11... | collective-permute-start | bytes 2064392 | tf_op jit(solution)/shard_map/ppermute | solution.py:13
  59.2 40.1 %collective-permute-start.21 = (bf16[2,24,7168]{2,1,0:T(8,128)(2,1)S(1)}, bf16[2,24,7168]{2,1,0:T(8,128)(2,1)S(1)}, u32[]{:S(2)}, u32[]{:S(2)}) collective-permute-start(bf16[2,24,7168]{2,1,0:T(8,128)(2,1)S(1)} %get-tuple-element.65), channel_id=1, source_target_pairs={{0,1},{1,0},{2,3},{3,2},{4,5},{5,4},{6,7},{7,6},{8,9},{9,8},{10,11... | collective-permute-start | bytes 2064392 | tf_op jit(solution)/shard_map/ppermute | solution.py:13
  59.5 70.3 %collective-permute-start.1 = (bf16[2,24,14336]{2,1,0:T(8,128)(2,1)}, bf16[2,24,14336]{2,1,0:T(8,128)(2,1)}, u32[]{:S(2)}, u32[]{:S(2)}) collective-permute-start(bf16[2,24,14336]{2,1,0:T(8,128)(2,1)} %get-tuple-element.51), channel_id=1, source_target_pairs={{0,1},{1,0},{2,3},{3,2},{4,5},{5,4},{6,7},{7,6},{8,9},{9,8},{10,11... | collective-permute-start | bytes 4128776 | tf_op jit(solution)/shard_map/ppermute | solution.py:13
  81.6 26.9 %collective-permute-start.3 = (bf16[24,14336]{1,0:T(8,128)(2,1)}, bf16[24,14336]{1,0:T(8,128)(2,1)}, u32[]{:S(2)}, u32[]{:S(2)}) collective-permute-start(bf16[24,14336]{1,0:T(8,128)(2,1)} %collective-permute-done.2), channel_id=1, source_target_pairs={{0,2},{2,0},{1,3},{3,1},{4,6},{6,4},{5,7},{7,5},{8,10},{10,8},{9,1... | collective-permute-start | bytes 2064392 | tf_op jit(solution)/shard_map/ppermute | solution.py:13
  97.1 18.7 %collective-permute-start.6 = (bf16[24,14336]{1,0:T(8,128)(2,1)}, bf16[24,14336]{1,0:T(8,128)(2,1)}, u32[]{:S(2)}, u32[]{:S(2)}) collective-permute-start(bf16[24,14336]{1,0:T(8,128)(2,1)} %collective-permute-done.5), channel_id=1, source_target_pairs={{0,2},{2,0},{1,3},{3,1},{4,6},{6,4},{5,7},{7,5},{8,10},{10,8},{9,1... | collective-permute-start | bytes 2064392 | tf_op jit(solution)/shard_map/ppermute | solution.py:13
  98.6 29.6 %collective-permute-start.9 = (bf16[24,14336]{1,0:T(8,128)(2,1)}, bf16[24,14336]{1,0:T(8,128)(2,1)}, u32[]{:S(2)}, u32[]{:S(2)}) collective-permute-start(bf16[24,14336]{1,0:T(8,128)(2,1)} %collective-permute-done.8), channel_id=1, source_target_pairs={{0,2},{2,0},{1,3},{3,1},{4,6},{6,4},{5,7},{7,5},{8,10},{10,8},{9,1... | collective-permute-start | bytes 2064392 | tf_op jit(solution)/shard_map/ppermute | solution.py:13
  100.4 2.0 copy-start
  102.4 2.0 copy-start.1
  104.4 2.0 copy-start.3
  108.5 24.7 %collective-permute-start.22 = (bf16[2,4,24,7168]{3,2,1,0:T(8,128)(2,1)S(1)}, bf16[2,4,24,7168]{3,2,1,0:T(8,128)(2,1)S(1)}, u32[]{:S(2)}, u32[]{:S(2)}) collective-permute-start(bf16[2,4,24,7168]{3,2,1,0:T(8,128)(2,1)S(1)} %bitcast.210), channel_id=1, source_target_pairs={{0,1},{1,0},{2,3},{3,2},{4,5},{5,4},{6,7},{7,6},{8,9},{9,8},{10,11... | collective-permute-start | bytes 8257544 | tf_op jit(solution)/shard_map/ppermute | solution.py:13
  110.0 21.3 %collective-permute-start.4 = (bf16[2,24,14336]{2,1,0:T(8,128)(2,1)S(1)}, bf16[2,24,14336]{2,1,0:T(8,128)(2,1)S(1)}, u32[]{:S(2)}, u32[]{:S(2)}) collective-permute-start(bf16[2,24,14336]{2,1,0:T(8,128)(2,1)S(1)} %get-tuple-element.53), channel_id=1, source_target_pairs={{0,1},{1,0},{2,3},{3,2},{4,5},{5,4},{6,7},{7,6},{8,9},{9,8},{10,11... | collective-permute-start | bytes 4128776 | tf_op jit(solution)/shard_map/ppermute | solution.py:13
  117.3 14.4 %collective-permute-start.7 = (bf16[2,24,14336]{2,1,0:T(8,128)(2,1)S(1)}, bf16[2,24,14336]{2,1,0:T(8,128)(2,1)S(1)}, u32[]{:S(2)}, u32[]{:S(2)}) collective-permute-start(bf16[2,24,14336]{2,1,0:T(8,128)(2,1)S(1)} %get-tuple-element.55), channel_id=1, source_target_pairs={{0,1},{1,0},{2,3},{3,2},{4,5},{5,4},{6,7},{7,6},{8,9},{9,8},{10,11... | collective-permute-start | bytes 4128776 | tf_op jit(solution)/shard_map/ppermute | solution.py:13
  129.7 3.2 %collective-permute-start.10 = (bf16[2,24,14336]{2,1,0:T(8,128)(2,1)S(1)}, bf16[2,24,14336]{2,1,0:T(8,128)(2,1)S(1)}, u32[]{:S(2)}, u32[]{:S(2)}) collective-permute-start(bf16[2,24,14336]{2,1,0:T(8,128)(2,1)S(1)} %get-tuple-element.57), channel_id=1, source_target_pairs={{0,1},{1,0},{2,3},{3,2},{4,5},{5,4},{6,7},{7,6},{8,9},{9,8},{10,11... | collective-permute-start | bytes 4128776 | tf_op jit(solution)/shard_map/ppermute | solution.py:13
  134.3 11.0 %collective-permute-start.23 = (bf16[24,7168]{1,0:T(8,128)(2,1)S(1)}, bf16[24,7168]{1,0:T(8,128)(2,1)S(1)}, u32[]{:S(2)}, u32[]{:S(2)}) collective-permute-start(bf16[24,7168]{1,0:T(8,128)(2,1)S(1)} %get-tuple-element.39), channel_id=1, source_target_pairs={{0,2},{2,0},{1,3},{3,1},{4,6},{6,4},{5,7},{7,5},{8,10},{10,8},{9,1... | collective-permute-start | bytes 1032200 | tf_op jit(solution)/shard_map/ppermute | solution.py:13
  135.9 16.8 %collective-permute-start.24 = (bf16[24,7168]{1,0:T(8,128)(2,1)S(1)}, bf16[24,7168]{1,0:T(8,128)(2,1)S(1)}, u32[]{:S(2)}, u32[]{:S(2)}) collective-permute-start(bf16[24,7168]{1,0:T(8,128)(2,1)S(1)} %get-tuple-element.38), channel_id=1, source_target_pairs={{0,2},{2,0},{1,3},{3,1},{4,6},{6,4},{5,7},{7,5},{8,10},{10,8},{9,1... | collective-permute-start | bytes 1032200 | tf_op jit(solution)/shard_map/ppermute | solution.py:13
  136.4 23.6 %collective-permute-start.25 = (bf16[24,7168]{1,0:T(8,128)(2,1)S(1)}, bf16[24,7168]{1,0:T(8,128)(2,1)S(1)}, u32[]{:S(2)}, u32[]{:S(2)}) collective-permute-start(bf16[24,7168]{1,0:T(8,128)(2,1)S(1)} %get-tuple-element.37), channel_id=1, source_target_pairs={{0,2},{2,0},{1,3},{3,1},{4,6},{6,4},{5,7},{7,5},{8,10},{10,8},{9,1... | collective-permute-start | bytes 1032200 | tf_op jit(solution)/shard_map/ppermute | solution.py:13
  137.9 28.7 %collective-permute-start.26 = (bf16[24,7168]{1,0:T(8,128)(2,1)S(1)}, bf16[24,7168]{1,0:T(8,128)(2,1)S(1)}, u32[]{:S(2)}, u32[]{:S(2)}) collective-permute-start(bf16[24,7168]{1,0:T(8,128)(2,1)S(1)} %get-tuple-element.36), channel_id=1, source_target_pairs={{0,2},{2,0},{1,3},{3,1},{4,6},{6,4},{5,7},{7,5},{8,10},{10,8},{9,1... | collective-permute-start | bytes 1032200 | tf_op jit(solution)/shard_map/ppermute | solution.py:13
  167.7 2.0 copy-start.4
  171.3 2.0 copy-start.2
  180.8 5.2 %collective-permute-start.31 = (bf16[2,4,24,7168]{3,2,1,0:T(8,128)(2,1)S(1)}, bf16[2,4,24,7168]{3,2,1,0:T(8,128)(2,1)S(1)}, u32[]{:S(2)}, u32[]{:S(2)}) collective-permute-start(bf16[2,4,24,7168]{3,2,1,0:T(8,128)(2,1)S(1)} %bitcast.211), channel_id=1, source_target_pairs={{0,1},{1,0},{2,3},{3,2},{4,5},{5,4},{6,7},{7,6},{8,9},{9,8},{10,11... | collective-permute-start | bytes 8257544 | tf_op jit(solution)/shard_map/ppermute | solution.py:13
  187.0 4.3 %copy-start.11 = (bf16[24,7168]{1,0:T(8,128)(2,1)S(1)}, bf16[24,7168]{1,0:T(8,128)(2,1)}, u32[]{:S(2)}) copy-start(bf16[24,7168]{1,0:T(8,128)(2,1)} %get-tuple-element.8) | copy-start | bytes 1032196
  187.0 11.1 %copy-start.10 = (bf16[24,7168]{1,0:T(8,128)(2,1)S(1)}, bf16[24,7168]{1,0:T(8,128)(2,1)}, u32[]{:S(2)}) copy-start(bf16[24,7168]{1,0:T(8,128)(2,1)} %get-tuple-element.9) | copy-start | bytes 1032196
  187.0 18.5 %copy-start.9 = (bf16[24,7168]{1,0:T(8,128)(2,1)S(1)}, bf16[24,7168]{1,0:T(8,128)(2,1)}, u32[]{:S(2)}) copy-start(bf16[24,7168]{1,0:T(8,128)(2,1)} %get-tuple-element.10) | copy-start | bytes 1032196
  187.1 11.0 %collective-permute-start.32 = (bf16[24,7168]{1,0:T(8,128)(2,1)S(1)}, bf16[24,7168]{1,0:T(8,128)(2,1)S(1)}, u32[]{:S(2)}, u32[]{:S(2)}) collective-permute-start(bf16[24,7168]{1,0:T(8,128)(2,1)S(1)} %get-tuple-element.32), channel_id=1, source_target_pairs={{0,2},{2,0},{1,3},{3,1},{4,6},{6,4},{5,7},{7,5},{8,10},{10,8},{9,1... | collective-permute-start | bytes 1032200 | tf_op jit(solution)/shard_map/ppermute | solution.py:13
  188.7 16.8 %collective-permute-start.33 = (bf16[24,7168]{1,0:T(8,128)(2,1)S(1)}, bf16[24,7168]{1,0:T(8,128)(2,1)S(1)}, u32[]{:S(2)}, u32[]{:S(2)}) collective-permute-start(bf16[24,7168]{1,0:T(8,128)(2,1)S(1)} %get-tuple-element.35), channel_id=1, source_target_pairs={{0,2},{2,0},{1,3},{3,1},{4,6},{6,4},{5,7},{7,5},{8,10},{10,8},{9,1... | collective-permute-start | bytes 1032200 | tf_op jit(solution)/shard_map/ppermute | solution.py:13
  189.2 23.6 %collective-permute-start.35 = (bf16[24,7168]{1,0:T(8,128)(2,1)S(1)}, bf16[24,7168]{1,0:T(8,128)(2,1)S(1)}, u32[]{:S(2)}, u32[]{:S(2)}) collective-permute-start(bf16[24,7168]{1,0:T(8,128)(2,1)S(1)} %get-tuple-element.34), channel_id=1, source_target_pairs={{0,2},{2,0},{1,3},{3,1},{4,6},{6,4},{5,7},{7,5},{8,10},{10,8},{9,1... | collective-permute-start | bytes 1032200 | tf_op jit(solution)/shard_map/ppermute | solution.py:13
  190.8 28.7 %collective-permute-start.37 = (bf16[24,7168]{1,0:T(8,128)(2,1)S(1)}, bf16[24,7168]{1,0:T(8,128)(2,1)S(1)}, u32[]{:S(2)}, u32[]{:S(2)}) collective-permute-start(bf16[24,7168]{1,0:T(8,128)(2,1)S(1)} %get-tuple-element.33), channel_id=1, source_target_pairs={{0,2},{2,0},{1,3},{3,1},{4,6},{6,4},{5,7},{7,5},{8,10},{10,8},{9,1... | collective-permute-start | bytes 1032200 | tf_op jit(solution)/shard_map/ppermute | solution.py:13
  191.3 30.5 %collective-permute-start.27 = (bf16[24,7168]{1,0:T(8,128)(2,1)S(1)}, bf16[24,7168]{1,0:T(8,128)(2,1)S(1)}, u32[]{:S(2)}, u32[]{:S(2)}) collective-permute-start(bf16[24,7168]{1,0:T(8,128)(2,1)S(1)} %copy-done.11), channel_id=1, source_target_pairs={{0,4},{4,0},{8,12},{12,8},{1,5},{5,1},{9,13},{13,9},{2,6},{6,2},{1... | collective-permute-start | bytes 1032200 | tf_op jit(solution)/shard_map/ppermute | solution.py:97
  198.1 25.2 %collective-permute-start.28 = (bf16[24,7168]{1,0:T(8,128)(2,1)S(1)}, bf16[24,7168]{1,0:T(8,128)(2,1)S(1)}, u32[]{:S(2)}, u32[]{:S(2)}) collective-permute-start(bf16[24,7168]{1,0:T(8,128)(2,1)S(1)} %copy-done.10), channel_id=1, source_target_pairs={{0,8},{4,12},{8,0},{12,4},{1,9},{5,13},{9,1},{13,5},{2,10},{6,14},... | collective-permute-start | bytes 1032200 | tf_op jit(solution)/shard_map/ppermute | solution.py:97
  205.5 39.0 %collective-permute-start.29 = (bf16[24,7168]{1,0:T(8,128)(2,1)S(1)}, bf16[24,7168]{1,0:T(8,128)(2,1)S(1)}, u32[]{:S(2)}, u32[]{:S(2)}) collective-permute-start(bf16[24,7168]{1,0:T(8,128)(2,1)S(1)} %copy-done.9), channel_id=1, source_target_pairs={{0,12},{4,8},{8,4},{12,0},{1,13},{5,9},{9,5},{13,1},{2,14},{6,10},... | collective-permute-start | bytes 1032200 | tf_op jit(solution)/shard_map/ppermute | solution.py:97
  219.7 24.9 %copy-start.5 = (bf16[1,32,7168]{2,1,0:T(8,128)(2,1)S(1)}, bf16[1,32,7168]{2,1,0:T(8,128)(2,1)}, u32[]{:S(2)}) copy-start(bf16[1,32,7168]{2,1,0:T(8,128)(2,1)} %param.10) | copy-start | bytes 1376260
  219.7 27.2 %collective-permute-start.34 = (bf16[24,7168]{1,0:T(8,128)(2,1)S(1)}, bf16[24,7168]{1,0:T(8,128)(2,1)S(1)}, u32[]{:S(2)}, u32[]{:S(2)}) collective-permute-start(bf16[24,7168]{1,0:T(8,128)(2,1)S(1)} %get-tuple-element.18), channel_id=1, source_target_pairs={{0,4},{4,0},{8,12},{12,8},{1,5},{5,1},{9,13},{13,9},{2,6},{6,2},{1... | collective-permute-start | bytes 1032200 | tf_op jit(solution)/shard_map/ppermute | solution.py:97
  221.3 29.7 %collective-permute-start.36 = (bf16[24,7168]{1,0:T(8,128)(2,1)S(1)}, bf16[24,7168]{1,0:T(8,128)(2,1)S(1)}, u32[]{:S(2)}, u32[]{:S(2)}) collective-permute-start(bf16[24,7168]{1,0:T(8,128)(2,1)S(1)} %get-tuple-element.17), channel_id=1, source_target_pairs={{0,8},{4,12},{8,0},{12,4},{1,9},{5,13},{9,1},{13,5},{2,10},{6,14},... | collective-permute-start | bytes 1032200 | tf_op jit(solution)/shard_map/ppermute | solution.py:97
  221.7 37.4 %collective-permute-start.38 = (bf16[24,7168]{1,0:T(8,128)(2,1)S(1)}, bf16[24,7168]{1,0:T(8,128)(2,1)S(1)}, u32[]{:S(2)}, u32[]{:S(2)}) collective-permute-start(bf16[24,7168]{1,0:T(8,128)(2,1)S(1)} %get-tuple-element.19), channel_id=1, source_target_pairs={{0,12},{4,8},{8,4},{12,0},{1,13},{5,9},{9,5},{13,1},{2,14},{6,10},... | collective-permute-start | bytes 1032200 | tf_op jit(solution)/shard_map/ppermute | solution.py:97
  244.6 14.6 %copy-start.7 = (bf16[1,32,7168]{2,1,0:T(8,128)(2,1)S(1)}, bf16[1,32,7168]{2,1,0:T(8,128)(2,1)}, u32[]{:S(2)}) copy-start(bf16[1,32,7168]{2,1,0:T(8,128)(2,1)} %param.14) | copy-start | bytes 1376260
  245.3 16.2 %collective-permute-start.30 = (bf16[1,32,7168]{2,1,0:T(8,128)(2,1)S(1)}, bf16[1,32,7168]{2,1,0:T(8,128)(2,1)S(1)}, u32[]{:S(2)}, u32[]{:S(2)}) collective-permute-start(bf16[1,32,7168]{2,1,0:T(8,128)(2,1)S(1)} %fusion.3), channel_id=1, source_target_pairs={{0,16},{16,0},{1,17},{17,1},{2,18},{18,2},{3,19},{19,3},{4,20},{20... | collective-permute-start | bytes 1376264 | tf_op jit(solution)/shard_map/ppermute | solution.py:19
  260.0 12.5 %collective-permute-start.39 = (bf16[1,32,7168]{2,1,0:T(8,128)(2,1)S(1)}, bf16[1,32,7168]{2,1,0:T(8,128)(2,1)S(1)}, u32[]{:S(2)}, u32[]{:S(2)}) collective-permute-start(bf16[1,32,7168]{2,1,0:T(8,128)(2,1)S(1)} %fusion.2), channel_id=1, source_target_pairs={{0,16},{16,0},{1,17},{17,1},{2,18},{18,2},{3,19},{19,3},{4,20},{20... | collective-permute-start | bytes 1376264 | tf_op jit(solution)/shard_map/ppermute | solution.py:19

commit v6 on v5

--- a/solution.py
+++ b/solution.py
@@ -81,12 +81,13 @@
 
 
 def reduce_group(partial):
-    from_core = swap(partial[1], "c")
-    chip_sum = partial[0].astype(jnp.float32) + from_core.astype(jnp.float32)
-    totals = []
-    for d in range(chip_sum.shape[1]):
-        from_x = swap(chip_sum[1, d].astype(jnp.bfloat16), "x")
-        totals.append((chip_sum[0, d] + from_x.astype(jnp.float32)).astype(jnp.bfloat16))
+    count = partial.shape[2]
+    totals = [None] * count
+    for d in list(range(1, count)) + [0]:
+        from_core = swap(partial[1, :, d], "c")
+        chip_sum = partial[0, :, d].astype(jnp.float32) + from_core.astype(jnp.float32)
+        from_x = swap(chip_sum[1].astype(jnp.bfloat16), "x")
+        totals[d] = (chip_sum[0] + from_x.astype(jnp.float32)).astype(jnp.bfloat16)
     return totals
 
 

time: 275 us -> 287 us (1.044)
  waiting for transfers between devices: 187 us -> 193 us
  other arithmetic: 19.5 us -> 22.7 us
    ppermute x6, waiting for transfers between devices: 33.3 us -> 50.1 us  [returned(): out.append(lax.ppermute(totals[d], 'z', [(i, i ^ d) for i in range(count)]))]
    ppermute x26 -> x32, waiting for transfers between devices: 105 us -> 95.7 us  [swap(): return lax.ppermute(value, axis, [(0, 1), (1, 0)])]
    ppermute x26 -> x32, starting transfers between devices: 21.4 us -> 23.9 us  [swap(): return lax.ppermute(value, axis, [(0, 1), (1, 0)])]
  transfers between devices with their start and end apart: 40 -> 46, of which waited for: 25 -> 24; matrix products, arithmetic and copies ran while one was open for 8% -> 9% of each run, Pallas kernels for 0% -> 0%
where the time goes in v6:
time: 287 us; the launch traced here: 286 us
  waiting for transfers between devices  193 us (67%)
  starting transfers between devices  37.7 us (13%)
  other arithmetic  22.7 us (8%)
  matrix products  20.7 us (7%)
  local copies, waits for them, and re-layouts  10.7 us (4%)
    ppermute x32, waiting for transfers between devices, swap(): return lax.ppermute(value, axis, [(0, 1), (1, 0)])  95.7 us
    ppermute x6, waiting for transfers between devices, returned(): out.append(lax.ppermute(totals[d], 'z', [(i, i ^ d) for i in range(count)]))  50.1 us
    ppermute x6, waiting for transfers between devices, dispatch(): received = lax.ppermute(slots[d], 'z', [(i, i ^ d) for i in range(count)])  38.2 us
    ppermute x32, starting transfers between devices, swap(): return lax.ppermute(value, axis, [(0, 1), (1, 0)])  23.9 us
    ppermute x2, waiting for transfers between devices, passed_along(): return lax.ppermute(value, axis, pairs)  9.18 us
    another operation x10, other arithmetic, dispatch(): return jnp.stack(pieces, axis=2)  7.96 us
    ppermute x6, starting transfers between devices, dispatch(): received = lax.ppermute(slots[d], 'z', [(i, i ^ d) for i in range(count)])  7.4 us
    another operation x8, other arithmetic, dispatch(): pieces.append(jnp.stack([across, swap(across, 'c')]))  6.54 us
  transfers between devices with their start and end apart: 46, of which 24 were waited for; matrix products, arithmetic and copies ran while one was open for 9% of the time, Pallas kernels for 0%

profile of v6, /device:TPU:16, one launch (start us, length us, event | category | flops | bytes accessed | tf_op | source)
XLA Modules:
  0.0 286.2 jit_solution(13331184703295419913)
XLA Ops:
  2.9 1.6 convolution_convert_fusion.2
  4.5 0.9 slice_bitcast_fusion.24
  5.4 1.6 collective-permute-start.13
  7.3 1.6 collective-permute-start.19
  8.9 1.5 collective-permute-start.11
  12.4 2.5 collective-permute-start.2
  15.0 2.8 collective-permute-done.11
  17.8 1.5 collective-permute-start
  19.4 2.4 collective-permute-done.13
  23.4 9.8 %collective-permute-done = bf16[24,14336]{1,0:T(8,128)(2,1)S(1)} collective-permute-done((bf16[24,14336]{1,0:T(8,128)(2,1)S(1)}, bf16[24,14336]{1,0:T(8,128)(2,1)S(1)}, u32[]{:S(2)}, u32[]{:S(2)}) %collective-permute-start) | collective-permute-done | bytes 688160 | tf_op jit(solution)/shard_map/ppermute | solution.py:13
  33.2 1.5 collective-permute-start.14
  35.4 5.9 %collective-permute-done.14 = bf16[24,7168]{1,0:T(8,128)(2,1)S(1)} collective-permute-done((bf16[24,7168]{1,0:T(8,128)(2,1)}, bf16[24,7168]{1,0:T(8,128)(2,1)S(1)}, u32[]{:S(2)}, u32[]{:S(2)}) %collective-permute-start.14) | collective-permute-done | bytes 344096 | tf_op jit(solution)/shard_map/ppermute | solution.py:13
  41.4 1.5 collective-permute-start.17
  43.1 7.2 %collective-permute-done.17 = bf16[24,7168]{1,0:T(8,128)(2,1)S(1)} collective-permute-done((bf16[24,7168]{1,0:T(8,128)(2,1)}, bf16[24,7168]{1,0:T(8,128)(2,1)S(1)}, u32[]{:S(2)}, u32[]{:S(2)}) %collective-permute-start.17) | collective-permute-done | bytes 344096 | tf_op jit(solution)/shard_map/ppermute | solution.py:13
  50.3 1.5 collective-permute-start.20
  51.8 1.1 fusion.84
  52.9 4.9 %collective-permute-done.20 = bf16[24,7168]{1,0:T(8,128)(2,1)S(1)} collective-permute-done((bf16[24,7168]{1,0:T(8,128)(2,1)}, bf16[24,7168]{1,0:T(8,128)(2,1)S(1)}, u32[]{:S(2)}, u32[]{:S(2)}) %collective-permute-start.20) | collective-permute-done | bytes 344096 | tf_op jit(solution)/shard_map/ppermute | solution.py:13
  57.7 1.1 fusion.83
  60.6 21.8 %collective-permute-done.5 = bf16[24,14336]{1,0:T(8,128)(2,1)S(1)} collective-permute-done((bf16[24,14336]{1,0:T(8,128)(2,1)S(1)}, bf16[24,14336]{1,0:T(8,128)(2,1)S(1)}, u32[]{:S(2)}, u32[]{:S(2)}) %collective-permute-start.5) | collective-permute-done | bytes 688160 | tf_op jit(solution)/shard_map/ppermute | solution.py:77
  82.4 1.5 collective-permute-start.3
  83.9 14.0 %collective-permute-done.8 = bf16[24,14336]{1,0:T(8,128)(2,1)} collective-permute-done((bf16[24,14336]{1,0:T(8,128)(2,1)S(1)}, bf16[24,14336]{1,0:T(8,128)(2,1)}, u32[]{:S(2)}, u32[]{:S(2)}) %collective-permute-start.8) | collective-permute-done | bytes 688160 | tf_op jit(solution)/shard_map/ppermute | solution.py:77
  97.9 1.5 collective-permute-start.6
  100.2 0.9 pad_maximum_fusion.1
  101.6 1.6 copy-done
  103.2 1.6 fusion.19
  105.2 1.6 fusion.44
  107.3 1.6 convolution_convert_fusion.1
  109.7 1.3 fusion.89
  111.0 5.4 %collective-permute-done.6 = bf16[24,14336]{1,0:T(8,128)(2,1)} collective-permute-done((bf16[24,14336]{1,0:T(8,128)(2,1)S(1)}, bf16[24,14336]{1,0:T(8,128)(2,1)}, u32[]{:S(2)}, u32[]{:S(2)}) %collective-permute-start.6) | collective-permute-done | bytes 688160 | tf_op jit(solution)/shard_map/ppermute | solution.py:13
  116.4 1.3 fusion.88
  117.7 11.1 %collective-permute-done.9 = bf16[24,14336]{1,0:T(8,128)(2,1)} collective-permute-done((bf16[24,14336]{1,0:T(8,128)(2,1)}, bf16[24,14336]{1,0:T(8,128)(2,1)}, u32[]{:S(2)}, u32[]{:S(2)}) %collective-permute-start.9) | collective-permute-done | bytes 688160 | tf_op jit(solution)/shard_map/ppermute | solution.py:13
  128.8 1.5 fusion.87
  131.4 2.0 convert_add_fusion.4
  133.5 1.6 collective-permute-start.29
  135.7 1.6 maximum_bitcast_fusion
  137.4 7.1 %collective-permute-done.29 = bf16[24,7168]{1,0:T(8,128)(2,1)S(1)} collective-permute-done((bf16[24,7168]{1,0:T(8,128)(2,1)S(1)}, bf16[24,7168]{1,0:T(8,128)(2,1)S(1)}, u32[]{:S(2)}, u32[]{:S(2)}) %collective-permute-start.29) | collective-permute-done | bytes 344096 | tf_op jit(solution)/shard_map/ppermute | solution.py:13
  144.4 1.5 collective-permute-start.25
  146.8 5.1 %collective-permute-done.27 = bf16[24,7168]{1,0:T(8,128)(2,1)S(1)} collective-permute-done((bf16[24,7168]{1,0:T(8,128)(2,1)S(1)}, bf16[24,7168]{1,0:T(8,128)(2,1)S(1)}, u32[]{:S(2)}, u32[]{:S(2)}) %collective-permute-start.27) | collective-permute-done | bytes 344096 | tf_op jit(solution)/shard_map/ppermute | solution.py:13
  151.8 1.5 collective-permute-start.23
  154.1 5.0 %collective-permute-done.25 = bf16[24,7168]{1,0:T(8,128)(2,1)S(1)} collective-permute-done((bf16[24,7168]{1,0:T(8,128)(2,1)S(1)}, bf16[24,7168]{1,0:T(8,128)(2,1)S(1)}, u32[]{:S(2)}, u32[]{:S(2)}) %collective-permute-start.25) | collective-permute-done | bytes 344096 | tf_op jit(solution)/shard_map/ppermute | solution.py:13
  160.0 5.7 %collective-permute-done.23 = bf16[24,7168]{1,0:T(8,128)(2,1)S(1)} collective-permute-done((bf16[24,7168]{1,0:T(8,128)(2,1)S(1)}, bf16[24,7168]{1,0:T(8,128)(2,1)S(1)}, u32[]{:S(2)}, u32[]{:S(2)}) %collective-permute-start.23) | collective-permute-done | bytes 344096 | tf_op jit(solution)/shard_map/ppermute | solution.py:13
  166.1 1.6 maximum_bitcast_fusion.2
  167.7 1.6 maximum_bitcast_fusion.3
  169.3 1.5 pad_maximum_fusion
  170.8 2.1 copy.70
  172.8 1.6 fusion.4
  174.5 2.4 fusion.6
  176.8 2.6 fusion.39
  179.5 1.6 fusion.16
  181.1 3.9 %add_convert_fusion = bf16[384,7168]{1,0:T(8,128)(2,1)S(1)} fusion(f32[384,7168]{1,0:T(8,128)S(1)} %fusion.16, bf16[1,7168,256]{2,1,0:T(8,128)(2,1)} %param.18, f32[384,256]{1,0:T(8,128)S(1)} %fusion.4, f32[384,256]{1,0:T(8,128)} %fusion.6), kind=kOutput, calls=%fused_computation.2 | convolution fusion | flops 1415380992 | bytes 20971520 | tf_op jit(solution)/shard_map/dot_general | solution.py:64
  185.0 1.4 collective-permute-start.30
  187.0 1.6 collective-permute-start.32
  189.4 10.0 %collective-permute-done.30 = bf16[24,7168]{1,0:T(8,128)(2,1)S(1)} collective-permute-done((bf16[24,7168]{1,0:T(8,128)(2,1)}, bf16[24,7168]{1,0:T(8,128)(2,1)S(1)}, u32[]{:S(2)}, u32[]{:S(2)}) %collective-permute-start.30) | collective-permute-done | bytes 344096 | tf_op jit(solution)/shard_map/ppermute | solution.py:98
  199.4 11.2 %collective-permute-done.31 = bf16[24,7168]{1,0:T(8,128)(2,1)S(1)} collective-permute-done((bf16[24,7168]{1,0:T(8,128)(2,1)}, bf16[24,7168]{1,0:T(8,128)(2,1)S(1)}, u32[]{:S(2)}, u32[]{:S(2)}) %collective-permute-start.31) | collective-permute-done | bytes 344096 | tf_op jit(solution)/shard_map/ppermute | solution.py:98
  210.6 7.3 %collective-permute-done.32 = bf16[24,7168]{1,0:T(8,128)(2,1)S(1)} collective-permute-done((bf16[24,7168]{1,0:T(8,128)(2,1)}, bf16[24,7168]{1,0:T(8,128)(2,1)S(1)}, u32[]{:S(2)}, u32[]{:S(2)}) %collective-permute-start.32) | collective-permute-done | bytes 344096 | tf_op jit(solution)/shard_map/ppermute | solution.py:98
  219.5 1.6 collective-permute-start.33
  221.9 1.6 collective-permute-start.35
  224.2 1.6 collective-permute-start.40
  226.4 14.0 %collective-permute-done.37 = bf16[24,7168]{1,0:T(8,128)(2,1)S(1)} collective-permute-done((bf16[24,7168]{1,0:T(8,128)(2,1)S(1)}, bf16[24,7168]{1,0:T(8,128)(2,1)S(1)}, u32[]{:S(2)}, u32[]{:S(2)}) %collective-permute-start.37) | collective-permute-done | bytes 344096 | tf_op jit(solution)/shard_map/ppermute | solution.py:13
  240.5 7.2 %collective-permute-done.40 = bf16[24,7168]{1,0:T(8,128)(2,1)S(1)} collective-permute-done((bf16[24,7168]{1,0:T(8,128)(2,1)S(1)}, bf16[24,7168]{1,0:T(8,128)(2,1)S(1)}, u32[]{:S(2)}, u32[]{:S(2)}) %collective-permute-start.40) | collective-permute-done | bytes 344096 | tf_op jit(solution)/shard_map/ppermute | solution.py:13
  247.9 4.0 %collective-permute-done.43 = bf16[24,7168]{1,0:T(8,128)(2,1)S(1)} collective-permute-done((bf16[24,7168]{1,0:T(8,128)(2,1)S(1)}, bf16[24,7168]{1,0:T(8,128)(2,1)S(1)}, u32[]{:S(2)}, u32[]{:S(2)}) %collective-permute-start.43) | collective-permute-done | bytes 344096 | tf_op jit(solution)/shard_map/ppermute | solution.py:13
  252.5 15.6 %collective-permute-done.41 = bf16[24,7168]{1,0:T(8,128)(2,1)S(1)} collective-permute-done((bf16[24,7168]{1,0:T(8,128)(2,1)S(1)}, bf16[24,7168]{1,0:T(8,128)(2,1)S(1)}, u32[]{:S(2)}, u32[]{:S(2)}) %collective-permute-start.41) | collective-permute-done | bytes 344096 | tf_op jit(solution)/shard_map/ppermute | solution.py:98
  268.1 6.0 %collective-permute-done.44 = bf16[24,7168]{1,0:T(8,128)(2,1)S(1)} collective-permute-done((bf16[24,7168]{1,0:T(8,128)(2,1)S(1)}, bf16[24,7168]{1,0:T(8,128)(2,1)S(1)}, u32[]{:S(2)}, u32[]{:S(2)}) %collective-permute-start.44) | collective-permute-done | bytes 344096 | tf_op jit(solution)/shard_map/ppermute | solution.py:98
  275.5 9.2 %collective-permute-done.45 = bf16[1,32,7168]{2,1,0:T(8,128)(2,1)S(1)} collective-permute-done((bf16[1,32,7168]{2,1,0:T(8,128)(2,1)S(1)}, bf16[1,32,7168]{2,1,0:T(8,128)(2,1)S(1)}, u32[]{:S(2)}, u32[]{:S(2)}) %collective-permute-start.45) | collective-permute-done | bytes 458784 | tf_op jit(solution)/shard_map/ppermute | solution.py:19
  (125 shorter events, 25.3 us)
Async XLA Ops:
  4.4 6.7 %copy-start.9 = (f32[1,32,2]{1,2,0:T(2,128)S(1)}, f32[1,32,2]{1,2,0:T(2,128)}, u32[]{:S(2)}) copy-start(f32[1,32,2]{1,2,0:T(2,128)} %param.16) | copy-start | bytes 772
  4.4 6.8 %copy-start.5 = (bf16[1,32,7168]{2,1,0:T(8,128)(2,1)S(1)}, bf16[1,32,7168]{2,1,0:T(8,128)(2,1)}, u32[]{:S(2)}) copy-start(bf16[1,32,7168]{2,1,0:T(8,128)(2,1)} %param.14) | copy-start | bytes 1376260
  4.5 6.8 %copy-start.6 = (bf16[1,32,7168]{2,1,0:T(8,128)(2,1)S(1)}, bf16[1,32,7168]{2,1,0:T(8,128)(2,1)}, u32[]{:S(2)}) copy-start(bf16[1,32,7168]{2,1,0:T(8,128)(2,1)} %param.13) | copy-start | bytes 1376260
  5.4 16.4 %collective-permute-start.13 = (bf16[24,7168]{1,0:T(8,128)(2,1)S(1)}, bf16[24,7168]{1,0:T(8,128)(2,1)S(1)}, u32[]{:S(2)}, u32[]{:S(2)}) collective-permute-start(bf16[24,7168]{1,0:T(8,128)(2,1)S(1)} %get-tuple-element.40), channel_id=1, source_target_pairs={{0,4},{4,0},{8,12},{12,8},{1,5},{5,1},{9,13},{13,9},{2,6},{6,2},{1... | collective-permute-start | bytes 1032200 | tf_op jit(solution)/shard_map/ppermute | solution.py:77
  6.9 28.0 %collective-permute-start.16 = (bf16[24,7168]{1,0:T(8,128)(2,1)}, bf16[24,7168]{1,0:T(8,128)(2,1)}, u32[]{:S(2)}, u32[]{:S(2)}) collective-permute-start(bf16[24,7168]{1,0:T(8,128)(2,1)} %get-tuple-element.39), channel_id=1, source_target_pairs={{0,8},{4,12},{8,0},{12,4},{1,9},{5,13},{9,1},{13,5},{2,10},{6,14},... | collective-permute-start | bytes 1032200 | tf_op jit(solution)/shard_map/ppermute | solution.py:77
  7.3 35.7 %collective-permute-start.19 = (bf16[24,7168]{1,0:T(8,128)(2,1)S(1)}, bf16[24,7168]{1,0:T(8,128)(2,1)}, u32[]{:S(2)}, u32[]{:S(2)}) collective-permute-start(bf16[24,7168]{1,0:T(8,128)(2,1)S(1)} %get-tuple-element.38), channel_id=1, source_target_pairs={{0,12},{4,8},{8,4},{12,0},{1,13},{5,9},{9,5},{13,1},{2,14},{6,10},... | collective-permute-start | bytes 1032200 | tf_op jit(solution)/shard_map/ppermute | solution.py:77
  8.9 9.0 %collective-permute-start.11 = (bf16[24,7168]{1,0:T(8,128)(2,1)S(1)}, bf16[24,7168]{1,0:T(8,128)(2,1)S(1)}, u32[]{:S(2)}, u32[]{:S(2)}) collective-permute-start(bf16[24,7168]{1,0:T(8,128)(2,1)S(1)} %get-tuple-element.41), channel_id=1, source_target_pairs={{0,2},{2,0},{1,3},{3,1},{4,6},{6,4},{5,7},{7,5},{8,10},{10,8},{9,1... | collective-permute-start | bytes 1032200 | tf_op jit(solution)/shard_map/ppermute | solution.py:13
  12.4 47.7 %collective-permute-start.2 = (bf16[24,14336]{1,0:T(8,128)(2,1)S(1)}, bf16[24,14336]{1,0:T(8,128)(2,1)S(1)}, u32[]{:S(2)}, u32[]{:S(2)}) collective-permute-start(bf16[24,14336]{1,0:T(8,128)(2,1)S(1)} %get-tuple-element.35), channel_id=1, source_target_pairs={{0,4},{4,0},{8,12},{12,8},{1,5},{5,1},{9,13},{13,9},{2,6},{6,2},{1... | collective-permute-start | bytes 2064392 | tf_op jit(solution)/shard_map/ppermute | solution.py:77
  17.8 15.4 %collective-permute-start = (bf16[24,14336]{1,0:T(8,128)(2,1)S(1)}, bf16[24,14336]{1,0:T(8,128)(2,1)S(1)}, u32[]{:S(2)}, u32[]{:S(2)}) collective-permute-start(bf16[24,14336]{1,0:T(8,128)(2,1)S(1)} %get-tuple-element.36), channel_id=1, source_target_pairs={{0,2},{2,0},{1,3},{3,1},{4,6},{6,4},{5,7},{7,5},{8,10},{10,8},{9,1... | collective-permute-start | bytes 2064392 | tf_op jit(solution)/shard_map/ppermute | solution.py:13
  21.8 0.7 copy-start.7
  22.5 59.9 %collective-permute-start.5 = (bf16[24,14336]{1,0:T(8,128)(2,1)S(1)}, bf16[24,14336]{1,0:T(8,128)(2,1)S(1)}, u32[]{:S(2)}, u32[]{:S(2)}) collective-permute-start(bf16[24,14336]{1,0:T(8,128)(2,1)S(1)} %get-tuple-element.34), channel_id=1, source_target_pairs={{0,8},{4,12},{8,0},{12,4},{1,9},{5,13},{9,1},{13,5},{2,10},{6,14},... | collective-permute-start | bytes 2064392 | tf_op jit(solution)/shard_map/ppermute | solution.py:77
  33.2 8.1 %collective-permute-start.14 = (bf16[24,7168]{1,0:T(8,128)(2,1)}, bf16[24,7168]{1,0:T(8,128)(2,1)S(1)}, u32[]{:S(2)}, u32[]{:S(2)}) collective-permute-start(bf16[24,7168]{1,0:T(8,128)(2,1)} %copy-done.7), channel_id=1, source_target_pairs={{0,2},{2,0},{1,3},{3,1},{4,6},{6,4},{5,7},{7,5},{8,10},{10,8},{9,1... | collective-permute-start | bytes 1032200 | tf_op jit(solution)/shard_map/ppermute | solution.py:13
  34.7 8.1 %copy-start.8 = (bf16[24,7168]{1,0:T(8,128)(2,1)S(1)}, bf16[24,7168]{1,0:T(8,128)(2,1)}, u32[]{:S(2)}) copy-start(bf16[24,7168]{1,0:T(8,128)(2,1)} %copy-done.7) | copy-start | bytes 1032196
  34.9 63.0 %collective-permute-start.8 = (bf16[24,14336]{1,0:T(8,128)(2,1)S(1)}, bf16[24,14336]{1,0:T(8,128)(2,1)}, u32[]{:S(2)}, u32[]{:S(2)}) collective-permute-start(bf16[24,14336]{1,0:T(8,128)(2,1)S(1)} %get-tuple-element.33), channel_id=1, source_target_pairs={{0,12},{4,8},{8,4},{12,0},{1,13},{5,9},{9,5},{13,1},{2,14},{6,10},... | collective-permute-start | bytes 2064392 | tf_op jit(solution)/shard_map/ppermute | solution.py:77
  41.4 8.9 %collective-permute-start.17 = (bf16[24,7168]{1,0:T(8,128)(2,1)}, bf16[24,7168]{1,0:T(8,128)(2,1)S(1)}, u32[]{:S(2)}, u32[]{:S(2)}) collective-permute-start(bf16[24,7168]{1,0:T(8,128)(2,1)} %collective-permute-done.16), channel_id=1, source_target_pairs={{0,2},{2,0},{1,3},{3,1},{4,6},{6,4},{5,7},{7,5},{8,10},{10,8},{9,1... | collective-permute-start | bytes 1032200 | tf_op jit(solution)/shard_map/ppermute | solution.py:13
  43.0 15.8 %collective-permute-start.12 = (bf16[2,24,7168]{2,1,0:T(8,128)(2,1)S(1)}, bf16[2,24,7168]{2,1,0:T(8,128)(2,1)S(1)}, u32[]{:S(2)}, u32[]{:S(2)}) collective-permute-start(bf16[2,24,7168]{2,1,0:T(8,128)(2,1)S(1)} %get-tuple-element.51), channel_id=1, source_target_pairs={{0,1},{1,0},{2,3},{3,2},{4,5},{5,4},{6,7},{7,6},{8,9},{9,8},{10,11... | collective-permute-start | bytes 2064392 | tf_op jit(solution)/shard_map/ppermute | solution.py:13
  50.3 7.5 %collective-permute-start.20 = (bf16[24,7168]{1,0:T(8,128)(2,1)}, bf16[24,7168]{1,0:T(8,128)(2,1)S(1)}, u32[]{:S(2)}, u32[]{:S(2)}) collective-permute-start(bf16[24,7168]{1,0:T(8,128)(2,1)} %collective-permute-done.19), channel_id=1, source_target_pairs={{0,2},{2,0},{1,3},{3,1},{4,6},{6,4},{5,7},{7,5},{8,10},{10,8},{9,1... | collective-permute-start | bytes 1032200 | tf_op jit(solution)/shard_map/ppermute | solution.py:13
  57.7 2.1 collective-permute-start.15
  58.8 40.6 %collective-permute-start.18 = (bf16[2,24,7168]{2,1,0:T(8,128)(2,1)S(1)}, bf16[2,24,7168]{2,1,0:T(8,128)(2,1)S(1)}, u32[]{:S(2)}, u32[]{:S(2)}) collective-permute-start(bf16[2,24,7168]{2,1,0:T(8,128)(2,1)S(1)} %get-tuple-element.55), channel_id=1, source_target_pairs={{0,1},{1,0},{2,3},{3,2},{4,5},{5,4},{6,7},{7,6},{8,9},{9,8},{10,11... | collective-permute-start | bytes 2064392 | tf_op jit(solution)/shard_map/ppermute | solution.py:13
  59.9 40.2 %collective-permute-start.21 = (bf16[2,24,7168]{2,1,0:T(8,128)(2,1)S(1)}, bf16[2,24,7168]{2,1,0:T(8,128)(2,1)S(1)}, u32[]{:S(2)}, u32[]{:S(2)}) collective-permute-start(bf16[2,24,7168]{2,1,0:T(8,128)(2,1)S(1)} %get-tuple-element.57), channel_id=1, source_target_pairs={{0,1},{1,0},{2,3},{3,2},{4,5},{5,4},{6,7},{7,6},{8,9},{9,8},{10,11... | collective-permute-start | bytes 2064392 | tf_op jit(solution)/shard_map/ppermute | solution.py:13
  60.2 75.0 %collective-permute-start.1 = (bf16[2,24,14336]{2,1,0:T(8,128)(2,1)S(1)}, bf16[2,24,14336]{2,1,0:T(8,128)(2,1)}, u32[]{:S(2)}, u32[]{:S(2)}) collective-permute-start(bf16[2,24,14336]{2,1,0:T(8,128)(2,1)S(1)} %get-tuple-element.43), channel_id=1, source_target_pairs={{0,1},{1,0},{2,3},{3,2},{4,5},{5,4},{6,7},{7,6},{8,9},{9,8},{10,11... | collective-permute-start | bytes 4128776 | tf_op jit(solution)/shard_map/ppermute | solution.py:13
  82.4 26.7 %collective-permute-start.3 = (bf16[24,14336]{1,0:T(8,128)(2,1)S(1)}, bf16[24,14336]{1,0:T(8,128)(2,1)}, u32[]{:S(2)}, u32[]{:S(2)}) collective-permute-start(bf16[24,14336]{1,0:T(8,128)(2,1)S(1)} %collective-permute-done.2), channel_id=1, source_target_pairs={{0,2},{2,0},{1,3},{3,1},{4,6},{6,4},{5,7},{7,5},{8,10},{10,8},{9,1... | collective-permute-start | bytes 2064392 | tf_op jit(solution)/shard_map/ppermute | solution.py:13
  97.9 18.5 %collective-permute-start.6 = (bf16[24,14336]{1,0:T(8,128)(2,1)S(1)}, bf16[24,14336]{1,0:T(8,128)(2,1)}, u32[]{:S(2)}, u32[]{:S(2)}) collective-permute-start(bf16[24,14336]{1,0:T(8,128)(2,1)S(1)} %collective-permute-done.5), channel_id=1, source_target_pairs={{0,2},{2,0},{1,3},{3,1},{4,6},{6,4},{5,7},{7,5},{8,10},{10,8},{9,1... | collective-permute-start | bytes 2064392 | tf_op jit(solution)/shard_map/ppermute | solution.py:13
  99.4 29.4 %collective-permute-start.9 = (bf16[24,14336]{1,0:T(8,128)(2,1)}, bf16[24,14336]{1,0:T(8,128)(2,1)}, u32[]{:S(2)}, u32[]{:S(2)}) collective-permute-start(bf16[24,14336]{1,0:T(8,128)(2,1)} %collective-permute-done.8), channel_id=1, source_target_pairs={{0,2},{2,0},{1,3},{3,1},{4,6},{6,4},{5,7},{7,5},{8,10},{10,8},{9,1... | collective-permute-start | bytes 2064392 | tf_op jit(solution)/shard_map/ppermute | solution.py:13
  101.1 2.0 copy-start
  103.2 2.0 copy-start.1
  105.2 2.0 copy-start.2
  109.1 21.2 %collective-permute-start.22 = (bf16[2,24,7168]{2,1,0:T(8,128)(2,1)S(1)}, bf16[2,24,7168]{2,1,0:T(8,128)(2,1)}, u32[]{:S(2)}, u32[]{:S(2)}) collective-permute-start(bf16[2,24,7168]{2,1,0:T(8,128)(2,1)S(1)} %get-tuple-element.31), channel_id=1, source_target_pairs={{0,1},{1,0},{2,3},{3,2},{4,5},{5,4},{6,7},{7,6},{8,9},{9,8},{10,11... | collective-permute-start | bytes 2064392 | tf_op jit(solution)/shard_map/ppermute | solution.py:13
  109.2 21.7 %collective-permute-start.24 = (bf16[2,24,7168]{2,1,0:T(8,128)(2,1)S(1)}, bf16[2,24,7168]{2,1,0:T(8,128)(2,1)}, u32[]{:S(2)}, u32[]{:S(2)}) collective-permute-start(bf16[2,24,7168]{2,1,0:T(8,128)(2,1)S(1)} %get-tuple-element.30), channel_id=1, source_target_pairs={{0,1},{1,0},{2,3},{3,2},{4,5},{5,4},{6,7},{7,6},{8,9},{9,8},{10,11... | collective-permute-start | bytes 2064392 | tf_op jit(solution)/shard_map/ppermute | solution.py:13
  116.4 14.6 %collective-permute-start.26 = (bf16[2,24,7168]{2,1,0:T(8,128)(2,1)S(1)}, bf16[2,24,7168]{2,1,0:T(8,128)(2,1)S(1)}, u32[]{:S(2)}, u32[]{:S(2)}) collective-permute-start(bf16[2,24,7168]{2,1,0:T(8,128)(2,1)S(1)} %get-tuple-element.29), channel_id=1, source_target_pairs={{0,1},{1,0},{2,3},{3,2},{4,5},{5,4},{6,7},{7,6},{8,9},{9,8},{10,11... | collective-permute-start | bytes 2064392 | tf_op jit(solution)/shard_map/ppermute | solution.py:13
  128.8 2.6 collective-permute-start.28
  130.3 35.5 %collective-permute-start.4 = (bf16[2,24,14336]{2,1,0:T(8,128)(2,1)S(1)}, bf16[2,24,14336]{2,1,0:T(8,128)(2,1)S(1)}, u32[]{:S(2)}, u32[]{:S(2)}) collective-permute-start(bf16[2,24,14336]{2,1,0:T(8,128)(2,1)S(1)} %get-tuple-element.45), channel_id=1, source_target_pairs={{0,1},{1,0},{2,3},{3,2},{4,5},{5,4},{6,7},{7,6},{8,9},{9,8},{10,11... | collective-permute-start | bytes 4128776 | tf_op jit(solution)/shard_map/ppermute | solution.py:13
  130.9 35.2 %collective-permute-start.7 = (bf16[2,24,14336]{2,1,0:T(8,128)(2,1)S(1)}, bf16[2,24,14336]{2,1,0:T(8,128)(2,1)}, u32[]{:S(2)}, u32[]{:S(2)}) collective-permute-start(bf16[2,24,14336]{2,1,0:T(8,128)(2,1)S(1)} %get-tuple-element.47), channel_id=1, source_target_pairs={{0,1},{1,0},{2,3},{3,2},{4,5},{5,4},{6,7},{7,6},{8,9},{9,8},{10,11... | collective-permute-start | bytes 4128776 | tf_op jit(solution)/shard_map/ppermute | solution.py:13
  130.9 36.7 %collective-permute-start.10 = (bf16[2,24,14336]{2,1,0:T(8,128)(2,1)S(1)}, bf16[2,24,14336]{2,1,0:T(8,128)(2,1)}, u32[]{:S(2)}, u32[]{:S(2)}) collective-permute-start(bf16[2,24,14336]{2,1,0:T(8,128)(2,1)S(1)} %get-tuple-element.49), channel_id=1, source_target_pairs={{0,1},{1,0},{2,3},{3,2},{4,5},{5,4},{6,7},{7,6},{8,9},{9,8},{10,11... | collective-permute-start | bytes 4128776 | tf_op jit(solution)/shard_map/ppermute | solution.py:13
  133.5 11.0 %collective-permute-start.29 = (bf16[24,7168]{1,0:T(8,128)(2,1)S(1)}, bf16[24,7168]{1,0:T(8,128)(2,1)S(1)}, u32[]{:S(2)}, u32[]{:S(2)}) collective-permute-start(bf16[24,7168]{1,0:T(8,128)(2,1)S(1)} %fusion.70), channel_id=1, source_target_pairs={{0,2},{2,0},{1,3},{3,1},{4,6},{6,4},{5,7},{7,5},{8,10},{10,8},{9,1... | collective-permute-start | bytes 1032200 | tf_op jit(solution)/shard_map/ppermute | solution.py:13
  135.1 16.7 %collective-permute-start.27 = (bf16[24,7168]{1,0:T(8,128)(2,1)S(1)}, bf16[24,7168]{1,0:T(8,128)(2,1)S(1)}, u32[]{:S(2)}, u32[]{:S(2)}) collective-permute-start(bf16[24,7168]{1,0:T(8,128)(2,1)S(1)} %fusion.69), channel_id=1, source_target_pairs={{0,2},{2,0},{1,3},{3,1},{4,6},{6,4},{5,7},{7,5},{8,10},{10,8},{9,1... | collective-permute-start | bytes 1032200 | tf_op jit(solution)/shard_map/ppermute | solution.py:13
  144.4 14.7 %collective-permute-start.25 = (bf16[24,7168]{1,0:T(8,128)(2,1)S(1)}, bf16[24,7168]{1,0:T(8,128)(2,1)S(1)}, u32[]{:S(2)}, u32[]{:S(2)}) collective-permute-start(bf16[24,7168]{1,0:T(8,128)(2,1)S(1)} %fusion.68), channel_id=1, source_target_pairs={{0,2},{2,0},{1,3},{3,1},{4,6},{6,4},{5,7},{7,5},{8,10},{10,8},{9,1... | collective-permute-start | bytes 1032200 | tf_op jit(solution)/shard_map/ppermute | solution.py:13
  151.8 13.9 %collective-permute-start.23 = (bf16[24,7168]{1,0:T(8,128)(2,1)S(1)}, bf16[24,7168]{1,0:T(8,128)(2,1)S(1)}, u32[]{:S(2)}, u32[]{:S(2)}) collective-permute-start(bf16[24,7168]{1,0:T(8,128)(2,1)S(1)} %fusion.67), channel_id=1, source_target_pairs={{0,2},{2,0},{1,3},{3,1},{4,6},{6,4},{5,7},{7,5},{8,10},{10,8},{9,1... | collective-permute-start | bytes 1032200 | tf_op jit(solution)/shard_map/ppermute | solution.py:13
  170.8 2.1 copy-start.3
  185.0 14.4 %collective-permute-start.30 = (bf16[24,7168]{1,0:T(8,128)(2,1)}, bf16[24,7168]{1,0:T(8,128)(2,1)S(1)}, u32[]{:S(2)}, u32[]{:S(2)}) collective-permute-start(bf16[24,7168]{1,0:T(8,128)(2,1)} %fusion.63), channel_id=1, source_target_pairs={{0,4},{4,0},{8,12},{12,8},{1,5},{5,1},{9,13},{13,9},{2,6},{6,2},{1... | collective-permute-start | bytes 1032200 | tf_op jit(solution)/shard_map/ppermute | solution.py:98
  186.4 24.1 %collective-permute-start.31 = (bf16[24,7168]{1,0:T(8,128)(2,1)}, bf16[24,7168]{1,0:T(8,128)(2,1)S(1)}, u32[]{:S(2)}, u32[]{:S(2)}) collective-permute-start(bf16[24,7168]{1,0:T(8,128)(2,1)} %fusion.61), channel_id=1, source_target_pairs={{0,8},{4,12},{8,0},{12,4},{1,9},{5,13},{9,1},{13,5},{2,10},{6,14},... | collective-permute-start | bytes 1032200 | tf_op jit(solution)/shard_map/ppermute | solution.py:98
  187.0 30.9 %collective-permute-start.32 = (bf16[24,7168]{1,0:T(8,128)(2,1)}, bf16[24,7168]{1,0:T(8,128)(2,1)S(1)}, u32[]{:S(2)}, u32[]{:S(2)}) collective-permute-start(bf16[24,7168]{1,0:T(8,128)(2,1)} %fusion.59), channel_id=1, source_target_pairs={{0,12},{4,8},{8,4},{12,0},{1,13},{5,9},{9,5},{13,1},{2,14},{6,10},... | collective-permute-start | bytes 1032200 | tf_op jit(solution)/shard_map/ppermute | solution.py:98
  188.8 32.4 %collective-permute-start.34 = (bf16[2,24,7168]{2,1,0:T(8,128)(2,1)S(1)}, bf16[2,24,7168]{2,1,0:T(8,128)(2,1)S(1)}, u32[]{:S(2)}, u32[]{:S(2)}) collective-permute-start(bf16[2,24,7168]{2,1,0:T(8,128)(2,1)S(1)} %get-tuple-element.20), channel_id=1, source_target_pairs={{0,1},{1,0},{2,3},{3,2},{4,5},{5,4},{6,7},{7,6},{8,9},{9,8},{10,11... | collective-permute-start | bytes 2064392 | tf_op jit(solution)/shard_map/ppermute | solution.py:13
  188.9 32.3 %collective-permute-start.36 = (bf16[2,24,7168]{2,1,0:T(8,128)(2,1)S(1)}, bf16[2,24,7168]{2,1,0:T(8,128)(2,1)S(1)}, u32[]{:S(2)}, u32[]{:S(2)}) collective-permute-start(bf16[2,24,7168]{2,1,0:T(8,128)(2,1)S(1)} %get-tuple-element.22), channel_id=1, source_target_pairs={{0,1},{1,0},{2,3},{3,2},{4,5},{5,4},{6,7},{7,6},{8,9},{9,8},{10,11... | collective-permute-start | bytes 2064392 | tf_op jit(solution)/shard_map/ppermute | solution.py:13
  199.4 21.8 %collective-permute-start.39 = (bf16[2,24,7168]{2,1,0:T(8,128)(2,1)S(1)}, bf16[2,24,7168]{2,1,0:T(8,128)(2,1)S(1)}, u32[]{:S(2)}, u32[]{:S(2)}) collective-permute-start(bf16[2,24,7168]{2,1,0:T(8,128)(2,1)S(1)} %get-tuple-element.21), channel_id=1, source_target_pairs={{0,1},{1,0},{2,3},{3,2},{4,5},{5,4},{6,7},{7,6},{8,9},{9,8},{10,11... | collective-permute-start | bytes 2064392 | tf_op jit(solution)/shard_map/ppermute | solution.py:13
  210.6 10.6 %collective-permute-start.42 = (bf16[2,24,7168]{2,1,0:T(8,128)(2,1)S(1)}, bf16[2,24,7168]{2,1,0:T(8,128)(2,1)S(1)}, u32[]{:S(2)}, u32[]{:S(2)}) collective-permute-start(bf16[2,24,7168]{2,1,0:T(8,128)(2,1)S(1)} %get-tuple-element.23), channel_id=1, source_target_pairs={{0,1},{1,0},{2,3},{3,2},{4,5},{5,4},{6,7},{7,6},{8,9},{9,8},{10,11... | collective-permute-start | bytes 2064392 | tf_op jit(solution)/shard_map/ppermute | solution.py:13
  217.8 1.0 copy-start.4
  219.5 56.0 %collective-permute-start.33 = (bf16[1,32,7168]{2,1,0:T(8,128)(2,1)S(1)}, bf16[1,32,7168]{2,1,0:T(8,128)(2,1)S(1)}, u32[]{:S(2)}, u32[]{:S(2)}) collective-permute-start(bf16[1,32,7168]{2,1,0:T(8,128)(2,1)S(1)} %fusion.3), channel_id=1, source_target_pairs={{0,16},{16,0},{1,17},{17,1},{2,18},{18,2},{3,19},{19,3},{4,20},{20... | collective-permute-start | bytes 1376264 | tf_op jit(solution)/shard_map/ppermute | solution.py:19
  221.9 30.5 %collective-permute-start.35 = (bf16[24,7168]{1,0:T(8,128)(2,1)S(1)}, bf16[24,7168]{1,0:T(8,128)(2,1)S(1)}, u32[]{:S(2)}, u32[]{:S(2)}) collective-permute-start(bf16[24,7168]{1,0:T(8,128)(2,1)S(1)} %fusion.72), channel_id=1, source_target_pairs={{0,2},{2,0},{1,3},{3,1},{4,6},{6,4},{5,7},{7,5},{8,10},{10,8},{9,1... | collective-permute-start | bytes 1032200 | tf_op jit(solution)/shard_map/ppermute | solution.py:13
  223.5 16.8 %collective-permute-start.37 = (bf16[24,7168]{1,0:T(8,128)(2,1)S(1)}, bf16[24,7168]{1,0:T(8,128)(2,1)S(1)}, u32[]{:S(2)}, u32[]{:S(2)}) collective-permute-start(bf16[24,7168]{1,0:T(8,128)(2,1)S(1)} %fusion.73), channel_id=1, source_target_pairs={{0,2},{2,0},{1,3},{3,1},{4,6},{6,4},{5,7},{7,5},{8,10},{10,8},{9,1... | collective-permute-start | bytes 1032200 | tf_op jit(solution)/shard_map/ppermute | solution.py:13
  224.2 23.6 %collective-permute-start.40 = (bf16[24,7168]{1,0:T(8,128)(2,1)S(1)}, bf16[24,7168]{1,0:T(8,128)(2,1)S(1)}, u32[]{:S(2)}, u32[]{:S(2)}) collective-permute-start(bf16[24,7168]{1,0:T(8,128)(2,1)S(1)} %fusion.74), channel_id=1, source_target_pairs={{0,2},{2,0},{1,3},{3,1},{4,6},{6,4},{5,7},{7,5},{8,10},{10,8},{9,1... | collective-permute-start | bytes 1032200 | tf_op jit(solution)/shard_map/ppermute | solution.py:13
  225.8 26.1 %collective-permute-start.43 = (bf16[24,7168]{1,0:T(8,128)(2,1)S(1)}, bf16[24,7168]{1,0:T(8,128)(2,1)S(1)}, u32[]{:S(2)}, u32[]{:S(2)}) collective-permute-start(bf16[24,7168]{1,0:T(8,128)(2,1)S(1)} %fusion.75), channel_id=1, source_target_pairs={{0,2},{2,0},{1,3},{3,1},{4,6},{6,4},{5,7},{7,5},{8,10},{10,8},{9,1... | collective-permute-start | bytes 1032200 | tf_op jit(solution)/shard_map/ppermute | solution.py:13
  240.4 12.1 %collective-permute-start.38 = (bf16[24,7168]{1,0:T(8,128)(2,1)S(1)}, bf16[24,7168]{1,0:T(8,128)(2,1)S(1)}, u32[]{:S(2)}, u32[]{:S(2)}) collective-permute-start(bf16[24,7168]{1,0:T(8,128)(2,1)S(1)} %fusion.55), channel_id=1, source_target_pairs={{0,4},{4,0},{8,12},{12,8},{1,5},{5,1},{9,13},{13,9},{2,6},{6,2},{1... | collective-permute-start | bytes 1032200 | tf_op jit(solution)/shard_map/ppermute | solution.py:98
  247.8 20.3 %collective-permute-start.41 = (bf16[24,7168]{1,0:T(8,128)(2,1)S(1)}, bf16[24,7168]{1,0:T(8,128)(2,1)S(1)}, u32[]{:S(2)}, u32[]{:S(2)}) collective-permute-start(bf16[24,7168]{1,0:T(8,128)(2,1)S(1)} %fusion.53), channel_id=1, source_target_pairs={{0,8},{4,12},{8,0},{12,4},{1,9},{5,13},{9,1},{13,5},{2,10},{6,14},... | collective-permute-start | bytes 1032200 | tf_op jit(solution)/shard_map/ppermute | solution.py:98
  251.9 22.2 %collective-permute-start.44 = (bf16[24,7168]{1,0:T(8,128)(2,1)S(1)}, bf16[24,7168]{1,0:T(8,128)(2,1)S(1)}, u32[]{:S(2)}, u32[]{:S(2)}) collective-permute-start(bf16[24,7168]{1,0:T(8,128)(2,1)S(1)} %fusion.51), channel_id=1, source_target_pairs={{0,12},{4,8},{8,4},{12,0},{1,13},{5,9},{9,5},{13,1},{2,14},{6,10},... | collective-permute-start | bytes 1032200 | tf_op jit(solution)/shard_map/ppermute | solution.py:98
  275.0 9.7 %collective-permute-start.45 = (bf16[1,32,7168]{2,1,0:T(8,128)(2,1)S(1)}, bf16[1,32,7168]{2,1,0:T(8,128)(2,1)S(1)}, u32[]{:S(2)}, u32[]{:S(2)}) collective-permute-start(bf16[1,32,7168]{2,1,0:T(8,128)(2,1)S(1)} %fusion.2), channel_id=1, source_target_pairs={{0,16},{16,0},{1,17},{17,1},{2,18},{18,2},{3,19},{19,3},{4,20},{20... | collective-permute-start | bytes 1376264 | tf_op jit(solution)/shard_map/ppermute | solution.py:19

commit v7 on v5

--- a/solution.py
+++ b/solution.py
@@ -130,6 +130,7 @@
     b_rows, f_totals = lax.optimization_barrier((b_rows, f_totals))
     f_out = returned(f_totals)
     b_partial = backward_rows(b_rows.reshape(-1, 2 * width), w_gate, w_up, w_down)
+    b_partial, f_out = lax.optimization_barrier((b_partial, f_out))
     b_out = returned(reduce_group(b_partial.reshape(2, 2, experts, capacity, width)))
     high = lax.Precision.HIGHEST
     f_mixed = jnp.dot(

time: 275 us -> 293 us (1.065)
  waiting for transfers between devices: 187 us -> 204 us
    ppermute x6, waiting for transfers between devices: 33.3 us -> 49.2 us  [returned(): out.append(lax.ppermute(totals[d], 'z', [(i, i ^ d) for i in range(count)]))]
    ppermute x26, waiting for transfers between devices: 105 us -> 108 us  [swap(): return lax.ppermute(value, axis, [(0, 1), (1, 0)])]
  transfers between devices with their start and end apart: 40 -> 40, of which waited for: 25 -> 28; matrix products, arithmetic and copies ran while one was open for 8% -> 10% of each run, Pallas kernels for 0% -> 0%
where the time goes in v7:
time: 293 us; the launch traced here: 292 us
  waiting for transfers between devices  204 us (70%)
  starting transfers between devices  39.1 us (13%)
  other arithmetic  20.6 us (7%)
  matrix products  18.9 us (6%)
  local copies, waits for them, and re-layouts  8.64 us (3%)
    ppermute x26, waiting for transfers between devices, swap(): return lax.ppermute(value, axis, [(0, 1), (1, 0)])  108 us
    ppermute x6, waiting for transfers between devices, returned(): out.append(lax.ppermute(totals[d], 'z', [(i, i ^ d) for i in range(count)]))  49.2 us
    ppermute x6, waiting for transfers between devices, dispatch(): received = lax.ppermute(slots[d], 'z', [(i, i ^ d) for i in range(count)])  37.3 us
    ppermute x26, starting transfers between devices, swap(): return lax.ppermute(value, axis, [(0, 1), (1, 0)])  21.4 us
    ppermute x2, waiting for transfers between devices, passed_along(): return lax.ppermute(value, axis, pairs)  9.06 us
    another operation x8, other arithmetic, dispatch(): pieces.append(jnp.stack([across, swap(across, 'c')]))  8.07 us
    ppermute x6, starting transfers between devices, dispatch(): received = lax.ppermute(slots[d], 'z', [(i, i ^ d) for i in range(count)])  7.38 us
    ppermute x6, starting transfers between devices, returned(): out.append(lax.ppermute(totals[d], 'z', [(i, i ^ d) for i in range(count)]))  7.1 us
  transfers between devices with their start and end apart: 40, of which 28 were waited for; matrix products, arithmetic and copies ran while one was open for 10% of the time, Pallas kernels for 0%

profile of v7, /device:TPU:16, one launch (start us, length us, event | category | flops | bytes accessed | tf_op | source)
XLA Modules:
  0.0 292.3 jit_solution(11062088301854288121)
XLA Ops:
  3.0 1.6 convolution_convert_fusion.2
  4.7 1.6 collective-permute-start.13
  6.7 1.6 collective-permute-start.19
  8.3 1.5 collective-permute-start.11
  11.9 2.5 collective-permute-start.2
  14.4 2.9 collective-permute-done.11
  17.3 1.5 collective-permute-start
  19.9 1.5 collective-permute-done.13
  22.3 10.5 %collective-permute-done = bf16[24,14336]{1,0:T(8,128)(2,1)S(1)} collective-permute-done((bf16[24,14336]{1,0:T(8,128)(2,1)S(1)}, bf16[24,14336]{1,0:T(8,128)(2,1)S(1)}, u32[]{:S(2)}, u32[]{:S(2)}) %collective-permute-start) | collective-permute-done | bytes 688160 | tf_op jit(solution)/shard_map/ppermute | solution.py:13
  32.8 1.5 collective-permute-start.14
  36.0 5.1 %collective-permute-done.14 = bf16[24,7168]{1,0:T(8,128)(2,1)S(1)} collective-permute-done((bf16[24,7168]{1,0:T(8,128)(2,1)}, bf16[24,7168]{1,0:T(8,128)(2,1)S(1)}, u32[]{:S(2)}, u32[]{:S(2)}) %collective-permute-start.14) | collective-permute-done | bytes 344096 | tf_op jit(solution)/shard_map/ppermute | solution.py:13
  41.1 1.5 collective-permute-start.17
  43.8 6.0 %collective-permute-done.17 = bf16[24,7168]{1,0:T(8,128)(2,1)S(1)} collective-permute-done((bf16[24,7168]{1,0:T(8,128)(2,1)S(1)}, bf16[24,7168]{1,0:T(8,128)(2,1)S(1)}, u32[]{:S(2)}, u32[]{:S(2)}) %collective-permute-start.17) | collective-permute-done | bytes 344096 | tf_op jit(solution)/shard_map/ppermute | solution.py:13
  49.8 1.6 collective-permute-start.20
  51.5 5.5 %collective-permute-done.20 = bf16[24,7168]{1,0:T(8,128)(2,1)S(1)} collective-permute-done((bf16[24,7168]{1,0:T(8,128)(2,1)S(1)}, bf16[24,7168]{1,0:T(8,128)(2,1)S(1)}, u32[]{:S(2)}, u32[]{:S(2)}) %collective-permute-start.20) | collective-permute-done | bytes 344096 | tf_op jit(solution)/shard_map/ppermute | solution.py:13
  57.8 1.3 collective-permute-done.15
  59.9 21.7 %collective-permute-done.5 = bf16[24,14336]{1,0:T(8,128)(2,1)} collective-permute-done((bf16[24,14336]{1,0:T(8,128)(2,1)S(1)}, bf16[24,14336]{1,0:T(8,128)(2,1)}, u32[]{:S(2)}, u32[]{:S(2)}) %collective-permute-start.5) | collective-permute-done | bytes 688160 | tf_op jit(solution)/shard_map/ppermute | solution.py:77
  81.6 1.5 collective-permute-start.3
  83.1 14.0 %collective-permute-done.8 = bf16[24,14336]{1,0:T(8,128)(2,1)} collective-permute-done((bf16[24,14336]{1,0:T(8,128)(2,1)S(1)}, bf16[24,14336]{1,0:T(8,128)(2,1)}, u32[]{:S(2)}, u32[]{:S(2)}) %collective-permute-start.8) | collective-permute-done | bytes 688160 | tf_op jit(solution)/shard_map/ppermute | solution.py:77
  97.1 1.5 collective-permute-start.6
  100.8 1.6 copy-done
  102.4 1.6 fusion.19
  104.4 1.6 fusion.44
  106.5 1.6 convolution_convert_fusion.1
  108.5 1.5 fusion.83
  110.6 5.2 %collective-permute-done.6 = bf16[24,14336]{1,0:T(8,128)(2,1)} collective-permute-done((bf16[24,14336]{1,0:T(8,128)(2,1)}, bf16[24,14336]{1,0:T(8,128)(2,1)}, u32[]{:S(2)}, u32[]{:S(2)}) %collective-permute-start.6) | collective-permute-done | bytes 688160 | tf_op jit(solution)/shard_map/ppermute | solution.py:13
  115.8 1.5 fusion.82
  117.4 10.8 %collective-permute-done.9 = bf16[24,14336]{1,0:T(8,128)(2,1)} collective-permute-done((bf16[24,14336]{1,0:T(8,128)(2,1)}, bf16[24,14336]{1,0:T(8,128)(2,1)}, u32[]{:S(2)}, u32[]{:S(2)}) %collective-permute-start.9) | collective-permute-done | bytes 688160 | tf_op jit(solution)/shard_map/ppermute | solution.py:13
  128.2 1.5 fusion.81
  129.8 1.6 maximum_bitcast_fusion
  134.3 1.6 collective-permute-start.23
  136.4 1.5 collective-permute-start.25
  138.4 1.5 pad_maximum_fusion
  139.9 5.4 %collective-permute-done.23 = bf16[24,7168]{1,0:T(8,128)(2,1)S(1)} collective-permute-done((bf16[24,7168]{1,0:T(8,128)(2,1)S(1)}, bf16[24,7168]{1,0:T(8,128)(2,1)S(1)}, u32[]{:S(2)}, u32[]{:S(2)}) %collective-permute-start.23) | collective-permute-done | bytes 344096 | tf_op jit(solution)/shard_map/ppermute | solution.py:13
  145.3 7.4 %collective-permute-done.24 = bf16[24,7168]{1,0:T(8,128)(2,1)S(1)} collective-permute-done((bf16[24,7168]{1,0:T(8,128)(2,1)S(1)}, bf16[24,7168]{1,0:T(8,128)(2,1)S(1)}, u32[]{:S(2)}, u32[]{:S(2)}) %collective-permute-start.24) | collective-permute-done | bytes 344096 | tf_op jit(solution)/shard_map/ppermute | solution.py:13
  152.6 7.4 %collective-permute-done.25 = bf16[24,7168]{1,0:T(8,128)(2,1)S(1)} collective-permute-done((bf16[24,7168]{1,0:T(8,128)(2,1)S(1)}, bf16[24,7168]{1,0:T(8,128)(2,1)S(1)}, u32[]{:S(2)}, u32[]{:S(2)}) %collective-permute-start.25) | collective-permute-done | bytes 344096 | tf_op jit(solution)/shard_map/ppermute | solution.py:13
  160.0 6.6 %collective-permute-done.26 = bf16[24,7168]{1,0:T(8,128)(2,1)S(1)} collective-permute-done((bf16[24,7168]{1,0:T(8,128)(2,1)S(1)}, bf16[24,7168]{1,0:T(8,128)(2,1)S(1)}, u32[]{:S(2)}, u32[]{:S(2)}) %collective-permute-start.26) | collective-permute-done | bytes 344096 | tf_op jit(solution)/shard_map/ppermute | solution.py:13
  167.7 1.9 copy.35
  169.7 1.6 fusion.4
  171.3 1.6 fusion.6
  172.9 1.5 collective-permute-start.27
  174.9 1.6 collective-permute-start.29
  176.5 1.6 fusion.39
  178.2 1.6 fusion.16
  179.8 3.8 %add_convert_fusion = bf16[384,7168]{1,0:T(8,128)(2,1)S(1)} fusion(f32[384,7168]{1,0:T(8,128)S(1)} %fusion.16, bf16[1,7168,256]{2,1,0:T(8,128)(2,1)} %param.18, f32[384,256]{1,0:T(8,128)S(1)} %fusion.4, f32[384,256]{1,0:T(8,128)S(1)} %fusion.6), kind=kOutput, calls=%fused_computation.2 | convolution fusion | flops 1415380992 | bytes 20971520 | tf_op jit(solution)/shard_map/dot_general | solution.py:64
  183.6 3.8 %collective-permute-done.27 = bf16[24,7168]{1,0:T(8,128)(2,1)} collective-permute-done((bf16[24,7168]{1,0:T(8,128)(2,1)}, bf16[24,7168]{1,0:T(8,128)(2,1)}, u32[]{:S(2)}, u32[]{:S(2)}) %collective-permute-start.27) | collective-permute-done | bytes 344096 | tf_op jit(solution)/shard_map/ppermute | solution.py:97
  187.4 11.1 %collective-permute-done.28 = bf16[24,7168]{1,0:T(8,128)(2,1)} collective-permute-done((bf16[24,7168]{1,0:T(8,128)(2,1)}, bf16[24,7168]{1,0:T(8,128)(2,1)}, u32[]{:S(2)}, u32[]{:S(2)}) %collective-permute-start.28) | collective-permute-done | bytes 344096 | tf_op jit(solution)/shard_map/ppermute | solution.py:97
  198.5 7.5 %collective-permute-done.29 = bf16[24,7168]{1,0:T(8,128)(2,1)} collective-permute-done((bf16[24,7168]{1,0:T(8,128)(2,1)}, bf16[24,7168]{1,0:T(8,128)(2,1)}, u32[]{:S(2)}, u32[]{:S(2)}) %collective-permute-start.29) | collective-permute-done | bytes 344096 | tf_op jit(solution)/shard_map/ppermute | solution.py:97
  205.9 1.4 pad_maximum_fusion.6
  207.8 5.1 %collective-permute-done.31 = bf16[2,4,24,7168]{3,2,1,0:T(8,128)(2,1)S(1)} collective-permute-done((bf16[2,4,24,7168]{3,2,1,0:T(8,128)(2,1)S(1)}, bf16[2,4,24,7168]{3,2,1,0:T(8,128)(2,1)S(1)}, u32[]{:S(2)}, u32[]{:S(2)}) %collective-permute-start.31) | collective-permute-done | bytes 2752544 | tf_op jit(solution)/shard_map/ppermute | solution.py:13
  214.0 1.5 collective-permute-start.32
  216.1 1.4 collective-permute-start.35
  218.1 6.8 %collective-permute-done.32 = bf16[24,7168]{1,0:T(8,128)(2,1)S(1)} collective-permute-done((bf16[24,7168]{1,0:T(8,128)(2,1)S(1)}, bf16[24,7168]{1,0:T(8,128)(2,1)S(1)}, u32[]{:S(2)}, u32[]{:S(2)}) %collective-permute-start.32) | collective-permute-done | bytes 344096 | tf_op jit(solution)/shard_map/ppermute | solution.py:13
  224.9 7.4 %collective-permute-done.33 = bf16[24,7168]{1,0:T(8,128)(2,1)S(1)} collective-permute-done((bf16[24,7168]{1,0:T(8,128)(2,1)S(1)}, bf16[24,7168]{1,0:T(8,128)(2,1)S(1)}, u32[]{:S(2)}, u32[]{:S(2)}) %collective-permute-start.33) | collective-permute-done | bytes 344096 | tf_op jit(solution)/shard_map/ppermute | solution.py:13
  232.3 7.4 %collective-permute-done.35 = bf16[24,7168]{1,0:T(8,128)(2,1)S(1)} collective-permute-done((bf16[24,7168]{1,0:T(8,128)(2,1)S(1)}, bf16[24,7168]{1,0:T(8,128)(2,1)S(1)}, u32[]{:S(2)}, u32[]{:S(2)}) %collective-permute-start.35) | collective-permute-done | bytes 344096 | tf_op jit(solution)/shard_map/ppermute | solution.py:13
  239.7 6.6 %collective-permute-done.37 = bf16[24,7168]{1,0:T(8,128)(2,1)S(1)} collective-permute-done((bf16[24,7168]{1,0:T(8,128)(2,1)S(1)}, bf16[24,7168]{1,0:T(8,128)(2,1)S(1)}, u32[]{:S(2)}, u32[]{:S(2)}) %collective-permute-start.37) | collective-permute-done | bytes 344096 | tf_op jit(solution)/shard_map/ppermute | solution.py:13
  246.6 1.9 collective-permute-start.36
  248.5 1.6 collective-permute-start.38
  250.8 1.6 collective-permute-start.30
  252.4 7.1 %collective-permute-done.34 = bf16[24,7168]{1,0:T(8,128)(2,1)S(1)} collective-permute-done((bf16[24,7168]{1,0:T(8,128)(2,1)S(1)}, bf16[24,7168]{1,0:T(8,128)(2,1)S(1)}, u32[]{:S(2)}, u32[]{:S(2)}) %collective-permute-start.34) | collective-permute-done | bytes 344096 | tf_op jit(solution)/shard_map/ppermute | solution.py:97
  259.5 12.3 %collective-permute-done.36 = bf16[24,7168]{1,0:T(8,128)(2,1)S(1)} collective-permute-done((bf16[24,7168]{1,0:T(8,128)(2,1)S(1)}, bf16[24,7168]{1,0:T(8,128)(2,1)S(1)}, u32[]{:S(2)}, u32[]{:S(2)}) %collective-permute-start.36) | collective-permute-done | bytes 344096 | tf_op jit(solution)/shard_map/ppermute | solution.py:97
  271.8 7.5 %collective-permute-done.38 = bf16[24,7168]{1,0:T(8,128)(2,1)S(1)} collective-permute-done((bf16[24,7168]{1,0:T(8,128)(2,1)S(1)}, bf16[24,7168]{1,0:T(8,128)(2,1)S(1)}, u32[]{:S(2)}, u32[]{:S(2)}) %collective-permute-start.38) | collective-permute-done | bytes 344096 | tf_op jit(solution)/shard_map/ppermute | solution.py:97
  280.1 1.6 collective-permute-start.39
  281.7 9.1 %collective-permute-done.39 = bf16[1,32,7168]{2,1,0:T(8,128)(2,1)S(1)} collective-permute-done((bf16[1,32,7168]{2,1,0:T(8,128)(2,1)S(1)}, bf16[1,32,7168]{2,1,0:T(8,128)(2,1)S(1)}, u32[]{:S(2)}, u32[]{:S(2)}) %collective-permute-start.39) | collective-permute-done | bytes 458784 | tf_op jit(solution)/shard_map/ppermute | solution.py:19
  (101 shorter events, 27.0 us)
Async XLA Ops:
  0.6 9.9 %copy-start.9 = (f32[1,32,2]{1,2,0:T(2,128)S(1)}, f32[1,32,2]{1,2,0:T(2,128)}, u32[]{:S(2)}) copy-start(f32[1,32,2]{1,2,0:T(2,128)} %param.16) | copy-start | bytes 772
  0.6 10.0 %copy-start.8 = (bf16[1,32,7168]{2,1,0:T(8,128)(2,1)S(1)}, bf16[1,32,7168]{2,1,0:T(8,128)(2,1)}, u32[]{:S(2)}) copy-start(bf16[1,32,7168]{2,1,0:T(8,128)(2,1)} %param.13) | copy-start | bytes 1376260
  0.7 10.0 %copy-start.6 = (bf16[1,32,7168]{2,1,0:T(8,128)(2,1)S(1)}, bf16[1,32,7168]{2,1,0:T(8,128)(2,1)}, u32[]{:S(2)}) copy-start(bf16[1,32,7168]{2,1,0:T(8,128)(2,1)} %param.14) | copy-start | bytes 1376260
  4.7 16.7 %collective-permute-start.13 = (bf16[24,7168]{1,0:T(8,128)(2,1)S(1)}, bf16[24,7168]{1,0:T(8,128)(2,1)}, u32[]{:S(2)}, u32[]{:S(2)}) collective-permute-start(bf16[24,7168]{1,0:T(8,128)(2,1)S(1)} %get-tuple-element.52), channel_id=1, source_target_pairs={{0,4},{4,0},{8,12},{12,8},{1,5},{5,1},{9,13},{13,9},{2,6},{6,2},{1... | collective-permute-start | bytes 1032200 | tf_op jit(solution)/shard_map/ppermute | solution.py:77
  6.4 29.2 %collective-permute-start.16 = (bf16[24,7168]{1,0:T(8,128)(2,1)S(1)}, bf16[24,7168]{1,0:T(8,128)(2,1)S(1)}, u32[]{:S(2)}, u32[]{:S(2)}) collective-permute-start(bf16[24,7168]{1,0:T(8,128)(2,1)S(1)} %get-tuple-element.51), channel_id=1, source_target_pairs={{0,8},{4,12},{8,0},{12,4},{1,9},{5,13},{9,1},{13,5},{2,10},{6,14},... | collective-permute-start | bytes 1032200 | tf_op jit(solution)/shard_map/ppermute | solution.py:77
  6.7 37.0 %collective-permute-start.19 = (bf16[24,7168]{1,0:T(8,128)(2,1)S(1)}, bf16[24,7168]{1,0:T(8,128)(2,1)S(1)}, u32[]{:S(2)}, u32[]{:S(2)}) collective-permute-start(bf16[24,7168]{1,0:T(8,128)(2,1)S(1)} %get-tuple-element.50), channel_id=1, source_target_pairs={{0,12},{4,8},{8,4},{12,0},{1,13},{5,9},{9,5},{13,1},{2,14},{6,10},... | collective-permute-start | bytes 1032200 | tf_op jit(solution)/shard_map/ppermute | solution.py:77
  8.3 9.1 %collective-permute-start.11 = (bf16[24,7168]{1,0:T(8,128)(2,1)S(1)}, bf16[24,7168]{1,0:T(8,128)(2,1)}, u32[]{:S(2)}, u32[]{:S(2)}) collective-permute-start(bf16[24,7168]{1,0:T(8,128)(2,1)S(1)} %get-tuple-element.53), channel_id=1, source_target_pairs={{0,2},{2,0},{1,3},{3,1},{4,6},{6,4},{5,7},{7,5},{8,10},{10,8},{9,1... | collective-permute-start | bytes 1032200 | tf_op jit(solution)/shard_map/ppermute | solution.py:13
  11.9 47.6 %collective-permute-start.2 = (bf16[24,14336]{1,0:T(8,128)(2,1)S(1)}, bf16[24,14336]{1,0:T(8,128)(2,1)}, u32[]{:S(2)}, u32[]{:S(2)}) collective-permute-start(bf16[24,14336]{1,0:T(8,128)(2,1)S(1)} %get-tuple-element.47), channel_id=1, source_target_pairs={{0,4},{4,0},{8,12},{12,8},{1,5},{5,1},{9,13},{13,9},{2,6},{6,2},{1... | collective-permute-start | bytes 2064392 | tf_op jit(solution)/shard_map/ppermute | solution.py:77
  17.3 15.4 %collective-permute-start = (bf16[24,14336]{1,0:T(8,128)(2,1)S(1)}, bf16[24,14336]{1,0:T(8,128)(2,1)S(1)}, u32[]{:S(2)}, u32[]{:S(2)}) collective-permute-start(bf16[24,14336]{1,0:T(8,128)(2,1)S(1)} %get-tuple-element.48), channel_id=1, source_target_pairs={{0,2},{2,0},{1,3},{3,1},{4,6},{6,4},{5,7},{7,5},{8,10},{10,8},{9,1... | collective-permute-start | bytes 2064392 | tf_op jit(solution)/shard_map/ppermute | solution.py:13
  21.5 60.2 %collective-permute-start.5 = (bf16[24,14336]{1,0:T(8,128)(2,1)S(1)}, bf16[24,14336]{1,0:T(8,128)(2,1)}, u32[]{:S(2)}, u32[]{:S(2)}) collective-permute-start(bf16[24,14336]{1,0:T(8,128)(2,1)S(1)} %get-tuple-element.46), channel_id=1, source_target_pairs={{0,8},{4,12},{8,0},{12,4},{1,9},{5,13},{9,1},{13,5},{2,10},{6,14},... | collective-permute-start | bytes 2064392 | tf_op jit(solution)/shard_map/ppermute | solution.py:77
  32.8 8.4 %collective-permute-start.14 = (bf16[24,7168]{1,0:T(8,128)(2,1)}, bf16[24,7168]{1,0:T(8,128)(2,1)S(1)}, u32[]{:S(2)}, u32[]{:S(2)}) collective-permute-start(bf16[24,7168]{1,0:T(8,128)(2,1)} %collective-permute-done.13), channel_id=1, source_target_pairs={{0,2},{2,0},{1,3},{3,1},{4,6},{6,4},{5,7},{7,5},{8,10},{10,8},{9,1... | collective-permute-start | bytes 1032200 | tf_op jit(solution)/shard_map/ppermute | solution.py:13
  35.6 61.6 %collective-permute-start.8 = (bf16[24,14336]{1,0:T(8,128)(2,1)S(1)}, bf16[24,14336]{1,0:T(8,128)(2,1)}, u32[]{:S(2)}, u32[]{:S(2)}) collective-permute-start(bf16[24,14336]{1,0:T(8,128)(2,1)S(1)} %get-tuple-element.45), channel_id=1, source_target_pairs={{0,12},{4,8},{8,4},{12,0},{1,13},{5,9},{9,5},{13,1},{2,14},{6,10},... | collective-permute-start | bytes 2064392 | tf_op jit(solution)/shard_map/ppermute | solution.py:77
  41.1 8.7 %collective-permute-start.17 = (bf16[24,7168]{1,0:T(8,128)(2,1)S(1)}, bf16[24,7168]{1,0:T(8,128)(2,1)S(1)}, u32[]{:S(2)}, u32[]{:S(2)}) collective-permute-start(bf16[24,7168]{1,0:T(8,128)(2,1)S(1)} %collective-permute-done.16), channel_id=1, source_target_pairs={{0,2},{2,0},{1,3},{3,1},{4,6},{6,4},{5,7},{7,5},{8,10},{10,8},{9,1... | collective-permute-start | bytes 1032200 | tf_op jit(solution)/shard_map/ppermute | solution.py:13
  43.7 13.4 %collective-permute-start.12 = (bf16[2,24,7168]{2,1,0:T(8,128)(2,1)S(1)}, bf16[2,24,7168]{2,1,0:T(8,128)(2,1)S(1)}, u32[]{:S(2)}, u32[]{:S(2)}) collective-permute-start(bf16[2,24,7168]{2,1,0:T(8,128)(2,1)S(1)} %get-tuple-element.63), channel_id=1, source_target_pairs={{0,1},{1,0},{2,3},{3,2},{4,5},{5,4},{6,7},{7,6},{8,9},{9,8},{10,11... | collective-permute-start | bytes 2064392 | tf_op jit(solution)/shard_map/ppermute | solution.py:13
  49.8 7.2 %collective-permute-start.20 = (bf16[24,7168]{1,0:T(8,128)(2,1)S(1)}, bf16[24,7168]{1,0:T(8,128)(2,1)S(1)}, u32[]{:S(2)}, u32[]{:S(2)}) collective-permute-start(bf16[24,7168]{1,0:T(8,128)(2,1)S(1)} %collective-permute-done.19), channel_id=1, source_target_pairs={{0,2},{2,0},{1,3},{3,1},{4,6},{6,4},{5,7},{7,5},{8,10},{10,8},{9,1... | collective-permute-start | bytes 1032200 | tf_op jit(solution)/shard_map/ppermute | solution.py:13
  57.0 2.1 collective-permute-start.15
  57.1 41.5 %collective-permute-start.18 = (bf16[2,24,7168]{2,1,0:T(8,128)(2,1)S(1)}, bf16[2,24,7168]{2,1,0:T(8,128)(2,1)S(1)}, u32[]{:S(2)}, u32[]{:S(2)}) collective-permute-start(bf16[2,24,7168]{2,1,0:T(8,128)(2,1)S(1)} %get-tuple-element.67), channel_id=1, source_target_pairs={{0,1},{1,0},{2,3},{3,2},{4,5},{5,4},{6,7},{7,6},{8,9},{9,8},{10,11... | collective-permute-start | bytes 2064392 | tf_op jit(solution)/shard_map/ppermute | solution.py:13
  59.2 40.1 %collective-permute-start.21 = (bf16[2,24,7168]{2,1,0:T(8,128)(2,1)S(1)}, bf16[2,24,7168]{2,1,0:T(8,128)(2,1)S(1)}, u32[]{:S(2)}, u32[]{:S(2)}) collective-permute-start(bf16[2,24,7168]{2,1,0:T(8,128)(2,1)S(1)} %get-tuple-element.69), channel_id=1, source_target_pairs={{0,1},{1,0},{2,3},{3,2},{4,5},{5,4},{6,7},{7,6},{8,9},{9,8},{10,11... | collective-permute-start | bytes 2064392 | tf_op jit(solution)/shard_map/ppermute | solution.py:13
  59.5 70.3 %collective-permute-start.1 = (bf16[2,24,14336]{2,1,0:T(8,128)(2,1)}, bf16[2,24,14336]{2,1,0:T(8,128)(2,1)}, u32[]{:S(2)}, u32[]{:S(2)}) collective-permute-start(bf16[2,24,14336]{2,1,0:T(8,128)(2,1)} %get-tuple-element.55), channel_id=1, source_target_pairs={{0,1},{1,0},{2,3},{3,2},{4,5},{5,4},{6,7},{7,6},{8,9},{9,8},{10,11... | collective-permute-start | bytes 4128776 | tf_op jit(solution)/shard_map/ppermute | solution.py:13
  81.6 26.9 %collective-permute-start.3 = (bf16[24,14336]{1,0:T(8,128)(2,1)}, bf16[24,14336]{1,0:T(8,128)(2,1)}, u32[]{:S(2)}, u32[]{:S(2)}) collective-permute-start(bf16[24,14336]{1,0:T(8,128)(2,1)} %collective-permute-done.2), channel_id=1, source_target_pairs={{0,2},{2,0},{1,3},{3,1},{4,6},{6,4},{5,7},{7,5},{8,10},{10,8},{9,1... | collective-permute-start | bytes 2064392 | tf_op jit(solution)/shard_map/ppermute | solution.py:13
  97.1 18.7 %collective-permute-start.6 = (bf16[24,14336]{1,0:T(8,128)(2,1)}, bf16[24,14336]{1,0:T(8,128)(2,1)}, u32[]{:S(2)}, u32[]{:S(2)}) collective-permute-start(bf16[24,14336]{1,0:T(8,128)(2,1)} %collective-permute-done.5), channel_id=1, source_target_pairs={{0,2},{2,0},{1,3},{3,1},{4,6},{6,4},{5,7},{7,5},{8,10},{10,8},{9,1... | collective-permute-start | bytes 2064392 | tf_op jit(solution)/shard_map/ppermute | solution.py:13
  98.6 29.6 %collective-permute-start.9 = (bf16[24,14336]{1,0:T(8,128)(2,1)}, bf16[24,14336]{1,0:T(8,128)(2,1)}, u32[]{:S(2)}, u32[]{:S(2)}) collective-permute-start(bf16[24,14336]{1,0:T(8,128)(2,1)} %collective-permute-done.8), channel_id=1, source_target_pairs={{0,2},{2,0},{1,3},{3,1},{4,6},{6,4},{5,7},{7,5},{8,10},{10,8},{9,1... | collective-permute-start | bytes 2064392 | tf_op jit(solution)/shard_map/ppermute | solution.py:13
  100.4 2.0 copy-start
  102.4 2.0 copy-start.1
  104.4 2.0 copy-start.3
  108.5 24.7 %collective-permute-start.22 = (bf16[2,4,24,7168]{3,2,1,0:T(8,128)(2,1)S(1)}, bf16[2,4,24,7168]{3,2,1,0:T(8,128)(2,1)S(1)}, u32[]{:S(2)}, u32[]{:S(2)}) collective-permute-start(bf16[2,4,24,7168]{3,2,1,0:T(8,128)(2,1)S(1)} %bitcast.210), channel_id=1, source_target_pairs={{0,1},{1,0},{2,3},{3,2},{4,5},{5,4},{6,7},{7,6},{8,9},{9,8},{10,11... | collective-permute-start | bytes 8257544 | tf_op jit(solution)/shard_map/ppermute | solution.py:13
  110.0 21.3 %collective-permute-start.4 = (bf16[2,24,14336]{2,1,0:T(8,128)(2,1)S(1)}, bf16[2,24,14336]{2,1,0:T(8,128)(2,1)S(1)}, u32[]{:S(2)}, u32[]{:S(2)}) collective-permute-start(bf16[2,24,14336]{2,1,0:T(8,128)(2,1)S(1)} %get-tuple-element.57), channel_id=1, source_target_pairs={{0,1},{1,0},{2,3},{3,2},{4,5},{5,4},{6,7},{7,6},{8,9},{9,8},{10,11... | collective-permute-start | bytes 4128776 | tf_op jit(solution)/shard_map/ppermute | solution.py:13
  117.3 14.4 %collective-permute-start.7 = (bf16[2,24,14336]{2,1,0:T(8,128)(2,1)S(1)}, bf16[2,24,14336]{2,1,0:T(8,128)(2,1)S(1)}, u32[]{:S(2)}, u32[]{:S(2)}) collective-permute-start(bf16[2,24,14336]{2,1,0:T(8,128)(2,1)S(1)} %get-tuple-element.59), channel_id=1, source_target_pairs={{0,1},{1,0},{2,3},{3,2},{4,5},{5,4},{6,7},{7,6},{8,9},{9,8},{10,11... | collective-permute-start | bytes 4128776 | tf_op jit(solution)/shard_map/ppermute | solution.py:13
  129.7 3.2 %collective-permute-start.10 = (bf16[2,24,14336]{2,1,0:T(8,128)(2,1)S(1)}, bf16[2,24,14336]{2,1,0:T(8,128)(2,1)S(1)}, u32[]{:S(2)}, u32[]{:S(2)}) collective-permute-start(bf16[2,24,14336]{2,1,0:T(8,128)(2,1)S(1)} %get-tuple-element.61), channel_id=1, source_target_pairs={{0,1},{1,0},{2,3},{3,2},{4,5},{5,4},{6,7},{7,6},{8,9},{9,8},{10,11... | collective-permute-start | bytes 4128776 | tf_op jit(solution)/shard_map/ppermute | solution.py:13
  134.3 11.0 %collective-permute-start.23 = (bf16[24,7168]{1,0:T(8,128)(2,1)S(1)}, bf16[24,7168]{1,0:T(8,128)(2,1)S(1)}, u32[]{:S(2)}, u32[]{:S(2)}) collective-permute-start(bf16[24,7168]{1,0:T(8,128)(2,1)S(1)} %get-tuple-element.43), channel_id=1, source_target_pairs={{0,2},{2,0},{1,3},{3,1},{4,6},{6,4},{5,7},{7,5},{8,10},{10,8},{9,1... | collective-permute-start | bytes 1032200 | tf_op jit(solution)/shard_map/ppermute | solution.py:13
  135.9 16.8 %collective-permute-start.24 = (bf16[24,7168]{1,0:T(8,128)(2,1)S(1)}, bf16[24,7168]{1,0:T(8,128)(2,1)S(1)}, u32[]{:S(2)}, u32[]{:S(2)}) collective-permute-start(bf16[24,7168]{1,0:T(8,128)(2,1)S(1)} %get-tuple-element.42), channel_id=1, source_target_pairs={{0,2},{2,0},{1,3},{3,1},{4,6},{6,4},{5,7},{7,5},{8,10},{10,8},{9,1... | collective-permute-start | bytes 1032200 | tf_op jit(solution)/shard_map/ppermute | solution.py:13
  136.4 23.6 %collective-permute-start.25 = (bf16[24,7168]{1,0:T(8,128)(2,1)S(1)}, bf16[24,7168]{1,0:T(8,128)(2,1)S(1)}, u32[]{:S(2)}, u32[]{:S(2)}) collective-permute-start(bf16[24,7168]{1,0:T(8,128)(2,1)S(1)} %get-tuple-element.41), channel_id=1, source_target_pairs={{0,2},{2,0},{1,3},{3,1},{4,6},{6,4},{5,7},{7,5},{8,10},{10,8},{9,1... | collective-permute-start | bytes 1032200 | tf_op jit(solution)/shard_map/ppermute | solution.py:13
  137.9 28.7 %collective-permute-start.26 = (bf16[24,7168]{1,0:T(8,128)(2,1)S(1)}, bf16[24,7168]{1,0:T(8,128)(2,1)S(1)}, u32[]{:S(2)}, u32[]{:S(2)}) collective-permute-start(bf16[24,7168]{1,0:T(8,128)(2,1)S(1)} %get-tuple-element.40), channel_id=1, source_target_pairs={{0,2},{2,0},{1,3},{3,1},{4,6},{6,4},{5,7},{7,5},{8,10},{10,8},{9,1... | collective-permute-start | bytes 1032200 | tf_op jit(solution)/shard_map/ppermute | solution.py:13
  167.6 2.0 copy-start.4
  171.3 5.2 %copy-start.2 = (bf16[1,7168,256]{2,1,0:T(8,128)(2,1)S(1)}, bf16[1,7168,256]{2,1,0:T(8,128)(2,1)}, u32[]{:S(2)}) copy-start(bf16[1,7168,256]{2,1,0:T(8,128)(2,1)} %param.18) | copy-start | bytes 11010052
  172.9 14.5 %collective-permute-start.27 = (bf16[24,7168]{1,0:T(8,128)(2,1)}, bf16[24,7168]{1,0:T(8,128)(2,1)}, u32[]{:S(2)}, u32[]{:S(2)}) collective-permute-start(bf16[24,7168]{1,0:T(8,128)(2,1)} %get-tuple-element.11), channel_id=1, source_target_pairs={{0,4},{4,0},{8,12},{12,8},{1,5},{5,1},{9,13},{13,9},{2,6},{6,2},{1... | collective-permute-start | bytes 1032200 | tf_op jit(solution)/shard_map/ppermute | solution.py:97
  174.5 24.0 %collective-permute-start.28 = (bf16[24,7168]{1,0:T(8,128)(2,1)}, bf16[24,7168]{1,0:T(8,128)(2,1)}, u32[]{:S(2)}, u32[]{:S(2)}) collective-permute-start(bf16[24,7168]{1,0:T(8,128)(2,1)} %get-tuple-element.12), channel_id=1, source_target_pairs={{0,8},{4,12},{8,0},{12,4},{1,9},{5,13},{9,1},{13,5},{2,10},{6,14},... | collective-permute-start | bytes 1032200 | tf_op jit(solution)/shard_map/ppermute | solution.py:97
  174.9 31.0 %collective-permute-start.29 = (bf16[24,7168]{1,0:T(8,128)(2,1)}, bf16[24,7168]{1,0:T(8,128)(2,1)}, u32[]{:S(2)}, u32[]{:S(2)}) collective-permute-start(bf16[24,7168]{1,0:T(8,128)(2,1)} %get-tuple-element.13), channel_id=1, source_target_pairs={{0,12},{4,8},{8,4},{12,0},{1,13},{5,9},{9,5},{13,1},{2,14},{6,10},... | collective-permute-start | bytes 1032200 | tf_op jit(solution)/shard_map/ppermute | solution.py:97
  207.7 5.2 %collective-permute-start.31 = (bf16[2,4,24,7168]{3,2,1,0:T(8,128)(2,1)S(1)}, bf16[2,4,24,7168]{3,2,1,0:T(8,128)(2,1)S(1)}, u32[]{:S(2)}, u32[]{:S(2)}) collective-permute-start(bf16[2,4,24,7168]{3,2,1,0:T(8,128)(2,1)S(1)} %bitcast.211), channel_id=1, source_target_pairs={{0,1},{1,0},{2,3},{3,2},{4,5},{5,4},{6,7},{7,6},{8,9},{9,8},{10,11... | collective-permute-start | bytes 8257544 | tf_op jit(solution)/shard_map/ppermute | solution.py:13
  214.0 11.0 %collective-permute-start.32 = (bf16[24,7168]{1,0:T(8,128)(2,1)S(1)}, bf16[24,7168]{1,0:T(8,128)(2,1)S(1)}, u32[]{:S(2)}, u32[]{:S(2)}) collective-permute-start(bf16[24,7168]{1,0:T(8,128)(2,1)S(1)} %get-tuple-element.36), channel_id=1, source_target_pairs={{0,2},{2,0},{1,3},{3,1},{4,6},{6,4},{5,7},{7,5},{8,10},{10,8},{9,1... | collective-permute-start | bytes 1032200 | tf_op jit(solution)/shard_map/ppermute | solution.py:13
  215.5 16.8 %collective-permute-start.33 = (bf16[24,7168]{1,0:T(8,128)(2,1)S(1)}, bf16[24,7168]{1,0:T(8,128)(2,1)S(1)}, u32[]{:S(2)}, u32[]{:S(2)}) collective-permute-start(bf16[24,7168]{1,0:T(8,128)(2,1)S(1)} %get-tuple-element.39), channel_id=1, source_target_pairs={{0,2},{2,0},{1,3},{3,1},{4,6},{6,4},{5,7},{7,5},{8,10},{10,8},{9,1... | collective-permute-start | bytes 1032200 | tf_op jit(solution)/shard_map/ppermute | solution.py:13
  216.1 23.6 %collective-permute-start.35 = (bf16[24,7168]{1,0:T(8,128)(2,1)S(1)}, bf16[24,7168]{1,0:T(8,128)(2,1)S(1)}, u32[]{:S(2)}, u32[]{:S(2)}) collective-permute-start(bf16[24,7168]{1,0:T(8,128)(2,1)S(1)} %get-tuple-element.38), channel_id=1, source_target_pairs={{0,2},{2,0},{1,3},{3,1},{4,6},{6,4},{5,7},{7,5},{8,10},{10,8},{9,1... | collective-permute-start | bytes 1032200 | tf_op jit(solution)/shard_map/ppermute | solution.py:13
  217.5 28.7 %collective-permute-start.37 = (bf16[24,7168]{1,0:T(8,128)(2,1)S(1)}, bf16[24,7168]{1,0:T(8,128)(2,1)S(1)}, u32[]{:S(2)}, u32[]{:S(2)}) collective-permute-start(bf16[24,7168]{1,0:T(8,128)(2,1)S(1)} %get-tuple-element.37), channel_id=1, source_target_pairs={{0,2},{2,0},{1,3},{3,1},{4,6},{6,4},{5,7},{7,5},{8,10},{10,8},{9,1... | collective-permute-start | bytes 1032200 | tf_op jit(solution)/shard_map/ppermute | solution.py:13
  246.3 3.8 %copy-start.5 = (bf16[1,32,7168]{2,1,0:T(8,128)(2,1)S(1)}, bf16[1,32,7168]{2,1,0:T(8,128)(2,1)}, u32[]{:S(2)}) copy-start(bf16[1,32,7168]{2,1,0:T(8,128)(2,1)} %param.10) | copy-start | bytes 1376260
  246.5 32.9 %copy-start.7 = (bf16[1,32,7168]{2,1,0:T(8,128)(2,1)S(1)}, bf16[1,32,7168]{2,1,0:T(8,128)(2,1)}, u32[]{:S(2)}) copy-start(bf16[1,32,7168]{2,1,0:T(8,128)(2,1)} %param.14) | copy-start | bytes 1376260
  246.5 12.9 %collective-permute-start.34 = (bf16[24,7168]{1,0:T(8,128)(2,1)S(1)}, bf16[24,7168]{1,0:T(8,128)(2,1)S(1)}, u32[]{:S(2)}, u32[]{:S(2)}) collective-permute-start(bf16[24,7168]{1,0:T(8,128)(2,1)S(1)} %get-tuple-element.22), channel_id=1, source_target_pairs={{0,4},{4,0},{8,12},{12,8},{1,5},{5,1},{9,13},{13,9},{2,6},{6,2},{1... | collective-permute-start | bytes 1032200 | tf_op jit(solution)/shard_map/ppermute | solution.py:97
  246.6 25.2 %collective-permute-start.36 = (bf16[24,7168]{1,0:T(8,128)(2,1)S(1)}, bf16[24,7168]{1,0:T(8,128)(2,1)S(1)}, u32[]{:S(2)}, u32[]{:S(2)}) collective-permute-start(bf16[24,7168]{1,0:T(8,128)(2,1)S(1)} %get-tuple-element.21), channel_id=1, source_target_pairs={{0,8},{4,12},{8,0},{12,4},{1,9},{5,13},{9,1},{13,5},{2,10},{6,14},... | collective-permute-start | bytes 1032200 | tf_op jit(solution)/shard_map/ppermute | solution.py:97
  248.5 30.7 %collective-permute-start.38 = (bf16[24,7168]{1,0:T(8,128)(2,1)S(1)}, bf16[24,7168]{1,0:T(8,128)(2,1)S(1)}, u32[]{:S(2)}, u32[]{:S(2)}) collective-permute-start(bf16[24,7168]{1,0:T(8,128)(2,1)S(1)} %get-tuple-element.23), channel_id=1, source_target_pairs={{0,12},{4,8},{8,4},{12,0},{1,13},{5,9},{9,5},{13,1},{2,14},{6,10},... | collective-permute-start | bytes 1032200 | tf_op jit(solution)/shard_map/ppermute | solution.py:97
  250.8 30.9 %collective-permute-start.30 = (bf16[1,32,7168]{2,1,0:T(8,128)(2,1)S(1)}, bf16[1,32,7168]{2,1,0:T(8,128)(2,1)S(1)}, u32[]{:S(2)}, u32[]{:S(2)}) collective-permute-start(bf16[1,32,7168]{2,1,0:T(8,128)(2,1)S(1)} %fusion.3), channel_id=1, source_target_pairs={{0,16},{16,0},{1,17},{17,1},{2,18},{18,2},{3,19},{19,3},{4,20},{20... | collective-permute-start | bytes 1376264 | tf_op jit(solution)/shard_map/ppermute | solution.py:19
  280.1 10.6 %collective-permute-start.39 = (bf16[1,32,7168]{2,1,0:T(8,128)(2,1)S(1)}, bf16[1,32,7168]{2,1,0:T(8,128)(2,1)S(1)}, u32[]{:S(2)}, u32[]{:S(2)}) collective-permute-start(bf16[1,32,7168]{2,1,0:T(8,128)(2,1)S(1)} %fusion.2), channel_id=1, source_target_pairs={{0,16},{16,0},{1,17},{17,1},{2,18},{18,2},{3,19},{19,3},{4,20},{20... | collective-permute-start | bytes 1376264 | tf_op jit(solution)/shard_map/ppermute | solution.py:19

commit v8 on v5

--- a/solution.py
+++ b/solution.py
@@ -123,14 +123,14 @@
     f_slots = into_slots(f_select, fwd_input[0]).reshape(experts, capacity, width)
     b_joined = jnp.concatenate([bwd_input[0], bwd_grad[0]], axis=1)
     b_slots = into_slots(b_select, b_joined).reshape(experts, capacity, 2 * width)
+    b_rows = dispatch(b_slots)
     f_rows = dispatch(f_slots)
-    b_rows = dispatch(b_slots)
+    b_partial = backward_rows(b_rows.reshape(-1, 2 * width), w_gate, w_up, w_down)
+    b_totals = reduce_group(b_partial.reshape(2, 2, experts, capacity, width))
+    f_rows, b_totals = lax.optimization_barrier((f_rows, b_totals))
+    b_out = returned(b_totals)
     f_partial = forward_rows(f_rows.reshape(-1, width), w_gate, w_up, w_down)
-    f_totals = reduce_group(f_partial.reshape(2, 2, experts, capacity, width))
-    b_rows, f_totals = lax.optimization_barrier((b_rows, f_totals))
-    f_out = returned(f_totals)
-    b_partial = backward_rows(b_rows.reshape(-1, 2 * width), w_gate, w_up, w_down)
-    b_out = returned(reduce_group(b_partial.reshape(2, 2, experts, capacity, width)))
+    f_out = returned(reduce_group(f_partial.reshape(2, 2, experts, capacity, width)))
     high = lax.Precision.HIGHEST
     f_mixed = jnp.dot(
         f_weights, f_out.reshape(experts * capacity, width).astype(jnp.float32), precision=high

time: 275 us -> 324 us (1.18)
  waiting for transfers between devices: 187 us -> 244 us
  starting transfers between devices: 38.8 us -> 29.2 us
    ppermute x6, waiting for transfers between devices: 37.3 us -> 77.8 us  [dispatch(): received = lax.ppermute(slots[d], 'z', [(i, i ^ d) for i in range(count)])]
    ppermute x26, waiting for transfers between devices: 105 us -> 126 us  [swap(): return lax.ppermute(value, axis, [(0, 1), (1, 0)])]
    ppermute x26, starting transfers between devices: 21.4 us -> 14.8 us  [swap(): return lax.ppermute(value, axis, [(0, 1), (1, 0)])]
    another operation x10, other arithmetic: 5.26 us -> 8.67 us  [dispatch(): return jnp.stack(pieces, axis=2)]
  transfers between devices with their start and end apart: 40 -> 40, of which waited for: 25 -> 24; matrix products, arithmetic and copies ran while one was open for 8% -> 10% of each run, Pallas kernels for 0% -> 0%
where the time goes in v8:
time: 324 us; the launch traced here: 322 us
  waiting for transfers between devices  244 us (75%)
  starting transfers between devices  29.2 us (9%)
  matrix products  19.2 us (6%)
  other arithmetic  19.1 us (6%)
  local copies, waits for them, and re-layouts  9.5 us (3%)
    ppermute x26, waiting for transfers between devices, swap(): return lax.ppermute(value, axis, [(0, 1), (1, 0)])  126 us
    ppermute x6, waiting for transfers between devices, dispatch(): received = lax.ppermute(slots[d], 'z', [(i, i ^ d) for i in range(count)])  77.8 us
    ppermute x6, waiting for transfers between devices, returned(): out.append(lax.ppermute(totals[d], 'z', [(i, i ^ d) for i in range(count)]))  31.3 us
    ppermute x26, starting transfers between devices, swap(): return lax.ppermute(value, axis, [(0, 1), (1, 0)])  14.8 us
    ppermute x2, waiting for transfers between devices, passed_along(): return lax.ppermute(value, axis, pairs)  8.79 us
    another operation x10, other arithmetic, dispatch(): return jnp.stack(pieces, axis=2)  8.67 us
    ppermute x6, starting transfers between devices, dispatch(): received = lax.ppermute(slots[d], 'z', [(i, i ^ d) for i in range(count)])  7.12 us
  transfers between devices with their start and end apart: 40, of which 24 were waited for; matrix products, arithmetic and copies ran while one was open for 10% of the time, Pallas kernels for 0%

profile of v8, /device:TPU:16, one launch (start us, length us, event | category | flops | bytes accessed | tf_op | source)
XLA Modules:
  0.0 321.9 jit_solution(15438266096867112188)
XLA Ops:
  0.7 0.8 broadcast_xor_fusion
  2.2 0.8 convert_reduce_fusion.1
  3.0 1.6 convolution_convert_fusion.2
  4.7 1.6 collective-permute-start
  7.1 0.9 convolution_convert_fusion
  8.4 1.6 collective-permute-start.13
  10.3 1.6 collective-permute-start.19
  12.5 3.3 %collective-permute-done = bf16[24,7168]{1,0:T(8,128)(2,1)S(1)} collective-permute-done((bf16[24,7168]{1,0:T(8,128)(2,1)S(1)}, bf16[24,7168]{1,0:T(8,128)(2,1)S(1)}, u32[]{:S(2)}, u32[]{:S(2)}) %collective-permute-start) | collective-permute-done | bytes 344096 | tf_op jit(solution)/shard_map/ppermute | solution.py:13
  15.7 0.8 collective-permute-start.2
  16.5 1.0 fusion.78
  17.5 44.8 %collective-permute-done.2 = bf16[24,7168]{1,0:T(8,128)(2,1)S(1)} collective-permute-done((bf16[24,7168]{1,0:T(8,128)(2,1)S(1)}, bf16[24,7168]{1,0:T(8,128)(2,1)S(1)}, u32[]{:S(2)}, u32[]{:S(2)}) %collective-permute-start.2) | collective-permute-done | bytes 344096 | tf_op jit(solution)/shard_map/ppermute | solution.py:77
  63.1 20.5 %collective-permute-done.5 = bf16[24,7168]{1,0:T(8,128)(2,1)S(1)} collective-permute-done((bf16[24,7168]{1,0:T(8,128)(2,1)S(1)}, bf16[24,7168]{1,0:T(8,128)(2,1)S(1)}, u32[]{:S(2)}, u32[]{:S(2)}) %collective-permute-start.5) | collective-permute-done | bytes 344096 | tf_op jit(solution)/shard_map/ppermute | solution.py:77
  83.5 2.5 collective-permute-start.8
  86.6 1.2 fusion.77
  87.8 12.5 %collective-permute-done.8 = bf16[24,7168]{1,0:T(8,128)(2,1)S(1)} collective-permute-done((bf16[24,7168]{1,0:T(8,128)(2,1)S(1)}, bf16[24,7168]{1,0:T(8,128)(2,1)S(1)}, u32[]{:S(2)}, u32[]{:S(2)}) %collective-permute-start.8) | collective-permute-done | bytes 344096 | tf_op jit(solution)/shard_map/ppermute | solution.py:77
  100.9 1.2 fusion.76
  102.3 8.5 %collective-permute-done.9 = bf16[24,7168]{1,0:T(8,128)(2,1)S(1)} collective-permute-done((bf16[24,7168]{1,0:T(8,128)(2,1)S(1)}, bf16[24,7168]{1,0:T(8,128)(2,1)S(1)}, u32[]{:S(2)}, u32[]{:S(2)}) %collective-permute-start.9) | collective-permute-done | bytes 344096 | tf_op jit(solution)/shard_map/ppermute | solution.py:13
  111.3 1.2 fusion.75
  112.5 15.3 %collective-permute-done.14 = bf16[24,14336]{1,0:T(8,128)(2,1)S(1)} collective-permute-done((bf16[24,14336]{1,0:T(8,128)(2,1)S(1)}, bf16[24,14336]{1,0:T(8,128)(2,1)S(1)}, u32[]{:S(2)}, u32[]{:S(2)}) %collective-permute-start.14) | collective-permute-done | bytes 688160 | tf_op jit(solution)/shard_map/ppermute | solution.py:13
  128.7 15.4 %collective-permute-done.17 = bf16[24,14336]{1,0:T(8,128)(2,1)S(1)} collective-permute-done((bf16[24,14336]{1,0:T(8,128)(2,1)S(1)}, bf16[24,14336]{1,0:T(8,128)(2,1)S(1)}, u32[]{:S(2)}, u32[]{:S(2)}) %collective-permute-start.17) | collective-permute-done | bytes 688160 | tf_op jit(solution)/shard_map/ppermute | solution.py:13
  144.8 14.5 %collective-permute-done.20 = bf16[24,14336]{1,0:T(8,128)(2,1)S(1)} collective-permute-done((bf16[24,14336]{1,0:T(8,128)(2,1)S(1)}, bf16[24,14336]{1,0:T(8,128)(2,1)S(1)}, u32[]{:S(2)}, u32[]{:S(2)}) %collective-permute-start.20) | collective-permute-done | bytes 688160 | tf_op jit(solution)/shard_map/ppermute | solution.py:13
  160.3 3.1 collective-permute-done.15
  163.8 2.7 collective-permute-done.18
  166.9 2.7 collective-permute-done.21
  169.9 1.7 pad_maximum_fusion
  171.6 1.8 copy.34
  173.7 1.7 fusion.4
  175.7 1.6 fusion.6
  177.9 1.6 fusion.39
  179.5 1.6 fusion.12
  181.2 4.0 %add_convert_fusion = bf16[384,7168]{1,0:T(8,128)(2,1)S(1)} fusion(f32[384,7168]{1,0:T(8,128)S(1)} %fusion.12, bf16[1,7168,256]{2,1,0:T(8,128)(2,1)} %param.18, f32[384,256]{1,0:T(8,128)} %copy-done.12, f32[384,256]{1,0:T(8,128)} %copy-done.13), kind=kOutput, calls=%fused_computation.2 | convolution fusion | flops 1415380992 | bytes 20971520 | tf_op jit(solution)/shard_map/dot_general | solution.py:64
  185.8 1.3 maximum_bitcast_fusion.4
  187.1 1.3 maximum_bitcast_fusion.5
  188.4 1.2 maximum_bitcast_fusion.6
  189.7 1.2 maximum_bitcast_fusion.7
  190.9 1.0 fusion.79
  192.7 1.5 collective-permute-start.24
  194.7 1.5 collective-permute-start.26
  196.2 0.9 pad_maximum_fusion.1
  197.1 5.9 %collective-permute-done.23 = bf16[24,7168]{1,0:T(8,128)(2,1)S(1)} collective-permute-done((bf16[24,7168]{1,0:T(8,128)(2,1)S(1)}, bf16[24,7168]{1,0:T(8,128)(2,1)S(1)}, u32[]{:S(2)}, u32[]{:S(2)}) %collective-permute-start.23) | collective-permute-done | bytes 344096 | tf_op jit(solution)/shard_map/ppermute | solution.py:13
  203.0 7.4 %collective-permute-done.24 = bf16[24,7168]{1,0:T(8,128)(2,1)S(1)} collective-permute-done((bf16[24,7168]{1,0:T(8,128)(2,1)S(1)}, bf16[24,7168]{1,0:T(8,128)(2,1)S(1)}, u32[]{:S(2)}, u32[]{:S(2)}) %collective-permute-start.24) | collective-permute-done | bytes 344096 | tf_op jit(solution)/shard_map/ppermute | solution.py:13
  210.4 7.4 %collective-permute-done.25 = bf16[24,7168]{1,0:T(8,128)(2,1)S(1)} collective-permute-done((bf16[24,7168]{1,0:T(8,128)(2,1)S(1)}, bf16[24,7168]{1,0:T(8,128)(2,1)S(1)}, u32[]{:S(2)}, u32[]{:S(2)}) %collective-permute-start.25) | collective-permute-done | bytes 344096 | tf_op jit(solution)/shard_map/ppermute | solution.py:13
  217.8 6.8 %collective-permute-done.26 = bf16[24,7168]{1,0:T(8,128)(2,1)S(1)} collective-permute-done((bf16[24,7168]{1,0:T(8,128)(2,1)S(1)}, bf16[24,7168]{1,0:T(8,128)(2,1)S(1)}, u32[]{:S(2)}, u32[]{:S(2)}) %collective-permute-start.26) | collective-permute-done | bytes 344096 | tf_op jit(solution)/shard_map/ppermute | solution.py:13
  225.3 1.6 copy-done.1
  226.9 1.6 fusion.10
  228.9 1.6 fusion.44
  230.9 1.6 convolution_convert_fusion.1
  233.0 5.1 %collective-permute-done.27 = bf16[2,4,24,7168]{3,2,1,0:T(8,128)(2,1)S(1)} collective-permute-done((bf16[2,4,24,7168]{3,2,1,0:T(8,128)(2,1)S(1)}, bf16[2,4,24,7168]{3,2,1,0:T(8,128)(2,1)S(1)}, u32[]{:S(2)}, u32[]{:S(2)}) %collective-permute-start.27) | collective-permute-done | bytes 2752544 | tf_op jit(solution)/shard_map/ppermute | solution.py:13
  238.1 1.0 fusion.80
  239.8 1.5 collective-permute-start.29
  241.8 1.5 collective-permute-start.33
  243.4 6.9 %collective-permute-done.28 = bf16[24,7168]{1,0:T(8,128)(2,1)S(1)} collective-permute-done((bf16[24,7168]{1,0:T(8,128)(2,1)S(1)}, bf16[24,7168]{1,0:T(8,128)(2,1)S(1)}, u32[]{:S(2)}, u32[]{:S(2)}) %collective-permute-start.28) | collective-permute-done | bytes 344096 | tf_op jit(solution)/shard_map/ppermute | solution.py:13
  250.2 7.4 %collective-permute-done.29 = bf16[24,7168]{1,0:T(8,128)(2,1)S(1)} collective-permute-done((bf16[24,7168]{1,0:T(8,128)(2,1)S(1)}, bf16[24,7168]{1,0:T(8,128)(2,1)S(1)}, u32[]{:S(2)}, u32[]{:S(2)}) %collective-permute-start.29) | collective-permute-done | bytes 344096 | tf_op jit(solution)/shard_map/ppermute | solution.py:13
  258.1 6.8 %collective-permute-done.31 = bf16[24,7168]{1,0:T(8,128)(2,1)S(1)} collective-permute-done((bf16[24,7168]{1,0:T(8,128)(2,1)S(1)}, bf16[24,7168]{1,0:T(8,128)(2,1)S(1)}, u32[]{:S(2)}, u32[]{:S(2)}) %collective-permute-start.31) | collective-permute-done | bytes 344096 | tf_op jit(solution)/shard_map/ppermute | solution.py:13
  265.0 6.5 %collective-permute-done.33 = bf16[24,7168]{1,0:T(8,128)(2,1)S(1)} collective-permute-done((bf16[24,7168]{1,0:T(8,128)(2,1)S(1)}, bf16[24,7168]{1,0:T(8,128)(2,1)S(1)}, u32[]{:S(2)}, u32[]{:S(2)}) %collective-permute-start.33) | collective-permute-done | bytes 344096 | tf_op jit(solution)/shard_map/ppermute | solution.py:13
  271.8 2.0 collective-permute-start.32
  273.8 1.5 collective-permute-start.34
  275.3 21.2 %collective-permute-done.38 = bf16[24,7168]{1,0:T(8,128)(2,1)S(1)} collective-permute-done((bf16[24,7168]{1,0:T(8,128)(2,1)S(1)}, bf16[24,7168]{1,0:T(8,128)(2,1)S(1)}, u32[]{:S(2)}, u32[]{:S(2)}) %collective-permute-start.38) | collective-permute-done | bytes 344096 | tf_op jit(solution)/shard_map/ppermute | solution.py:97
  297.4 1.6 collective-permute-start.39
  299.0 3.4 %collective-permute-done.32 = bf16[24,7168]{1,0:T(8,128)(2,1)S(1)} collective-permute-done((bf16[24,7168]{1,0:T(8,128)(2,1)S(1)}, bf16[24,7168]{1,0:T(8,128)(2,1)S(1)}, u32[]{:S(2)}, u32[]{:S(2)}) %collective-permute-start.32) | collective-permute-done | bytes 344096 | tf_op jit(solution)/shard_map/ppermute | solution.py:97
  302.5 6.6 %collective-permute-done.34 = bf16[24,7168]{1,0:T(8,128)(2,1)S(1)} collective-permute-done((bf16[24,7168]{1,0:T(8,128)(2,1)S(1)}, bf16[24,7168]{1,0:T(8,128)(2,1)S(1)}, u32[]{:S(2)}, u32[]{:S(2)}) %collective-permute-start.34) | collective-permute-done | bytes 344096 | tf_op jit(solution)/shard_map/ppermute | solution.py:97
  310.0 1.6 collective-permute-start.35
  311.6 8.8 %collective-permute-done.35 = bf16[1,32,7168]{2,1,0:T(8,128)(2,1)S(1)} collective-permute-done((bf16[1,32,7168]{2,1,0:T(8,128)(2,1)S(1)}, bf16[1,32,7168]{2,1,0:T(8,128)(2,1)S(1)}, u32[]{:S(2)}, u32[]{:S(2)}) %collective-permute-start.35) | collective-permute-done | bytes 458784 | tf_op jit(solution)/shard_map/ppermute | solution.py:19
  320.3 0.8 copy.38
  (111 shorter events, 18.5 us)
Async XLA Ops:
  0.6 6.4 %copy-start.14 = (f32[1,32,2]{1,2,0:T(2,128)S(1)}, f32[1,32,2]{1,2,0:T(2,128)}, u32[]{:S(2)}) copy-start(f32[1,32,2]{1,2,0:T(2,128)} %param.16) | copy-start | bytes 772
  0.6 6.5 %copy-start.11 = (bf16[1,32,7168]{2,1,0:T(8,128)(2,1)S(1)}, bf16[1,32,7168]{2,1,0:T(8,128)(2,1)}, u32[]{:S(2)}) copy-start(bf16[1,32,7168]{2,1,0:T(8,128)(2,1)} %param.13) | copy-start | bytes 1376260
  0.7 6.5 %copy-start.9 = (bf16[1,32,7168]{2,1,0:T(8,128)(2,1)S(1)}, bf16[1,32,7168]{2,1,0:T(8,128)(2,1)}, u32[]{:S(2)}) copy-start(bf16[1,32,7168]{2,1,0:T(8,128)(2,1)} %param.14) | copy-start | bytes 1376260
  4.7 11.0 %collective-permute-start = (bf16[24,7168]{1,0:T(8,128)(2,1)S(1)}, bf16[24,7168]{1,0:T(8,128)(2,1)S(1)}, u32[]{:S(2)}, u32[]{:S(2)}) collective-permute-start(bf16[24,7168]{1,0:T(8,128)(2,1)S(1)} %get-tuple-element.57), channel_id=1, source_target_pairs={{0,2},{2,0},{1,3},{3,1},{4,6},{6,4},{5,7},{7,5},{8,10},{10,8},{9,1... | collective-permute-start | bytes 1032200 | tf_op jit(solution)/shard_map/ppermute | solution.py:13
  8.4 93.7 %collective-permute-start.13 = (bf16[24,14336]{1,0:T(8,128)(2,1)S(1)}, bf16[24,14336]{1,0:T(8,128)(2,1)S(1)}, u32[]{:S(2)}, u32[]{:S(2)}) collective-permute-start(bf16[24,14336]{1,0:T(8,128)(2,1)S(1)} %get-tuple-element.43), channel_id=1, source_target_pairs={{0,4},{4,0},{8,12},{12,8},{1,5},{5,1},{9,13},{13,9},{2,6},{6,2},{1... | collective-permute-start | bytes 2064392 | tf_op jit(solution)/shard_map/ppermute | solution.py:77
  10.0 102.5 %collective-permute-start.16 = (bf16[24,14336]{1,0:T(8,128)(2,1)S(1)}, bf16[24,14336]{1,0:T(8,128)(2,1)S(1)}, u32[]{:S(2)}, u32[]{:S(2)}) collective-permute-start(bf16[24,14336]{1,0:T(8,128)(2,1)S(1)} %get-tuple-element.42), channel_id=1, source_target_pairs={{0,8},{4,12},{8,0},{12,4},{1,9},{5,13},{9,1},{13,5},{2,10},{6,14},... | collective-permute-start | bytes 2064392 | tf_op jit(solution)/shard_map/ppermute | solution.py:77
  10.3 118.3 %collective-permute-start.19 = (bf16[24,14336]{1,0:T(8,128)(2,1)S(1)}, bf16[24,14336]{1,0:T(8,128)(2,1)S(1)}, u32[]{:S(2)}, u32[]{:S(2)}) collective-permute-start(bf16[24,14336]{1,0:T(8,128)(2,1)S(1)} %get-tuple-element.41), channel_id=1, source_target_pairs={{0,12},{4,8},{8,4},{12,0},{1,13},{5,9},{9,5},{13,1},{2,14},{6,10},... | collective-permute-start | bytes 2064392 | tf_op jit(solution)/shard_map/ppermute | solution.py:77
  11.9 50.6 %collective-permute-start.11 = (bf16[24,14336]{1,0:T(8,128)(2,1)S(1)}, bf16[24,14336]{1,0:T(8,128)(2,1)S(1)}, u32[]{:S(2)}, u32[]{:S(2)}) collective-permute-start(bf16[24,14336]{1,0:T(8,128)(2,1)S(1)} %get-tuple-element.44), channel_id=1, source_target_pairs={{0,2},{2,0},{1,3},{3,1},{4,6},{6,4},{5,7},{7,5},{8,10},{10,8},{9,1... | collective-permute-start | bytes 2064392 | tf_op jit(solution)/shard_map/ppermute | solution.py:13
  15.7 46.5 %collective-permute-start.2 = (bf16[24,7168]{1,0:T(8,128)(2,1)S(1)}, bf16[24,7168]{1,0:T(8,128)(2,1)S(1)}, u32[]{:S(2)}, u32[]{:S(2)}) collective-permute-start(bf16[24,7168]{1,0:T(8,128)(2,1)S(1)} %get-tuple-element.56), channel_id=1, source_target_pairs={{0,4},{4,0},{8,12},{12,8},{1,5},{5,1},{9,13},{13,9},{2,6},{6,2},{1... | collective-permute-start | bytes 1032200 | tf_op jit(solution)/shard_map/ppermute | solution.py:77
  62.3 21.3 %collective-permute-start.5 = (bf16[24,7168]{1,0:T(8,128)(2,1)S(1)}, bf16[24,7168]{1,0:T(8,128)(2,1)S(1)}, u32[]{:S(2)}, u32[]{:S(2)}) collective-permute-start(bf16[24,7168]{1,0:T(8,128)(2,1)S(1)} %get-tuple-element.55), channel_id=1, source_target_pairs={{0,8},{4,12},{8,0},{12,4},{1,9},{5,13},{9,1},{13,5},{2,10},{6,14},... | collective-permute-start | bytes 1032200 | tf_op jit(solution)/shard_map/ppermute | solution.py:77
  62.5 23.6 %collective-permute-start.3 = (bf16[24,7168]{1,0:T(8,128)(2,1)S(1)}, bf16[24,7168]{1,0:T(8,128)(2,1)S(1)}, u32[]{:S(2)}, u32[]{:S(2)}) collective-permute-start(bf16[24,7168]{1,0:T(8,128)(2,1)S(1)} %collective-permute-done.2), channel_id=1, source_target_pairs={{0,2},{2,0},{1,3},{3,1},{4,6},{6,4},{5,7},{7,5},{8,10},{10,8},{9,1... | collective-permute-start | bytes 1032200 | tf_op jit(solution)/shard_map/ppermute | solution.py:13
  83.5 16.8 %collective-permute-start.8 = (bf16[24,7168]{1,0:T(8,128)(2,1)S(1)}, bf16[24,7168]{1,0:T(8,128)(2,1)S(1)}, u32[]{:S(2)}, u32[]{:S(2)}) collective-permute-start(bf16[24,7168]{1,0:T(8,128)(2,1)S(1)} %get-tuple-element.54), channel_id=1, source_target_pairs={{0,12},{4,8},{8,4},{12,0},{1,13},{5,9},{9,5},{13,1},{2,14},{6,10},... | collective-permute-start | bytes 1032200 | tf_op jit(solution)/shard_map/ppermute | solution.py:77
  86.1 14.2 %collective-permute-start.6 = (bf16[24,7168]{1,0:T(8,128)(2,1)S(1)}, bf16[24,7168]{1,0:T(8,128)(2,1)S(1)}, u32[]{:S(2)}, u32[]{:S(2)}) collective-permute-start(bf16[24,7168]{1,0:T(8,128)(2,1)S(1)} %collective-permute-done.5), channel_id=1, source_target_pairs={{0,2},{2,0},{1,3},{3,1},{4,6},{6,4},{5,7},{7,5},{8,10},{10,8},{9,1... | collective-permute-start | bytes 1032200 | tf_op jit(solution)/shard_map/ppermute | solution.py:13
  100.3 85.4 %collective-permute-start.1 = (bf16[2,24,7168]{2,1,0:T(8,128)(2,1)}, bf16[2,24,7168]{2,1,0:T(8,128)(2,1)}, u32[]{:S(2)}, u32[]{:S(2)}) collective-permute-start(bf16[2,24,7168]{2,1,0:T(8,128)(2,1)} %get-tuple-element.59), channel_id=1, source_target_pairs={{0,1},{1,0},{2,3},{3,2},{4,5},{5,4},{6,7},{7,6},{8,9},{9,8},{10,11... | collective-permute-start | bytes 2064392 | tf_op jit(solution)/shard_map/ppermute | solution.py:13
  100.3 10.5 %collective-permute-start.9 = (bf16[24,7168]{1,0:T(8,128)(2,1)S(1)}, bf16[24,7168]{1,0:T(8,128)(2,1)S(1)}, u32[]{:S(2)}, u32[]{:S(2)}) collective-permute-start(bf16[24,7168]{1,0:T(8,128)(2,1)S(1)} %collective-permute-done.8), channel_id=1, source_target_pairs={{0,2},{2,0},{1,3},{3,1},{4,6},{6,4},{5,7},{7,5},{8,10},{10,8},{9,1... | collective-permute-start | bytes 1032200 | tf_op jit(solution)/shard_map/ppermute | solution.py:13
  102.0 57.4 %collective-permute-start.12 = (bf16[2,24,14336]{2,1,0:T(8,128)(2,1)S(1)}, bf16[2,24,14336]{2,1,0:T(8,128)(2,1)S(1)}, u32[]{:S(2)}, u32[]{:S(2)}) collective-permute-start(bf16[2,24,14336]{2,1,0:T(8,128)(2,1)S(1)} %get-tuple-element.46), channel_id=1, source_target_pairs={{0,1},{1,0},{2,3},{3,2},{4,5},{5,4},{6,7},{7,6},{8,9},{9,8},{10,11... | collective-permute-start | bytes 4128776 | tf_op jit(solution)/shard_map/ppermute | solution.py:13
  110.8 17.1 %collective-permute-start.14 = (bf16[24,14336]{1,0:T(8,128)(2,1)S(1)}, bf16[24,14336]{1,0:T(8,128)(2,1)S(1)}, u32[]{:S(2)}, u32[]{:S(2)}) collective-permute-start(bf16[24,14336]{1,0:T(8,128)(2,1)S(1)} %collective-permute-done.13), channel_id=1, source_target_pairs={{0,2},{2,0},{1,3},{3,1},{4,6},{6,4},{5,7},{7,5},{8,10},{10,8},{9,1... | collective-permute-start | bytes 2064392 | tf_op jit(solution)/shard_map/ppermute | solution.py:13
  112.5 74.5 %collective-permute-start.4 = (bf16[2,24,7168]{2,1,0:T(8,128)(2,1)}, bf16[2,24,7168]{2,1,0:T(8,128)(2,1)}, u32[]{:S(2)}, u32[]{:S(2)}) collective-permute-start(bf16[2,24,7168]{2,1,0:T(8,128)(2,1)} %get-tuple-element.61), channel_id=1, source_target_pairs={{0,1},{1,0},{2,3},{3,2},{4,5},{5,4},{6,7},{7,6},{8,9},{9,8},{10,11... | collective-permute-start | bytes 2064392 | tf_op jit(solution)/shard_map/ppermute | solution.py:13
  127.9 16.2 %collective-permute-start.17 = (bf16[24,14336]{1,0:T(8,128)(2,1)S(1)}, bf16[24,14336]{1,0:T(8,128)(2,1)S(1)}, u32[]{:S(2)}, u32[]{:S(2)}) collective-permute-start(bf16[24,14336]{1,0:T(8,128)(2,1)S(1)} %collective-permute-done.16), channel_id=1, source_target_pairs={{0,2},{2,0},{1,3},{3,1},{4,6},{6,4},{5,7},{7,5},{8,10},{10,8},{9,1... | collective-permute-start | bytes 2064392 | tf_op jit(solution)/shard_map/ppermute | solution.py:13
  128.6 59.8 %collective-permute-start.7 = (bf16[2,24,7168]{2,1,0:T(8,128)(2,1)}, bf16[2,24,7168]{2,1,0:T(8,128)(2,1)}, u32[]{:S(2)}, u32[]{:S(2)}) collective-permute-start(bf16[2,24,7168]{2,1,0:T(8,128)(2,1)} %get-tuple-element.63), channel_id=1, source_target_pairs={{0,1},{1,0},{2,3},{3,2},{4,5},{5,4},{6,7},{7,6},{8,9},{9,8},{10,11... | collective-permute-start | bytes 2064392 | tf_op jit(solution)/shard_map/ppermute | solution.py:13
  144.1 15.3 %collective-permute-start.20 = (bf16[24,14336]{1,0:T(8,128)(2,1)S(1)}, bf16[24,14336]{1,0:T(8,128)(2,1)S(1)}, u32[]{:S(2)}, u32[]{:S(2)}) collective-permute-start(bf16[24,14336]{1,0:T(8,128)(2,1)S(1)} %collective-permute-done.19), channel_id=1, source_target_pairs={{0,2},{2,0},{1,3},{3,1},{4,6},{6,4},{5,7},{7,5},{8,10},{10,8},{9,1... | collective-permute-start | bytes 2064392 | tf_op jit(solution)/shard_map/ppermute | solution.py:13
  159.3 30.3 %collective-permute-start.10 = (bf16[2,24,7168]{2,1,0:T(8,128)(2,1)}, bf16[2,24,7168]{2,1,0:T(8,128)(2,1)}, u32[]{:S(2)}, u32[]{:S(2)}) collective-permute-start(bf16[2,24,7168]{2,1,0:T(8,128)(2,1)} %get-tuple-element.65), channel_id=1, source_target_pairs={{0,1},{1,0},{2,3},{3,2},{4,5},{5,4},{6,7},{7,6},{8,9},{9,8},{10,11... | collective-permute-start | bytes 2064392 | tf_op jit(solution)/shard_map/ppermute | solution.py:13
  159.5 3.9 %collective-permute-start.15 = (bf16[2,24,14336]{2,1,0:T(8,128)(2,1)S(1)}, bf16[2,24,14336]{2,1,0:T(8,128)(2,1)S(1)}, u32[]{:S(2)}, u32[]{:S(2)}) collective-permute-start(bf16[2,24,14336]{2,1,0:T(8,128)(2,1)S(1)} %get-tuple-element.48), channel_id=1, source_target_pairs={{0,1},{1,0},{2,3},{3,2},{4,5},{5,4},{6,7},{7,6},{8,9},{9,8},{10,11... | collective-permute-start | bytes 4128776 | tf_op jit(solution)/shard_map/ppermute | solution.py:13
  163.4 3.1 collective-permute-start.18
  166.5 3.1 collective-permute-start.21
  171.6 2.0 copy-start.4
  173.7 2.0 copy-start
  175.7 1.6 copy-start.12
  175.7 2.2 copy-start.2
  177.9 1.7 copy-start.13
  185.6 1.5 copy-start.6
  185.6 5.3 %collective-permute-start.22 = (bf16[2,4,24,7168]{3,2,1,0:T(8,128)(2,1)S(1)}, bf16[2,4,24,7168]{3,2,1,0:T(8,128)(2,1)S(1)}, u32[]{:S(2)}, u32[]{:S(2)}) collective-permute-start(bf16[2,4,24,7168]{3,2,1,0:T(8,128)(2,1)S(1)} %bitcast.210), channel_id=1, source_target_pairs={{0,1},{1,0},{2,3},{3,2},{4,5},{5,4},{6,7},{7,6},{8,9},{9,8},{10,11... | collective-permute-start | bytes 8257544 | tf_op jit(solution)/shard_map/ppermute | solution.py:13
  185.8 2.6 copy-start.7
  187.1 2.6 copy-start.8
  192.1 11.0 %collective-permute-start.23 = (bf16[24,7168]{1,0:T(8,128)(2,1)S(1)}, bf16[24,7168]{1,0:T(8,128)(2,1)S(1)}, u32[]{:S(2)}, u32[]{:S(2)}) collective-permute-start(bf16[24,7168]{1,0:T(8,128)(2,1)S(1)} %get-tuple-element.39), channel_id=1, source_target_pairs={{0,2},{2,0},{1,3},{3,1},{4,6},{6,4},{5,7},{7,5},{8,10},{10,8},{9,1... | collective-permute-start | bytes 1032200 | tf_op jit(solution)/shard_map/ppermute | solution.py:13
  192.7 17.7 %collective-permute-start.24 = (bf16[24,7168]{1,0:T(8,128)(2,1)S(1)}, bf16[24,7168]{1,0:T(8,128)(2,1)S(1)}, u32[]{:S(2)}, u32[]{:S(2)}) collective-permute-start(bf16[24,7168]{1,0:T(8,128)(2,1)S(1)} %get-tuple-element.38), channel_id=1, source_target_pairs={{0,2},{2,0},{1,3},{3,1},{4,6},{6,4},{5,7},{7,5},{8,10},{10,8},{9,1... | collective-permute-start | bytes 1032200 | tf_op jit(solution)/shard_map/ppermute | solution.py:13
  194.2 23.6 %collective-permute-start.25 = (bf16[24,7168]{1,0:T(8,128)(2,1)S(1)}, bf16[24,7168]{1,0:T(8,128)(2,1)S(1)}, u32[]{:S(2)}, u32[]{:S(2)}) collective-permute-start(bf16[24,7168]{1,0:T(8,128)(2,1)S(1)} %get-tuple-element.37), channel_id=1, source_target_pairs={{0,2},{2,0},{1,3},{3,1},{4,6},{6,4},{5,7},{7,5},{8,10},{10,8},{9,1... | collective-permute-start | bytes 1032200 | tf_op jit(solution)/shard_map/ppermute | solution.py:13
  194.7 29.9 %collective-permute-start.26 = (bf16[24,7168]{1,0:T(8,128)(2,1)S(1)}, bf16[24,7168]{1,0:T(8,128)(2,1)S(1)}, u32[]{:S(2)}, u32[]{:S(2)}) collective-permute-start(bf16[24,7168]{1,0:T(8,128)(2,1)S(1)} %get-tuple-element.36), channel_id=1, source_target_pairs={{0,2},{2,0},{1,3},{3,1},{4,6},{6,4},{5,7},{7,5},{8,10},{10,8},{9,1... | collective-permute-start | bytes 1032200 | tf_op jit(solution)/shard_map/ppermute | solution.py:13
  224.8 2.0 copy-start.1
  226.9 2.0 copy-start.3
  228.9 2.0 copy-start.5
  232.9 5.2 %collective-permute-start.27 = (bf16[2,4,24,7168]{3,2,1,0:T(8,128)(2,1)S(1)}, bf16[2,4,24,7168]{3,2,1,0:T(8,128)(2,1)S(1)}, u32[]{:S(2)}, u32[]{:S(2)}) collective-permute-start(bf16[2,4,24,7168]{3,2,1,0:T(8,128)(2,1)S(1)} %bitcast.211), channel_id=1, source_target_pairs={{0,1},{1,0},{2,3},{3,2},{4,5},{5,4},{6,7},{7,6},{8,9},{9,8},{10,11... | collective-permute-start | bytes 8257544 | tf_op jit(solution)/shard_map/ppermute | solution.py:13
  239.2 11.0 %collective-permute-start.28 = (bf16[24,7168]{1,0:T(8,128)(2,1)S(1)}, bf16[24,7168]{1,0:T(8,128)(2,1)S(1)}, u32[]{:S(2)}, u32[]{:S(2)}) collective-permute-start(bf16[24,7168]{1,0:T(8,128)(2,1)S(1)} %get-tuple-element.32), channel_id=1, source_target_pairs={{0,2},{2,0},{1,3},{3,1},{4,6},{6,4},{5,7},{7,5},{8,10},{10,8},{9,1... | collective-permute-start | bytes 1032200 | tf_op jit(solution)/shard_map/ppermute | solution.py:13
  239.8 17.8 %collective-permute-start.29 = (bf16[24,7168]{1,0:T(8,128)(2,1)S(1)}, bf16[24,7168]{1,0:T(8,128)(2,1)S(1)}, u32[]{:S(2)}, u32[]{:S(2)}) collective-permute-start(bf16[24,7168]{1,0:T(8,128)(2,1)S(1)} %get-tuple-element.35), channel_id=1, source_target_pairs={{0,2},{2,0},{1,3},{3,1},{4,6},{6,4},{5,7},{7,5},{8,10},{10,8},{9,1... | collective-permute-start | bytes 1032200 | tf_op jit(solution)/shard_map/ppermute | solution.py:13
  241.3 23.6 %collective-permute-start.31 = (bf16[24,7168]{1,0:T(8,128)(2,1)S(1)}, bf16[24,7168]{1,0:T(8,128)(2,1)S(1)}, u32[]{:S(2)}, u32[]{:S(2)}) collective-permute-start(bf16[24,7168]{1,0:T(8,128)(2,1)S(1)} %get-tuple-element.34), channel_id=1, source_target_pairs={{0,2},{2,0},{1,3},{3,1},{4,6},{6,4},{5,7},{7,5},{8,10},{10,8},{9,1... | collective-permute-start | bytes 1032200 | tf_op jit(solution)/shard_map/ppermute | solution.py:13
  241.8 29.7 %collective-permute-start.33 = (bf16[24,7168]{1,0:T(8,128)(2,1)S(1)}, bf16[24,7168]{1,0:T(8,128)(2,1)S(1)}, u32[]{:S(2)}, u32[]{:S(2)}) collective-permute-start(bf16[24,7168]{1,0:T(8,128)(2,1)S(1)} %get-tuple-element.33), channel_id=1, source_target_pairs={{0,2},{2,0},{1,3},{3,1},{4,6},{6,4},{5,7},{7,5},{8,10},{10,8},{9,1... | collective-permute-start | bytes 1032200 | tf_op jit(solution)/shard_map/ppermute | solution.py:13
  243.4 30.5 %collective-permute-start.36 = (bf16[24,7168]{1,0:T(8,128)(2,1)S(1)}, bf16[24,7168]{1,0:T(8,128)(2,1)S(1)}, u32[]{:S(2)}, u32[]{:S(2)}) collective-permute-start(bf16[24,7168]{1,0:T(8,128)(2,1)S(1)} %get-tuple-element.9), channel_id=1, source_target_pairs={{0,4},{4,0},{8,12},{12,8},{1,5},{5,1},{9,13},{13,9},{2,6},{6,2},{1... | collective-permute-start | bytes 1032200 | tf_op jit(solution)/shard_map/ppermute | solution.py:97
  250.2 25.1 %collective-permute-start.37 = (bf16[24,7168]{1,0:T(8,128)(2,1)S(1)}, bf16[24,7168]{1,0:T(8,128)(2,1)S(1)}, u32[]{:S(2)}, u32[]{:S(2)}) collective-permute-start(bf16[24,7168]{1,0:T(8,128)(2,1)S(1)} %get-tuple-element.10), channel_id=1, source_target_pairs={{0,8},{4,12},{8,0},{12,4},{1,9},{5,13},{9,1},{13,5},{2,10},{6,14},... | collective-permute-start | bytes 1032200 | tf_op jit(solution)/shard_map/ppermute | solution.py:97
  257.6 39.0 %collective-permute-start.38 = (bf16[24,7168]{1,0:T(8,128)(2,1)S(1)}, bf16[24,7168]{1,0:T(8,128)(2,1)S(1)}, u32[]{:S(2)}, u32[]{:S(2)}) collective-permute-start(bf16[24,7168]{1,0:T(8,128)(2,1)S(1)} %get-tuple-element.11), channel_id=1, source_target_pairs={{0,12},{4,8},{8,4},{12,0},{1,13},{5,9},{9,5},{13,1},{2,14},{6,10},... | collective-permute-start | bytes 1032200 | tf_op jit(solution)/shard_map/ppermute | solution.py:97
  271.8 27.3 %collective-permute-start.30 = (bf16[24,7168]{1,0:T(8,128)(2,1)S(1)}, bf16[24,7168]{1,0:T(8,128)(2,1)S(1)}, u32[]{:S(2)}, u32[]{:S(2)}) collective-permute-start(bf16[24,7168]{1,0:T(8,128)(2,1)S(1)} %get-tuple-element.18), channel_id=1, source_target_pairs={{0,4},{4,0},{8,12},{12,8},{1,5},{5,1},{9,13},{13,9},{2,6},{6,2},{1... | collective-permute-start | bytes 1032200 | tf_op jit(solution)/shard_map/ppermute | solution.py:97
  271.8 30.6 %collective-permute-start.32 = (bf16[24,7168]{1,0:T(8,128)(2,1)S(1)}, bf16[24,7168]{1,0:T(8,128)(2,1)S(1)}, u32[]{:S(2)}, u32[]{:S(2)}) collective-permute-start(bf16[24,7168]{1,0:T(8,128)(2,1)S(1)} %get-tuple-element.17), channel_id=1, source_target_pairs={{0,8},{4,12},{8,0},{12,4},{1,9},{5,13},{9,1},{13,5},{2,10},{6,14},... | collective-permute-start | bytes 1032200 | tf_op jit(solution)/shard_map/ppermute | solution.py:97
  273.8 35.3 %collective-permute-start.34 = (bf16[24,7168]{1,0:T(8,128)(2,1)S(1)}, bf16[24,7168]{1,0:T(8,128)(2,1)S(1)}, u32[]{:S(2)}, u32[]{:S(2)}) collective-permute-start(bf16[24,7168]{1,0:T(8,128)(2,1)S(1)} %get-tuple-element.19), channel_id=1, source_target_pairs={{0,12},{4,8},{8,4},{12,0},{1,13},{5,9},{9,5},{13,1},{2,14},{6,10},... | collective-permute-start | bytes 1032200 | tf_op jit(solution)/shard_map/ppermute | solution.py:97
  296.7 12.5 %copy-start.10 = (bf16[1,32,7168]{2,1,0:T(8,128)(2,1)S(1)}, bf16[1,32,7168]{2,1,0:T(8,128)(2,1)}, u32[]{:S(2)}) copy-start(bf16[1,32,7168]{2,1,0:T(8,128)(2,1)} %param.10) | copy-start | bytes 1376260
  297.4 14.1 %collective-permute-start.39 = (bf16[1,32,7168]{2,1,0:T(8,128)(2,1)S(1)}, bf16[1,32,7168]{2,1,0:T(8,128)(2,1)S(1)}, u32[]{:S(2)}, u32[]{:S(2)}) collective-permute-start(bf16[1,32,7168]{2,1,0:T(8,128)(2,1)S(1)} %fusion.2), channel_id=1, source_target_pairs={{0,16},{16,0},{1,17},{17,1},{2,18},{18,2},{3,19},{19,3},{4,20},{20... | collective-permute-start | bytes 1376264 | tf_op jit(solution)/shard_map/ppermute | solution.py:19
  310.0 10.4 %collective-permute-start.35 = (bf16[1,32,7168]{2,1,0:T(8,128)(2,1)S(1)}, bf16[1,32,7168]{2,1,0:T(8,128)(2,1)S(1)}, u32[]{:S(2)}, u32[]{:S(2)}) collective-permute-start(bf16[1,32,7168]{2,1,0:T(8,128)(2,1)S(1)} %fusion.3), channel_id=1, source_target_pairs={{0,16},{16,0},{1,17},{17,1},{2,18},{18,2},{3,19},{19,3},{4,20},{20... | collective-permute-start | bytes 1376264 | tf_op jit(solution)/shard_map/ppermute | solution.py:19

commit v9 on v5

--- a/solution.py
+++ b/solution.py
@@ -120,16 +120,18 @@
     here = lax.axis_index("z")
     f_select, f_weights = routing(fwd_experts[0] ^ here, fwd_gates[0], experts, capacity)
     b_select, b_weights = routing(bwd_experts[0] ^ here, bwd_gates[0], experts, capacity)
-    f_slots = into_slots(f_select, fwd_input[0]).reshape(experts, capacity, width)
-    b_joined = jnp.concatenate([bwd_input[0], bwd_grad[0]], axis=1)
-    b_slots = into_slots(b_select, b_joined).reshape(experts, capacity, 2 * width)
-    f_rows = dispatch(f_slots)
-    b_rows = dispatch(b_slots)
-    f_partial = forward_rows(f_rows.reshape(-1, width), w_gate, w_up, w_down)
+    joined = jnp.concatenate([fwd_input[0], bwd_input[0], bwd_grad[0]], axis=1)
+    f_slots = into_slots(f_select, fwd_input[0])
+    b_slots = into_slots(b_select, joined[:, width:])
+    both = jnp.concatenate([f_slots, b_slots], axis=1).reshape(experts, capacity, 3 * width)
+    rows = dispatch(both).reshape(-1, 3 * width)
+    f_rows = rows[:, :width]
+    b_rows = rows[:, width:]
+    f_partial = forward_rows(f_rows, w_gate, w_up, w_down)
     f_totals = reduce_group(f_partial.reshape(2, 2, experts, capacity, width))
     b_rows, f_totals = lax.optimization_barrier((b_rows, f_totals))
     f_out = returned(f_totals)
-    b_partial = backward_rows(b_rows.reshape(-1, 2 * width), w_gate, w_up, w_down)
+    b_partial = backward_rows(b_rows, w_gate, w_up, w_down)
     b_out = returned(reduce_group(b_partial.reshape(2, 2, experts, capacity, width)))
     high = lax.Precision.HIGHEST
     f_mixed = jnp.dot(

time: 275 us -> 297 us (1.080)
  waiting for transfers between devices: 187 us -> 213 us
  starting transfers between devices: 38.8 us -> 27.1 us
  matrix products: 18.9 us -> 28.1 us
  other arithmetic: 19.5 us -> 16.4 us
    ppermute x6 -> x3, waiting for transfers between devices: 37.3 us -> 82.9 us  [dispatch(): received = lax.ppermute(slots[d], 'z', [(i, i ^ d) for i in range(count)])]
    ppermute x26 -> x18, waiting for transfers between devices: 105 us -> 85.8 us  [swap(): return lax.ppermute(value, axis, [(0, 1), (1, 0)])]
    ppermute x26 -> x18, starting transfers between devices: 21.4 us -> 12.8 us  [swap(): return lax.ppermute(value, axis, [(0, 1), (1, 0)])]
    another operation x8 -> x4, other arithmetic: 8.09 us -> 1.07 us  [dispatch(): pieces.append(jnp.stack([across, swap(across, 'c')]))]
    slice x2 -> x1, local copies, waits for them, and re-layouts: 0.51 us -> 4.81 us  [body(): b_rows = rows[:, width:]]
    ppermute x6 -> x3, starting transfers between devices: 7.38 us -> 4.46 us  [dispatch(): received = lax.ppermute(slots[d], 'z', [(i, i ^ d) for i in range(count)])]
  transfers between devices with their start and end apart: 40 -> 29, of which waited for: 25 -> 21; matrix products, arithmetic and copies ran while one was open for 8% -> 3% of each run, Pallas kernels for 0% -> 0%
where the time goes in v9:
time: 297 us
  waiting for transfers between devices  213 us (72%)
  matrix products  28.1 us (9%)
  starting transfers between devices  27.1 us (9%)
  other arithmetic  16.4 us (6%)
  local copies, waits for them, and re-layouts  11.2 us (4%)
    ppermute x18, waiting for transfers between devices, swap(): return lax.ppermute(value, axis, [(0, 1), (1, 0)])  85.8 us
    ppermute x3, waiting for transfers between devices, dispatch(): received = lax.ppermute(slots[d], 'z', [(i, i ^ d) for i in range(count)])  82.9 us
    ppermute x6, waiting for transfers between devices, returned(): out.append(lax.ppermute(totals[d], 'z', [(i, i ^ d) for i in range(count)]))  33.4 us
    ppermute x18, starting transfers between devices, swap(): return lax.ppermute(value, axis, [(0, 1), (1, 0)])  12.8 us
    ppermute x2, waiting for transfers between devices, passed_along(): return lax.ppermute(value, axis, pairs)  10.9 us
    ppermute x6, starting transfers between devices, returned(): out.append(lax.ppermute(totals[d], 'z', [(i, i ^ d) for i in range(count)]))  6.56 us
  transfers between devices with their start and end apart: 29, of which 21 were waited for; matrix products, arithmetic and copies ran while one was open for 3% of the time, Pallas kernels for 0%

profile of v9, /device:TPU:16, one launch (start us, length us, event | category | flops | bytes accessed | tf_op | source)
XLA Modules:
  0.0 296.7 jit_solution(6137922889742139271)
XLA Ops:
  0.6 0.7 broadcast_xor_fusion
  2.8 0.8 convert_reduce_fusion.1
  3.6 0.8 select_reduce_fusion
  4.4 1.6 convolution_convert_fusion.2
  6.0 2.0 convolution_convert_fusion
  8.0 1.6 fusion.54
  9.6 1.6 collective-permute-start.2
  11.2 1.5 collective-permute-start
  12.7 2.8 collective-permute-start.5
  15.5 19.8 %collective-permute-done.2 = bf16[24,21504]{1,0:T(8,128)(2,1)S(1)} collective-permute-done((bf16[24,21504]{1,0:T(8,128)(2,1)S(1)}, bf16[24,21504]{1,0:T(8,128)(2,1)S(1)}, u32[]{:S(2)}, u32[]{:S(2)}) %collective-permute-start.2) | collective-permute-done | bytes 1032224 | tf_op jit(solution)/shard_map/ppermute | solution.py:77
  35.3 1.5 collective-permute-start.3
  37.2 45.5 %collective-permute-done.8 = bf16[24,21504]{1,0:T(8,128)(2,1)S(1)} collective-permute-done((bf16[24,21504]{1,0:T(8,128)(2,1)S(1)}, bf16[24,21504]{1,0:T(8,128)(2,1)S(1)}, u32[]{:S(2)}, u32[]{:S(2)}) %collective-permute-start.8) | collective-permute-done | bytes 1032224 | tf_op jit(solution)/shard_map/ppermute | solution.py:77
  82.7 0.5 collective-permute-start.9
  83.2 17.6 %collective-permute-done.5 = bf16[24,21504]{1,0:T(8,128)(2,1)S(1)} collective-permute-done((bf16[24,21504]{1,0:T(8,128)(2,1)S(1)}, bf16[24,21504]{1,0:T(8,128)(2,1)S(1)}, u32[]{:S(2)}, u32[]{:S(2)}) %collective-permute-start.5) | collective-permute-done | bytes 1032224 | tf_op jit(solution)/shard_map/ppermute | solution.py:77
  100.9 0.5 collective-permute-start.6
  101.8 4.1 %collective-permute-done.9 = bf16[24,21504]{1,0:T(8,128)(2,1)S(1)} collective-permute-done((bf16[24,21504]{1,0:T(8,128)(2,1)S(1)}, bf16[24,21504]{1,0:T(8,128)(2,1)S(1)}, u32[]{:S(2)}, u32[]{:S(2)}) %collective-permute-start.9) | collective-permute-done | bytes 1032224 | tf_op jit(solution)/shard_map/ppermute | solution.py:13
  106.2 19.9 %collective-permute-done.6 = bf16[24,21504]{1,0:T(8,128)(2,1)S(1)} collective-permute-done((bf16[24,21504]{1,0:T(8,128)(2,1)S(1)}, bf16[24,21504]{1,0:T(8,128)(2,1)S(1)}, u32[]{:S(2)}, u32[]{:S(2)}) %collective-permute-start.6) | collective-permute-done | bytes 1032224 | tf_op jit(solution)/shard_map/ppermute | solution.py:13
  127.7 3.0 %collective-permute-done.7 = bf16[2,24,21504]{2,1,0:T(8,128)(2,1)} collective-permute-done((bf16[2,24,21504]{2,1,0:T(8,128)(2,1)S(1)}, bf16[2,24,21504]{2,1,0:T(8,128)(2,1)}, u32[]{:S(2)}, u32[]{:S(2)}) %collective-permute-start.7) | collective-permute-done | bytes 2064416 | tf_op jit(solution)/shard_map/ppermute | solution.py:13
  130.7 2.0 maximum_bitcast_fusion.2
  132.7 2.2 pad_maximum_fusion
  134.9 2.3 copy.33
  137.3 1.6 fusion.8
  138.9 0.4 copy-done.2
  139.3 1.6 fusion.43
  140.9 0.4 copy-done.4
  141.3 1.6 convolution_convert_fusion.1
  143.5 5.1 %collective-permute-done.11 = bf16[2,4,24,7168]{3,2,1,0:T(8,128)(2,1)} collective-permute-done((bf16[2,4,24,7168]{3,2,1,0:T(8,128)(2,1)S(1)}, bf16[2,4,24,7168]{3,2,1,0:T(8,128)(2,1)}, u32[]{:S(2)}, u32[]{:S(2)}) %collective-permute-start.11) | collective-permute-done | bytes 2752544 | tf_op jit(solution)/shard_map/ppermute | solution.py:13
  148.6 2.8 fusion.84
  151.9 1.7 collective-permute-start.14
  153.9 1.7 collective-permute-start.12
  155.6 4.8 %slice.137 = bf16[384,14336]{1,0:T(8,128)(2,1)} slice(bf16[384,21504]{1,0:T(8,128)(2,1)S(1)} %bitcast.170), slice={[0:384], [7168:21504]} | slice | bytes 22020096 | tf_op jit(solution)/shard_map/slice | solution.py:129
  160.4 2.0 collective-permute-done.15
  162.5 7.4 %collective-permute-done.14 = bf16[24,7168]{1,0:T(8,128)(2,1)S(1)} collective-permute-done((bf16[24,7168]{1,0:T(8,128)(2,1)S(1)}, bf16[24,7168]{1,0:T(8,128)(2,1)S(1)}, u32[]{:S(2)}, u32[]{:S(2)}) %collective-permute-start.14) | collective-permute-done | bytes 344096 | tf_op jit(solution)/shard_map/ppermute | solution.py:13
  169.9 7.4 %collective-permute-done.13 = bf16[24,7168]{1,0:T(8,128)(2,1)S(1)} collective-permute-done((bf16[24,7168]{1,0:T(8,128)(2,1)S(1)}, bf16[24,7168]{1,0:T(8,128)(2,1)S(1)}, u32[]{:S(2)}, u32[]{:S(2)}) %collective-permute-start.13) | collective-permute-done | bytes 344096 | tf_op jit(solution)/shard_map/ppermute | solution.py:13
  177.2 6.6 %collective-permute-done.12 = bf16[24,7168]{1,0:T(8,128)(2,1)S(1)} collective-permute-done((bf16[24,7168]{1,0:T(8,128)(2,1)S(1)}, bf16[24,7168]{1,0:T(8,128)(2,1)S(1)}, u32[]{:S(2)}, u32[]{:S(2)}) %collective-permute-start.12) | collective-permute-done | bytes 344096 | tf_op jit(solution)/shard_map/ppermute | solution.py:13
  183.8 1.1 fusion.68
  184.9 4.3 %fusion.10 = f32[384,256]{1,0:T(8,128)S(1)} fusion(bf16[384,14336]{1,0:T(8,128)(2,1)} %slice.137, bf16[1,7168,256]{2,1,0:T(8,128)(2,1)S(1)} %copy-done.1), kind=kOutput, calls=%fused_computation.22 | convolution fusion | flops 1409286144 | bytes 9568256 | tf_op jit(solution)/shard_map/dot_general | solution.py:53
  189.2 4.3 %fusion.4 = f32[384,256]{1,0:T(8,128)S(1)} fusion(bf16[384,14336]{1,0:T(8,128)(2,1)} %slice.137, bf16[1,256,7168]{2,1,0:T(8,128)(2,1)S(1)} %copy-done.5), kind=kOutput, calls=%fused_computation.16 | convolution fusion | flops 1409286144 | bytes 9568256 | tf_op jit(solution)/shard_map/dot_general | solution.py:55
  193.6 4.2 %fusion.48 = bf16[384,256]{1,0:T(8,128)(2,1)S(1)} fusion(f32[384,256]{1,0:T(8,128)S(1)} %fusion.4, bf16[1,7168,256]{2,1,0:T(8,128)(2,1)S(1)} %copy-done.3, bf16[384,14336]{1,0:T(8,128)(2,1)} %slice.137, f32[384,256]{1,0:T(8,128)S(1)} %fusion.10), kind=kOutput, calls=%fused_computation.53 | convolution fusion | flops 1410269184 | bytes 10158080 | tf_op jit(solution)/shard_map/dot_general | solution.py:54
  197.8 1.6 fusion.19
  199.4 3.8 %add_convert_fusion = bf16[384,7168]{1,0:T(8,128)(2,1)S(1)} fusion(f32[384,7168]{1,0:T(8,128)S(1)} %fusion.19, bf16[1,7168,256]{2,1,0:T(8,128)(2,1)} %param.18, f32[384,256]{1,0:T(8,128)S(1)} %fusion.4, f32[384,256]{1,0:T(8,128)S(1)} %fusion.10), kind=kOutput, calls=%fused_computation.2 | convolution fusion | flops 1415380992 | bytes 20971520 | tf_op jit(solution)/shard_map/dot_general | solution.py:64
  203.7 5.1 %collective-permute-done.20 = bf16[2,4,24,7168]{3,2,1,0:T(8,128)(2,1)S(1)} collective-permute-done((bf16[2,4,24,7168]{3,2,1,0:T(8,128)(2,1)S(1)}, bf16[2,4,24,7168]{3,2,1,0:T(8,128)(2,1)S(1)}, u32[]{:S(2)}, u32[]{:S(2)}) %collective-permute-start.20) | collective-permute-done | bytes 2752544 | tf_op jit(solution)/shard_map/ppermute | solution.py:13
  208.8 1.0 fusion.85
  210.3 1.7 collective-permute-start.26
  212.3 1.7 collective-permute-start.22
  214.0 1.5 collective-permute-start.16
  215.5 5.4 %collective-permute-done.21 = bf16[24,7168]{1,0:T(8,128)(2,1)S(1)} collective-permute-done((bf16[24,7168]{1,0:T(8,128)(2,1)S(1)}, bf16[24,7168]{1,0:T(8,128)(2,1)S(1)}, u32[]{:S(2)}, u32[]{:S(2)}) %collective-permute-start.21) | collective-permute-done | bytes 344096 | tf_op jit(solution)/shard_map/ppermute | solution.py:13
  220.9 1.5 collective-permute-start.17
  222.4 5.9 %collective-permute-done.26 = bf16[24,7168]{1,0:T(8,128)(2,1)S(1)} collective-permute-done((bf16[24,7168]{1,0:T(8,128)(2,1)S(1)}, bf16[24,7168]{1,0:T(8,128)(2,1)S(1)}, u32[]{:S(2)}, u32[]{:S(2)}) %collective-permute-start.26) | collective-permute-done | bytes 344096 | tf_op jit(solution)/shard_map/ppermute | solution.py:13
  228.3 7.4 %collective-permute-done.24 = bf16[24,7168]{1,0:T(8,128)(2,1)S(1)} collective-permute-done((bf16[24,7168]{1,0:T(8,128)(2,1)S(1)}, bf16[24,7168]{1,0:T(8,128)(2,1)S(1)}, u32[]{:S(2)}, u32[]{:S(2)}) %collective-permute-start.24) | collective-permute-done | bytes 344096 | tf_op jit(solution)/shard_map/ppermute | solution.py:13
  235.6 6.6 %collective-permute-done.22 = bf16[24,7168]{1,0:T(8,128)(2,1)S(1)} collective-permute-done((bf16[24,7168]{1,0:T(8,128)(2,1)S(1)}, bf16[24,7168]{1,0:T(8,128)(2,1)S(1)}, u32[]{:S(2)}, u32[]{:S(2)}) %collective-permute-start.22) | collective-permute-done | bytes 344096 | tf_op jit(solution)/shard_map/ppermute | solution.py:13
  242.4 1.5 collective-permute-start.25
  244.1 2.0 collective-permute-start.27
  246.0 4.9 %collective-permute-done.17 = bf16[24,7168]{1,0:T(8,128)(2,1)S(1)} collective-permute-done((bf16[24,7168]{1,0:T(8,128)(2,1)S(1)}, bf16[24,7168]{1,0:T(8,128)(2,1)S(1)}, u32[]{:S(2)}, u32[]{:S(2)}) %collective-permute-start.17) | collective-permute-done | bytes 344096 | tf_op jit(solution)/shard_map/ppermute | solution.py:97
  250.9 15.5 %collective-permute-done.18 = bf16[24,7168]{1,0:T(8,128)(2,1)S(1)} collective-permute-done((bf16[24,7168]{1,0:T(8,128)(2,1)S(1)}, bf16[24,7168]{1,0:T(8,128)(2,1)S(1)}, u32[]{:S(2)}, u32[]{:S(2)}) %collective-permute-start.18) | collective-permute-done | bytes 344096 | tf_op jit(solution)/shard_map/ppermute | solution.py:97
  266.6 0.7 fusion.3
  267.3 1.6 collective-permute-start.19
  268.9 4.9 %collective-permute-done.25 = bf16[24,7168]{1,0:T(8,128)(2,1)S(1)} collective-permute-done((bf16[24,7168]{1,0:T(8,128)(2,1)S(1)}, bf16[24,7168]{1,0:T(8,128)(2,1)S(1)}, u32[]{:S(2)}, u32[]{:S(2)}) %collective-permute-start.25) | collective-permute-done | bytes 344096 | tf_op jit(solution)/shard_map/ppermute | solution.py:97
  273.8 8.1 %collective-permute-done.27 = bf16[24,7168]{1,0:T(8,128)(2,1)S(1)} collective-permute-done((bf16[24,7168]{1,0:T(8,128)(2,1)S(1)}, bf16[24,7168]{1,0:T(8,128)(2,1)S(1)}, u32[]{:S(2)}, u32[]{:S(2)}) %collective-permute-start.27) | collective-permute-done | bytes 344096 | tf_op jit(solution)/shard_map/ppermute | solution.py:97
  282.0 0.7 fusion.2
  282.7 1.6 collective-permute-start.28
  284.3 10.9 %collective-permute-done.28 = bf16[1,32,7168]{2,1,0:T(8,128)(2,1)S(1)} collective-permute-done((bf16[1,32,7168]{2,1,0:T(8,128)(2,1)S(1)}, bf16[1,32,7168]{2,1,0:T(8,128)(2,1)S(1)}, u32[]{:S(2)}, u32[]{:S(2)}) %collective-permute-start.28) | collective-permute-done | bytes 458784 | tf_op jit(solution)/shard_map/ppermute | solution.py:19
  295.2 0.8 copy.36
  295.9 0.8 copy.37
  (71 shorter events, 7.1 us)
Async XLA Ops:
  9.6 25.8 %collective-permute-start.2 = (bf16[24,21504]{1,0:T(8,128)(2,1)S(1)}, bf16[24,21504]{1,0:T(8,128)(2,1)S(1)}, u32[]{:S(2)}, u32[]{:S(2)}) collective-permute-start(bf16[24,21504]{1,0:T(8,128)(2,1)S(1)} %get-tuple-element.33), channel_id=1, source_target_pairs={{0,4},{4,0},{8,12},{12,8},{1,5},{5,1},{9,13},{13,9},{2,6},{6,2},{1... | collective-permute-start | bytes 3096584 | tf_op jit(solution)/shard_map/ppermute | solution.py:77
  11.2 25.6 %collective-permute-start = (bf16[24,21504]{1,0:T(8,128)(2,1)S(1)}, bf16[24,21504]{1,0:T(8,128)(2,1)S(1)}, u32[]{:S(2)}, u32[]{:S(2)}) collective-permute-start(bf16[24,21504]{1,0:T(8,128)(2,1)S(1)} %get-tuple-element.32), channel_id=1, source_target_pairs={{0,2},{2,0},{1,3},{3,1},{4,6},{6,4},{5,7},{7,5},{8,10},{10,8},{9,1... | collective-permute-start | bytes 3096584 | tf_op jit(solution)/shard_map/ppermute | solution.py:13
  12.7 70.0 %collective-permute-start.8 = (bf16[24,21504]{1,0:T(8,128)(2,1)S(1)}, bf16[24,21504]{1,0:T(8,128)(2,1)S(1)}, u32[]{:S(2)}, u32[]{:S(2)}) collective-permute-start(bf16[24,21504]{1,0:T(8,128)(2,1)S(1)} %get-tuple-element.34), channel_id=1, source_target_pairs={{0,12},{4,8},{8,4},{12,0},{1,13},{5,9},{9,5},{13,1},{2,14},{6,10},... | collective-permute-start | bytes 3096584 | tf_op jit(solution)/shard_map/ppermute | solution.py:77
  12.7 88.1 %collective-permute-start.5 = (bf16[24,21504]{1,0:T(8,128)(2,1)S(1)}, bf16[24,21504]{1,0:T(8,128)(2,1)S(1)}, u32[]{:S(2)}, u32[]{:S(2)}) collective-permute-start(bf16[24,21504]{1,0:T(8,128)(2,1)S(1)} %get-tuple-element.35), channel_id=1, source_target_pairs={{0,8},{4,12},{8,0},{12,4},{1,9},{5,13},{9,1},{13,5},{2,10},{6,14},... | collective-permute-start | bytes 3096584 | tf_op jit(solution)/shard_map/ppermute | solution.py:77
  35.3 66.1 %collective-permute-start.3 = (bf16[24,21504]{1,0:T(8,128)(2,1)S(1)}, bf16[24,21504]{1,0:T(8,128)(2,1)S(1)}, u32[]{:S(2)}, u32[]{:S(2)}) collective-permute-start(bf16[24,21504]{1,0:T(8,128)(2,1)S(1)} %collective-permute-done.2), channel_id=1, source_target_pairs={{0,2},{2,0},{1,3},{3,1},{4,6},{6,4},{5,7},{7,5},{8,10},{10,8},{9,1... | collective-permute-start | bytes 3096584 | tf_op jit(solution)/shard_map/ppermute | solution.py:13
  37.1 89.4 %collective-permute-start.1 = (bf16[2,24,21504]{2,1,0:T(8,128)(2,1)S(1)}, bf16[2,24,21504]{2,1,0:T(8,128)(2,1)S(1)}, u32[]{:S(2)}, u32[]{:S(2)}) collective-permute-start(bf16[2,24,21504]{2,1,0:T(8,128)(2,1)S(1)} %get-tuple-element.45), channel_id=1, source_target_pairs={{0,1},{1,0},{2,3},{3,2},{4,5},{5,4},{6,7},{7,6},{8,9},{9,8},{10,11... | collective-permute-start | bytes 6193160 | tf_op jit(solution)/shard_map/ppermute | solution.py:13
  82.7 23.1 %collective-permute-start.9 = (bf16[24,21504]{1,0:T(8,128)(2,1)S(1)}, bf16[24,21504]{1,0:T(8,128)(2,1)S(1)}, u32[]{:S(2)}, u32[]{:S(2)}) collective-permute-start(bf16[24,21504]{1,0:T(8,128)(2,1)S(1)} %collective-permute-done.8), channel_id=1, source_target_pairs={{0,2},{2,0},{1,3},{3,1},{4,6},{6,4},{5,7},{7,5},{8,10},{10,8},{9,1... | collective-permute-start | bytes 3096584 | tf_op jit(solution)/shard_map/ppermute | solution.py:13
  100.9 25.3 %collective-permute-start.6 = (bf16[24,21504]{1,0:T(8,128)(2,1)S(1)}, bf16[24,21504]{1,0:T(8,128)(2,1)S(1)}, u32[]{:S(2)}, u32[]{:S(2)}) collective-permute-start(bf16[24,21504]{1,0:T(8,128)(2,1)S(1)} %collective-permute-done.5), channel_id=1, source_target_pairs={{0,2},{2,0},{1,3},{3,1},{4,6},{6,4},{5,7},{7,5},{8,10},{10,8},{9,1... | collective-permute-start | bytes 3096584 | tf_op jit(solution)/shard_map/ppermute | solution.py:13
  101.7 25.2 %collective-permute-start.4 = (bf16[2,24,21504]{2,1,0:T(8,128)(2,1)S(1)}, bf16[2,24,21504]{2,1,0:T(8,128)(2,1)S(1)}, u32[]{:S(2)}, u32[]{:S(2)}) collective-permute-start(bf16[2,24,21504]{2,1,0:T(8,128)(2,1)S(1)} %get-tuple-element.47), channel_id=1, source_target_pairs={{0,1},{1,0},{2,3},{3,2},{4,5},{5,4},{6,7},{7,6},{8,9},{9,8},{10,11... | collective-permute-start | bytes 6193160 | tf_op jit(solution)/shard_map/ppermute | solution.py:13
  106.1 21.2 %collective-permute-start.10 = (bf16[2,24,21504]{2,1,0:T(8,128)(2,1)S(1)}, bf16[2,24,21504]{2,1,0:T(8,128)(2,1)S(1)}, u32[]{:S(2)}, u32[]{:S(2)}) collective-permute-start(bf16[2,24,21504]{2,1,0:T(8,128)(2,1)S(1)} %get-tuple-element.51), channel_id=1, source_target_pairs={{0,1},{1,0},{2,3},{3,2},{4,5},{5,4},{6,7},{7,6},{8,9},{9,8},{10,11... | collective-permute-start | bytes 6193160 | tf_op jit(solution)/shard_map/ppermute | solution.py:13
  126.4 4.3 %collective-permute-start.7 = (bf16[2,24,21504]{2,1,0:T(8,128)(2,1)S(1)}, bf16[2,24,21504]{2,1,0:T(8,128)(2,1)}, u32[]{:S(2)}, u32[]{:S(2)}) collective-permute-start(bf16[2,24,21504]{2,1,0:T(8,128)(2,1)S(1)} %get-tuple-element.49), channel_id=1, source_target_pairs={{0,1},{1,0},{2,3},{3,2},{4,5},{5,4},{6,7},{7,6},{8,9},{9,8},{10,11... | collective-permute-start | bytes 6193160 | tf_op jit(solution)/shard_map/ppermute | solution.py:13
  134.9 2.4 copy-start
  137.3 2.0 copy-start.2
  139.3 2.0 copy-start.4
  143.3 5.3 %collective-permute-start.11 = (bf16[2,4,24,7168]{3,2,1,0:T(8,128)(2,1)S(1)}, bf16[2,4,24,7168]{3,2,1,0:T(8,128)(2,1)}, u32[]{:S(2)}, u32[]{:S(2)}) collective-permute-start(bf16[2,4,24,7168]{3,2,1,0:T(8,128)(2,1)S(1)} %bitcast.176), channel_id=1, source_target_pairs={{0,1},{1,0},{2,3},{3,2},{4,5},{5,4},{6,7},{7,6},{8,9},{9,8},{10,11... | collective-permute-start | bytes 8257544 | tf_op jit(solution)/shard_map/ppermute | solution.py:13
  151.5 11.0 %collective-permute-start.15 = (bf16[24,7168]{1,0:T(8,128)(2,1)S(1)}, bf16[24,7168]{1,0:T(8,128)(2,1)S(1)}, u32[]{:S(2)}, u32[]{:S(2)}) collective-permute-start(bf16[24,7168]{1,0:T(8,128)(2,1)S(1)} %get-tuple-element.40), channel_id=1, source_target_pairs={{0,2},{2,0},{1,3},{3,1},{4,6},{6,4},{5,7},{7,5},{8,10},{10,8},{9,1... | collective-permute-start | bytes 1032200 | tf_op jit(solution)/shard_map/ppermute | solution.py:13
  151.9 18.0 %collective-permute-start.14 = (bf16[24,7168]{1,0:T(8,128)(2,1)S(1)}, bf16[24,7168]{1,0:T(8,128)(2,1)S(1)}, u32[]{:S(2)}, u32[]{:S(2)}) collective-permute-start(bf16[24,7168]{1,0:T(8,128)(2,1)S(1)} %get-tuple-element.41), channel_id=1, source_target_pairs={{0,2},{2,0},{1,3},{3,1},{4,6},{6,4},{5,7},{7,5},{8,10},{10,8},{9,1... | collective-permute-start | bytes 1032200 | tf_op jit(solution)/shard_map/ppermute | solution.py:13
  153.6 23.6 %collective-permute-start.13 = (bf16[24,7168]{1,0:T(8,128)(2,1)S(1)}, bf16[24,7168]{1,0:T(8,128)(2,1)S(1)}, u32[]{:S(2)}, u32[]{:S(2)}) collective-permute-start(bf16[24,7168]{1,0:T(8,128)(2,1)S(1)} %get-tuple-element.42), channel_id=1, source_target_pairs={{0,2},{2,0},{1,3},{3,1},{4,6},{6,4},{5,7},{7,5},{8,10},{10,8},{9,1... | collective-permute-start | bytes 1032200 | tf_op jit(solution)/shard_map/ppermute | solution.py:13
  153.9 29.9 %collective-permute-start.12 = (bf16[24,7168]{1,0:T(8,128)(2,1)S(1)}, bf16[24,7168]{1,0:T(8,128)(2,1)S(1)}, u32[]{:S(2)}, u32[]{:S(2)}) collective-permute-start(bf16[24,7168]{1,0:T(8,128)(2,1)S(1)} %get-tuple-element.43), channel_id=1, source_target_pairs={{0,2},{2,0},{1,3},{3,1},{4,6},{6,4},{5,7},{7,5},{8,10},{10,8},{9,1... | collective-permute-start | bytes 1032200 | tf_op jit(solution)/shard_map/ppermute | solution.py:13
  160.4 24.4 %copy-start.1 = (bf16[1,7168,256]{2,1,0:T(8,128)(2,1)S(1)}, bf16[1,7168,256]{2,1,0:T(8,128)(2,1)}, u32[]{:S(2)}) copy-start(bf16[1,7168,256]{2,1,0:T(8,128)(2,1)} %param.17) | copy-start | bytes 11010052
  184.9 4.3 %copy-start.5 = (bf16[1,256,7168]{2,1,0:T(8,128)(2,1)S(1)}, bf16[1,256,7168]{2,1,0:T(8,128)(2,1)}, u32[]{:S(2)}) copy-start(bf16[1,256,7168]{2,1,0:T(8,128)(2,1)} %param.19) | copy-start | bytes 11010052
  189.2 4.4 %copy-start.3 = (bf16[1,7168,256]{2,1,0:T(8,128)(2,1)S(1)}, bf16[1,7168,256]{2,1,0:T(8,128)(2,1)}, u32[]{:S(2)}) copy-start(bf16[1,7168,256]{2,1,0:T(8,128)(2,1)} %param.18) | copy-start | bytes 11010052
  203.6 5.2 %collective-permute-start.20 = (bf16[2,4,24,7168]{3,2,1,0:T(8,128)(2,1)S(1)}, bf16[2,4,24,7168]{3,2,1,0:T(8,128)(2,1)S(1)}, u32[]{:S(2)}, u32[]{:S(2)}) collective-permute-start(bf16[2,4,24,7168]{3,2,1,0:T(8,128)(2,1)S(1)} %bitcast.177), channel_id=1, source_target_pairs={{0,1},{1,0},{2,3},{3,2},{4,5},{5,4},{6,7},{7,6},{8,9},{9,8},{10,11... | collective-permute-start | bytes 8257544 | tf_op jit(solution)/shard_map/ppermute | solution.py:13
  208.8 5.3 %copy-start.10 = (bf16[24,7168]{1,0:T(8,128)(2,1)S(1)}, bf16[24,7168]{1,0:T(8,128)(2,1)}, u32[]{:S(2)}) copy-start(bf16[24,7168]{1,0:T(8,128)(2,1)} %get-tuple-element.8) | copy-start | bytes 1032196
  208.8 12.1 %copy-start.9 = (bf16[24,7168]{1,0:T(8,128)(2,1)S(1)}, bf16[24,7168]{1,0:T(8,128)(2,1)}, u32[]{:S(2)}) copy-start(bf16[24,7168]{1,0:T(8,128)(2,1)} %get-tuple-element.9) | copy-start | bytes 1032196
  208.8 19.5 %copy-start.8 = (bf16[24,7168]{1,0:T(8,128)(2,1)S(1)}, bf16[24,7168]{1,0:T(8,128)(2,1)}, u32[]{:S(2)}) copy-start(bf16[24,7168]{1,0:T(8,128)(2,1)} %get-tuple-element.10) | copy-start | bytes 1032196
  209.9 11.0 %collective-permute-start.21 = (bf16[24,7168]{1,0:T(8,128)(2,1)S(1)}, bf16[24,7168]{1,0:T(8,128)(2,1)S(1)}, u32[]{:S(2)}, u32[]{:S(2)}) collective-permute-start(bf16[24,7168]{1,0:T(8,128)(2,1)S(1)} %get-tuple-element.36), channel_id=1, source_target_pairs={{0,2},{2,0},{1,3},{3,1},{4,6},{6,4},{5,7},{7,5},{8,10},{10,8},{9,1... | collective-permute-start | bytes 1032200 | tf_op jit(solution)/shard_map/ppermute | solution.py:13
  210.3 18.0 %collective-permute-start.26 = (bf16[24,7168]{1,0:T(8,128)(2,1)S(1)}, bf16[24,7168]{1,0:T(8,128)(2,1)S(1)}, u32[]{:S(2)}, u32[]{:S(2)}) collective-permute-start(bf16[24,7168]{1,0:T(8,128)(2,1)S(1)} %get-tuple-element.37), channel_id=1, source_target_pairs={{0,2},{2,0},{1,3},{3,1},{4,6},{6,4},{5,7},{7,5},{8,10},{10,8},{9,1... | collective-permute-start | bytes 1032200 | tf_op jit(solution)/shard_map/ppermute | solution.py:13
  212.0 23.6 %collective-permute-start.24 = (bf16[24,7168]{1,0:T(8,128)(2,1)S(1)}, bf16[24,7168]{1,0:T(8,128)(2,1)S(1)}, u32[]{:S(2)}, u32[]{:S(2)}) collective-permute-start(bf16[24,7168]{1,0:T(8,128)(2,1)S(1)} %get-tuple-element.38), channel_id=1, source_target_pairs={{0,2},{2,0},{1,3},{3,1},{4,6},{6,4},{5,7},{7,5},{8,10},{10,8},{9,1... | collective-permute-start | bytes 1032200 | tf_op jit(solution)/shard_map/ppermute | solution.py:13
  212.3 29.9 %collective-permute-start.22 = (bf16[24,7168]{1,0:T(8,128)(2,1)S(1)}, bf16[24,7168]{1,0:T(8,128)(2,1)S(1)}, u32[]{:S(2)}, u32[]{:S(2)}) collective-permute-start(bf16[24,7168]{1,0:T(8,128)(2,1)S(1)} %get-tuple-element.39), channel_id=1, source_target_pairs={{0,2},{2,0},{1,3},{3,1},{4,6},{6,4},{5,7},{7,5},{8,10},{10,8},{9,1... | collective-permute-start | bytes 1032200 | tf_op jit(solution)/shard_map/ppermute | solution.py:13
  214.0 30.0 %collective-permute-start.16 = (bf16[24,7168]{1,0:T(8,128)(2,1)S(1)}, bf16[24,7168]{1,0:T(8,128)(2,1)S(1)}, u32[]{:S(2)}, u32[]{:S(2)}) collective-permute-start(bf16[24,7168]{1,0:T(8,128)(2,1)S(1)} %copy-done.10), channel_id=1, source_target_pairs={{0,4},{4,0},{8,12},{12,8},{1,5},{5,1},{9,13},{13,9},{2,6},{6,2},{1... | collective-permute-start | bytes 1032200 | tf_op jit(solution)/shard_map/ppermute | solution.py:97
  220.9 30.0 %collective-permute-start.17 = (bf16[24,7168]{1,0:T(8,128)(2,1)S(1)}, bf16[24,7168]{1,0:T(8,128)(2,1)S(1)}, u32[]{:S(2)}, u32[]{:S(2)}) collective-permute-start(bf16[24,7168]{1,0:T(8,128)(2,1)S(1)} %copy-done.9), channel_id=1, source_target_pairs={{0,8},{4,12},{8,0},{12,4},{1,9},{5,13},{9,1},{13,5},{2,10},{6,14},... | collective-permute-start | bytes 1032200 | tf_op jit(solution)/shard_map/ppermute | solution.py:97
  228.3 38.1 %collective-permute-start.18 = (bf16[24,7168]{1,0:T(8,128)(2,1)S(1)}, bf16[24,7168]{1,0:T(8,128)(2,1)S(1)}, u32[]{:S(2)}, u32[]{:S(2)}) collective-permute-start(bf16[24,7168]{1,0:T(8,128)(2,1)S(1)} %copy-done.8), channel_id=1, source_target_pairs={{0,12},{4,8},{8,4},{12,0},{1,13},{5,9},{9,5},{13,1},{2,14},{6,10},... | collective-permute-start | bytes 1032200 | tf_op jit(solution)/shard_map/ppermute | solution.py:97
  242.2 24.4 %copy-start.6 = (bf16[1,32,7168]{2,1,0:T(8,128)(2,1)S(1)}, bf16[1,32,7168]{2,1,0:T(8,128)(2,1)}, u32[]{:S(2)}) copy-start(bf16[1,32,7168]{2,1,0:T(8,128)(2,1)} %param.10) | copy-start | bytes 1376260
  242.4 31.3 %collective-permute-start.25 = (bf16[24,7168]{1,0:T(8,128)(2,1)S(1)}, bf16[24,7168]{1,0:T(8,128)(2,1)S(1)}, u32[]{:S(2)}, u32[]{:S(2)}) collective-permute-start(bf16[24,7168]{1,0:T(8,128)(2,1)S(1)} %get-tuple-element.17), channel_id=1, source_target_pairs={{0,8},{4,12},{8,0},{12,4},{1,9},{5,13},{9,1},{13,5},{2,10},{6,14},... | collective-permute-start | bytes 1032200 | tf_op jit(solution)/shard_map/ppermute | solution.py:97
  244.0 29.8 %collective-permute-start.23 = (bf16[24,7168]{1,0:T(8,128)(2,1)S(1)}, bf16[24,7168]{1,0:T(8,128)(2,1)S(1)}, u32[]{:S(2)}, u32[]{:S(2)}) collective-permute-start(bf16[24,7168]{1,0:T(8,128)(2,1)S(1)} %get-tuple-element.18), channel_id=1, source_target_pairs={{0,4},{4,0},{8,12},{12,8},{1,5},{5,1},{9,13},{13,9},{2,6},{6,2},{1... | collective-permute-start | bytes 1032200 | tf_op jit(solution)/shard_map/ppermute | solution.py:97
  244.1 37.8 %collective-permute-start.27 = (bf16[24,7168]{1,0:T(8,128)(2,1)S(1)}, bf16[24,7168]{1,0:T(8,128)(2,1)S(1)}, u32[]{:S(2)}, u32[]{:S(2)}) collective-permute-start(bf16[24,7168]{1,0:T(8,128)(2,1)S(1)} %get-tuple-element.19), channel_id=1, source_target_pairs={{0,12},{4,8},{8,4},{12,0},{1,13},{5,9},{9,5},{13,1},{2,14},{6,10},... | collective-permute-start | bytes 1032200 | tf_op jit(solution)/shard_map/ppermute | solution.py:97
  266.4 15.6 %copy-start.7 = (bf16[1,32,7168]{2,1,0:T(8,128)(2,1)S(1)}, bf16[1,32,7168]{2,1,0:T(8,128)(2,1)}, u32[]{:S(2)}) copy-start(bf16[1,32,7168]{2,1,0:T(8,128)(2,1)} %param.14) | copy-start | bytes 1376260
  267.3 17.0 %collective-permute-start.19 = (bf16[1,32,7168]{2,1,0:T(8,128)(2,1)S(1)}, bf16[1,32,7168]{2,1,0:T(8,128)(2,1)S(1)}, u32[]{:S(2)}, u32[]{:S(2)}) collective-permute-start(bf16[1,32,7168]{2,1,0:T(8,128)(2,1)S(1)} %fusion.3), channel_id=1, source_target_pairs={{0,16},{16,0},{1,17},{17,1},{2,18},{18,2},{3,19},{19,3},{4,20},{20... | collective-permute-start | bytes 1376264 | tf_op jit(solution)/shard_map/ppermute | solution.py:19
  282.7 12.5 %collective-permute-start.28 = (bf16[1,32,7168]{2,1,0:T(8,128)(2,1)S(1)}, bf16[1,32,7168]{2,1,0:T(8,128)(2,1)S(1)}, u32[]{:S(2)}, u32[]{:S(2)}) collective-permute-start(bf16[1,32,7168]{2,1,0:T(8,128)(2,1)S(1)} %fusion.2), channel_id=1, source_target_pairs={{0,16},{16,0},{1,17},{17,1},{2,18},{18,2},{3,19},{19,3},{4,20},{20... | collective-permute-start | bytes 1376264 | tf_op jit(solution)/shard_map/ppermute | solution.py:19

commit v10 on v5

--- a/solution.py
+++ b/solution.py
@@ -80,9 +80,12 @@
     return jnp.stack(pieces, axis=2)
 
 
-def reduce_group(partial):
+def chip_reduce(partial):
     from_core = swap(partial[1], "c")
-    chip_sum = partial[0].astype(jnp.float32) + from_core.astype(jnp.float32)
+    return partial[0].astype(jnp.float32) + from_core.astype(jnp.float32)
+
+
+def x_reduce(chip_sum):
     totals = []
     for d in range(chip_sum.shape[1]):
         from_x = swap(chip_sum[1, d].astype(jnp.bfloat16), "x")
@@ -126,11 +129,11 @@
     f_rows = dispatch(f_slots)
     b_rows = dispatch(b_slots)
     f_partial = forward_rows(f_rows.reshape(-1, width), w_gate, w_up, w_down)
-    f_totals = reduce_group(f_partial.reshape(2, 2, experts, capacity, width))
-    b_rows, f_totals = lax.optimization_barrier((b_rows, f_totals))
-    f_out = returned(f_totals)
+    f_chip = chip_reduce(f_partial.reshape(2, 2, experts, capacity, width))
+    b_rows, f_chip = lax.optimization_barrier((b_rows, f_chip))
+    f_out = returned(x_reduce(f_chip))
     b_partial = backward_rows(b_rows.reshape(-1, 2 * width), w_gate, w_up, w_down)
-    b_out = returned(reduce_group(b_partial.reshape(2, 2, experts, capacity, width)))
+    b_out = returned(x_reduce(chip_reduce(b_partial.reshape(2, 2, experts, capacity, width))))
     high = lax.Precision.HIGHEST
     f_mixed = jnp.dot(
         f_weights, f_out.reshape(experts * capacity, width).astype(jnp.float32), precision=high

time: 275 us -> 324 us (1.18); the launches traced: 274 us -> 319 us
  waiting for transfers between devices: 187 us -> 227 us
  starting transfers between devices: 38.8 us -> 32.9 us
  local copies, waits for them, and re-layouts: 9.07 us -> 13.9 us
  matrix products: 18.9 us -> 23.5 us
    ppermute x6, waiting for transfers between devices: 37.3 us -> 86.4 us  [dispatch(): received = lax.ppermute(slots[d], 'z', [(i, i ^ d) for i in range(count)])]
    ppermute x6, waiting for transfers between devices: 33.3 us -> 23.8 us  [returned(): out.append(lax.ppermute(totals[d], 'z', [(i, i ^ d) for i in range(count)]))]
    ppermute x26, starting transfers between devices: 21.4 us -> 13.3 us  [swap(): return lax.ppermute(value, axis, [(0, 1), (1, 0)])]
    slice x2, local copies, waits for them, and re-layouts: 0.71 us -> 4.85 us  [chip_reduce(): from_core = swap(partial[1], 'c')]
    another operation x10, other arithmetic: 5.26 us -> 9.3 us  [dispatch(): return jnp.stack(pieces, axis=2)]
  transfers between devices with their start and end apart: 40 -> 40, of which waited for: 25 -> 21; matrix products, arithmetic and copies ran while one was open for 8% -> 9% of each run, Pallas kernels for 0% -> 0%
where the time goes in v10:
time: 324 us; the launch traced here: 319 us
  waiting for transfers between devices  227 us (70%)
  starting transfers between devices  32.9 us (10%)
  matrix products  23.5 us (7%)
  other arithmetic  20 us (6%)
  local copies, waits for them, and re-layouts  13.9 us (4%)
    ppermute x26, waiting for transfers between devices, swap(): return lax.ppermute(value, axis, [(0, 1), (1, 0)])  107 us
    ppermute x6, waiting for transfers between devices, dispatch(): received = lax.ppermute(slots[d], 'z', [(i, i ^ d) for i in range(count)])  86.4 us
    ppermute x6, waiting for transfers between devices, returned(): out.append(lax.ppermute(totals[d], 'z', [(i, i ^ d) for i in range(count)]))  23.8 us
    ppermute x26, starting transfers between devices, swap(): return lax.ppermute(value, axis, [(0, 1), (1, 0)])  13.3 us
    ppermute x2, waiting for transfers between devices, passed_along(): return lax.ppermute(value, axis, pairs)  9.67 us
    another operation x10, other arithmetic, dispatch(): return jnp.stack(pieces, axis=2)  9.3 us
    ppermute x6, starting transfers between devices, returned(): out.append(lax.ppermute(totals[d], 'z', [(i, i ^ d) for i in range(count)]))  9.17 us
    ppermute x6, starting transfers between devices, dispatch(): received = lax.ppermute(slots[d], 'z', [(i, i ^ d) for i in range(count)])  7.2 us
  transfers between devices with their start and end apart: 40, of which 21 were waited for; matrix products, arithmetic and copies ran while one was open for 9% of the time, Pallas kernels for 0%

profile of v10, /device:TPU:16, one launch (start us, length us, event | category | flops | bytes accessed | tf_op | source)
XLA Modules:
  0.0 318.6 jit_solution(10901634553340456565)
XLA Ops:
  0.7 0.8 broadcast_xor_fusion
  2.2 0.8 convert_reduce_fusion
  3.0 1.6 convolution_convert_fusion.2
  4.5 0.8 slice_bitcast_fusion.12
  5.4 1.5 collective-permute-start.11
  7.8 0.9 convolution_convert_fusion
  9.5 3.5 %collective-permute-start.5 = (bf16[24,14336]{1,0:T(8,128)(2,1)S(1)}, bf16[24,14336]{1,0:T(8,128)(2,1)S(1)}, u32[]{:S(2)}, u32[]{:S(2)}) collective-permute-start(bf16[24,14336]{1,0:T(8,128)(2,1)S(1)} %get-tuple-element.34), channel_id=1, source_target_pairs={{0,8},{4,12},{8,0},{12,4},{1,9},{5,13},{9,1},{13,5},{2,10},{6,14},... | collective-permute-start | bytes 2064392 | tf_op jit(solution)/shard_map/ppermute | solution.py:77
  13.5 2.8 collective-permute-done.11
  16.6 1.1 fusion.75
  17.7 67.2 %collective-permute-done.19 = bf16[24,7168]{1,0:T(8,128)(2,1)S(1)} collective-permute-done((bf16[24,7168]{1,0:T(8,128)(2,1)S(1)}, bf16[24,7168]{1,0:T(8,128)(2,1)S(1)}, u32[]{:S(2)}, u32[]{:S(2)}) %collective-permute-start.19) | collective-permute-done | bytes 344096 | tf_op jit(solution)/shard_map/ppermute | solution.py:77
  85.6 13.1 %collective-permute-done.16 = bf16[24,7168]{1,0:T(8,128)(2,1)S(1)} collective-permute-done((bf16[24,7168]{1,0:T(8,128)(2,1)S(1)}, bf16[24,7168]{1,0:T(8,128)(2,1)S(1)}, u32[]{:S(2)}, u32[]{:S(2)}) %collective-permute-start.16) | collective-permute-done | bytes 344096 | tf_op jit(solution)/shard_map/ppermute | solution.py:77
  98.7 2.8 collective-permute-start.13
  102.2 6.1 %collective-permute-done.13 = bf16[24,7168]{1,0:T(8,128)(2,1)S(1)} collective-permute-done((bf16[24,7168]{1,0:T(8,128)(2,1)S(1)}, bf16[24,7168]{1,0:T(8,128)(2,1)S(1)}, u32[]{:S(2)}, u32[]{:S(2)}) %collective-permute-start.13) | collective-permute-done | bytes 344096 | tf_op jit(solution)/shard_map/ppermute | solution.py:77
  108.2 1.5 collective-permute-done.17
  110.3 8.4 %collective-permute-done.14 = bf16[24,7168]{1,0:T(8,128)(2,1)S(1)} collective-permute-done((bf16[24,7168]{1,0:T(8,128)(2,1)S(1)}, bf16[24,7168]{1,0:T(8,128)(2,1)S(1)}, u32[]{:S(2)}, u32[]{:S(2)}) %collective-permute-start.14) | collective-permute-done | bytes 344096 | tf_op jit(solution)/shard_map/ppermute | solution.py:13
  120.2 16.7 %collective-permute-done.9 = bf16[24,14336]{1,0:T(8,128)(2,1)S(1)} collective-permute-done((bf16[24,14336]{1,0:T(8,128)(2,1)S(1)}, bf16[24,14336]{1,0:T(8,128)(2,1)S(1)}, u32[]{:S(2)}, u32[]{:S(2)}) %collective-permute-start.9) | collective-permute-done | bytes 688160 | tf_op jit(solution)/shard_map/ppermute | solution.py:13
  137.4 1.3 fusion.77
  138.7 14.8 %collective-permute-done.6 = bf16[24,14336]{1,0:T(8,128)(2,1)S(1)} collective-permute-done((bf16[24,14336]{1,0:T(8,128)(2,1)S(1)}, bf16[24,14336]{1,0:T(8,128)(2,1)S(1)}, u32[]{:S(2)}, u32[]{:S(2)}) %collective-permute-start.6) | collective-permute-done | bytes 688160 | tf_op jit(solution)/shard_map/ppermute | solution.py:13
  153.9 1.3 fusion.78
  155.2 13.9 %collective-permute-done.3 = bf16[24,14336]{1,0:T(8,128)(2,1)S(1)} collective-permute-done((bf16[24,14336]{1,0:T(8,128)(2,1)S(1)}, bf16[24,14336]{1,0:T(8,128)(2,1)S(1)}, u32[]{:S(2)}, u32[]{:S(2)}) %collective-permute-start.3) | collective-permute-done | bytes 688160 | tf_op jit(solution)/shard_map/ppermute | solution.py:13
  169.1 1.3 fusion.79
  171.4 0.9 pad_maximum_fusion.1
  172.8 1.6 copy-done
  174.4 1.6 fusion.19
  176.4 1.6 fusion.44
  178.4 1.6 convolution_convert_fusion.1
  180.1 1.9 fusion.82
  182.4 1.6 maximum_bitcast_fusion
  184.0 1.6 maximum_bitcast_fusion.3
  185.6 1.6 maximum_bitcast_fusion.2
  187.2 1.6 maximum_bitcast_fusion.1
  188.8 1.5 pad_maximum_fusion
  190.4 0.7 convert_add_fusion.1
  191.1 2.1 copy.35
  193.2 3.8 %fusion.4 = f32[384,256]{1,0:T(8,128)S(1)} fusion(bf16[384,14336]{1,0:T(8,128)(2,1)S(1)} %bitcast.196, bf16[1,256,7168]{2,1,0:T(8,128)(2,1)} %param.19), kind=kOutput, calls=%fused_computation.11 | convolution fusion | flops 1409286144 | bytes 9568256 | tf_op jit(solution)/shard_map/dot_general | solution.py:55
  197.0 1.6 fusion.6
  199.0 1.6 fusion.39
  200.7 1.6 fusion.16
  202.3 6.2 %add_convert_fusion = bf16[384,7168]{1,0:T(8,128)(2,1)} fusion(f32[384,7168]{1,0:T(8,128)S(1)} %fusion.16, bf16[1,7168,256]{2,1,0:T(8,128)(2,1)} %param.18, f32[384,256]{1,0:T(8,128)S(1)} %fusion.4, f32[384,256]{1,0:T(8,128)S(1)} %fusion.6), kind=kOutput, calls=%fused_computation.2 | convolution fusion | flops 1415380992 | bytes 20971520 | tf_op jit(solution)/shard_map/dot_general | solution.py:64
  208.5 3.0 fusion.81
  212.7 1.5 collective-permute-start.28
  214.7 1.5 collective-permute-start.24
  216.7 1.0 fusion.76
  218.4 4.6 %collective-permute-done.23 = bf16[24,7168]{1,0:T(8,128)(2,1)S(1)} collective-permute-done((bf16[24,7168]{1,0:T(8,128)(2,1)S(1)}, bf16[24,7168]{1,0:T(8,128)(2,1)S(1)}, u32[]{:S(2)}, u32[]{:S(2)}) %collective-permute-start.23) | collective-permute-done | bytes 344096 | tf_op jit(solution)/shard_map/ppermute | solution.py:13
  223.5 6.8 %collective-permute-done.28 = bf16[24,7168]{1,0:T(8,128)(2,1)S(1)} collective-permute-done((bf16[24,7168]{1,0:T(8,128)(2,1)S(1)}, bf16[24,7168]{1,0:T(8,128)(2,1)S(1)}, u32[]{:S(2)}, u32[]{:S(2)}) %collective-permute-start.28) | collective-permute-done | bytes 344096 | tf_op jit(solution)/shard_map/ppermute | solution.py:13
  230.9 6.8 %collective-permute-done.26 = bf16[24,7168]{1,0:T(8,128)(2,1)S(1)} collective-permute-done((bf16[24,7168]{1,0:T(8,128)(2,1)S(1)}, bf16[24,7168]{1,0:T(8,128)(2,1)S(1)}, u32[]{:S(2)}, u32[]{:S(2)}) %collective-permute-start.26) | collective-permute-done | bytes 344096 | tf_op jit(solution)/shard_map/ppermute | solution.py:13
  238.3 6.8 %collective-permute-done.24 = bf16[24,7168]{1,0:T(8,128)(2,1)S(1)} collective-permute-done((bf16[24,7168]{1,0:T(8,128)(2,1)S(1)}, bf16[24,7168]{1,0:T(8,128)(2,1)S(1)}, u32[]{:S(2)}, u32[]{:S(2)}) %collective-permute-start.24) | collective-permute-done | bytes 344096 | tf_op jit(solution)/shard_map/ppermute | solution.py:13
  245.4 1.1 collective-permute-start.29
  246.5 6.0 %collective-permute-done.32 = bf16[24,7168]{1,0:T(8,128)(2,1)S(1)} collective-permute-done((bf16[24,7168]{1,0:T(8,128)(2,1)S(1)}, bf16[24,7168]{1,0:T(8,128)(2,1)S(1)}, u32[]{:S(2)}, u32[]{:S(2)}) %collective-permute-start.32) | collective-permute-done | bytes 344096 | tf_op jit(solution)/shard_map/ppermute | solution.py:13
  252.5 2.2 collective-permute-start.27
  254.7 5.2 %collective-permute-done.35 = bf16[24,7168]{1,0:T(8,128)(2,1)S(1)} collective-permute-done((bf16[24,7168]{1,0:T(8,128)(2,1)S(1)}, bf16[24,7168]{1,0:T(8,128)(2,1)S(1)}, u32[]{:S(2)}, u32[]{:S(2)}) %collective-permute-start.35) | collective-permute-done | bytes 344096 | tf_op jit(solution)/shard_map/ppermute | solution.py:13
  259.9 1.7 collective-permute-start.25
  261.6 5.6 %collective-permute-done.33 = bf16[24,7168]{1,0:T(8,128)(2,1)S(1)} collective-permute-done((bf16[24,7168]{1,0:T(8,128)(2,1)S(1)}, bf16[24,7168]{1,0:T(8,128)(2,1)S(1)}, u32[]{:S(2)}, u32[]{:S(2)}) %collective-permute-start.33) | collective-permute-done | bytes 344096 | tf_op jit(solution)/shard_map/ppermute | solution.py:13
  267.2 7.0 %collective-permute-done.37 = bf16[24,7168]{1,0:T(8,128)(2,1)S(1)} collective-permute-done((bf16[24,7168]{1,0:T(8,128)(2,1)S(1)}, bf16[24,7168]{1,0:T(8,128)(2,1)S(1)}, u32[]{:S(2)}, u32[]{:S(2)}) %collective-permute-start.37) | collective-permute-done | bytes 344096 | tf_op jit(solution)/shard_map/ppermute | solution.py:13
  274.4 1.1 collective-permute-start.38
  275.5 3.1 collective-permute-start.36
  278.8 0.7 fusion.3
  279.5 1.5 collective-permute-start.30
  281.0 19.2 %collective-permute-done.38 = bf16[24,7168]{1,0:T(8,128)(2,1)S(1)} collective-permute-done((bf16[24,7168]{1,0:T(8,128)(2,1)S(1)}, bf16[24,7168]{1,0:T(8,128)(2,1)S(1)}, u32[]{:S(2)}, u32[]{:S(2)}) %collective-permute-start.38) | collective-permute-done | bytes 344096 | tf_op jit(solution)/shard_map/ppermute | solution.py:100
  300.2 4.6 %collective-permute-done.36 = bf16[24,7168]{1,0:T(8,128)(2,1)S(1)} collective-permute-done((bf16[24,7168]{1,0:T(8,128)(2,1)S(1)}, bf16[24,7168]{1,0:T(8,128)(2,1)S(1)}, u32[]{:S(2)}, u32[]{:S(2)}) %collective-permute-start.36) | collective-permute-done | bytes 344096 | tf_op jit(solution)/shard_map/ppermute | solution.py:100
  305.7 1.7 collective-permute-start.39
  307.4 9.7 %collective-permute-done.39 = bf16[1,32,7168]{2,1,0:T(8,128)(2,1)S(1)} collective-permute-done((bf16[1,32,7168]{2,1,0:T(8,128)(2,1)S(1)}, bf16[1,32,7168]{2,1,0:T(8,128)(2,1)S(1)}, u32[]{:S(2)}, u32[]{:S(2)}) %collective-permute-start.39) | collective-permute-done | bytes 458784 | tf_op jit(solution)/shard_map/ppermute | solution.py:19
  317.0 0.8 copy.38
  317.8 0.8 copy.39
  (100 shorter events, 16.9 us)
Async XLA Ops:
  0.6 7.0 %copy-start.8 = (f32[1,32,2]{1,2,0:T(2,128)S(1)}, f32[1,32,2]{1,2,0:T(2,128)}, u32[]{:S(2)}) copy-start(f32[1,32,2]{1,2,0:T(2,128)} %param.16) | copy-start | bytes 772
  0.6 7.1 %copy-start.6 = (bf16[1,32,7168]{2,1,0:T(8,128)(2,1)S(1)}, bf16[1,32,7168]{2,1,0:T(8,128)(2,1)}, u32[]{:S(2)}) copy-start(bf16[1,32,7168]{2,1,0:T(8,128)(2,1)} %param.14) | copy-start | bytes 1376260
  0.7 7.1 %copy-start.7 = (bf16[1,32,7168]{2,1,0:T(8,128)(2,1)S(1)}, bf16[1,32,7168]{2,1,0:T(8,128)(2,1)}, u32[]{:S(2)}) copy-start(bf16[1,32,7168]{2,1,0:T(8,128)(2,1)} %param.13) | copy-start | bytes 1376260
  5.4 10.9 %collective-permute-start.11 = (bf16[24,7168]{1,0:T(8,128)(2,1)}, bf16[24,7168]{1,0:T(8,128)(2,1)}, u32[]{:S(2)}, u32[]{:S(2)}) collective-permute-start(bf16[24,7168]{1,0:T(8,128)(2,1)} %get-tuple-element.41), channel_id=1, source_target_pairs={{0,2},{2,0},{1,3},{3,1},{4,6},{6,4},{5,7},{7,5},{8,10},{10,8},{9,1... | collective-permute-start | bytes 1032200 | tf_op jit(solution)/shard_map/ppermute | solution.py:13
  9.0 109.9 %collective-permute-start.8 = (bf16[24,14336]{1,0:T(8,128)(2,1)S(1)}, bf16[24,14336]{1,0:T(8,128)(2,1)S(1)}, u32[]{:S(2)}, u32[]{:S(2)}) collective-permute-start(bf16[24,14336]{1,0:T(8,128)(2,1)S(1)} %get-tuple-element.33), channel_id=1, source_target_pairs={{0,12},{4,8},{8,4},{12,0},{1,13},{5,9},{9,5},{13,1},{2,14},{6,10},... | collective-permute-start | bytes 2064392 | tf_op jit(solution)/shard_map/ppermute | solution.py:77
  9.5 110.6 %collective-permute-start.5 = (bf16[24,14336]{1,0:T(8,128)(2,1)S(1)}, bf16[24,14336]{1,0:T(8,128)(2,1)S(1)}, u32[]{:S(2)}, u32[]{:S(2)}) collective-permute-start(bf16[24,14336]{1,0:T(8,128)(2,1)S(1)} %get-tuple-element.34), channel_id=1, source_target_pairs={{0,8},{4,12},{8,0},{12,4},{1,9},{5,13},{9,1},{13,5},{2,10},{6,14},... | collective-permute-start | bytes 2064392 | tf_op jit(solution)/shard_map/ppermute | solution.py:77
  13.0 125.7 %collective-permute-start.2 = (bf16[24,14336]{1,0:T(8,128)(2,1)S(1)}, bf16[24,14336]{1,0:T(8,128)(2,1)S(1)}, u32[]{:S(2)}, u32[]{:S(2)}) collective-permute-start(bf16[24,14336]{1,0:T(8,128)(2,1)S(1)} %get-tuple-element.35), channel_id=1, source_target_pairs={{0,4},{4,0},{8,12},{12,8},{1,5},{5,1},{9,13},{13,9},{2,6},{6,2},{1... | collective-permute-start | bytes 2064392 | tf_op jit(solution)/shard_map/ppermute | solution.py:77
  13.0 71.9 %collective-permute-start = (bf16[24,14336]{1,0:T(8,128)(2,1)S(1)}, bf16[24,14336]{1,0:T(8,128)(2,1)S(1)}, u32[]{:S(2)}, u32[]{:S(2)}) collective-permute-start(bf16[24,14336]{1,0:T(8,128)(2,1)S(1)} %get-tuple-element.36), channel_id=1, source_target_pairs={{0,2},{2,0},{1,3},{3,1},{4,6},{6,4},{5,7},{7,5},{8,10},{10,8},{9,1... | collective-permute-start | bytes 2064392 | tf_op jit(solution)/shard_map/ppermute | solution.py:13
  16.3 68.6 %collective-permute-start.19 = (bf16[24,7168]{1,0:T(8,128)(2,1)S(1)}, bf16[24,7168]{1,0:T(8,128)(2,1)S(1)}, u32[]{:S(2)}, u32[]{:S(2)}) collective-permute-start(bf16[24,7168]{1,0:T(8,128)(2,1)S(1)} %get-tuple-element.38), channel_id=1, source_target_pairs={{0,12},{4,8},{8,4},{12,0},{1,13},{5,9},{9,5},{13,1},{2,14},{6,10},... | collective-permute-start | bytes 1032200 | tf_op jit(solution)/shard_map/ppermute | solution.py:77
  84.9 13.8 %collective-permute-start.16 = (bf16[24,7168]{1,0:T(8,128)(2,1)S(1)}, bf16[24,7168]{1,0:T(8,128)(2,1)S(1)}, u32[]{:S(2)}, u32[]{:S(2)}) collective-permute-start(bf16[24,7168]{1,0:T(8,128)(2,1)S(1)} %get-tuple-element.39), channel_id=1, source_target_pairs={{0,8},{4,12},{8,0},{12,4},{1,9},{5,13},{9,1},{13,5},{2,10},{6,14},... | collective-permute-start | bytes 1032200 | tf_op jit(solution)/shard_map/ppermute | solution.py:77
  84.9 16.6 %collective-permute-start.20 = (bf16[24,7168]{1,0:T(8,128)(2,1)S(1)}, bf16[24,7168]{1,0:T(8,128)(2,1)S(1)}, u32[]{:S(2)}, u32[]{:S(2)}) collective-permute-start(bf16[24,7168]{1,0:T(8,128)(2,1)S(1)} %collective-permute-done.19), channel_id=1, source_target_pairs={{0,2},{2,0},{1,3},{3,1},{4,6},{6,4},{5,7},{7,5},{8,10},{10,8},{9,1... | collective-permute-start | bytes 1032200 | tf_op jit(solution)/shard_map/ppermute | solution.py:13
  98.7 9.5 %collective-permute-start.13 = (bf16[24,7168]{1,0:T(8,128)(2,1)S(1)}, bf16[24,7168]{1,0:T(8,128)(2,1)S(1)}, u32[]{:S(2)}, u32[]{:S(2)}) collective-permute-start(bf16[24,7168]{1,0:T(8,128)(2,1)S(1)} %get-tuple-element.40), channel_id=1, source_target_pairs={{0,4},{4,0},{8,12},{12,8},{1,5},{5,1},{9,13},{13,9},{2,6},{6,2},{1... | collective-permute-start | bytes 1032200 | tf_op jit(solution)/shard_map/ppermute | solution.py:77
  101.5 8.2 %collective-permute-start.17 = (bf16[24,7168]{1,0:T(8,128)(2,1)S(1)}, bf16[24,7168]{1,0:T(8,128)(2,1)S(1)}, u32[]{:S(2)}, u32[]{:S(2)}) collective-permute-start(bf16[24,7168]{1,0:T(8,128)(2,1)S(1)} %collective-permute-done.16), channel_id=1, source_target_pairs={{0,2},{2,0},{1,3},{3,1},{4,6},{6,4},{5,7},{7,5},{8,10},{10,8},{9,1... | collective-permute-start | bytes 1032200 | tf_op jit(solution)/shard_map/ppermute | solution.py:13
  108.2 11.2 %collective-permute-start.12 = (bf16[2,24,7168]{2,1,0:T(8,128)(2,1)S(1)}, bf16[2,24,7168]{2,1,0:T(8,128)(2,1)S(1)}, u32[]{:S(2)}, u32[]{:S(2)}) collective-permute-start(bf16[2,24,7168]{2,1,0:T(8,128)(2,1)S(1)} %get-tuple-element.51), channel_id=1, source_target_pairs={{0,1},{1,0},{2,3},{3,2},{4,5},{5,4},{6,7},{7,6},{8,9},{9,8},{10,11... | collective-permute-start | bytes 2064392 | tf_op jit(solution)/shard_map/ppermute | solution.py:13
  109.7 9.0 %collective-permute-start.14 = (bf16[24,7168]{1,0:T(8,128)(2,1)S(1)}, bf16[24,7168]{1,0:T(8,128)(2,1)S(1)}, u32[]{:S(2)}, u32[]{:S(2)}) collective-permute-start(bf16[24,7168]{1,0:T(8,128)(2,1)S(1)} %collective-permute-done.13), channel_id=1, source_target_pairs={{0,2},{2,0},{1,3},{3,1},{4,6},{6,4},{5,7},{7,5},{8,10},{10,8},{9,1... | collective-permute-start | bytes 1032200 | tf_op jit(solution)/shard_map/ppermute | solution.py:13
  118.7 63.7 %collective-permute-start.1 = (bf16[2,24,14336]{2,1,0:T(8,128)(2,1)S(1)}, bf16[2,24,14336]{2,1,0:T(8,128)(2,1)}, u32[]{:S(2)}, u32[]{:S(2)}) collective-permute-start(bf16[2,24,14336]{2,1,0:T(8,128)(2,1)S(1)} %get-tuple-element.43), channel_id=1, source_target_pairs={{0,1},{1,0},{2,3},{3,2},{4,5},{5,4},{6,7},{7,6},{8,9},{9,8},{10,11... | collective-permute-start | bytes 4128776 | tf_op jit(solution)/shard_map/ppermute | solution.py:13
  118.8 51.5 %collective-permute-start.21 = (bf16[2,24,7168]{2,1,0:T(8,128)(2,1)S(1)}, bf16[2,24,7168]{2,1,0:T(8,128)(2,1)S(1)}, u32[]{:S(2)}, u32[]{:S(2)}) collective-permute-start(bf16[2,24,7168]{2,1,0:T(8,128)(2,1)S(1)} %get-tuple-element.57), channel_id=1, source_target_pairs={{0,1},{1,0},{2,3},{3,2},{4,5},{5,4},{6,7},{7,6},{8,9},{9,8},{10,11... | collective-permute-start | bytes 2064392 | tf_op jit(solution)/shard_map/ppermute | solution.py:13
  119.4 17.4 %collective-permute-start.9 = (bf16[24,14336]{1,0:T(8,128)(2,1)S(1)}, bf16[24,14336]{1,0:T(8,128)(2,1)S(1)}, u32[]{:S(2)}, u32[]{:S(2)}) collective-permute-start(bf16[24,14336]{1,0:T(8,128)(2,1)S(1)} %collective-permute-done.8), channel_id=1, source_target_pairs={{0,2},{2,0},{1,3},{3,1},{4,6},{6,4},{5,7},{7,5},{8,10},{10,8},{9,1... | collective-permute-start | bytes 2064392 | tf_op jit(solution)/shard_map/ppermute | solution.py:13
  120.1 50.9 %collective-permute-start.18 = (bf16[2,24,7168]{2,1,0:T(8,128)(2,1)S(1)}, bf16[2,24,7168]{2,1,0:T(8,128)(2,1)S(1)}, u32[]{:S(2)}, u32[]{:S(2)}) collective-permute-start(bf16[2,24,7168]{2,1,0:T(8,128)(2,1)S(1)} %get-tuple-element.55), channel_id=1, source_target_pairs={{0,1},{1,0},{2,3},{3,2},{4,5},{5,4},{6,7},{7,6},{8,9},{9,8},{10,11... | collective-permute-start | bytes 2064392 | tf_op jit(solution)/shard_map/ppermute | solution.py:13
  136.8 16.6 %collective-permute-start.6 = (bf16[24,14336]{1,0:T(8,128)(2,1)S(1)}, bf16[24,14336]{1,0:T(8,128)(2,1)S(1)}, u32[]{:S(2)}, u32[]{:S(2)}) collective-permute-start(bf16[24,14336]{1,0:T(8,128)(2,1)S(1)} %collective-permute-done.5), channel_id=1, source_target_pairs={{0,2},{2,0},{1,3},{3,1},{4,6},{6,4},{5,7},{7,5},{8,10},{10,8},{9,1... | collective-permute-start | bytes 2064392 | tf_op jit(solution)/shard_map/ppermute | solution.py:13
  138.6 32.6 %collective-permute-start.15 = (bf16[2,24,7168]{2,1,0:T(8,128)(2,1)S(1)}, bf16[2,24,7168]{2,1,0:T(8,128)(2,1)S(1)}, u32[]{:S(2)}, u32[]{:S(2)}) collective-permute-start(bf16[2,24,7168]{2,1,0:T(8,128)(2,1)S(1)} %get-tuple-element.53), channel_id=1, source_target_pairs={{0,1},{1,0},{2,3},{3,2},{4,5},{5,4},{6,7},{7,6},{8,9},{9,8},{10,11... | collective-permute-start | bytes 2064392 | tf_op jit(solution)/shard_map/ppermute | solution.py:13
  153.4 15.7 %collective-permute-start.3 = (bf16[24,14336]{1,0:T(8,128)(2,1)S(1)}, bf16[24,14336]{1,0:T(8,128)(2,1)S(1)}, u32[]{:S(2)}, u32[]{:S(2)}) collective-permute-start(bf16[24,14336]{1,0:T(8,128)(2,1)S(1)} %collective-permute-done.2), channel_id=1, source_target_pairs={{0,2},{2,0},{1,3},{3,1},{4,6},{6,4},{5,7},{7,5},{8,10},{10,8},{9,1... | collective-permute-start | bytes 2064392 | tf_op jit(solution)/shard_map/ppermute | solution.py:13
  169.1 15.0 %collective-permute-start.10 = (bf16[2,24,14336]{2,1,0:T(8,128)(2,1)}, bf16[2,24,14336]{2,1,0:T(8,128)(2,1)}, u32[]{:S(2)}, u32[]{:S(2)}) collective-permute-start(bf16[2,24,14336]{2,1,0:T(8,128)(2,1)} %get-tuple-element.49), channel_id=1, source_target_pairs={{0,1},{1,0},{2,3},{3,2},{4,5},{5,4},{6,7},{7,6},{8,9},{9,8},{10,11... | collective-permute-start | bytes 4128776 | tf_op jit(solution)/shard_map/ppermute | solution.py:13
  170.4 15.3 %collective-permute-start.7 = (bf16[2,24,14336]{2,1,0:T(8,128)(2,1)}, bf16[2,24,14336]{2,1,0:T(8,128)(2,1)}, u32[]{:S(2)}, u32[]{:S(2)}) collective-permute-start(bf16[2,24,14336]{2,1,0:T(8,128)(2,1)} %get-tuple-element.47), channel_id=1, source_target_pairs={{0,1},{1,0},{2,3},{3,2},{4,5},{5,4},{6,7},{7,6},{8,9},{9,8},{10,11... | collective-permute-start | bytes 4128776 | tf_op jit(solution)/shard_map/ppermute | solution.py:13
  171.0 16.2 %collective-permute-start.4 = (bf16[2,24,14336]{2,1,0:T(8,128)(2,1)}, bf16[2,24,14336]{2,1,0:T(8,128)(2,1)}, u32[]{:S(2)}, u32[]{:S(2)}) collective-permute-start(bf16[2,24,14336]{2,1,0:T(8,128)(2,1)} %get-tuple-element.45), channel_id=1, source_target_pairs={{0,1},{1,0},{2,3},{3,2},{4,5},{5,4},{6,7},{7,6},{8,9},{9,8},{10,11... | collective-permute-start | bytes 4128776 | tf_op jit(solution)/shard_map/ppermute | solution.py:13
  172.3 2.0 copy-start
  174.4 2.0 copy-start.2
  176.4 2.0 copy-start.4
  181.9 8.4 %collective-permute-start.22 = (bf16[2,4,24,7168]{3,2,1,0:T(8,128)(2,1)}, bf16[2,4,24,7168]{3,2,1,0:T(8,128)(2,1)S(1)}, u32[]{:S(2)}, u32[]{:S(2)}) collective-permute-start(bf16[2,4,24,7168]{3,2,1,0:T(8,128)(2,1)} %bitcast.51), channel_id=1, source_target_pairs={{0,1},{1,0},{2,3},{3,2},{4,5},{5,4},{6,7},{7,6},{8,9},{9,8},{10,11... | collective-permute-start | bytes 8257544 | tf_op jit(solution)/shard_map/ppermute | solution.py:13
  193.2 3.8 %copy-start.1 = (bf16[1,7168,256]{2,1,0:T(8,128)(2,1)S(1)}, bf16[1,7168,256]{2,1,0:T(8,128)(2,1)}, u32[]{:S(2)}) copy-start(bf16[1,7168,256]{2,1,0:T(8,128)(2,1)} %param.17) | copy-start | bytes 11010052
  197.0 2.0 copy-start.3
  211.5 5.2 %collective-permute-start.31 = (bf16[2,4,24,7168]{3,2,1,0:T(8,128)(2,1)S(1)}, bf16[2,4,24,7168]{3,2,1,0:T(8,128)(2,1)S(1)}, u32[]{:S(2)}, u32[]{:S(2)}) collective-permute-start(bf16[2,4,24,7168]{3,2,1,0:T(8,128)(2,1)S(1)} %bitcast.205), channel_id=1, source_target_pairs={{0,1},{1,0},{2,3},{3,2},{4,5},{5,4},{6,7},{7,6},{8,9},{9,8},{10,11... | collective-permute-start | bytes 8257544 | tf_op jit(solution)/shard_map/ppermute | solution.py:13
  212.1 10.9 %collective-permute-start.23 = (bf16[24,7168]{1,0:T(8,128)(2,1)S(1)}, bf16[24,7168]{1,0:T(8,128)(2,1)S(1)}, u32[]{:S(2)}, u32[]{:S(2)}) collective-permute-start(bf16[24,7168]{1,0:T(8,128)(2,1)S(1)} %get-tuple-element.28), channel_id=1, source_target_pairs={{0,2},{2,0},{1,3},{3,1},{4,6},{6,4},{5,7},{7,5},{8,10},{10,8},{9,1... | collective-permute-start | bytes 1032200 | tf_op jit(solution)/shard_map/ppermute | solution.py:13
  212.7 17.7 %collective-permute-start.28 = (bf16[24,7168]{1,0:T(8,128)(2,1)S(1)}, bf16[24,7168]{1,0:T(8,128)(2,1)S(1)}, u32[]{:S(2)}, u32[]{:S(2)}) collective-permute-start(bf16[24,7168]{1,0:T(8,128)(2,1)S(1)} %get-tuple-element.29), channel_id=1, source_target_pairs={{0,2},{2,0},{1,3},{3,1},{4,6},{6,4},{5,7},{7,5},{8,10},{10,8},{9,1... | collective-permute-start | bytes 1032200 | tf_op jit(solution)/shard_map/ppermute | solution.py:13
  214.1 23.6 %collective-permute-start.26 = (bf16[24,7168]{1,0:T(8,128)(2,1)S(1)}, bf16[24,7168]{1,0:T(8,128)(2,1)S(1)}, u32[]{:S(2)}, u32[]{:S(2)}) collective-permute-start(bf16[24,7168]{1,0:T(8,128)(2,1)S(1)} %get-tuple-element.30), channel_id=1, source_target_pairs={{0,2},{2,0},{1,3},{3,1},{4,6},{6,4},{5,7},{7,5},{8,10},{10,8},{9,1... | collective-permute-start | bytes 1032200 | tf_op jit(solution)/shard_map/ppermute | solution.py:13
  214.7 30.4 %collective-permute-start.24 = (bf16[24,7168]{1,0:T(8,128)(2,1)S(1)}, bf16[24,7168]{1,0:T(8,128)(2,1)S(1)}, u32[]{:S(2)}, u32[]{:S(2)}) collective-permute-start(bf16[24,7168]{1,0:T(8,128)(2,1)S(1)} %get-tuple-element.31), channel_id=1, source_target_pairs={{0,2},{2,0},{1,3},{3,1},{4,6},{6,4},{5,7},{7,5},{8,10},{10,8},{9,1... | collective-permute-start | bytes 1032200 | tf_op jit(solution)/shard_map/ppermute | solution.py:13
  217.8 34.7 %collective-permute-start.32 = (bf16[24,7168]{1,0:T(8,128)(2,1)S(1)}, bf16[24,7168]{1,0:T(8,128)(2,1)S(1)}, u32[]{:S(2)}, u32[]{:S(2)}) collective-permute-start(bf16[24,7168]{1,0:T(8,128)(2,1)S(1)} %get-tuple-element.24), channel_id=1, source_target_pairs={{0,2},{2,0},{1,3},{3,1},{4,6},{6,4},{5,7},{7,5},{8,10},{10,8},{9,1... | collective-permute-start | bytes 1032200 | tf_op jit(solution)/shard_map/ppermute | solution.py:13
  223.0 36.9 %collective-permute-start.35 = (bf16[24,7168]{1,0:T(8,128)(2,1)S(1)}, bf16[24,7168]{1,0:T(8,128)(2,1)S(1)}, u32[]{:S(2)}, u32[]{:S(2)}) collective-permute-start(bf16[24,7168]{1,0:T(8,128)(2,1)S(1)} %get-tuple-element.26), channel_id=1, source_target_pairs={{0,2},{2,0},{1,3},{3,1},{4,6},{6,4},{5,7},{7,5},{8,10},{10,8},{9,1... | collective-permute-start | bytes 1032200 | tf_op jit(solution)/shard_map/ppermute | solution.py:13
  230.4 36.9 %collective-permute-start.33 = (bf16[24,7168]{1,0:T(8,128)(2,1)S(1)}, bf16[24,7168]{1,0:T(8,128)(2,1)S(1)}, u32[]{:S(2)}, u32[]{:S(2)}) collective-permute-start(bf16[24,7168]{1,0:T(8,128)(2,1)S(1)} %get-tuple-element.27), channel_id=1, source_target_pairs={{0,2},{2,0},{1,3},{3,1},{4,6},{6,4},{5,7},{7,5},{8,10},{10,8},{9,1... | collective-permute-start | bytes 1032200 | tf_op jit(solution)/shard_map/ppermute | solution.py:13
  237.7 36.4 %collective-permute-start.37 = (bf16[24,7168]{1,0:T(8,128)(2,1)S(1)}, bf16[24,7168]{1,0:T(8,128)(2,1)S(1)}, u32[]{:S(2)}, u32[]{:S(2)}) collective-permute-start(bf16[24,7168]{1,0:T(8,128)(2,1)S(1)} %get-tuple-element.25), channel_id=1, source_target_pairs={{0,2},{2,0},{1,3},{3,1},{4,6},{6,4},{5,7},{7,5},{8,10},{10,8},{9,1... | collective-permute-start | bytes 1032200 | tf_op jit(solution)/shard_map/ppermute | solution.py:13
  245.4 33.2 %collective-permute-start.29 = (bf16[24,7168]{1,0:T(8,128)(2,1)S(1)}, bf16[24,7168]{1,0:T(8,128)(2,1)S(1)}, u32[]{:S(2)}, u32[]{:S(2)}) collective-permute-start(bf16[24,7168]{1,0:T(8,128)(2,1)S(1)} %get-tuple-element.19), channel_id=1, source_target_pairs={{0,12},{4,8},{8,4},{12,0},{1,13},{5,9},{9,5},{13,1},{2,14},{6,10},... | collective-permute-start | bytes 1032200 | tf_op jit(solution)/shard_map/ppermute | solution.py:100
  252.5 26.1 %collective-permute-start.27 = (bf16[24,7168]{1,0:T(8,128)(2,1)S(1)}, bf16[24,7168]{1,0:T(8,128)(2,1)S(1)}, u32[]{:S(2)}, u32[]{:S(2)}) collective-permute-start(bf16[24,7168]{1,0:T(8,128)(2,1)S(1)} %get-tuple-element.20), channel_id=1, source_target_pairs={{0,8},{4,12},{8,0},{12,4},{1,9},{5,13},{9,1},{13,5},{2,10},{6,14},... | collective-permute-start | bytes 1032200 | tf_op jit(solution)/shard_map/ppermute | solution.py:100
  259.9 18.8 %collective-permute-start.25 = (bf16[24,7168]{1,0:T(8,128)(2,1)S(1)}, bf16[24,7168]{1,0:T(8,128)(2,1)S(1)}, u32[]{:S(2)}, u32[]{:S(2)}) collective-permute-start(bf16[24,7168]{1,0:T(8,128)(2,1)S(1)} %get-tuple-element.21), channel_id=1, source_target_pairs={{0,4},{4,0},{8,12},{12,8},{1,5},{5,1},{9,13},{13,9},{2,6},{6,2},{1... | collective-permute-start | bytes 1032200 | tf_op jit(solution)/shard_map/ppermute | solution.py:100
  274.4 4.4 %copy-start.5 = (bf16[1,32,7168]{2,1,0:T(8,128)(2,1)S(1)}, bf16[1,32,7168]{2,1,0:T(8,128)(2,1)}, u32[]{:S(2)}) copy-start(bf16[1,32,7168]{2,1,0:T(8,128)(2,1)} %param.10) | copy-start | bytes 1376260
  274.4 25.8 %collective-permute-start.38 = (bf16[24,7168]{1,0:T(8,128)(2,1)S(1)}, bf16[24,7168]{1,0:T(8,128)(2,1)S(1)}, u32[]{:S(2)}, u32[]{:S(2)}) collective-permute-start(bf16[24,7168]{1,0:T(8,128)(2,1)S(1)} %get-tuple-element.13), channel_id=1, source_target_pairs={{0,12},{4,8},{8,4},{12,0},{1,13},{5,9},{9,5},{13,1},{2,14},{6,10},... | collective-permute-start | bytes 1032200 | tf_op jit(solution)/shard_map/ppermute | solution.py:100
  275.5 29.3 %collective-permute-start.36 = (bf16[24,7168]{1,0:T(8,128)(2,1)S(1)}, bf16[24,7168]{1,0:T(8,128)(2,1)S(1)}, u32[]{:S(2)}, u32[]{:S(2)}) collective-permute-start(bf16[24,7168]{1,0:T(8,128)(2,1)S(1)} %get-tuple-element.11), channel_id=1, source_target_pairs={{0,8},{4,12},{8,0},{12,4},{1,9},{5,13},{9,1},{13,5},{2,10},{6,14},... | collective-permute-start | bytes 1032200 | tf_op jit(solution)/shard_map/ppermute | solution.py:100
  278.6 26.2 %collective-permute-start.34 = (bf16[24,7168]{1,0:T(8,128)(2,1)S(1)}, bf16[24,7168]{1,0:T(8,128)(2,1)S(1)}, u32[]{:S(2)}, u32[]{:S(2)}) collective-permute-start(bf16[24,7168]{1,0:T(8,128)(2,1)S(1)} %get-tuple-element.12), channel_id=1, source_target_pairs={{0,4},{4,0},{8,12},{12,8},{1,5},{5,1},{9,13},{13,9},{2,6},{6,2},{1... | collective-permute-start | bytes 1032200 | tf_op jit(solution)/shard_map/ppermute | solution.py:100
  279.5 27.9 %collective-permute-start.30 = (bf16[1,32,7168]{2,1,0:T(8,128)(2,1)S(1)}, bf16[1,32,7168]{2,1,0:T(8,128)(2,1)S(1)}, u32[]{:S(2)}, u32[]{:S(2)}) collective-permute-start(bf16[1,32,7168]{2,1,0:T(8,128)(2,1)S(1)} %fusion.3), channel_id=1, source_target_pairs={{0,16},{16,0},{1,17},{17,1},{2,18},{18,2},{3,19},{19,3},{4,20},{20... | collective-permute-start | bytes 1376264 | tf_op jit(solution)/shard_map/ppermute | solution.py:19
  305.7 11.3 %collective-permute-start.39 = (bf16[1,32,7168]{2,1,0:T(8,128)(2,1)S(1)}, bf16[1,32,7168]{2,1,0:T(8,128)(2,1)S(1)}, u32[]{:S(2)}, u32[]{:S(2)}) collective-permute-start(bf16[1,32,7168]{2,1,0:T(8,128)(2,1)S(1)} %fusion.2), channel_id=1, source_target_pairs={{0,16},{16,0},{1,17},{17,1},{2,18},{18,2},{3,19},{19,3},{4,20},{20... | collective-permute-start | bytes 1376264 | tf_op jit(solution)/shard_map/ppermute | solution.py:19

commit v11 on v5

--- a/solution.py
+++ b/solution.py
@@ -124,6 +124,7 @@
     b_joined = jnp.concatenate([bwd_input[0], bwd_grad[0]], axis=1)
     b_slots = into_slots(b_select, b_joined).reshape(experts, capacity, 2 * width)
     f_rows = dispatch(f_slots)
+    b_slots, f_rows = lax.optimization_barrier((b_slots, f_rows))
     b_rows = dispatch(b_slots)
     f_partial = forward_rows(f_rows.reshape(-1, width), w_gate, w_up, w_down)
     f_totals = reduce_group(f_partial.reshape(2, 2, experts, capacity, width))

time: 275 us -> 283 us (1.029)
  waiting for transfers between devices: 187 us -> 199 us
    ppermute x6, waiting for transfers between devices: 37.3 us -> 81 us  [dispatch(): received = lax.ppermute(slots[d], 'z', [(i, i ^ d) for i in range(count)])]
    ppermute x26, waiting for transfers between devices: 105 us -> 73.7 us  [swap(): return lax.ppermute(value, axis, [(0, 1), (1, 0)])]
  transfers between devices with their start and end apart: 40 -> 40, of which waited for: 25 -> 22; matrix products, arithmetic and copies ran while one was open for 8% -> 8% of each run, Pallas kernels for 0% -> 0%
where the time goes in v11:
time: 283 us; the launch traced here: 282 us
  waiting for transfers between devices  199 us (70%)
  starting transfers between devices  36 us (13%)
  other arithmetic  19.4 us (7%)
  matrix products  19.1 us (7%)
  local copies, waits for them, and re-layouts  7.54 us (3%)
    ppermute x6, waiting for transfers between devices, dispatch(): received = lax.ppermute(slots[d], 'z', [(i, i ^ d) for i in range(count)])  81 us
    ppermute x26, waiting for transfers between devices, swap(): return lax.ppermute(value, axis, [(0, 1), (1, 0)])  73.7 us
    ppermute x6, waiting for transfers between devices, returned(): out.append(lax.ppermute(totals[d], 'z', [(i, i ^ d) for i in range(count)]))  33.3 us
    ppermute x26, starting transfers between devices, swap(): return lax.ppermute(value, axis, [(0, 1), (1, 0)])  18.8 us
    ppermute x2, waiting for transfers between devices, passed_along(): return lax.ppermute(value, axis, pairs)  10.8 us
    ppermute x6, starting transfers between devices, dispatch(): received = lax.ppermute(slots[d], 'z', [(i, i ^ d) for i in range(count)])  7.1 us
    another operation x10, other arithmetic, dispatch(): return jnp.stack(pieces, axis=2)  6.84 us
    ppermute x6, starting transfers between devices, returned(): out.append(lax.ppermute(totals[d], 'z', [(i, i ^ d) for i in range(count)]))  6.83 us
  transfers between devices with their start and end apart: 40, of which 22 were waited for; matrix products, arithmetic and copies ran while one was open for 8% of the time, Pallas kernels for 0%

profile of v11, /device:TPU:16, one launch (start us, length us, event | category | flops | bytes accessed | tf_op | source)
XLA Modules:
  0.0 282.0 jit_solution(3137581084415253885)
XLA Ops:
  3.0 1.6 convolution_convert_fusion.2
  4.7 1.6 collective-permute-start.2
  6.7 1.6 collective-permute-start.8
  8.3 1.5 collective-permute-start
  11.5 8.2 %collective-permute-done.2 = bf16[24,7168]{1,0:T(8,128)(2,1)} collective-permute-done((bf16[24,7168]{1,0:T(8,128)(2,1)S(1)}, bf16[24,7168]{1,0:T(8,128)(2,1)}, u32[]{:S(2)}, u32[]{:S(2)}) %collective-permute-start.2) | collective-permute-done | bytes 344096 | tf_op jit(solution)/shard_map/ppermute | solution.py:77
  19.7 1.5 collective-permute-start.3
  21.2 1.1 fusion.78
  22.4 7.6 %collective-permute-done.5 = bf16[24,7168]{1,0:T(8,128)(2,1)S(1)} collective-permute-done((bf16[24,7168]{1,0:T(8,128)(2,1)S(1)}, bf16[24,7168]{1,0:T(8,128)(2,1)S(1)}, u32[]{:S(2)}, u32[]{:S(2)}) %collective-permute-start.5) | collective-permute-done | bytes 344096 | tf_op jit(solution)/shard_map/ppermute | solution.py:77
  29.9 1.5 collective-permute-start.6
  31.4 6.5 %collective-permute-done.8 = bf16[24,7168]{1,0:T(8,128)(2,1)S(1)} collective-permute-done((bf16[24,7168]{1,0:T(8,128)(2,1)S(1)}, bf16[24,7168]{1,0:T(8,128)(2,1)S(1)}, u32[]{:S(2)}, u32[]{:S(2)}) %collective-permute-start.8) | collective-permute-done | bytes 344096 | tf_op jit(solution)/shard_map/ppermute | solution.py:77
  37.9 1.5 collective-permute-start.9
  39.4 1.1 fusion.77
  41.2 5.3 %collective-permute-done.9 = bf16[24,7168]{1,0:T(8,128)(2,1)S(1)} collective-permute-done((bf16[24,7168]{1,0:T(8,128)(2,1)S(1)}, bf16[24,7168]{1,0:T(8,128)(2,1)S(1)}, u32[]{:S(2)}, u32[]{:S(2)}) %collective-permute-start.9) | collective-permute-done | bytes 344096 | tf_op jit(solution)/shard_map/ppermute | solution.py:13
  47.2 1.7 collective-permute-done.10
  49.0 0.9 pad_maximum_fusion.1
  50.4 1.1 fusion.87
  51.6 1.5 collective-permute-start.11
  53.1 1.6 fusion.19
  55.1 1.6 fusion.44
  57.2 1.6 convolution_convert_fusion.1
  59.2 2.0 collective-permute-start.16
  61.2 1.6 collective-permute-start.19
  62.8 12.2 %collective-permute-done.13 = bf16[24,14336]{1,0:T(8,128)(2,1)S(1)} collective-permute-done((bf16[24,14336]{1,0:T(8,128)(2,1)}, bf16[24,14336]{1,0:T(8,128)(2,1)S(1)}, u32[]{:S(2)}, u32[]{:S(2)}) %collective-permute-start.13) | collective-permute-done | bytes 688160 | tf_op jit(solution)/shard_map/ppermute | solution.py:77
  75.8 30.7 %collective-permute-done.16 = bf16[24,14336]{1,0:T(8,128)(2,1)S(1)} collective-permute-done((bf16[24,14336]{1,0:T(8,128)(2,1)S(1)}, bf16[24,14336]{1,0:T(8,128)(2,1)S(1)}, u32[]{:S(2)}, u32[]{:S(2)}) %collective-permute-start.16) | collective-permute-done | bytes 688160 | tf_op jit(solution)/shard_map/ppermute | solution.py:77
  107.0 15.8 %collective-permute-done.19 = bf16[24,14336]{1,0:T(8,128)(2,1)S(1)} collective-permute-done((bf16[24,14336]{1,0:T(8,128)(2,1)S(1)}, bf16[24,14336]{1,0:T(8,128)(2,1)S(1)}, u32[]{:S(2)}, u32[]{:S(2)}) %collective-permute-start.19) | collective-permute-done | bytes 688160 | tf_op jit(solution)/shard_map/ppermute | solution.py:77
  123.4 1.3 fusion.83
  124.7 1.3 fusion.82
  126.4 13.4 %collective-permute-done.20 = bf16[24,14336]{1,0:T(8,128)(2,1)S(1)} collective-permute-done((bf16[24,14336]{1,0:T(8,128)(2,1)S(1)}, bf16[24,14336]{1,0:T(8,128)(2,1)S(1)}, u32[]{:S(2)}, u32[]{:S(2)}) %collective-permute-start.20) | collective-permute-done | bytes 688160 | tf_op jit(solution)/shard_map/ppermute | solution.py:13
  139.8 1.3 fusion.81
  141.4 1.0 fusion.79
  143.2 1.5 collective-permute-start.24
  145.2 1.6 maximum_bitcast_fusion.1
  146.8 1.6 collective-permute-start.26
  148.6 1.6 maximum_bitcast_fusion.3
  150.2 1.7 pad_maximum_fusion
  151.9 1.6 collective-permute-done.23
  153.5 7.4 %collective-permute-done.24 = bf16[24,7168]{1,0:T(8,128)(2,1)S(1)} collective-permute-done((bf16[24,7168]{1,0:T(8,128)(2,1)S(1)}, bf16[24,7168]{1,0:T(8,128)(2,1)S(1)}, u32[]{:S(2)}, u32[]{:S(2)}) %collective-permute-start.24) | collective-permute-done | bytes 344096 | tf_op jit(solution)/shard_map/ppermute | solution.py:13
  160.9 7.4 %collective-permute-done.25 = bf16[24,7168]{1,0:T(8,128)(2,1)S(1)} collective-permute-done((bf16[24,7168]{1,0:T(8,128)(2,1)S(1)}, bf16[24,7168]{1,0:T(8,128)(2,1)S(1)}, u32[]{:S(2)}, u32[]{:S(2)}) %collective-permute-start.25) | collective-permute-done | bytes 344096 | tf_op jit(solution)/shard_map/ppermute | solution.py:13
  168.2 7.0 %collective-permute-done.26 = bf16[24,7168]{1,0:T(8,128)(2,1)S(1)} collective-permute-done((bf16[24,7168]{1,0:T(8,128)(2,1)S(1)}, bf16[24,7168]{1,0:T(8,128)(2,1)S(1)}, u32[]{:S(2)}, u32[]{:S(2)}) %collective-permute-start.26) | collective-permute-done | bytes 344096 | tf_op jit(solution)/shard_map/ppermute | solution.py:13
  175.2 1.1 fusion.59
  176.4 1.3 copy-done.4
  177.6 1.7 fusion.4
  179.4 1.6 fusion.6
  181.4 1.6 fusion.39
  183.0 1.6 fusion.16
  184.7 3.9 %add_convert_fusion = bf16[384,7168]{1,0:T(8,128)(2,1)S(1)} fusion(f32[384,7168]{1,0:T(8,128)S(1)} %fusion.16, bf16[1,7168,256]{2,1,0:T(8,128)(2,1)} %param.18, f32[384,256]{1,0:T(8,128)S(1)} %fusion.4, f32[384,256]{1,0:T(8,128)} %copy-done.8), kind=kOutput, calls=%fused_computation.2 | convolution fusion | flops 1415380992 | bytes 20971520 | tf_op jit(solution)/shard_map/dot_general | solution.py:64
  189.0 5.1 %collective-permute-done.31 = bf16[2,4,24,7168]{3,2,1,0:T(8,128)(2,1)S(1)} collective-permute-done((bf16[2,4,24,7168]{3,2,1,0:T(8,128)(2,1)S(1)}, bf16[2,4,24,7168]{3,2,1,0:T(8,128)(2,1)S(1)}, u32[]{:S(2)}, u32[]{:S(2)}) %collective-permute-start.31) | collective-permute-done | bytes 2752544 | tf_op jit(solution)/shard_map/ppermute | solution.py:13
  194.1 1.0 fusion.80
  195.9 1.5 collective-permute-start.33
  197.9 1.5 collective-permute-start.37
  199.4 1.5 collective-permute-start.27
  200.9 5.4 %collective-permute-done.32 = bf16[24,7168]{1,0:T(8,128)(2,1)S(1)} collective-permute-done((bf16[24,7168]{1,0:T(8,128)(2,1)S(1)}, bf16[24,7168]{1,0:T(8,128)(2,1)S(1)}, u32[]{:S(2)}, u32[]{:S(2)}) %collective-permute-start.32) | collective-permute-done | bytes 344096 | tf_op jit(solution)/shard_map/ppermute | solution.py:13
  206.3 1.4 collective-permute-start.28
  207.6 6.0 %collective-permute-done.33 = bf16[24,7168]{1,0:T(8,128)(2,1)S(1)} collective-permute-done((bf16[24,7168]{1,0:T(8,128)(2,1)S(1)}, bf16[24,7168]{1,0:T(8,128)(2,1)S(1)}, u32[]{:S(2)}, u32[]{:S(2)}) %collective-permute-start.33) | collective-permute-done | bytes 344096 | tf_op jit(solution)/shard_map/ppermute | solution.py:13
  214.1 6.9 %collective-permute-done.35 = bf16[24,7168]{1,0:T(8,128)(2,1)S(1)} collective-permute-done((bf16[24,7168]{1,0:T(8,128)(2,1)S(1)}, bf16[24,7168]{1,0:T(8,128)(2,1)S(1)}, u32[]{:S(2)}, u32[]{:S(2)}) %collective-permute-start.35) | collective-permute-done | bytes 344096 | tf_op jit(solution)/shard_map/ppermute | solution.py:13
  221.0 6.5 %collective-permute-done.37 = bf16[24,7168]{1,0:T(8,128)(2,1)S(1)} collective-permute-done((bf16[24,7168]{1,0:T(8,128)(2,1)S(1)}, bf16[24,7168]{1,0:T(8,128)(2,1)S(1)}, u32[]{:S(2)}, u32[]{:S(2)}) %collective-permute-start.37) | collective-permute-done | bytes 344096 | tf_op jit(solution)/shard_map/ppermute | solution.py:13
  227.9 1.5 collective-permute-start.34
  229.9 1.6 collective-permute-start.38
  231.4 21.2 %collective-permute-done.29 = bf16[24,7168]{1,0:T(8,128)(2,1)S(1)} collective-permute-done((bf16[24,7168]{1,0:T(8,128)(2,1)S(1)}, bf16[24,7168]{1,0:T(8,128)(2,1)S(1)}, u32[]{:S(2)}, u32[]{:S(2)}) %collective-permute-start.29) | collective-permute-done | bytes 344096 | tf_op jit(solution)/shard_map/ppermute | solution.py:97
  253.5 1.6 collective-permute-start.30
  255.1 4.1 %collective-permute-done.36 = bf16[24,7168]{1,0:T(8,128)(2,1)S(1)} collective-permute-done((bf16[24,7168]{1,0:T(8,128)(2,1)S(1)}, bf16[24,7168]{1,0:T(8,128)(2,1)S(1)}, u32[]{:S(2)}, u32[]{:S(2)}) %collective-permute-start.36) | collective-permute-done | bytes 344096 | tf_op jit(solution)/shard_map/ppermute | solution.py:97
  259.1 8.1 %collective-permute-done.38 = bf16[24,7168]{1,0:T(8,128)(2,1)S(1)} collective-permute-done((bf16[24,7168]{1,0:T(8,128)(2,1)S(1)}, bf16[24,7168]{1,0:T(8,128)(2,1)S(1)}, u32[]{:S(2)}, u32[]{:S(2)}) %collective-permute-start.38) | collective-permute-done | bytes 344096 | tf_op jit(solution)/shard_map/ppermute | solution.py:97
  268.1 1.6 collective-permute-start.39
  269.7 10.8 %collective-permute-done.39 = bf16[1,32,7168]{2,1,0:T(8,128)(2,1)S(1)} collective-permute-done((bf16[1,32,7168]{2,1,0:T(8,128)(2,1)S(1)}, bf16[1,32,7168]{2,1,0:T(8,128)(2,1)S(1)}, u32[]{:S(2)}, u32[]{:S(2)}) %collective-permute-start.39) | collective-permute-done | bytes 458784 | tf_op jit(solution)/shard_map/ppermute | solution.py:19
  (106 shorter events, 18.3 us)
Async XLA Ops:
  0.6 9.9 %copy-start.12 = (f32[1,32,2]{1,2,0:T(2,128)S(1)}, f32[1,32,2]{1,2,0:T(2,128)}, u32[]{:S(2)}) copy-start(f32[1,32,2]{1,2,0:T(2,128)} %param.16) | copy-start | bytes 772
  0.6 10.0 %copy-start.7 = (bf16[1,32,7168]{2,1,0:T(8,128)(2,1)S(1)}, bf16[1,32,7168]{2,1,0:T(8,128)(2,1)}, u32[]{:S(2)}) copy-start(bf16[1,32,7168]{2,1,0:T(8,128)(2,1)} %param.13) | copy-start | bytes 1376260
  0.7 10.0 %copy-start.6 = (bf16[1,32,7168]{2,1,0:T(8,128)(2,1)S(1)}, bf16[1,32,7168]{2,1,0:T(8,128)(2,1)}, u32[]{:S(2)}) copy-start(bf16[1,32,7168]{2,1,0:T(8,128)(2,1)} %param.14) | copy-start | bytes 1376260
  4.7 15.0 %collective-permute-start.2 = (bf16[24,7168]{1,0:T(8,128)(2,1)S(1)}, bf16[24,7168]{1,0:T(8,128)(2,1)}, u32[]{:S(2)}, u32[]{:S(2)}) collective-permute-start(bf16[24,7168]{1,0:T(8,128)(2,1)S(1)} %get-tuple-element.60), channel_id=1, source_target_pairs={{0,4},{4,0},{8,12},{12,8},{1,5},{5,1},{9,13},{13,9},{2,6},{6,2},{1... | collective-permute-start | bytes 1032200 | tf_op jit(solution)/shard_map/ppermute | solution.py:77
  6.4 23.6 %collective-permute-start.5 = (bf16[24,7168]{1,0:T(8,128)(2,1)S(1)}, bf16[24,7168]{1,0:T(8,128)(2,1)S(1)}, u32[]{:S(2)}, u32[]{:S(2)}) collective-permute-start(bf16[24,7168]{1,0:T(8,128)(2,1)S(1)} %get-tuple-element.59), channel_id=1, source_target_pairs={{0,8},{4,12},{8,0},{12,4},{1,9},{5,13},{9,1},{13,5},{2,10},{6,14},... | collective-permute-start | bytes 1032200 | tf_op jit(solution)/shard_map/ppermute | solution.py:77
  6.7 31.2 %collective-permute-start.8 = (bf16[24,7168]{1,0:T(8,128)(2,1)S(1)}, bf16[24,7168]{1,0:T(8,128)(2,1)S(1)}, u32[]{:S(2)}, u32[]{:S(2)}) collective-permute-start(bf16[24,7168]{1,0:T(8,128)(2,1)S(1)} %get-tuple-element.58), channel_id=1, source_target_pairs={{0,12},{4,8},{8,4},{12,0},{1,13},{5,9},{9,5},{13,1},{2,14},{6,10},... | collective-permute-start | bytes 1032200 | tf_op jit(solution)/shard_map/ppermute | solution.py:77
  8.3 12.9 %collective-permute-start = (bf16[24,7168]{1,0:T(8,128)(2,1)S(1)}, bf16[24,7168]{1,0:T(8,128)(2,1)}, u32[]{:S(2)}, u32[]{:S(2)}) collective-permute-start(bf16[24,7168]{1,0:T(8,128)(2,1)S(1)} %get-tuple-element.61), channel_id=1, source_target_pairs={{0,2},{2,0},{1,3},{3,1},{4,6},{6,4},{5,7},{7,5},{8,10},{10,8},{9,1... | collective-permute-start | bytes 1032200 | tf_op jit(solution)/shard_map/ppermute | solution.py:13
  19.7 19.7 %collective-permute-start.3 = (bf16[24,7168]{1,0:T(8,128)(2,1)}, bf16[24,7168]{1,0:T(8,128)(2,1)S(1)}, u32[]{:S(2)}, u32[]{:S(2)}) collective-permute-start(bf16[24,7168]{1,0:T(8,128)(2,1)} %collective-permute-done.2), channel_id=1, source_target_pairs={{0,2},{2,0},{1,3},{3,1},{4,6},{6,4},{5,7},{7,5},{8,10},{10,8},{9,1... | collective-permute-start | bytes 1032200 | tf_op jit(solution)/shard_map/ppermute | solution.py:13
  22.3 24.5 %collective-permute-start.1 = (bf16[2,24,7168]{2,1,0:T(8,128)(2,1)S(1)}, bf16[2,24,7168]{2,1,0:T(8,128)(2,1)S(1)}, u32[]{:S(2)}, u32[]{:S(2)}) collective-permute-start(bf16[2,24,7168]{2,1,0:T(8,128)(2,1)S(1)} %get-tuple-element.63), channel_id=1, source_target_pairs={{0,1},{1,0},{2,3},{3,2},{4,5},{5,4},{6,7},{7,6},{8,9},{9,8},{10,11... | collective-permute-start | bytes 2064392 | tf_op jit(solution)/shard_map/ppermute | solution.py:13
  29.9 10.6 %collective-permute-start.6 = (bf16[24,7168]{1,0:T(8,128)(2,1)S(1)}, bf16[24,7168]{1,0:T(8,128)(2,1)S(1)}, u32[]{:S(2)}, u32[]{:S(2)}) collective-permute-start(bf16[24,7168]{1,0:T(8,128)(2,1)S(1)} %collective-permute-done.5), channel_id=1, source_target_pairs={{0,2},{2,0},{1,3},{3,1},{4,6},{6,4},{5,7},{7,5},{8,10},{10,8},{9,1... | collective-permute-start | bytes 1032200 | tf_op jit(solution)/shard_map/ppermute | solution.py:13
  37.9 8.7 %collective-permute-start.9 = (bf16[24,7168]{1,0:T(8,128)(2,1)S(1)}, bf16[24,7168]{1,0:T(8,128)(2,1)S(1)}, u32[]{:S(2)}, u32[]{:S(2)}) collective-permute-start(bf16[24,7168]{1,0:T(8,128)(2,1)S(1)} %collective-permute-done.8), channel_id=1, source_target_pairs={{0,2},{2,0},{1,3},{3,1},{4,6},{6,4},{5,7},{7,5},{8,10},{10,8},{9,1... | collective-permute-start | bytes 1032200 | tf_op jit(solution)/shard_map/ppermute | solution.py:13
  40.5 6.4 %collective-permute-start.4 = (bf16[2,24,7168]{2,1,0:T(8,128)(2,1)S(1)}, bf16[2,24,7168]{2,1,0:T(8,128)(2,1)S(1)}, u32[]{:S(2)}, u32[]{:S(2)}) collective-permute-start(bf16[2,24,7168]{2,1,0:T(8,128)(2,1)S(1)} %get-tuple-element.65), channel_id=1, source_target_pairs={{0,1},{1,0},{2,3},{3,2},{4,5},{5,4},{6,7},{7,6},{8,9},{9,8},{10,11... | collective-permute-start | bytes 2064392 | tf_op jit(solution)/shard_map/ppermute | solution.py:13
  40.7 6.4 %collective-permute-start.7 = (bf16[2,24,7168]{2,1,0:T(8,128)(2,1)S(1)}, bf16[2,24,7168]{2,1,0:T(8,128)(2,1)S(1)}, u32[]{:S(2)}, u32[]{:S(2)}) collective-permute-start(bf16[2,24,7168]{2,1,0:T(8,128)(2,1)S(1)} %get-tuple-element.67), channel_id=1, source_target_pairs={{0,1},{1,0},{2,3},{3,2},{4,5},{5,4},{6,7},{7,6},{8,9},{9,8},{10,11... | collective-permute-start | bytes 2064392 | tf_op jit(solution)/shard_map/ppermute | solution.py:13
  46.7 2.2 collective-permute-start.10
  50.4 2.7 copy-start
  51.6 24.0 %collective-permute-start.11 = (bf16[24,14336]{1,0:T(8,128)(2,1)S(1)}, bf16[24,14336]{1,0:T(8,128)(2,1)S(1)}, u32[]{:S(2)}, u32[]{:S(2)}) collective-permute-start(bf16[24,14336]{1,0:T(8,128)(2,1)S(1)} %get-tuple-element.45), channel_id=1, source_target_pairs={{0,2},{2,0},{1,3},{3,1},{4,6},{6,4},{5,7},{7,5},{8,10},{10,8},{9,1... | collective-permute-start | bytes 2064392 | tf_op jit(solution)/shard_map/ppermute | solution.py:13
  53.1 22.0 %collective-permute-start.13 = (bf16[24,14336]{1,0:T(8,128)(2,1)}, bf16[24,14336]{1,0:T(8,128)(2,1)S(1)}, u32[]{:S(2)}, u32[]{:S(2)}) collective-permute-start(bf16[24,14336]{1,0:T(8,128)(2,1)} %get-tuple-element.48), channel_id=1, source_target_pairs={{0,4},{4,0},{8,12},{12,8},{1,5},{5,1},{9,13},{13,9},{2,6},{6,2},{1... | collective-permute-start | bytes 2064392 | tf_op jit(solution)/shard_map/ppermute | solution.py:77
  53.1 2.0 copy-start.1
  55.1 2.0 copy-start.3
  59.2 82.3 %collective-permute-start.22 = (bf16[2,4,24,7168]{3,2,1,0:T(8,128)(2,1)S(1)}, bf16[2,4,24,7168]{3,2,1,0:T(8,128)(2,1)S(1)}, u32[]{:S(2)}, u32[]{:S(2)}) collective-permute-start(bf16[2,4,24,7168]{3,2,1,0:T(8,128)(2,1)S(1)} %bitcast.224), channel_id=1, source_target_pairs={{0,1},{1,0},{2,3},{3,2},{4,5},{5,4},{6,7},{7,6},{8,9},{9,8},{10,11... | collective-permute-start | bytes 8257544 | tf_op jit(solution)/shard_map/ppermute | solution.py:13
  59.2 47.3 %collective-permute-start.16 = (bf16[24,14336]{1,0:T(8,128)(2,1)S(1)}, bf16[24,14336]{1,0:T(8,128)(2,1)S(1)}, u32[]{:S(2)}, u32[]{:S(2)}) collective-permute-start(bf16[24,14336]{1,0:T(8,128)(2,1)S(1)} %get-tuple-element.47), channel_id=1, source_target_pairs={{0,8},{4,12},{8,0},{12,4},{1,9},{5,13},{9,1},{13,5},{2,10},{6,14},... | collective-permute-start | bytes 2064392 | tf_op jit(solution)/shard_map/ppermute | solution.py:77
  61.2 61.6 %collective-permute-start.19 = (bf16[24,14336]{1,0:T(8,128)(2,1)S(1)}, bf16[24,14336]{1,0:T(8,128)(2,1)S(1)}, u32[]{:S(2)}, u32[]{:S(2)}) collective-permute-start(bf16[24,14336]{1,0:T(8,128)(2,1)S(1)} %get-tuple-element.46), channel_id=1, source_target_pairs={{0,12},{4,8},{8,4},{12,0},{1,13},{5,9},{9,5},{13,1},{2,14},{6,10},... | collective-permute-start | bytes 2064392 | tf_op jit(solution)/shard_map/ppermute | solution.py:77
  75.0 48.3 %collective-permute-start.14 = (bf16[24,14336]{1,0:T(8,128)(2,1)S(1)}, bf16[24,14336]{1,0:T(8,128)(2,1)S(1)}, u32[]{:S(2)}, u32[]{:S(2)}) collective-permute-start(bf16[24,14336]{1,0:T(8,128)(2,1)S(1)} %collective-permute-done.13), channel_id=1, source_target_pairs={{0,2},{2,0},{1,3},{3,1},{4,6},{6,4},{5,7},{7,5},{8,10},{10,8},{9,1... | collective-permute-start | bytes 2064392 | tf_op jit(solution)/shard_map/ppermute | solution.py:13
  75.7 65.4 %collective-permute-start.12 = (bf16[2,24,14336]{2,1,0:T(8,128)(2,1)S(1)}, bf16[2,24,14336]{2,1,0:T(8,128)(2,1)S(1)}, u32[]{:S(2)}, u32[]{:S(2)}) collective-permute-start(bf16[2,24,14336]{2,1,0:T(8,128)(2,1)S(1)} %get-tuple-element.50), channel_id=1, source_target_pairs={{0,1},{1,0},{2,3},{3,2},{4,5},{5,4},{6,7},{7,6},{8,9},{9,8},{10,11... | collective-permute-start | bytes 4128776 | tf_op jit(solution)/shard_map/ppermute | solution.py:13
  106.5 18.1 %collective-permute-start.17 = (bf16[24,14336]{1,0:T(8,128)(2,1)S(1)}, bf16[24,14336]{1,0:T(8,128)(2,1)S(1)}, u32[]{:S(2)}, u32[]{:S(2)}) collective-permute-start(bf16[24,14336]{1,0:T(8,128)(2,1)S(1)} %collective-permute-done.16), channel_id=1, source_target_pairs={{0,2},{2,0},{1,3},{3,1},{4,6},{6,4},{5,7},{7,5},{8,10},{10,8},{9,1... | collective-permute-start | bytes 2064392 | tf_op jit(solution)/shard_map/ppermute | solution.py:13
  122.8 17.0 %collective-permute-start.20 = (bf16[24,14336]{1,0:T(8,128)(2,1)S(1)}, bf16[24,14336]{1,0:T(8,128)(2,1)S(1)}, u32[]{:S(2)}, u32[]{:S(2)}) collective-permute-start(bf16[24,14336]{1,0:T(8,128)(2,1)S(1)} %collective-permute-done.19), channel_id=1, source_target_pairs={{0,2},{2,0},{1,3},{3,1},{4,6},{6,4},{5,7},{7,5},{8,10},{10,8},{9,1... | collective-permute-start | bytes 2064392 | tf_op jit(solution)/shard_map/ppermute | solution.py:13
  124.7 20.0 %collective-permute-start.15 = (bf16[2,24,14336]{2,1,0:T(8,128)(2,1)}, bf16[2,24,14336]{2,1,0:T(8,128)(2,1)}, u32[]{:S(2)}, u32[]{:S(2)}) collective-permute-start(bf16[2,24,14336]{2,1,0:T(8,128)(2,1)} %get-tuple-element.52), channel_id=1, source_target_pairs={{0,1},{1,0},{2,3},{3,2},{4,5},{5,4},{6,7},{7,6},{8,9},{9,8},{10,11... | collective-permute-start | bytes 4128776 | tf_op jit(solution)/shard_map/ppermute | solution.py:13
  125.9 20.9 %collective-permute-start.18 = (bf16[2,24,14336]{2,1,0:T(8,128)(2,1)}, bf16[2,24,14336]{2,1,0:T(8,128)(2,1)S(1)}, u32[]{:S(2)}, u32[]{:S(2)}) collective-permute-start(bf16[2,24,14336]{2,1,0:T(8,128)(2,1)} %get-tuple-element.54), channel_id=1, source_target_pairs={{0,1},{1,0},{2,3},{3,2},{4,5},{5,4},{6,7},{7,6},{8,9},{9,8},{10,11... | collective-permute-start | bytes 4128776 | tf_op jit(solution)/shard_map/ppermute | solution.py:13
  141.2 7.5 %collective-permute-start.21 = (bf16[2,24,14336]{2,1,0:T(8,128)(2,1)}, bf16[2,24,14336]{2,1,0:T(8,128)(2,1)}, u32[]{:S(2)}, u32[]{:S(2)}) collective-permute-start(bf16[2,24,14336]{2,1,0:T(8,128)(2,1)} %get-tuple-element.56), channel_id=1, source_target_pairs={{0,1},{1,0},{2,3},{3,2},{4,5},{5,4},{6,7},{7,6},{8,9},{9,8},{10,11... | collective-permute-start | bytes 4128776 | tf_op jit(solution)/shard_map/ppermute | solution.py:13
  142.6 10.9 %collective-permute-start.23 = (bf16[24,7168]{1,0:T(8,128)(2,1)S(1)}, bf16[24,7168]{1,0:T(8,128)(2,1)S(1)}, u32[]{:S(2)}, u32[]{:S(2)}) collective-permute-start(bf16[24,7168]{1,0:T(8,128)(2,1)S(1)} %get-tuple-element.43), channel_id=1, source_target_pairs={{0,2},{2,0},{1,3},{3,1},{4,6},{6,4},{5,7},{7,5},{8,10},{10,8},{9,1... | collective-permute-start | bytes 1032200 | tf_op jit(solution)/shard_map/ppermute | solution.py:13
  143.2 17.7 %collective-permute-start.24 = (bf16[24,7168]{1,0:T(8,128)(2,1)S(1)}, bf16[24,7168]{1,0:T(8,128)(2,1)S(1)}, u32[]{:S(2)}, u32[]{:S(2)}) collective-permute-start(bf16[24,7168]{1,0:T(8,128)(2,1)S(1)} %get-tuple-element.42), channel_id=1, source_target_pairs={{0,2},{2,0},{1,3},{3,1},{4,6},{6,4},{5,7},{7,5},{8,10},{10,8},{9,1... | collective-permute-start | bytes 1032200 | tf_op jit(solution)/shard_map/ppermute | solution.py:13
  144.7 23.6 %collective-permute-start.25 = (bf16[24,7168]{1,0:T(8,128)(2,1)S(1)}, bf16[24,7168]{1,0:T(8,128)(2,1)S(1)}, u32[]{:S(2)}, u32[]{:S(2)}) collective-permute-start(bf16[24,7168]{1,0:T(8,128)(2,1)S(1)} %get-tuple-element.41), channel_id=1, source_target_pairs={{0,2},{2,0},{1,3},{3,1},{4,6},{6,4},{5,7},{7,5},{8,10},{10,8},{9,1... | collective-permute-start | bytes 1032200 | tf_op jit(solution)/shard_map/ppermute | solution.py:13
  146.8 28.4 %collective-permute-start.26 = (bf16[24,7168]{1,0:T(8,128)(2,1)S(1)}, bf16[24,7168]{1,0:T(8,128)(2,1)S(1)}, u32[]{:S(2)}, u32[]{:S(2)}) collective-permute-start(bf16[24,7168]{1,0:T(8,128)(2,1)S(1)} %get-tuple-element.40), channel_id=1, source_target_pairs={{0,2},{2,0},{1,3},{3,1},{4,6},{6,4},{5,7},{7,5},{8,10},{10,8},{9,1... | collective-permute-start | bytes 1032200 | tf_op jit(solution)/shard_map/ppermute | solution.py:13
  175.2 2.4 copy-start.4
  179.4 2.0 copy-start.2
  181.4 1.6 copy-start.8
  188.9 5.2 %collective-permute-start.31 = (bf16[2,4,24,7168]{3,2,1,0:T(8,128)(2,1)S(1)}, bf16[2,4,24,7168]{3,2,1,0:T(8,128)(2,1)S(1)}, u32[]{:S(2)}, u32[]{:S(2)}) collective-permute-start(bf16[2,4,24,7168]{3,2,1,0:T(8,128)(2,1)S(1)} %bitcast.225), channel_id=1, source_target_pairs={{0,1},{1,0},{2,3},{3,2},{4,5},{5,4},{6,7},{7,6},{8,9},{9,8},{10,11... | collective-permute-start | bytes 8257544 | tf_op jit(solution)/shard_map/ppermute | solution.py:13
  195.1 4.3 %copy-start.11 = (bf16[24,7168]{1,0:T(8,128)(2,1)S(1)}, bf16[24,7168]{1,0:T(8,128)(2,1)}, u32[]{:S(2)}) copy-start(bf16[24,7168]{1,0:T(8,128)(2,1)} %get-tuple-element.12) | copy-start | bytes 1032196
  195.1 11.1 %copy-start.10 = (bf16[24,7168]{1,0:T(8,128)(2,1)S(1)}, bf16[24,7168]{1,0:T(8,128)(2,1)}, u32[]{:S(2)}) copy-start(bf16[24,7168]{1,0:T(8,128)(2,1)} %get-tuple-element.13) | copy-start | bytes 1032196
  195.2 18.5 %copy-start.9 = (bf16[24,7168]{1,0:T(8,128)(2,1)S(1)}, bf16[24,7168]{1,0:T(8,128)(2,1)}, u32[]{:S(2)}) copy-start(bf16[24,7168]{1,0:T(8,128)(2,1)} %get-tuple-element.14) | copy-start | bytes 1032196
  195.3 11.0 %collective-permute-start.32 = (bf16[24,7168]{1,0:T(8,128)(2,1)S(1)}, bf16[24,7168]{1,0:T(8,128)(2,1)S(1)}, u32[]{:S(2)}, u32[]{:S(2)}) collective-permute-start(bf16[24,7168]{1,0:T(8,128)(2,1)S(1)} %get-tuple-element.36), channel_id=1, source_target_pairs={{0,2},{2,0},{1,3},{3,1},{4,6},{6,4},{5,7},{7,5},{8,10},{10,8},{9,1... | collective-permute-start | bytes 1032200 | tf_op jit(solution)/shard_map/ppermute | solution.py:13
  195.9 17.8 %collective-permute-start.33 = (bf16[24,7168]{1,0:T(8,128)(2,1)S(1)}, bf16[24,7168]{1,0:T(8,128)(2,1)S(1)}, u32[]{:S(2)}, u32[]{:S(2)}) collective-permute-start(bf16[24,7168]{1,0:T(8,128)(2,1)S(1)} %get-tuple-element.39), channel_id=1, source_target_pairs={{0,2},{2,0},{1,3},{3,1},{4,6},{6,4},{5,7},{7,5},{8,10},{10,8},{9,1... | collective-permute-start | bytes 1032200 | tf_op jit(solution)/shard_map/ppermute | solution.py:13
  197.4 23.6 %collective-permute-start.35 = (bf16[24,7168]{1,0:T(8,128)(2,1)S(1)}, bf16[24,7168]{1,0:T(8,128)(2,1)S(1)}, u32[]{:S(2)}, u32[]{:S(2)}) collective-permute-start(bf16[24,7168]{1,0:T(8,128)(2,1)S(1)} %get-tuple-element.38), channel_id=1, source_target_pairs={{0,2},{2,0},{1,3},{3,1},{4,6},{6,4},{5,7},{7,5},{8,10},{10,8},{9,1... | collective-permute-start | bytes 1032200 | tf_op jit(solution)/shard_map/ppermute | solution.py:13
  197.9 29.7 %collective-permute-start.37 = (bf16[24,7168]{1,0:T(8,128)(2,1)S(1)}, bf16[24,7168]{1,0:T(8,128)(2,1)S(1)}, u32[]{:S(2)}, u32[]{:S(2)}) collective-permute-start(bf16[24,7168]{1,0:T(8,128)(2,1)S(1)} %get-tuple-element.37), channel_id=1, source_target_pairs={{0,2},{2,0},{1,3},{3,1},{4,6},{6,4},{5,7},{7,5},{8,10},{10,8},{9,1... | collective-permute-start | bytes 1032200 | tf_op jit(solution)/shard_map/ppermute | solution.py:13
  199.4 30.5 %collective-permute-start.27 = (bf16[24,7168]{1,0:T(8,128)(2,1)S(1)}, bf16[24,7168]{1,0:T(8,128)(2,1)S(1)}, u32[]{:S(2)}, u32[]{:S(2)}) collective-permute-start(bf16[24,7168]{1,0:T(8,128)(2,1)S(1)} %copy-done.11), channel_id=1, source_target_pairs={{0,4},{4,0},{8,12},{12,8},{1,5},{5,1},{9,13},{13,9},{2,6},{6,2},{1... | collective-permute-start | bytes 1032200 | tf_op jit(solution)/shard_map/ppermute | solution.py:97
  206.3 25.2 %collective-permute-start.28 = (bf16[24,7168]{1,0:T(8,128)(2,1)S(1)}, bf16[24,7168]{1,0:T(8,128)(2,1)S(1)}, u32[]{:S(2)}, u32[]{:S(2)}) collective-permute-start(bf16[24,7168]{1,0:T(8,128)(2,1)S(1)} %copy-done.10), channel_id=1, source_target_pairs={{0,8},{4,12},{8,0},{12,4},{1,9},{5,13},{9,1},{13,5},{2,10},{6,14},... | collective-permute-start | bytes 1032200 | tf_op jit(solution)/shard_map/ppermute | solution.py:97
  213.6 39.0 %collective-permute-start.29 = (bf16[24,7168]{1,0:T(8,128)(2,1)S(1)}, bf16[24,7168]{1,0:T(8,128)(2,1)S(1)}, u32[]{:S(2)}, u32[]{:S(2)}) collective-permute-start(bf16[24,7168]{1,0:T(8,128)(2,1)S(1)} %copy-done.9), channel_id=1, source_target_pairs={{0,12},{4,8},{8,4},{12,0},{1,13},{5,9},{9,5},{13,1},{2,14},{6,10},... | collective-permute-start | bytes 1032200 | tf_op jit(solution)/shard_map/ppermute | solution.py:97
  227.9 24.9 %copy-start.5 = (bf16[1,32,7168]{2,1,0:T(8,128)(2,1)S(1)}, bf16[1,32,7168]{2,1,0:T(8,128)(2,1)}, u32[]{:S(2)}) copy-start(bf16[1,32,7168]{2,1,0:T(8,128)(2,1)} %param.10) | copy-start | bytes 1376260
  227.9 27.2 %collective-permute-start.34 = (bf16[24,7168]{1,0:T(8,128)(2,1)S(1)}, bf16[24,7168]{1,0:T(8,128)(2,1)S(1)}, u32[]{:S(2)}, u32[]{:S(2)}) collective-permute-start(bf16[24,7168]{1,0:T(8,128)(2,1)S(1)} %get-tuple-element.22), channel_id=1, source_target_pairs={{0,4},{4,0},{8,12},{12,8},{1,5},{5,1},{9,13},{13,9},{2,6},{6,2},{1... | collective-permute-start | bytes 1032200 | tf_op jit(solution)/shard_map/ppermute | solution.py:97
  229.4 29.7 %collective-permute-start.36 = (bf16[24,7168]{1,0:T(8,128)(2,1)S(1)}, bf16[24,7168]{1,0:T(8,128)(2,1)S(1)}, u32[]{:S(2)}, u32[]{:S(2)}) collective-permute-start(bf16[24,7168]{1,0:T(8,128)(2,1)S(1)} %get-tuple-element.21), channel_id=1, source_target_pairs={{0,8},{4,12},{8,0},{12,4},{1,9},{5,13},{9,1},{13,5},{2,10},{6,14},... | collective-permute-start | bytes 1032200 | tf_op jit(solution)/shard_map/ppermute | solution.py:97
  229.9 37.3 %collective-permute-start.38 = (bf16[24,7168]{1,0:T(8,128)(2,1)S(1)}, bf16[24,7168]{1,0:T(8,128)(2,1)S(1)}, u32[]{:S(2)}, u32[]{:S(2)}) collective-permute-start(bf16[24,7168]{1,0:T(8,128)(2,1)S(1)} %get-tuple-element.23), channel_id=1, source_target_pairs={{0,12},{4,8},{8,4},{12,0},{1,13},{5,9},{9,5},{13,1},{2,14},{6,10},... | collective-permute-start | bytes 1032200 | tf_op jit(solution)/shard_map/ppermute | solution.py:97
  253.5 16.2 %collective-permute-start.30 = (bf16[1,32,7168]{2,1,0:T(8,128)(2,1)S(1)}, bf16[1,32,7168]{2,1,0:T(8,128)(2,1)S(1)}, u32[]{:S(2)}, u32[]{:S(2)}) collective-permute-start(bf16[1,32,7168]{2,1,0:T(8,128)(2,1)S(1)} %fusion.3), channel_id=1, source_target_pairs={{0,16},{16,0},{1,17},{17,1},{2,18},{18,2},{3,19},{19,3},{4,20},{20... | collective-permute-start | bytes 1376264 | tf_op jit(solution)/shard_map/ppermute | solution.py:19
  268.1 12.4 %collective-permute-start.39 = (bf16[1,32,7168]{2,1,0:T(8,128)(2,1)S(1)}, bf16[1,32,7168]{2,1,0:T(8,128)(2,1)S(1)}, u32[]{:S(2)}, u32[]{:S(2)}) collective-permute-start(bf16[1,32,7168]{2,1,0:T(8,128)(2,1)S(1)} %fusion.2), channel_id=1, source_target_pairs={{0,16},{16,0},{1,17},{17,1},{2,18},{18,2},{3,19},{19,3},{4,20},{20... | collective-permute-start | bytes 1376264 | tf_op jit(solution)/shard_map/ppermute | solution.py:19

commit v12 on v5

--- a/solution.py
+++ b/solution.py
@@ -77,7 +77,7 @@
             received = lax.ppermute(slots[d], "z", [(i, i ^ d) for i in range(count)])
         across = jnp.stack([received, swap(received, "x")])
         pieces.append(jnp.stack([across, swap(across, "c")]))
-    return jnp.stack(pieces, axis=2)
+    return pieces
 
 
 def reduce_group(partial):
@@ -90,12 +90,15 @@
     return totals
 
 
-def returned(totals):
+def returned(totals, first=0):
     count = lax.axis_size("z")
-    out = [totals[0]]
-    for d in range(1, count):
-        out.append(lax.ppermute(totals[d], "z", [(i, i ^ d) for i in range(count)]))
-    return jnp.stack(out)
+    out = []
+    for d, total in enumerate(totals, start=first):
+        if d == 0:
+            out.append(total)
+        else:
+            out.append(lax.ppermute(total, "z", [(i, i ^ d) for i in range(count)]))
+    return out
 
 
 def body(
@@ -123,14 +126,21 @@
     f_slots = into_slots(f_select, fwd_input[0]).reshape(experts, capacity, width)
     b_joined = jnp.concatenate([bwd_input[0], bwd_grad[0]], axis=1)
     b_slots = into_slots(b_select, b_joined).reshape(experts, capacity, 2 * width)
-    f_rows = dispatch(f_slots)
-    b_rows = dispatch(b_slots)
+    f_rows = jnp.stack(dispatch(f_slots), axis=2)
+    b_pieces = dispatch(b_slots)
+    early = experts // 2
+    b_first = jnp.stack(b_pieces[:early], axis=2)
+    b_second = jnp.stack(b_pieces[early:], axis=2)
     f_partial = forward_rows(f_rows.reshape(-1, width), w_gate, w_up, w_down)
     f_totals = reduce_group(f_partial.reshape(2, 2, experts, capacity, width))
-    b_rows, f_totals = lax.optimization_barrier((b_rows, f_totals))
-    f_out = returned(f_totals)
-    b_partial = backward_rows(b_rows.reshape(-1, 2 * width), w_gate, w_up, w_down)
-    b_out = returned(reduce_group(b_partial.reshape(2, 2, experts, capacity, width)))
+    b_first, f_totals = lax.optimization_barrier((b_first, f_totals))
+    f_out = jnp.stack(returned(f_totals))
+    b_outs = []
+    for first, rows in ((0, b_first), (early, b_second)):
+        b_partial = backward_rows(rows.reshape(-1, 2 * width), w_gate, w_up, w_down)
+        b_partial = b_partial.reshape(2, 2, rows.shape[2], capacity, width)
+        b_outs += returned(reduce_group(b_partial), first)
+    b_out = jnp.stack(b_outs)
     high = lax.Precision.HIGHEST
     f_mixed = jnp.dot(
         f_weights, f_out.reshape(experts * capacity, width).astype(jnp.float32), precision=high

time: 275 us -> 325 us (1.18)
  matrix products: 18.9 us -> 45.3 us
  local copies, waits for them, and re-layouts: 9.07 us -> 19.8 us
  waiting for transfers between devices: 187 us -> 194 us
  other arithmetic: 19.5 us -> 26.1 us
    dot_general x1 -> x2, matrix products: 1.63 us -> 19.6 us  [backward_rows(): lax.dot_general(grad_gate, w_gate, (((1,), (1,)), ((), ())), preferred_el...]
    ppermute x6, waiting for transfers between devices: 33.3 us -> 45.8 us  [returned(): out.append(lax.ppermute(total, 'z', [(i, i ^ d) for i in range(count)]))]
    ppermute x26 -> x27, waiting for transfers between devices: 105 us -> 93.3 us  [swap(): return lax.ppermute(value, axis, [(0, 1), (1, 0)])]
    unnamed x28 -> x46, local copies, waits for them, and re-layouts: 4.49 us -> 14.6 us
    ppermute x2, waiting for transfers between devices: 10.9 us -> 19.3 us  [passed_along(): return lax.ppermute(value, axis, pairs)]
    dot_general x1 -> x2, matrix products: 3.79 us -> 10.6 us  [backward_rows(): lax.dot_general(grad_up, w_up, (((1,), (1,)), ((), ())), preferred_elemen...]
    another operation x15 -> x17, other arithmetic: 7.95 us -> 11.8 us  [the longest x10 5.26 us: dispatch(): return jnp.stack(pieces, axis=2)]
    ppermute x26 -> x27, starting transfers between devices: 21.4 us -> 21.4 us  [swap(): return lax.ppermute(value, axis, [(0, 1), (1, 0)])]
  transfers between devices with their start and end apart: 40 -> 41, of which waited for: 25 -> 25; matrix products, arithmetic and copies ran while one was open for 8% -> 16% of each run, Pallas kernels for 0% -> 0%
where the time goes in v12:
time: 325 us; the launch traced here: 324 us
  waiting for transfers between devices  194 us (60%)
  matrix products  45.3 us (14%)
  starting transfers between devices  37.3 us (11%)
  other arithmetic  26.1 us (8%)
  local copies, waits for them, and re-layouts  19.8 us (6%)
    ppermute x27, waiting for transfers between devices, swap(): return lax.ppermute(value, axis, [(0, 1), (1, 0)])  93.3 us
    ppermute x6, waiting for transfers between devices, returned(): out.append(lax.ppermute(total, 'z', [(i, i ^ d) for i in range(count)]))  45.8 us
    ppermute x6, waiting for transfers between devices, dispatch(): received = lax.ppermute(slots[d], 'z', [(i, i ^ d) for i in range(count)])  35.9 us
    ppermute x27, starting transfers between devices, swap(): return lax.ppermute(value, axis, [(0, 1), (1, 0)])  21.4 us
    dot_general x2, matrix products, backward_rows(): lax.dot_general(grad_gate, w_gate, (((1,), (1,)), ((), ())), preferred_el...  19.6 us
    ppermute x2, waiting for transfers between devices, passed_along(): return lax.ppermute(value, axis, pairs)  19.3 us
    unnamed x46, local copies, waits for them, and re-layouts  14.6 us
    dot_general x2, matrix products, backward_rows(): lax.dot_general(grad_up, w_up, (((1,), (1,)), ((), ())), preferred_elemen...  10.6 us
  transfers between devices with their start and end apart: 41, of which 25 were waited for; matrix products, arithmetic and copies ran while one was open for 16% of the time, Pallas kernels for 0%

profile of v12, /device:TPU:16, one launch (start us, length us, event | category | flops | bytes accessed | tf_op | source)
XLA Modules:
  0.0 324.0 jit_solution(11401692918507254779)
XLA Ops:
  2.2 1.4 convert_reduce_fusion
  3.6 1.6 convolution_convert_fusion.2
  5.3 1.6 collective-permute-start.7
  7.3 1.6 collective-permute-start.13
  8.9 1.5 collective-permute-start.5
  13.0 2.6 collective-permute-start.2
  15.6 2.2 collective-permute-done.5
  18.6 1.5 collective-permute-start
  22.9 11.2 %collective-permute-done = bf16[24,14336]{1,0:T(8,128)(2,1)S(1)} collective-permute-done((bf16[24,14336]{1,0:T(8,128)(2,1)S(1)}, bf16[24,14336]{1,0:T(8,128)(2,1)S(1)}, u32[]{:S(2)}, u32[]{:S(2)}) %collective-permute-start) | collective-permute-done | bytes 688160 | tf_op jit(solution)/shard_map/ppermute | solution.py:13
  34.1 1.5 collective-permute-start.8
  36.3 5.9 %collective-permute-done.8 = bf16[24,7168]{1,0:T(8,128)(2,1)S(1)} collective-permute-done((bf16[24,7168]{1,0:T(8,128)(2,1)}, bf16[24,7168]{1,0:T(8,128)(2,1)S(1)}, u32[]{:S(2)}, u32[]{:S(2)}) %collective-permute-start.8) | collective-permute-done | bytes 344096 | tf_op jit(solution)/shard_map/ppermute | solution.py:13
  42.2 1.5 collective-permute-start.11
  44.9 6.3 %collective-permute-done.11 = bf16[24,7168]{1,0:T(8,128)(2,1)S(1)} collective-permute-done((bf16[24,7168]{1,0:T(8,128)(2,1)}, bf16[24,7168]{1,0:T(8,128)(2,1)S(1)}, u32[]{:S(2)}, u32[]{:S(2)}) %collective-permute-start.11) | collective-permute-done | bytes 344096 | tf_op jit(solution)/shard_map/ppermute | solution.py:13
  51.1 1.5 collective-permute-start.14
  53.7 4.7 %collective-permute-done.14 = bf16[24,7168]{1,0:T(8,128)(2,1)S(1)} collective-permute-done((bf16[24,7168]{1,0:T(8,128)(2,1)S(1)}, bf16[24,7168]{1,0:T(8,128)(2,1)S(1)}, u32[]{:S(2)}, u32[]{:S(2)}) %collective-permute-start.14) | collective-permute-done | bytes 344096 | tf_op jit(solution)/shard_map/ppermute | solution.py:13
  61.2 21.0 %collective-permute-done.29 = bf16[24,14336]{1,0:T(8,128)(2,1)} collective-permute-done((bf16[24,14336]{1,0:T(8,128)(2,1)S(1)}, bf16[24,14336]{1,0:T(8,128)(2,1)}, u32[]{:S(2)}, u32[]{:S(2)}) %collective-permute-start.29) | collective-permute-done | bytes 688160 | tf_op jit(solution)/shard_map/ppermute | solution.py:77
  82.2 1.5 collective-permute-start.3
  83.7 14.0 %collective-permute-done.32 = bf16[24,14336]{1,0:T(8,128)(2,1)} collective-permute-done((bf16[24,14336]{1,0:T(8,128)(2,1)S(1)}, bf16[24,14336]{1,0:T(8,128)(2,1)}, u32[]{:S(2)}, u32[]{:S(2)}) %collective-permute-start.32) | collective-permute-done | bytes 688160 | tf_op jit(solution)/shard_map/ppermute | solution.py:77
  97.7 1.5 collective-permute-start.30
  101.4 1.6 copy-done.1
  103.0 1.6 fusion.27
  105.0 1.6 fusion.38
  107.1 1.6 convolution_convert_fusion.1
  108.7 1.9 fusion.140
  110.6 3.0 fusion.138
  114.2 2.2 collective-permute-done.30
  116.4 1.5 fusion.137
  118.0 10.7 %collective-permute-done.33 = bf16[24,14336]{1,0:T(8,128)(2,1)S(1)} collective-permute-done((bf16[24,14336]{1,0:T(8,128)(2,1)}, bf16[24,14336]{1,0:T(8,128)(2,1)S(1)}, u32[]{:S(2)}, u32[]{:S(2)}) %collective-permute-start.33) | collective-permute-done | bytes 688160 | tf_op jit(solution)/shard_map/ppermute | solution.py:13
  129.5 1.5 fusion.136
  131.1 1.8 maximum_bitcast_fusion
  136.5 1.9 copy-done.3
  139.6 2.0 fusion.6
  141.6 9.8 %fusion.19 = f32[192,7168]{1,0:T(8,128)} fusion(bf16[1,7168,256]{2,1,0:T(8,128)(2,1)} %param.17, f32[192,256]{1,0:T(8,128)} %fusion.6, bf16[1,7168,256]{2,1,0:T(8,128)(2,1)} %param.18, bf16[192,14336]{1,0:T(8,128)(2,1)} %bitcast.228, f32[192,256]{1,0:T(8,128)S(1)} %fusion.21), kind=kOutput, calls=%fused_computation.30 | convolution fusion | flops 1409777664 | bytes 15990784 | tf_op jit(solution)/shard_map/dot_general | solution.py:61
  151.4 5.3 %fusion.1 = bf16[192,7168]{1,0:T(8,128)(2,1)S(1)} fusion(f32[192,7168]{1,0:T(8,128)} %fusion.19, bf16[1,7168,256]{2,1,0:T(8,128)(2,1)} %param.18, f32[192,256]{1,0:T(8,128)} %fusion.6, f32[192,256]{1,0:T(8,128)S(1)} %fusion.21), kind=kOutput, calls=%fused_computation.5 | convolution fusion | flops 707690496 | bytes 12320768 | tf_op jit(solution)/shard_map/dot_general | solution.py:64
  158.1 1.7 maximum_bitcast_fusion.1
  160.8 2.9 fusion.135
  163.8 1.6 collective-permute-start.17
  165.8 1.5 collective-permute-start.19
  167.9 1.6 fusion.130
  169.5 5.3 %collective-permute-done.17 = bf16[24,7168]{1,0:T(8,128)(2,1)S(1)} collective-permute-done((bf16[24,7168]{1,0:T(8,128)(2,1)S(1)}, bf16[24,7168]{1,0:T(8,128)(2,1)S(1)}, u32[]{:S(2)}, u32[]{:S(2)}) %collective-permute-start.17) | collective-permute-done | bytes 344096 | tf_op jit(solution)/shard_map/ppermute | solution.py:13
  174.7 7.4 %collective-permute-done.18 = bf16[24,7168]{1,0:T(8,128)(2,1)S(1)} collective-permute-done((bf16[24,7168]{1,0:T(8,128)(2,1)S(1)}, bf16[24,7168]{1,0:T(8,128)(2,1)S(1)}, u32[]{:S(2)}, u32[]{:S(2)}) %collective-permute-start.18) | collective-permute-done | bytes 344096 | tf_op jit(solution)/shard_map/ppermute | solution.py:13
  182.1 7.4 %collective-permute-done.19 = bf16[24,7168]{1,0:T(8,128)(2,1)S(1)} collective-permute-done((bf16[24,7168]{1,0:T(8,128)(2,1)S(1)}, bf16[24,7168]{1,0:T(8,128)(2,1)S(1)}, u32[]{:S(2)}, u32[]{:S(2)}) %collective-permute-start.19) | collective-permute-done | bytes 344096 | tf_op jit(solution)/shard_map/ppermute | solution.py:13
  189.5 6.6 %collective-permute-done.20 = bf16[24,7168]{1,0:T(8,128)(2,1)S(1)} collective-permute-done((bf16[24,7168]{1,0:T(8,128)(2,1)S(1)}, bf16[24,7168]{1,0:T(8,128)(2,1)S(1)}, u32[]{:S(2)}, u32[]{:S(2)}) %collective-permute-start.20) | collective-permute-done | bytes 344096 | tf_op jit(solution)/shard_map/ppermute | solution.py:13
  197.7 2.8 copy-done.2
  200.6 1.5 fusion.25
  202.7 2.0 fusion.8
  204.7 9.8 %fusion.23 = f32[192,7168]{1,0:T(8,128)} fusion(bf16[1,7168,256]{2,1,0:T(8,128)(2,1)} %param.17, f32[192,256]{1,0:T(8,128)} %fusion.8, bf16[1,7168,256]{2,1,0:T(8,128)(2,1)} %param.18, bf16[192,14336]{1,0:T(8,128)(2,1)} %bitcast.231, f32[192,256]{1,0:T(8,128)} %fusion.25), kind=kOutput, calls=%fused_computation.34 | convolution fusion | flops 1409777664 | bytes 15990784 | tf_op jit(solution)/shard_map/dot_general | solution.py:61
  214.5 5.3 %fusion = bf16[192,7168]{1,0:T(8,128)(2,1)S(1)} fusion(f32[192,7168]{1,0:T(8,128)} %fusion.23, bf16[1,7168,256]{2,1,0:T(8,128)(2,1)} %param.18, f32[192,256]{1,0:T(8,128)} %fusion.8, f32[192,256]{1,0:T(8,128)} %fusion.25), kind=kOutput, calls=%fused_computation.4 | convolution fusion | flops 707690496 | bytes 12320768 | tf_op jit(solution)/shard_map/dot_general | solution.py:64
  221.2 1.6 collective-permute-start.36
  223.8 1.6 collective-permute-start.26
  225.9 6.4 %collective-permute-done.36 = bf16[24,7168]{1,0:T(8,128)(2,1)S(1)} collective-permute-done((bf16[24,7168]{1,0:T(8,128)(2,1)S(1)}, bf16[24,7168]{1,0:T(8,128)(2,1)S(1)}, u32[]{:S(2)}, u32[]{:S(2)}) %collective-permute-start.36) | collective-permute-done | bytes 344096 | tf_op jit(solution)/shard_map/ppermute | solution.py:13
  232.2 7.4 %collective-permute-done.38 = bf16[24,7168]{1,0:T(8,128)(2,1)S(1)} collective-permute-done((bf16[24,7168]{1,0:T(8,128)(2,1)S(1)}, bf16[24,7168]{1,0:T(8,128)(2,1)S(1)}, u32[]{:S(2)}, u32[]{:S(2)}) %collective-permute-start.38) | collective-permute-done | bytes 344096 | tf_op jit(solution)/shard_map/ppermute | solution.py:13
  239.8 1.4 collective-permute-start.37
  241.2 1.6 collective-permute-start.39
  242.8 1.5 collective-permute-start.21
  244.2 2.8 collective-permute-done.26
  247.0 1.3 collective-permute-start.22
  248.3 4.4 %collective-permute-done.27 = bf16[24,7168]{1,0:T(8,128)(2,1)S(1)} collective-permute-done((bf16[24,7168]{1,0:T(8,128)(2,1)S(1)}, bf16[24,7168]{1,0:T(8,128)(2,1)S(1)}, u32[]{:S(2)}, u32[]{:S(2)}) %collective-permute-start.27) | collective-permute-done | bytes 344096 | tf_op jit(solution)/shard_map/ppermute | solution.py:13
  253.4 12.1 %collective-permute-done.21 = bf16[24,7168]{1,0:T(8,128)(2,1)S(1)} collective-permute-done((bf16[24,7168]{1,0:T(8,128)(2,1)S(1)}, bf16[24,7168]{1,0:T(8,128)(2,1)S(1)}, u32[]{:S(2)}, u32[]{:S(2)}) %collective-permute-start.21) | collective-permute-done | bytes 344096 | tf_op jit(solution)/shard_map/ppermute | solution.py:100
  265.5 24.4 %collective-permute-done.22 = bf16[24,7168]{1,0:T(8,128)(2,1)S(1)} collective-permute-done((bf16[24,7168]{1,0:T(8,128)(2,1)S(1)}, bf16[24,7168]{1,0:T(8,128)(2,1)S(1)}, u32[]{:S(2)}, u32[]{:S(2)}) %collective-permute-start.22) | collective-permute-done | bytes 344096 | tf_op jit(solution)/shard_map/ppermute | solution.py:100
  289.9 9.3 %collective-permute-done.23 = bf16[24,7168]{1,0:T(8,128)(2,1)S(1)} collective-permute-done((bf16[24,7168]{1,0:T(8,128)(2,1)S(1)}, bf16[24,7168]{1,0:T(8,128)(2,1)S(1)}, u32[]{:S(2)}, u32[]{:S(2)}) %collective-permute-start.23) | collective-permute-done | bytes 344096 | tf_op jit(solution)/shard_map/ppermute | solution.py:100
  300.1 1.6 collective-permute-start.24
  303.2 10.4 %collective-permute-done.24 = bf16[1,32,7168]{2,1,0:T(8,128)(2,1)S(1)} collective-permute-done((bf16[1,32,7168]{2,1,0:T(8,128)(2,1)S(1)}, bf16[1,32,7168]{2,1,0:T(8,128)(2,1)S(1)}, u32[]{:S(2)}, u32[]{:S(2)}) %collective-permute-start.24) | collective-permute-done | bytes 458784 | tf_op jit(solution)/shard_map/ppermute | solution.py:19
  313.6 8.9 %collective-permute-done.40 = bf16[1,32,7168]{2,1,0:T(8,128)(2,1)S(1)} collective-permute-done((bf16[1,32,7168]{2,1,0:T(8,128)(2,1)S(1)}, bf16[1,32,7168]{2,1,0:T(8,128)(2,1)S(1)}, u32[]{:S(2)}, u32[]{:S(2)}) %collective-permute-start.40) | collective-permute-done | bytes 458784 | tf_op jit(solution)/shard_map/ppermute | solution.py:19
  (136 shorter events, 36.4 us)
Async XLA Ops:
  0.6 10.5 %copy-start.21 = (f32[1,32,2]{1,2,0:T(2,128)S(1)}, f32[1,32,2]{1,2,0:T(2,128)}, u32[]{:S(2)}) copy-start(f32[1,32,2]{1,2,0:T(2,128)} %param.16) | copy-start | bytes 772
  0.6 11.2 %copy-start.14 = (bf16[1,32,7168]{2,1,0:T(8,128)(2,1)S(1)}, bf16[1,32,7168]{2,1,0:T(8,128)(2,1)}, u32[]{:S(2)}) copy-start(bf16[1,32,7168]{2,1,0:T(8,128)(2,1)} %param.13) | copy-start | bytes 1376260
  0.7 11.1 %copy-start.12 = (bf16[1,32,7168]{2,1,0:T(8,128)(2,1)S(1)}, bf16[1,32,7168]{2,1,0:T(8,128)(2,1)}, u32[]{:S(2)}) copy-start(bf16[1,32,7168]{2,1,0:T(8,128)(2,1)} %param.14) | copy-start | bytes 1376260
  5.3 16.7 %collective-permute-start.7 = (bf16[24,7168]{1,0:T(8,128)(2,1)S(1)}, bf16[24,7168]{1,0:T(8,128)(2,1)}, u32[]{:S(2)}, u32[]{:S(2)}) collective-permute-start(bf16[24,7168]{1,0:T(8,128)(2,1)S(1)} %get-tuple-element.56), channel_id=1, source_target_pairs={{0,4},{4,0},{8,12},{12,8},{1,5},{5,1},{9,13},{13,9},{2,6},{6,2},{1... | collective-permute-start | bytes 1032200 | tf_op jit(solution)/shard_map/ppermute | solution.py:77
  7.0 28.8 %collective-permute-start.10 = (bf16[24,7168]{1,0:T(8,128)(2,1)S(1)}, bf16[24,7168]{1,0:T(8,128)(2,1)}, u32[]{:S(2)}, u32[]{:S(2)}) collective-permute-start(bf16[24,7168]{1,0:T(8,128)(2,1)S(1)} %get-tuple-element.55), channel_id=1, source_target_pairs={{0,8},{4,12},{8,0},{12,4},{1,9},{5,13},{9,1},{13,5},{2,10},{6,14},... | collective-permute-start | bytes 1032200 | tf_op jit(solution)/shard_map/ppermute | solution.py:77
  7.3 37.5 %collective-permute-start.13 = (bf16[24,7168]{1,0:T(8,128)(2,1)S(1)}, bf16[24,7168]{1,0:T(8,128)(2,1)S(1)}, u32[]{:S(2)}, u32[]{:S(2)}) collective-permute-start(bf16[24,7168]{1,0:T(8,128)(2,1)S(1)} %get-tuple-element.54), channel_id=1, source_target_pairs={{0,12},{4,8},{8,4},{12,0},{1,13},{5,9},{9,5},{13,1},{2,14},{6,10},... | collective-permute-start | bytes 1032200 | tf_op jit(solution)/shard_map/ppermute | solution.py:77
  8.9 9.0 %collective-permute-start.5 = (bf16[24,7168]{1,0:T(8,128)(2,1)S(1)}, bf16[24,7168]{1,0:T(8,128)(2,1)S(1)}, u32[]{:S(2)}, u32[]{:S(2)}) collective-permute-start(bf16[24,7168]{1,0:T(8,128)(2,1)S(1)} %get-tuple-element.57), channel_id=1, source_target_pairs={{0,2},{2,0},{1,3},{3,1},{4,6},{6,4},{5,7},{7,5},{8,10},{10,8},{9,1... | collective-permute-start | bytes 1032200 | tf_op jit(solution)/shard_map/ppermute | solution.py:13
  13.0 47.8 %collective-permute-start.2 = (bf16[24,14336]{1,0:T(8,128)(2,1)S(1)}, bf16[24,14336]{1,0:T(8,128)(2,1)}, u32[]{:S(2)}, u32[]{:S(2)}) collective-permute-start(bf16[24,14336]{1,0:T(8,128)(2,1)S(1)} %get-tuple-element.39), channel_id=1, source_target_pairs={{0,4},{4,0},{8,12},{12,8},{1,5},{5,1},{9,13},{13,9},{2,6},{6,2},{1... | collective-permute-start | bytes 2064392 | tf_op jit(solution)/shard_map/ppermute | solution.py:77
  17.8 0.7 copy-start.15
  18.6 15.5 %collective-permute-start = (bf16[24,14336]{1,0:T(8,128)(2,1)S(1)}, bf16[24,14336]{1,0:T(8,128)(2,1)S(1)}, u32[]{:S(2)}, u32[]{:S(2)}) collective-permute-start(bf16[24,14336]{1,0:T(8,128)(2,1)S(1)} %get-tuple-element.40), channel_id=1, source_target_pairs={{0,2},{2,0},{1,3},{3,1},{4,6},{6,4},{5,7},{7,5},{8,10},{10,8},{9,1... | collective-permute-start | bytes 2064392 | tf_op jit(solution)/shard_map/ppermute | solution.py:13
  22.0 60.2 %collective-permute-start.29 = (bf16[24,14336]{1,0:T(8,128)(2,1)S(1)}, bf16[24,14336]{1,0:T(8,128)(2,1)}, u32[]{:S(2)}, u32[]{:S(2)}) collective-permute-start(bf16[24,14336]{1,0:T(8,128)(2,1)S(1)} %get-tuple-element.36), channel_id=1, source_target_pairs={{0,8},{4,12},{8,0},{12,4},{1,9},{5,13},{9,1},{13,5},{2,10},{6,14},... | collective-permute-start | bytes 2064392 | tf_op jit(solution)/shard_map/ppermute | solution.py:77
  34.1 8.1 %collective-permute-start.8 = (bf16[24,7168]{1,0:T(8,128)(2,1)}, bf16[24,7168]{1,0:T(8,128)(2,1)S(1)}, u32[]{:S(2)}, u32[]{:S(2)}) collective-permute-start(bf16[24,7168]{1,0:T(8,128)(2,1)} %collective-permute-done.7), channel_id=1, source_target_pairs={{0,2},{2,0},{1,3},{3,1},{4,6},{6,4},{5,7},{7,5},{8,10},{10,8},{9,1... | collective-permute-start | bytes 1032200 | tf_op jit(solution)/shard_map/ppermute | solution.py:13
  35.8 61.9 %collective-permute-start.32 = (bf16[24,14336]{1,0:T(8,128)(2,1)S(1)}, bf16[24,14336]{1,0:T(8,128)(2,1)}, u32[]{:S(2)}, u32[]{:S(2)}) collective-permute-start(bf16[24,14336]{1,0:T(8,128)(2,1)S(1)} %get-tuple-element.38), channel_id=1, source_target_pairs={{0,12},{4,8},{8,4},{12,0},{1,13},{5,9},{9,5},{13,1},{2,14},{6,10},... | collective-permute-start | bytes 2064392 | tf_op jit(solution)/shard_map/ppermute | solution.py:77
  42.2 8.9 %collective-permute-start.11 = (bf16[24,7168]{1,0:T(8,128)(2,1)}, bf16[24,7168]{1,0:T(8,128)(2,1)S(1)}, u32[]{:S(2)}, u32[]{:S(2)}) collective-permute-start(bf16[24,7168]{1,0:T(8,128)(2,1)} %collective-permute-done.10), channel_id=1, source_target_pairs={{0,2},{2,0},{1,3},{3,1},{4,6},{6,4},{5,7},{7,5},{8,10},{10,8},{9,1... | collective-permute-start | bytes 1032200 | tf_op jit(solution)/shard_map/ppermute | solution.py:13
  44.8 13.7 %collective-permute-start.6 = (bf16[2,24,7168]{2,1,0:T(8,128)(2,1)S(1)}, bf16[2,24,7168]{2,1,0:T(8,128)(2,1)S(1)}, u32[]{:S(2)}, u32[]{:S(2)}) collective-permute-start(bf16[2,24,7168]{2,1,0:T(8,128)(2,1)S(1)} %get-tuple-element.63), channel_id=1, source_target_pairs={{0,1},{1,0},{2,3},{3,2},{4,5},{5,4},{6,7},{7,6},{8,9},{9,8},{10,11... | collective-permute-start | bytes 2064392 | tf_op jit(solution)/shard_map/ppermute | solution.py:13
  51.1 7.2 %collective-permute-start.14 = (bf16[24,7168]{1,0:T(8,128)(2,1)S(1)}, bf16[24,7168]{1,0:T(8,128)(2,1)S(1)}, u32[]{:S(2)}, u32[]{:S(2)}) collective-permute-start(bf16[24,7168]{1,0:T(8,128)(2,1)S(1)} %collective-permute-done.13), channel_id=1, source_target_pairs={{0,2},{2,0},{1,3},{3,1},{4,6},{6,4},{5,7},{7,5},{8,10},{10,8},{9,1... | collective-permute-start | bytes 1032200 | tf_op jit(solution)/shard_map/ppermute | solution.py:13
  58.4 2.1 collective-permute-start.9
  58.5 40.7 %collective-permute-start.12 = (bf16[2,24,7168]{2,1,0:T(8,128)(2,1)S(1)}, bf16[2,24,7168]{2,1,0:T(8,128)(2,1)S(1)}, u32[]{:S(2)}, u32[]{:S(2)}) collective-permute-start(bf16[2,24,7168]{2,1,0:T(8,128)(2,1)S(1)} %get-tuple-element.67), channel_id=1, source_target_pairs={{0,1},{1,0},{2,3},{3,2},{4,5},{5,4},{6,7},{7,6},{8,9},{9,8},{10,11... | collective-permute-start | bytes 2064392 | tf_op jit(solution)/shard_map/ppermute | solution.py:13
  60.5 39.3 %collective-permute-start.15 = (bf16[2,24,7168]{2,1,0:T(8,128)(2,1)S(1)}, bf16[2,24,7168]{2,1,0:T(8,128)(2,1)S(1)}, u32[]{:S(2)}, u32[]{:S(2)}) collective-permute-start(bf16[2,24,7168]{2,1,0:T(8,128)(2,1)S(1)} %get-tuple-element.69), channel_id=1, source_target_pairs={{0,1},{1,0},{2,3},{3,2},{4,5},{5,4},{6,7},{7,6},{8,9},{9,8},{10,11... | collective-permute-start | bytes 2064392 | tf_op jit(solution)/shard_map/ppermute | solution.py:13
  60.8 70.3 %collective-permute-start.1 = (bf16[2,24,14336]{2,1,0:T(8,128)(2,1)S(1)}, bf16[2,24,14336]{2,1,0:T(8,128)(2,1)S(1)}, u32[]{:S(2)}, u32[]{:S(2)}) collective-permute-start(bf16[2,24,14336]{2,1,0:T(8,128)(2,1)S(1)} %get-tuple-element.59), channel_id=1, source_target_pairs={{0,1},{1,0},{2,3},{3,2},{4,5},{5,4},{6,7},{7,6},{8,9},{9,8},{10,11... | collective-permute-start | bytes 4128776 | tf_op jit(solution)/shard_map/ppermute | solution.py:13
  82.2 28.4 %collective-permute-start.3 = (bf16[24,14336]{1,0:T(8,128)(2,1)}, bf16[24,14336]{1,0:T(8,128)(2,1)}, u32[]{:S(2)}, u32[]{:S(2)}) collective-permute-start(bf16[24,14336]{1,0:T(8,128)(2,1)} %collective-permute-done.2), channel_id=1, source_target_pairs={{0,2},{2,0},{1,3},{3,1},{4,6},{6,4},{5,7},{7,5},{8,10},{10,8},{9,1... | collective-permute-start | bytes 2064392 | tf_op jit(solution)/shard_map/ppermute | solution.py:13
  97.7 18.7 %collective-permute-start.30 = (bf16[24,14336]{1,0:T(8,128)(2,1)}, bf16[24,14336]{1,0:T(8,128)(2,1)}, u32[]{:S(2)}, u32[]{:S(2)}) collective-permute-start(bf16[24,14336]{1,0:T(8,128)(2,1)} %collective-permute-done.29), channel_id=1, source_target_pairs={{0,2},{2,0},{1,3},{3,1},{4,6},{6,4},{5,7},{7,5},{8,10},{10,8},{9,1... | collective-permute-start | bytes 2064392 | tf_op jit(solution)/shard_map/ppermute | solution.py:13
  99.2 29.5 %collective-permute-start.33 = (bf16[24,14336]{1,0:T(8,128)(2,1)}, bf16[24,14336]{1,0:T(8,128)(2,1)S(1)}, u32[]{:S(2)}, u32[]{:S(2)}) collective-permute-start(bf16[24,14336]{1,0:T(8,128)(2,1)} %collective-permute-done.32), channel_id=1, source_target_pairs={{0,2},{2,0},{1,3},{3,1},{4,6},{6,4},{5,7},{7,5},{8,10},{10,8},{9,1... | collective-permute-start | bytes 2064392 | tf_op jit(solution)/shard_map/ppermute | solution.py:13
  100.9 2.0 copy-start.1
  103.0 2.0 copy-start
  105.0 2.0 copy-start.7
  110.6 50.2 %collective-permute-start.16 = (bf16[2,4,24,7168]{3,2,1,0:T(8,128)(2,1)}, bf16[2,4,24,7168]{3,2,1,0:T(8,128)(2,1)}, u32[]{:S(2)}, u32[]{:S(2)}) collective-permute-start(bf16[2,4,24,7168]{3,2,1,0:T(8,128)(2,1)} %bitcast.41), channel_id=1, source_target_pairs={{0,1},{1,0},{2,3},{3,2},{4,5},{5,4},{6,7},{7,6},{8,9},{9,8},{10,11... | collective-permute-start | bytes 8257544 | tf_op jit(solution)/shard_map/ppermute | solution.py:13
  113.7 43.5 %collective-permute-start.4 = (bf16[2,24,14336]{2,1,0:T(8,128)(2,1)}, bf16[2,24,14336]{2,1,0:T(8,128)(2,1)}, u32[]{:S(2)}, u32[]{:S(2)}) collective-permute-start(bf16[2,24,14336]{2,1,0:T(8,128)(2,1)} %get-tuple-element.61), channel_id=1, source_target_pairs={{0,1},{1,0},{2,3},{3,2},{4,5},{5,4},{6,7},{7,6},{8,9},{9,8},{10,11... | collective-permute-start | bytes 4128776 | tf_op jit(solution)/shard_map/ppermute | solution.py:13
  117.9 15.0 %collective-permute-start.31 = (bf16[2,24,14336]{2,1,0:T(8,128)(2,1)S(1)}, bf16[2,24,14336]{2,1,0:T(8,128)(2,1)S(1)}, u32[]{:S(2)}, u32[]{:S(2)}) collective-permute-start(bf16[2,24,14336]{2,1,0:T(8,128)(2,1)S(1)} %get-tuple-element.50), channel_id=1, source_target_pairs={{0,1},{1,0},{2,3},{3,2},{4,5},{5,4},{6,7},{7,6},{8,9},{9,8},{10,11... | collective-permute-start | bytes 4128776 | tf_op jit(solution)/shard_map/ppermute | solution.py:13
  128.7 0.9 copy-start.13
  131.0 3.2 collective-permute-start.34
  135.5 2.8 copy-start.3
  135.6 4.0 %copy-start.8 = (bf16[1,256,7168]{2,1,0:T(8,128)(2,1)S(1)}, bf16[1,256,7168]{2,1,0:T(8,128)(2,1)}, u32[]{:S(2)}) copy-start(bf16[1,256,7168]{2,1,0:T(8,128)(2,1)} %param.19) | copy-start | bytes 11010052
  156.7 1.3 copy-start.6
  156.9 10.9 %collective-permute-start.35 = (bf16[2,2,24,7168]{3,2,1,0:T(8,128)(2,1)S(1)}, bf16[2,2,24,7168]{3,2,1,0:T(8,128)(2,1)S(1)}, u32[]{:S(2)}, u32[]{:S(2)}) collective-permute-start(bf16[2,2,24,7168]{3,2,1,0:T(8,128)(2,1)S(1)} %bitcast.241), channel_id=1, source_target_pairs={{0,1},{1,0},{2,3},{3,2},{4,5},{5,4},{6,7},{7,6},{8,9},{9,8},{10,11... | collective-permute-start | bytes 4128776 | tf_op jit(solution)/shard_map/ppermute | solution.py:13
  158.1 2.2 copy-start.5
  163.8 11.0 %collective-permute-start.17 = (bf16[24,7168]{1,0:T(8,128)(2,1)S(1)}, bf16[24,7168]{1,0:T(8,128)(2,1)S(1)}, u32[]{:S(2)}, u32[]{:S(2)}) collective-permute-start(bf16[24,7168]{1,0:T(8,128)(2,1)S(1)} %get-tuple-element.44), channel_id=1, source_target_pairs={{0,2},{2,0},{1,3},{3,1},{4,6},{6,4},{5,7},{7,5},{8,10},{10,8},{9,1... | collective-permute-start | bytes 1032200 | tf_op jit(solution)/shard_map/ppermute | solution.py:13
  165.3 16.8 %collective-permute-start.18 = (bf16[24,7168]{1,0:T(8,128)(2,1)S(1)}, bf16[24,7168]{1,0:T(8,128)(2,1)S(1)}, u32[]{:S(2)}, u32[]{:S(2)}) collective-permute-start(bf16[24,7168]{1,0:T(8,128)(2,1)S(1)} %get-tuple-element.43), channel_id=1, source_target_pairs={{0,2},{2,0},{1,3},{3,1},{4,6},{6,4},{5,7},{7,5},{8,10},{10,8},{9,1... | collective-permute-start | bytes 1032200 | tf_op jit(solution)/shard_map/ppermute | solution.py:13
  165.8 23.6 %collective-permute-start.19 = (bf16[24,7168]{1,0:T(8,128)(2,1)S(1)}, bf16[24,7168]{1,0:T(8,128)(2,1)S(1)}, u32[]{:S(2)}, u32[]{:S(2)}) collective-permute-start(bf16[24,7168]{1,0:T(8,128)(2,1)S(1)} %get-tuple-element.42), channel_id=1, source_target_pairs={{0,2},{2,0},{1,3},{3,1},{4,6},{6,4},{5,7},{7,5},{8,10},{10,8},{9,1... | collective-permute-start | bytes 1032200 | tf_op jit(solution)/shard_map/ppermute | solution.py:13
  167.4 28.7 %collective-permute-start.20 = (bf16[24,7168]{1,0:T(8,128)(2,1)S(1)}, bf16[24,7168]{1,0:T(8,128)(2,1)S(1)}, u32[]{:S(2)}, u32[]{:S(2)}) collective-permute-start(bf16[24,7168]{1,0:T(8,128)(2,1)S(1)} %get-tuple-element.41), channel_id=1, source_target_pairs={{0,2},{2,0},{1,3},{3,1},{4,6},{6,4},{5,7},{7,5},{8,10},{10,8},{9,1... | collective-permute-start | bytes 1032200 | tf_op jit(solution)/shard_map/ppermute | solution.py:13
  197.2 3.4 %copy-start.2 = (bf16[1,7168,256]{2,1,0:T(8,128)(2,1)S(1)}, bf16[1,7168,256]{2,1,0:T(8,128)(2,1)}, u32[]{:S(2)}) copy-start(bf16[1,7168,256]{2,1,0:T(8,128)(2,1)} %param.17) | copy-start | bytes 11010052
  197.7 4.4 %copy-start.4 = (bf16[2,2,2,24,14336]{4,3,2,1,0:T(8,128)(2,1)}, bf16[2,2,2,24,14336]{4,3,2,1,0:T(8,128)(2,1)S(1)}, u32[]{:S(2)}) copy-start(bf16[2,2,2,24,14336]{4,3,2,1,0:T(8,128)(2,1)S(1)} %copy.36) | copy-start | bytes 16515076
  200.5 2.1 copy-start.9
  219.8 1.3 copy-start.10
  220.0 3.3 %collective-permute-start.25 = (bf16[2,2,24,7168]{3,2,1,0:T(8,128)(2,1)S(1)}, bf16[2,2,24,7168]{3,2,1,0:T(8,128)(2,1)S(1)}, u32[]{:S(2)}, u32[]{:S(2)}) collective-permute-start(bf16[2,2,24,7168]{3,2,1,0:T(8,128)(2,1)S(1)} %bitcast.244), channel_id=1, source_target_pairs={{0,1},{1,0},{2,3},{3,2},{4,5},{5,4},{6,7},{7,6},{8,9},{9,8},{10,11... | collective-permute-start | bytes 4128776 | tf_op jit(solution)/shard_map/ppermute | solution.py:13
  221.2 11.1 %collective-permute-start.36 = (bf16[24,7168]{1,0:T(8,128)(2,1)S(1)}, bf16[24,7168]{1,0:T(8,128)(2,1)S(1)}, u32[]{:S(2)}, u32[]{:S(2)}) collective-permute-start(bf16[24,7168]{1,0:T(8,128)(2,1)S(1)} %get-tuple-element.47), channel_id=1, source_target_pairs={{0,2},{2,0},{1,3},{3,1},{4,6},{6,4},{5,7},{7,5},{8,10},{10,8},{9,1... | collective-permute-start | bytes 1032200 | tf_op jit(solution)/shard_map/ppermute | solution.py:13
  222.7 16.9 %collective-permute-start.38 = (bf16[24,7168]{1,0:T(8,128)(2,1)S(1)}, bf16[24,7168]{1,0:T(8,128)(2,1)S(1)}, u32[]{:S(2)}, u32[]{:S(2)}) collective-permute-start(bf16[24,7168]{1,0:T(8,128)(2,1)S(1)} %get-tuple-element.48), channel_id=1, source_target_pairs={{0,2},{2,0},{1,3},{3,1},{4,6},{6,4},{5,7},{7,5},{8,10},{10,8},{9,1... | collective-permute-start | bytes 1032200 | tf_op jit(solution)/shard_map/ppermute | solution.py:13
  223.7 19.1 %copy-start.18 = (bf16[24,7168]{1,0:T(8,128)(2,1)S(1)}, bf16[24,7168]{1,0:T(8,128)(2,1)}, u32[]{:S(2)}) copy-start(bf16[24,7168]{1,0:T(8,128)(2,1)} %get-tuple-element.8) | copy-start | bytes 1032196
  223.7 23.3 %copy-start.17 = (bf16[24,7168]{1,0:T(8,128)(2,1)S(1)}, bf16[24,7168]{1,0:T(8,128)(2,1)}, u32[]{:S(2)}) copy-start(bf16[24,7168]{1,0:T(8,128)(2,1)} %get-tuple-element.9) | copy-start | bytes 1032196
  223.7 29.1 %copy-start.16 = (bf16[24,7168]{1,0:T(8,128)(2,1)S(1)}, bf16[24,7168]{1,0:T(8,128)(2,1)}, u32[]{:S(2)}) copy-start(bf16[24,7168]{1,0:T(8,128)(2,1)} %get-tuple-element.10) | copy-start | bytes 1032196
  223.8 23.2 %collective-permute-start.26 = (bf16[24,7168]{1,0:T(8,128)(2,1)S(1)}, bf16[24,7168]{1,0:T(8,128)(2,1)S(1)}, u32[]{:S(2)}, u32[]{:S(2)}) collective-permute-start(bf16[24,7168]{1,0:T(8,128)(2,1)S(1)} %get-tuple-element.45), channel_id=1, source_target_pairs={{0,2},{2,0},{1,3},{3,1},{4,6},{6,4},{5,7},{7,5},{8,10},{10,8},{9,1... | collective-permute-start | bytes 1032200 | tf_op jit(solution)/shard_map/ppermute | solution.py:13
  225.3 27.4 %collective-permute-start.27 = (bf16[24,7168]{1,0:T(8,128)(2,1)S(1)}, bf16[24,7168]{1,0:T(8,128)(2,1)S(1)}, u32[]{:S(2)}, u32[]{:S(2)}) collective-permute-start(bf16[24,7168]{1,0:T(8,128)(2,1)S(1)} %get-tuple-element.46), channel_id=1, source_target_pairs={{0,2},{2,0},{1,3},{3,1},{4,6},{6,4},{5,7},{7,5},{8,10},{10,8},{9,1... | collective-permute-start | bytes 1032200 | tf_op jit(solution)/shard_map/ppermute | solution.py:13
  239.8 61.9 %collective-permute-start.37 = (bf16[24,7168]{1,0:T(8,128)(2,1)S(1)}, bf16[24,7168]{1,0:T(8,128)(2,1)S(1)}, u32[]{:S(2)}, u32[]{:S(2)}) collective-permute-start(bf16[24,7168]{1,0:T(8,128)(2,1)S(1)} %get-tuple-element.30), channel_id=1, source_target_pairs={{0,8},{4,12},{8,0},{12,4},{1,9},{5,13},{9,1},{13,5},{2,10},{6,14},... | collective-permute-start | bytes 1032200 | tf_op jit(solution)/shard_map/ppermute | solution.py:100
  241.2 60.5 %collective-permute-start.39 = (bf16[24,7168]{1,0:T(8,128)(2,1)S(1)}, bf16[24,7168]{1,0:T(8,128)(2,1)S(1)}, u32[]{:S(2)}, u32[]{:S(2)}) collective-permute-start(bf16[24,7168]{1,0:T(8,128)(2,1)S(1)} %get-tuple-element.31), channel_id=1, source_target_pairs={{0,12},{4,8},{8,4},{12,0},{1,13},{5,9},{9,5},{13,1},{2,14},{6,10},... | collective-permute-start | bytes 1032200 | tf_op jit(solution)/shard_map/ppermute | solution.py:100
  242.8 22.7 %collective-permute-start.21 = (bf16[24,7168]{1,0:T(8,128)(2,1)S(1)}, bf16[24,7168]{1,0:T(8,128)(2,1)S(1)}, u32[]{:S(2)}, u32[]{:S(2)}) collective-permute-start(bf16[24,7168]{1,0:T(8,128)(2,1)S(1)} %copy-done.18), channel_id=1, source_target_pairs={{0,4},{4,0},{8,12},{12,8},{1,5},{5,1},{9,13},{13,9},{2,6},{6,2},{1... | collective-permute-start | bytes 1032200 | tf_op jit(solution)/shard_map/ppermute | solution.py:100
  247.0 42.9 %collective-permute-start.22 = (bf16[24,7168]{1,0:T(8,128)(2,1)S(1)}, bf16[24,7168]{1,0:T(8,128)(2,1)S(1)}, u32[]{:S(2)}, u32[]{:S(2)}) collective-permute-start(bf16[24,7168]{1,0:T(8,128)(2,1)S(1)} %copy-done.17), channel_id=1, source_target_pairs={{0,8},{4,12},{8,0},{12,4},{1,9},{5,13},{9,1},{13,5},{2,10},{6,14},... | collective-permute-start | bytes 1032200 | tf_op jit(solution)/shard_map/ppermute | solution.py:100
  252.8 46.5 %collective-permute-start.23 = (bf16[24,7168]{1,0:T(8,128)(2,1)S(1)}, bf16[24,7168]{1,0:T(8,128)(2,1)S(1)}, u32[]{:S(2)}, u32[]{:S(2)}) collective-permute-start(bf16[24,7168]{1,0:T(8,128)(2,1)S(1)} %copy-done.16), channel_id=1, source_target_pairs={{0,12},{4,8},{8,4},{12,0},{1,13},{5,9},{9,5},{13,1},{2,14},{6,10},... | collective-permute-start | bytes 1032200 | tf_op jit(solution)/shard_map/ppermute | solution.py:100
  253.2 46.2 %copy-start.11 = (bf16[1,32,7168]{2,1,0:T(8,128)(2,1)S(1)}, bf16[1,32,7168]{2,1,0:T(8,128)(2,1)}, u32[]{:S(2)}) copy-start(bf16[1,32,7168]{2,1,0:T(8,128)(2,1)} %param.10) | copy-start | bytes 1376260
  253.2 46.2 %copy-start.19 = (f32[32,96]{1,0:T(8,128)S(1)}, f32[32,96]{1,0:T(8,128)}, u32[]{:S(2)}) copy-start(f32[32,96]{1,0:T(8,128)} %get-tuple-element.15) | copy-start | bytes 36868
  265.5 36.3 %collective-permute-start.28 = (bf16[24,7168]{1,0:T(8,128)(2,1)S(1)}, bf16[24,7168]{1,0:T(8,128)(2,1)S(1)}, u32[]{:S(2)}, u32[]{:S(2)}) collective-permute-start(bf16[24,7168]{1,0:T(8,128)(2,1)S(1)} %get-tuple-element.25), channel_id=1, source_target_pairs={{0,4},{4,0},{8,12},{12,8},{1,5},{5,1},{9,13},{13,9},{2,6},{6,2},{1... | collective-permute-start | bytes 1032200 | tf_op jit(solution)/shard_map/ppermute | solution.py:100
  299.4 2.5 copy-start.20
  300.1 13.4 %collective-permute-start.24 = (bf16[1,32,7168]{2,1,0:T(8,128)(2,1)S(1)}, bf16[1,32,7168]{2,1,0:T(8,128)(2,1)S(1)}, u32[]{:S(2)}, u32[]{:S(2)}) collective-permute-start(bf16[1,32,7168]{2,1,0:T(8,128)(2,1)S(1)} %fusion.5), channel_id=1, source_target_pairs={{0,16},{16,0},{1,17},{17,1},{2,18},{18,2},{3,19},{19,3},{4,20},{20... | collective-permute-start | bytes 1376264 | tf_op jit(solution)/shard_map/ppermute | solution.py:19
  302.6 19.9 %collective-permute-start.40 = (bf16[1,32,7168]{2,1,0:T(8,128)(2,1)S(1)}, bf16[1,32,7168]{2,1,0:T(8,128)(2,1)S(1)}, u32[]{:S(2)}, u32[]{:S(2)}) collective-permute-start(bf16[1,32,7168]{2,1,0:T(8,128)(2,1)S(1)} %fusion.4), channel_id=1, source_target_pairs={{0,16},{16,0},{1,17},{17,1},{2,18},{18,2},{3,19},{19,3},{4,20},{20... | collective-permute-start | bytes 1376264 | tf_op jit(solution)/shard_map/ppermute | solution.py:19

commit v13 on v5

--- a/solution.py
+++ b/solution.py
@@ -75,9 +75,9 @@
             received = slots[0]
         else:
             received = lax.ppermute(slots[d], "z", [(i, i ^ d) for i in range(count)])
-        across = jnp.stack([received, swap(received, "x")])
-        pieces.append(jnp.stack([across, swap(across, "c")]))
-    return jnp.stack(pieces, axis=2)
+        pieces.append(jnp.stack([received, swap(received, "x")]))
+    across = jnp.stack(pieces, axis=1)
+    return jnp.stack([across, swap(across, "c")])
 
 
 def reduce_group(partial):

time: 275 us -> 294 us (1.069)
  waiting for transfers between devices: 187 us -> 211 us
  other arithmetic: 19.5 us -> 15.3 us
  starting transfers between devices: 38.8 us -> 35.1 us
    ppermute x26 -> x20, waiting for transfers between devices: 105 us -> 120 us  [swap(): return lax.ppermute(value, axis, [(0, 1), (1, 0)])]
    ppermute x6, waiting for transfers between devices: 37.3 us -> 49.6 us  [dispatch(): received = lax.ppermute(slots[d], 'z', [(i, i ^ d) for i in range(count)])]
    another operation x20 -> x14, other arithmetic: 15.4 us -> 11.2 us  [the longest x8 3.82 us: dispatch(): across = jnp.stack(pieces, axis=1)]
    ppermute x26 -> x20, starting transfers between devices: 21.4 us -> 18.7 us  [swap(): return lax.ppermute(value, axis, [(0, 1), (1, 0)])]
    unnamed x28 -> x32, local copies, waits for them, and re-layouts: 4.49 us -> 6.32 us
  transfers between devices with their start and end apart: 40 -> 34, of which waited for: 25 -> 20; matrix products, arithmetic and copies ran while one was open for 8% -> 7% of each run, Pallas kernels for 0% -> 0%
where the time goes in v13:
time: 294 us; the launch traced here: 293 us
  waiting for transfers between devices  211 us (72%)
  starting transfers between devices  35.1 us (12%)
  matrix products  19 us (6%)
  other arithmetic  15.3 us (5%)
  local copies, waits for them, and re-layouts  11 us (4%)
    ppermute x20, waiting for transfers between devices, swap(): return lax.ppermute(value, axis, [(0, 1), (1, 0)])  120 us
    ppermute x6, waiting for transfers between devices, dispatch(): received = lax.ppermute(slots[d], 'z', [(i, i ^ d) for i in range(count)])  49.6 us
    ppermute x6, waiting for transfers between devices, returned(): out.append(lax.ppermute(totals[d], 'z', [(i, i ^ d) for i in range(count)]))  32.3 us
    ppermute x20, starting transfers between devices, swap(): return lax.ppermute(value, axis, [(0, 1), (1, 0)])  18.7 us
    ppermute x2, waiting for transfers between devices, passed_along(): return lax.ppermute(value, axis, pairs)  9.45 us
    ppermute x6, starting transfers between devices, dispatch(): received = lax.ppermute(slots[d], 'z', [(i, i ^ d) for i in range(count)])  8.32 us
    unnamed x32, local copies, waits for them, and re-layouts  6.32 us
  transfers between devices with their start and end apart: 34, of which 20 were waited for; matrix products, arithmetic and copies ran while one was open for 7% of the time, Pallas kernels for 0%

profile of v13, /device:TPU:16, one launch (start us, length us, event | category | flops | bytes accessed | tf_op | source)
XLA Modules:
  0.0 293.0 jit_solution(11448344678135408155)
XLA Ops:
  0.7 0.8 broadcast_xor_fusion
  2.2 0.8 convert_reduce_fusion
  3.0 1.6 convolution_convert_fusion.2
  5.2 3.5 %collective-permute-start.11 = (bf16[24,7168]{1,0:T(8,128)(2,1)S(1)}, bf16[24,7168]{1,0:T(8,128)(2,1)S(1)}, u32[]{:S(2)}, u32[]{:S(2)}) collective-permute-start(bf16[24,7168]{1,0:T(8,128)(2,1)S(1)} %get-tuple-element.51), channel_id=1, source_target_pairs={{0,8},{4,12},{8,0},{12,4},{1,9},{5,13},{9,1},{13,5},{2,10},{6,14},... | collective-permute-start | bytes 1032200 | tf_op jit(solution)/shard_map/ppermute | solution.py:77
  8.7 1.5 collective-permute-start.8
  11.1 0.9 convolution_convert_fusion
  13.0 17.9 %collective-permute-done.13 = bf16[24,7168]{1,0:T(8,128)(2,1)} collective-permute-done((bf16[24,7168]{1,0:T(8,128)(2,1)S(1)}, bf16[24,7168]{1,0:T(8,128)(2,1)}, u32[]{:S(2)}, u32[]{:S(2)}) %collective-permute-start.13) | collective-permute-done | bytes 344096 | tf_op jit(solution)/shard_map/ppermute | solution.py:77
  30.9 1.5 collective-permute-start.14
  32.3 1.0 maximum_bitcast_fusion.4
  33.4 31.7 %collective-permute-done.11 = bf16[24,7168]{1,0:T(8,128)(2,1)S(1)} collective-permute-done((bf16[24,7168]{1,0:T(8,128)(2,1)S(1)}, bf16[24,7168]{1,0:T(8,128)(2,1)S(1)}, u32[]{:S(2)}, u32[]{:S(2)}) %collective-permute-start.11) | collective-permute-done | bytes 344096 | tf_op jit(solution)/shard_map/ppermute | solution.py:77
  65.1 3.7 %collective-permute-start.1 = (bf16[24,14336]{1,0:T(8,128)(2,1)S(1)}, bf16[24,14336]{1,0:T(8,128)(2,1)S(1)}, u32[]{:S(2)}, u32[]{:S(2)}) collective-permute-start(bf16[24,14336]{1,0:T(8,128)(2,1)S(1)} %get-tuple-element.47), channel_id=1, source_target_pairs={{0,4},{4,0},{8,12},{12,8},{1,5},{5,1},{9,13},{13,9},{2,6},{6,2},{1... | collective-permute-start | bytes 2064392 | tf_op jit(solution)/shard_map/ppermute | solution.py:77
  68.8 1.5 collective-permute-start.12
  70.3 1.0 maximum_bitcast_fusion.7
  72.0 7.9 %collective-permute-done.12 = bf16[24,7168]{1,0:T(8,128)(2,1)S(1)} collective-permute-done((bf16[24,7168]{1,0:T(8,128)(2,1)S(1)}, bf16[24,7168]{1,0:T(8,128)(2,1)S(1)}, u32[]{:S(2)}, u32[]{:S(2)}) %collective-permute-start.12) | collective-permute-done | bytes 344096 | tf_op jit(solution)/shard_map/ppermute | solution.py:13
  79.8 1.5 collective-permute-start.10
  81.4 17.0 %collective-permute-done.10 = bf16[24,7168]{1,0:T(8,128)(2,1)S(1)} collective-permute-done((bf16[24,7168]{1,0:T(8,128)(2,1)S(1)}, bf16[24,7168]{1,0:T(8,128)(2,1)S(1)}, u32[]{:S(2)}, u32[]{:S(2)}) %collective-permute-start.10) | collective-permute-done | bytes 344096 | tf_op jit(solution)/shard_map/ppermute | solution.py:13
  98.5 0.7 fusion.77
  99.3 1.6 collective-permute-start.6
  101.6 1.5 collective-permute-start.2
  103.1 14.5 %collective-permute-done.6 = bf16[24,14336]{1,0:T(8,128)(2,1)S(1)} collective-permute-done((bf16[24,14336]{1,0:T(8,128)(2,1)S(1)}, bf16[24,14336]{1,0:T(8,128)(2,1)S(1)}, u32[]{:S(2)}, u32[]{:S(2)}) %collective-permute-start.6) | collective-permute-done | bytes 688160 | tf_op jit(solution)/shard_map/ppermute | solution.py:13
  117.7 14.6 %collective-permute-done.4 = bf16[24,14336]{1,0:T(8,128)(2,1)S(1)} collective-permute-done((bf16[24,14336]{1,0:T(8,128)(2,1)S(1)}, bf16[24,14336]{1,0:T(8,128)(2,1)S(1)}, u32[]{:S(2)}, u32[]{:S(2)}) %collective-permute-start.4) | collective-permute-done | bytes 688160 | tf_op jit(solution)/shard_map/ppermute | solution.py:13
  133.5 1.6 copy-done
  135.0 1.6 fusion.19
  137.1 1.6 fusion.44
  139.1 1.6 convolution_convert_fusion.1
  141.1 5.6 %collective-permute-done.2 = bf16[24,14336]{1,0:T(8,128)(2,1)} collective-permute-done((bf16[24,14336]{1,0:T(8,128)(2,1)S(1)}, bf16[24,14336]{1,0:T(8,128)(2,1)}, u32[]{:S(2)}, u32[]{:S(2)}) %collective-permute-start.2) | collective-permute-done | bytes 688160 | tf_op jit(solution)/shard_map/ppermute | solution.py:13
  146.7 1.2 maximum_bitcast_fusion.1
  147.9 1.0 fusion.78
  149.0 1.5 copy-done.6
  150.5 2.8 fusion.75
  153.4 1.6 collective-permute-start.20
  155.5 1.5 collective-permute-start.18
  157.6 6.8 %collective-permute-done.20 = bf16[24,7168]{1,0:T(8,128)(2,1)S(1)} collective-permute-done((bf16[24,7168]{1,0:T(8,128)(2,1)S(1)}, bf16[24,7168]{1,0:T(8,128)(2,1)S(1)}, u32[]{:S(2)}, u32[]{:S(2)}) %collective-permute-start.20) | collective-permute-done | bytes 344096 | tf_op jit(solution)/shard_map/ppermute | solution.py:13
  164.4 7.4 %collective-permute-done.19 = bf16[24,7168]{1,0:T(8,128)(2,1)S(1)} collective-permute-done((bf16[24,7168]{1,0:T(8,128)(2,1)S(1)}, bf16[24,7168]{1,0:T(8,128)(2,1)S(1)}, u32[]{:S(2)}, u32[]{:S(2)}) %collective-permute-start.19) | collective-permute-done | bytes 344096 | tf_op jit(solution)/shard_map/ppermute | solution.py:13
  171.7 7.4 %collective-permute-done.18 = bf16[24,7168]{1,0:T(8,128)(2,1)S(1)} collective-permute-done((bf16[24,7168]{1,0:T(8,128)(2,1)S(1)}, bf16[24,7168]{1,0:T(8,128)(2,1)S(1)}, u32[]{:S(2)}, u32[]{:S(2)}) %collective-permute-start.18) | collective-permute-done | bytes 344096 | tf_op jit(solution)/shard_map/ppermute | solution.py:13
  179.1 7.0 %collective-permute-done.17 = bf16[24,7168]{1,0:T(8,128)(2,1)S(1)} collective-permute-done((bf16[24,7168]{1,0:T(8,128)(2,1)S(1)}, bf16[24,7168]{1,0:T(8,128)(2,1)S(1)}, u32[]{:S(2)}, u32[]{:S(2)}) %collective-permute-start.17) | collective-permute-done | bytes 344096 | tf_op jit(solution)/shard_map/ppermute | solution.py:13
  186.1 1.2 fusion.59
  187.2 1.4 pad_maximum_fusion
  188.7 2.0 copy.35
  190.8 1.6 fusion.6
  192.8 1.7 fusion.4
  194.8 1.6 fusion.39
  196.5 1.6 fusion.16
  198.1 3.9 %add_convert_fusion = bf16[384,7168]{1,0:T(8,128)(2,1)S(1)} fusion(f32[384,7168]{1,0:T(8,128)S(1)} %fusion.16, bf16[1,7168,256]{2,1,0:T(8,128)(2,1)} %param.18, f32[384,256]{1,0:T(8,128)} %copy-done.10, f32[384,256]{1,0:T(8,128)S(1)} %fusion.6), kind=kOutput, calls=%fused_computation.2 | convolution fusion | flops 1415380992 | bytes 20971520 | tf_op jit(solution)/shard_map/dot_general | solution.py:64
  202.5 5.1 %collective-permute-done.25 = bf16[2,4,24,7168]{3,2,1,0:T(8,128)(2,1)S(1)} collective-permute-done((bf16[2,4,24,7168]{3,2,1,0:T(8,128)(2,1)S(1)}, bf16[2,4,24,7168]{3,2,1,0:T(8,128)(2,1)S(1)}, u32[]{:S(2)}, u32[]{:S(2)}) %collective-permute-start.25) | collective-permute-done | bytes 2752544 | tf_op jit(solution)/shard_map/ppermute | solution.py:13
  207.6 1.0 fusion.76
  208.7 1.6 collective-permute-start.26
  210.8 1.5 collective-permute-start.29
  213.1 6.6 %collective-permute-done.26 = bf16[24,7168]{1,0:T(8,128)(2,1)S(1)} collective-permute-done((bf16[24,7168]{1,0:T(8,128)(2,1)S(1)}, bf16[24,7168]{1,0:T(8,128)(2,1)S(1)}, u32[]{:S(2)}, u32[]{:S(2)}) %collective-permute-start.26) | collective-permute-done | bytes 344096 | tf_op jit(solution)/shard_map/ppermute | solution.py:13
  220.0 7.0 %collective-permute-done.31 = bf16[24,7168]{1,0:T(8,128)(2,1)S(1)} collective-permute-done((bf16[24,7168]{1,0:T(8,128)(2,1)S(1)}, bf16[24,7168]{1,0:T(8,128)(2,1)S(1)}, u32[]{:S(2)}, u32[]{:S(2)}) %collective-permute-start.31) | collective-permute-done | bytes 344096 | tf_op jit(solution)/shard_map/ppermute | solution.py:13
  227.7 6.7 %collective-permute-done.29 = bf16[24,7168]{1,0:T(8,128)(2,1)S(1)} collective-permute-done((bf16[24,7168]{1,0:T(8,128)(2,1)S(1)}, bf16[24,7168]{1,0:T(8,128)(2,1)S(1)}, u32[]{:S(2)}, u32[]{:S(2)}) %collective-permute-start.29) | collective-permute-done | bytes 344096 | tf_op jit(solution)/shard_map/ppermute | solution.py:13
  234.4 6.6 %collective-permute-done.27 = bf16[24,7168]{1,0:T(8,128)(2,1)S(1)} collective-permute-done((bf16[24,7168]{1,0:T(8,128)(2,1)S(1)}, bf16[24,7168]{1,0:T(8,128)(2,1)S(1)}, u32[]{:S(2)}, u32[]{:S(2)}) %collective-permute-start.27) | collective-permute-done | bytes 344096 | tf_op jit(solution)/shard_map/ppermute | solution.py:13
  241.7 1.7 collective-permute-start.28
  243.4 1.4 collective-permute-start.32
  244.8 15.8 %collective-permute-done.23 = bf16[24,7168]{1,0:T(8,128)(2,1)S(1)} collective-permute-done((bf16[24,7168]{1,0:T(8,128)(2,1)S(1)}, bf16[24,7168]{1,0:T(8,128)(2,1)S(1)}, u32[]{:S(2)}, u32[]{:S(2)}) %collective-permute-start.23) | collective-permute-done | bytes 344096 | tf_op jit(solution)/shard_map/ppermute | solution.py:97
  260.8 0.7 fusion.3
  261.5 1.6 collective-permute-start.24
  263.1 9.1 %collective-permute-done.30 = bf16[24,7168]{1,0:T(8,128)(2,1)S(1)} collective-permute-done((bf16[24,7168]{1,0:T(8,128)(2,1)S(1)}, bf16[24,7168]{1,0:T(8,128)(2,1)S(1)}, u32[]{:S(2)}, u32[]{:S(2)}) %collective-permute-start.30) | collective-permute-done | bytes 344096 | tf_op jit(solution)/shard_map/ppermute | solution.py:97
  272.2 7.3 %collective-permute-done.32 = bf16[24,7168]{1,0:T(8,128)(2,1)S(1)} collective-permute-done((bf16[24,7168]{1,0:T(8,128)(2,1)S(1)}, bf16[24,7168]{1,0:T(8,128)(2,1)S(1)}, u32[]{:S(2)}, u32[]{:S(2)}) %collective-permute-start.32) | collective-permute-done | bytes 344096 | tf_op jit(solution)/shard_map/ppermute | solution.py:97
  279.7 0.7 fusion.2
  280.4 1.6 collective-permute-start.33
  282.0 9.4 %collective-permute-done.33 = bf16[1,32,7168]{2,1,0:T(8,128)(2,1)S(1)} collective-permute-done((bf16[1,32,7168]{2,1,0:T(8,128)(2,1)S(1)}, bf16[1,32,7168]{2,1,0:T(8,128)(2,1)S(1)}, u32[]{:S(2)}, u32[]{:S(2)}) %collective-permute-start.33) | collective-permute-done | bytes 458784 | tf_op jit(solution)/shard_map/ppermute | solution.py:19
  291.4 0.8 copy.38
  292.2 0.8 copy.39
  (93 shorter events, 13.2 us)
Async XLA Ops:
  0.6 10.3 %copy-start.14 = (f32[1,32,2]{1,2,0:T(2,128)S(1)}, f32[1,32,2]{1,2,0:T(2,128)}, u32[]{:S(2)}) copy-start(f32[1,32,2]{1,2,0:T(2,128)} %param.16) | copy-start | bytes 772
  0.6 10.4 %copy-start.8 = (bf16[1,32,7168]{2,1,0:T(8,128)(2,1)S(1)}, bf16[1,32,7168]{2,1,0:T(8,128)(2,1)}, u32[]{:S(2)}) copy-start(bf16[1,32,7168]{2,1,0:T(8,128)(2,1)} %param.14) | copy-start | bytes 1376260
  0.7 10.4 %copy-start.9 = (bf16[1,32,7168]{2,1,0:T(8,128)(2,1)S(1)}, bf16[1,32,7168]{2,1,0:T(8,128)(2,1)}, u32[]{:S(2)}) copy-start(bf16[1,32,7168]{2,1,0:T(8,128)(2,1)} %param.13) | copy-start | bytes 1376260
  4.7 26.1 %collective-permute-start.13 = (bf16[24,7168]{1,0:T(8,128)(2,1)S(1)}, bf16[24,7168]{1,0:T(8,128)(2,1)}, u32[]{:S(2)}, u32[]{:S(2)}) collective-permute-start(bf16[24,7168]{1,0:T(8,128)(2,1)S(1)} %get-tuple-element.50), channel_id=1, source_target_pairs={{0,12},{4,8},{8,4},{12,0},{1,13},{5,9},{9,5},{13,1},{2,14},{6,10},... | collective-permute-start | bytes 1032200 | tf_op jit(solution)/shard_map/ppermute | solution.py:77
  5.2 59.9 %collective-permute-start.11 = (bf16[24,7168]{1,0:T(8,128)(2,1)S(1)}, bf16[24,7168]{1,0:T(8,128)(2,1)S(1)}, u32[]{:S(2)}, u32[]{:S(2)}) collective-permute-start(bf16[24,7168]{1,0:T(8,128)(2,1)S(1)} %get-tuple-element.51), channel_id=1, source_target_pairs={{0,8},{4,12},{8,0},{12,4},{1,9},{5,13},{9,1},{13,5},{2,10},{6,14},... | collective-permute-start | bytes 1032200 | tf_op jit(solution)/shard_map/ppermute | solution.py:77
  8.7 62.6 %collective-permute-start.9 = (bf16[24,7168]{1,0:T(8,128)(2,1)S(1)}, bf16[24,7168]{1,0:T(8,128)(2,1)S(1)}, u32[]{:S(2)}, u32[]{:S(2)}) collective-permute-start(bf16[24,7168]{1,0:T(8,128)(2,1)S(1)} %get-tuple-element.52), channel_id=1, source_target_pairs={{0,4},{4,0},{8,12},{12,8},{1,5},{5,1},{9,13},{13,9},{2,6},{6,2},{1... | collective-permute-start | bytes 1032200 | tf_op jit(solution)/shard_map/ppermute | solution.py:77
  8.7 22.1 %collective-permute-start.8 = (bf16[24,7168]{1,0:T(8,128)(2,1)S(1)}, bf16[24,7168]{1,0:T(8,128)(2,1)}, u32[]{:S(2)}, u32[]{:S(2)}) collective-permute-start(bf16[24,7168]{1,0:T(8,128)(2,1)S(1)} %get-tuple-element.53), channel_id=1, source_target_pairs={{0,2},{2,0},{1,3},{3,1},{4,6},{6,4},{5,7},{7,5},{8,10},{10,8},{9,1... | collective-permute-start | bytes 1032200 | tf_op jit(solution)/shard_map/ppermute | solution.py:13
  12.3 86.9 %collective-permute-start.5 = (bf16[24,14336]{1,0:T(8,128)(2,1)S(1)}, bf16[24,14336]{1,0:T(8,128)(2,1)S(1)}, u32[]{:S(2)}, u32[]{:S(2)}) collective-permute-start(bf16[24,14336]{1,0:T(8,128)(2,1)S(1)} %get-tuple-element.45), channel_id=1, source_target_pairs={{0,12},{4,8},{8,4},{12,0},{1,13},{5,9},{9,5},{13,1},{2,14},{6,10},... | collective-permute-start | bytes 2064392 | tf_op jit(solution)/shard_map/ppermute | solution.py:77
  30.8 70.1 %collective-permute-start.3 = (bf16[24,14336]{1,0:T(8,128)(2,1)S(1)}, bf16[24,14336]{1,0:T(8,128)(2,1)S(1)}, u32[]{:S(2)}, u32[]{:S(2)}) collective-permute-start(bf16[24,14336]{1,0:T(8,128)(2,1)S(1)} %get-tuple-element.46), channel_id=1, source_target_pairs={{0,8},{4,12},{8,0},{12,4},{1,9},{5,13},{9,1},{13,5},{2,10},{6,14},... | collective-permute-start | bytes 2064392 | tf_op jit(solution)/shard_map/ppermute | solution.py:77
  30.9 38.0 %collective-permute-start.14 = (bf16[24,7168]{1,0:T(8,128)(2,1)}, bf16[24,7168]{1,0:T(8,128)(2,1)S(1)}, u32[]{:S(2)}, u32[]{:S(2)}) collective-permute-start(bf16[24,7168]{1,0:T(8,128)(2,1)} %collective-permute-done.13), channel_id=1, source_target_pairs={{0,2},{2,0},{1,3},{3,1},{4,6},{6,4},{5,7},{7,5},{8,10},{10,8},{9,1... | collective-permute-start | bytes 1032200 | tf_op jit(solution)/shard_map/ppermute | solution.py:13
  65.1 36.4 %collective-permute-start.1 = (bf16[24,14336]{1,0:T(8,128)(2,1)S(1)}, bf16[24,14336]{1,0:T(8,128)(2,1)S(1)}, u32[]{:S(2)}, u32[]{:S(2)}) collective-permute-start(bf16[24,14336]{1,0:T(8,128)(2,1)S(1)} %get-tuple-element.47), channel_id=1, source_target_pairs={{0,4},{4,0},{8,12},{12,8},{1,5},{5,1},{9,13},{13,9},{2,6},{6,2},{1... | collective-permute-start | bytes 2064392 | tf_op jit(solution)/shard_map/ppermute | solution.py:77
  68.8 11.0 %collective-permute-start.12 = (bf16[24,7168]{1,0:T(8,128)(2,1)S(1)}, bf16[24,7168]{1,0:T(8,128)(2,1)S(1)}, u32[]{:S(2)}, u32[]{:S(2)}) collective-permute-start(bf16[24,7168]{1,0:T(8,128)(2,1)S(1)} %collective-permute-done.11), channel_id=1, source_target_pairs={{0,2},{2,0},{1,3},{3,1},{4,6},{6,4},{5,7},{7,5},{8,10},{10,8},{9,1... | collective-permute-start | bytes 1032200 | tf_op jit(solution)/shard_map/ppermute | solution.py:13
  71.4 29.5 %collective-permute-start = (bf16[24,14336]{1,0:T(8,128)(2,1)S(1)}, bf16[24,14336]{1,0:T(8,128)(2,1)S(1)}, u32[]{:S(2)}, u32[]{:S(2)}) collective-permute-start(bf16[24,14336]{1,0:T(8,128)(2,1)S(1)} %get-tuple-element.48), channel_id=1, source_target_pairs={{0,2},{2,0},{1,3},{3,1},{4,6},{6,4},{5,7},{7,5},{8,10},{10,8},{9,1... | collective-permute-start | bytes 2064392 | tf_op jit(solution)/shard_map/ppermute | solution.py:13
  79.8 18.6 %collective-permute-start.10 = (bf16[24,7168]{1,0:T(8,128)(2,1)S(1)}, bf16[24,7168]{1,0:T(8,128)(2,1)S(1)}, u32[]{:S(2)}, u32[]{:S(2)}) collective-permute-start(bf16[24,7168]{1,0:T(8,128)(2,1)S(1)} %collective-permute-done.9), channel_id=1, source_target_pairs={{0,2},{2,0},{1,3},{3,1},{4,6},{6,4},{5,7},{7,5},{8,10},{10,8},{9,1... | collective-permute-start | bytes 1032200 | tf_op jit(solution)/shard_map/ppermute | solution.py:13
  99.2 33.3 %collective-permute-start.15 = (bf16[2,4,24,7168]{3,2,0,1:T(8,128)(2,1)S(1)}, bf16[2,4,24,7168]{3,2,0,1:T(8,128)(2,1)S(1)}, u32[]{:S(2)}, u32[]{:S(2)}) collective-permute-start(bf16[2,4,24,7168]{3,2,0,1:T(8,128)(2,1)S(1)} %get-tuple-element.43), channel_id=1, source_target_pairs={{0,1},{1,0},{2,3},{3,2},{4,5},{5,4},{6,7},{7,6},{8,9},{9,8},{10,11... | collective-permute-start | bytes 8257544 | tf_op jit(solution)/shard_map/ppermute | solution.py:13
  99.3 18.3 %collective-permute-start.6 = (bf16[24,14336]{1,0:T(8,128)(2,1)S(1)}, bf16[24,14336]{1,0:T(8,128)(2,1)S(1)}, u32[]{:S(2)}, u32[]{:S(2)}) collective-permute-start(bf16[24,14336]{1,0:T(8,128)(2,1)S(1)} %collective-permute-done.5), channel_id=1, source_target_pairs={{0,2},{2,0},{1,3},{3,1},{4,6},{6,4},{5,7},{7,5},{8,10},{10,8},{9,1... | collective-permute-start | bytes 2064392 | tf_op jit(solution)/shard_map/ppermute | solution.py:13
  101.0 31.3 %collective-permute-start.4 = (bf16[24,14336]{1,0:T(8,128)(2,1)S(1)}, bf16[24,14336]{1,0:T(8,128)(2,1)S(1)}, u32[]{:S(2)}, u32[]{:S(2)}) collective-permute-start(bf16[24,14336]{1,0:T(8,128)(2,1)S(1)} %collective-permute-done.3), channel_id=1, source_target_pairs={{0,2},{2,0},{1,3},{3,1},{4,6},{6,4},{5,7},{7,5},{8,10},{10,8},{9,1... | collective-permute-start | bytes 2064392 | tf_op jit(solution)/shard_map/ppermute | solution.py:13
  101.6 45.1 %collective-permute-start.2 = (bf16[24,14336]{1,0:T(8,128)(2,1)S(1)}, bf16[24,14336]{1,0:T(8,128)(2,1)}, u32[]{:S(2)}, u32[]{:S(2)}) collective-permute-start(bf16[24,14336]{1,0:T(8,128)(2,1)S(1)} %collective-permute-done.1), channel_id=1, source_target_pairs={{0,2},{2,0},{1,3},{3,1},{4,6},{6,4},{5,7},{7,5},{8,10},{10,8},{9,1... | collective-permute-start | bytes 2064392 | tf_op jit(solution)/shard_map/ppermute | solution.py:13
  133.0 2.0 copy-start
  135.0 2.0 copy-start.2
  137.1 2.0 copy-start.4
  141.1 7.9 %collective-permute-start.16 = (bf16[2,4,24,7168]{3,2,1,0:T(8,128)(2,1)S(1)}, bf16[2,4,24,7168]{3,2,1,0:T(8,128)(2,1)S(1)}, u32[]{:S(2)}, u32[]{:S(2)}) collective-permute-start(bf16[2,4,24,7168]{3,2,1,0:T(8,128)(2,1)S(1)} %bitcast.194), channel_id=1, source_target_pairs={{0,1},{1,0},{2,3},{3,2},{4,5},{5,4},{6,7},{7,6},{8,9},{9,8},{10,11... | collective-permute-start | bytes 8257544 | tf_op jit(solution)/shard_map/ppermute | solution.py:13
  148.9 38.4 %collective-permute-start.7 = (bf16[2,4,24,14336]{3,2,0,1:T(8,128)(2,1)S(1)}, bf16[2,4,24,14336]{3,2,0,1:T(8,128)(2,1)S(1)}, u32[]{:S(2)}, u32[]{:S(2)}) collective-permute-start(bf16[2,4,24,14336]{3,2,0,1:T(8,128)(2,1)S(1)} %get-tuple-element.33), channel_id=1, source_target_pairs={{0,1},{1,0},{2,3},{3,2},{4,5},{5,4},{6,7},{7,6},{8,9},{9,8},{10,11... | collective-permute-start | bytes 16515080 | tf_op jit(solution)/shard_map/ppermute | solution.py:13
  149.0 1.5 copy-start.6
  153.4 10.9 %collective-permute-start.20 = (bf16[24,7168]{1,0:T(8,128)(2,1)S(1)}, bf16[24,7168]{1,0:T(8,128)(2,1)S(1)}, u32[]{:S(2)}, u32[]{:S(2)}) collective-permute-start(bf16[24,7168]{1,0:T(8,128)(2,1)S(1)} %get-tuple-element.38), channel_id=1, source_target_pairs={{0,2},{2,0},{1,3},{3,1},{4,6},{6,4},{5,7},{7,5},{8,10},{10,8},{9,1... | collective-permute-start | bytes 1032200 | tf_op jit(solution)/shard_map/ppermute | solution.py:13
  155.0 16.7 %collective-permute-start.19 = (bf16[24,7168]{1,0:T(8,128)(2,1)S(1)}, bf16[24,7168]{1,0:T(8,128)(2,1)S(1)}, u32[]{:S(2)}, u32[]{:S(2)}) collective-permute-start(bf16[24,7168]{1,0:T(8,128)(2,1)S(1)} %get-tuple-element.39), channel_id=1, source_target_pairs={{0,2},{2,0},{1,3},{3,1},{4,6},{6,4},{5,7},{7,5},{8,10},{10,8},{9,1... | collective-permute-start | bytes 1032200 | tf_op jit(solution)/shard_map/ppermute | solution.py:13
  155.5 23.6 %collective-permute-start.18 = (bf16[24,7168]{1,0:T(8,128)(2,1)S(1)}, bf16[24,7168]{1,0:T(8,128)(2,1)S(1)}, u32[]{:S(2)}, u32[]{:S(2)}) collective-permute-start(bf16[24,7168]{1,0:T(8,128)(2,1)S(1)} %get-tuple-element.40), channel_id=1, source_target_pairs={{0,2},{2,0},{1,3},{3,1},{4,6},{6,4},{5,7},{7,5},{8,10},{10,8},{9,1... | collective-permute-start | bytes 1032200 | tf_op jit(solution)/shard_map/ppermute | solution.py:13
  157.0 29.0 %collective-permute-start.17 = (bf16[24,7168]{1,0:T(8,128)(2,1)S(1)}, bf16[24,7168]{1,0:T(8,128)(2,1)S(1)}, u32[]{:S(2)}, u32[]{:S(2)}) collective-permute-start(bf16[24,7168]{1,0:T(8,128)(2,1)S(1)} %get-tuple-element.41), channel_id=1, source_target_pairs={{0,2},{2,0},{1,3},{3,1},{4,6},{6,4},{5,7},{7,5},{8,10},{10,8},{9,1... | collective-permute-start | bytes 1032200 | tf_op jit(solution)/shard_map/ppermute | solution.py:13
  188.7 2.1 copy-start.1
  190.7 2.0 copy-start.5
  192.8 2.0 copy-start.3
  194.8 1.6 copy-start.10
  202.4 5.2 %collective-permute-start.25 = (bf16[2,4,24,7168]{3,2,1,0:T(8,128)(2,1)S(1)}, bf16[2,4,24,7168]{3,2,1,0:T(8,128)(2,1)S(1)}, u32[]{:S(2)}, u32[]{:S(2)}) collective-permute-start(bf16[2,4,24,7168]{3,2,1,0:T(8,128)(2,1)S(1)} %bitcast.195), channel_id=1, source_target_pairs={{0,1},{1,0},{2,3},{3,2},{4,5},{5,4},{6,7},{7,6},{8,9},{9,8},{10,11... | collective-permute-start | bytes 8257544 | tf_op jit(solution)/shard_map/ppermute | solution.py:13
  207.6 5.3 %copy-start.13 = (bf16[24,7168]{1,0:T(8,128)(2,1)S(1)}, bf16[24,7168]{1,0:T(8,128)(2,1)}, u32[]{:S(2)}) copy-start(bf16[24,7168]{1,0:T(8,128)(2,1)} %get-tuple-element.8) | copy-start | bytes 1032196
  207.6 12.1 %copy-start.12 = (bf16[24,7168]{1,0:T(8,128)(2,1)S(1)}, bf16[24,7168]{1,0:T(8,128)(2,1)}, u32[]{:S(2)}) copy-start(bf16[24,7168]{1,0:T(8,128)(2,1)} %get-tuple-element.9) | copy-start | bytes 1032196
  207.6 19.5 %copy-start.11 = (bf16[24,7168]{1,0:T(8,128)(2,1)S(1)}, bf16[24,7168]{1,0:T(8,128)(2,1)}, u32[]{:S(2)}) copy-start(bf16[24,7168]{1,0:T(8,128)(2,1)} %get-tuple-element.10) | copy-start | bytes 1032196
  208.7 11.0 %collective-permute-start.26 = (bf16[24,7168]{1,0:T(8,128)(2,1)S(1)}, bf16[24,7168]{1,0:T(8,128)(2,1)S(1)}, u32[]{:S(2)}, u32[]{:S(2)}) collective-permute-start(bf16[24,7168]{1,0:T(8,128)(2,1)S(1)} %get-tuple-element.34), channel_id=1, source_target_pairs={{0,2},{2,0},{1,3},{3,1},{4,6},{6,4},{5,7},{7,5},{8,10},{10,8},{9,1... | collective-permute-start | bytes 1032200 | tf_op jit(solution)/shard_map/ppermute | solution.py:13
  210.3 16.8 %collective-permute-start.31 = (bf16[24,7168]{1,0:T(8,128)(2,1)S(1)}, bf16[24,7168]{1,0:T(8,128)(2,1)S(1)}, u32[]{:S(2)}, u32[]{:S(2)}) collective-permute-start(bf16[24,7168]{1,0:T(8,128)(2,1)S(1)} %get-tuple-element.35), channel_id=1, source_target_pairs={{0,2},{2,0},{1,3},{3,1},{4,6},{6,4},{5,7},{7,5},{8,10},{10,8},{9,1... | collective-permute-start | bytes 1032200 | tf_op jit(solution)/shard_map/ppermute | solution.py:13
  210.8 23.6 %collective-permute-start.29 = (bf16[24,7168]{1,0:T(8,128)(2,1)S(1)}, bf16[24,7168]{1,0:T(8,128)(2,1)S(1)}, u32[]{:S(2)}, u32[]{:S(2)}) collective-permute-start(bf16[24,7168]{1,0:T(8,128)(2,1)S(1)} %get-tuple-element.36), channel_id=1, source_target_pairs={{0,2},{2,0},{1,3},{3,1},{4,6},{6,4},{5,7},{7,5},{8,10},{10,8},{9,1... | collective-permute-start | bytes 1032200 | tf_op jit(solution)/shard_map/ppermute | solution.py:13
  212.3 28.7 %collective-permute-start.27 = (bf16[24,7168]{1,0:T(8,128)(2,1)S(1)}, bf16[24,7168]{1,0:T(8,128)(2,1)S(1)}, u32[]{:S(2)}, u32[]{:S(2)}) collective-permute-start(bf16[24,7168]{1,0:T(8,128)(2,1)S(1)} %get-tuple-element.37), channel_id=1, source_target_pairs={{0,2},{2,0},{1,3},{3,1},{4,6},{6,4},{5,7},{7,5},{8,10},{10,8},{9,1... | collective-permute-start | bytes 1032200 | tf_op jit(solution)/shard_map/ppermute | solution.py:13
  212.8 30.6 %collective-permute-start.21 = (bf16[24,7168]{1,0:T(8,128)(2,1)S(1)}, bf16[24,7168]{1,0:T(8,128)(2,1)S(1)}, u32[]{:S(2)}, u32[]{:S(2)}) collective-permute-start(bf16[24,7168]{1,0:T(8,128)(2,1)S(1)} %copy-done.13), channel_id=1, source_target_pairs={{0,4},{4,0},{8,12},{12,8},{1,5},{5,1},{9,13},{13,9},{2,6},{6,2},{1... | collective-permute-start | bytes 1032200 | tf_op jit(solution)/shard_map/ppermute | solution.py:97
  219.7 25.1 %collective-permute-start.22 = (bf16[24,7168]{1,0:T(8,128)(2,1)S(1)}, bf16[24,7168]{1,0:T(8,128)(2,1)S(1)}, u32[]{:S(2)}, u32[]{:S(2)}) collective-permute-start(bf16[24,7168]{1,0:T(8,128)(2,1)S(1)} %copy-done.12), channel_id=1, source_target_pairs={{0,8},{4,12},{8,0},{12,4},{1,9},{5,13},{9,1},{13,5},{2,10},{6,14},... | collective-permute-start | bytes 1032200 | tf_op jit(solution)/shard_map/ppermute | solution.py:97
  227.0 33.6 %collective-permute-start.23 = (bf16[24,7168]{1,0:T(8,128)(2,1)S(1)}, bf16[24,7168]{1,0:T(8,128)(2,1)S(1)}, u32[]{:S(2)}, u32[]{:S(2)}) collective-permute-start(bf16[24,7168]{1,0:T(8,128)(2,1)S(1)} %copy-done.11), channel_id=1, source_target_pairs={{0,12},{4,8},{8,4},{12,0},{1,13},{5,9},{9,5},{13,1},{2,14},{6,10},... | collective-permute-start | bytes 1032200 | tf_op jit(solution)/shard_map/ppermute | solution.py:97
  241.0 19.8 %copy-start.7 = (bf16[1,32,7168]{2,1,0:T(8,128)(2,1)S(1)}, bf16[1,32,7168]{2,1,0:T(8,128)(2,1)}, u32[]{:S(2)}) copy-start(bf16[1,32,7168]{2,1,0:T(8,128)(2,1)} %param.10) | copy-start | bytes 1376260
  241.2 31.0 %collective-permute-start.30 = (bf16[24,7168]{1,0:T(8,128)(2,1)S(1)}, bf16[24,7168]{1,0:T(8,128)(2,1)S(1)}, u32[]{:S(2)}, u32[]{:S(2)}) collective-permute-start(bf16[24,7168]{1,0:T(8,128)(2,1)S(1)} %get-tuple-element.17), channel_id=1, source_target_pairs={{0,8},{4,12},{8,0},{12,4},{1,9},{5,13},{9,1},{13,5},{2,10},{6,14},... | collective-permute-start | bytes 1032200 | tf_op jit(solution)/shard_map/ppermute | solution.py:97
  241.7 30.5 %collective-permute-start.28 = (bf16[24,7168]{1,0:T(8,128)(2,1)S(1)}, bf16[24,7168]{1,0:T(8,128)(2,1)S(1)}, u32[]{:S(2)}, u32[]{:S(2)}) collective-permute-start(bf16[24,7168]{1,0:T(8,128)(2,1)S(1)} %get-tuple-element.18), channel_id=1, source_target_pairs={{0,4},{4,0},{8,12},{12,8},{1,5},{5,1},{9,13},{13,9},{2,6},{6,2},{1... | collective-permute-start | bytes 1032200 | tf_op jit(solution)/shard_map/ppermute | solution.py:97
  243.4 36.1 %collective-permute-start.32 = (bf16[24,7168]{1,0:T(8,128)(2,1)S(1)}, bf16[24,7168]{1,0:T(8,128)(2,1)S(1)}, u32[]{:S(2)}, u32[]{:S(2)}) collective-permute-start(bf16[24,7168]{1,0:T(8,128)(2,1)S(1)} %get-tuple-element.19), channel_id=1, source_target_pairs={{0,12},{4,8},{8,4},{12,0},{1,13},{5,9},{9,5},{13,1},{2,14},{6,10},... | collective-permute-start | bytes 1032200 | tf_op jit(solution)/shard_map/ppermute | solution.py:97
  261.5 20.5 %collective-permute-start.24 = (bf16[1,32,7168]{2,1,0:T(8,128)(2,1)S(1)}, bf16[1,32,7168]{2,1,0:T(8,128)(2,1)S(1)}, u32[]{:S(2)}, u32[]{:S(2)}) collective-permute-start(bf16[1,32,7168]{2,1,0:T(8,128)(2,1)S(1)} %fusion.3), channel_id=1, source_target_pairs={{0,16},{16,0},{1,17},{17,1},{2,18},{18,2},{3,19},{19,3},{4,20},{20... | collective-permute-start | bytes 1376264 | tf_op jit(solution)/shard_map/ppermute | solution.py:19
  280.4 11.1 %collective-permute-start.33 = (bf16[1,32,7168]{2,1,0:T(8,128)(2,1)S(1)}, bf16[1,32,7168]{2,1,0:T(8,128)(2,1)S(1)}, u32[]{:S(2)}, u32[]{:S(2)}) collective-permute-start(bf16[1,32,7168]{2,1,0:T(8,128)(2,1)S(1)} %fusion.2), channel_id=1, source_target_pairs={{0,16},{16,0},{1,17},{17,1},{2,18},{18,2},{3,19},{19,3},{4,20},{20... | collective-permute-start | bytes 1376264 | tf_op jit(solution)/shard_map/ppermute | solution.py:19

commit v14 on v5

--- a/solution.py
+++ b/solution.py
@@ -124,8 +124,11 @@
     b_joined = jnp.concatenate([bwd_input[0], bwd_grad[0]], axis=1)
     b_slots = into_slots(b_select, b_joined).reshape(experts, capacity, 2 * width)
     f_rows = dispatch(f_slots)
-    b_rows = dispatch(b_slots)
     f_partial = forward_rows(f_rows.reshape(-1, width), w_gate, w_up, w_down)
+    early = experts // 2
+    far = tuple(b_slots[d] for d in range(early, experts))
+    far, f_partial = lax.optimization_barrier((far, f_partial))
+    b_rows = dispatch([b_slots[d] for d in range(early)] + list(far))
     f_totals = reduce_group(f_partial.reshape(2, 2, experts, capacity, width))
     b_rows, f_totals = lax.optimization_barrier((b_rows, f_totals))
     f_out = returned(f_totals)

time: 275 us -> 297 us (1.080)
  waiting for transfers between devices: 187 us -> 204 us
    ppermute x6, waiting for transfers between devices: 37.3 us -> 73.8 us  [dispatch(): received = lax.ppermute(slots[d], 'z', [(i, i ^ d) for i in range(count)])]
    ppermute x26, waiting for transfers between devices: 105 us -> 86.1 us  [swap(): return lax.ppermute(value, axis, [(0, 1), (1, 0)])]
  transfers between devices with their start and end apart: 40 -> 40, of which waited for: 25 -> 24; matrix products, arithmetic and copies ran while one was open for 8% -> 9% of each run, Pallas kernels for 0% -> 0%
where the time goes in v14:
time: 297 us; the launch traced here: 296 us
  waiting for transfers between devices  204 us (69%)
  starting transfers between devices  41 us (14%)
  other arithmetic  20.9 us (7%)
  matrix products  19.1 us (6%)
  local copies, waits for them, and re-layouts  10.1 us (3%)
    ppermute x26, waiting for transfers between devices, swap(): return lax.ppermute(value, axis, [(0, 1), (1, 0)])  86.1 us
    ppermute x6, waiting for transfers between devices, dispatch(): received = lax.ppermute(slots[d], 'z', [(i, i ^ d) for i in range(count)])  73.8 us
    ppermute x6, waiting for transfers between devices, returned(): out.append(lax.ppermute(totals[d], 'z', [(i, i ^ d) for i in range(count)]))  33.7 us
    ppermute x26, starting transfers between devices, swap(): return lax.ppermute(value, axis, [(0, 1), (1, 0)])  20.3 us
    ppermute x2, waiting for transfers between devices, passed_along(): return lax.ppermute(value, axis, pairs)  10.5 us
    ppermute x6, starting transfers between devices, dispatch(): received = lax.ppermute(slots[d], 'z', [(i, i ^ d) for i in range(count)])  10.2 us
    ppermute x6, starting transfers between devices, returned(): out.append(lax.ppermute(totals[d], 'z', [(i, i ^ d) for i in range(count)]))  7.68 us
    another operation x10, other arithmetic, dispatch(): return jnp.stack(pieces, axis=2)  6.62 us
  transfers between devices with their start and end apart: 40, of which 24 were waited for; matrix products, arithmetic and copies ran while one was open for 9% of the time, Pallas kernels for 0%

profile of v14, /device:TPU:16, one launch (start us, length us, event | category | flops | bytes accessed | tf_op | source)
XLA Modules:
  0.0 296.4 jit_solution(8456179609159093510)
XLA Ops:
  3.0 1.6 convolution_convert_fusion.2
  4.7 1.6 collective-permute-start.7
  6.7 1.6 collective-permute-start.13
  8.3 1.5 collective-permute-start.5
  11.9 2.5 collective-permute-start.2
  14.4 7.0 %collective-permute-done.7 = bf16[24,7168]{1,0:T(8,128)(2,1)} collective-permute-done((bf16[24,7168]{1,0:T(8,128)(2,1)S(1)}, bf16[24,7168]{1,0:T(8,128)(2,1)}, u32[]{:S(2)}, u32[]{:S(2)}) %collective-permute-start.7) | collective-permute-done | bytes 344096 | tf_op jit(solution)/shard_map/ppermute | solution.py:77
  21.4 1.5 collective-permute-start
  24.5 5.3 %collective-permute-done.10 = bf16[24,7168]{1,0:T(8,128)(2,1)S(1)} collective-permute-done((bf16[24,7168]{1,0:T(8,128)(2,1)S(1)}, bf16[24,7168]{1,0:T(8,128)(2,1)S(1)}, u32[]{:S(2)}, u32[]{:S(2)}) %collective-permute-start.10) | collective-permute-done | bytes 344096 | tf_op jit(solution)/shard_map/ppermute | solution.py:77
  29.9 8.1 %collective-permute-done.13 = bf16[24,7168]{1,0:T(8,128)(2,1)S(1)} collective-permute-done((bf16[24,7168]{1,0:T(8,128)(2,1)S(1)}, bf16[24,7168]{1,0:T(8,128)(2,1)S(1)}, u32[]{:S(2)}, u32[]{:S(2)}) %collective-permute-start.13) | collective-permute-done | bytes 344096 | tf_op jit(solution)/shard_map/ppermute | solution.py:77
  38.0 1.5 collective-permute-start.11
  39.5 7.7 %collective-permute-done.8 = bf16[24,7168]{1,0:T(8,128)(2,1)S(1)} collective-permute-done((bf16[24,7168]{1,0:T(8,128)(2,1)}, bf16[24,7168]{1,0:T(8,128)(2,1)S(1)}, u32[]{:S(2)}, u32[]{:S(2)}) %collective-permute-start.8) | collective-permute-done | bytes 344096 | tf_op jit(solution)/shard_map/ppermute | solution.py:13
  47.2 1.5 collective-permute-start.14
  49.7 4.7 %collective-permute-done.11 = bf16[24,7168]{1,0:T(8,128)(2,1)S(1)} collective-permute-done((bf16[24,7168]{1,0:T(8,128)(2,1)S(1)}, bf16[24,7168]{1,0:T(8,128)(2,1)S(1)}, u32[]{:S(2)}, u32[]{:S(2)}) %collective-permute-start.11) | collective-permute-done | bytes 344096 | tf_op jit(solution)/shard_map/ppermute | solution.py:13
  54.6 3.6 %collective-permute-done.14 = bf16[24,7168]{1,0:T(8,128)(2,1)S(1)} collective-permute-done((bf16[24,7168]{1,0:T(8,128)(2,1)S(1)}, bf16[24,7168]{1,0:T(8,128)(2,1)S(1)}, u32[]{:S(2)}, u32[]{:S(2)}) %collective-permute-start.14) | collective-permute-done | bytes 344096 | tf_op jit(solution)/shard_map/ppermute | solution.py:13
  59.1 1.6 collective-permute-start.3
  62.8 1.6 copy-done
  64.4 1.6 fusion.19
  66.4 1.6 fusion.44
  68.5 1.6 convolution_convert_fusion.1
  70.7 2.1 collective-permute-start.16
  72.7 2.0 collective-permute-start.19
  74.7 2.3 collective-permute-done.3
  77.1 1.3 fusion.83
  78.4 39.4 %collective-permute-done.16 = bf16[24,14336]{1,0:T(8,128)(2,1)S(1)} collective-permute-done((bf16[24,14336]{1,0:T(8,128)(2,1)S(1)}, bf16[24,14336]{1,0:T(8,128)(2,1)S(1)}, u32[]{:S(2)}, u32[]{:S(2)}) %collective-permute-start.16) | collective-permute-done | bytes 688160 | tf_op jit(solution)/shard_map/ppermute | solution.py:77
  117.8 1.5 collective-permute-start.17
  119.5 14.0 %collective-permute-done.19 = bf16[24,14336]{1,0:T(8,128)(2,1)S(1)} collective-permute-done((bf16[24,14336]{1,0:T(8,128)(2,1)S(1)}, bf16[24,14336]{1,0:T(8,128)(2,1)S(1)}, u32[]{:S(2)}, u32[]{:S(2)}) %collective-permute-start.19) | collective-permute-done | bytes 688160 | tf_op jit(solution)/shard_map/ppermute | solution.py:77
  133.5 1.5 collective-permute-start.20
  135.0 1.3 fusion.82
  136.3 14.6 %collective-permute-done.20 = bf16[24,14336]{1,0:T(8,128)(2,1)S(1)} collective-permute-done((bf16[24,14336]{1,0:T(8,128)(2,1)S(1)}, bf16[24,14336]{1,0:T(8,128)(2,1)S(1)}, u32[]{:S(2)}, u32[]{:S(2)}) %collective-permute-start.20) | collective-permute-done | bytes 688160 | tf_op jit(solution)/shard_map/ppermute | solution.py:13
  150.9 1.3 fusion.81
  152.5 1.5 copy-done.4
  154.0 2.8 fusion.79
  156.9 1.6 collective-permute-start.23
  158.9 1.5 collective-permute-start.25
  161.0 1.6 maximum_bitcast_fusion.2
  162.6 1.6 maximum_bitcast_fusion.3
  164.2 1.5 pad_maximum_fusion
  165.7 2.1 collective-permute-done.23
  167.8 7.4 %collective-permute-done.24 = bf16[24,7168]{1,0:T(8,128)(2,1)S(1)} collective-permute-done((bf16[24,7168]{1,0:T(8,128)(2,1)S(1)}, bf16[24,7168]{1,0:T(8,128)(2,1)S(1)}, u32[]{:S(2)}, u32[]{:S(2)}) %collective-permute-start.24) | collective-permute-done | bytes 344096 | tf_op jit(solution)/shard_map/ppermute | solution.py:13
  175.1 7.4 %collective-permute-done.25 = bf16[24,7168]{1,0:T(8,128)(2,1)S(1)} collective-permute-done((bf16[24,7168]{1,0:T(8,128)(2,1)S(1)}, bf16[24,7168]{1,0:T(8,128)(2,1)S(1)}, u32[]{:S(2)}, u32[]{:S(2)}) %collective-permute-start.25) | collective-permute-done | bytes 344096 | tf_op jit(solution)/shard_map/ppermute | solution.py:13
  182.5 7.0 %collective-permute-done.26 = bf16[24,7168]{1,0:T(8,128)(2,1)S(1)} collective-permute-done((bf16[24,7168]{1,0:T(8,128)(2,1)S(1)}, bf16[24,7168]{1,0:T(8,128)(2,1)S(1)}, u32[]{:S(2)}, u32[]{:S(2)}) %collective-permute-start.26) | collective-permute-done | bytes 344096 | tf_op jit(solution)/shard_map/ppermute | solution.py:13
  189.5 1.2 fusion.59
  190.7 1.9 copy.35
  192.7 1.7 fusion.4
  194.4 1.6 fusion.6
  196.1 1.6 fusion.39
  197.7 1.6 fusion.16
  199.3 3.9 %add_convert_fusion = bf16[384,7168]{1,0:T(8,128)(2,1)S(1)} fusion(f32[384,7168]{1,0:T(8,128)S(1)} %fusion.16, bf16[1,7168,256]{2,1,0:T(8,128)(2,1)} %param.18, f32[384,256]{1,0:T(8,128)S(1)} %fusion.4, f32[384,256]{1,0:T(8,128)} %copy-done.8), kind=kOutput, calls=%fused_computation.2 | convolution fusion | flops 1415380992 | bytes 20971520 | tf_op jit(solution)/shard_map/dot_general | solution.py:64
  203.7 5.1 %collective-permute-done.31 = bf16[2,4,24,7168]{3,2,1,0:T(8,128)(2,1)S(1)} collective-permute-done((bf16[2,4,24,7168]{3,2,1,0:T(8,128)(2,1)S(1)}, bf16[2,4,24,7168]{3,2,1,0:T(8,128)(2,1)S(1)}, u32[]{:S(2)}, u32[]{:S(2)}) %collective-permute-start.31) | collective-permute-done | bytes 2752544 | tf_op jit(solution)/shard_map/ppermute | solution.py:13
  210.0 1.6 collective-permute-start.32
  212.0 1.5 collective-permute-start.35
  214.1 1.5 collective-permute-start.27
  215.5 5.4 %collective-permute-done.32 = bf16[24,7168]{1,0:T(8,128)(2,1)S(1)} collective-permute-done((bf16[24,7168]{1,0:T(8,128)(2,1)S(1)}, bf16[24,7168]{1,0:T(8,128)(2,1)S(1)}, u32[]{:S(2)}, u32[]{:S(2)}) %collective-permute-start.32) | collective-permute-done | bytes 344096 | tf_op jit(solution)/shard_map/ppermute | solution.py:13
  220.9 1.8 collective-permute-start.28
  222.7 5.6 %collective-permute-done.33 = bf16[24,7168]{1,0:T(8,128)(2,1)S(1)} collective-permute-done((bf16[24,7168]{1,0:T(8,128)(2,1)S(1)}, bf16[24,7168]{1,0:T(8,128)(2,1)S(1)}, u32[]{:S(2)}, u32[]{:S(2)}) %collective-permute-start.33) | collective-permute-done | bytes 344096 | tf_op jit(solution)/shard_map/ppermute | solution.py:13
  229.2 6.5 %collective-permute-done.35 = bf16[24,7168]{1,0:T(8,128)(2,1)S(1)} collective-permute-done((bf16[24,7168]{1,0:T(8,128)(2,1)S(1)}, bf16[24,7168]{1,0:T(8,128)(2,1)S(1)}, u32[]{:S(2)}, u32[]{:S(2)}) %collective-permute-start.35) | collective-permute-done | bytes 344096 | tf_op jit(solution)/shard_map/ppermute | solution.py:13
  235.7 6.6 %collective-permute-done.37 = bf16[24,7168]{1,0:T(8,128)(2,1)S(1)} collective-permute-done((bf16[24,7168]{1,0:T(8,128)(2,1)S(1)}, bf16[24,7168]{1,0:T(8,128)(2,1)S(1)}, u32[]{:S(2)}, u32[]{:S(2)}) %collective-permute-start.37) | collective-permute-done | bytes 344096 | tf_op jit(solution)/shard_map/ppermute | solution.py:13
  242.5 1.5 collective-permute-start.34
  246.1 21.7 %collective-permute-done.29 = bf16[24,7168]{1,0:T(8,128)(2,1)S(1)} collective-permute-done((bf16[24,7168]{1,0:T(8,128)(2,1)S(1)}, bf16[24,7168]{1,0:T(8,128)(2,1)S(1)}, u32[]{:S(2)}, u32[]{:S(2)}) %collective-permute-start.29) | collective-permute-done | bytes 344096 | tf_op jit(solution)/shard_map/ppermute | solution.py:97
  268.6 1.3 collective-permute-start.30
  269.9 3.9 %collective-permute-done.36 = bf16[24,7168]{1,0:T(8,128)(2,1)S(1)} collective-permute-done((bf16[24,7168]{1,0:T(8,128)(2,1)S(1)}, bf16[24,7168]{1,0:T(8,128)(2,1)S(1)}, u32[]{:S(2)}, u32[]{:S(2)}) %collective-permute-start.36) | collective-permute-done | bytes 344096 | tf_op jit(solution)/shard_map/ppermute | solution.py:97
  273.8 8.1 %collective-permute-done.38 = bf16[24,7168]{1,0:T(8,128)(2,1)S(1)} collective-permute-done((bf16[24,7168]{1,0:T(8,128)(2,1)S(1)}, bf16[24,7168]{1,0:T(8,128)(2,1)S(1)}, u32[]{:S(2)}, u32[]{:S(2)}) %collective-permute-start.38) | collective-permute-done | bytes 344096 | tf_op jit(solution)/shard_map/ppermute | solution.py:97
  282.8 1.6 collective-permute-start.39
  284.4 10.5 %collective-permute-done.39 = bf16[1,32,7168]{2,1,0:T(8,128)(2,1)S(1)} collective-permute-done((bf16[1,32,7168]{2,1,0:T(8,128)(2,1)S(1)}, bf16[1,32,7168]{2,1,0:T(8,128)(2,1)S(1)}, u32[]{:S(2)}, u32[]{:S(2)}) %collective-permute-start.39) | collective-permute-done | bytes 458784 | tf_op jit(solution)/shard_map/ppermute | solution.py:19
  (107 shorter events, 22.8 us)
Async XLA Ops:
  0.6 9.9 %copy-start.12 = (f32[1,32,2]{1,2,0:T(2,128)S(1)}, f32[1,32,2]{1,2,0:T(2,128)}, u32[]{:S(2)}) copy-start(f32[1,32,2]{1,2,0:T(2,128)} %param.16) | copy-start | bytes 772
  0.6 10.0 %copy-start.7 = (bf16[1,32,7168]{2,1,0:T(8,128)(2,1)S(1)}, bf16[1,32,7168]{2,1,0:T(8,128)(2,1)}, u32[]{:S(2)}) copy-start(bf16[1,32,7168]{2,1,0:T(8,128)(2,1)} %param.13) | copy-start | bytes 1376260
  0.7 10.0 %copy-start.6 = (bf16[1,32,7168]{2,1,0:T(8,128)(2,1)S(1)}, bf16[1,32,7168]{2,1,0:T(8,128)(2,1)}, u32[]{:S(2)}) copy-start(bf16[1,32,7168]{2,1,0:T(8,128)(2,1)} %param.14) | copy-start | bytes 1376260
  4.7 16.7 %collective-permute-start.7 = (bf16[24,7168]{1,0:T(8,128)(2,1)S(1)}, bf16[24,7168]{1,0:T(8,128)(2,1)}, u32[]{:S(2)}, u32[]{:S(2)}) collective-permute-start(bf16[24,7168]{1,0:T(8,128)(2,1)S(1)} %get-tuple-element.62), channel_id=1, source_target_pairs={{0,4},{4,0},{8,12},{12,8},{1,5},{5,1},{9,13},{13,9},{2,6},{6,2},{1... | collective-permute-start | bytes 1032200 | tf_op jit(solution)/shard_map/ppermute | solution.py:77
  6.4 23.5 %collective-permute-start.10 = (bf16[24,7168]{1,0:T(8,128)(2,1)S(1)}, bf16[24,7168]{1,0:T(8,128)(2,1)S(1)}, u32[]{:S(2)}, u32[]{:S(2)}) collective-permute-start(bf16[24,7168]{1,0:T(8,128)(2,1)S(1)} %get-tuple-element.61), channel_id=1, source_target_pairs={{0,8},{4,12},{8,0},{12,4},{1,9},{5,13},{9,1},{13,5},{2,10},{6,14},... | collective-permute-start | bytes 1032200 | tf_op jit(solution)/shard_map/ppermute | solution.py:77
  6.7 31.3 %collective-permute-start.13 = (bf16[24,7168]{1,0:T(8,128)(2,1)S(1)}, bf16[24,7168]{1,0:T(8,128)(2,1)S(1)}, u32[]{:S(2)}, u32[]{:S(2)}) collective-permute-start(bf16[24,7168]{1,0:T(8,128)(2,1)S(1)} %get-tuple-element.60), channel_id=1, source_target_pairs={{0,12},{4,8},{8,4},{12,0},{1,13},{5,9},{9,5},{13,1},{2,14},{6,10},... | collective-permute-start | bytes 1032200 | tf_op jit(solution)/shard_map/ppermute | solution.py:77
  8.3 14.7 %collective-permute-start.5 = (bf16[24,7168]{1,0:T(8,128)(2,1)S(1)}, bf16[24,7168]{1,0:T(8,128)(2,1)}, u32[]{:S(2)}, u32[]{:S(2)}) collective-permute-start(bf16[24,7168]{1,0:T(8,128)(2,1)S(1)} %get-tuple-element.63), channel_id=1, source_target_pairs={{0,2},{2,0},{1,3},{3,1},{4,6},{6,4},{5,7},{7,5},{8,10},{10,8},{9,1... | collective-permute-start | bytes 1032200 | tf_op jit(solution)/shard_map/ppermute | solution.py:13
  11.9 47.1 %collective-permute-start.2 = (bf16[24,14336]{1,0:T(8,128)(2,1)S(1)}, bf16[24,14336]{1,0:T(8,128)(2,1)S(1)}, u32[]{:S(2)}, u32[]{:S(2)}) collective-permute-start(bf16[24,14336]{1,0:T(8,128)(2,1)S(1)} %get-tuple-element.49), channel_id=1, source_target_pairs={{0,4},{4,0},{8,12},{12,8},{1,5},{5,1},{9,13},{13,9},{2,6},{6,2},{1... | collective-permute-start | bytes 2064392 | tf_op jit(solution)/shard_map/ppermute | solution.py:77
  21.4 36.8 %collective-permute-start = (bf16[24,14336]{1,0:T(8,128)(2,1)S(1)}, bf16[24,14336]{1,0:T(8,128)(2,1)S(1)}, u32[]{:S(2)}, u32[]{:S(2)}) collective-permute-start(bf16[24,14336]{1,0:T(8,128)(2,1)S(1)} %get-tuple-element.50), channel_id=1, source_target_pairs={{0,2},{2,0},{1,3},{3,1},{4,6},{6,4},{5,7},{7,5},{8,10},{10,8},{9,1... | collective-permute-start | bytes 2064392 | tf_op jit(solution)/shard_map/ppermute | solution.py:13
  22.9 24.2 %collective-permute-start.8 = (bf16[24,7168]{1,0:T(8,128)(2,1)}, bf16[24,7168]{1,0:T(8,128)(2,1)S(1)}, u32[]{:S(2)}, u32[]{:S(2)}) collective-permute-start(bf16[24,7168]{1,0:T(8,128)(2,1)} %collective-permute-done.7), channel_id=1, source_target_pairs={{0,2},{2,0},{1,3},{3,1},{4,6},{6,4},{5,7},{7,5},{8,10},{10,8},{9,1... | collective-permute-start | bytes 1032200 | tf_op jit(solution)/shard_map/ppermute | solution.py:13
  29.9 29.3 %collective-permute-start.6 = (bf16[2,24,7168]{2,1,0:T(8,128)(2,1)S(1)}, bf16[2,24,7168]{2,1,0:T(8,128)(2,1)S(1)}, u32[]{:S(2)}, u32[]{:S(2)}) collective-permute-start(bf16[2,24,7168]{2,1,0:T(8,128)(2,1)S(1)} %get-tuple-element.65), channel_id=1, source_target_pairs={{0,1},{1,0},{2,3},{3,2},{4,5},{5,4},{6,7},{7,6},{8,9},{9,8},{10,11... | collective-permute-start | bytes 2064392 | tf_op jit(solution)/shard_map/ppermute | solution.py:13
  38.0 16.5 %collective-permute-start.11 = (bf16[24,7168]{1,0:T(8,128)(2,1)S(1)}, bf16[24,7168]{1,0:T(8,128)(2,1)S(1)}, u32[]{:S(2)}, u32[]{:S(2)}) collective-permute-start(bf16[24,7168]{1,0:T(8,128)(2,1)S(1)} %collective-permute-done.10), channel_id=1, source_target_pairs={{0,2},{2,0},{1,3},{3,1},{4,6},{6,4},{5,7},{7,5},{8,10},{10,8},{9,1... | collective-permute-start | bytes 1032200 | tf_op jit(solution)/shard_map/ppermute | solution.py:13
  47.2 11.0 %collective-permute-start.14 = (bf16[24,7168]{1,0:T(8,128)(2,1)S(1)}, bf16[24,7168]{1,0:T(8,128)(2,1)S(1)}, u32[]{:S(2)}, u32[]{:S(2)}) collective-permute-start(bf16[24,7168]{1,0:T(8,128)(2,1)S(1)} %collective-permute-done.13), channel_id=1, source_target_pairs={{0,2},{2,0},{1,3},{3,1},{4,6},{6,4},{5,7},{7,5},{8,10},{10,8},{9,1... | collective-permute-start | bytes 1032200 | tf_op jit(solution)/shard_map/ppermute | solution.py:13
  54.5 6.4 %collective-permute-start.9 = (bf16[2,24,7168]{2,1,0:T(8,128)(2,1)S(1)}, bf16[2,24,7168]{2,1,0:T(8,128)(2,1)S(1)}, u32[]{:S(2)}, u32[]{:S(2)}) collective-permute-start(bf16[2,24,7168]{2,1,0:T(8,128)(2,1)S(1)} %get-tuple-element.67), channel_id=1, source_target_pairs={{0,1},{1,0},{2,3},{3,2},{4,5},{5,4},{6,7},{7,6},{8,9},{9,8},{10,11... | collective-permute-start | bytes 2064392 | tf_op jit(solution)/shard_map/ppermute | solution.py:13
  58.1 2.8 collective-permute-start.12
  58.3 3.0 %collective-permute-start.15 = (bf16[2,24,7168]{2,1,0:T(8,128)(2,1)S(1)}, bf16[2,24,7168]{2,1,0:T(8,128)(2,1)S(1)}, u32[]{:S(2)}, u32[]{:S(2)}) collective-permute-start(bf16[2,24,7168]{2,1,0:T(8,128)(2,1)S(1)} %get-tuple-element.71), channel_id=1, source_target_pairs={{0,1},{1,0},{2,3},{3,2},{4,5},{5,4},{6,7},{7,6},{8,9},{9,8},{10,11... | collective-permute-start | bytes 2064392 | tf_op jit(solution)/shard_map/ppermute | solution.py:13
  59.0 60.2 %collective-permute-start.1 = (bf16[2,24,14336]{2,1,0:T(8,128)(2,1)S(1)}, bf16[2,24,14336]{2,1,0:T(8,128)(2,1)S(1)}, u32[]{:S(2)}, u32[]{:S(2)}) collective-permute-start(bf16[2,24,14336]{2,1,0:T(8,128)(2,1)S(1)} %get-tuple-element.52), channel_id=1, source_target_pairs={{0,1},{1,0},{2,3},{3,2},{4,5},{5,4},{6,7},{7,6},{8,9},{9,8},{10,11... | collective-permute-start | bytes 4128776 | tf_op jit(solution)/shard_map/ppermute | solution.py:13
  59.1 17.9 %collective-permute-start.3 = (bf16[24,14336]{1,0:T(8,128)(2,1)S(1)}, bf16[24,14336]{1,0:T(8,128)(2,1)}, u32[]{:S(2)}, u32[]{:S(2)}) collective-permute-start(bf16[24,14336]{1,0:T(8,128)(2,1)S(1)} %collective-permute-done.2), channel_id=1, source_target_pairs={{0,2},{2,0},{1,3},{3,1},{4,6},{6,4},{5,7},{7,5},{8,10},{10,8},{9,1... | collective-permute-start | bytes 2064392 | tf_op jit(solution)/shard_map/ppermute | solution.py:13
  62.3 2.0 copy-start
  64.4 2.0 copy-start.1
  66.4 2.0 copy-start.2
  70.5 82.0 %collective-permute-start.22 = (bf16[2,4,24,7168]{3,2,1,0:T(8,128)(2,1)S(1)}, bf16[2,4,24,7168]{3,2,1,0:T(8,128)(2,1)S(1)}, u32[]{:S(2)}, u32[]{:S(2)}) collective-permute-start(bf16[2,4,24,7168]{3,2,1,0:T(8,128)(2,1)S(1)} %bitcast.210), channel_id=1, source_target_pairs={{0,1},{1,0},{2,3},{3,2},{4,5},{5,4},{6,7},{7,6},{8,9},{9,8},{10,11... | collective-permute-start | bytes 8257544 | tf_op jit(solution)/shard_map/ppermute | solution.py:13
  70.7 47.1 %collective-permute-start.16 = (bf16[24,14336]{1,0:T(8,128)(2,1)S(1)}, bf16[24,14336]{1,0:T(8,128)(2,1)S(1)}, u32[]{:S(2)}, u32[]{:S(2)}) collective-permute-start(bf16[24,14336]{1,0:T(8,128)(2,1)S(1)} %get-tuple-element.10), channel_id=1, source_target_pairs={{0,8},{4,12},{8,0},{12,4},{1,9},{5,13},{9,1},{13,5},{2,10},{6,14},... | collective-permute-start | bytes 2064392 | tf_op jit(solution)/shard_map/ppermute | solution.py:77
  72.7 60.8 %collective-permute-start.19 = (bf16[24,14336]{1,0:T(8,128)(2,1)S(1)}, bf16[24,14336]{1,0:T(8,128)(2,1)S(1)}, u32[]{:S(2)}, u32[]{:S(2)}) collective-permute-start(bf16[24,14336]{1,0:T(8,128)(2,1)S(1)} %get-tuple-element.11), channel_id=1, source_target_pairs={{0,12},{4,8},{8,4},{12,0},{1,13},{5,9},{9,5},{13,1},{2,14},{6,10},... | collective-permute-start | bytes 2064392 | tf_op jit(solution)/shard_map/ppermute | solution.py:77
  78.3 73.8 %collective-permute-start.4 = (bf16[2,24,14336]{2,1,0:T(8,128)(2,1)S(1)}, bf16[2,24,14336]{2,1,0:T(8,128)(2,1)S(1)}, u32[]{:S(2)}, u32[]{:S(2)}) collective-permute-start(bf16[2,24,14336]{2,1,0:T(8,128)(2,1)S(1)} %get-tuple-element.54), channel_id=1, source_target_pairs={{0,1},{1,0},{2,3},{3,2},{4,5},{5,4},{6,7},{7,6},{8,9},{9,8},{10,11... | collective-permute-start | bytes 4128776 | tf_op jit(solution)/shard_map/ppermute | solution.py:13
  117.8 17.2 %collective-permute-start.17 = (bf16[24,14336]{1,0:T(8,128)(2,1)S(1)}, bf16[24,14336]{1,0:T(8,128)(2,1)S(1)}, u32[]{:S(2)}, u32[]{:S(2)}) collective-permute-start(bf16[24,14336]{1,0:T(8,128)(2,1)S(1)} %collective-permute-done.16), channel_id=1, source_target_pairs={{0,2},{2,0},{1,3},{3,1},{4,6},{6,4},{5,7},{7,5},{8,10},{10,8},{9,1... | collective-permute-start | bytes 2064392 | tf_op jit(solution)/shard_map/ppermute | solution.py:13
  133.5 17.4 %collective-permute-start.20 = (bf16[24,14336]{1,0:T(8,128)(2,1)S(1)}, bf16[24,14336]{1,0:T(8,128)(2,1)S(1)}, u32[]{:S(2)}, u32[]{:S(2)}) collective-permute-start(bf16[24,14336]{1,0:T(8,128)(2,1)S(1)} %collective-permute-done.19), channel_id=1, source_target_pairs={{0,2},{2,0},{1,3},{3,1},{4,6},{6,4},{5,7},{7,5},{8,10},{10,8},{9,1... | collective-permute-start | bytes 2064392 | tf_op jit(solution)/shard_map/ppermute | solution.py:13
  136.3 24.2 %collective-permute-start.18 = (bf16[2,24,14336]{2,1,0:T(8,128)(2,1)}, bf16[2,24,14336]{2,1,0:T(8,128)(2,1)}, u32[]{:S(2)}, u32[]{:S(2)}) collective-permute-start(bf16[2,24,14336]{2,1,0:T(8,128)(2,1)} %get-tuple-element.56), channel_id=1, source_target_pairs={{0,1},{1,0},{2,3},{3,2},{4,5},{5,4},{6,7},{7,6},{8,9},{9,8},{10,11... | collective-permute-start | bytes 4128776 | tf_op jit(solution)/shard_map/ppermute | solution.py:13
  152.2 10.4 %collective-permute-start.21 = (bf16[2,24,14336]{2,1,0:T(8,128)(2,1)}, bf16[2,24,14336]{2,1,0:T(8,128)(2,1)}, u32[]{:S(2)}, u32[]{:S(2)}) collective-permute-start(bf16[2,24,14336]{2,1,0:T(8,128)(2,1)} %get-tuple-element.58), channel_id=1, source_target_pairs={{0,1},{1,0},{2,3},{3,2},{4,5},{5,4},{6,7},{7,6},{8,9},{9,8},{10,11... | collective-permute-start | bytes 4128776 | tf_op jit(solution)/shard_map/ppermute | solution.py:13
  152.5 1.5 copy-start.4
  156.9 10.9 %collective-permute-start.23 = (bf16[24,7168]{1,0:T(8,128)(2,1)S(1)}, bf16[24,7168]{1,0:T(8,128)(2,1)S(1)}, u32[]{:S(2)}, u32[]{:S(2)}) collective-permute-start(bf16[24,7168]{1,0:T(8,128)(2,1)S(1)} %get-tuple-element.45), channel_id=1, source_target_pairs={{0,2},{2,0},{1,3},{3,1},{4,6},{6,4},{5,7},{7,5},{8,10},{10,8},{9,1... | collective-permute-start | bytes 1032200 | tf_op jit(solution)/shard_map/ppermute | solution.py:13
  158.4 16.7 %collective-permute-start.24 = (bf16[24,7168]{1,0:T(8,128)(2,1)S(1)}, bf16[24,7168]{1,0:T(8,128)(2,1)S(1)}, u32[]{:S(2)}, u32[]{:S(2)}) collective-permute-start(bf16[24,7168]{1,0:T(8,128)(2,1)S(1)} %get-tuple-element.44), channel_id=1, source_target_pairs={{0,2},{2,0},{1,3},{3,1},{4,6},{6,4},{5,7},{7,5},{8,10},{10,8},{9,1... | collective-permute-start | bytes 1032200 | tf_op jit(solution)/shard_map/ppermute | solution.py:13
  158.9 23.6 %collective-permute-start.25 = (bf16[24,7168]{1,0:T(8,128)(2,1)S(1)}, bf16[24,7168]{1,0:T(8,128)(2,1)S(1)}, u32[]{:S(2)}, u32[]{:S(2)}) collective-permute-start(bf16[24,7168]{1,0:T(8,128)(2,1)S(1)} %get-tuple-element.43), channel_id=1, source_target_pairs={{0,2},{2,0},{1,3},{3,1},{4,6},{6,4},{5,7},{7,5},{8,10},{10,8},{9,1... | collective-permute-start | bytes 1032200 | tf_op jit(solution)/shard_map/ppermute | solution.py:13
  160.5 29.1 %collective-permute-start.26 = (bf16[24,7168]{1,0:T(8,128)(2,1)S(1)}, bf16[24,7168]{1,0:T(8,128)(2,1)S(1)}, u32[]{:S(2)}, u32[]{:S(2)}) collective-permute-start(bf16[24,7168]{1,0:T(8,128)(2,1)S(1)} %get-tuple-element.42), channel_id=1, source_target_pairs={{0,2},{2,0},{1,3},{3,1},{4,6},{6,4},{5,7},{7,5},{8,10},{10,8},{9,1... | collective-permute-start | bytes 1032200 | tf_op jit(solution)/shard_map/ppermute | solution.py:13
  190.7 2.0 copy-start.3
  196.1 1.6 copy-start.8
  203.6 5.2 %collective-permute-start.31 = (bf16[2,4,24,7168]{3,2,1,0:T(8,128)(2,1)S(1)}, bf16[2,4,24,7168]{3,2,1,0:T(8,128)(2,1)S(1)}, u32[]{:S(2)}, u32[]{:S(2)}) collective-permute-start(bf16[2,4,24,7168]{3,2,1,0:T(8,128)(2,1)S(1)} %bitcast.211), channel_id=1, source_target_pairs={{0,1},{1,0},{2,3},{3,2},{4,5},{5,4},{6,7},{7,6},{8,9},{9,8},{10,11... | collective-permute-start | bytes 8257544 | tf_op jit(solution)/shard_map/ppermute | solution.py:13
  209.8 4.3 %copy-start.11 = (bf16[24,7168]{1,0:T(8,128)(2,1)S(1)}, bf16[24,7168]{1,0:T(8,128)(2,1)}, u32[]{:S(2)}) copy-start(bf16[24,7168]{1,0:T(8,128)(2,1)} %get-tuple-element.14) | copy-start | bytes 1032196
  209.8 11.1 %copy-start.10 = (bf16[24,7168]{1,0:T(8,128)(2,1)S(1)}, bf16[24,7168]{1,0:T(8,128)(2,1)}, u32[]{:S(2)}) copy-start(bf16[24,7168]{1,0:T(8,128)(2,1)} %get-tuple-element.15) | copy-start | bytes 1032196
  209.8 18.5 %copy-start.9 = (bf16[24,7168]{1,0:T(8,128)(2,1)S(1)}, bf16[24,7168]{1,0:T(8,128)(2,1)}, u32[]{:S(2)}) copy-start(bf16[24,7168]{1,0:T(8,128)(2,1)} %get-tuple-element.16) | copy-start | bytes 1032196
  210.0 11.0 %collective-permute-start.32 = (bf16[24,7168]{1,0:T(8,128)(2,1)S(1)}, bf16[24,7168]{1,0:T(8,128)(2,1)S(1)}, u32[]{:S(2)}, u32[]{:S(2)}) collective-permute-start(bf16[24,7168]{1,0:T(8,128)(2,1)S(1)} %get-tuple-element.38), channel_id=1, source_target_pairs={{0,2},{2,0},{1,3},{3,1},{4,6},{6,4},{5,7},{7,5},{8,10},{10,8},{9,1... | collective-permute-start | bytes 1032200 | tf_op jit(solution)/shard_map/ppermute | solution.py:13
  211.5 16.8 %collective-permute-start.33 = (bf16[24,7168]{1,0:T(8,128)(2,1)S(1)}, bf16[24,7168]{1,0:T(8,128)(2,1)S(1)}, u32[]{:S(2)}, u32[]{:S(2)}) collective-permute-start(bf16[24,7168]{1,0:T(8,128)(2,1)S(1)} %get-tuple-element.41), channel_id=1, source_target_pairs={{0,2},{2,0},{1,3},{3,1},{4,6},{6,4},{5,7},{7,5},{8,10},{10,8},{9,1... | collective-permute-start | bytes 1032200 | tf_op jit(solution)/shard_map/ppermute | solution.py:13
  212.0 23.6 %collective-permute-start.35 = (bf16[24,7168]{1,0:T(8,128)(2,1)S(1)}, bf16[24,7168]{1,0:T(8,128)(2,1)S(1)}, u32[]{:S(2)}, u32[]{:S(2)}) collective-permute-start(bf16[24,7168]{1,0:T(8,128)(2,1)S(1)} %get-tuple-element.40), channel_id=1, source_target_pairs={{0,2},{2,0},{1,3},{3,1},{4,6},{6,4},{5,7},{7,5},{8,10},{10,8},{9,1... | collective-permute-start | bytes 1032200 | tf_op jit(solution)/shard_map/ppermute | solution.py:13
  213.6 28.7 %collective-permute-start.37 = (bf16[24,7168]{1,0:T(8,128)(2,1)S(1)}, bf16[24,7168]{1,0:T(8,128)(2,1)S(1)}, u32[]{:S(2)}, u32[]{:S(2)}) collective-permute-start(bf16[24,7168]{1,0:T(8,128)(2,1)S(1)} %get-tuple-element.39), channel_id=1, source_target_pairs={{0,2},{2,0},{1,3},{3,1},{4,6},{6,4},{5,7},{7,5},{8,10},{10,8},{9,1... | collective-permute-start | bytes 1032200 | tf_op jit(solution)/shard_map/ppermute | solution.py:13
  214.1 30.8 %collective-permute-start.27 = (bf16[24,7168]{1,0:T(8,128)(2,1)S(1)}, bf16[24,7168]{1,0:T(8,128)(2,1)S(1)}, u32[]{:S(2)}, u32[]{:S(2)}) collective-permute-start(bf16[24,7168]{1,0:T(8,128)(2,1)S(1)} %copy-done.11), channel_id=1, source_target_pairs={{0,4},{4,0},{8,12},{12,8},{1,5},{5,1},{9,13},{13,9},{2,6},{6,2},{1... | collective-permute-start | bytes 1032200 | tf_op jit(solution)/shard_map/ppermute | solution.py:97
  220.9 25.1 %collective-permute-start.28 = (bf16[24,7168]{1,0:T(8,128)(2,1)S(1)}, bf16[24,7168]{1,0:T(8,128)(2,1)S(1)}, u32[]{:S(2)}, u32[]{:S(2)}) collective-permute-start(bf16[24,7168]{1,0:T(8,128)(2,1)S(1)} %copy-done.10), channel_id=1, source_target_pairs={{0,8},{4,12},{8,0},{12,4},{1,9},{5,13},{9,1},{13,5},{2,10},{6,14},... | collective-permute-start | bytes 1032200 | tf_op jit(solution)/shard_map/ppermute | solution.py:97
  228.3 39.5 %collective-permute-start.29 = (bf16[24,7168]{1,0:T(8,128)(2,1)S(1)}, bf16[24,7168]{1,0:T(8,128)(2,1)S(1)}, u32[]{:S(2)}, u32[]{:S(2)}) collective-permute-start(bf16[24,7168]{1,0:T(8,128)(2,1)S(1)} %copy-done.9), channel_id=1, source_target_pairs={{0,12},{4,8},{8,4},{12,0},{1,13},{5,9},{9,5},{13,1},{2,14},{6,10},... | collective-permute-start | bytes 1032200 | tf_op jit(solution)/shard_map/ppermute | solution.py:97
  242.5 25.5 %copy-start.5 = (bf16[1,32,7168]{2,1,0:T(8,128)(2,1)S(1)}, bf16[1,32,7168]{2,1,0:T(8,128)(2,1)}, u32[]{:S(2)}) copy-start(bf16[1,32,7168]{2,1,0:T(8,128)(2,1)} %param.10) | copy-start | bytes 1376260
  242.5 27.4 %collective-permute-start.34 = (bf16[24,7168]{1,0:T(8,128)(2,1)S(1)}, bf16[24,7168]{1,0:T(8,128)(2,1)S(1)}, u32[]{:S(2)}, u32[]{:S(2)}) collective-permute-start(bf16[24,7168]{1,0:T(8,128)(2,1)S(1)} %get-tuple-element.24), channel_id=1, source_target_pairs={{0,4},{4,0},{8,12},{12,8},{1,5},{5,1},{9,13},{13,9},{2,6},{6,2},{1... | collective-permute-start | bytes 1032200 | tf_op jit(solution)/shard_map/ppermute | solution.py:97
  244.0 29.8 %collective-permute-start.36 = (bf16[24,7168]{1,0:T(8,128)(2,1)S(1)}, bf16[24,7168]{1,0:T(8,128)(2,1)S(1)}, u32[]{:S(2)}, u32[]{:S(2)}) collective-permute-start(bf16[24,7168]{1,0:T(8,128)(2,1)S(1)} %get-tuple-element.23), channel_id=1, source_target_pairs={{0,8},{4,12},{8,0},{12,4},{1,9},{5,13},{9,1},{13,5},{2,10},{6,14},... | collective-permute-start | bytes 1032200 | tf_op jit(solution)/shard_map/ppermute | solution.py:97
  244.9 37.0 %collective-permute-start.38 = (bf16[24,7168]{1,0:T(8,128)(2,1)S(1)}, bf16[24,7168]{1,0:T(8,128)(2,1)S(1)}, u32[]{:S(2)}, u32[]{:S(2)}) collective-permute-start(bf16[24,7168]{1,0:T(8,128)(2,1)S(1)} %get-tuple-element.25), channel_id=1, source_target_pairs={{0,12},{4,8},{8,4},{12,0},{1,13},{5,9},{9,5},{13,1},{2,14},{6,10},... | collective-permute-start | bytes 1032200 | tf_op jit(solution)/shard_map/ppermute | solution.py:97
  268.6 15.7 %collective-permute-start.30 = (bf16[1,32,7168]{2,1,0:T(8,128)(2,1)S(1)}, bf16[1,32,7168]{2,1,0:T(8,128)(2,1)S(1)}, u32[]{:S(2)}, u32[]{:S(2)}) collective-permute-start(bf16[1,32,7168]{2,1,0:T(8,128)(2,1)S(1)} %fusion.3), channel_id=1, source_target_pairs={{0,16},{16,0},{1,17},{17,1},{2,18},{18,2},{3,19},{19,3},{4,20},{20... | collective-permute-start | bytes 1376264 | tf_op jit(solution)/shard_map/ppermute | solution.py:19
  282.8 12.1 %collective-permute-start.39 = (bf16[1,32,7168]{2,1,0:T(8,128)(2,1)S(1)}, bf16[1,32,7168]{2,1,0:T(8,128)(2,1)S(1)}, u32[]{:S(2)}, u32[]{:S(2)}) collective-permute-start(bf16[1,32,7168]{2,1,0:T(8,128)(2,1)S(1)} %fusion.2), channel_id=1, source_target_pairs={{0,16},{16,0},{1,17},{17,1},{2,18},{18,2},{3,19},{19,3},{4,20},{20... | collective-permute-start | bytes 1376264 | tf_op jit(solution)/shard_map/ppermute | solution.py:19

commit v15 on v13

--- a/solution.py
+++ b/solution.py
@@ -67,16 +67,15 @@
     return part.astype(jnp.bfloat16)
 
 
-def dispatch(slots):
+def z_round(chunk, d):
     count = lax.axis_size("z")
-    pieces = []
-    for d in range(count):
-        if d == 0:
-            received = slots[0]
-        else:
-            received = lax.ppermute(slots[d], "z", [(i, i ^ d) for i in range(count)])
-        pieces.append(jnp.stack([received, swap(received, "x")]))
-    across = jnp.stack(pieces, axis=1)
+    if d == 0:
+        return chunk
+    return lax.ppermute(chunk, "z", [(i, i ^ d) for i in range(count)])
+
+
+def spread(received):
+    across = jnp.stack([received, swap(received, "x")])
     return jnp.stack([across, swap(across, "c")])
 
 
@@ -123,8 +122,14 @@
     f_slots = into_slots(f_select, fwd_input[0]).reshape(experts, capacity, width)
     b_joined = jnp.concatenate([bwd_input[0], bwd_grad[0]], axis=1)
     b_slots = into_slots(b_select, b_joined).reshape(experts, capacity, 2 * width)
-    f_rows = dispatch(f_slots)
-    b_rows = dispatch(b_slots)
+    early = experts // 2
+    f_received = [z_round(f_slots[d], d) for d in range(experts)]
+    f_rows = jnp.stack([spread(r) for r in f_received], axis=2)
+    b_near = [z_round(b_slots[d], d) for d in range(early)]
+    far = tuple(b_slots[d] for d in range(early, experts))
+    far, _ = lax.optimization_barrier((far, tuple(f_received[early:])))
+    b_far = [z_round(chunk, d) for d, chunk in enumerate(far, start=early)]
+    b_rows = jnp.stack([spread(r) for r in b_near + b_far], axis=2)
     f_partial = forward_rows(f_rows.reshape(-1, width), w_gate, w_up, w_down)
     f_totals = reduce_group(f_partial.reshape(2, 2, experts, capacity, width))
     b_rows, f_totals = lax.optimization_barrier((b_rows, f_totals))

time: 294 us -> 278 us (0.946)
  waiting for transfers between devices: 211 us -> 185 us
  starting transfers between devices: 35.1 us -> 41.2 us
  other arithmetic: 15.3 us -> 19.5 us
    ppermute x20 -> x26, waiting for transfers between devices: 120 us -> 97.7 us  [swap(): return lax.ppermute(value, axis, [(0, 1), (1, 0)])]
    ppermute x6, starting transfers between devices: 4.87 us -> 11.6 us  [returned(): out.append(lax.ppermute(totals[d], 'z', [(i, i ^ d) for i in range(count)]))]
    ppermute x6, waiting for transfers between devices: 49.6 us -> 43.8 us  [z_round(): return lax.ppermute(chunk, 'z', [(i, i ^ d) for i in range(count)])]
    another operation x14 -> x20, other arithmetic: 11.2 us -> 15.4 us  [the longest x8 8.09 us: spread(): return jnp.stack([across, swap(across, 'c')])]
    ppermute x6, starting transfers between devices: 8.32 us -> 5.27 us  [z_round(): return lax.ppermute(chunk, 'z', [(i, i ^ d) for i in range(count)])]
    ppermute x20 -> x26, starting transfers between devices: 18.7 us -> 21.2 us  [swap(): return lax.ppermute(value, axis, [(0, 1), (1, 0)])]
    unnamed x32 -> x28, local copies, waits for them, and re-layouts: 6.32 us -> 4.49 us
  transfers between devices with their start and end apart: 34 -> 40, of which waited for: 20 -> 25; matrix products, arithmetic and copies ran while one was open for 7% -> 8% of each run, Pallas kernels for 0% -> 0%
where the time goes in v15:
time: 278 us; the launch traced here: 275 us
  waiting for transfers between devices  185 us (67%)
  starting transfers between devices  41.2 us (15%)
  other arithmetic  19.5 us (7%)
  matrix products  18.9 us (7%)
  local copies, waits for them, and re-layouts  9.07 us (3%)
    ppermute x26, waiting for transfers between devices, swap(): return lax.ppermute(value, axis, [(0, 1), (1, 0)])  97.7 us
    ppermute x6, waiting for transfers between devices, z_round(): return lax.ppermute(chunk, 'z', [(i, i ^ d) for i in range(count)])  43.8 us
    ppermute x6, waiting for transfers between devices, returned(): out.append(lax.ppermute(totals[d], 'z', [(i, i ^ d) for i in range(count)]))  32.9 us
    ppermute x26, starting transfers between devices, swap(): return lax.ppermute(value, axis, [(0, 1), (1, 0)])  21.2 us
    ppermute x6, starting transfers between devices, returned(): out.append(lax.ppermute(totals[d], 'z', [(i, i ^ d) for i in range(count)]))  11.6 us
    ppermute x2, waiting for transfers between devices, passed_along(): return lax.ppermute(value, axis, pairs)  10.9 us
    another operation x8, other arithmetic, spread(): return jnp.stack([across, swap(across, 'c')])  8.09 us
  transfers between devices with their start and end apart: 40, of which 25 were waited for; matrix products, arithmetic and copies ran while one was open for 8% of the time, Pallas kernels for 0%

profile of v15, /device:TPU:16, one launch (start us, length us, event | category | flops | bytes accessed | tf_op | source)
XLA Modules:
  0.0 275.1 jit_solution(16702273016376263485)
XLA Ops:
  3.0 1.6 convolution_convert_fusion.2
  4.8 3.0 %collective-permute-start.6 = (bf16[24,7168]{1,0:T(8,128)(2,1)S(1)}, bf16[24,7168]{1,0:T(8,128)(2,1)S(1)}, u32[]{:S(2)}, u32[]{:S(2)}) collective-permute-start(bf16[24,7168]{1,0:T(8,128)(2,1)S(1)} %get-tuple-element.52), channel_id=1, source_target_pairs={{0,12},{4,8},{8,4},{12,0},{1,13},{5,9},{9,5},{13,1},{2,14},{6,10},... | collective-permute-start | bytes 1032200 | tf_op jit(solution)/shard_map/ppermute | solution.py:74
  7.8 1.3 collective-permute-start.15
  9.2 1.5 collective-permute-start.13
  13.5 4.7 %collective-permute-done.13 = bf16[24,7168]{1,0:T(8,128)(2,1)} collective-permute-done((bf16[24,7168]{1,0:T(8,128)(2,1)S(1)}, bf16[24,7168]{1,0:T(8,128)(2,1)}, u32[]{:S(2)}, u32[]{:S(2)}) %collective-permute-start.13) | collective-permute-done | bytes 344096 | tf_op jit(solution)/shard_map/ppermute | solution.py:13
  18.2 1.5 collective-permute-start
  19.7 1.1 fusion.78
  20.8 7.2 %collective-permute-done.5 = bf16[24,7168]{1,0:T(8,128)(2,1)} collective-permute-done((bf16[24,7168]{1,0:T(8,128)(2,1)S(1)}, bf16[24,7168]{1,0:T(8,128)(2,1)}, u32[]{:S(2)}, u32[]{:S(2)}) %collective-permute-start.5) | collective-permute-done | bytes 344096 | tf_op jit(solution)/shard_map/ppermute | solution.py:74
  28.0 9.6 %collective-permute-done.6 = bf16[24,7168]{1,0:T(8,128)(2,1)S(1)} collective-permute-done((bf16[24,7168]{1,0:T(8,128)(2,1)S(1)}, bf16[24,7168]{1,0:T(8,128)(2,1)S(1)}, u32[]{:S(2)}, u32[]{:S(2)}) %collective-permute-start.6) | collective-permute-done | bytes 344096 | tf_op jit(solution)/shard_map/ppermute | solution.py:74
  37.7 1.5 collective-permute-start.18
  39.1 1.3 fusion.84
  40.5 7.5 %collective-permute-done.18 = bf16[24,7168]{1,0:T(8,128)(2,1)S(1)} collective-permute-done((bf16[24,7168]{1,0:T(8,128)(2,1)}, bf16[24,7168]{1,0:T(8,128)(2,1)S(1)}, u32[]{:S(2)}, u32[]{:S(2)}) %collective-permute-start.18) | collective-permute-done | bytes 344096 | tf_op jit(solution)/shard_map/ppermute | solution.py:13
  48.0 1.5 collective-permute-start.20
  49.4 1.1 fusion.76
  50.6 6.7 %collective-permute-done.20 = bf16[24,7168]{1,0:T(8,128)(2,1)S(1)} collective-permute-done((bf16[24,7168]{1,0:T(8,128)(2,1)S(1)}, bf16[24,7168]{1,0:T(8,128)(2,1)S(1)}, u32[]{:S(2)}, u32[]{:S(2)}) %collective-permute-start.20) | collective-permute-done | bytes 344096 | tf_op jit(solution)/shard_map/ppermute | solution.py:13
  57.3 1.5 collective-permute-start.16
  58.9 7.0 %collective-permute-done.16 = bf16[24,7168]{1,0:T(8,128)(2,1)S(1)} collective-permute-done((bf16[24,7168]{1,0:T(8,128)(2,1)S(1)}, bf16[24,7168]{1,0:T(8,128)(2,1)S(1)}, u32[]{:S(2)}, u32[]{:S(2)}) %collective-permute-start.16) | collective-permute-done | bytes 344096 | tf_op jit(solution)/shard_map/ppermute | solution.py:13
  66.7 1.3 collective-permute-done.19
  68.7 14.2 %collective-permute-done.7 = bf16[24,14336]{1,0:T(8,128)(2,1)} collective-permute-done((bf16[24,14336]{1,0:T(8,128)(2,1)S(1)}, bf16[24,14336]{1,0:T(8,128)(2,1)}, u32[]{:S(2)}, u32[]{:S(2)}) %collective-permute-start.7) | collective-permute-done | bytes 688160 | tf_op jit(solution)/shard_map/ppermute | solution.py:74
  83.0 1.5 collective-permute-start.3
  84.4 12.8 %collective-permute-done.10 = bf16[24,14336]{1,0:T(8,128)(2,1)} collective-permute-done((bf16[24,14336]{1,0:T(8,128)(2,1)S(1)}, bf16[24,14336]{1,0:T(8,128)(2,1)}, u32[]{:S(2)}, u32[]{:S(2)}) %collective-permute-start.10) | collective-permute-done | bytes 688160 | tf_op jit(solution)/shard_map/ppermute | solution.py:74
  97.2 1.5 collective-permute-start.8
  100.9 1.6 copy-done
  102.5 1.6 fusion.19
  104.5 1.6 fusion.44
  106.6 1.6 convolution_convert_fusion.1
  108.6 1.5 fusion.83
  110.7 5.2 %collective-permute-done.8 = bf16[24,14336]{1,0:T(8,128)(2,1)} collective-permute-done((bf16[24,14336]{1,0:T(8,128)(2,1)}, bf16[24,14336]{1,0:T(8,128)(2,1)}, u32[]{:S(2)}, u32[]{:S(2)}) %collective-permute-start.8) | collective-permute-done | bytes 688160 | tf_op jit(solution)/shard_map/ppermute | solution.py:13
  115.9 1.5 fusion.82
  117.4 11.8 %collective-permute-done.11 = bf16[24,14336]{1,0:T(8,128)(2,1)} collective-permute-done((bf16[24,14336]{1,0:T(8,128)(2,1)}, bf16[24,14336]{1,0:T(8,128)(2,1)}, u32[]{:S(2)}, u32[]{:S(2)}) %collective-permute-start.11) | collective-permute-done | bytes 688160 | tf_op jit(solution)/shard_map/ppermute | solution.py:13
  129.2 1.5 fusion.81
  130.8 1.6 maximum_bitcast_fusion
  135.3 1.6 collective-permute-start.23
  137.4 1.5 collective-permute-start.25
  139.4 1.5 pad_maximum_fusion
  140.9 5.4 %collective-permute-done.23 = bf16[24,7168]{1,0:T(8,128)(2,1)S(1)} collective-permute-done((bf16[24,7168]{1,0:T(8,128)(2,1)S(1)}, bf16[24,7168]{1,0:T(8,128)(2,1)S(1)}, u32[]{:S(2)}, u32[]{:S(2)}) %collective-permute-start.23) | collective-permute-done | bytes 344096 | tf_op jit(solution)/shard_map/ppermute | solution.py:13
  146.3 7.4 %collective-permute-done.24 = bf16[24,7168]{1,0:T(8,128)(2,1)S(1)} collective-permute-done((bf16[24,7168]{1,0:T(8,128)(2,1)S(1)}, bf16[24,7168]{1,0:T(8,128)(2,1)S(1)}, u32[]{:S(2)}, u32[]{:S(2)}) %collective-permute-start.24) | collective-permute-done | bytes 344096 | tf_op jit(solution)/shard_map/ppermute | solution.py:13
  153.6 7.4 %collective-permute-done.25 = bf16[24,7168]{1,0:T(8,128)(2,1)S(1)} collective-permute-done((bf16[24,7168]{1,0:T(8,128)(2,1)S(1)}, bf16[24,7168]{1,0:T(8,128)(2,1)S(1)}, u32[]{:S(2)}, u32[]{:S(2)}) %collective-permute-start.25) | collective-permute-done | bytes 344096 | tf_op jit(solution)/shard_map/ppermute | solution.py:13
  161.0 6.6 %collective-permute-done.26 = bf16[24,7168]{1,0:T(8,128)(2,1)S(1)} collective-permute-done((bf16[24,7168]{1,0:T(8,128)(2,1)S(1)}, bf16[24,7168]{1,0:T(8,128)(2,1)S(1)}, u32[]{:S(2)}, u32[]{:S(2)}) %collective-permute-start.26) | collective-permute-done | bytes 344096 | tf_op jit(solution)/shard_map/ppermute | solution.py:13
  167.6 1.1 fusion.59
  168.7 1.9 copy.35
  170.7 1.6 fusion.4
  172.3 1.6 fusion.6
  174.4 1.6 fusion.39
  176.0 1.6 fusion.16
  177.6 3.8 %add_convert_fusion = bf16[384,7168]{1,0:T(8,128)(2,1)S(1)} fusion(f32[384,7168]{1,0:T(8,128)S(1)} %fusion.16, bf16[1,7168,256]{2,1,0:T(8,128)(2,1)} %param.18, f32[384,256]{1,0:T(8,128)S(1)} %fusion.4, f32[384,256]{1,0:T(8,128)S(1)} %fusion.6), kind=kOutput, calls=%fused_computation.2 | convolution fusion | flops 1415380992 | bytes 20971520 | tf_op jit(solution)/shard_map/dot_general | solution.py:64
  181.9 5.1 %collective-permute-done.31 = bf16[2,4,24,7168]{3,2,1,0:T(8,128)(2,1)S(1)} collective-permute-done((bf16[2,4,24,7168]{3,2,1,0:T(8,128)(2,1)S(1)}, bf16[2,4,24,7168]{3,2,1,0:T(8,128)(2,1)S(1)}, u32[]{:S(2)}, u32[]{:S(2)}) %collective-permute-start.31) | collective-permute-done | bytes 2752544 | tf_op jit(solution)/shard_map/ppermute | solution.py:13
  188.1 1.6 collective-permute-start.32
  190.2 1.5 collective-permute-start.35
  192.3 1.4 collective-permute-start.27
  193.6 5.5 %collective-permute-done.32 = bf16[24,7168]{1,0:T(8,128)(2,1)S(1)} collective-permute-done((bf16[24,7168]{1,0:T(8,128)(2,1)S(1)}, bf16[24,7168]{1,0:T(8,128)(2,1)S(1)}, u32[]{:S(2)}, u32[]{:S(2)}) %collective-permute-start.32) | collective-permute-done | bytes 344096 | tf_op jit(solution)/shard_map/ppermute | solution.py:13
  199.1 3.5 %collective-permute-start.28 = (bf16[24,7168]{1,0:T(8,128)(2,1)S(1)}, bf16[24,7168]{1,0:T(8,128)(2,1)S(1)}, u32[]{:S(2)}, u32[]{:S(2)}) collective-permute-start(bf16[24,7168]{1,0:T(8,128)(2,1)S(1)} %copy-done.10), channel_id=1, source_target_pairs={{0,8},{4,12},{8,0},{12,4},{1,9},{5,13},{9,1},{13,5},{2,10},{6,14},... | collective-permute-start | bytes 1032200 | tf_op jit(solution)/shard_map/ppermute | solution.py:96
  202.6 3.9 %collective-permute-done.33 = bf16[24,7168]{1,0:T(8,128)(2,1)S(1)} collective-permute-done((bf16[24,7168]{1,0:T(8,128)(2,1)S(1)}, bf16[24,7168]{1,0:T(8,128)(2,1)S(1)}, u32[]{:S(2)}, u32[]{:S(2)}) %collective-permute-start.33) | collective-permute-done | bytes 344096 | tf_op jit(solution)/shard_map/ppermute | solution.py:13
  206.5 2.6 collective-permute-start.29
  209.1 4.8 %collective-permute-done.35 = bf16[24,7168]{1,0:T(8,128)(2,1)S(1)} collective-permute-done((bf16[24,7168]{1,0:T(8,128)(2,1)S(1)}, bf16[24,7168]{1,0:T(8,128)(2,1)S(1)}, u32[]{:S(2)}, u32[]{:S(2)}) %collective-permute-start.35) | collective-permute-done | bytes 344096 | tf_op jit(solution)/shard_map/ppermute | solution.py:13
  213.9 6.6 %collective-permute-done.37 = bf16[24,7168]{1,0:T(8,128)(2,1)S(1)} collective-permute-done((bf16[24,7168]{1,0:T(8,128)(2,1)S(1)}, bf16[24,7168]{1,0:T(8,128)(2,1)S(1)}, u32[]{:S(2)}, u32[]{:S(2)}) %collective-permute-start.37) | collective-permute-done | bytes 344096 | tf_op jit(solution)/shard_map/ppermute | solution.py:13
  220.7 1.4 collective-permute-start.34
  222.2 2.7 collective-permute-start.36
  224.9 22.2 %collective-permute-done.29 = bf16[24,7168]{1,0:T(8,128)(2,1)S(1)} collective-permute-done((bf16[24,7168]{1,0:T(8,128)(2,1)S(1)}, bf16[24,7168]{1,0:T(8,128)(2,1)S(1)}, u32[]{:S(2)}, u32[]{:S(2)}) %collective-permute-start.29) | collective-permute-done | bytes 344096 | tf_op jit(solution)/shard_map/ppermute | solution.py:96
  247.9 1.6 collective-permute-start.30
  249.5 3.4 %collective-permute-done.36 = bf16[24,7168]{1,0:T(8,128)(2,1)S(1)} collective-permute-done((bf16[24,7168]{1,0:T(8,128)(2,1)S(1)}, bf16[24,7168]{1,0:T(8,128)(2,1)S(1)}, u32[]{:S(2)}, u32[]{:S(2)}) %collective-permute-start.36) | collective-permute-done | bytes 344096 | tf_op jit(solution)/shard_map/ppermute | solution.py:96
  252.9 7.3 %collective-permute-done.38 = bf16[24,7168]{1,0:T(8,128)(2,1)S(1)} collective-permute-done((bf16[24,7168]{1,0:T(8,128)(2,1)S(1)}, bf16[24,7168]{1,0:T(8,128)(2,1)S(1)}, u32[]{:S(2)}, u32[]{:S(2)}) %collective-permute-start.38) | collective-permute-done | bytes 344096 | tf_op jit(solution)/shard_map/ppermute | solution.py:96
  261.1 1.6 collective-permute-start.39
  262.7 10.9 %collective-permute-done.39 = bf16[1,32,7168]{2,1,0:T(8,128)(2,1)S(1)} collective-permute-done((bf16[1,32,7168]{2,1,0:T(8,128)(2,1)S(1)}, bf16[1,32,7168]{2,1,0:T(8,128)(2,1)S(1)}, u32[]{:S(2)}, u32[]{:S(2)}) %collective-permute-start.39) | collective-permute-done | bytes 458784 | tf_op jit(solution)/shard_map/ppermute | solution.py:19
  (107 shorter events, 21.8 us)
Async XLA Ops:
  0.6 10.8 %copy-start.12 = (f32[1,32,2]{1,2,0:T(2,128)S(1)}, f32[1,32,2]{1,2,0:T(2,128)}, u32[]{:S(2)}) copy-start(f32[1,32,2]{1,2,0:T(2,128)} %param.16) | copy-start | bytes 772
  0.6 10.9 %copy-start.8 = (bf16[1,32,7168]{2,1,0:T(8,128)(2,1)S(1)}, bf16[1,32,7168]{2,1,0:T(8,128)(2,1)}, u32[]{:S(2)}) copy-start(bf16[1,32,7168]{2,1,0:T(8,128)(2,1)} %param.13) | copy-start | bytes 1376260
  0.7 10.9 %copy-start.6 = (bf16[1,32,7168]{2,1,0:T(8,128)(2,1)S(1)}, bf16[1,32,7168]{2,1,0:T(8,128)(2,1)}, u32[]{:S(2)}) copy-start(bf16[1,32,7168]{2,1,0:T(8,128)(2,1)} %param.14) | copy-start | bytes 1376260
  4.7 23.3 %collective-permute-start.5 = (bf16[24,7168]{1,0:T(8,128)(2,1)S(1)}, bf16[24,7168]{1,0:T(8,128)(2,1)}, u32[]{:S(2)}, u32[]{:S(2)}) collective-permute-start(bf16[24,7168]{1,0:T(8,128)(2,1)S(1)} %get-tuple-element.53), channel_id=1, source_target_pairs={{0,8},{4,12},{8,0},{12,4},{1,9},{5,13},{9,1},{13,5},{2,10},{6,14},... | collective-permute-start | bytes 1032200 | tf_op jit(solution)/shard_map/ppermute | solution.py:74
  4.8 32.9 %collective-permute-start.6 = (bf16[24,7168]{1,0:T(8,128)(2,1)S(1)}, bf16[24,7168]{1,0:T(8,128)(2,1)S(1)}, u32[]{:S(2)}, u32[]{:S(2)}) collective-permute-start(bf16[24,7168]{1,0:T(8,128)(2,1)S(1)} %get-tuple-element.52), channel_id=1, source_target_pairs={{0,12},{4,8},{8,4},{12,0},{1,13},{5,9},{9,5},{13,1},{2,14},{6,10},... | collective-permute-start | bytes 1032200 | tf_op jit(solution)/shard_map/ppermute | solution.py:74
  7.8 42.7 %collective-permute-start.15 = (bf16[24,7168]{1,0:T(8,128)(2,1)S(1)}, bf16[24,7168]{1,0:T(8,128)(2,1)S(1)}, u32[]{:S(2)}, u32[]{:S(2)}) collective-permute-start(bf16[24,7168]{1,0:T(8,128)(2,1)S(1)} %get-tuple-element.50), channel_id=1, source_target_pairs={{0,4},{4,0},{8,12},{12,8},{1,5},{5,1},{9,13},{13,9},{2,6},{6,2},{1... | collective-permute-start | bytes 1032200 | tf_op jit(solution)/shard_map/ppermute | solution.py:74
  9.2 9.1 %collective-permute-start.13 = (bf16[24,7168]{1,0:T(8,128)(2,1)S(1)}, bf16[24,7168]{1,0:T(8,128)(2,1)}, u32[]{:S(2)}, u32[]{:S(2)}) collective-permute-start(bf16[24,7168]{1,0:T(8,128)(2,1)S(1)} %get-tuple-element.51), channel_id=1, source_target_pairs={{0,2},{2,0},{1,3},{3,1},{4,6},{6,4},{5,7},{7,5},{8,10},{10,8},{9,1... | collective-permute-start | bytes 1032200 | tf_op jit(solution)/shard_map/ppermute | solution.py:13
  12.8 55.5 %collective-permute-start.2 = (bf16[24,14336]{1,0:T(8,128)(2,1)S(1)}, bf16[24,14336]{1,0:T(8,128)(2,1)}, u32[]{:S(2)}, u32[]{:S(2)}) collective-permute-start(bf16[24,14336]{1,0:T(8,128)(2,1)S(1)} %get-tuple-element.47), channel_id=1, source_target_pairs={{0,4},{4,0},{8,12},{12,8},{1,5},{5,1},{9,13},{13,9},{2,6},{6,2},{1... | collective-permute-start | bytes 2064392 | tf_op jit(solution)/shard_map/ppermute | solution.py:74
  18.2 19.4 %collective-permute-start = (bf16[24,14336]{1,0:T(8,128)(2,1)S(1)}, bf16[24,14336]{1,0:T(8,128)(2,1)S(1)}, u32[]{:S(2)}, u32[]{:S(2)}) collective-permute-start(bf16[24,14336]{1,0:T(8,128)(2,1)S(1)} %get-tuple-element.48), channel_id=1, source_target_pairs={{0,2},{2,0},{1,3},{3,1},{4,6},{6,4},{5,7},{7,5},{8,10},{10,8},{9,1... | collective-permute-start | bytes 2064392 | tf_op jit(solution)/shard_map/ppermute | solution.py:13
  28.0 37.9 %collective-permute-start.14 = (bf16[2,24,7168]{2,1,0:T(8,128)(2,1)S(1)}, bf16[2,24,7168]{2,1,0:T(8,128)(2,1)S(1)}, u32[]{:S(2)}, u32[]{:S(2)}) collective-permute-start(bf16[2,24,7168]{2,1,0:T(8,128)(2,1)S(1)} %get-tuple-element.63), channel_id=1, source_target_pairs={{0,1},{1,0},{2,3},{3,2},{4,5},{5,4},{6,7},{7,6},{8,9},{9,8},{10,11... | collective-permute-start | bytes 2064392 | tf_op jit(solution)/shard_map/ppermute | solution.py:13
  37.7 45.3 %collective-permute-start.7 = (bf16[24,14336]{1,0:T(8,128)(2,1)S(1)}, bf16[24,14336]{1,0:T(8,128)(2,1)}, u32[]{:S(2)}, u32[]{:S(2)}) collective-permute-start(bf16[24,14336]{1,0:T(8,128)(2,1)S(1)} %get-tuple-element.9), channel_id=1, source_target_pairs={{0,8},{4,12},{8,0},{12,4},{1,9},{5,13},{9,1},{13,5},{2,10},{6,14},... | collective-permute-start | bytes 2064392 | tf_op jit(solution)/shard_map/ppermute | solution.py:74
  37.7 10.3 %collective-permute-start.18 = (bf16[24,7168]{1,0:T(8,128)(2,1)}, bf16[24,7168]{1,0:T(8,128)(2,1)S(1)}, u32[]{:S(2)}, u32[]{:S(2)}) collective-permute-start(bf16[24,7168]{1,0:T(8,128)(2,1)} %collective-permute-done.5), channel_id=1, source_target_pairs={{0,2},{2,0},{1,3},{3,1},{4,6},{6,4},{5,7},{7,5},{8,10},{10,8},{9,1... | collective-permute-start | bytes 1032200 | tf_op jit(solution)/shard_map/ppermute | solution.py:13
  48.0 9.4 %collective-permute-start.20 = (bf16[24,7168]{1,0:T(8,128)(2,1)S(1)}, bf16[24,7168]{1,0:T(8,128)(2,1)S(1)}, u32[]{:S(2)}, u32[]{:S(2)}) collective-permute-start(bf16[24,7168]{1,0:T(8,128)(2,1)S(1)} %collective-permute-done.6), channel_id=1, source_target_pairs={{0,2},{2,0},{1,3},{3,1},{4,6},{6,4},{5,7},{7,5},{8,10},{10,8},{9,1... | collective-permute-start | bytes 1032200 | tf_op jit(solution)/shard_map/ppermute | solution.py:13
  50.5 46.7 %collective-permute-start.10 = (bf16[24,14336]{1,0:T(8,128)(2,1)S(1)}, bf16[24,14336]{1,0:T(8,128)(2,1)}, u32[]{:S(2)}, u32[]{:S(2)}) collective-permute-start(bf16[24,14336]{1,0:T(8,128)(2,1)S(1)} %get-tuple-element.10), channel_id=1, source_target_pairs={{0,12},{4,8},{8,4},{12,0},{1,13},{5,9},{9,5},{13,1},{2,14},{6,10},... | collective-permute-start | bytes 2064392 | tf_op jit(solution)/shard_map/ppermute | solution.py:74
  57.3 8.5 %collective-permute-start.16 = (bf16[24,7168]{1,0:T(8,128)(2,1)S(1)}, bf16[24,7168]{1,0:T(8,128)(2,1)S(1)}, u32[]{:S(2)}, u32[]{:S(2)}) collective-permute-start(bf16[24,7168]{1,0:T(8,128)(2,1)S(1)} %collective-permute-done.15), channel_id=1, source_target_pairs={{0,2},{2,0},{1,3},{3,1},{4,6},{6,4},{5,7},{7,5},{8,10},{10,8},{9,1... | collective-permute-start | bytes 1032200 | tf_op jit(solution)/shard_map/ppermute | solution.py:13
  65.9 2.1 collective-permute-start.19
  66.0 32.7 %collective-permute-start.21 = (bf16[2,24,7168]{2,1,0:T(8,128)(2,1)S(1)}, bf16[2,24,7168]{2,1,0:T(8,128)(2,1)S(1)}, u32[]{:S(2)}, u32[]{:S(2)}) collective-permute-start(bf16[2,24,7168]{2,1,0:T(8,128)(2,1)S(1)} %get-tuple-element.69), channel_id=1, source_target_pairs={{0,1},{1,0},{2,3},{3,2},{4,5},{5,4},{6,7},{7,6},{8,9},{9,8},{10,11... | collective-permute-start | bytes 2064392 | tf_op jit(solution)/shard_map/ppermute | solution.py:13
  68.0 31.4 %collective-permute-start.17 = (bf16[2,24,7168]{2,1,0:T(8,128)(2,1)S(1)}, bf16[2,24,7168]{2,1,0:T(8,128)(2,1)S(1)}, u32[]{:S(2)}, u32[]{:S(2)}) collective-permute-start(bf16[2,24,7168]{2,1,0:T(8,128)(2,1)S(1)} %get-tuple-element.65), channel_id=1, source_target_pairs={{0,1},{1,0},{2,3},{3,2},{4,5},{5,4},{6,7},{7,6},{8,9},{9,8},{10,11... | collective-permute-start | bytes 2064392 | tf_op jit(solution)/shard_map/ppermute | solution.py:13
  68.3 62.5 %collective-permute-start.1 = (bf16[2,24,14336]{2,1,0:T(8,128)(2,1)}, bf16[2,24,14336]{2,1,0:T(8,128)(2,1)}, u32[]{:S(2)}, u32[]{:S(2)}) collective-permute-start(bf16[2,24,14336]{2,1,0:T(8,128)(2,1)} %get-tuple-element.55), channel_id=1, source_target_pairs={{0,1},{1,0},{2,3},{3,2},{4,5},{5,4},{6,7},{7,6},{8,9},{9,8},{10,11... | collective-permute-start | bytes 4128776 | tf_op jit(solution)/shard_map/ppermute | solution.py:13
  83.0 25.7 %collective-permute-start.3 = (bf16[24,14336]{1,0:T(8,128)(2,1)}, bf16[24,14336]{1,0:T(8,128)(2,1)}, u32[]{:S(2)}, u32[]{:S(2)}) collective-permute-start(bf16[24,14336]{1,0:T(8,128)(2,1)} %collective-permute-done.2), channel_id=1, source_target_pairs={{0,2},{2,0},{1,3},{3,1},{4,6},{6,4},{5,7},{7,5},{8,10},{10,8},{9,1... | collective-permute-start | bytes 2064392 | tf_op jit(solution)/shard_map/ppermute | solution.py:13
  97.2 18.7 %collective-permute-start.8 = (bf16[24,14336]{1,0:T(8,128)(2,1)}, bf16[24,14336]{1,0:T(8,128)(2,1)}, u32[]{:S(2)}, u32[]{:S(2)}) collective-permute-start(bf16[24,14336]{1,0:T(8,128)(2,1)} %collective-permute-done.7), channel_id=1, source_target_pairs={{0,2},{2,0},{1,3},{3,1},{4,6},{6,4},{5,7},{7,5},{8,10},{10,8},{9,1... | collective-permute-start | bytes 2064392 | tf_op jit(solution)/shard_map/ppermute | solution.py:13
  98.7 30.5 %collective-permute-start.11 = (bf16[24,14336]{1,0:T(8,128)(2,1)}, bf16[24,14336]{1,0:T(8,128)(2,1)}, u32[]{:S(2)}, u32[]{:S(2)}) collective-permute-start(bf16[24,14336]{1,0:T(8,128)(2,1)} %collective-permute-done.10), channel_id=1, source_target_pairs={{0,2},{2,0},{1,3},{3,1},{4,6},{6,4},{5,7},{7,5},{8,10},{10,8},{9,1... | collective-permute-start | bytes 2064392 | tf_op jit(solution)/shard_map/ppermute | solution.py:13
  100.5 2.0 copy-start
  102.5 2.0 copy-start.1
  104.5 2.0 copy-start.3
  108.5 25.6 %collective-permute-start.22 = (bf16[2,4,24,7168]{3,2,1,0:T(8,128)(2,1)S(1)}, bf16[2,4,24,7168]{3,2,1,0:T(8,128)(2,1)S(1)}, u32[]{:S(2)}, u32[]{:S(2)}) collective-permute-start(bf16[2,4,24,7168]{3,2,1,0:T(8,128)(2,1)S(1)} %bitcast.210), channel_id=1, source_target_pairs={{0,1},{1,0},{2,3},{3,2},{4,5},{5,4},{6,7},{7,6},{8,9},{9,8},{10,11... | collective-permute-start | bytes 8257544 | tf_op jit(solution)/shard_map/ppermute | solution.py:13
  110.1 22.3 %collective-permute-start.4 = (bf16[2,24,14336]{2,1,0:T(8,128)(2,1)S(1)}, bf16[2,24,14336]{2,1,0:T(8,128)(2,1)S(1)}, u32[]{:S(2)}, u32[]{:S(2)}) collective-permute-start(bf16[2,24,14336]{2,1,0:T(8,128)(2,1)S(1)} %get-tuple-element.57), channel_id=1, source_target_pairs={{0,1},{1,0},{2,3},{3,2},{4,5},{5,4},{6,7},{7,6},{8,9},{9,8},{10,11... | collective-permute-start | bytes 4128776 | tf_op jit(solution)/shard_map/ppermute | solution.py:13
  117.4 15.3 %collective-permute-start.9 = (bf16[2,24,14336]{2,1,0:T(8,128)(2,1)S(1)}, bf16[2,24,14336]{2,1,0:T(8,128)(2,1)S(1)}, u32[]{:S(2)}, u32[]{:S(2)}) collective-permute-start(bf16[2,24,14336]{2,1,0:T(8,128)(2,1)S(1)} %get-tuple-element.59), channel_id=1, source_target_pairs={{0,1},{1,0},{2,3},{3,2},{4,5},{5,4},{6,7},{7,6},{8,9},{9,8},{10,11... | collective-permute-start | bytes 4128776 | tf_op jit(solution)/shard_map/ppermute | solution.py:13
  130.7 3.2 %collective-permute-start.12 = (bf16[2,24,14336]{2,1,0:T(8,128)(2,1)S(1)}, bf16[2,24,14336]{2,1,0:T(8,128)(2,1)S(1)}, u32[]{:S(2)}, u32[]{:S(2)}) collective-permute-start(bf16[2,24,14336]{2,1,0:T(8,128)(2,1)S(1)} %get-tuple-element.61), channel_id=1, source_target_pairs={{0,1},{1,0},{2,3},{3,2},{4,5},{5,4},{6,7},{7,6},{8,9},{9,8},{10,11... | collective-permute-start | bytes 4128776 | tf_op jit(solution)/shard_map/ppermute | solution.py:13
  135.3 11.0 %collective-permute-start.23 = (bf16[24,7168]{1,0:T(8,128)(2,1)S(1)}, bf16[24,7168]{1,0:T(8,128)(2,1)S(1)}, u32[]{:S(2)}, u32[]{:S(2)}) collective-permute-start(bf16[24,7168]{1,0:T(8,128)(2,1)S(1)} %get-tuple-element.43), channel_id=1, source_target_pairs={{0,2},{2,0},{1,3},{3,1},{4,6},{6,4},{5,7},{7,5},{8,10},{10,8},{9,1... | collective-permute-start | bytes 1032200 | tf_op jit(solution)/shard_map/ppermute | solution.py:13
  136.9 16.8 %collective-permute-start.24 = (bf16[24,7168]{1,0:T(8,128)(2,1)S(1)}, bf16[24,7168]{1,0:T(8,128)(2,1)S(1)}, u32[]{:S(2)}, u32[]{:S(2)}) collective-permute-start(bf16[24,7168]{1,0:T(8,128)(2,1)S(1)} %get-tuple-element.42), channel_id=1, source_target_pairs={{0,2},{2,0},{1,3},{3,1},{4,6},{6,4},{5,7},{7,5},{8,10},{10,8},{9,1... | collective-permute-start | bytes 1032200 | tf_op jit(solution)/shard_map/ppermute | solution.py:13
  137.4 23.6 %collective-permute-start.25 = (bf16[24,7168]{1,0:T(8,128)(2,1)S(1)}, bf16[24,7168]{1,0:T(8,128)(2,1)S(1)}, u32[]{:S(2)}, u32[]{:S(2)}) collective-permute-start(bf16[24,7168]{1,0:T(8,128)(2,1)S(1)} %get-tuple-element.41), channel_id=1, source_target_pairs={{0,2},{2,0},{1,3},{3,1},{4,6},{6,4},{5,7},{7,5},{8,10},{10,8},{9,1... | collective-permute-start | bytes 1032200 | tf_op jit(solution)/shard_map/ppermute | solution.py:13
  138.9 28.7 %collective-permute-start.26 = (bf16[24,7168]{1,0:T(8,128)(2,1)S(1)}, bf16[24,7168]{1,0:T(8,128)(2,1)S(1)}, u32[]{:S(2)}, u32[]{:S(2)}) collective-permute-start(bf16[24,7168]{1,0:T(8,128)(2,1)S(1)} %get-tuple-element.40), channel_id=1, source_target_pairs={{0,2},{2,0},{1,3},{3,1},{4,6},{6,4},{5,7},{7,5},{8,10},{10,8},{9,1... | collective-permute-start | bytes 1032200 | tf_op jit(solution)/shard_map/ppermute | solution.py:13
  168.7 2.0 copy-start.4
  172.3 2.0 copy-start.2
  181.8 5.2 %collective-permute-start.31 = (bf16[2,4,24,7168]{3,2,1,0:T(8,128)(2,1)S(1)}, bf16[2,4,24,7168]{3,2,1,0:T(8,128)(2,1)S(1)}, u32[]{:S(2)}, u32[]{:S(2)}) collective-permute-start(bf16[2,4,24,7168]{3,2,1,0:T(8,128)(2,1)S(1)} %bitcast.211), channel_id=1, source_target_pairs={{0,1},{1,0},{2,3},{3,2},{4,5},{5,4},{6,7},{7,6},{8,9},{9,8},{10,11... | collective-permute-start | bytes 8257544 | tf_op jit(solution)/shard_map/ppermute | solution.py:13
  188.0 4.3 %copy-start.11 = (bf16[24,7168]{1,0:T(8,128)(2,1)S(1)}, bf16[24,7168]{1,0:T(8,128)(2,1)}, u32[]{:S(2)}) copy-start(bf16[24,7168]{1,0:T(8,128)(2,1)} %get-tuple-element.12) | copy-start | bytes 1032196
  188.0 11.1 %copy-start.10 = (bf16[24,7168]{1,0:T(8,128)(2,1)S(1)}, bf16[24,7168]{1,0:T(8,128)(2,1)}, u32[]{:S(2)}) copy-start(bf16[24,7168]{1,0:T(8,128)(2,1)} %get-tuple-element.13) | copy-start | bytes 1032196
  188.0 18.5 %copy-start.9 = (bf16[24,7168]{1,0:T(8,128)(2,1)S(1)}, bf16[24,7168]{1,0:T(8,128)(2,1)}, u32[]{:S(2)}) copy-start(bf16[24,7168]{1,0:T(8,128)(2,1)} %get-tuple-element.14) | copy-start | bytes 1032196
  188.1 11.0 %collective-permute-start.32 = (bf16[24,7168]{1,0:T(8,128)(2,1)S(1)}, bf16[24,7168]{1,0:T(8,128)(2,1)S(1)}, u32[]{:S(2)}, u32[]{:S(2)}) collective-permute-start(bf16[24,7168]{1,0:T(8,128)(2,1)S(1)} %get-tuple-element.36), channel_id=1, source_target_pairs={{0,2},{2,0},{1,3},{3,1},{4,6},{6,4},{5,7},{7,5},{8,10},{10,8},{9,1... | collective-permute-start | bytes 1032200 | tf_op jit(solution)/shard_map/ppermute | solution.py:13
  189.7 16.8 %collective-permute-start.33 = (bf16[24,7168]{1,0:T(8,128)(2,1)S(1)}, bf16[24,7168]{1,0:T(8,128)(2,1)S(1)}, u32[]{:S(2)}, u32[]{:S(2)}) collective-permute-start(bf16[24,7168]{1,0:T(8,128)(2,1)S(1)} %get-tuple-element.39), channel_id=1, source_target_pairs={{0,2},{2,0},{1,3},{3,1},{4,6},{6,4},{5,7},{7,5},{8,10},{10,8},{9,1... | collective-permute-start | bytes 1032200 | tf_op jit(solution)/shard_map/ppermute | solution.py:13
  190.2 23.6 %collective-permute-start.35 = (bf16[24,7168]{1,0:T(8,128)(2,1)S(1)}, bf16[24,7168]{1,0:T(8,128)(2,1)S(1)}, u32[]{:S(2)}, u32[]{:S(2)}) collective-permute-start(bf16[24,7168]{1,0:T(8,128)(2,1)S(1)} %get-tuple-element.38), channel_id=1, source_target_pairs={{0,2},{2,0},{1,3},{3,1},{4,6},{6,4},{5,7},{7,5},{8,10},{10,8},{9,1... | collective-permute-start | bytes 1032200 | tf_op jit(solution)/shard_map/ppermute | solution.py:13
  191.8 28.7 %collective-permute-start.37 = (bf16[24,7168]{1,0:T(8,128)(2,1)S(1)}, bf16[24,7168]{1,0:T(8,128)(2,1)S(1)}, u32[]{:S(2)}, u32[]{:S(2)}) collective-permute-start(bf16[24,7168]{1,0:T(8,128)(2,1)S(1)} %get-tuple-element.37), channel_id=1, source_target_pairs={{0,2},{2,0},{1,3},{3,1},{4,6},{6,4},{5,7},{7,5},{8,10},{10,8},{9,1... | collective-permute-start | bytes 1032200 | tf_op jit(solution)/shard_map/ppermute | solution.py:13
  192.3 32.6 %collective-permute-start.27 = (bf16[24,7168]{1,0:T(8,128)(2,1)S(1)}, bf16[24,7168]{1,0:T(8,128)(2,1)S(1)}, u32[]{:S(2)}, u32[]{:S(2)}) collective-permute-start(bf16[24,7168]{1,0:T(8,128)(2,1)S(1)} %copy-done.11), channel_id=1, source_target_pairs={{0,4},{4,0},{8,12},{12,8},{1,5},{5,1},{9,13},{13,9},{2,6},{6,2},{1... | collective-permute-start | bytes 1032200 | tf_op jit(solution)/shard_map/ppermute | solution.py:96
  199.1 25.8 %collective-permute-start.28 = (bf16[24,7168]{1,0:T(8,128)(2,1)S(1)}, bf16[24,7168]{1,0:T(8,128)(2,1)S(1)}, u32[]{:S(2)}, u32[]{:S(2)}) collective-permute-start(bf16[24,7168]{1,0:T(8,128)(2,1)S(1)} %copy-done.10), channel_id=1, source_target_pairs={{0,8},{4,12},{8,0},{12,4},{1,9},{5,13},{9,1},{13,5},{2,10},{6,14},... | collective-permute-start | bytes 1032200 | tf_op jit(solution)/shard_map/ppermute | solution.py:96
  206.5 40.6 %collective-permute-start.29 = (bf16[24,7168]{1,0:T(8,128)(2,1)S(1)}, bf16[24,7168]{1,0:T(8,128)(2,1)S(1)}, u32[]{:S(2)}, u32[]{:S(2)}) collective-permute-start(bf16[24,7168]{1,0:T(8,128)(2,1)S(1)} %copy-done.9), channel_id=1, source_target_pairs={{0,12},{4,8},{8,4},{12,0},{1,13},{5,9},{9,5},{13,1},{2,14},{6,10},... | collective-permute-start | bytes 1032200 | tf_op jit(solution)/shard_map/ppermute | solution.py:96
  220.7 26.5 %copy-start.5 = (bf16[1,32,7168]{2,1,0:T(8,128)(2,1)S(1)}, bf16[1,32,7168]{2,1,0:T(8,128)(2,1)}, u32[]{:S(2)}) copy-start(bf16[1,32,7168]{2,1,0:T(8,128)(2,1)} %param.10) | copy-start | bytes 1376260
  220.7 28.8 %collective-permute-start.34 = (bf16[24,7168]{1,0:T(8,128)(2,1)S(1)}, bf16[24,7168]{1,0:T(8,128)(2,1)S(1)}, u32[]{:S(2)}, u32[]{:S(2)}) collective-permute-start(bf16[24,7168]{1,0:T(8,128)(2,1)S(1)} %get-tuple-element.22), channel_id=1, source_target_pairs={{0,4},{4,0},{8,12},{12,8},{1,5},{5,1},{9,13},{13,9},{2,6},{6,2},{1... | collective-permute-start | bytes 1032200 | tf_op jit(solution)/shard_map/ppermute | solution.py:96
  222.2 30.8 %collective-permute-start.36 = (bf16[24,7168]{1,0:T(8,128)(2,1)S(1)}, bf16[24,7168]{1,0:T(8,128)(2,1)S(1)}, u32[]{:S(2)}, u32[]{:S(2)}) collective-permute-start(bf16[24,7168]{1,0:T(8,128)(2,1)S(1)} %get-tuple-element.21), channel_id=1, source_target_pairs={{0,8},{4,12},{8,0},{12,4},{1,9},{5,13},{9,1},{13,5},{2,10},{6,14},... | collective-permute-start | bytes 1032200 | tf_op jit(solution)/shard_map/ppermute | solution.py:96
  224.9 35.3 %collective-permute-start.38 = (bf16[24,7168]{1,0:T(8,128)(2,1)S(1)}, bf16[24,7168]{1,0:T(8,128)(2,1)S(1)}, u32[]{:S(2)}, u32[]{:S(2)}) collective-permute-start(bf16[24,7168]{1,0:T(8,128)(2,1)S(1)} %get-tuple-element.23), channel_id=1, source_target_pairs={{0,12},{4,8},{8,4},{12,0},{1,13},{5,9},{9,5},{13,1},{2,14},{6,10},... | collective-permute-start | bytes 1032200 | tf_op jit(solution)/shard_map/ppermute | solution.py:96
  247.2 13.2 %copy-start.7 = (bf16[1,32,7168]{2,1,0:T(8,128)(2,1)S(1)}, bf16[1,32,7168]{2,1,0:T(8,128)(2,1)}, u32[]{:S(2)}) copy-start(bf16[1,32,7168]{2,1,0:T(8,128)(2,1)} %param.14) | copy-start | bytes 1376260
  247.9 14.7 %collective-permute-start.30 = (bf16[1,32,7168]{2,1,0:T(8,128)(2,1)S(1)}, bf16[1,32,7168]{2,1,0:T(8,128)(2,1)S(1)}, u32[]{:S(2)}, u32[]{:S(2)}) collective-permute-start(bf16[1,32,7168]{2,1,0:T(8,128)(2,1)S(1)} %fusion.3), channel_id=1, source_target_pairs={{0,16},{16,0},{1,17},{17,1},{2,18},{18,2},{3,19},{19,3},{4,20},{20... | collective-permute-start | bytes 1376264 | tf_op jit(solution)/shard_map/ppermute | solution.py:19
  261.1 12.5 %collective-permute-start.39 = (bf16[1,32,7168]{2,1,0:T(8,128)(2,1)S(1)}, bf16[1,32,7168]{2,1,0:T(8,128)(2,1)S(1)}, u32[]{:S(2)}, u32[]{:S(2)}) collective-permute-start(bf16[1,32,7168]{2,1,0:T(8,128)(2,1)S(1)} %fusion.2), channel_id=1, source_target_pairs={{0,16},{16,0},{1,17},{17,1},{2,18},{18,2},{3,19},{19,3},{4,20},{20... | collective-permute-start | bytes 1376264 | tf_op jit(solution)/shard_map/ppermute | solution.py:19

commit v16 on v15

--- a/solution.py
+++ b/solution.py
@@ -123,16 +123,13 @@
     b_joined = jnp.concatenate([bwd_input[0], bwd_grad[0]], axis=1)
     b_slots = into_slots(b_select, b_joined).reshape(experts, capacity, 2 * width)
     early = experts // 2
-    f_received = [z_round(f_slots[d], d) for d in range(experts)]
-    f_rows = jnp.stack([spread(r) for r in f_received], axis=2)
-    b_near = [z_round(b_slots[d], d) for d in range(early)]
-    far = tuple(b_slots[d] for d in range(early, experts))
-    far, _ = lax.optimization_barrier((far, tuple(f_received[early:])))
-    b_far = [z_round(chunk, d) for d, chunk in enumerate(far, start=early)]
-    b_rows = jnp.stack([spread(r) for r in b_near + b_far], axis=2)
+    f_rows = jnp.stack([spread(z_round(f_slots[d], d)) for d in range(experts)], axis=2)
+    b_received = [z_round(b_slots[d], d) for d in range(experts)]
+    b_near = [spread(r) for r in b_received[:early]]
     f_partial = forward_rows(f_rows.reshape(-1, width), w_gate, w_up, w_down)
     f_totals = reduce_group(f_partial.reshape(2, 2, experts, capacity, width))
-    b_rows, f_totals = lax.optimization_barrier((b_rows, f_totals))
+    b_far, f_totals = lax.optimization_barrier((tuple(b_received[early:]), f_totals))
+    b_rows = jnp.stack(b_near + [spread(r) for r in b_far], axis=2)
     f_out = returned(f_totals)
     b_partial = backward_rows(b_rows.reshape(-1, 2 * width), w_gate, w_up, w_down)
     b_out = returned(reduce_group(b_partial.reshape(2, 2, experts, capacity, width)))

time: 278 us -> 275 us (0.989)
  starting transfers between devices: 41.2 us -> 52.3 us
  waiting for transfers between devices: 185 us -> 175 us
    ppermute x6, waiting for transfers between devices: 43.8 us -> 21.4 us  [z_round(): return lax.ppermute(chunk, 'z', [(i, i ^ d) for i in range(count)])]
    ppermute x26, waiting for transfers between devices: 97.7 us -> 110 us  [swap(): return lax.ppermute(value, axis, [(0, 1), (1, 0)])]
    ppermute x6, starting transfers between devices: 11.6 us -> 19.1 us  [returned(): out.append(lax.ppermute(totals[d], 'z', [(i, i ^ d) for i in range(count)]))]
    ppermute x6, starting transfers between devices: 5.27 us -> 10.6 us  [z_round(): return lax.ppermute(chunk, 'z', [(i, i ^ d) for i in range(count)])]
  transfers between devices with their start and end apart: 40 -> 40, of which waited for: 25 -> 24; matrix products, arithmetic and copies ran while one was open for 8% -> 8% of each run, Pallas kernels for 0% -> 0%
where the time goes in v16:
time: 275 us
  waiting for transfers between devices  175 us (64%)
  starting transfers between devices  52.3 us (19%)
  matrix products  18.9 us (7%)
  other arithmetic  17.7 us (6%)
  local copies, waits for them, and re-layouts  9.94 us (4%)
    ppermute x26, waiting for transfers between devices, swap(): return lax.ppermute(value, axis, [(0, 1), (1, 0)])  110 us
    ppermute x6, waiting for transfers between devices, returned(): out.append(lax.ppermute(totals[d], 'z', [(i, i ^ d) for i in range(count)]))  32.5 us
    ppermute x6, waiting for transfers between devices, z_round(): return lax.ppermute(chunk, 'z', [(i, i ^ d) for i in range(count)])  21.4 us
    ppermute x26, starting transfers between devices, swap(): return lax.ppermute(value, axis, [(0, 1), (1, 0)])  19.6 us
    ppermute x6, starting transfers between devices, returned(): out.append(lax.ppermute(totals[d], 'z', [(i, i ^ d) for i in range(count)]))  19.1 us
    ppermute x6, starting transfers between devices, z_round(): return lax.ppermute(chunk, 'z', [(i, i ^ d) for i in range(count)])  10.6 us
    ppermute x2, waiting for transfers between devices, passed_along(): return lax.ppermute(value, axis, pairs)  10.4 us
    another operation x8, other arithmetic, spread(): return jnp.stack([across, swap(across, 'c')])  7.66 us
  transfers between devices with their start and end apart: 40, of which 24 were waited for; matrix products, arithmetic and copies ran while one was open for 8% of the time, Pallas kernels for 0%

profile of v16, /device:TPU:16, one launch (start us, length us, event | category | flops | bytes accessed | tf_op | source)
XLA Modules:
  0.0 274.6 jit_solution(3836987371969937851)
XLA Ops:
  3.0 1.6 convolution_convert_fusion.2
  5.2 3.5 %collective-permute-start.7 = (bf16[24,7168]{1,0:T(8,128)(2,1)S(1)}, bf16[24,7168]{1,0:T(8,128)(2,1)S(1)}, u32[]{:S(2)}, u32[]{:S(2)}) collective-permute-start(bf16[24,7168]{1,0:T(8,128)(2,1)S(1)} %get-tuple-element.57), channel_id=1, source_target_pairs={{0,8},{4,12},{8,0},{12,4},{1,9},{5,13},{9,1},{13,5},{2,10},{6,14},... | collective-permute-start | bytes 1032200 | tf_op jit(solution)/shard_map/ppermute | solution.py:74
  8.7 1.5 collective-permute-start.2
  12.0 1.2 slice_bitcast_fusion.17
  13.2 2.0 collective-permute-start.24
  15.2 15.0 %collective-permute-done.4 = bf16[24,7168]{1,0:T(8,128)(2,1)} collective-permute-done((bf16[24,7168]{1,0:T(8,128)(2,1)S(1)}, bf16[24,7168]{1,0:T(8,128)(2,1)}, u32[]{:S(2)}, u32[]{:S(2)}) %collective-permute-start.4) | collective-permute-done | bytes 344096 | tf_op jit(solution)/shard_map/ppermute | solution.py:74
  30.2 1.7 collective-permute-start.22
  32.2 1.1 fusion.78
  33.3 3.0 %collective-permute-start.1 = (bf16[24,14336]{1,0:T(8,128)(2,1)}, bf16[24,14336]{1,0:T(8,128)(2,1)}, u32[]{:S(2)}, u32[]{:S(2)}) collective-permute-start(bf16[24,14336]{1,0:T(8,128)(2,1)} %get-tuple-element.41), channel_id=1, source_target_pairs={{0,12},{4,8},{8,4},{12,0},{1,13},{5,9},{9,5},{13,1},{2,14},{6,10},... | collective-permute-start | bytes 2064392 | tf_op jit(solution)/shard_map/ppermute | solution.py:74
  36.3 17.1 %collective-permute-done.5 = bf16[24,7168]{1,0:T(8,128)(2,1)S(1)} collective-permute-done((bf16[24,7168]{1,0:T(8,128)(2,1)}, bf16[24,7168]{1,0:T(8,128)(2,1)S(1)}, u32[]{:S(2)}, u32[]{:S(2)}) %collective-permute-start.5) | collective-permute-done | bytes 344096 | tf_op jit(solution)/shard_map/ppermute | solution.py:13
  53.3 1.4 collective-permute-start.11
  54.7 1.1 fusion.77
  55.9 5.6 %collective-permute-done.11 = bf16[24,7168]{1,0:T(8,128)(2,1)S(1)} collective-permute-done((bf16[24,7168]{1,0:T(8,128)(2,1)S(1)}, bf16[24,7168]{1,0:T(8,128)(2,1)S(1)}, u32[]{:S(2)}, u32[]{:S(2)}) %collective-permute-start.11) | collective-permute-done | bytes 344096 | tf_op jit(solution)/shard_map/ppermute | solution.py:13
  61.5 1.4 collective-permute-start.8
  62.9 5.8 %collective-permute-done.8 = bf16[24,7168]{1,0:T(8,128)(2,1)S(1)} collective-permute-done((bf16[24,7168]{1,0:T(8,128)(2,1)S(1)}, bf16[24,7168]{1,0:T(8,128)(2,1)S(1)}, u32[]{:S(2)}, u32[]{:S(2)}) %collective-permute-start.8) | collective-permute-done | bytes 344096 | tf_op jit(solution)/shard_map/ppermute | solution.py:13
  69.6 1.2 collective-permute-done.12
  70.9 1.4 collective-permute-start.25
  74.4 1.6 copy-done
  75.9 1.6 fusion.19
  78.0 1.6 fusion.44
  80.0 1.6 convolution_convert_fusion.1
  82.2 2.4 fusion.84
  85.0 3.7 %collective-permute-done.25 = bf16[24,14336]{1,0:T(8,128)(2,1)} collective-permute-done((bf16[24,14336]{1,0:T(8,128)(2,1)}, bf16[24,14336]{1,0:T(8,128)(2,1)}, u32[]{:S(2)}, u32[]{:S(2)}) %collective-permute-start.25) | collective-permute-done | bytes 688160 | tf_op jit(solution)/shard_map/ppermute | solution.py:13
  88.7 1.5 fusion.83
  91.3 1.4 collective-permute-start.17
  93.4 1.4 collective-permute-start.15
  95.7 6.7 %collective-permute-done.17 = bf16[24,7168]{1,0:T(8,128)(2,1)S(1)} collective-permute-done((bf16[24,7168]{1,0:T(8,128)(2,1)S(1)}, bf16[24,7168]{1,0:T(8,128)(2,1)S(1)}, u32[]{:S(2)}, u32[]{:S(2)}) %collective-permute-start.17) | collective-permute-done | bytes 344096 | tf_op jit(solution)/shard_map/ppermute | solution.py:13
  102.4 1.6 collective-permute-start
  103.9 5.8 %collective-permute-done.16 = bf16[24,7168]{1,0:T(8,128)(2,1)S(1)} collective-permute-done((bf16[24,7168]{1,0:T(8,128)(2,1)S(1)}, bf16[24,7168]{1,0:T(8,128)(2,1)S(1)}, u32[]{:S(2)}, u32[]{:S(2)}) %collective-permute-start.16) | collective-permute-done | bytes 344096 | tf_op jit(solution)/shard_map/ppermute | solution.py:13
  109.7 7.4 %collective-permute-done.15 = bf16[24,7168]{1,0:T(8,128)(2,1)S(1)} collective-permute-done((bf16[24,7168]{1,0:T(8,128)(2,1)S(1)}, bf16[24,7168]{1,0:T(8,128)(2,1)S(1)}, u32[]{:S(2)}, u32[]{:S(2)}) %collective-permute-start.15) | collective-permute-done | bytes 344096 | tf_op jit(solution)/shard_map/ppermute | solution.py:13
  117.1 5.7 %collective-permute-done.14 = bf16[24,7168]{1,0:T(8,128)(2,1)S(1)} collective-permute-done((bf16[24,7168]{1,0:T(8,128)(2,1)S(1)}, bf16[24,7168]{1,0:T(8,128)(2,1)S(1)}, u32[]{:S(2)}, u32[]{:S(2)}) %collective-permute-start.14) | collective-permute-done | bytes 344096 | tf_op jit(solution)/shard_map/ppermute | solution.py:13
  122.8 1.1 fusion.59
  123.8 6.4 %collective-permute-done = bf16[24,14336]{1,0:T(8,128)(2,1)S(1)} collective-permute-done((bf16[24,14336]{1,0:T(8,128)(2,1)S(1)}, bf16[24,14336]{1,0:T(8,128)(2,1)S(1)}, u32[]{:S(2)}, u32[]{:S(2)}) %collective-permute-start) | collective-permute-done | bytes 688160 | tf_op jit(solution)/shard_map/ppermute | solution.py:74
  130.2 1.5 collective-permute-start.27
  132.5 16.0 %collective-permute-done.27 = bf16[24,14336]{1,0:T(8,128)(2,1)S(1)} collective-permute-done((bf16[24,14336]{1,0:T(8,128)(2,1)S(1)}, bf16[24,14336]{1,0:T(8,128)(2,1)S(1)}, u32[]{:S(2)}, u32[]{:S(2)}) %collective-permute-start.27) | collective-permute-done | bytes 688160 | tf_op jit(solution)/shard_map/ppermute | solution.py:13
  148.8 11.4 %collective-permute-done.29 = bf16[24,14336]{1,0:T(8,128)(2,1)S(1)} collective-permute-done((bf16[24,14336]{1,0:T(8,128)(2,1)}, bf16[24,14336]{1,0:T(8,128)(2,1)S(1)}, u32[]{:S(2)}, u32[]{:S(2)}) %collective-permute-start.29) | collective-permute-done | bytes 688160 | tf_op jit(solution)/shard_map/ppermute | solution.py:13
  160.2 1.3 fusion.81
  161.8 2.8 %collective-permute-done.30 = bf16[2,24,14336]{2,1,0:T(8,128)(2,1)S(1)} collective-permute-done((bf16[2,24,14336]{2,1,0:T(8,128)(2,1)S(1)}, bf16[2,24,14336]{2,1,0:T(8,128)(2,1)S(1)}, u32[]{:S(2)}, u32[]{:S(2)}) %collective-permute-start.30) | collective-permute-done | bytes 1376288 | tf_op jit(solution)/shard_map/ppermute | solution.py:13
  164.9 1.5 pad_maximum_fusion
  166.4 2.1 copy.35
  168.5 1.6 fusion.6
  170.5 1.6 fusion.4
  172.2 1.6 fusion.39
  173.8 1.6 fusion.16
  175.4 3.8 %add_convert_fusion = bf16[384,7168]{1,0:T(8,128)(2,1)S(1)} fusion(f32[384,7168]{1,0:T(8,128)S(1)} %fusion.16, bf16[1,7168,256]{2,1,0:T(8,128)(2,1)} %param.18, f32[384,256]{1,0:T(8,128)S(1)} %fusion.4, f32[384,256]{1,0:T(8,128)S(1)} %fusion.6), kind=kOutput, calls=%fused_computation.2 | convolution fusion | flops 1415380992 | bytes 20971520 | tf_op jit(solution)/shard_map/dot_general | solution.py:64
  179.8 5.0 %collective-permute-done.31 = bf16[2,4,24,7168]{3,2,1,0:T(8,128)(2,1)S(1)} collective-permute-done((bf16[2,4,24,7168]{3,2,1,0:T(8,128)(2,1)S(1)}, bf16[2,4,24,7168]{3,2,1,0:T(8,128)(2,1)S(1)}, u32[]{:S(2)}, u32[]{:S(2)}) %collective-permute-start.31) | collective-permute-done | bytes 2752544 | tf_op jit(solution)/shard_map/ppermute | solution.py:13
  185.9 1.5 collective-permute-start.32
  188.0 1.5 collective-permute-start.35
  190.0 5.4 %collective-permute-start.18 = (bf16[24,7168]{1,0:T(8,128)(2,1)S(1)}, bf16[24,7168]{1,0:T(8,128)(2,1)S(1)}, u32[]{:S(2)}, u32[]{:S(2)}) collective-permute-start(bf16[24,7168]{1,0:T(8,128)(2,1)S(1)} %copy-done.10), channel_id=1, source_target_pairs={{0,4},{4,0},{8,12},{12,8},{1,5},{5,1},{9,13},{13,9},{2,6},{6,2},{1... | collective-permute-start | bytes 1032200 | tf_op jit(solution)/shard_map/ppermute | solution.py:96
  195.4 1.5 collective-permute-done.32
  196.9 3.4 %collective-permute-start.19 = (bf16[24,7168]{1,0:T(8,128)(2,1)S(1)}, bf16[24,7168]{1,0:T(8,128)(2,1)S(1)}, u32[]{:S(2)}, u32[]{:S(2)}) collective-permute-start(bf16[24,7168]{1,0:T(8,128)(2,1)S(1)} %copy-done.9), channel_id=1, source_target_pairs={{0,8},{4,12},{8,0},{12,4},{1,9},{5,13},{9,1},{13,5},{2,10},{6,14},... | collective-permute-start | bytes 1032200 | tf_op jit(solution)/shard_map/ppermute | solution.py:96
  200.3 4.0 %collective-permute-done.37 = bf16[24,7168]{1,0:T(8,128)(2,1)S(1)} collective-permute-done((bf16[24,7168]{1,0:T(8,128)(2,1)S(1)}, bf16[24,7168]{1,0:T(8,128)(2,1)S(1)}, u32[]{:S(2)}, u32[]{:S(2)}) %collective-permute-start.37) | collective-permute-done | bytes 344096 | tf_op jit(solution)/shard_map/ppermute | solution.py:13
  204.3 3.4 %collective-permute-start.20 = (bf16[24,7168]{1,0:T(8,128)(2,1)S(1)}, bf16[24,7168]{1,0:T(8,128)(2,1)S(1)}, u32[]{:S(2)}, u32[]{:S(2)}) collective-permute-start(bf16[24,7168]{1,0:T(8,128)(2,1)S(1)} %copy-done.8), channel_id=1, source_target_pairs={{0,12},{4,8},{8,4},{12,0},{1,13},{5,9},{9,5},{13,1},{2,14},{6,10},... | collective-permute-start | bytes 1032200 | tf_op jit(solution)/shard_map/ppermute | solution.py:96
  207.7 3.9 %collective-permute-done.35 = bf16[24,7168]{1,0:T(8,128)(2,1)S(1)} collective-permute-done((bf16[24,7168]{1,0:T(8,128)(2,1)S(1)}, bf16[24,7168]{1,0:T(8,128)(2,1)S(1)}, u32[]{:S(2)}, u32[]{:S(2)}) %collective-permute-start.35) | collective-permute-done | bytes 344096 | tf_op jit(solution)/shard_map/ppermute | solution.py:13
  211.6 6.6 %collective-permute-done.33 = bf16[24,7168]{1,0:T(8,128)(2,1)S(1)} collective-permute-done((bf16[24,7168]{1,0:T(8,128)(2,1)S(1)}, bf16[24,7168]{1,0:T(8,128)(2,1)S(1)}, u32[]{:S(2)}, u32[]{:S(2)}) %collective-permute-start.33) | collective-permute-done | bytes 344096 | tf_op jit(solution)/shard_map/ppermute | solution.py:13
  218.5 3.4 %collective-permute-start.36 = (bf16[24,7168]{1,0:T(8,128)(2,1)S(1)}, bf16[24,7168]{1,0:T(8,128)(2,1)S(1)}, u32[]{:S(2)}, u32[]{:S(2)}) collective-permute-start(bf16[24,7168]{1,0:T(8,128)(2,1)S(1)} %get-tuple-element.19), channel_id=1, source_target_pairs={{0,8},{4,12},{8,0},{12,4},{1,9},{5,13},{9,1},{13,5},{2,10},{6,14},... | collective-permute-start | bytes 1032200 | tf_op jit(solution)/shard_map/ppermute | solution.py:96
  222.0 2.1 collective-permute-start.34
  224.0 1.4 collective-permute-start.38
  225.4 20.9 %collective-permute-done.20 = bf16[24,7168]{1,0:T(8,128)(2,1)S(1)} collective-permute-done((bf16[24,7168]{1,0:T(8,128)(2,1)S(1)}, bf16[24,7168]{1,0:T(8,128)(2,1)S(1)}, u32[]{:S(2)}, u32[]{:S(2)}) %collective-permute-start.20) | collective-permute-done | bytes 344096 | tf_op jit(solution)/shard_map/ppermute | solution.py:96
  247.2 1.5 collective-permute-start.21
  248.7 4.0 %collective-permute-done.36 = bf16[24,7168]{1,0:T(8,128)(2,1)S(1)} collective-permute-done((bf16[24,7168]{1,0:T(8,128)(2,1)S(1)}, bf16[24,7168]{1,0:T(8,128)(2,1)S(1)}, u32[]{:S(2)}, u32[]{:S(2)}) %collective-permute-start.36) | collective-permute-done | bytes 344096 | tf_op jit(solution)/shard_map/ppermute | solution.py:96
  252.7 7.6 %collective-permute-done.38 = bf16[24,7168]{1,0:T(8,128)(2,1)S(1)} collective-permute-done((bf16[24,7168]{1,0:T(8,128)(2,1)S(1)}, bf16[24,7168]{1,0:T(8,128)(2,1)S(1)}, u32[]{:S(2)}, u32[]{:S(2)}) %collective-permute-start.38) | collective-permute-done | bytes 344096 | tf_op jit(solution)/shard_map/ppermute | solution.py:96
  261.2 1.5 collective-permute-start.39
  262.7 10.4 %collective-permute-done.39 = bf16[1,32,7168]{2,1,0:T(8,128)(2,1)S(1)} collective-permute-done((bf16[1,32,7168]{2,1,0:T(8,128)(2,1)S(1)}, bf16[1,32,7168]{2,1,0:T(8,128)(2,1)S(1)}, u32[]{:S(2)}, u32[]{:S(2)}) %collective-permute-start.39) | collective-permute-done | bytes 458784 | tf_op jit(solution)/shard_map/ppermute | solution.py:19
  (105 shorter events, 21.2 us)
Async XLA Ops:
  0.6 10.3 %copy-start.11 = (f32[1,32,2]{1,2,0:T(2,128)S(1)}, f32[1,32,2]{1,2,0:T(2,128)}, u32[]{:S(2)}) copy-start(f32[1,32,2]{1,2,0:T(2,128)} %param.16) | copy-start | bytes 772
  0.6 10.4 %copy-start.5 = (bf16[1,32,7168]{2,1,0:T(8,128)(2,1)S(1)}, bf16[1,32,7168]{2,1,0:T(8,128)(2,1)}, u32[]{:S(2)}) copy-start(bf16[1,32,7168]{2,1,0:T(8,128)(2,1)} %param.14) | copy-start | bytes 1376260
  0.7 10.4 %copy-start.7 = (bf16[1,32,7168]{2,1,0:T(8,128)(2,1)S(1)}, bf16[1,32,7168]{2,1,0:T(8,128)(2,1)}, u32[]{:S(2)}) copy-start(bf16[1,32,7168]{2,1,0:T(8,128)(2,1)} %param.13) | copy-start | bytes 1376260
  4.7 28.6 %collective-permute-start.10 = (bf16[24,7168]{1,0:T(8,128)(2,1)S(1)}, bf16[24,7168]{1,0:T(8,128)(2,1)S(1)}, u32[]{:S(2)}, u32[]{:S(2)}) collective-permute-start(bf16[24,7168]{1,0:T(8,128)(2,1)S(1)} %get-tuple-element.56), channel_id=1, source_target_pairs={{0,12},{4,8},{8,4},{12,0},{1,13},{5,9},{9,5},{13,1},{2,14},{6,10},... | collective-permute-start | bytes 1032200 | tf_op jit(solution)/shard_map/ppermute | solution.py:74
  5.2 50.6 %collective-permute-start.7 = (bf16[24,7168]{1,0:T(8,128)(2,1)S(1)}, bf16[24,7168]{1,0:T(8,128)(2,1)S(1)}, u32[]{:S(2)}, u32[]{:S(2)}) collective-permute-start(bf16[24,7168]{1,0:T(8,128)(2,1)S(1)} %get-tuple-element.57), channel_id=1, source_target_pairs={{0,8},{4,12},{8,0},{12,4},{1,9},{5,13},{9,1},{13,5},{2,10},{6,14},... | collective-permute-start | bytes 1032200 | tf_op jit(solution)/shard_map/ppermute | solution.py:74
  8.7 21.5 %collective-permute-start.4 = (bf16[24,7168]{1,0:T(8,128)(2,1)S(1)}, bf16[24,7168]{1,0:T(8,128)(2,1)}, u32[]{:S(2)}, u32[]{:S(2)}) collective-permute-start(bf16[24,7168]{1,0:T(8,128)(2,1)S(1)} %get-tuple-element.58), channel_id=1, source_target_pairs={{0,4},{4,0},{8,12},{12,8},{1,5},{5,1},{9,13},{13,9},{2,6},{6,2},{1... | collective-permute-start | bytes 1032200 | tf_op jit(solution)/shard_map/ppermute | solution.py:74
  8.7 23.2 %collective-permute-start.2 = (bf16[24,7168]{1,0:T(8,128)(2,1)S(1)}, bf16[24,7168]{1,0:T(8,128)(2,1)}, u32[]{:S(2)}, u32[]{:S(2)}) collective-permute-start(bf16[24,7168]{1,0:T(8,128)(2,1)S(1)} %get-tuple-element.59), channel_id=1, source_target_pairs={{0,2},{2,0},{1,3},{3,1},{4,6},{6,4},{5,7},{7,5},{8,10},{10,8},{9,1... | collective-permute-start | bytes 1032200 | tf_op jit(solution)/shard_map/ppermute | solution.py:13
  13.2 56.3 %collective-permute-start.24 = (bf16[24,14336]{1,0:T(8,128)(2,1)S(1)}, bf16[24,14336]{1,0:T(8,128)(2,1)}, u32[]{:S(2)}, u32[]{:S(2)}) collective-permute-start(bf16[24,14336]{1,0:T(8,128)(2,1)S(1)} %get-tuple-element.39), channel_id=1, source_target_pairs={{0,4},{4,0},{8,12},{12,8},{1,5},{5,1},{9,13},{13,9},{2,6},{6,2},{1... | collective-permute-start | bytes 2064392 | tf_op jit(solution)/shard_map/ppermute | solution.py:74
  30.2 52.0 %collective-permute-start.22 = (bf16[24,14336]{1,0:T(8,128)(2,1)S(1)}, bf16[24,14336]{1,0:T(8,128)(2,1)}, u32[]{:S(2)}, u32[]{:S(2)}) collective-permute-start(bf16[24,14336]{1,0:T(8,128)(2,1)S(1)} %get-tuple-element.40), channel_id=1, source_target_pairs={{0,2},{2,0},{1,3},{3,1},{4,6},{6,4},{5,7},{7,5},{8,10},{10,8},{9,1... | collective-permute-start | bytes 2064392 | tf_op jit(solution)/shard_map/ppermute | solution.py:13
  31.9 21.5 %collective-permute-start.5 = (bf16[24,7168]{1,0:T(8,128)(2,1)}, bf16[24,7168]{1,0:T(8,128)(2,1)S(1)}, u32[]{:S(2)}, u32[]{:S(2)}) collective-permute-start(bf16[24,7168]{1,0:T(8,128)(2,1)} %collective-permute-done.4), channel_id=1, source_target_pairs={{0,2},{2,0},{1,3},{3,1},{4,6},{6,4},{5,7},{7,5},{8,10},{10,8},{9,1... | collective-permute-start | bytes 1032200 | tf_op jit(solution)/shard_map/ppermute | solution.py:13
  33.3 90.5 %collective-permute-start.1 = (bf16[24,14336]{1,0:T(8,128)(2,1)}, bf16[24,14336]{1,0:T(8,128)(2,1)}, u32[]{:S(2)}, u32[]{:S(2)}) collective-permute-start(bf16[24,14336]{1,0:T(8,128)(2,1)} %get-tuple-element.41), channel_id=1, source_target_pairs={{0,12},{4,8},{8,4},{12,0},{1,13},{5,9},{9,5},{13,1},{2,14},{6,10},... | collective-permute-start | bytes 2064392 | tf_op jit(solution)/shard_map/ppermute | solution.py:74
  53.3 8.1 %collective-permute-start.11 = (bf16[24,7168]{1,0:T(8,128)(2,1)S(1)}, bf16[24,7168]{1,0:T(8,128)(2,1)S(1)}, u32[]{:S(2)}, u32[]{:S(2)}) collective-permute-start(bf16[24,7168]{1,0:T(8,128)(2,1)S(1)} %collective-permute-done.10), channel_id=1, source_target_pairs={{0,2},{2,0},{1,3},{3,1},{4,6},{6,4},{5,7},{7,5},{8,10},{10,8},{9,1... | collective-permute-start | bytes 1032200 | tf_op jit(solution)/shard_map/ppermute | solution.py:13
  55.8 13.0 %collective-permute-start.3 = (bf16[2,24,7168]{2,1,0:T(8,128)(2,1)S(1)}, bf16[2,24,7168]{2,1,0:T(8,128)(2,1)S(1)}, u32[]{:S(2)}, u32[]{:S(2)}) collective-permute-start(bf16[2,24,7168]{2,1,0:T(8,128)(2,1)S(1)} %get-tuple-element.61), channel_id=1, source_target_pairs={{0,1},{1,0},{2,3},{3,2},{4,5},{5,4},{6,7},{7,6},{8,9},{9,8},{10,11... | collective-permute-start | bytes 2064392 | tf_op jit(solution)/shard_map/ppermute | solution.py:13
  61.5 7.2 %collective-permute-start.8 = (bf16[24,7168]{1,0:T(8,128)(2,1)S(1)}, bf16[24,7168]{1,0:T(8,128)(2,1)S(1)}, u32[]{:S(2)}, u32[]{:S(2)}) collective-permute-start(bf16[24,7168]{1,0:T(8,128)(2,1)S(1)} %collective-permute-done.7), channel_id=1, source_target_pairs={{0,2},{2,0},{1,3},{3,1},{4,6},{6,4},{5,7},{7,5},{8,10},{10,8},{9,1... | collective-permute-start | bytes 1032200 | tf_op jit(solution)/shard_map/ppermute | solution.py:13
  68.7 2.1 collective-permute-start.12
  68.8 3.5 %collective-permute-start.9 = (bf16[2,24,7168]{2,1,0:T(8,128)(2,1)S(1)}, bf16[2,24,7168]{2,1,0:T(8,128)(2,1)S(1)}, u32[]{:S(2)}, u32[]{:S(2)}) collective-permute-start(bf16[2,24,7168]{2,1,0:T(8,128)(2,1)S(1)} %get-tuple-element.65), channel_id=1, source_target_pairs={{0,1},{1,0},{2,3},{3,2},{4,5},{5,4},{6,7},{7,6},{8,9},{9,8},{10,11... | collective-permute-start | bytes 2064392 | tf_op jit(solution)/shard_map/ppermute | solution.py:13
  69.5 3.3 %collective-permute-start.6 = (bf16[2,24,7168]{2,1,0:T(8,128)(2,1)S(1)}, bf16[2,24,7168]{2,1,0:T(8,128)(2,1)S(1)}, u32[]{:S(2)}, u32[]{:S(2)}) collective-permute-start(bf16[2,24,7168]{2,1,0:T(8,128)(2,1)S(1)} %get-tuple-element.63), channel_id=1, source_target_pairs={{0,1},{1,0},{2,3},{3,2},{4,5},{5,4},{6,7},{7,6},{8,9},{9,8},{10,11... | collective-permute-start | bytes 2064392 | tf_op jit(solution)/shard_map/ppermute | solution.py:13
  70.9 17.8 %collective-permute-start.25 = (bf16[24,14336]{1,0:T(8,128)(2,1)}, bf16[24,14336]{1,0:T(8,128)(2,1)}, u32[]{:S(2)}, u32[]{:S(2)}) collective-permute-start(bf16[24,14336]{1,0:T(8,128)(2,1)} %collective-permute-done.24), channel_id=1, source_target_pairs={{0,2},{2,0},{1,3},{3,1},{4,6},{6,4},{5,7},{7,5},{8,10},{10,8},{9,1... | collective-permute-start | bytes 2064392 | tf_op jit(solution)/shard_map/ppermute | solution.py:13
  73.9 2.0 copy-start
  75.9 2.0 copy-start.1
  78.0 2.0 copy-start.2
  82.0 8.1 %collective-permute-start.13 = (bf16[2,4,24,7168]{3,2,1,0:T(8,128)(2,1)S(1)}, bf16[2,4,24,7168]{3,2,1,0:T(8,128)(2,1)S(1)}, u32[]{:S(2)}, u32[]{:S(2)}) collective-permute-start(bf16[2,4,24,7168]{3,2,1,0:T(8,128)(2,1)S(1)} %bitcast.210), channel_id=1, source_target_pairs={{0,1},{1,0},{2,3},{3,2},{4,5},{5,4},{6,7},{7,6},{8,9},{9,8},{10,11... | collective-permute-start | bytes 8257544 | tf_op jit(solution)/shard_map/ppermute | solution.py:13
  84.6 10.1 %collective-permute-start.23 = (bf16[2,24,14336]{2,1,0:T(8,128)(2,1)}, bf16[2,24,14336]{2,1,0:T(8,128)(2,1)S(1)}, u32[]{:S(2)}, u32[]{:S(2)}) collective-permute-start(bf16[2,24,14336]{2,1,0:T(8,128)(2,1)} %get-tuple-element.48), channel_id=1, source_target_pairs={{0,1},{1,0},{2,3},{3,2},{4,5},{5,4},{6,7},{7,6},{8,9},{9,8},{10,11... | collective-permute-start | bytes 4128776 | tf_op jit(solution)/shard_map/ppermute | solution.py:13
  91.3 11.1 %collective-permute-start.17 = (bf16[24,7168]{1,0:T(8,128)(2,1)S(1)}, bf16[24,7168]{1,0:T(8,128)(2,1)S(1)}, u32[]{:S(2)}, u32[]{:S(2)}) collective-permute-start(bf16[24,7168]{1,0:T(8,128)(2,1)S(1)} %get-tuple-element.43), channel_id=1, source_target_pairs={{0,2},{2,0},{1,3},{3,1},{4,6},{6,4},{5,7},{7,5},{8,10},{10,8},{9,1... | collective-permute-start | bytes 1032200 | tf_op jit(solution)/shard_map/ppermute | solution.py:13
  92.7 17.0 %collective-permute-start.16 = (bf16[24,7168]{1,0:T(8,128)(2,1)S(1)}, bf16[24,7168]{1,0:T(8,128)(2,1)S(1)}, u32[]{:S(2)}, u32[]{:S(2)}) collective-permute-start(bf16[24,7168]{1,0:T(8,128)(2,1)S(1)} %get-tuple-element.44), channel_id=1, source_target_pairs={{0,2},{2,0},{1,3},{3,1},{4,6},{6,4},{5,7},{7,5},{8,10},{10,8},{9,1... | collective-permute-start | bytes 1032200 | tf_op jit(solution)/shard_map/ppermute | solution.py:13
  93.4 23.7 %collective-permute-start.15 = (bf16[24,7168]{1,0:T(8,128)(2,1)S(1)}, bf16[24,7168]{1,0:T(8,128)(2,1)S(1)}, u32[]{:S(2)}, u32[]{:S(2)}) collective-permute-start(bf16[24,7168]{1,0:T(8,128)(2,1)S(1)} %get-tuple-element.45), channel_id=1, source_target_pairs={{0,2},{2,0},{1,3},{3,1},{4,6},{6,4},{5,7},{7,5},{8,10},{10,8},{9,1... | collective-permute-start | bytes 1032200 | tf_op jit(solution)/shard_map/ppermute | solution.py:13
  94.8 28.0 %collective-permute-start.14 = (bf16[24,7168]{1,0:T(8,128)(2,1)S(1)}, bf16[24,7168]{1,0:T(8,128)(2,1)S(1)}, u32[]{:S(2)}, u32[]{:S(2)}) collective-permute-start(bf16[24,7168]{1,0:T(8,128)(2,1)S(1)} %get-tuple-element.46), channel_id=1, source_target_pairs={{0,2},{2,0},{1,3},{3,1},{4,6},{6,4},{5,7},{7,5},{8,10},{10,8},{9,1... | collective-permute-start | bytes 1032200 | tf_op jit(solution)/shard_map/ppermute | solution.py:13
  102.4 27.8 %collective-permute-start = (bf16[24,14336]{1,0:T(8,128)(2,1)S(1)}, bf16[24,14336]{1,0:T(8,128)(2,1)S(1)}, u32[]{:S(2)}, u32[]{:S(2)}) collective-permute-start(bf16[24,14336]{1,0:T(8,128)(2,1)S(1)} %get-tuple-element.42), channel_id=1, source_target_pairs={{0,8},{4,12},{8,0},{12,4},{1,9},{5,13},{9,1},{13,5},{2,10},{6,14},... | collective-permute-start | bytes 2064392 | tf_op jit(solution)/shard_map/ppermute | solution.py:74
  109.7 21.9 %collective-permute-start.26 = (bf16[2,24,14336]{2,1,0:T(8,128)(2,1)S(1)}, bf16[2,24,14336]{2,1,0:T(8,128)(2,1)S(1)}, u32[]{:S(2)}, u32[]{:S(2)}) collective-permute-start(bf16[2,24,14336]{2,1,0:T(8,128)(2,1)S(1)} %get-tuple-element.50), channel_id=1, source_target_pairs={{0,1},{1,0},{2,3},{3,2},{4,5},{5,4},{6,7},{7,6},{8,9},{9,8},{10,11... | collective-permute-start | bytes 4128776 | tf_op jit(solution)/shard_map/ppermute | solution.py:13
  130.2 18.4 %collective-permute-start.27 = (bf16[24,14336]{1,0:T(8,128)(2,1)S(1)}, bf16[24,14336]{1,0:T(8,128)(2,1)S(1)}, u32[]{:S(2)}, u32[]{:S(2)}) collective-permute-start(bf16[24,14336]{1,0:T(8,128)(2,1)S(1)} %collective-permute-done), channel_id=1, source_target_pairs={{0,2},{2,0},{1,3},{3,1},{4,6},{6,4},{5,7},{7,5},{8,10},{10,8},{9,1... | collective-permute-start | bytes 2064392 | tf_op jit(solution)/shard_map/ppermute | solution.py:13
  131.9 28.3 %collective-permute-start.29 = (bf16[24,14336]{1,0:T(8,128)(2,1)}, bf16[24,14336]{1,0:T(8,128)(2,1)S(1)}, u32[]{:S(2)}, u32[]{:S(2)}) collective-permute-start(bf16[24,14336]{1,0:T(8,128)(2,1)} %collective-permute-done.1), channel_id=1, source_target_pairs={{0,2},{2,0},{1,3},{3,1},{4,6},{6,4},{5,7},{7,5},{8,10},{10,8},{9,1... | collective-permute-start | bytes 2064392 | tf_op jit(solution)/shard_map/ppermute | solution.py:13
  148.7 12.8 %collective-permute-start.28 = (bf16[2,24,14336]{2,1,0:T(8,128)(2,1)S(1)}, bf16[2,24,14336]{2,1,0:T(8,128)(2,1)S(1)}, u32[]{:S(2)}, u32[]{:S(2)}) collective-permute-start(bf16[2,24,14336]{2,1,0:T(8,128)(2,1)S(1)} %get-tuple-element.52), channel_id=1, source_target_pairs={{0,1},{1,0},{2,3},{3,2},{4,5},{5,4},{6,7},{7,6},{8,9},{9,8},{10,11... | collective-permute-start | bytes 4128776 | tf_op jit(solution)/shard_map/ppermute | solution.py:13
  161.5 3.2 %collective-permute-start.30 = (bf16[2,24,14336]{2,1,0:T(8,128)(2,1)S(1)}, bf16[2,24,14336]{2,1,0:T(8,128)(2,1)S(1)}, u32[]{:S(2)}, u32[]{:S(2)}) collective-permute-start(bf16[2,24,14336]{2,1,0:T(8,128)(2,1)S(1)} %get-tuple-element.54), channel_id=1, source_target_pairs={{0,1},{1,0},{2,3},{3,2},{4,5},{5,4},{6,7},{7,6},{8,9},{9,8},{10,11... | collective-permute-start | bytes 4128776 | tf_op jit(solution)/shard_map/ppermute | solution.py:13
  168.5 2.0 copy-start.3
  179.6 5.2 %collective-permute-start.31 = (bf16[2,4,24,7168]{3,2,1,0:T(8,128)(2,1)S(1)}, bf16[2,4,24,7168]{3,2,1,0:T(8,128)(2,1)S(1)}, u32[]{:S(2)}, u32[]{:S(2)}) collective-permute-start(bf16[2,4,24,7168]{3,2,1,0:T(8,128)(2,1)S(1)} %bitcast.211), channel_id=1, source_target_pairs={{0,1},{1,0},{2,3},{3,2},{4,5},{5,4},{6,7},{7,6},{8,9},{9,8},{10,11... | collective-permute-start | bytes 8257544 | tf_op jit(solution)/shard_map/ppermute | solution.py:13
  185.8 4.3 %copy-start.10 = (bf16[24,7168]{1,0:T(8,128)(2,1)S(1)}, bf16[24,7168]{1,0:T(8,128)(2,1)}, u32[]{:S(2)}) copy-start(bf16[24,7168]{1,0:T(8,128)(2,1)} %get-tuple-element.9) | copy-start | bytes 1032196
  185.8 11.1 %copy-start.9 = (bf16[24,7168]{1,0:T(8,128)(2,1)S(1)}, bf16[24,7168]{1,0:T(8,128)(2,1)}, u32[]{:S(2)}) copy-start(bf16[24,7168]{1,0:T(8,128)(2,1)} %get-tuple-element.10) | copy-start | bytes 1032196
  185.8 18.5 %copy-start.8 = (bf16[24,7168]{1,0:T(8,128)(2,1)S(1)}, bf16[24,7168]{1,0:T(8,128)(2,1)}, u32[]{:S(2)}) copy-start(bf16[24,7168]{1,0:T(8,128)(2,1)} %get-tuple-element.11) | copy-start | bytes 1032196
  185.9 11.0 %collective-permute-start.32 = (bf16[24,7168]{1,0:T(8,128)(2,1)S(1)}, bf16[24,7168]{1,0:T(8,128)(2,1)S(1)}, u32[]{:S(2)}, u32[]{:S(2)}) collective-permute-start(bf16[24,7168]{1,0:T(8,128)(2,1)S(1)} %get-tuple-element.34), channel_id=1, source_target_pairs={{0,2},{2,0},{1,3},{3,1},{4,6},{6,4},{5,7},{7,5},{8,10},{10,8},{9,1... | collective-permute-start | bytes 1032200 | tf_op jit(solution)/shard_map/ppermute | solution.py:13
  187.5 16.8 %collective-permute-start.37 = (bf16[24,7168]{1,0:T(8,128)(2,1)S(1)}, bf16[24,7168]{1,0:T(8,128)(2,1)S(1)}, u32[]{:S(2)}, u32[]{:S(2)}) collective-permute-start(bf16[24,7168]{1,0:T(8,128)(2,1)S(1)} %get-tuple-element.35), channel_id=1, source_target_pairs={{0,2},{2,0},{1,3},{3,1},{4,6},{6,4},{5,7},{7,5},{8,10},{10,8},{9,1... | collective-permute-start | bytes 1032200 | tf_op jit(solution)/shard_map/ppermute | solution.py:13
  188.0 23.6 %collective-permute-start.35 = (bf16[24,7168]{1,0:T(8,128)(2,1)S(1)}, bf16[24,7168]{1,0:T(8,128)(2,1)S(1)}, u32[]{:S(2)}, u32[]{:S(2)}) collective-permute-start(bf16[24,7168]{1,0:T(8,128)(2,1)S(1)} %get-tuple-element.36), channel_id=1, source_target_pairs={{0,2},{2,0},{1,3},{3,1},{4,6},{6,4},{5,7},{7,5},{8,10},{10,8},{9,1... | collective-permute-start | bytes 1032200 | tf_op jit(solution)/shard_map/ppermute | solution.py:13
  189.5 28.7 %collective-permute-start.33 = (bf16[24,7168]{1,0:T(8,128)(2,1)S(1)}, bf16[24,7168]{1,0:T(8,128)(2,1)S(1)}, u32[]{:S(2)}, u32[]{:S(2)}) collective-permute-start(bf16[24,7168]{1,0:T(8,128)(2,1)S(1)} %get-tuple-element.37), channel_id=1, source_target_pairs={{0,2},{2,0},{1,3},{3,1},{4,6},{6,4},{5,7},{7,5},{8,10},{10,8},{9,1... | collective-permute-start | bytes 1032200 | tf_op jit(solution)/shard_map/ppermute | solution.py:13
  190.0 34.0 %collective-permute-start.18 = (bf16[24,7168]{1,0:T(8,128)(2,1)S(1)}, bf16[24,7168]{1,0:T(8,128)(2,1)S(1)}, u32[]{:S(2)}, u32[]{:S(2)}) collective-permute-start(bf16[24,7168]{1,0:T(8,128)(2,1)S(1)} %copy-done.10), channel_id=1, source_target_pairs={{0,4},{4,0},{8,12},{12,8},{1,5},{5,1},{9,13},{13,9},{2,6},{6,2},{1... | collective-permute-start | bytes 1032200 | tf_op jit(solution)/shard_map/ppermute | solution.py:96
  196.9 28.5 %collective-permute-start.19 = (bf16[24,7168]{1,0:T(8,128)(2,1)S(1)}, bf16[24,7168]{1,0:T(8,128)(2,1)S(1)}, u32[]{:S(2)}, u32[]{:S(2)}) collective-permute-start(bf16[24,7168]{1,0:T(8,128)(2,1)S(1)} %copy-done.9), channel_id=1, source_target_pairs={{0,8},{4,12},{8,0},{12,4},{1,9},{5,13},{9,1},{13,5},{2,10},{6,14},... | collective-permute-start | bytes 1032200 | tf_op jit(solution)/shard_map/ppermute | solution.py:96
  204.3 42.0 %collective-permute-start.20 = (bf16[24,7168]{1,0:T(8,128)(2,1)S(1)}, bf16[24,7168]{1,0:T(8,128)(2,1)S(1)}, u32[]{:S(2)}, u32[]{:S(2)}) collective-permute-start(bf16[24,7168]{1,0:T(8,128)(2,1)S(1)} %copy-done.8), channel_id=1, source_target_pairs={{0,12},{4,8},{8,4},{12,0},{1,13},{5,9},{9,5},{13,1},{2,14},{6,10},... | collective-permute-start | bytes 1032200 | tf_op jit(solution)/shard_map/ppermute | solution.py:96
  218.5 28.0 %copy-start.4 = (bf16[1,32,7168]{2,1,0:T(8,128)(2,1)S(1)}, bf16[1,32,7168]{2,1,0:T(8,128)(2,1)}, u32[]{:S(2)}) copy-start(bf16[1,32,7168]{2,1,0:T(8,128)(2,1)} %param.10) | copy-start | bytes 1376260
  218.5 34.2 %collective-permute-start.36 = (bf16[24,7168]{1,0:T(8,128)(2,1)S(1)}, bf16[24,7168]{1,0:T(8,128)(2,1)S(1)}, u32[]{:S(2)}, u32[]{:S(2)}) collective-permute-start(bf16[24,7168]{1,0:T(8,128)(2,1)S(1)} %get-tuple-element.19), channel_id=1, source_target_pairs={{0,8},{4,12},{8,0},{12,4},{1,9},{5,13},{9,1},{13,5},{2,10},{6,14},... | collective-permute-start | bytes 1032200 | tf_op jit(solution)/shard_map/ppermute | solution.py:96
  222.0 30.7 %collective-permute-start.34 = (bf16[24,7168]{1,0:T(8,128)(2,1)S(1)}, bf16[24,7168]{1,0:T(8,128)(2,1)S(1)}, u32[]{:S(2)}, u32[]{:S(2)}) collective-permute-start(bf16[24,7168]{1,0:T(8,128)(2,1)S(1)} %get-tuple-element.20), channel_id=1, source_target_pairs={{0,4},{4,0},{8,12},{12,8},{1,5},{5,1},{9,13},{13,9},{2,6},{6,2},{1... | collective-permute-start | bytes 1032200 | tf_op jit(solution)/shard_map/ppermute | solution.py:96
  224.0 36.3 %collective-permute-start.38 = (bf16[24,7168]{1,0:T(8,128)(2,1)S(1)}, bf16[24,7168]{1,0:T(8,128)(2,1)S(1)}, u32[]{:S(2)}, u32[]{:S(2)}) collective-permute-start(bf16[24,7168]{1,0:T(8,128)(2,1)S(1)} %get-tuple-element.21), channel_id=1, source_target_pairs={{0,12},{4,8},{8,4},{12,0},{1,13},{5,9},{9,5},{13,1},{2,14},{6,10},... | collective-permute-start | bytes 1032200 | tf_op jit(solution)/shard_map/ppermute | solution.py:96
  246.5 14.0 %copy-start.6 = (bf16[1,32,7168]{2,1,0:T(8,128)(2,1)S(1)}, bf16[1,32,7168]{2,1,0:T(8,128)(2,1)}, u32[]{:S(2)}) copy-start(bf16[1,32,7168]{2,1,0:T(8,128)(2,1)} %param.14) | copy-start | bytes 1376260
  247.2 15.5 %collective-permute-start.21 = (bf16[1,32,7168]{2,1,0:T(8,128)(2,1)S(1)}, bf16[1,32,7168]{2,1,0:T(8,128)(2,1)S(1)}, u32[]{:S(2)}, u32[]{:S(2)}) collective-permute-start(bf16[1,32,7168]{2,1,0:T(8,128)(2,1)S(1)} %fusion.3), channel_id=1, source_target_pairs={{0,16},{16,0},{1,17},{17,1},{2,18},{18,2},{3,19},{19,3},{4,20},{20... | collective-permute-start | bytes 1376264 | tf_op jit(solution)/shard_map/ppermute | solution.py:19
  261.2 11.9 %collective-permute-start.39 = (bf16[1,32,7168]{2,1,0:T(8,128)(2,1)S(1)}, bf16[1,32,7168]{2,1,0:T(8,128)(2,1)S(1)}, u32[]{:S(2)}, u32[]{:S(2)}) collective-permute-start(bf16[1,32,7168]{2,1,0:T(8,128)(2,1)S(1)} %fusion.2), channel_id=1, source_target_pairs={{0,16},{16,0},{1,17},{17,1},{2,18},{18,2},{3,19},{19,3},{4,20},{20... | collective-permute-start | bytes 1376264 | tf_op jit(solution)/shard_map/ppermute | solution.py:19

commit v17 on v5

--- a/solution.py
+++ b/solution.py
@@ -130,7 +130,9 @@
     b_rows, f_totals = lax.optimization_barrier((b_rows, f_totals))
     f_out = returned(f_totals)
     b_partial = backward_rows(b_rows.reshape(-1, 2 * width), w_gate, w_up, w_down)
-    b_out = returned(reduce_group(b_partial.reshape(2, 2, experts, capacity, width)))
+    b_totals = reduce_group(b_partial.reshape(2, 2, experts, capacity, width))
+    b_totals, f_out = lax.optimization_barrier((b_totals, f_out))
+    b_out = returned(b_totals)
     high = lax.Precision.HIGHEST
     f_mixed = jnp.dot(
         f_weights, f_out.reshape(experts * capacity, width).astype(jnp.float32), precision=high

time: 275 us -> 266 us (0.967)
  waiting for transfers between devices: 187 us -> 176 us
    ppermute x26, waiting for transfers between devices: 105 us -> 80.6 us  [swap(): return lax.ppermute(value, axis, [(0, 1), (1, 0)])]
    ppermute x6, waiting for transfers between devices: 33.3 us -> 49.4 us  [returned(): out.append(lax.ppermute(totals[d], 'z', [(i, i ^ d) for i in range(count)]))]
  transfers between devices with their start and end apart: 40 -> 40, of which waited for: 25 -> 25; matrix products, arithmetic and copies ran while one was open for 8% -> 9% of each run, Pallas kernels for 0% -> 0%
where the time goes in v17:
time: 266 us; the launch traced here: 265 us
  waiting for transfers between devices  176 us (66%)
  starting transfers between devices  40 us (15%)
  other arithmetic  19.4 us (7%)
  matrix products  18.9 us (7%)
  local copies, waits for them, and re-layouts  9.57 us (4%)
    ppermute x26, waiting for transfers between devices, swap(): return lax.ppermute(value, axis, [(0, 1), (1, 0)])  80.6 us
    ppermute x6, waiting for transfers between devices, returned(): out.append(lax.ppermute(totals[d], 'z', [(i, i ^ d) for i in range(count)]))  49.4 us
    ppermute x6, waiting for transfers between devices, dispatch(): received = lax.ppermute(slots[d], 'z', [(i, i ^ d) for i in range(count)])  37.3 us
    ppermute x26, starting transfers between devices, swap(): return lax.ppermute(value, axis, [(0, 1), (1, 0)])  22.4 us
    ppermute x2, waiting for transfers between devices, passed_along(): return lax.ppermute(value, axis, pairs)  9.05 us
    another operation x8, other arithmetic, dispatch(): pieces.append(jnp.stack([across, swap(across, 'c')]))  8.09 us
    ppermute x6, starting transfers between devices, dispatch(): received = lax.ppermute(slots[d], 'z', [(i, i ^ d) for i in range(count)])  7.38 us
    ppermute x6, starting transfers between devices, returned(): out.append(lax.ppermute(totals[d], 'z', [(i, i ^ d) for i in range(count)]))  7.04 us
  transfers between devices with their start and end apart: 40, of which 25 were waited for; matrix products, arithmetic and copies ran while one was open for 9% of the time, Pallas kernels for 0%

profile of v17, /device:TPU:16, one launch (start us, length us, event | category | flops | bytes accessed | tf_op | source)
XLA Modules:
  0.0 265.4 jit_solution(6075357197382586988)
XLA Ops:
  3.0 1.6 convolution_convert_fusion.2
  4.7 1.6 collective-permute-start.13
  6.7 1.6 collective-permute-start.19
  8.3 1.5 collective-permute-start.11
  11.9 2.5 collective-permute-start.2
  14.4 2.9 %collective-permute-done.11 = bf16[24,7168]{1,0:T(8,128)(2,1)} collective-permute-done((bf16[24,7168]{1,0:T(8,128)(2,1)S(1)}, bf16[24,7168]{1,0:T(8,128)(2,1)}, u32[]{:S(2)}, u32[]{:S(2)}) %collective-permute-start.11) | collective-permute-done | bytes 344096 | tf_op jit(solution)/shard_map/ppermute | solution.py:13
  17.3 1.5 collective-permute-start
  19.9 1.5 collective-permute-done.13
  22.3 10.5 %collective-permute-done = bf16[24,14336]{1,0:T(8,128)(2,1)S(1)} collective-permute-done((bf16[24,14336]{1,0:T(8,128)(2,1)S(1)}, bf16[24,14336]{1,0:T(8,128)(2,1)S(1)}, u32[]{:S(2)}, u32[]{:S(2)}) %collective-permute-start) | collective-permute-done | bytes 688160 | tf_op jit(solution)/shard_map/ppermute | solution.py:13
  32.8 1.5 collective-permute-start.14
  34.3 1.3 fusion.83
  36.0 5.1 %collective-permute-done.14 = bf16[24,7168]{1,0:T(8,128)(2,1)S(1)} collective-permute-done((bf16[24,7168]{1,0:T(8,128)(2,1)}, bf16[24,7168]{1,0:T(8,128)(2,1)S(1)}, u32[]{:S(2)}, u32[]{:S(2)}) %collective-permute-start.14) | collective-permute-done | bytes 344096 | tf_op jit(solution)/shard_map/ppermute | solution.py:13
  41.1 1.5 collective-permute-start.17
  42.6 1.1 fusion.76
  43.8 6.0 %collective-permute-done.17 = bf16[24,7168]{1,0:T(8,128)(2,1)S(1)} collective-permute-done((bf16[24,7168]{1,0:T(8,128)(2,1)S(1)}, bf16[24,7168]{1,0:T(8,128)(2,1)S(1)}, u32[]{:S(2)}, u32[]{:S(2)}) %collective-permute-start.17) | collective-permute-done | bytes 344096 | tf_op jit(solution)/shard_map/ppermute | solution.py:13
  49.8 1.6 collective-permute-start.20
  51.5 5.5 %collective-permute-done.20 = bf16[24,7168]{1,0:T(8,128)(2,1)S(1)} collective-permute-done((bf16[24,7168]{1,0:T(8,128)(2,1)S(1)}, bf16[24,7168]{1,0:T(8,128)(2,1)S(1)}, u32[]{:S(2)}, u32[]{:S(2)}) %collective-permute-start.20) | collective-permute-done | bytes 344096 | tf_op jit(solution)/shard_map/ppermute | solution.py:13
  57.8 1.3 collective-permute-done.15
  59.9 21.7 %collective-permute-done.5 = bf16[24,14336]{1,0:T(8,128)(2,1)} collective-permute-done((bf16[24,14336]{1,0:T(8,128)(2,1)S(1)}, bf16[24,14336]{1,0:T(8,128)(2,1)}, u32[]{:S(2)}, u32[]{:S(2)}) %collective-permute-start.5) | collective-permute-done | bytes 688160 | tf_op jit(solution)/shard_map/ppermute | solution.py:77
  81.6 1.5 collective-permute-start.3
  83.1 14.0 %collective-permute-done.8 = bf16[24,14336]{1,0:T(8,128)(2,1)} collective-permute-done((bf16[24,14336]{1,0:T(8,128)(2,1)S(1)}, bf16[24,14336]{1,0:T(8,128)(2,1)}, u32[]{:S(2)}, u32[]{:S(2)}) %collective-permute-start.8) | collective-permute-done | bytes 688160 | tf_op jit(solution)/shard_map/ppermute | solution.py:77
  97.1 1.5 collective-permute-start.6
  100.8 1.6 copy-done
  102.4 1.6 fusion.19
  104.4 1.6 fusion.44
  106.5 1.6 convolution_convert_fusion.1
  108.5 1.5 fusion.82
  110.6 5.2 %collective-permute-done.6 = bf16[24,14336]{1,0:T(8,128)(2,1)} collective-permute-done((bf16[24,14336]{1,0:T(8,128)(2,1)}, bf16[24,14336]{1,0:T(8,128)(2,1)}, u32[]{:S(2)}, u32[]{:S(2)}) %collective-permute-start.6) | collective-permute-done | bytes 688160 | tf_op jit(solution)/shard_map/ppermute | solution.py:13
  115.8 1.5 fusion.81
  117.4 10.8 %collective-permute-done.9 = bf16[24,14336]{1,0:T(8,128)(2,1)} collective-permute-done((bf16[24,14336]{1,0:T(8,128)(2,1)}, bf16[24,14336]{1,0:T(8,128)(2,1)}, u32[]{:S(2)}, u32[]{:S(2)}) %collective-permute-start.9) | collective-permute-done | bytes 688160 | tf_op jit(solution)/shard_map/ppermute | solution.py:13
  128.2 1.5 fusion.80
  129.8 1.6 maximum_bitcast_fusion
  134.3 1.6 collective-permute-start.23
  136.4 1.5 collective-permute-start.25
  138.4 1.5 pad_maximum_fusion
  139.9 5.4 %collective-permute-done.23 = bf16[24,7168]{1,0:T(8,128)(2,1)S(1)} collective-permute-done((bf16[24,7168]{1,0:T(8,128)(2,1)S(1)}, bf16[24,7168]{1,0:T(8,128)(2,1)S(1)}, u32[]{:S(2)}, u32[]{:S(2)}) %collective-permute-start.23) | collective-permute-done | bytes 344096 | tf_op jit(solution)/shard_map/ppermute | solution.py:13
  145.3 7.4 %collective-permute-done.24 = bf16[24,7168]{1,0:T(8,128)(2,1)S(1)} collective-permute-done((bf16[24,7168]{1,0:T(8,128)(2,1)S(1)}, bf16[24,7168]{1,0:T(8,128)(2,1)S(1)}, u32[]{:S(2)}, u32[]{:S(2)}) %collective-permute-start.24) | collective-permute-done | bytes 344096 | tf_op jit(solution)/shard_map/ppermute | solution.py:13
  152.6 7.4 %collective-permute-done.25 = bf16[24,7168]{1,0:T(8,128)(2,1)S(1)} collective-permute-done((bf16[24,7168]{1,0:T(8,128)(2,1)S(1)}, bf16[24,7168]{1,0:T(8,128)(2,1)S(1)}, u32[]{:S(2)}, u32[]{:S(2)}) %collective-permute-start.25) | collective-permute-done | bytes 344096 | tf_op jit(solution)/shard_map/ppermute | solution.py:13
  160.0 6.6 %collective-permute-done.26 = bf16[24,7168]{1,0:T(8,128)(2,1)S(1)} collective-permute-done((bf16[24,7168]{1,0:T(8,128)(2,1)S(1)}, bf16[24,7168]{1,0:T(8,128)(2,1)S(1)}, u32[]{:S(2)}, u32[]{:S(2)}) %collective-permute-start.26) | collective-permute-done | bytes 344096 | tf_op jit(solution)/shard_map/ppermute | solution.py:13
  166.6 1.1 fusion.59
  167.7 1.9 copy.35
  169.7 1.6 fusion.4
  171.3 1.6 fusion.6
  173.4 1.6 fusion.39
  175.0 1.6 fusion.16
  176.6 3.8 %add_convert_fusion = bf16[384,7168]{1,0:T(8,128)(2,1)S(1)} fusion(f32[384,7168]{1,0:T(8,128)S(1)} %fusion.16, bf16[1,7168,256]{2,1,0:T(8,128)(2,1)} %param.18, f32[384,256]{1,0:T(8,128)S(1)} %fusion.4, f32[384,256]{1,0:T(8,128)S(1)} %fusion.6), kind=kOutput, calls=%fused_computation.2 | convolution fusion | flops 1415380992 | bytes 20971520 | tf_op jit(solution)/shard_map/dot_general | solution.py:64
  181.4 1.5 collective-permute-start.32
  183.3 1.6 collective-permute-start.34
  184.9 1.1 collective-permute-done.27
  187.1 1.6 collective-permute-start.28
  189.2 7.2 %collective-permute-done.32 = bf16[24,7168]{1,0:T(8,128)(2,1)S(1)} collective-permute-done((bf16[24,7168]{1,0:T(8,128)(2,1)S(1)}, bf16[24,7168]{1,0:T(8,128)(2,1)S(1)}, u32[]{:S(2)}, u32[]{:S(2)}) %collective-permute-start.32) | collective-permute-done | bytes 344096 | tf_op jit(solution)/shard_map/ppermute | solution.py:97
  196.5 1.5 collective-permute-start.30
  198.0 8.6 %collective-permute-done.33 = bf16[24,7168]{1,0:T(8,128)(2,1)S(1)} collective-permute-done((bf16[24,7168]{1,0:T(8,128)(2,1)S(1)}, bf16[24,7168]{1,0:T(8,128)(2,1)S(1)}, u32[]{:S(2)}, u32[]{:S(2)}) %collective-permute-start.33) | collective-permute-done | bytes 344096 | tf_op jit(solution)/shard_map/ppermute | solution.py:97
  206.6 1.5 collective-permute-start.31
  208.0 6.7 %collective-permute-done.34 = bf16[24,7168]{1,0:T(8,128)(2,1)S(1)} collective-permute-done((bf16[24,7168]{1,0:T(8,128)(2,1)S(1)}, bf16[24,7168]{1,0:T(8,128)(2,1)S(1)}, u32[]{:S(2)}, u32[]{:S(2)}) %collective-permute-start.34) | collective-permute-done | bytes 344096 | tf_op jit(solution)/shard_map/ppermute | solution.py:97
  214.9 4.5 %collective-permute-done.31 = bf16[24,7168]{1,0:T(8,128)(2,1)S(1)} collective-permute-done((bf16[24,7168]{1,0:T(8,128)(2,1)S(1)}, bf16[24,7168]{1,0:T(8,128)(2,1)S(1)}, u32[]{:S(2)}, u32[]{:S(2)}) %collective-permute-start.31) | collective-permute-done | bytes 344096 | tf_op jit(solution)/shard_map/ppermute | solution.py:13
  219.7 1.5 collective-permute-start.36
  221.7 1.6 collective-permute-start.38
  223.9 1.6 collective-permute-start.35
  225.5 8.3 %collective-permute-done.36 = bf16[24,7168]{1,0:T(8,128)(2,1)S(1)} collective-permute-done((bf16[24,7168]{1,0:T(8,128)(2,1)S(1)}, bf16[24,7168]{1,0:T(8,128)(2,1)S(1)}, u32[]{:S(2)}, u32[]{:S(2)}) %collective-permute-start.36) | collective-permute-done | bytes 344096 | tf_op jit(solution)/shard_map/ppermute | solution.py:97
  233.8 11.1 %collective-permute-done.37 = bf16[24,7168]{1,0:T(8,128)(2,1)S(1)} collective-permute-done((bf16[24,7168]{1,0:T(8,128)(2,1)S(1)}, bf16[24,7168]{1,0:T(8,128)(2,1)S(1)}, u32[]{:S(2)}, u32[]{:S(2)}) %collective-permute-start.37) | collective-permute-done | bytes 344096 | tf_op jit(solution)/shard_map/ppermute | solution.py:97
  244.9 7.5 %collective-permute-done.38 = bf16[24,7168]{1,0:T(8,128)(2,1)S(1)} collective-permute-done((bf16[24,7168]{1,0:T(8,128)(2,1)S(1)}, bf16[24,7168]{1,0:T(8,128)(2,1)S(1)}, u32[]{:S(2)}, u32[]{:S(2)}) %collective-permute-start.38) | collective-permute-done | bytes 344096 | tf_op jit(solution)/shard_map/ppermute | solution.py:97
  253.3 1.6 collective-permute-start.39
  254.9 9.0 %collective-permute-done.39 = bf16[1,32,7168]{2,1,0:T(8,128)(2,1)S(1)} collective-permute-done((bf16[1,32,7168]{2,1,0:T(8,128)(2,1)S(1)}, bf16[1,32,7168]{2,1,0:T(8,128)(2,1)S(1)}, u32[]{:S(2)}, u32[]{:S(2)}) %collective-permute-start.39) | collective-permute-done | bytes 458784 | tf_op jit(solution)/shard_map/ppermute | solution.py:19
  (107 shorter events, 24.4 us)
Async XLA Ops:
  0.6 9.9 %copy-start.12 = (f32[1,32,2]{1,2,0:T(2,128)S(1)}, f32[1,32,2]{1,2,0:T(2,128)}, u32[]{:S(2)}) copy-start(f32[1,32,2]{1,2,0:T(2,128)} %param.16) | copy-start | bytes 772
  0.6 10.0 %copy-start.8 = (bf16[1,32,7168]{2,1,0:T(8,128)(2,1)S(1)}, bf16[1,32,7168]{2,1,0:T(8,128)(2,1)}, u32[]{:S(2)}) copy-start(bf16[1,32,7168]{2,1,0:T(8,128)(2,1)} %param.13) | copy-start | bytes 1376260
  0.7 10.0 %copy-start.6 = (bf16[1,32,7168]{2,1,0:T(8,128)(2,1)S(1)}, bf16[1,32,7168]{2,1,0:T(8,128)(2,1)}, u32[]{:S(2)}) copy-start(bf16[1,32,7168]{2,1,0:T(8,128)(2,1)} %param.14) | copy-start | bytes 1376260
  4.7 16.7 %collective-permute-start.13 = (bf16[24,7168]{1,0:T(8,128)(2,1)S(1)}, bf16[24,7168]{1,0:T(8,128)(2,1)}, u32[]{:S(2)}, u32[]{:S(2)}) collective-permute-start(bf16[24,7168]{1,0:T(8,128)(2,1)S(1)} %get-tuple-element.58), channel_id=1, source_target_pairs={{0,4},{4,0},{8,12},{12,8},{1,5},{5,1},{9,13},{13,9},{2,6},{6,2},{1... | collective-permute-start | bytes 1032200 | tf_op jit(solution)/shard_map/ppermute | solution.py:77
  6.4 29.2 %collective-permute-start.16 = (bf16[24,7168]{1,0:T(8,128)(2,1)S(1)}, bf16[24,7168]{1,0:T(8,128)(2,1)S(1)}, u32[]{:S(2)}, u32[]{:S(2)}) collective-permute-start(bf16[24,7168]{1,0:T(8,128)(2,1)S(1)} %get-tuple-element.57), channel_id=1, source_target_pairs={{0,8},{4,12},{8,0},{12,4},{1,9},{5,13},{9,1},{13,5},{2,10},{6,14},... | collective-permute-start | bytes 1032200 | tf_op jit(solution)/shard_map/ppermute | solution.py:77
  6.7 37.0 %collective-permute-start.19 = (bf16[24,7168]{1,0:T(8,128)(2,1)S(1)}, bf16[24,7168]{1,0:T(8,128)(2,1)S(1)}, u32[]{:S(2)}, u32[]{:S(2)}) collective-permute-start(bf16[24,7168]{1,0:T(8,128)(2,1)S(1)} %get-tuple-element.56), channel_id=1, source_target_pairs={{0,12},{4,8},{8,4},{12,0},{1,13},{5,9},{9,5},{13,1},{2,14},{6,10},... | collective-permute-start | bytes 1032200 | tf_op jit(solution)/shard_map/ppermute | solution.py:77
  8.3 9.1 %collective-permute-start.11 = (bf16[24,7168]{1,0:T(8,128)(2,1)S(1)}, bf16[24,7168]{1,0:T(8,128)(2,1)}, u32[]{:S(2)}, u32[]{:S(2)}) collective-permute-start(bf16[24,7168]{1,0:T(8,128)(2,1)S(1)} %get-tuple-element.59), channel_id=1, source_target_pairs={{0,2},{2,0},{1,3},{3,1},{4,6},{6,4},{5,7},{7,5},{8,10},{10,8},{9,1... | collective-permute-start | bytes 1032200 | tf_op jit(solution)/shard_map/ppermute | solution.py:13
  11.9 47.6 %collective-permute-start.2 = (bf16[24,14336]{1,0:T(8,128)(2,1)S(1)}, bf16[24,14336]{1,0:T(8,128)(2,1)}, u32[]{:S(2)}, u32[]{:S(2)}) collective-permute-start(bf16[24,14336]{1,0:T(8,128)(2,1)S(1)} %get-tuple-element.53), channel_id=1, source_target_pairs={{0,4},{4,0},{8,12},{12,8},{1,5},{5,1},{9,13},{13,9},{2,6},{6,2},{1... | collective-permute-start | bytes 2064392 | tf_op jit(solution)/shard_map/ppermute | solution.py:77
  17.3 15.4 %collective-permute-start = (bf16[24,14336]{1,0:T(8,128)(2,1)S(1)}, bf16[24,14336]{1,0:T(8,128)(2,1)S(1)}, u32[]{:S(2)}, u32[]{:S(2)}) collective-permute-start(bf16[24,14336]{1,0:T(8,128)(2,1)S(1)} %get-tuple-element.54), channel_id=1, source_target_pairs={{0,2},{2,0},{1,3},{3,1},{4,6},{6,4},{5,7},{7,5},{8,10},{10,8},{9,1... | collective-permute-start | bytes 2064392 | tf_op jit(solution)/shard_map/ppermute | solution.py:13
  21.5 60.2 %collective-permute-start.5 = (bf16[24,14336]{1,0:T(8,128)(2,1)S(1)}, bf16[24,14336]{1,0:T(8,128)(2,1)}, u32[]{:S(2)}, u32[]{:S(2)}) collective-permute-start(bf16[24,14336]{1,0:T(8,128)(2,1)S(1)} %get-tuple-element.52), channel_id=1, source_target_pairs={{0,8},{4,12},{8,0},{12,4},{1,9},{5,13},{9,1},{13,5},{2,10},{6,14},... | collective-permute-start | bytes 2064392 | tf_op jit(solution)/shard_map/ppermute | solution.py:77
  32.8 8.4 %collective-permute-start.14 = (bf16[24,7168]{1,0:T(8,128)(2,1)}, bf16[24,7168]{1,0:T(8,128)(2,1)S(1)}, u32[]{:S(2)}, u32[]{:S(2)}) collective-permute-start(bf16[24,7168]{1,0:T(8,128)(2,1)} %collective-permute-done.13), channel_id=1, source_target_pairs={{0,2},{2,0},{1,3},{3,1},{4,6},{6,4},{5,7},{7,5},{8,10},{10,8},{9,1... | collective-permute-start | bytes 1032200 | tf_op jit(solution)/shard_map/ppermute | solution.py:13
  35.6 61.5 %collective-permute-start.8 = (bf16[24,14336]{1,0:T(8,128)(2,1)S(1)}, bf16[24,14336]{1,0:T(8,128)(2,1)}, u32[]{:S(2)}, u32[]{:S(2)}) collective-permute-start(bf16[24,14336]{1,0:T(8,128)(2,1)S(1)} %get-tuple-element.51), channel_id=1, source_target_pairs={{0,12},{4,8},{8,4},{12,0},{1,13},{5,9},{9,5},{13,1},{2,14},{6,10},... | collective-permute-start | bytes 2064392 | tf_op jit(solution)/shard_map/ppermute | solution.py:77
  41.1 8.7 %collective-permute-start.17 = (bf16[24,7168]{1,0:T(8,128)(2,1)S(1)}, bf16[24,7168]{1,0:T(8,128)(2,1)S(1)}, u32[]{:S(2)}, u32[]{:S(2)}) collective-permute-start(bf16[24,7168]{1,0:T(8,128)(2,1)S(1)} %collective-permute-done.16), channel_id=1, source_target_pairs={{0,2},{2,0},{1,3},{3,1},{4,6},{6,4},{5,7},{7,5},{8,10},{10,8},{9,1... | collective-permute-start | bytes 1032200 | tf_op jit(solution)/shard_map/ppermute | solution.py:13
  43.7 13.4 %collective-permute-start.12 = (bf16[2,24,7168]{2,1,0:T(8,128)(2,1)S(1)}, bf16[2,24,7168]{2,1,0:T(8,128)(2,1)S(1)}, u32[]{:S(2)}, u32[]{:S(2)}) collective-permute-start(bf16[2,24,7168]{2,1,0:T(8,128)(2,1)S(1)} %get-tuple-element.69), channel_id=1, source_target_pairs={{0,1},{1,0},{2,3},{3,2},{4,5},{5,4},{6,7},{7,6},{8,9},{9,8},{10,11... | collective-permute-start | bytes 2064392 | tf_op jit(solution)/shard_map/ppermute | solution.py:13
  49.8 7.2 %collective-permute-start.20 = (bf16[24,7168]{1,0:T(8,128)(2,1)S(1)}, bf16[24,7168]{1,0:T(8,128)(2,1)S(1)}, u32[]{:S(2)}, u32[]{:S(2)}) collective-permute-start(bf16[24,7168]{1,0:T(8,128)(2,1)S(1)} %collective-permute-done.19), channel_id=1, source_target_pairs={{0,2},{2,0},{1,3},{3,1},{4,6},{6,4},{5,7},{7,5},{8,10},{10,8},{9,1... | collective-permute-start | bytes 1032200 | tf_op jit(solution)/shard_map/ppermute | solution.py:13
  57.0 2.1 collective-permute-start.15
  57.1 41.5 %collective-permute-start.18 = (bf16[2,24,7168]{2,1,0:T(8,128)(2,1)S(1)}, bf16[2,24,7168]{2,1,0:T(8,128)(2,1)S(1)}, u32[]{:S(2)}, u32[]{:S(2)}) collective-permute-start(bf16[2,24,7168]{2,1,0:T(8,128)(2,1)S(1)} %get-tuple-element.73), channel_id=1, source_target_pairs={{0,1},{1,0},{2,3},{3,2},{4,5},{5,4},{6,7},{7,6},{8,9},{9,8},{10,11... | collective-permute-start | bytes 2064392 | tf_op jit(solution)/shard_map/ppermute | solution.py:13
  59.2 40.1 %collective-permute-start.21 = (bf16[2,24,7168]{2,1,0:T(8,128)(2,1)S(1)}, bf16[2,24,7168]{2,1,0:T(8,128)(2,1)S(1)}, u32[]{:S(2)}, u32[]{:S(2)}) collective-permute-start(bf16[2,24,7168]{2,1,0:T(8,128)(2,1)S(1)} %get-tuple-element.75), channel_id=1, source_target_pairs={{0,1},{1,0},{2,3},{3,2},{4,5},{5,4},{6,7},{7,6},{8,9},{9,8},{10,11... | collective-permute-start | bytes 2064392 | tf_op jit(solution)/shard_map/ppermute | solution.py:13
  59.5 70.3 %collective-permute-start.1 = (bf16[2,24,14336]{2,1,0:T(8,128)(2,1)}, bf16[2,24,14336]{2,1,0:T(8,128)(2,1)}, u32[]{:S(2)}, u32[]{:S(2)}) collective-permute-start(bf16[2,24,14336]{2,1,0:T(8,128)(2,1)} %get-tuple-element.61), channel_id=1, source_target_pairs={{0,1},{1,0},{2,3},{3,2},{4,5},{5,4},{6,7},{7,6},{8,9},{9,8},{10,11... | collective-permute-start | bytes 4128776 | tf_op jit(solution)/shard_map/ppermute | solution.py:13
  81.6 26.9 %collective-permute-start.3 = (bf16[24,14336]{1,0:T(8,128)(2,1)}, bf16[24,14336]{1,0:T(8,128)(2,1)}, u32[]{:S(2)}, u32[]{:S(2)}) collective-permute-start(bf16[24,14336]{1,0:T(8,128)(2,1)} %collective-permute-done.2), channel_id=1, source_target_pairs={{0,2},{2,0},{1,3},{3,1},{4,6},{6,4},{5,7},{7,5},{8,10},{10,8},{9,1... | collective-permute-start | bytes 2064392 | tf_op jit(solution)/shard_map/ppermute | solution.py:13
  97.1 18.7 %collective-permute-start.6 = (bf16[24,14336]{1,0:T(8,128)(2,1)}, bf16[24,14336]{1,0:T(8,128)(2,1)}, u32[]{:S(2)}, u32[]{:S(2)}) collective-permute-start(bf16[24,14336]{1,0:T(8,128)(2,1)} %collective-permute-done.5), channel_id=1, source_target_pairs={{0,2},{2,0},{1,3},{3,1},{4,6},{6,4},{5,7},{7,5},{8,10},{10,8},{9,1... | collective-permute-start | bytes 2064392 | tf_op jit(solution)/shard_map/ppermute | solution.py:13
  98.6 29.6 %collective-permute-start.9 = (bf16[24,14336]{1,0:T(8,128)(2,1)}, bf16[24,14336]{1,0:T(8,128)(2,1)}, u32[]{:S(2)}, u32[]{:S(2)}) collective-permute-start(bf16[24,14336]{1,0:T(8,128)(2,1)} %collective-permute-done.8), channel_id=1, source_target_pairs={{0,2},{2,0},{1,3},{3,1},{4,6},{6,4},{5,7},{7,5},{8,10},{10,8},{9,1... | collective-permute-start | bytes 2064392 | tf_op jit(solution)/shard_map/ppermute | solution.py:13
  100.4 2.0 copy-start
  102.4 2.0 copy-start.1
  104.4 2.0 copy-start.3
  108.5 24.7 %collective-permute-start.22 = (bf16[2,4,24,7168]{3,2,1,0:T(8,128)(2,1)S(1)}, bf16[2,4,24,7168]{3,2,1,0:T(8,128)(2,1)S(1)}, u32[]{:S(2)}, u32[]{:S(2)}) collective-permute-start(bf16[2,4,24,7168]{3,2,1,0:T(8,128)(2,1)S(1)} %bitcast.207), channel_id=1, source_target_pairs={{0,1},{1,0},{2,3},{3,2},{4,5},{5,4},{6,7},{7,6},{8,9},{9,8},{10,11... | collective-permute-start | bytes 8257544 | tf_op jit(solution)/shard_map/ppermute | solution.py:13
  110.0 21.3 %collective-permute-start.4 = (bf16[2,24,14336]{2,1,0:T(8,128)(2,1)S(1)}, bf16[2,24,14336]{2,1,0:T(8,128)(2,1)S(1)}, u32[]{:S(2)}, u32[]{:S(2)}) collective-permute-start(bf16[2,24,14336]{2,1,0:T(8,128)(2,1)S(1)} %get-tuple-element.63), channel_id=1, source_target_pairs={{0,1},{1,0},{2,3},{3,2},{4,5},{5,4},{6,7},{7,6},{8,9},{9,8},{10,11... | collective-permute-start | bytes 4128776 | tf_op jit(solution)/shard_map/ppermute | solution.py:13
  117.3 14.4 %collective-permute-start.7 = (bf16[2,24,14336]{2,1,0:T(8,128)(2,1)S(1)}, bf16[2,24,14336]{2,1,0:T(8,128)(2,1)S(1)}, u32[]{:S(2)}, u32[]{:S(2)}) collective-permute-start(bf16[2,24,14336]{2,1,0:T(8,128)(2,1)S(1)} %get-tuple-element.65), channel_id=1, source_target_pairs={{0,1},{1,0},{2,3},{3,2},{4,5},{5,4},{6,7},{7,6},{8,9},{9,8},{10,11... | collective-permute-start | bytes 4128776 | tf_op jit(solution)/shard_map/ppermute | solution.py:13
  129.7 3.2 %collective-permute-start.10 = (bf16[2,24,14336]{2,1,0:T(8,128)(2,1)S(1)}, bf16[2,24,14336]{2,1,0:T(8,128)(2,1)S(1)}, u32[]{:S(2)}, u32[]{:S(2)}) collective-permute-start(bf16[2,24,14336]{2,1,0:T(8,128)(2,1)S(1)} %get-tuple-element.67), channel_id=1, source_target_pairs={{0,1},{1,0},{2,3},{3,2},{4,5},{5,4},{6,7},{7,6},{8,9},{9,8},{10,11... | collective-permute-start | bytes 4128776 | tf_op jit(solution)/shard_map/ppermute | solution.py:13
  134.3 11.0 %collective-permute-start.23 = (bf16[24,7168]{1,0:T(8,128)(2,1)S(1)}, bf16[24,7168]{1,0:T(8,128)(2,1)S(1)}, u32[]{:S(2)}, u32[]{:S(2)}) collective-permute-start(bf16[24,7168]{1,0:T(8,128)(2,1)S(1)} %get-tuple-element.49), channel_id=1, source_target_pairs={{0,2},{2,0},{1,3},{3,1},{4,6},{6,4},{5,7},{7,5},{8,10},{10,8},{9,1... | collective-permute-start | bytes 1032200 | tf_op jit(solution)/shard_map/ppermute | solution.py:13
  135.9 16.8 %collective-permute-start.24 = (bf16[24,7168]{1,0:T(8,128)(2,1)S(1)}, bf16[24,7168]{1,0:T(8,128)(2,1)S(1)}, u32[]{:S(2)}, u32[]{:S(2)}) collective-permute-start(bf16[24,7168]{1,0:T(8,128)(2,1)S(1)} %get-tuple-element.48), channel_id=1, source_target_pairs={{0,2},{2,0},{1,3},{3,1},{4,6},{6,4},{5,7},{7,5},{8,10},{10,8},{9,1... | collective-permute-start | bytes 1032200 | tf_op jit(solution)/shard_map/ppermute | solution.py:13
  136.4 23.6 %collective-permute-start.25 = (bf16[24,7168]{1,0:T(8,128)(2,1)S(1)}, bf16[24,7168]{1,0:T(8,128)(2,1)S(1)}, u32[]{:S(2)}, u32[]{:S(2)}) collective-permute-start(bf16[24,7168]{1,0:T(8,128)(2,1)S(1)} %get-tuple-element.47), channel_id=1, source_target_pairs={{0,2},{2,0},{1,3},{3,1},{4,6},{6,4},{5,7},{7,5},{8,10},{10,8},{9,1... | collective-permute-start | bytes 1032200 | tf_op jit(solution)/shard_map/ppermute | solution.py:13
  137.9 28.7 %collective-permute-start.26 = (bf16[24,7168]{1,0:T(8,128)(2,1)S(1)}, bf16[24,7168]{1,0:T(8,128)(2,1)S(1)}, u32[]{:S(2)}, u32[]{:S(2)}) collective-permute-start(bf16[24,7168]{1,0:T(8,128)(2,1)S(1)} %get-tuple-element.46), channel_id=1, source_target_pairs={{0,2},{2,0},{1,3},{3,1},{4,6},{6,4},{5,7},{7,5},{8,10},{10,8},{9,1... | collective-permute-start | bytes 1032200 | tf_op jit(solution)/shard_map/ppermute | solution.py:13
  167.7 2.0 copy-start.4
  171.3 2.0 copy-start.2
  180.4 1.0 copy-start.11
  180.5 2.4 copy-start.10
  180.5 2.9 %copy-start.9 = (bf16[24,7168]{1,0:T(8,128)(2,1)S(1)}, bf16[24,7168]{1,0:T(8,128)(2,1)}, u32[]{:S(2)}) copy-start(bf16[24,7168]{1,0:T(8,128)(2,1)} %get-tuple-element.16) | copy-start | bytes 1032196
  180.8 5.2 %collective-permute-start.27 = (bf16[2,4,24,7168]{3,2,1,0:T(8,128)(2,1)S(1)}, bf16[2,4,24,7168]{3,2,1,0:T(8,128)(2,1)S(1)}, u32[]{:S(2)}, u32[]{:S(2)}) collective-permute-start(bf16[2,4,24,7168]{3,2,1,0:T(8,128)(2,1)S(1)} %bitcast.208), channel_id=1, source_target_pairs={{0,1},{1,0},{2,3},{3,2},{4,5},{5,4},{6,7},{7,6},{8,9},{9,8},{10,11... | collective-permute-start | bytes 8257544 | tf_op jit(solution)/shard_map/ppermute | solution.py:13
  181.4 15.1 %collective-permute-start.32 = (bf16[24,7168]{1,0:T(8,128)(2,1)S(1)}, bf16[24,7168]{1,0:T(8,128)(2,1)S(1)}, u32[]{:S(2)}, u32[]{:S(2)}) collective-permute-start(bf16[24,7168]{1,0:T(8,128)(2,1)S(1)} %copy-done.11), channel_id=1, source_target_pairs={{0,4},{4,0},{8,12},{12,8},{1,5},{5,1},{9,13},{13,9},{2,6},{6,2},{1... | collective-permute-start | bytes 1032200 | tf_op jit(solution)/shard_map/ppermute | solution.py:97
  182.9 23.7 %collective-permute-start.33 = (bf16[24,7168]{1,0:T(8,128)(2,1)S(1)}, bf16[24,7168]{1,0:T(8,128)(2,1)S(1)}, u32[]{:S(2)}, u32[]{:S(2)}) collective-permute-start(bf16[24,7168]{1,0:T(8,128)(2,1)S(1)} %copy-done.10), channel_id=1, source_target_pairs={{0,8},{4,12},{8,0},{12,4},{1,9},{5,13},{9,1},{13,5},{2,10},{6,14},... | collective-permute-start | bytes 1032200 | tf_op jit(solution)/shard_map/ppermute | solution.py:97
  183.3 31.4 %collective-permute-start.34 = (bf16[24,7168]{1,0:T(8,128)(2,1)S(1)}, bf16[24,7168]{1,0:T(8,128)(2,1)S(1)}, u32[]{:S(2)}, u32[]{:S(2)}) collective-permute-start(bf16[24,7168]{1,0:T(8,128)(2,1)S(1)} %copy-done.9), channel_id=1, source_target_pairs={{0,12},{4,8},{8,4},{12,0},{1,13},{5,9},{9,5},{13,1},{2,14},{6,10},... | collective-permute-start | bytes 1032200 | tf_op jit(solution)/shard_map/ppermute | solution.py:97
  187.1 27.8 %collective-permute-start.28 = (bf16[24,7168]{1,0:T(8,128)(2,1)S(1)}, bf16[24,7168]{1,0:T(8,128)(2,1)S(1)}, u32[]{:S(2)}, u32[]{:S(2)}) collective-permute-start(bf16[24,7168]{1,0:T(8,128)(2,1)S(1)} %get-tuple-element.45), channel_id=1, source_target_pairs={{0,2},{2,0},{1,3},{3,1},{4,6},{6,4},{5,7},{7,5},{8,10},{10,8},{9,1... | collective-permute-start | bytes 1032200 | tf_op jit(solution)/shard_map/ppermute | solution.py:13
  188.7 26.2 %collective-permute-start.29 = (bf16[24,7168]{1,0:T(8,128)(2,1)S(1)}, bf16[24,7168]{1,0:T(8,128)(2,1)S(1)}, u32[]{:S(2)}, u32[]{:S(2)}) collective-permute-start(bf16[24,7168]{1,0:T(8,128)(2,1)S(1)} %get-tuple-element.44), channel_id=1, source_target_pairs={{0,2},{2,0},{1,3},{3,1},{4,6},{6,4},{5,7},{7,5},{8,10},{10,8},{9,1... | collective-permute-start | bytes 1032200 | tf_op jit(solution)/shard_map/ppermute | solution.py:13
  196.5 18.5 %collective-permute-start.30 = (bf16[24,7168]{1,0:T(8,128)(2,1)S(1)}, bf16[24,7168]{1,0:T(8,128)(2,1)S(1)}, u32[]{:S(2)}, u32[]{:S(2)}) collective-permute-start(bf16[24,7168]{1,0:T(8,128)(2,1)S(1)} %get-tuple-element.43), channel_id=1, source_target_pairs={{0,2},{2,0},{1,3},{3,1},{4,6},{6,4},{5,7},{7,5},{8,10},{10,8},{9,1... | collective-permute-start | bytes 1032200 | tf_op jit(solution)/shard_map/ppermute | solution.py:13
  206.6 12.9 %collective-permute-start.31 = (bf16[24,7168]{1,0:T(8,128)(2,1)S(1)}, bf16[24,7168]{1,0:T(8,128)(2,1)S(1)}, u32[]{:S(2)}, u32[]{:S(2)}) collective-permute-start(bf16[24,7168]{1,0:T(8,128)(2,1)S(1)} %get-tuple-element.42), channel_id=1, source_target_pairs={{0,2},{2,0},{1,3},{3,1},{4,6},{6,4},{5,7},{7,5},{8,10},{10,8},{9,1... | collective-permute-start | bytes 1032200 | tf_op jit(solution)/shard_map/ppermute | solution.py:13
  219.4 3.8 %copy-start.5 = (bf16[1,32,7168]{2,1,0:T(8,128)(2,1)S(1)}, bf16[1,32,7168]{2,1,0:T(8,128)(2,1)}, u32[]{:S(2)}) copy-start(bf16[1,32,7168]{2,1,0:T(8,128)(2,1)} %param.10) | copy-start | bytes 1376260
  219.7 32.9 %copy-start.7 = (bf16[1,32,7168]{2,1,0:T(8,128)(2,1)S(1)}, bf16[1,32,7168]{2,1,0:T(8,128)(2,1)}, u32[]{:S(2)}) copy-start(bf16[1,32,7168]{2,1,0:T(8,128)(2,1)} %param.14) | copy-start | bytes 1376260
  219.7 14.2 %collective-permute-start.36 = (bf16[24,7168]{1,0:T(8,128)(2,1)S(1)}, bf16[24,7168]{1,0:T(8,128)(2,1)S(1)}, u32[]{:S(2)}, u32[]{:S(2)}) collective-permute-start(bf16[24,7168]{1,0:T(8,128)(2,1)S(1)} %get-tuple-element.19), channel_id=1, source_target_pairs={{0,4},{4,0},{8,12},{12,8},{1,5},{5,1},{9,13},{13,9},{2,6},{6,2},{1... | collective-permute-start | bytes 1032200 | tf_op jit(solution)/shard_map/ppermute | solution.py:97
  221.2 23.7 %collective-permute-start.37 = (bf16[24,7168]{1,0:T(8,128)(2,1)S(1)}, bf16[24,7168]{1,0:T(8,128)(2,1)S(1)}, u32[]{:S(2)}, u32[]{:S(2)}) collective-permute-start(bf16[24,7168]{1,0:T(8,128)(2,1)S(1)} %get-tuple-element.20), channel_id=1, source_target_pairs={{0,8},{4,12},{8,0},{12,4},{1,9},{5,13},{9,1},{13,5},{2,10},{6,14},... | collective-permute-start | bytes 1032200 | tf_op jit(solution)/shard_map/ppermute | solution.py:97
  221.7 30.7 %collective-permute-start.38 = (bf16[24,7168]{1,0:T(8,128)(2,1)S(1)}, bf16[24,7168]{1,0:T(8,128)(2,1)S(1)}, u32[]{:S(2)}, u32[]{:S(2)}) collective-permute-start(bf16[24,7168]{1,0:T(8,128)(2,1)S(1)} %get-tuple-element.21), channel_id=1, source_target_pairs={{0,12},{4,8},{8,4},{12,0},{1,13},{5,9},{9,5},{13,1},{2,14},{6,10},... | collective-permute-start | bytes 1032200 | tf_op jit(solution)/shard_map/ppermute | solution.py:97
  223.9 30.9 %collective-permute-start.35 = (bf16[1,32,7168]{2,1,0:T(8,128)(2,1)S(1)}, bf16[1,32,7168]{2,1,0:T(8,128)(2,1)S(1)}, u32[]{:S(2)}, u32[]{:S(2)}) collective-permute-start(bf16[1,32,7168]{2,1,0:T(8,128)(2,1)S(1)} %fusion.3), channel_id=1, source_target_pairs={{0,16},{16,0},{1,17},{17,1},{2,18},{18,2},{3,19},{19,3},{4,20},{20... | collective-permute-start | bytes 1376264 | tf_op jit(solution)/shard_map/ppermute | solution.py:19
  253.3 10.6 %collective-permute-start.39 = (bf16[1,32,7168]{2,1,0:T(8,128)(2,1)S(1)}, bf16[1,32,7168]{2,1,0:T(8,128)(2,1)S(1)}, u32[]{:S(2)}, u32[]{:S(2)}) collective-permute-start(bf16[1,32,7168]{2,1,0:T(8,128)(2,1)S(1)} %fusion.2), channel_id=1, source_target_pairs={{0,16},{16,0},{1,17},{17,1},{2,18},{18,2},{3,19},{19,3},{4,20},{20... | collective-permute-start | bytes 1376264 | tf_op jit(solution)/shard_map/ppermute | solution.py:19

commit v18 on v17

--- a/solution.py
+++ b/solution.py
@@ -131,18 +131,18 @@
     f_out = returned(f_totals)
     b_partial = backward_rows(b_rows.reshape(-1, 2 * width), w_gate, w_up, w_down)
     b_totals = reduce_group(b_partial.reshape(2, 2, experts, capacity, width))
-    b_totals, f_out = lax.optimization_barrier((b_totals, f_out))
-    b_out = returned(b_totals)
     high = lax.Precision.HIGHEST
     f_mixed = jnp.dot(
         f_weights, f_out.reshape(experts * capacity, width).astype(jnp.float32), precision=high
     )
     f_result = (fwd_input[0].astype(jnp.float32) + f_mixed).astype(jnp.bfloat16)
+    next_section_input = passed_along(f_result[None], "pp", 1)
+    b_totals, next_section_input = lax.optimization_barrier((b_totals, next_section_input))
+    b_out = returned(b_totals)
     b_mixed = jnp.dot(
         b_weights, b_out.reshape(experts * capacity, width).astype(jnp.float32), precision=high
     )
     b_result = (bwd_grad[0].astype(jnp.float32) + b_mixed).astype(jnp.bfloat16)
-    next_section_input = passed_along(f_result[None], "pp", 1)
     prev_section_grad = passed_along(b_result[None], "pp", -1)
     return (next_section_input, prev_section_grad)
 

time: 266 us -> 271 us (1.019)
  waiting for transfers between devices: 176 us -> 181 us
    ppermute x2, waiting for transfers between devices: 9.05 us -> 15.1 us  [passed_along(): return lax.ppermute(value, axis, pairs)]
  transfers between devices with their start and end apart: 40 -> 40, of which waited for: 25 -> 26; matrix products, arithmetic and copies ran while one was open for 9% -> 9% of each run, Pallas kernels for 0% -> 0%
where the time goes in v18:
time: 271 us; the launch traced here: 270 us
  waiting for transfers between devices  181 us (67%)
  starting transfers between devices  40 us (15%)
  other arithmetic  19.4 us (7%)
  matrix products  18.9 us (7%)
  local copies, waits for them, and re-layouts  9.57 us (4%)
    ppermute x26, waiting for transfers between devices, swap(): return lax.ppermute(value, axis, [(0, 1), (1, 0)])  78.3 us
    ppermute x6, waiting for transfers between devices, returned(): out.append(lax.ppermute(totals[d], 'z', [(i, i ^ d) for i in range(count)]))  50.3 us
    ppermute x6, waiting for transfers between devices, dispatch(): received = lax.ppermute(slots[d], 'z', [(i, i ^ d) for i in range(count)])  37.3 us
    ppermute x26, starting transfers between devices, swap(): return lax.ppermute(value, axis, [(0, 1), (1, 0)])  22.4 us
    ppermute x2, waiting for transfers between devices, passed_along(): return lax.ppermute(value, axis, pairs)  15.1 us
    another operation x8, other arithmetic, dispatch(): pieces.append(jnp.stack([across, swap(across, 'c')]))  8.09 us
    ppermute x6, starting transfers between devices, dispatch(): received = lax.ppermute(slots[d], 'z', [(i, i ^ d) for i in range(count)])  7.39 us
    ppermute x6, starting transfers between devices, returned(): out.append(lax.ppermute(totals[d], 'z', [(i, i ^ d) for i in range(count)]))  6.98 us
  transfers between devices with their start and end apart: 40, of which 26 were waited for; matrix products, arithmetic and copies ran while one was open for 9% of the time, Pallas kernels for 0%

profile of v18, /device:TPU:16, one launch (start us, length us, event | category | flops | bytes accessed | tf_op | source)
XLA Modules:
  0.0 270.1 jit_solution(12521064207578519758)
XLA Ops:
  3.0 1.6 convolution_convert_fusion.2
  4.7 1.6 collective-permute-start.13
  6.7 1.6 collective-permute-start.19
  8.3 1.5 collective-permute-start.11
  11.9 2.5 collective-permute-start.2
  14.4 2.9 %collective-permute-done.11 = bf16[24,7168]{1,0:T(8,128)(2,1)} collective-permute-done((bf16[24,7168]{1,0:T(8,128)(2,1)S(1)}, bf16[24,7168]{1,0:T(8,128)(2,1)}, u32[]{:S(2)}, u32[]{:S(2)}) %collective-permute-start.11) | collective-permute-done | bytes 344096 | tf_op jit(solution)/shard_map/ppermute | solution.py:13
  17.3 1.5 collective-permute-start
  19.9 1.5 collective-permute-done.13
  22.3 10.4 %collective-permute-done = bf16[24,14336]{1,0:T(8,128)(2,1)S(1)} collective-permute-done((bf16[24,14336]{1,0:T(8,128)(2,1)S(1)}, bf16[24,14336]{1,0:T(8,128)(2,1)S(1)}, u32[]{:S(2)}, u32[]{:S(2)}) %collective-permute-start) | collective-permute-done | bytes 688160 | tf_op jit(solution)/shard_map/ppermute | solution.py:13
  32.7 1.5 collective-permute-start.14
  34.3 1.3 fusion.83
  36.0 5.1 %collective-permute-done.14 = bf16[24,7168]{1,0:T(8,128)(2,1)S(1)} collective-permute-done((bf16[24,7168]{1,0:T(8,128)(2,1)}, bf16[24,7168]{1,0:T(8,128)(2,1)S(1)}, u32[]{:S(2)}, u32[]{:S(2)}) %collective-permute-start.14) | collective-permute-done | bytes 344096 | tf_op jit(solution)/shard_map/ppermute | solution.py:13
  41.1 1.5 collective-permute-start.17
  43.8 6.0 %collective-permute-done.17 = bf16[24,7168]{1,0:T(8,128)(2,1)S(1)} collective-permute-done((bf16[24,7168]{1,0:T(8,128)(2,1)S(1)}, bf16[24,7168]{1,0:T(8,128)(2,1)S(1)}, u32[]{:S(2)}, u32[]{:S(2)}) %collective-permute-start.17) | collective-permute-done | bytes 344096 | tf_op jit(solution)/shard_map/ppermute | solution.py:13
  49.8 1.7 collective-permute-start.20
  51.5 5.5 %collective-permute-done.20 = bf16[24,7168]{1,0:T(8,128)(2,1)S(1)} collective-permute-done((bf16[24,7168]{1,0:T(8,128)(2,1)S(1)}, bf16[24,7168]{1,0:T(8,128)(2,1)S(1)}, u32[]{:S(2)}, u32[]{:S(2)}) %collective-permute-start.20) | collective-permute-done | bytes 344096 | tf_op jit(solution)/shard_map/ppermute | solution.py:13
  57.8 1.3 collective-permute-done.15
  59.9 21.8 %collective-permute-done.5 = bf16[24,14336]{1,0:T(8,128)(2,1)} collective-permute-done((bf16[24,14336]{1,0:T(8,128)(2,1)S(1)}, bf16[24,14336]{1,0:T(8,128)(2,1)}, u32[]{:S(2)}, u32[]{:S(2)}) %collective-permute-start.5) | collective-permute-done | bytes 688160 | tf_op jit(solution)/shard_map/ppermute | solution.py:77
  81.6 1.5 collective-permute-start.3
  83.1 14.0 %collective-permute-done.8 = bf16[24,14336]{1,0:T(8,128)(2,1)} collective-permute-done((bf16[24,14336]{1,0:T(8,128)(2,1)S(1)}, bf16[24,14336]{1,0:T(8,128)(2,1)}, u32[]{:S(2)}, u32[]{:S(2)}) %collective-permute-start.8) | collective-permute-done | bytes 688160 | tf_op jit(solution)/shard_map/ppermute | solution.py:77
  97.1 1.5 collective-permute-start.6
  100.8 1.6 copy-done
  102.4 1.6 fusion.19
  104.4 1.6 fusion.44
  106.5 1.6 convolution_convert_fusion.1
  108.5 1.5 fusion.82
  110.6 5.2 %collective-permute-done.6 = bf16[24,14336]{1,0:T(8,128)(2,1)} collective-permute-done((bf16[24,14336]{1,0:T(8,128)(2,1)}, bf16[24,14336]{1,0:T(8,128)(2,1)}, u32[]{:S(2)}, u32[]{:S(2)}) %collective-permute-start.6) | collective-permute-done | bytes 688160 | tf_op jit(solution)/shard_map/ppermute | solution.py:13
  115.8 1.5 fusion.81
  117.4 10.8 %collective-permute-done.9 = bf16[24,14336]{1,0:T(8,128)(2,1)} collective-permute-done((bf16[24,14336]{1,0:T(8,128)(2,1)}, bf16[24,14336]{1,0:T(8,128)(2,1)}, u32[]{:S(2)}, u32[]{:S(2)}) %collective-permute-start.9) | collective-permute-done | bytes 688160 | tf_op jit(solution)/shard_map/ppermute | solution.py:13
  128.2 1.5 fusion.80
  129.8 1.6 maximum_bitcast_fusion
  134.3 1.6 collective-permute-start.23
  136.4 1.5 collective-permute-start.25
  138.4 1.5 pad_maximum_fusion
  139.9 5.4 %collective-permute-done.23 = bf16[24,7168]{1,0:T(8,128)(2,1)S(1)} collective-permute-done((bf16[24,7168]{1,0:T(8,128)(2,1)S(1)}, bf16[24,7168]{1,0:T(8,128)(2,1)S(1)}, u32[]{:S(2)}, u32[]{:S(2)}) %collective-permute-start.23) | collective-permute-done | bytes 344096 | tf_op jit(solution)/shard_map/ppermute | solution.py:13
  145.3 7.4 %collective-permute-done.24 = bf16[24,7168]{1,0:T(8,128)(2,1)S(1)} collective-permute-done((bf16[24,7168]{1,0:T(8,128)(2,1)S(1)}, bf16[24,7168]{1,0:T(8,128)(2,1)S(1)}, u32[]{:S(2)}, u32[]{:S(2)}) %collective-permute-start.24) | collective-permute-done | bytes 344096 | tf_op jit(solution)/shard_map/ppermute | solution.py:13
  152.6 7.4 %collective-permute-done.25 = bf16[24,7168]{1,0:T(8,128)(2,1)S(1)} collective-permute-done((bf16[24,7168]{1,0:T(8,128)(2,1)S(1)}, bf16[24,7168]{1,0:T(8,128)(2,1)S(1)}, u32[]{:S(2)}, u32[]{:S(2)}) %collective-permute-start.25) | collective-permute-done | bytes 344096 | tf_op jit(solution)/shard_map/ppermute | solution.py:13
  160.0 6.6 %collective-permute-done.26 = bf16[24,7168]{1,0:T(8,128)(2,1)S(1)} collective-permute-done((bf16[24,7168]{1,0:T(8,128)(2,1)S(1)}, bf16[24,7168]{1,0:T(8,128)(2,1)S(1)}, u32[]{:S(2)}, u32[]{:S(2)}) %collective-permute-start.26) | collective-permute-done | bytes 344096 | tf_op jit(solution)/shard_map/ppermute | solution.py:13
  166.6 1.1 fusion.59
  167.6 1.9 copy.35
  169.7 1.6 fusion.4
  171.3 1.6 fusion.6
  173.3 1.6 fusion.39
  175.0 1.6 fusion.16
  176.6 3.8 %add_convert_fusion = bf16[384,7168]{1,0:T(8,128)(2,1)S(1)} fusion(f32[384,7168]{1,0:T(8,128)S(1)} %fusion.16, bf16[1,7168,256]{2,1,0:T(8,128)(2,1)} %param.18, f32[384,256]{1,0:T(8,128)S(1)} %fusion.4, f32[384,256]{1,0:T(8,128)S(1)} %fusion.6), kind=kOutput, calls=%fused_computation.2 | convolution fusion | flops 1415380992 | bytes 20971520 | tf_op jit(solution)/shard_map/dot_general | solution.py:64
  181.4 1.5 collective-permute-start.32
  183.3 1.6 collective-permute-start.34
  184.9 1.1 collective-permute-done.27
  187.1 1.6 collective-permute-start.28
  189.2 7.3 %collective-permute-done.32 = bf16[24,7168]{1,0:T(8,128)(2,1)S(1)} collective-permute-done((bf16[24,7168]{1,0:T(8,128)(2,1)S(1)}, bf16[24,7168]{1,0:T(8,128)(2,1)S(1)}, u32[]{:S(2)}, u32[]{:S(2)}) %collective-permute-start.32) | collective-permute-done | bytes 344096 | tf_op jit(solution)/shard_map/ppermute | solution.py:97
  196.5 1.5 collective-permute-start.30
  198.0 8.6 %collective-permute-done.33 = bf16[24,7168]{1,0:T(8,128)(2,1)S(1)} collective-permute-done((bf16[24,7168]{1,0:T(8,128)(2,1)S(1)}, bf16[24,7168]{1,0:T(8,128)(2,1)S(1)}, u32[]{:S(2)}, u32[]{:S(2)}) %collective-permute-start.33) | collective-permute-done | bytes 344096 | tf_op jit(solution)/shard_map/ppermute | solution.py:97
  206.6 1.5 collective-permute-start.31
  208.1 6.7 %collective-permute-done.34 = bf16[24,7168]{1,0:T(8,128)(2,1)S(1)} collective-permute-done((bf16[24,7168]{1,0:T(8,128)(2,1)S(1)}, bf16[24,7168]{1,0:T(8,128)(2,1)S(1)}, u32[]{:S(2)}, u32[]{:S(2)}) %collective-permute-start.34) | collective-permute-done | bytes 344096 | tf_op jit(solution)/shard_map/ppermute | solution.py:97
  215.6 1.6 collective-permute-start.35
  217.2 2.2 collective-permute-done.31
  219.7 7.3 %collective-permute-done.35 = bf16[1,32,7168]{2,1,0:T(8,128)(2,1)S(1)} collective-permute-done((bf16[1,32,7168]{2,1,0:T(8,128)(2,1)S(1)}, bf16[1,32,7168]{2,1,0:T(8,128)(2,1)S(1)}, u32[]{:S(2)}, u32[]{:S(2)}) %collective-permute-start.35) | collective-permute-done | bytes 458784 | tf_op jit(solution)/shard_map/ppermute | solution.py:19
  227.0 1.9 collective-permute-start.37
  228.9 1.6 collective-permute-start.38
  230.4 7.5 %collective-permute-done.36 = bf16[24,7168]{1,0:T(8,128)(2,1)S(1)} collective-permute-done((bf16[24,7168]{1,0:T(8,128)(2,1)S(1)}, bf16[24,7168]{1,0:T(8,128)(2,1)S(1)}, u32[]{:S(2)}, u32[]{:S(2)}) %collective-permute-start.36) | collective-permute-done | bytes 344096 | tf_op jit(solution)/shard_map/ppermute | solution.py:97
  238.0 14.2 %collective-permute-done.37 = bf16[24,7168]{1,0:T(8,128)(2,1)S(1)} collective-permute-done((bf16[24,7168]{1,0:T(8,128)(2,1)S(1)}, bf16[24,7168]{1,0:T(8,128)(2,1)S(1)}, u32[]{:S(2)}, u32[]{:S(2)}) %collective-permute-start.37) | collective-permute-done | bytes 344096 | tf_op jit(solution)/shard_map/ppermute | solution.py:97
  252.1 6.1 %collective-permute-done.38 = bf16[24,7168]{1,0:T(8,128)(2,1)S(1)} collective-permute-done((bf16[24,7168]{1,0:T(8,128)(2,1)S(1)}, bf16[24,7168]{1,0:T(8,128)(2,1)S(1)}, u32[]{:S(2)}, u32[]{:S(2)}) %collective-permute-start.38) | collective-permute-done | bytes 344096 | tf_op jit(solution)/shard_map/ppermute | solution.py:97
  259.1 1.6 collective-permute-start.39
  260.7 7.8 %collective-permute-done.39 = bf16[1,32,7168]{2,1,0:T(8,128)(2,1)S(1)} collective-permute-done((bf16[1,32,7168]{2,1,0:T(8,128)(2,1)S(1)}, bf16[1,32,7168]{2,1,0:T(8,128)(2,1)S(1)}, u32[]{:S(2)}, u32[]{:S(2)}) %collective-permute-start.39) | collective-permute-done | bytes 458784 | tf_op jit(solution)/shard_map/ppermute | solution.py:19
  (107 shorter events, 25.0 us)
Async XLA Ops:
  0.6 9.9 %copy-start.12 = (f32[1,32,2]{1,2,0:T(2,128)S(1)}, f32[1,32,2]{1,2,0:T(2,128)}, u32[]{:S(2)}) copy-start(f32[1,32,2]{1,2,0:T(2,128)} %param.16) | copy-start | bytes 772
  0.6 10.0 %copy-start.8 = (bf16[1,32,7168]{2,1,0:T(8,128)(2,1)S(1)}, bf16[1,32,7168]{2,1,0:T(8,128)(2,1)}, u32[]{:S(2)}) copy-start(bf16[1,32,7168]{2,1,0:T(8,128)(2,1)} %param.13) | copy-start | bytes 1376260
  0.7 10.0 %copy-start.6 = (bf16[1,32,7168]{2,1,0:T(8,128)(2,1)S(1)}, bf16[1,32,7168]{2,1,0:T(8,128)(2,1)}, u32[]{:S(2)}) copy-start(bf16[1,32,7168]{2,1,0:T(8,128)(2,1)} %param.14) | copy-start | bytes 1376260
  4.7 16.7 %collective-permute-start.13 = (bf16[24,7168]{1,0:T(8,128)(2,1)S(1)}, bf16[24,7168]{1,0:T(8,128)(2,1)}, u32[]{:S(2)}, u32[]{:S(2)}) collective-permute-start(bf16[24,7168]{1,0:T(8,128)(2,1)S(1)} %get-tuple-element.58), channel_id=1, source_target_pairs={{0,4},{4,0},{8,12},{12,8},{1,5},{5,1},{9,13},{13,9},{2,6},{6,2},{1... | collective-permute-start | bytes 1032200 | tf_op jit(solution)/shard_map/ppermute | solution.py:77
  6.4 29.2 %collective-permute-start.16 = (bf16[24,7168]{1,0:T(8,128)(2,1)S(1)}, bf16[24,7168]{1,0:T(8,128)(2,1)S(1)}, u32[]{:S(2)}, u32[]{:S(2)}) collective-permute-start(bf16[24,7168]{1,0:T(8,128)(2,1)S(1)} %get-tuple-element.57), channel_id=1, source_target_pairs={{0,8},{4,12},{8,0},{12,4},{1,9},{5,13},{9,1},{13,5},{2,10},{6,14},... | collective-permute-start | bytes 1032200 | tf_op jit(solution)/shard_map/ppermute | solution.py:77
  6.7 37.0 %collective-permute-start.19 = (bf16[24,7168]{1,0:T(8,128)(2,1)S(1)}, bf16[24,7168]{1,0:T(8,128)(2,1)S(1)}, u32[]{:S(2)}, u32[]{:S(2)}) collective-permute-start(bf16[24,7168]{1,0:T(8,128)(2,1)S(1)} %get-tuple-element.56), channel_id=1, source_target_pairs={{0,12},{4,8},{8,4},{12,0},{1,13},{5,9},{9,5},{13,1},{2,14},{6,10},... | collective-permute-start | bytes 1032200 | tf_op jit(solution)/shard_map/ppermute | solution.py:77
  8.3 9.1 %collective-permute-start.11 = (bf16[24,7168]{1,0:T(8,128)(2,1)S(1)}, bf16[24,7168]{1,0:T(8,128)(2,1)}, u32[]{:S(2)}, u32[]{:S(2)}) collective-permute-start(bf16[24,7168]{1,0:T(8,128)(2,1)S(1)} %get-tuple-element.59), channel_id=1, source_target_pairs={{0,2},{2,0},{1,3},{3,1},{4,6},{6,4},{5,7},{7,5},{8,10},{10,8},{9,1... | collective-permute-start | bytes 1032200 | tf_op jit(solution)/shard_map/ppermute | solution.py:13
  11.9 47.6 %collective-permute-start.2 = (bf16[24,14336]{1,0:T(8,128)(2,1)S(1)}, bf16[24,14336]{1,0:T(8,128)(2,1)}, u32[]{:S(2)}, u32[]{:S(2)}) collective-permute-start(bf16[24,14336]{1,0:T(8,128)(2,1)S(1)} %get-tuple-element.53), channel_id=1, source_target_pairs={{0,4},{4,0},{8,12},{12,8},{1,5},{5,1},{9,13},{13,9},{2,6},{6,2},{1... | collective-permute-start | bytes 2064392 | tf_op jit(solution)/shard_map/ppermute | solution.py:77
  17.3 15.4 %collective-permute-start = (bf16[24,14336]{1,0:T(8,128)(2,1)S(1)}, bf16[24,14336]{1,0:T(8,128)(2,1)S(1)}, u32[]{:S(2)}, u32[]{:S(2)}) collective-permute-start(bf16[24,14336]{1,0:T(8,128)(2,1)S(1)} %get-tuple-element.54), channel_id=1, source_target_pairs={{0,2},{2,0},{1,3},{3,1},{4,6},{6,4},{5,7},{7,5},{8,10},{10,8},{9,1... | collective-permute-start | bytes 2064392 | tf_op jit(solution)/shard_map/ppermute | solution.py:13
  21.5 60.2 %collective-permute-start.5 = (bf16[24,14336]{1,0:T(8,128)(2,1)S(1)}, bf16[24,14336]{1,0:T(8,128)(2,1)}, u32[]{:S(2)}, u32[]{:S(2)}) collective-permute-start(bf16[24,14336]{1,0:T(8,128)(2,1)S(1)} %get-tuple-element.52), channel_id=1, source_target_pairs={{0,8},{4,12},{8,0},{12,4},{1,9},{5,13},{9,1},{13,5},{2,10},{6,14},... | collective-permute-start | bytes 2064392 | tf_op jit(solution)/shard_map/ppermute | solution.py:77
  32.7 8.4 %collective-permute-start.14 = (bf16[24,7168]{1,0:T(8,128)(2,1)}, bf16[24,7168]{1,0:T(8,128)(2,1)S(1)}, u32[]{:S(2)}, u32[]{:S(2)}) collective-permute-start(bf16[24,7168]{1,0:T(8,128)(2,1)} %collective-permute-done.13), channel_id=1, source_target_pairs={{0,2},{2,0},{1,3},{3,1},{4,6},{6,4},{5,7},{7,5},{8,10},{10,8},{9,1... | collective-permute-start | bytes 1032200 | tf_op jit(solution)/shard_map/ppermute | solution.py:13
  35.6 61.5 %collective-permute-start.8 = (bf16[24,14336]{1,0:T(8,128)(2,1)S(1)}, bf16[24,14336]{1,0:T(8,128)(2,1)}, u32[]{:S(2)}, u32[]{:S(2)}) collective-permute-start(bf16[24,14336]{1,0:T(8,128)(2,1)S(1)} %get-tuple-element.51), channel_id=1, source_target_pairs={{0,12},{4,8},{8,4},{12,0},{1,13},{5,9},{9,5},{13,1},{2,14},{6,10},... | collective-permute-start | bytes 2064392 | tf_op jit(solution)/shard_map/ppermute | solution.py:77
  41.1 8.7 %collective-permute-start.17 = (bf16[24,7168]{1,0:T(8,128)(2,1)S(1)}, bf16[24,7168]{1,0:T(8,128)(2,1)S(1)}, u32[]{:S(2)}, u32[]{:S(2)}) collective-permute-start(bf16[24,7168]{1,0:T(8,128)(2,1)S(1)} %collective-permute-done.16), channel_id=1, source_target_pairs={{0,2},{2,0},{1,3},{3,1},{4,6},{6,4},{5,7},{7,5},{8,10},{10,8},{9,1... | collective-permute-start | bytes 1032200 | tf_op jit(solution)/shard_map/ppermute | solution.py:13
  43.7 13.4 %collective-permute-start.12 = (bf16[2,24,7168]{2,1,0:T(8,128)(2,1)S(1)}, bf16[2,24,7168]{2,1,0:T(8,128)(2,1)S(1)}, u32[]{:S(2)}, u32[]{:S(2)}) collective-permute-start(bf16[2,24,7168]{2,1,0:T(8,128)(2,1)S(1)} %get-tuple-element.69), channel_id=1, source_target_pairs={{0,1},{1,0},{2,3},{3,2},{4,5},{5,4},{6,7},{7,6},{8,9},{9,8},{10,11... | collective-permute-start | bytes 2064392 | tf_op jit(solution)/shard_map/ppermute | solution.py:13
  49.8 7.2 %collective-permute-start.20 = (bf16[24,7168]{1,0:T(8,128)(2,1)S(1)}, bf16[24,7168]{1,0:T(8,128)(2,1)S(1)}, u32[]{:S(2)}, u32[]{:S(2)}) collective-permute-start(bf16[24,7168]{1,0:T(8,128)(2,1)S(1)} %collective-permute-done.19), channel_id=1, source_target_pairs={{0,2},{2,0},{1,3},{3,1},{4,6},{6,4},{5,7},{7,5},{8,10},{10,8},{9,1... | collective-permute-start | bytes 1032200 | tf_op jit(solution)/shard_map/ppermute | solution.py:13
  57.0 2.1 collective-permute-start.15
  57.1 41.5 %collective-permute-start.18 = (bf16[2,24,7168]{2,1,0:T(8,128)(2,1)S(1)}, bf16[2,24,7168]{2,1,0:T(8,128)(2,1)S(1)}, u32[]{:S(2)}, u32[]{:S(2)}) collective-permute-start(bf16[2,24,7168]{2,1,0:T(8,128)(2,1)S(1)} %get-tuple-element.73), channel_id=1, source_target_pairs={{0,1},{1,0},{2,3},{3,2},{4,5},{5,4},{6,7},{7,6},{8,9},{9,8},{10,11... | collective-permute-start | bytes 2064392 | tf_op jit(solution)/shard_map/ppermute | solution.py:13
  59.2 40.1 %collective-permute-start.21 = (bf16[2,24,7168]{2,1,0:T(8,128)(2,1)S(1)}, bf16[2,24,7168]{2,1,0:T(8,128)(2,1)S(1)}, u32[]{:S(2)}, u32[]{:S(2)}) collective-permute-start(bf16[2,24,7168]{2,1,0:T(8,128)(2,1)S(1)} %get-tuple-element.75), channel_id=1, source_target_pairs={{0,1},{1,0},{2,3},{3,2},{4,5},{5,4},{6,7},{7,6},{8,9},{9,8},{10,11... | collective-permute-start | bytes 2064392 | tf_op jit(solution)/shard_map/ppermute | solution.py:13
  59.4 70.3 %collective-permute-start.1 = (bf16[2,24,14336]{2,1,0:T(8,128)(2,1)}, bf16[2,24,14336]{2,1,0:T(8,128)(2,1)}, u32[]{:S(2)}, u32[]{:S(2)}) collective-permute-start(bf16[2,24,14336]{2,1,0:T(8,128)(2,1)} %get-tuple-element.61), channel_id=1, source_target_pairs={{0,1},{1,0},{2,3},{3,2},{4,5},{5,4},{6,7},{7,6},{8,9},{9,8},{10,11... | collective-permute-start | bytes 4128776 | tf_op jit(solution)/shard_map/ppermute | solution.py:13
  81.6 26.9 %collective-permute-start.3 = (bf16[24,14336]{1,0:T(8,128)(2,1)}, bf16[24,14336]{1,0:T(8,128)(2,1)}, u32[]{:S(2)}, u32[]{:S(2)}) collective-permute-start(bf16[24,14336]{1,0:T(8,128)(2,1)} %collective-permute-done.2), channel_id=1, source_target_pairs={{0,2},{2,0},{1,3},{3,1},{4,6},{6,4},{5,7},{7,5},{8,10},{10,8},{9,1... | collective-permute-start | bytes 2064392 | tf_op jit(solution)/shard_map/ppermute | solution.py:13
  97.1 18.7 %collective-permute-start.6 = (bf16[24,14336]{1,0:T(8,128)(2,1)}, bf16[24,14336]{1,0:T(8,128)(2,1)}, u32[]{:S(2)}, u32[]{:S(2)}) collective-permute-start(bf16[24,14336]{1,0:T(8,128)(2,1)} %collective-permute-done.5), channel_id=1, source_target_pairs={{0,2},{2,0},{1,3},{3,1},{4,6},{6,4},{5,7},{7,5},{8,10},{10,8},{9,1... | collective-permute-start | bytes 2064392 | tf_op jit(solution)/shard_map/ppermute | solution.py:13
  98.6 29.6 %collective-permute-start.9 = (bf16[24,14336]{1,0:T(8,128)(2,1)}, bf16[24,14336]{1,0:T(8,128)(2,1)}, u32[]{:S(2)}, u32[]{:S(2)}) collective-permute-start(bf16[24,14336]{1,0:T(8,128)(2,1)} %collective-permute-done.8), channel_id=1, source_target_pairs={{0,2},{2,0},{1,3},{3,1},{4,6},{6,4},{5,7},{7,5},{8,10},{10,8},{9,1... | collective-permute-start | bytes 2064392 | tf_op jit(solution)/shard_map/ppermute | solution.py:13
  100.4 2.0 copy-start
  102.4 2.0 copy-start.1
  104.4 2.0 copy-start.3
  108.4 24.7 %collective-permute-start.22 = (bf16[2,4,24,7168]{3,2,1,0:T(8,128)(2,1)S(1)}, bf16[2,4,24,7168]{3,2,1,0:T(8,128)(2,1)S(1)}, u32[]{:S(2)}, u32[]{:S(2)}) collective-permute-start(bf16[2,4,24,7168]{3,2,1,0:T(8,128)(2,1)S(1)} %bitcast.207), channel_id=1, source_target_pairs={{0,1},{1,0},{2,3},{3,2},{4,5},{5,4},{6,7},{7,6},{8,9},{9,8},{10,11... | collective-permute-start | bytes 8257544 | tf_op jit(solution)/shard_map/ppermute | solution.py:13
  110.0 21.3 %collective-permute-start.4 = (bf16[2,24,14336]{2,1,0:T(8,128)(2,1)S(1)}, bf16[2,24,14336]{2,1,0:T(8,128)(2,1)S(1)}, u32[]{:S(2)}, u32[]{:S(2)}) collective-permute-start(bf16[2,24,14336]{2,1,0:T(8,128)(2,1)S(1)} %get-tuple-element.63), channel_id=1, source_target_pairs={{0,1},{1,0},{2,3},{3,2},{4,5},{5,4},{6,7},{7,6},{8,9},{9,8},{10,11... | collective-permute-start | bytes 4128776 | tf_op jit(solution)/shard_map/ppermute | solution.py:13
  117.3 14.4 %collective-permute-start.7 = (bf16[2,24,14336]{2,1,0:T(8,128)(2,1)S(1)}, bf16[2,24,14336]{2,1,0:T(8,128)(2,1)S(1)}, u32[]{:S(2)}, u32[]{:S(2)}) collective-permute-start(bf16[2,24,14336]{2,1,0:T(8,128)(2,1)S(1)} %get-tuple-element.65), channel_id=1, source_target_pairs={{0,1},{1,0},{2,3},{3,2},{4,5},{5,4},{6,7},{7,6},{8,9},{9,8},{10,11... | collective-permute-start | bytes 4128776 | tf_op jit(solution)/shard_map/ppermute | solution.py:13
  129.7 3.2 %collective-permute-start.10 = (bf16[2,24,14336]{2,1,0:T(8,128)(2,1)S(1)}, bf16[2,24,14336]{2,1,0:T(8,128)(2,1)S(1)}, u32[]{:S(2)}, u32[]{:S(2)}) collective-permute-start(bf16[2,24,14336]{2,1,0:T(8,128)(2,1)S(1)} %get-tuple-element.67), channel_id=1, source_target_pairs={{0,1},{1,0},{2,3},{3,2},{4,5},{5,4},{6,7},{7,6},{8,9},{9,8},{10,11... | collective-permute-start | bytes 4128776 | tf_op jit(solution)/shard_map/ppermute | solution.py:13
  134.3 11.0 %collective-permute-start.23 = (bf16[24,7168]{1,0:T(8,128)(2,1)S(1)}, bf16[24,7168]{1,0:T(8,128)(2,1)S(1)}, u32[]{:S(2)}, u32[]{:S(2)}) collective-permute-start(bf16[24,7168]{1,0:T(8,128)(2,1)S(1)} %get-tuple-element.49), channel_id=1, source_target_pairs={{0,2},{2,0},{1,3},{3,1},{4,6},{6,4},{5,7},{7,5},{8,10},{10,8},{9,1... | collective-permute-start | bytes 1032200 | tf_op jit(solution)/shard_map/ppermute | solution.py:13
  135.9 16.8 %collective-permute-start.24 = (bf16[24,7168]{1,0:T(8,128)(2,1)S(1)}, bf16[24,7168]{1,0:T(8,128)(2,1)S(1)}, u32[]{:S(2)}, u32[]{:S(2)}) collective-permute-start(bf16[24,7168]{1,0:T(8,128)(2,1)S(1)} %get-tuple-element.48), channel_id=1, source_target_pairs={{0,2},{2,0},{1,3},{3,1},{4,6},{6,4},{5,7},{7,5},{8,10},{10,8},{9,1... | collective-permute-start | bytes 1032200 | tf_op jit(solution)/shard_map/ppermute | solution.py:13
  136.4 23.6 %collective-permute-start.25 = (bf16[24,7168]{1,0:T(8,128)(2,1)S(1)}, bf16[24,7168]{1,0:T(8,128)(2,1)S(1)}, u32[]{:S(2)}, u32[]{:S(2)}) collective-permute-start(bf16[24,7168]{1,0:T(8,128)(2,1)S(1)} %get-tuple-element.47), channel_id=1, source_target_pairs={{0,2},{2,0},{1,3},{3,1},{4,6},{6,4},{5,7},{7,5},{8,10},{10,8},{9,1... | collective-permute-start | bytes 1032200 | tf_op jit(solution)/shard_map/ppermute | solution.py:13
  137.9 28.7 %collective-permute-start.26 = (bf16[24,7168]{1,0:T(8,128)(2,1)S(1)}, bf16[24,7168]{1,0:T(8,128)(2,1)S(1)}, u32[]{:S(2)}, u32[]{:S(2)}) collective-permute-start(bf16[24,7168]{1,0:T(8,128)(2,1)S(1)} %get-tuple-element.46), channel_id=1, source_target_pairs={{0,2},{2,0},{1,3},{3,1},{4,6},{6,4},{5,7},{7,5},{8,10},{10,8},{9,1... | collective-permute-start | bytes 1032200 | tf_op jit(solution)/shard_map/ppermute | solution.py:13
  167.6 2.0 copy-start.4
  171.3 2.0 copy-start.2
  180.4 1.0 copy-start.11
  180.4 2.4 copy-start.10
  180.4 2.9 %copy-start.9 = (bf16[24,7168]{1,0:T(8,128)(2,1)S(1)}, bf16[24,7168]{1,0:T(8,128)(2,1)}, u32[]{:S(2)}) copy-start(bf16[24,7168]{1,0:T(8,128)(2,1)} %get-tuple-element.16) | copy-start | bytes 1032196
  180.8 5.2 %collective-permute-start.27 = (bf16[2,4,24,7168]{3,2,1,0:T(8,128)(2,1)S(1)}, bf16[2,4,24,7168]{3,2,1,0:T(8,128)(2,1)S(1)}, u32[]{:S(2)}, u32[]{:S(2)}) collective-permute-start(bf16[2,4,24,7168]{3,2,1,0:T(8,128)(2,1)S(1)} %bitcast.208), channel_id=1, source_target_pairs={{0,1},{1,0},{2,3},{3,2},{4,5},{5,4},{6,7},{7,6},{8,9},{9,8},{10,11... | collective-permute-start | bytes 8257544 | tf_op jit(solution)/shard_map/ppermute | solution.py:13
  181.4 15.1 %collective-permute-start.32 = (bf16[24,7168]{1,0:T(8,128)(2,1)S(1)}, bf16[24,7168]{1,0:T(8,128)(2,1)S(1)}, u32[]{:S(2)}, u32[]{:S(2)}) collective-permute-start(bf16[24,7168]{1,0:T(8,128)(2,1)S(1)} %copy-done.11), channel_id=1, source_target_pairs={{0,4},{4,0},{8,12},{12,8},{1,5},{5,1},{9,13},{13,9},{2,6},{6,2},{1... | collective-permute-start | bytes 1032200 | tf_op jit(solution)/shard_map/ppermute | solution.py:97
  182.9 23.7 %collective-permute-start.33 = (bf16[24,7168]{1,0:T(8,128)(2,1)S(1)}, bf16[24,7168]{1,0:T(8,128)(2,1)S(1)}, u32[]{:S(2)}, u32[]{:S(2)}) collective-permute-start(bf16[24,7168]{1,0:T(8,128)(2,1)S(1)} %copy-done.10), channel_id=1, source_target_pairs={{0,8},{4,12},{8,0},{12,4},{1,9},{5,13},{9,1},{13,5},{2,10},{6,14},... | collective-permute-start | bytes 1032200 | tf_op jit(solution)/shard_map/ppermute | solution.py:97
  183.3 31.4 %collective-permute-start.34 = (bf16[24,7168]{1,0:T(8,128)(2,1)S(1)}, bf16[24,7168]{1,0:T(8,128)(2,1)S(1)}, u32[]{:S(2)}, u32[]{:S(2)}) collective-permute-start(bf16[24,7168]{1,0:T(8,128)(2,1)S(1)} %copy-done.9), channel_id=1, source_target_pairs={{0,12},{4,8},{8,4},{12,0},{1,13},{5,9},{9,5},{13,1},{2,14},{6,10},... | collective-permute-start | bytes 1032200 | tf_op jit(solution)/shard_map/ppermute | solution.py:97
  187.0 27.9 %copy-start.5 = (bf16[1,32,7168]{2,1,0:T(8,128)(2,1)S(1)}, bf16[1,32,7168]{2,1,0:T(8,128)(2,1)}, u32[]{:S(2)}) copy-start(bf16[1,32,7168]{2,1,0:T(8,128)(2,1)} %param.10) | copy-start | bytes 1376260
  187.1 30.1 %collective-permute-start.28 = (bf16[24,7168]{1,0:T(8,128)(2,1)S(1)}, bf16[24,7168]{1,0:T(8,128)(2,1)S(1)}, u32[]{:S(2)}, u32[]{:S(2)}) collective-permute-start(bf16[24,7168]{1,0:T(8,128)(2,1)S(1)} %get-tuple-element.45), channel_id=1, source_target_pairs={{0,2},{2,0},{1,3},{3,1},{4,6},{6,4},{5,7},{7,5},{8,10},{10,8},{9,1... | collective-permute-start | bytes 1032200 | tf_op jit(solution)/shard_map/ppermute | solution.py:13
  188.7 28.5 %collective-permute-start.29 = (bf16[24,7168]{1,0:T(8,128)(2,1)S(1)}, bf16[24,7168]{1,0:T(8,128)(2,1)S(1)}, u32[]{:S(2)}, u32[]{:S(2)}) collective-permute-start(bf16[24,7168]{1,0:T(8,128)(2,1)S(1)} %get-tuple-element.44), channel_id=1, source_target_pairs={{0,2},{2,0},{1,3},{3,1},{4,6},{6,4},{5,7},{7,5},{8,10},{10,8},{9,1... | collective-permute-start | bytes 1032200 | tf_op jit(solution)/shard_map/ppermute | solution.py:13
  196.5 20.7 %collective-permute-start.30 = (bf16[24,7168]{1,0:T(8,128)(2,1)S(1)}, bf16[24,7168]{1,0:T(8,128)(2,1)S(1)}, u32[]{:S(2)}, u32[]{:S(2)}) collective-permute-start(bf16[24,7168]{1,0:T(8,128)(2,1)S(1)} %get-tuple-element.43), channel_id=1, source_target_pairs={{0,2},{2,0},{1,3},{3,1},{4,6},{6,4},{5,7},{7,5},{8,10},{10,8},{9,1... | collective-permute-start | bytes 1032200 | tf_op jit(solution)/shard_map/ppermute | solution.py:13
  206.6 12.9 %collective-permute-start.31 = (bf16[24,7168]{1,0:T(8,128)(2,1)S(1)}, bf16[24,7168]{1,0:T(8,128)(2,1)S(1)}, u32[]{:S(2)}, u32[]{:S(2)}) collective-permute-start(bf16[24,7168]{1,0:T(8,128)(2,1)S(1)} %get-tuple-element.42), channel_id=1, source_target_pairs={{0,2},{2,0},{1,3},{3,1},{4,6},{6,4},{5,7},{7,5},{8,10},{10,8},{9,1... | collective-permute-start | bytes 1032200 | tf_op jit(solution)/shard_map/ppermute | solution.py:13
  215.6 11.4 %collective-permute-start.35 = (bf16[1,32,7168]{2,1,0:T(8,128)(2,1)S(1)}, bf16[1,32,7168]{2,1,0:T(8,128)(2,1)S(1)}, u32[]{:S(2)}, u32[]{:S(2)}) collective-permute-start(bf16[1,32,7168]{2,1,0:T(8,128)(2,1)S(1)} %fusion.3), channel_id=1, source_target_pairs={{0,16},{16,0},{1,17},{17,1},{2,18},{18,2},{3,19},{19,3},{4,20},{20... | collective-permute-start | bytes 1376264 | tf_op jit(solution)/shard_map/ppermute | solution.py:19
  219.7 38.7 %copy-start.7 = (bf16[1,32,7168]{2,1,0:T(8,128)(2,1)S(1)}, bf16[1,32,7168]{2,1,0:T(8,128)(2,1)}, u32[]{:S(2)}) copy-start(bf16[1,32,7168]{2,1,0:T(8,128)(2,1)} %param.14) | copy-start | bytes 1376260
  227.0 11.0 %collective-permute-start.36 = (bf16[24,7168]{1,0:T(8,128)(2,1)S(1)}, bf16[24,7168]{1,0:T(8,128)(2,1)S(1)}, u32[]{:S(2)}, u32[]{:S(2)}) collective-permute-start(bf16[24,7168]{1,0:T(8,128)(2,1)S(1)} %get-tuple-element.19), channel_id=1, source_target_pairs={{0,4},{4,0},{8,12},{12,8},{1,5},{5,1},{9,13},{13,9},{2,6},{6,2},{1... | collective-permute-start | bytes 1032200 | tf_op jit(solution)/shard_map/ppermute | solution.py:97
  227.0 25.2 %collective-permute-start.37 = (bf16[24,7168]{1,0:T(8,128)(2,1)S(1)}, bf16[24,7168]{1,0:T(8,128)(2,1)S(1)}, u32[]{:S(2)}, u32[]{:S(2)}) collective-permute-start(bf16[24,7168]{1,0:T(8,128)(2,1)S(1)} %get-tuple-element.20), channel_id=1, source_target_pairs={{0,8},{4,12},{8,0},{12,4},{1,9},{5,13},{9,1},{13,5},{2,10},{6,14},... | collective-permute-start | bytes 1032200 | tf_op jit(solution)/shard_map/ppermute | solution.py:97
  228.9 29.3 %collective-permute-start.38 = (bf16[24,7168]{1,0:T(8,128)(2,1)S(1)}, bf16[24,7168]{1,0:T(8,128)(2,1)S(1)}, u32[]{:S(2)}, u32[]{:S(2)}) collective-permute-start(bf16[24,7168]{1,0:T(8,128)(2,1)S(1)} %get-tuple-element.21), channel_id=1, source_target_pairs={{0,12},{4,8},{8,4},{12,0},{1,13},{5,9},{9,5},{13,1},{2,14},{6,10},... | collective-permute-start | bytes 1032200 | tf_op jit(solution)/shard_map/ppermute | solution.py:97
  259.1 9.4 %collective-permute-start.39 = (bf16[1,32,7168]{2,1,0:T(8,128)(2,1)S(1)}, bf16[1,32,7168]{2,1,0:T(8,128)(2,1)S(1)}, u32[]{:S(2)}, u32[]{:S(2)}) collective-permute-start(bf16[1,32,7168]{2,1,0:T(8,128)(2,1)S(1)} %fusion.2), channel_id=1, source_target_pairs={{0,16},{16,0},{1,17},{17,1},{2,18},{18,2},{3,19},{19,3},{4,20},{20... | collective-permute-start | bytes 1376264 | tf_op jit(solution)/shard_map/ppermute | solution.py:19

commit v19 on v16

--- a/solution.py
+++ b/solution.py
@@ -132,7 +132,9 @@
     b_rows = jnp.stack(b_near + [spread(r) for r in b_far], axis=2)
     f_out = returned(f_totals)
     b_partial = backward_rows(b_rows.reshape(-1, 2 * width), w_gate, w_up, w_down)
-    b_out = returned(reduce_group(b_partial.reshape(2, 2, experts, capacity, width)))
+    b_totals = reduce_group(b_partial.reshape(2, 2, experts, capacity, width))
+    b_totals, f_out = lax.optimization_barrier((b_totals, f_out))
+    b_out = returned(b_totals)
     high = lax.Precision.HIGHEST
     f_mixed = jnp.dot(
         f_weights, f_out.reshape(experts * capacity, width).astype(jnp.float32), precision=high

time: 275 us -> 270 us (0.982)
  starting transfers between devices: 52.3 us -> 40.3 us
  waiting for transfers between devices: 175 us -> 180 us
    ppermute x26, waiting for transfers between devices: 110 us -> 90 us  [swap(): return lax.ppermute(value, axis, [(0, 1), (1, 0)])]
    ppermute x6, waiting for transfers between devices: 32.5 us -> 50.4 us  [returned(): out.append(lax.ppermute(totals[d], 'z', [(i, i ^ d) for i in range(count)]))]
    ppermute x6, starting transfers between devices: 19.1 us -> 8.02 us  [returned(): out.append(lax.ppermute(totals[d], 'z', [(i, i ^ d) for i in range(count)]))]
    ppermute x6, waiting for transfers between devices: 21.4 us -> 30.7 us  [z_round(): return lax.ppermute(chunk, 'z', [(i, i ^ d) for i in range(count)])]
  transfers between devices with their start and end apart: 40 -> 40, of which waited for: 24 -> 25; matrix products, arithmetic and copies ran while one was open for 8% -> 9% of each run, Pallas kernels for 0% -> 0%
where the time goes in v19:
time: 270 us; the launch traced here: 269 us
  waiting for transfers between devices  180 us (67%)
  starting transfers between devices  40.3 us (15%)
  matrix products  18.9 us (7%)
  other arithmetic  17.7 us (7%)
  local copies, waits for them, and re-layouts  10.3 us (4%)
    ppermute x26, waiting for transfers between devices, swap(): return lax.ppermute(value, axis, [(0, 1), (1, 0)])  90 us
    ppermute x6, waiting for transfers between devices, returned(): out.append(lax.ppermute(totals[d], 'z', [(i, i ^ d) for i in range(count)]))  50.4 us
    ppermute x6, waiting for transfers between devices, z_round(): return lax.ppermute(chunk, 'z', [(i, i ^ d) for i in range(count)])  30.7 us
    ppermute x26, starting transfers between devices, swap(): return lax.ppermute(value, axis, [(0, 1), (1, 0)])  20.8 us
    ppermute x2, waiting for transfers between devices, passed_along(): return lax.ppermute(value, axis, pairs)  9.34 us
    ppermute x6, starting transfers between devices, z_round(): return lax.ppermute(chunk, 'z', [(i, i ^ d) for i in range(count)])  8.32 us
    ppermute x6, starting transfers between devices, returned(): out.append(lax.ppermute(totals[d], 'z', [(i, i ^ d) for i in range(count)]))  8.02 us
    another operation x8, other arithmetic, spread(): return jnp.stack([across, swap(across, 'c')])  7.66 us
  transfers between devices with their start and end apart: 40, of which 25 were waited for; matrix products, arithmetic and copies ran while one was open for 9% of the time, Pallas kernels for 0%

profile of v19, /device:TPU:16, one launch (start us, length us, event | category | flops | bytes accessed | tf_op | source)
XLA Modules:
  0.0 268.8 jit_solution(4715409437811185748)
XLA Ops:
  3.0 1.6 convolution_convert_fusion.2
  5.2 3.5 %collective-permute-start.12 = (bf16[24,7168]{1,0:T(8,128)(2,1)S(1)}, bf16[24,7168]{1,0:T(8,128)(2,1)S(1)}, u32[]{:S(2)}, u32[]{:S(2)}) collective-permute-start(bf16[24,7168]{1,0:T(8,128)(2,1)S(1)} %get-tuple-element.67), channel_id=1, source_target_pairs={{0,8},{4,12},{8,0},{12,4},{1,9},{5,13},{9,1},{13,5},{2,10},{6,14},... | collective-permute-start | bytes 1032200 | tf_op jit(solution)/shard_map/ppermute | solution.py:74
  8.7 1.5 collective-permute-start.7
  12.0 1.2 slice_bitcast_fusion.17
  13.8 16.4 %collective-permute-done.9 = bf16[24,7168]{1,0:T(8,128)(2,1)} collective-permute-done((bf16[24,7168]{1,0:T(8,128)(2,1)S(1)}, bf16[24,7168]{1,0:T(8,128)(2,1)}, u32[]{:S(2)}, u32[]{:S(2)}) %collective-permute-start.9) | collective-permute-done | bytes 344096 | tf_op jit(solution)/shard_map/ppermute | solution.py:74
  30.2 1.7 collective-permute-start.10
  31.9 1.1 fusion.77
  33.4 8.0 %collective-permute-done.10 = bf16[24,7168]{1,0:T(8,128)(2,1)S(1)} collective-permute-done((bf16[24,7168]{1,0:T(8,128)(2,1)}, bf16[24,7168]{1,0:T(8,128)(2,1)S(1)}, u32[]{:S(2)}, u32[]{:S(2)}) %collective-permute-start.10) | collective-permute-done | bytes 344096 | tf_op jit(solution)/shard_map/ppermute | solution.py:13
  41.4 1.7 collective-permute-start.16
  43.1 1.1 fusion.76
  44.2 6.3 %collective-permute-done.12 = bf16[24,7168]{1,0:T(8,128)(2,1)S(1)} collective-permute-done((bf16[24,7168]{1,0:T(8,128)(2,1)S(1)}, bf16[24,7168]{1,0:T(8,128)(2,1)S(1)}, u32[]{:S(2)}, u32[]{:S(2)}) %collective-permute-start.12) | collective-permute-done | bytes 344096 | tf_op jit(solution)/shard_map/ppermute | solution.py:74
  50.4 10.5 %collective-permute-done.16 = bf16[24,7168]{1,0:T(8,128)(2,1)S(1)} collective-permute-done((bf16[24,7168]{1,0:T(8,128)(2,1)S(1)}, bf16[24,7168]{1,0:T(8,128)(2,1)S(1)}, u32[]{:S(2)}, u32[]{:S(2)}) %collective-permute-start.16) | collective-permute-done | bytes 344096 | tf_op jit(solution)/shard_map/ppermute | solution.py:13
  60.9 1.4 collective-permute-start.13
  62.4 6.1 %collective-permute-done.13 = bf16[24,7168]{1,0:T(8,128)(2,1)S(1)} collective-permute-done((bf16[24,7168]{1,0:T(8,128)(2,1)S(1)}, bf16[24,7168]{1,0:T(8,128)(2,1)S(1)}, u32[]{:S(2)}, u32[]{:S(2)}) %collective-permute-start.13) | collective-permute-done | bytes 344096 | tf_op jit(solution)/shard_map/ppermute | solution.py:13
  69.4 1.2 collective-permute-done.17
  70.7 1.1 collective-permute-start.3
  72.8 0.9 pad_maximum_fusion.1
  74.2 1.6 copy-done
  75.7 1.6 fusion.19
  77.8 1.6 fusion.44
  79.8 1.6 convolution_convert_fusion.1
  82.0 2.4 fusion.83
  84.8 3.7 %collective-permute-done.3 = bf16[24,14336]{1,0:T(8,128)(2,1)} collective-permute-done((bf16[24,14336]{1,0:T(8,128)(2,1)}, bf16[24,14336]{1,0:T(8,128)(2,1)}, u32[]{:S(2)}, u32[]{:S(2)}) %collective-permute-start.3) | collective-permute-done | bytes 688160 | tf_op jit(solution)/shard_map/ppermute | solution.py:13
  88.5 1.5 fusion.82
  90.0 1.0 fusion.78
  91.1 1.2 collective-permute-start.22
  92.3 0.9 collective-permute-start.21
  93.2 1.1 collective-permute-start.20
  94.3 0.9 collective-permute-start.19
  95.5 6.7 %collective-permute-done.22 = bf16[24,7168]{1,0:T(8,128)(2,1)S(1)} collective-permute-done((bf16[24,7168]{1,0:T(8,128)(2,1)S(1)}, bf16[24,7168]{1,0:T(8,128)(2,1)S(1)}, u32[]{:S(2)}, u32[]{:S(2)}) %collective-permute-start.22) | collective-permute-done | bytes 344096 | tf_op jit(solution)/shard_map/ppermute | solution.py:13
  102.2 3.8 %collective-permute-start.5 = (bf16[24,14336]{1,0:T(8,128)(2,1)S(1)}, bf16[24,14336]{1,0:T(8,128)(2,1)S(1)}, u32[]{:S(2)}, u32[]{:S(2)}) collective-permute-start(bf16[24,14336]{1,0:T(8,128)(2,1)S(1)} %get-tuple-element.50), channel_id=1, source_target_pairs={{0,8},{4,12},{8,0},{12,4},{1,9},{5,13},{9,1},{13,5},{2,10},{6,14},... | collective-permute-start | bytes 2064392 | tf_op jit(solution)/shard_map/ppermute | solution.py:74
  105.9 3.6 %collective-permute-done.21 = bf16[24,7168]{1,0:T(8,128)(2,1)S(1)} collective-permute-done((bf16[24,7168]{1,0:T(8,128)(2,1)S(1)}, bf16[24,7168]{1,0:T(8,128)(2,1)S(1)}, u32[]{:S(2)}, u32[]{:S(2)}) %collective-permute-start.21) | collective-permute-done | bytes 344096 | tf_op jit(solution)/shard_map/ppermute | solution.py:13
  109.5 7.4 %collective-permute-done.20 = bf16[24,7168]{1,0:T(8,128)(2,1)S(1)} collective-permute-done((bf16[24,7168]{1,0:T(8,128)(2,1)S(1)}, bf16[24,7168]{1,0:T(8,128)(2,1)S(1)}, u32[]{:S(2)}, u32[]{:S(2)}) %collective-permute-start.20) | collective-permute-done | bytes 344096 | tf_op jit(solution)/shard_map/ppermute | solution.py:13
  116.9 5.7 %collective-permute-done.19 = bf16[24,7168]{1,0:T(8,128)(2,1)S(1)} collective-permute-done((bf16[24,7168]{1,0:T(8,128)(2,1)S(1)}, bf16[24,7168]{1,0:T(8,128)(2,1)S(1)}, u32[]{:S(2)}, u32[]{:S(2)}) %collective-permute-start.19) | collective-permute-done | bytes 344096 | tf_op jit(solution)/shard_map/ppermute | solution.py:13
  122.5 1.1 fusion.59
  123.6 8.0 %collective-permute-done.5 = bf16[24,14336]{1,0:T(8,128)(2,1)S(1)} collective-permute-done((bf16[24,14336]{1,0:T(8,128)(2,1)S(1)}, bf16[24,14336]{1,0:T(8,128)(2,1)S(1)}, u32[]{:S(2)}, u32[]{:S(2)}) %collective-permute-start.5) | collective-permute-done | bytes 688160 | tf_op jit(solution)/shard_map/ppermute | solution.py:74
  131.6 1.5 collective-permute-start.23
  134.0 15.9 %collective-permute-done.23 = bf16[24,14336]{1,0:T(8,128)(2,1)S(1)} collective-permute-done((bf16[24,14336]{1,0:T(8,128)(2,1)S(1)}, bf16[24,14336]{1,0:T(8,128)(2,1)S(1)}, u32[]{:S(2)}, u32[]{:S(2)}) %collective-permute-start.23) | collective-permute-done | bytes 688160 | tf_op jit(solution)/shard_map/ppermute | solution.py:13
  150.2 13.5 %collective-permute-done.25 = bf16[24,14336]{1,0:T(8,128)(2,1)S(1)} collective-permute-done((bf16[24,14336]{1,0:T(8,128)(2,1)}, bf16[24,14336]{1,0:T(8,128)(2,1)S(1)}, u32[]{:S(2)}, u32[]{:S(2)}) %collective-permute-start.25) | collective-permute-done | bytes 688160 | tf_op jit(solution)/shard_map/ppermute | solution.py:13
  163.7 1.3 fusion.80
  165.4 2.8 %collective-permute-done.26 = bf16[2,24,14336]{2,1,0:T(8,128)(2,1)S(1)} collective-permute-done((bf16[2,24,14336]{2,1,0:T(8,128)(2,1)S(1)}, bf16[2,24,14336]{2,1,0:T(8,128)(2,1)S(1)}, u32[]{:S(2)}, u32[]{:S(2)}) %collective-permute-start.26) | collective-permute-done | bytes 1376288 | tf_op jit(solution)/shard_map/ppermute | solution.py:13
  168.5 1.5 pad_maximum_fusion
  170.0 2.1 copy.35
  172.0 1.6 fusion.6
  174.1 1.6 fusion.4
  175.7 1.6 fusion.39
  177.3 1.6 fusion.16
  179.0 3.8 %add_convert_fusion = bf16[384,7168]{1,0:T(8,128)(2,1)S(1)} fusion(f32[384,7168]{1,0:T(8,128)S(1)} %fusion.16, bf16[1,7168,256]{2,1,0:T(8,128)(2,1)} %param.18, f32[384,256]{1,0:T(8,128)S(1)} %fusion.4, f32[384,256]{1,0:T(8,128)S(1)} %fusion.6), kind=kOutput, calls=%fused_computation.2 | convolution fusion | flops 1415380992 | bytes 20971520 | tf_op jit(solution)/shard_map/dot_general | solution.py:64
  184.3 2.9 %collective-permute-start.33 = (bf16[24,7168]{1,0:T(8,128)(2,1)S(1)}, bf16[24,7168]{1,0:T(8,128)(2,1)S(1)}, u32[]{:S(2)}, u32[]{:S(2)}) collective-permute-start(bf16[24,7168]{1,0:T(8,128)(2,1)S(1)} %copy-done.9), channel_id=1, source_target_pairs={{0,8},{4,12},{8,0},{12,4},{1,9},{5,13},{9,1},{13,5},{2,10},{6,14},... | collective-permute-start | bytes 1032200 | tf_op jit(solution)/shard_map/ppermute | solution.py:96
  188.3 1.0 fusion.79
  189.5 1.5 collective-permute-start.31
  191.5 7.3 %collective-permute-done.32 = bf16[24,7168]{1,0:T(8,128)(2,1)S(1)} collective-permute-done((bf16[24,7168]{1,0:T(8,128)(2,1)S(1)}, bf16[24,7168]{1,0:T(8,128)(2,1)S(1)}, u32[]{:S(2)}, u32[]{:S(2)}) %collective-permute-start.32) | collective-permute-done | bytes 344096 | tf_op jit(solution)/shard_map/ppermute | solution.py:96
  198.8 1.6 collective-permute-start.29
  200.4 10.0 %collective-permute-done.33 = bf16[24,7168]{1,0:T(8,128)(2,1)S(1)} collective-permute-done((bf16[24,7168]{1,0:T(8,128)(2,1)S(1)}, bf16[24,7168]{1,0:T(8,128)(2,1)S(1)}, u32[]{:S(2)}, u32[]{:S(2)}) %collective-permute-start.33) | collective-permute-done | bytes 344096 | tf_op jit(solution)/shard_map/ppermute | solution.py:96
  210.4 1.5 collective-permute-start.28
  211.9 6.0 %collective-permute-done.34 = bf16[24,7168]{1,0:T(8,128)(2,1)S(1)} collective-permute-done((bf16[24,7168]{1,0:T(8,128)(2,1)S(1)}, bf16[24,7168]{1,0:T(8,128)(2,1)S(1)}, u32[]{:S(2)}, u32[]{:S(2)}) %collective-permute-start.34) | collective-permute-done | bytes 344096 | tf_op jit(solution)/shard_map/ppermute | solution.py:96
  218.1 3.6 %collective-permute-done.28 = bf16[24,7168]{1,0:T(8,128)(2,1)S(1)} collective-permute-done((bf16[24,7168]{1,0:T(8,128)(2,1)S(1)}, bf16[24,7168]{1,0:T(8,128)(2,1)S(1)}, u32[]{:S(2)}, u32[]{:S(2)}) %collective-permute-start.28) | collective-permute-done | bytes 344096 | tf_op jit(solution)/shard_map/ppermute | solution.py:13
  222.7 2.9 %collective-permute-start.37 = (bf16[24,7168]{1,0:T(8,128)(2,1)S(1)}, bf16[24,7168]{1,0:T(8,128)(2,1)S(1)}, u32[]{:S(2)}, u32[]{:S(2)}) collective-permute-start(bf16[24,7168]{1,0:T(8,128)(2,1)S(1)} %get-tuple-element.22), channel_id=1, source_target_pairs={{0,8},{4,12},{8,0},{12,4},{1,9},{5,13},{9,1},{13,5},{2,10},{6,14},... | collective-permute-start | bytes 1032200 | tf_op jit(solution)/shard_map/ppermute | solution.py:96
  226.7 1.6 collective-permute-start.35
  228.3 7.3 %collective-permute-done.36 = bf16[24,7168]{1,0:T(8,128)(2,1)S(1)} collective-permute-done((bf16[24,7168]{1,0:T(8,128)(2,1)S(1)}, bf16[24,7168]{1,0:T(8,128)(2,1)S(1)}, u32[]{:S(2)}, u32[]{:S(2)}) %collective-permute-start.36) | collective-permute-done | bytes 344096 | tf_op jit(solution)/shard_map/ppermute | solution.py:96
  235.6 13.2 %collective-permute-done.37 = bf16[24,7168]{1,0:T(8,128)(2,1)S(1)} collective-permute-done((bf16[24,7168]{1,0:T(8,128)(2,1)S(1)}, bf16[24,7168]{1,0:T(8,128)(2,1)S(1)}, u32[]{:S(2)}, u32[]{:S(2)}) %collective-permute-start.37) | collective-permute-done | bytes 344096 | tf_op jit(solution)/shard_map/ppermute | solution.py:96
  248.8 6.6 %collective-permute-done.38 = bf16[24,7168]{1,0:T(8,128)(2,1)S(1)} collective-permute-done((bf16[24,7168]{1,0:T(8,128)(2,1)S(1)}, bf16[24,7168]{1,0:T(8,128)(2,1)S(1)}, u32[]{:S(2)}, u32[]{:S(2)}) %collective-permute-start.38) | collective-permute-done | bytes 344096 | tf_op jit(solution)/shard_map/ppermute | solution.py:96
  256.3 1.6 collective-permute-start.39
  257.9 9.3 %collective-permute-done.39 = bf16[1,32,7168]{2,1,0:T(8,128)(2,1)S(1)} collective-permute-done((bf16[1,32,7168]{2,1,0:T(8,128)(2,1)S(1)}, bf16[1,32,7168]{2,1,0:T(8,128)(2,1)S(1)}, u32[]{:S(2)}, u32[]{:S(2)}) %collective-permute-start.39) | collective-permute-done | bytes 458784 | tf_op jit(solution)/shard_map/ppermute | solution.py:19
  (105 shorter events, 20.3 us)
Async XLA Ops:
  0.6 10.3 %copy-start.11 = (f32[1,32,2]{1,2,0:T(2,128)S(1)}, f32[1,32,2]{1,2,0:T(2,128)}, u32[]{:S(2)}) copy-start(f32[1,32,2]{1,2,0:T(2,128)} %param.16) | copy-start | bytes 772
  0.6 10.4 %copy-start.5 = (bf16[1,32,7168]{2,1,0:T(8,128)(2,1)S(1)}, bf16[1,32,7168]{2,1,0:T(8,128)(2,1)}, u32[]{:S(2)}) copy-start(bf16[1,32,7168]{2,1,0:T(8,128)(2,1)} %param.14) | copy-start | bytes 1376260
  0.7 10.4 %copy-start.7 = (bf16[1,32,7168]{2,1,0:T(8,128)(2,1)S(1)}, bf16[1,32,7168]{2,1,0:T(8,128)(2,1)}, u32[]{:S(2)}) copy-start(bf16[1,32,7168]{2,1,0:T(8,128)(2,1)} %param.13) | copy-start | bytes 1376260
  4.7 28.2 %collective-permute-start.15 = (bf16[24,7168]{1,0:T(8,128)(2,1)S(1)}, bf16[24,7168]{1,0:T(8,128)(2,1)S(1)}, u32[]{:S(2)}, u32[]{:S(2)}) collective-permute-start(bf16[24,7168]{1,0:T(8,128)(2,1)S(1)} %get-tuple-element.66), channel_id=1, source_target_pairs={{0,12},{4,8},{8,4},{12,0},{1,13},{5,9},{9,5},{13,1},{2,14},{6,10},... | collective-permute-start | bytes 1032200 | tf_op jit(solution)/shard_map/ppermute | solution.py:74
  5.2 45.2 %collective-permute-start.12 = (bf16[24,7168]{1,0:T(8,128)(2,1)S(1)}, bf16[24,7168]{1,0:T(8,128)(2,1)S(1)}, u32[]{:S(2)}, u32[]{:S(2)}) collective-permute-start(bf16[24,7168]{1,0:T(8,128)(2,1)S(1)} %get-tuple-element.67), channel_id=1, source_target_pairs={{0,8},{4,12},{8,0},{12,4},{1,9},{5,13},{9,1},{13,5},{2,10},{6,14},... | collective-permute-start | bytes 1032200 | tf_op jit(solution)/shard_map/ppermute | solution.py:74
  8.7 21.5 %collective-permute-start.9 = (bf16[24,7168]{1,0:T(8,128)(2,1)S(1)}, bf16[24,7168]{1,0:T(8,128)(2,1)}, u32[]{:S(2)}, u32[]{:S(2)}) collective-permute-start(bf16[24,7168]{1,0:T(8,128)(2,1)S(1)} %get-tuple-element.68), channel_id=1, source_target_pairs={{0,4},{4,0},{8,12},{12,8},{1,5},{5,1},{9,13},{13,9},{2,6},{6,2},{1... | collective-permute-start | bytes 1032200 | tf_op jit(solution)/shard_map/ppermute | solution.py:74
  8.7 21.5 %collective-permute-start.7 = (bf16[24,7168]{1,0:T(8,128)(2,1)S(1)}, bf16[24,7168]{1,0:T(8,128)(2,1)}, u32[]{:S(2)}, u32[]{:S(2)}) collective-permute-start(bf16[24,7168]{1,0:T(8,128)(2,1)S(1)} %get-tuple-element.69), channel_id=1, source_target_pairs={{0,2},{2,0},{1,3},{3,1},{4,6},{6,4},{5,7},{7,5},{8,10},{10,8},{9,1... | collective-permute-start | bytes 1032200 | tf_op jit(solution)/shard_map/ppermute | solution.py:13
  13.2 110.4 %collective-permute-start.6 = (bf16[24,14336]{1,0:T(8,128)(2,1)}, bf16[24,14336]{1,0:T(8,128)(2,1)}, u32[]{:S(2)}, u32[]{:S(2)}) collective-permute-start(bf16[24,14336]{1,0:T(8,128)(2,1)} %get-tuple-element.49), channel_id=1, source_target_pairs={{0,12},{4,8},{8,4},{12,0},{1,13},{5,9},{9,5},{13,1},{2,14},{6,10},... | collective-permute-start | bytes 2064392 | tf_op jit(solution)/shard_map/ppermute | solution.py:74
  30.2 39.1 %collective-permute-start.2 = (bf16[24,14336]{1,0:T(8,128)(2,1)S(1)}, bf16[24,14336]{1,0:T(8,128)(2,1)}, u32[]{:S(2)}, u32[]{:S(2)}) collective-permute-start(bf16[24,14336]{1,0:T(8,128)(2,1)S(1)} %get-tuple-element.51), channel_id=1, source_target_pairs={{0,4},{4,0},{8,12},{12,8},{1,5},{5,1},{9,13},{13,9},{2,6},{6,2},{1... | collective-permute-start | bytes 2064392 | tf_op jit(solution)/shard_map/ppermute | solution.py:74
  30.2 11.2 %collective-permute-start.10 = (bf16[24,7168]{1,0:T(8,128)(2,1)}, bf16[24,7168]{1,0:T(8,128)(2,1)S(1)}, u32[]{:S(2)}, u32[]{:S(2)}) collective-permute-start(bf16[24,7168]{1,0:T(8,128)(2,1)} %collective-permute-done.9), channel_id=1, source_target_pairs={{0,2},{2,0},{1,3},{3,1},{4,6},{6,4},{5,7},{7,5},{8,10},{10,8},{9,1... | collective-permute-start | bytes 1032200 | tf_op jit(solution)/shard_map/ppermute | solution.py:13
  33.0 49.1 %collective-permute-start = (bf16[24,14336]{1,0:T(8,128)(2,1)S(1)}, bf16[24,14336]{1,0:T(8,128)(2,1)}, u32[]{:S(2)}, u32[]{:S(2)}) collective-permute-start(bf16[24,14336]{1,0:T(8,128)(2,1)S(1)} %get-tuple-element.52), channel_id=1, source_target_pairs={{0,2},{2,0},{1,3},{3,1},{4,6},{6,4},{5,7},{7,5},{8,10},{10,8},{9,1... | collective-permute-start | bytes 2064392 | tf_op jit(solution)/shard_map/ppermute | solution.py:13
  41.4 19.5 %collective-permute-start.16 = (bf16[24,7168]{1,0:T(8,128)(2,1)S(1)}, bf16[24,7168]{1,0:T(8,128)(2,1)S(1)}, u32[]{:S(2)}, u32[]{:S(2)}) collective-permute-start(bf16[24,7168]{1,0:T(8,128)(2,1)S(1)} %collective-permute-done.15), channel_id=1, source_target_pairs={{0,2},{2,0},{1,3},{3,1},{4,6},{6,4},{5,7},{7,5},{8,10},{10,8},{9,1... | collective-permute-start | bytes 1032200 | tf_op jit(solution)/shard_map/ppermute | solution.py:13
  50.4 18.2 %collective-permute-start.8 = (bf16[2,24,7168]{2,1,0:T(8,128)(2,1)S(1)}, bf16[2,24,7168]{2,1,0:T(8,128)(2,1)S(1)}, u32[]{:S(2)}, u32[]{:S(2)}) collective-permute-start(bf16[2,24,7168]{2,1,0:T(8,128)(2,1)S(1)} %get-tuple-element.71), channel_id=1, source_target_pairs={{0,1},{1,0},{2,3},{3,2},{4,5},{5,4},{6,7},{7,6},{8,9},{9,8},{10,11... | collective-permute-start | bytes 2064392 | tf_op jit(solution)/shard_map/ppermute | solution.py:13
  60.9 7.6 %collective-permute-start.13 = (bf16[24,7168]{1,0:T(8,128)(2,1)S(1)}, bf16[24,7168]{1,0:T(8,128)(2,1)S(1)}, u32[]{:S(2)}, u32[]{:S(2)}) collective-permute-start(bf16[24,7168]{1,0:T(8,128)(2,1)S(1)} %collective-permute-done.12), channel_id=1, source_target_pairs={{0,2},{2,0},{1,3},{3,1},{4,6},{6,4},{5,7},{7,5},{8,10},{10,8},{9,1... | collective-permute-start | bytes 1032200 | tf_op jit(solution)/shard_map/ppermute | solution.py:13
  68.5 2.1 collective-permute-start.17
  68.6 3.3 %collective-permute-start.14 = (bf16[2,24,7168]{2,1,0:T(8,128)(2,1)S(1)}, bf16[2,24,7168]{2,1,0:T(8,128)(2,1)S(1)}, u32[]{:S(2)}, u32[]{:S(2)}) collective-permute-start(bf16[2,24,7168]{2,1,0:T(8,128)(2,1)S(1)} %get-tuple-element.75), channel_id=1, source_target_pairs={{0,1},{1,0},{2,3},{3,2},{4,5},{5,4},{6,7},{7,6},{8,9},{9,8},{10,11... | collective-permute-start | bytes 2064392 | tf_op jit(solution)/shard_map/ppermute | solution.py:13
  69.3 3.3 %collective-permute-start.11 = (bf16[2,24,7168]{2,1,0:T(8,128)(2,1)S(1)}, bf16[2,24,7168]{2,1,0:T(8,128)(2,1)S(1)}, u32[]{:S(2)}, u32[]{:S(2)}) collective-permute-start(bf16[2,24,7168]{2,1,0:T(8,128)(2,1)S(1)} %get-tuple-element.73), channel_id=1, source_target_pairs={{0,1},{1,0},{2,3},{3,2},{4,5},{5,4},{6,7},{7,6},{8,9},{9,8},{10,11... | collective-permute-start | bytes 2064392 | tf_op jit(solution)/shard_map/ppermute | solution.py:13
  70.7 17.8 %collective-permute-start.3 = (bf16[24,14336]{1,0:T(8,128)(2,1)}, bf16[24,14336]{1,0:T(8,128)(2,1)}, u32[]{:S(2)}, u32[]{:S(2)}) collective-permute-start(bf16[24,14336]{1,0:T(8,128)(2,1)} %collective-permute-done.2), channel_id=1, source_target_pairs={{0,2},{2,0},{1,3},{3,1},{4,6},{6,4},{5,7},{7,5},{8,10},{10,8},{9,1... | collective-permute-start | bytes 2064392 | tf_op jit(solution)/shard_map/ppermute | solution.py:13
  73.7 2.0 copy-start
  75.7 2.0 copy-start.1
  77.8 2.0 copy-start.2
  81.8 8.1 %collective-permute-start.18 = (bf16[2,4,24,7168]{3,2,1,0:T(8,128)(2,1)S(1)}, bf16[2,4,24,7168]{3,2,1,0:T(8,128)(2,1)S(1)}, u32[]{:S(2)}, u32[]{:S(2)}) collective-permute-start(bf16[2,4,24,7168]{3,2,1,0:T(8,128)(2,1)S(1)} %bitcast.207), channel_id=1, source_target_pairs={{0,1},{1,0},{2,3},{3,2},{4,5},{5,4},{6,7},{7,6},{8,9},{9,8},{10,11... | collective-permute-start | bytes 8257544 | tf_op jit(solution)/shard_map/ppermute | solution.py:13
  84.4 9.9 %collective-permute-start.1 = (bf16[2,24,14336]{2,1,0:T(8,128)(2,1)}, bf16[2,24,14336]{2,1,0:T(8,128)(2,1)S(1)}, u32[]{:S(2)}, u32[]{:S(2)}) collective-permute-start(bf16[2,24,14336]{2,1,0:T(8,128)(2,1)} %get-tuple-element.58), channel_id=1, source_target_pairs={{0,1},{1,0},{2,3},{3,2},{4,5},{5,4},{6,7},{7,6},{8,9},{9,8},{10,11... | collective-permute-start | bytes 4128776 | tf_op jit(solution)/shard_map/ppermute | solution.py:13
  91.1 11.1 %collective-permute-start.22 = (bf16[24,7168]{1,0:T(8,128)(2,1)S(1)}, bf16[24,7168]{1,0:T(8,128)(2,1)S(1)}, u32[]{:S(2)}, u32[]{:S(2)}) collective-permute-start(bf16[24,7168]{1,0:T(8,128)(2,1)S(1)} %get-tuple-element.53), channel_id=1, source_target_pairs={{0,2},{2,0},{1,3},{3,1},{4,6},{6,4},{5,7},{7,5},{8,10},{10,8},{9,1... | collective-permute-start | bytes 1032200 | tf_op jit(solution)/shard_map/ppermute | solution.py:13
  92.3 17.3 %collective-permute-start.21 = (bf16[24,7168]{1,0:T(8,128)(2,1)S(1)}, bf16[24,7168]{1,0:T(8,128)(2,1)S(1)}, u32[]{:S(2)}, u32[]{:S(2)}) collective-permute-start(bf16[24,7168]{1,0:T(8,128)(2,1)S(1)} %get-tuple-element.54), channel_id=1, source_target_pairs={{0,2},{2,0},{1,3},{3,1},{4,6},{6,4},{5,7},{7,5},{8,10},{10,8},{9,1... | collective-permute-start | bytes 1032200 | tf_op jit(solution)/shard_map/ppermute | solution.py:13
  93.2 23.7 %collective-permute-start.20 = (bf16[24,7168]{1,0:T(8,128)(2,1)S(1)}, bf16[24,7168]{1,0:T(8,128)(2,1)S(1)}, u32[]{:S(2)}, u32[]{:S(2)}) collective-permute-start(bf16[24,7168]{1,0:T(8,128)(2,1)S(1)} %get-tuple-element.55), channel_id=1, source_target_pairs={{0,2},{2,0},{1,3},{3,1},{4,6},{6,4},{5,7},{7,5},{8,10},{10,8},{9,1... | collective-permute-start | bytes 1032200 | tf_op jit(solution)/shard_map/ppermute | solution.py:13
  94.3 28.3 %collective-permute-start.19 = (bf16[24,7168]{1,0:T(8,128)(2,1)S(1)}, bf16[24,7168]{1,0:T(8,128)(2,1)S(1)}, u32[]{:S(2)}, u32[]{:S(2)}) collective-permute-start(bf16[24,7168]{1,0:T(8,128)(2,1)S(1)} %get-tuple-element.56), channel_id=1, source_target_pairs={{0,2},{2,0},{1,3},{3,1},{4,6},{6,4},{5,7},{7,5},{8,10},{10,8},{9,1... | collective-permute-start | bytes 1032200 | tf_op jit(solution)/shard_map/ppermute | solution.py:13
  102.2 29.5 %collective-permute-start.5 = (bf16[24,14336]{1,0:T(8,128)(2,1)S(1)}, bf16[24,14336]{1,0:T(8,128)(2,1)S(1)}, u32[]{:S(2)}, u32[]{:S(2)}) collective-permute-start(bf16[24,14336]{1,0:T(8,128)(2,1)S(1)} %get-tuple-element.50), channel_id=1, source_target_pairs={{0,8},{4,12},{8,0},{12,4},{1,9},{5,13},{9,1},{13,5},{2,10},{6,14},... | collective-permute-start | bytes 2064392 | tf_op jit(solution)/shard_map/ppermute | solution.py:74
  109.5 23.6 %collective-permute-start.4 = (bf16[2,24,14336]{2,1,0:T(8,128)(2,1)S(1)}, bf16[2,24,14336]{2,1,0:T(8,128)(2,1)S(1)}, u32[]{:S(2)}, u32[]{:S(2)}) collective-permute-start(bf16[2,24,14336]{2,1,0:T(8,128)(2,1)S(1)} %get-tuple-element.60), channel_id=1, source_target_pairs={{0,1},{1,0},{2,3},{3,2},{4,5},{5,4},{6,7},{7,6},{8,9},{9,8},{10,11... | collective-permute-start | bytes 4128776 | tf_op jit(solution)/shard_map/ppermute | solution.py:13
  131.6 18.3 %collective-permute-start.23 = (bf16[24,14336]{1,0:T(8,128)(2,1)S(1)}, bf16[24,14336]{1,0:T(8,128)(2,1)S(1)}, u32[]{:S(2)}, u32[]{:S(2)}) collective-permute-start(bf16[24,14336]{1,0:T(8,128)(2,1)S(1)} %collective-permute-done.5), channel_id=1, source_target_pairs={{0,2},{2,0},{1,3},{3,1},{4,6},{6,4},{5,7},{7,5},{8,10},{10,8},{9,1... | collective-permute-start | bytes 2064392 | tf_op jit(solution)/shard_map/ppermute | solution.py:13
  133.4 30.4 %collective-permute-start.25 = (bf16[24,14336]{1,0:T(8,128)(2,1)}, bf16[24,14336]{1,0:T(8,128)(2,1)S(1)}, u32[]{:S(2)}, u32[]{:S(2)}) collective-permute-start(bf16[24,14336]{1,0:T(8,128)(2,1)} %collective-permute-done.6), channel_id=1, source_target_pairs={{0,2},{2,0},{1,3},{3,1},{4,6},{6,4},{5,7},{7,5},{8,10},{10,8},{9,1... | collective-permute-start | bytes 2064392 | tf_op jit(solution)/shard_map/ppermute | solution.py:13
  150.1 15.0 %collective-permute-start.24 = (bf16[2,24,14336]{2,1,0:T(8,128)(2,1)S(1)}, bf16[2,24,14336]{2,1,0:T(8,128)(2,1)S(1)}, u32[]{:S(2)}, u32[]{:S(2)}) collective-permute-start(bf16[2,24,14336]{2,1,0:T(8,128)(2,1)S(1)} %get-tuple-element.62), channel_id=1, source_target_pairs={{0,1},{1,0},{2,3},{3,2},{4,5},{5,4},{6,7},{7,6},{8,9},{9,8},{10,11... | collective-permute-start | bytes 4128776 | tf_op jit(solution)/shard_map/ppermute | solution.py:13
  165.0 3.2 %collective-permute-start.26 = (bf16[2,24,14336]{2,1,0:T(8,128)(2,1)S(1)}, bf16[2,24,14336]{2,1,0:T(8,128)(2,1)S(1)}, u32[]{:S(2)}, u32[]{:S(2)}) collective-permute-start(bf16[2,24,14336]{2,1,0:T(8,128)(2,1)S(1)} %get-tuple-element.64), channel_id=1, source_target_pairs={{0,1},{1,0},{2,3},{3,2},{4,5},{5,4},{6,7},{7,6},{8,9},{9,8},{10,11... | collective-permute-start | bytes 4128776 | tf_op jit(solution)/shard_map/ppermute | solution.py:13
  172.0 2.0 copy-start.3
  182.7 1.0 copy-start.10
  182.8 1.6 copy-start.9
  182.8 4.4 %copy-start.8 = (bf16[24,7168]{1,0:T(8,128)(2,1)S(1)}, bf16[24,7168]{1,0:T(8,128)(2,1)}, u32[]{:S(2)}) copy-start(bf16[24,7168]{1,0:T(8,128)(2,1)} %get-tuple-element.18) | copy-start | bytes 1032196
  183.1 5.2 %collective-permute-start.27 = (bf16[2,4,24,7168]{3,2,1,0:T(8,128)(2,1)S(1)}, bf16[2,4,24,7168]{3,2,1,0:T(8,128)(2,1)S(1)}, u32[]{:S(2)}, u32[]{:S(2)}) collective-permute-start(bf16[2,4,24,7168]{3,2,1,0:T(8,128)(2,1)S(1)} %bitcast.208), channel_id=1, source_target_pairs={{0,1},{1,0},{2,3},{3,2},{4,5},{5,4},{6,7},{7,6},{8,9},{9,8},{10,11... | collective-permute-start | bytes 8257544 | tf_op jit(solution)/shard_map/ppermute | solution.py:13
  183.7 15.1 %collective-permute-start.32 = (bf16[24,7168]{1,0:T(8,128)(2,1)S(1)}, bf16[24,7168]{1,0:T(8,128)(2,1)S(1)}, u32[]{:S(2)}, u32[]{:S(2)}) collective-permute-start(bf16[24,7168]{1,0:T(8,128)(2,1)S(1)} %copy-done.10), channel_id=1, source_target_pairs={{0,4},{4,0},{8,12},{12,8},{1,5},{5,1},{9,13},{13,9},{2,6},{6,2},{1... | collective-permute-start | bytes 1032200 | tf_op jit(solution)/shard_map/ppermute | solution.py:96
  184.3 26.1 %collective-permute-start.33 = (bf16[24,7168]{1,0:T(8,128)(2,1)S(1)}, bf16[24,7168]{1,0:T(8,128)(2,1)S(1)}, u32[]{:S(2)}, u32[]{:S(2)}) collective-permute-start(bf16[24,7168]{1,0:T(8,128)(2,1)S(1)} %copy-done.9), channel_id=1, source_target_pairs={{0,8},{4,12},{8,0},{12,4},{1,9},{5,13},{9,1},{13,5},{2,10},{6,14},... | collective-permute-start | bytes 1032200 | tf_op jit(solution)/shard_map/ppermute | solution.py:96
  187.2 30.7 %collective-permute-start.34 = (bf16[24,7168]{1,0:T(8,128)(2,1)S(1)}, bf16[24,7168]{1,0:T(8,128)(2,1)S(1)}, u32[]{:S(2)}, u32[]{:S(2)}) collective-permute-start(bf16[24,7168]{1,0:T(8,128)(2,1)S(1)} %copy-done.8), channel_id=1, source_target_pairs={{0,12},{4,8},{8,4},{12,0},{1,13},{5,9},{9,5},{13,1},{2,14},{6,10},... | collective-permute-start | bytes 1032200 | tf_op jit(solution)/shard_map/ppermute | solution.py:96
  189.5 28.6 %collective-permute-start.31 = (bf16[24,7168]{1,0:T(8,128)(2,1)S(1)}, bf16[24,7168]{1,0:T(8,128)(2,1)S(1)}, u32[]{:S(2)}, u32[]{:S(2)}) collective-permute-start(bf16[24,7168]{1,0:T(8,128)(2,1)S(1)} %get-tuple-element.44), channel_id=1, source_target_pairs={{0,2},{2,0},{1,3},{3,1},{4,6},{6,4},{5,7},{7,5},{8,10},{10,8},{9,1... | collective-permute-start | bytes 1032200 | tf_op jit(solution)/shard_map/ppermute | solution.py:13
  191.0 27.1 %collective-permute-start.30 = (bf16[24,7168]{1,0:T(8,128)(2,1)S(1)}, bf16[24,7168]{1,0:T(8,128)(2,1)S(1)}, u32[]{:S(2)}, u32[]{:S(2)}) collective-permute-start(bf16[24,7168]{1,0:T(8,128)(2,1)S(1)} %get-tuple-element.45), channel_id=1, source_target_pairs={{0,2},{2,0},{1,3},{3,1},{4,6},{6,4},{5,7},{7,5},{8,10},{10,8},{9,1... | collective-permute-start | bytes 1032200 | tf_op jit(solution)/shard_map/ppermute | solution.py:13
  198.8 19.3 %collective-permute-start.29 = (bf16[24,7168]{1,0:T(8,128)(2,1)S(1)}, bf16[24,7168]{1,0:T(8,128)(2,1)S(1)}, u32[]{:S(2)}, u32[]{:S(2)}) collective-permute-start(bf16[24,7168]{1,0:T(8,128)(2,1)S(1)} %get-tuple-element.46), channel_id=1, source_target_pairs={{0,2},{2,0},{1,3},{3,1},{4,6},{6,4},{5,7},{7,5},{8,10},{10,8},{9,1... | collective-permute-start | bytes 1032200 | tf_op jit(solution)/shard_map/ppermute | solution.py:13
  210.4 11.3 %collective-permute-start.28 = (bf16[24,7168]{1,0:T(8,128)(2,1)S(1)}, bf16[24,7168]{1,0:T(8,128)(2,1)S(1)}, u32[]{:S(2)}, u32[]{:S(2)}) collective-permute-start(bf16[24,7168]{1,0:T(8,128)(2,1)S(1)} %get-tuple-element.47), channel_id=1, source_target_pairs={{0,2},{2,0},{1,3},{3,1},{4,6},{6,4},{5,7},{7,5},{8,10},{10,8},{9,1... | collective-permute-start | bytes 1032200 | tf_op jit(solution)/shard_map/ppermute | solution.py:13
  221.7 4.3 %copy-start.4 = (bf16[1,32,7168]{2,1,0:T(8,128)(2,1)S(1)}, bf16[1,32,7168]{2,1,0:T(8,128)(2,1)}, u32[]{:S(2)}) copy-start(bf16[1,32,7168]{2,1,0:T(8,128)(2,1)} %param.10) | copy-start | bytes 1376260
  222.0 33.6 %copy-start.6 = (bf16[1,32,7168]{2,1,0:T(8,128)(2,1)S(1)}, bf16[1,32,7168]{2,1,0:T(8,128)(2,1)}, u32[]{:S(2)}) copy-start(bf16[1,32,7168]{2,1,0:T(8,128)(2,1)} %param.14) | copy-start | bytes 1376260
  222.0 13.6 %collective-permute-start.36 = (bf16[24,7168]{1,0:T(8,128)(2,1)S(1)}, bf16[24,7168]{1,0:T(8,128)(2,1)S(1)}, u32[]{:S(2)}, u32[]{:S(2)}) collective-permute-start(bf16[24,7168]{1,0:T(8,128)(2,1)S(1)} %get-tuple-element.21), channel_id=1, source_target_pairs={{0,4},{4,0},{8,12},{12,8},{1,5},{5,1},{9,13},{13,9},{2,6},{6,2},{1... | collective-permute-start | bytes 1032200 | tf_op jit(solution)/shard_map/ppermute | solution.py:96
  222.7 26.1 %collective-permute-start.37 = (bf16[24,7168]{1,0:T(8,128)(2,1)S(1)}, bf16[24,7168]{1,0:T(8,128)(2,1)S(1)}, u32[]{:S(2)}, u32[]{:S(2)}) collective-permute-start(bf16[24,7168]{1,0:T(8,128)(2,1)S(1)} %get-tuple-element.22), channel_id=1, source_target_pairs={{0,8},{4,12},{8,0},{12,4},{1,9},{5,13},{9,1},{13,5},{2,10},{6,14},... | collective-permute-start | bytes 1032200 | tf_op jit(solution)/shard_map/ppermute | solution.py:96
  225.5 29.9 %collective-permute-start.38 = (bf16[24,7168]{1,0:T(8,128)(2,1)S(1)}, bf16[24,7168]{1,0:T(8,128)(2,1)S(1)}, u32[]{:S(2)}, u32[]{:S(2)}) collective-permute-start(bf16[24,7168]{1,0:T(8,128)(2,1)S(1)} %get-tuple-element.23), channel_id=1, source_target_pairs={{0,12},{4,8},{8,4},{12,0},{1,13},{5,9},{9,5},{13,1},{2,14},{6,10},... | collective-permute-start | bytes 1032200 | tf_op jit(solution)/shard_map/ppermute | solution.py:96
  226.7 31.2 %collective-permute-start.35 = (bf16[1,32,7168]{2,1,0:T(8,128)(2,1)S(1)}, bf16[1,32,7168]{2,1,0:T(8,128)(2,1)S(1)}, u32[]{:S(2)}, u32[]{:S(2)}) collective-permute-start(bf16[1,32,7168]{2,1,0:T(8,128)(2,1)S(1)} %fusion.3), channel_id=1, source_target_pairs={{0,16},{16,0},{1,17},{17,1},{2,18},{18,2},{3,19},{19,3},{4,20},{20... | collective-permute-start | bytes 1376264 | tf_op jit(solution)/shard_map/ppermute | solution.py:19
  256.3 10.9 %collective-permute-start.39 = (bf16[1,32,7168]{2,1,0:T(8,128)(2,1)S(1)}, bf16[1,32,7168]{2,1,0:T(8,128)(2,1)S(1)}, u32[]{:S(2)}, u32[]{:S(2)}) collective-permute-start(bf16[1,32,7168]{2,1,0:T(8,128)(2,1)S(1)} %fusion.2), channel_id=1, source_target_pairs={{0,16},{16,0},{1,17},{17,1},{2,18},{18,2},{3,19},{19,3},{4,20},{20... | collective-permute-start | bytes 1376264 | tf_op jit(solution)/shard_map/ppermute | solution.py:19

commit v20 on v17

--- a/solution.py
+++ b/solution.py
@@ -130,7 +130,8 @@
     b_rows, f_totals = lax.optimization_barrier((b_rows, f_totals))
     f_out = returned(f_totals)
     b_partial = backward_rows(b_rows.reshape(-1, 2 * width), w_gate, w_up, w_down)
-    b_totals = reduce_group(b_partial.reshape(2, 2, experts, capacity, width))
+    b_sum = reduce_group(b_partial.reshape(2, 2, experts, capacity, width)[:, :, None])
+    b_totals = list(b_sum[0])
     b_totals, f_out = lax.optimization_barrier((b_totals, f_out))
     b_out = returned(b_totals)
     high = lax.Precision.HIGHEST

time: 266 us -> 296 us (1.11)
  waiting for transfers between devices: 176 us -> 206 us
  starting transfers between devices: 40 us -> 36.5 us
    ppermute x26 -> x23, waiting for transfers between devices: 80.6 us -> 106 us  [swap(): return lax.ppermute(value, axis, [(0, 1), (1, 0)])]
    ppermute x6, waiting for transfers between devices: 49.4 us -> 55.3 us  [returned(): out.append(lax.ppermute(totals[d], 'z', [(i, i ^ d) for i in range(count)]))]
    ppermute x26 -> x23, starting transfers between devices: 22.4 us -> 18.8 us  [swap(): return lax.ppermute(value, axis, [(0, 1), (1, 0)])]
  transfers between devices with their start and end apart: 40 -> 37, of which waited for: 25 -> 24; matrix products, arithmetic and copies ran while one was open for 9% -> 7% of each run, Pallas kernels for 0% -> 0%
where the time goes in v20:
time: 296 us; the launch traced here: 295 us
  waiting for transfers between devices  206 us (70%)
  starting transfers between devices  36.5 us (12%)
  matrix products  20.8 us (7%)
  other arithmetic  19.8 us (7%)
  local copies, waits for them, and re-layouts  10.7 us (4%)
    ppermute x23, waiting for transfers between devices, swap(): return lax.ppermute(value, axis, [(0, 1), (1, 0)])  106 us
    ppermute x6, waiting for transfers between devices, returned(): out.append(lax.ppermute(totals[d], 'z', [(i, i ^ d) for i in range(count)]))  55.3 us
    ppermute x6, waiting for transfers between devices, dispatch(): received = lax.ppermute(slots[d], 'z', [(i, i ^ d) for i in range(count)])  37.1 us
    ppermute x23, starting transfers between devices, swap(): return lax.ppermute(value, axis, [(0, 1), (1, 0)])  18.8 us
    ppermute x2, waiting for transfers between devices, passed_along(): return lax.ppermute(value, axis, pairs)  7.84 us
    ppermute x6, starting transfers between devices, dispatch(): received = lax.ppermute(slots[d], 'z', [(i, i ^ d) for i in range(count)])  7.47 us
    another operation x8, other arithmetic, dispatch(): pieces.append(jnp.stack([across, swap(across, 'c')]))  7.39 us
    ppermute x6, starting transfers between devices, returned(): out.append(lax.ppermute(totals[d], 'z', [(i, i ^ d) for i in range(count)]))  7.03 us
  transfers between devices with their start and end apart: 37, of which 24 were waited for; matrix products, arithmetic and copies ran while one was open for 7% of the time, Pallas kernels for 0%

profile of v20, /device:TPU:16, one launch (start us, length us, event | category | flops | bytes accessed | tf_op | source)
XLA Modules:
  0.0 295.3 jit_solution(7597017105374639612)
XLA Ops:
  3.0 1.6 convolution_convert_fusion.2
  4.7 1.6 collective-permute-start.13
  6.7 1.6 collective-permute-start.19
  8.3 1.5 collective-permute-start.11
  11.8 2.5 collective-permute-start.2
  14.4 2.9 collective-permute-done.11
  17.3 1.5 collective-permute-start
  18.8 1.1 fusion.72
  19.9 1.5 collective-permute-done.13
  22.3 10.4 %collective-permute-done = bf16[24,14336]{1,0:T(8,128)(2,1)S(1)} collective-permute-done((bf16[24,14336]{1,0:T(8,128)(2,1)S(1)}, bf16[24,14336]{1,0:T(8,128)(2,1)S(1)}, u32[]{:S(2)}, u32[]{:S(2)}) %collective-permute-start) | collective-permute-done | bytes 688160 | tf_op jit(solution)/shard_map/ppermute | solution.py:13
  32.7 1.5 collective-permute-start.14
  35.0 5.9 %collective-permute-done.14 = bf16[24,7168]{1,0:T(8,128)(2,1)S(1)} collective-permute-done((bf16[24,7168]{1,0:T(8,128)(2,1)}, bf16[24,7168]{1,0:T(8,128)(2,1)S(1)}, u32[]{:S(2)}, u32[]{:S(2)}) %collective-permute-start.14) | collective-permute-done | bytes 344096 | tf_op jit(solution)/shard_map/ppermute | solution.py:13
  40.9 1.5 collective-permute-start.17
  42.4 1.1 fusion.71
  43.5 6.2 %collective-permute-done.17 = bf16[24,7168]{1,0:T(8,128)(2,1)S(1)} collective-permute-done((bf16[24,7168]{1,0:T(8,128)(2,1)}, bf16[24,7168]{1,0:T(8,128)(2,1)S(1)}, u32[]{:S(2)}, u32[]{:S(2)}) %collective-permute-start.17) | collective-permute-done | bytes 344096 | tf_op jit(solution)/shard_map/ppermute | solution.py:13
  49.8 1.6 collective-permute-start.20
  51.3 1.1 fusion.70
  52.4 4.8 %collective-permute-done.20 = bf16[24,7168]{1,0:T(8,128)(2,1)S(1)} collective-permute-done((bf16[24,7168]{1,0:T(8,128)(2,1)}, bf16[24,7168]{1,0:T(8,128)(2,1)S(1)}, u32[]{:S(2)}, u32[]{:S(2)}) %collective-permute-start.20) | collective-permute-done | bytes 344096 | tf_op jit(solution)/shard_map/ppermute | solution.py:13
  57.2 1.1 fusion.69
  60.1 21.6 %collective-permute-done.5 = bf16[24,14336]{1,0:T(8,128)(2,1)} collective-permute-done((bf16[24,14336]{1,0:T(8,128)(2,1)S(1)}, bf16[24,14336]{1,0:T(8,128)(2,1)}, u32[]{:S(2)}, u32[]{:S(2)}) %collective-permute-start.5) | collective-permute-done | bytes 688160 | tf_op jit(solution)/shard_map/ppermute | solution.py:77
  81.7 1.5 collective-permute-start.3
  83.1 14.0 %collective-permute-done.8 = bf16[24,14336]{1,0:T(8,128)(2,1)} collective-permute-done((bf16[24,14336]{1,0:T(8,128)(2,1)S(1)}, bf16[24,14336]{1,0:T(8,128)(2,1)}, u32[]{:S(2)}, u32[]{:S(2)}) %collective-permute-start.8) | collective-permute-done | bytes 688160 | tf_op jit(solution)/shard_map/ppermute | solution.py:77
  97.1 1.5 collective-permute-start.6
  100.8 1.6 copy-done
  102.4 1.6 fusion.19
  104.4 1.6 fusion.47
  106.5 1.6 convolution_convert_fusion.1
  109.3 6.4 %collective-permute-done.6 = bf16[24,14336]{1,0:T(8,128)(2,1)S(1)} collective-permute-done((bf16[24,14336]{1,0:T(8,128)(2,1)}, bf16[24,14336]{1,0:T(8,128)(2,1)S(1)}, u32[]{:S(2)}, u32[]{:S(2)}) %collective-permute-start.6) | collective-permute-done | bytes 688160 | tf_op jit(solution)/shard_map/ppermute | solution.py:13
  115.7 1.3 fusion.76
  117.0 11.1 %collective-permute-done.9 = bf16[24,14336]{1,0:T(8,128)(2,1)} collective-permute-done((bf16[24,14336]{1,0:T(8,128)(2,1)}, bf16[24,14336]{1,0:T(8,128)(2,1)}, u32[]{:S(2)}, u32[]{:S(2)}) %collective-permute-start.9) | collective-permute-done | bytes 688160 | tf_op jit(solution)/shard_map/ppermute | solution.py:13
  128.2 1.5 fusion.75
  130.6 2.3 collective-permute-done.10
  133.1 1.5 copy-done.5
  134.7 2.8 fusion.73
  137.6 1.6 collective-permute-start.23
  139.7 1.5 collective-permute-start.25
  141.7 1.5 pad_maximum_fusion
  143.1 5.4 %collective-permute-done.23 = bf16[24,7168]{1,0:T(8,128)(2,1)S(1)} collective-permute-done((bf16[24,7168]{1,0:T(8,128)(2,1)S(1)}, bf16[24,7168]{1,0:T(8,128)(2,1)S(1)}, u32[]{:S(2)}, u32[]{:S(2)}) %collective-permute-start.23) | collective-permute-done | bytes 344096 | tf_op jit(solution)/shard_map/ppermute | solution.py:13
  148.5 7.4 %collective-permute-done.24 = bf16[24,7168]{1,0:T(8,128)(2,1)S(1)} collective-permute-done((bf16[24,7168]{1,0:T(8,128)(2,1)S(1)}, bf16[24,7168]{1,0:T(8,128)(2,1)S(1)}, u32[]{:S(2)}, u32[]{:S(2)}) %collective-permute-start.24) | collective-permute-done | bytes 344096 | tf_op jit(solution)/shard_map/ppermute | solution.py:13
  155.9 7.4 %collective-permute-done.25 = bf16[24,7168]{1,0:T(8,128)(2,1)S(1)} collective-permute-done((bf16[24,7168]{1,0:T(8,128)(2,1)S(1)}, bf16[24,7168]{1,0:T(8,128)(2,1)S(1)}, u32[]{:S(2)}, u32[]{:S(2)}) %collective-permute-start.25) | collective-permute-done | bytes 344096 | tf_op jit(solution)/shard_map/ppermute | solution.py:13
  163.3 6.6 %collective-permute-done.26 = bf16[24,7168]{1,0:T(8,128)(2,1)S(1)} collective-permute-done((bf16[24,7168]{1,0:T(8,128)(2,1)S(1)}, bf16[24,7168]{1,0:T(8,128)(2,1)S(1)}, u32[]{:S(2)}, u32[]{:S(2)}) %collective-permute-start.26) | collective-permute-done | bytes 344096 | tf_op jit(solution)/shard_map/ppermute | solution.py:13
  169.8 1.1 fusion.54
  170.9 1.9 copy.37
  172.9 1.7 fusion.4
  174.7 2.3 fusion.6
  177.0 2.6 fusion.42
  179.6 1.6 fusion.16
  181.3 3.9 %add_convert_fusion = bf16[384,7168]{1,0:T(8,128)(2,1)S(1)} fusion(f32[384,7168]{1,0:T(8,128)S(1)} %fusion.16, bf16[1,7168,256]{2,1,0:T(8,128)(2,1)} %param.18, f32[384,256]{1,0:T(8,128)S(1)} %fusion.4, f32[384,256]{1,0:T(8,128)} %fusion.6), kind=kOutput, calls=%fused_computation.2 | convolution fusion | flops 1415380992 | bytes 20971520 | tf_op jit(solution)/shard_map/dot_general | solution.py:64
  186.2 1.3 collective-permute-start.29
  188.1 1.6 collective-permute-start.31
  189.7 11.4 %collective-permute-done.29 = bf16[24,7168]{1,0:T(8,128)(2,1)S(1)} collective-permute-done((bf16[24,7168]{1,0:T(8,128)(2,1)S(1)}, bf16[24,7168]{1,0:T(8,128)(2,1)S(1)}, u32[]{:S(2)}, u32[]{:S(2)}) %collective-permute-start.29) | collective-permute-done | bytes 344096 | tf_op jit(solution)/shard_map/ppermute | solution.py:97
  201.0 10.3 %collective-permute-done.30 = bf16[24,7168]{1,0:T(8,128)(2,1)S(1)} collective-permute-done((bf16[24,7168]{1,0:T(8,128)(2,1)S(1)}, bf16[24,7168]{1,0:T(8,128)(2,1)S(1)}, u32[]{:S(2)}, u32[]{:S(2)}) %collective-permute-start.30) | collective-permute-done | bytes 344096 | tf_op jit(solution)/shard_map/ppermute | solution.py:97
  211.3 8.2 %collective-permute-done.31 = bf16[24,7168]{1,0:T(8,128)(2,1)S(1)} collective-permute-done((bf16[24,7168]{1,0:T(8,128)(2,1)S(1)}, bf16[24,7168]{1,0:T(8,128)(2,1)S(1)}, u32[]{:S(2)}, u32[]{:S(2)}) %collective-permute-start.31) | collective-permute-done | bytes 344096 | tf_op jit(solution)/shard_map/ppermute | solution.py:97
  219.7 0.9 convert_add_fusion
  220.7 1.6 collective-permute-start.28
  223.0 28.7 %collective-permute-done.28 = bf16[4,24,7168]{2,1,0:T(8,128)(2,1)S(1)} collective-permute-done((bf16[4,24,7168]{2,1,0:T(8,128)(2,1)S(1)}, bf16[4,24,7168]{2,1,0:T(8,128)(2,1)S(1)}, u32[]{:S(2)}, u32[]{:S(2)}) %collective-permute-start.28) | collective-permute-done | bytes 1376288 | tf_op jit(solution)/shard_map/ppermute | solution.py:13
  252.2 1.9 collective-permute-start.34
  254.1 1.6 collective-permute-start.35
  256.3 1.6 collective-permute-start.32
  258.0 5.2 %collective-permute-done.33 = bf16[24,7168]{1,0:T(8,128)(2,1)S(1)} collective-permute-done((bf16[24,7168]{1,0:T(8,128)(2,1)S(1)}, bf16[24,7168]{1,0:T(8,128)(2,1)S(1)}, u32[]{:S(2)}, u32[]{:S(2)}) %collective-permute-start.33) | collective-permute-done | bytes 344096 | tf_op jit(solution)/shard_map/ppermute | solution.py:97
  263.2 14.2 %collective-permute-done.34 = bf16[24,7168]{1,0:T(8,128)(2,1)S(1)} collective-permute-done((bf16[24,7168]{1,0:T(8,128)(2,1)S(1)}, bf16[24,7168]{1,0:T(8,128)(2,1)S(1)}, u32[]{:S(2)}, u32[]{:S(2)}) %collective-permute-start.34) | collective-permute-done | bytes 344096 | tf_op jit(solution)/shard_map/ppermute | solution.py:97
  277.4 6.1 %collective-permute-done.35 = bf16[24,7168]{1,0:T(8,128)(2,1)S(1)} collective-permute-done((bf16[24,7168]{1,0:T(8,128)(2,1)S(1)}, bf16[24,7168]{1,0:T(8,128)(2,1)S(1)}, u32[]{:S(2)}, u32[]{:S(2)}) %collective-permute-start.35) | collective-permute-done | bytes 344096 | tf_op jit(solution)/shard_map/ppermute | solution.py:97
  284.3 1.6 collective-permute-start.36
  285.9 7.8 %collective-permute-done.36 = bf16[1,32,7168]{2,1,0:T(8,128)(2,1)S(1)} collective-permute-done((bf16[1,32,7168]{2,1,0:T(8,128)(2,1)S(1)}, bf16[1,32,7168]{2,1,0:T(8,128)(2,1)S(1)}, u32[]{:S(2)}, u32[]{:S(2)}) %collective-permute-start.36) | collective-permute-done | bytes 458784 | tf_op jit(solution)/shard_map/ppermute | solution.py:19
  (103 shorter events, 20.9 us)
Async XLA Ops:
  0.6 9.9 %copy-start.12 = (f32[1,32,2]{1,2,0:T(2,128)S(1)}, f32[1,32,2]{1,2,0:T(2,128)}, u32[]{:S(2)}) copy-start(f32[1,32,2]{1,2,0:T(2,128)} %param.16) | copy-start | bytes 772
  0.6 10.0 %copy-start.8 = (bf16[1,32,7168]{2,1,0:T(8,128)(2,1)S(1)}, bf16[1,32,7168]{2,1,0:T(8,128)(2,1)}, u32[]{:S(2)}) copy-start(bf16[1,32,7168]{2,1,0:T(8,128)(2,1)} %param.13) | copy-start | bytes 1376260
  0.7 10.0 %copy-start.7 = (bf16[1,32,7168]{2,1,0:T(8,128)(2,1)S(1)}, bf16[1,32,7168]{2,1,0:T(8,128)(2,1)}, u32[]{:S(2)}) copy-start(bf16[1,32,7168]{2,1,0:T(8,128)(2,1)} %param.14) | copy-start | bytes 1376260
  4.7 16.7 %collective-permute-start.13 = (bf16[24,7168]{1,0:T(8,128)(2,1)S(1)}, bf16[24,7168]{1,0:T(8,128)(2,1)}, u32[]{:S(2)}, u32[]{:S(2)}) collective-permute-start(bf16[24,7168]{1,0:T(8,128)(2,1)S(1)} %get-tuple-element.52), channel_id=1, source_target_pairs={{0,4},{4,0},{8,12},{12,8},{1,5},{5,1},{9,13},{13,9},{2,6},{6,2},{1... | collective-permute-start | bytes 1032200 | tf_op jit(solution)/shard_map/ppermute | solution.py:77
  6.4 28.1 %collective-permute-start.16 = (bf16[24,7168]{1,0:T(8,128)(2,1)S(1)}, bf16[24,7168]{1,0:T(8,128)(2,1)}, u32[]{:S(2)}, u32[]{:S(2)}) collective-permute-start(bf16[24,7168]{1,0:T(8,128)(2,1)S(1)} %get-tuple-element.51), channel_id=1, source_target_pairs={{0,8},{4,12},{8,0},{12,4},{1,9},{5,13},{9,1},{13,5},{2,10},{6,14},... | collective-permute-start | bytes 1032200 | tf_op jit(solution)/shard_map/ppermute | solution.py:77
  6.7 36.8 %collective-permute-start.19 = (bf16[24,7168]{1,0:T(8,128)(2,1)S(1)}, bf16[24,7168]{1,0:T(8,128)(2,1)}, u32[]{:S(2)}, u32[]{:S(2)}) collective-permute-start(bf16[24,7168]{1,0:T(8,128)(2,1)S(1)} %get-tuple-element.50), channel_id=1, source_target_pairs={{0,12},{4,8},{8,4},{12,0},{1,13},{5,9},{9,5},{13,1},{2,14},{6,10},... | collective-permute-start | bytes 1032200 | tf_op jit(solution)/shard_map/ppermute | solution.py:77
  8.3 9.1 %collective-permute-start.11 = (bf16[24,7168]{1,0:T(8,128)(2,1)S(1)}, bf16[24,7168]{1,0:T(8,128)(2,1)}, u32[]{:S(2)}, u32[]{:S(2)}) collective-permute-start(bf16[24,7168]{1,0:T(8,128)(2,1)S(1)} %get-tuple-element.53), channel_id=1, source_target_pairs={{0,2},{2,0},{1,3},{3,1},{4,6},{6,4},{5,7},{7,5},{8,10},{10,8},{9,1... | collective-permute-start | bytes 1032200 | tf_op jit(solution)/shard_map/ppermute | solution.py:13
  11.8 47.8 %collective-permute-start.2 = (bf16[24,14336]{1,0:T(8,128)(2,1)S(1)}, bf16[24,14336]{1,0:T(8,128)(2,1)S(1)}, u32[]{:S(2)}, u32[]{:S(2)}) collective-permute-start(bf16[24,14336]{1,0:T(8,128)(2,1)S(1)} %get-tuple-element.43), channel_id=1, source_target_pairs={{0,4},{4,0},{8,12},{12,8},{1,5},{5,1},{9,13},{13,9},{2,6},{6,2},{1... | collective-permute-start | bytes 2064392 | tf_op jit(solution)/shard_map/ppermute | solution.py:77
  17.3 15.4 %collective-permute-start = (bf16[24,14336]{1,0:T(8,128)(2,1)S(1)}, bf16[24,14336]{1,0:T(8,128)(2,1)S(1)}, u32[]{:S(2)}, u32[]{:S(2)}) collective-permute-start(bf16[24,14336]{1,0:T(8,128)(2,1)S(1)} %get-tuple-element.44), channel_id=1, source_target_pairs={{0,2},{2,0},{1,3},{3,1},{4,6},{6,4},{5,7},{7,5},{8,10},{10,8},{9,1... | collective-permute-start | bytes 2064392 | tf_op jit(solution)/shard_map/ppermute | solution.py:13
  21.4 60.2 %collective-permute-start.5 = (bf16[24,14336]{1,0:T(8,128)(2,1)S(1)}, bf16[24,14336]{1,0:T(8,128)(2,1)}, u32[]{:S(2)}, u32[]{:S(2)}) collective-permute-start(bf16[24,14336]{1,0:T(8,128)(2,1)S(1)} %get-tuple-element.42), channel_id=1, source_target_pairs={{0,8},{4,12},{8,0},{12,4},{1,9},{5,13},{9,1},{13,5},{2,10},{6,14},... | collective-permute-start | bytes 2064392 | tf_op jit(solution)/shard_map/ppermute | solution.py:77
  32.7 8.1 %collective-permute-start.14 = (bf16[24,7168]{1,0:T(8,128)(2,1)}, bf16[24,7168]{1,0:T(8,128)(2,1)S(1)}, u32[]{:S(2)}, u32[]{:S(2)}) collective-permute-start(bf16[24,7168]{1,0:T(8,128)(2,1)} %collective-permute-done.13), channel_id=1, source_target_pairs={{0,2},{2,0},{1,3},{3,1},{4,6},{6,4},{5,7},{7,5},{8,10},{10,8},{9,1... | collective-permute-start | bytes 1032200 | tf_op jit(solution)/shard_map/ppermute | solution.py:13
  34.4 62.7 %collective-permute-start.8 = (bf16[24,14336]{1,0:T(8,128)(2,1)S(1)}, bf16[24,14336]{1,0:T(8,128)(2,1)}, u32[]{:S(2)}, u32[]{:S(2)}) collective-permute-start(bf16[24,14336]{1,0:T(8,128)(2,1)S(1)} %get-tuple-element.41), channel_id=1, source_target_pairs={{0,12},{4,8},{8,4},{12,0},{1,13},{5,9},{9,5},{13,1},{2,14},{6,10},... | collective-permute-start | bytes 2064392 | tf_op jit(solution)/shard_map/ppermute | solution.py:77
  40.9 8.9 %collective-permute-start.17 = (bf16[24,7168]{1,0:T(8,128)(2,1)}, bf16[24,7168]{1,0:T(8,128)(2,1)S(1)}, u32[]{:S(2)}, u32[]{:S(2)}) collective-permute-start(bf16[24,7168]{1,0:T(8,128)(2,1)} %collective-permute-done.16), channel_id=1, source_target_pairs={{0,2},{2,0},{1,3},{3,1},{4,6},{6,4},{5,7},{7,5},{8,10},{10,8},{9,1... | collective-permute-start | bytes 1032200 | tf_op jit(solution)/shard_map/ppermute | solution.py:13
  43.5 14.8 %collective-permute-start.12 = (bf16[2,24,7168]{2,1,0:T(8,128)(2,1)S(1)}, bf16[2,24,7168]{2,1,0:T(8,128)(2,1)S(1)}, u32[]{:S(2)}, u32[]{:S(2)}) collective-permute-start(bf16[2,24,7168]{2,1,0:T(8,128)(2,1)S(1)} %get-tuple-element.63), channel_id=1, source_target_pairs={{0,1},{1,0},{2,3},{3,2},{4,5},{5,4},{6,7},{7,6},{8,9},{9,8},{10,11... | collective-permute-start | bytes 2064392 | tf_op jit(solution)/shard_map/ppermute | solution.py:13
  49.8 7.5 %collective-permute-start.20 = (bf16[24,7168]{1,0:T(8,128)(2,1)}, bf16[24,7168]{1,0:T(8,128)(2,1)S(1)}, u32[]{:S(2)}, u32[]{:S(2)}) collective-permute-start(bf16[24,7168]{1,0:T(8,128)(2,1)} %collective-permute-done.19), channel_id=1, source_target_pairs={{0,2},{2,0},{1,3},{3,1},{4,6},{6,4},{5,7},{7,5},{8,10},{10,8},{9,1... | collective-permute-start | bytes 1032200 | tf_op jit(solution)/shard_map/ppermute | solution.py:13
  57.2 2.1 collective-permute-start.15
  58.3 40.3 %collective-permute-start.18 = (bf16[2,24,7168]{2,1,0:T(8,128)(2,1)S(1)}, bf16[2,24,7168]{2,1,0:T(8,128)(2,1)S(1)}, u32[]{:S(2)}, u32[]{:S(2)}) collective-permute-start(bf16[2,24,7168]{2,1,0:T(8,128)(2,1)S(1)} %get-tuple-element.67), channel_id=1, source_target_pairs={{0,1},{1,0},{2,3},{3,2},{4,5},{5,4},{6,7},{7,6},{8,9},{9,8},{10,11... | collective-permute-start | bytes 2064392 | tf_op jit(solution)/shard_map/ppermute | solution.py:13
  59.4 39.9 %collective-permute-start.21 = (bf16[2,24,7168]{2,1,0:T(8,128)(2,1)S(1)}, bf16[2,24,7168]{2,1,0:T(8,128)(2,1)S(1)}, u32[]{:S(2)}, u32[]{:S(2)}) collective-permute-start(bf16[2,24,7168]{2,1,0:T(8,128)(2,1)S(1)} %get-tuple-element.69), channel_id=1, source_target_pairs={{0,1},{1,0},{2,3},{3,2},{4,5},{5,4},{6,7},{7,6},{8,9},{9,8},{10,11... | collective-permute-start | bytes 2064392 | tf_op jit(solution)/shard_map/ppermute | solution.py:13
  59.6 70.1 %collective-permute-start.1 = (bf16[2,24,14336]{2,1,0:T(8,128)(2,1)S(1)}, bf16[2,24,14336]{2,1,0:T(8,128)(2,1)S(1)}, u32[]{:S(2)}, u32[]{:S(2)}) collective-permute-start(bf16[2,24,14336]{2,1,0:T(8,128)(2,1)S(1)} %get-tuple-element.55), channel_id=1, source_target_pairs={{0,1},{1,0},{2,3},{3,2},{4,5},{5,4},{6,7},{7,6},{8,9},{9,8},{10,11... | collective-permute-start | bytes 4128776 | tf_op jit(solution)/shard_map/ppermute | solution.py:13
  81.7 26.9 %collective-permute-start.3 = (bf16[24,14336]{1,0:T(8,128)(2,1)S(1)}, bf16[24,14336]{1,0:T(8,128)(2,1)S(1)}, u32[]{:S(2)}, u32[]{:S(2)}) collective-permute-start(bf16[24,14336]{1,0:T(8,128)(2,1)S(1)} %collective-permute-done.2), channel_id=1, source_target_pairs={{0,2},{2,0},{1,3},{3,1},{4,6},{6,4},{5,7},{7,5},{8,10},{10,8},{9,1... | collective-permute-start | bytes 2064392 | tf_op jit(solution)/shard_map/ppermute | solution.py:13
  97.1 18.6 %collective-permute-start.6 = (bf16[24,14336]{1,0:T(8,128)(2,1)}, bf16[24,14336]{1,0:T(8,128)(2,1)S(1)}, u32[]{:S(2)}, u32[]{:S(2)}) collective-permute-start(bf16[24,14336]{1,0:T(8,128)(2,1)} %collective-permute-done.5), channel_id=1, source_target_pairs={{0,2},{2,0},{1,3},{3,1},{4,6},{6,4},{5,7},{7,5},{8,10},{10,8},{9,1... | collective-permute-start | bytes 2064392 | tf_op jit(solution)/shard_map/ppermute | solution.py:13
  98.6 29.6 %collective-permute-start.9 = (bf16[24,14336]{1,0:T(8,128)(2,1)}, bf16[24,14336]{1,0:T(8,128)(2,1)}, u32[]{:S(2)}, u32[]{:S(2)}) collective-permute-start(bf16[24,14336]{1,0:T(8,128)(2,1)} %collective-permute-done.8), channel_id=1, source_target_pairs={{0,2},{2,0},{1,3},{3,1},{4,6},{6,4},{5,7},{7,5},{8,10},{10,8},{9,1... | collective-permute-start | bytes 2064392 | tf_op jit(solution)/shard_map/ppermute | solution.py:13
  100.3 2.0 copy-start
  102.4 2.0 copy-start.1
  104.4 2.0 copy-start.3
  108.4 24.7 %collective-permute-start.22 = (bf16[2,4,24,7168]{3,2,1,0:T(8,128)(2,1)S(1)}, bf16[2,4,24,7168]{3,2,1,0:T(8,128)(2,1)S(1)}, u32[]{:S(2)}, u32[]{:S(2)}) collective-permute-start(bf16[2,4,24,7168]{3,2,1,0:T(8,128)(2,1)S(1)} %bitcast.194), channel_id=1, source_target_pairs={{0,1},{1,0},{2,3},{3,2},{4,5},{5,4},{6,7},{7,6},{8,9},{9,8},{10,11... | collective-permute-start | bytes 8257544 | tf_op jit(solution)/shard_map/ppermute | solution.py:13
  108.7 21.3 %collective-permute-start.4 = (bf16[2,24,14336]{2,1,0:T(8,128)(2,1)S(1)}, bf16[2,24,14336]{2,1,0:T(8,128)(2,1)S(1)}, u32[]{:S(2)}, u32[]{:S(2)}) collective-permute-start(bf16[2,24,14336]{2,1,0:T(8,128)(2,1)S(1)} %get-tuple-element.57), channel_id=1, source_target_pairs={{0,1},{1,0},{2,3},{3,2},{4,5},{5,4},{6,7},{7,6},{8,9},{9,8},{10,11... | collective-permute-start | bytes 4128776 | tf_op jit(solution)/shard_map/ppermute | solution.py:13
  117.0 13.3 %collective-permute-start.7 = (bf16[2,24,14336]{2,1,0:T(8,128)(2,1)S(1)}, bf16[2,24,14336]{2,1,0:T(8,128)(2,1)S(1)}, u32[]{:S(2)}, u32[]{:S(2)}) collective-permute-start(bf16[2,24,14336]{2,1,0:T(8,128)(2,1)S(1)} %get-tuple-element.59), channel_id=1, source_target_pairs={{0,1},{1,0},{2,3},{3,2},{4,5},{5,4},{6,7},{7,6},{8,9},{9,8},{10,11... | collective-permute-start | bytes 4128776 | tf_op jit(solution)/shard_map/ppermute | solution.py:13
  129.7 3.2 %collective-permute-start.10 = (bf16[2,24,14336]{2,1,0:T(8,128)(2,1)S(1)}, bf16[2,24,14336]{2,1,0:T(8,128)(2,1)S(1)}, u32[]{:S(2)}, u32[]{:S(2)}) collective-permute-start(bf16[2,24,14336]{2,1,0:T(8,128)(2,1)S(1)} %get-tuple-element.61), channel_id=1, source_target_pairs={{0,1},{1,0},{2,3},{3,2},{4,5},{5,4},{6,7},{7,6},{8,9},{9,8},{10,11... | collective-permute-start | bytes 4128776 | tf_op jit(solution)/shard_map/ppermute | solution.py:13
  133.1 1.5 copy-start.5
  137.6 11.0 %collective-permute-start.23 = (bf16[24,7168]{1,0:T(8,128)(2,1)S(1)}, bf16[24,7168]{1,0:T(8,128)(2,1)S(1)}, u32[]{:S(2)}, u32[]{:S(2)}) collective-permute-start(bf16[24,7168]{1,0:T(8,128)(2,1)S(1)} %get-tuple-element.39), channel_id=1, source_target_pairs={{0,2},{2,0},{1,3},{3,1},{4,6},{6,4},{5,7},{7,5},{8,10},{10,8},{9,1... | collective-permute-start | bytes 1032200 | tf_op jit(solution)/shard_map/ppermute | solution.py:13
  139.1 16.8 %collective-permute-start.24 = (bf16[24,7168]{1,0:T(8,128)(2,1)S(1)}, bf16[24,7168]{1,0:T(8,128)(2,1)S(1)}, u32[]{:S(2)}, u32[]{:S(2)}) collective-permute-start(bf16[24,7168]{1,0:T(8,128)(2,1)S(1)} %get-tuple-element.38), channel_id=1, source_target_pairs={{0,2},{2,0},{1,3},{3,1},{4,6},{6,4},{5,7},{7,5},{8,10},{10,8},{9,1... | collective-permute-start | bytes 1032200 | tf_op jit(solution)/shard_map/ppermute | solution.py:13
  139.7 23.6 %collective-permute-start.25 = (bf16[24,7168]{1,0:T(8,128)(2,1)S(1)}, bf16[24,7168]{1,0:T(8,128)(2,1)S(1)}, u32[]{:S(2)}, u32[]{:S(2)}) collective-permute-start(bf16[24,7168]{1,0:T(8,128)(2,1)S(1)} %get-tuple-element.37), channel_id=1, source_target_pairs={{0,2},{2,0},{1,3},{3,1},{4,6},{6,4},{5,7},{7,5},{8,10},{10,8},{9,1... | collective-permute-start | bytes 1032200 | tf_op jit(solution)/shard_map/ppermute | solution.py:13
  141.2 28.7 %collective-permute-start.26 = (bf16[24,7168]{1,0:T(8,128)(2,1)S(1)}, bf16[24,7168]{1,0:T(8,128)(2,1)S(1)}, u32[]{:S(2)}, u32[]{:S(2)}) collective-permute-start(bf16[24,7168]{1,0:T(8,128)(2,1)S(1)} %get-tuple-element.36), channel_id=1, source_target_pairs={{0,2},{2,0},{1,3},{3,1},{4,6},{6,4},{5,7},{7,5},{8,10},{10,8},{9,1... | collective-permute-start | bytes 1032200 | tf_op jit(solution)/shard_map/ppermute | solution.py:13
  170.9 2.0 copy-start.4
  174.7 2.3 copy-start.2
  185.2 1.0 copy-start.11
  185.2 2.2 copy-start.10
  185.2 2.9 copy-start.9
  185.6 34.1 %collective-permute-start.27 = (bf16[2,1,4,24,7168]{4,3,2,0,1:T(8,128)(2,1)S(1)}, bf16[2,1,4,24,7168]{4,3,2,0,1:T(8,128)(2,1)S(1)}, u32[]{:S(2)}, u32[]{:S(2)}) collective-permute-start(bf16[2,1,4,24,7168]{4,3,2,0,1:T(8,128)(2,1)S(1)} %bitcast.195), channel_id=1, source_target_pairs={{0,1},{1,0},{2,3},{3,2},{4,5},{5,4},{6,7},{7,6},{8,9},{9,8},{10,11... | collective-permute-start | bytes 8257544 | tf_op jit(solution)/shard_map/ppermute | solution.py:13
  186.2 14.9 %collective-permute-start.29 = (bf16[24,7168]{1,0:T(8,128)(2,1)S(1)}, bf16[24,7168]{1,0:T(8,128)(2,1)S(1)}, u32[]{:S(2)}, u32[]{:S(2)}) collective-permute-start(bf16[24,7168]{1,0:T(8,128)(2,1)S(1)} %copy-done.11), channel_id=1, source_target_pairs={{0,4},{4,0},{8,12},{12,8},{1,5},{5,1},{9,13},{13,9},{2,6},{6,2},{1... | collective-permute-start | bytes 1032200 | tf_op jit(solution)/shard_map/ppermute | solution.py:97
  187.4 23.9 %collective-permute-start.30 = (bf16[24,7168]{1,0:T(8,128)(2,1)S(1)}, bf16[24,7168]{1,0:T(8,128)(2,1)S(1)}, u32[]{:S(2)}, u32[]{:S(2)}) collective-permute-start(bf16[24,7168]{1,0:T(8,128)(2,1)S(1)} %copy-done.10), channel_id=1, source_target_pairs={{0,8},{4,12},{8,0},{12,4},{1,9},{5,13},{9,1},{13,5},{2,10},{6,14},... | collective-permute-start | bytes 1032200 | tf_op jit(solution)/shard_map/ppermute | solution.py:97
  188.1 31.4 %collective-permute-start.31 = (bf16[24,7168]{1,0:T(8,128)(2,1)S(1)}, bf16[24,7168]{1,0:T(8,128)(2,1)S(1)}, u32[]{:S(2)}, u32[]{:S(2)}) collective-permute-start(bf16[24,7168]{1,0:T(8,128)(2,1)S(1)} %copy-done.9), channel_id=1, source_target_pairs={{0,12},{4,8},{8,4},{12,0},{1,13},{5,9},{9,5},{13,1},{2,14},{6,10},... | collective-permute-start | bytes 1032200 | tf_op jit(solution)/shard_map/ppermute | solution.py:97
  220.7 31.0 %collective-permute-start.28 = (bf16[4,24,7168]{2,1,0:T(8,128)(2,1)S(1)}, bf16[4,24,7168]{2,1,0:T(8,128)(2,1)S(1)}, u32[]{:S(2)}, u32[]{:S(2)}) collective-permute-start(bf16[4,24,7168]{2,1,0:T(8,128)(2,1)S(1)} %fusion.23), channel_id=1, source_target_pairs={{0,2},{2,0},{1,3},{3,1},{4,6},{6,4},{5,7},{7,5},{8,10},{10,8},{9,1... | collective-permute-start | bytes 4128776 | tf_op jit(solution)/shard_map/ppermute | solution.py:13
  252.0 3.7 %copy-start.6 = (bf16[1,32,7168]{2,1,0:T(8,128)(2,1)S(1)}, bf16[1,32,7168]{2,1,0:T(8,128)(2,1)}, u32[]{:S(2)}) copy-start(bf16[1,32,7168]{2,1,0:T(8,128)(2,1)} %param.10) | copy-start | bytes 1376260
  252.1 11.1 %collective-permute-start.33 = (bf16[24,7168]{1,0:T(8,128)(2,1)S(1)}, bf16[24,7168]{1,0:T(8,128)(2,1)S(1)}, u32[]{:S(2)}, u32[]{:S(2)}) collective-permute-start(bf16[24,7168]{1,0:T(8,128)(2,1)S(1)} %get-tuple-element.19), channel_id=1, source_target_pairs={{0,4},{4,0},{8,12},{12,8},{1,5},{5,1},{9,13},{13,9},{2,6},{6,2},{1... | collective-permute-start | bytes 1032200 | tf_op jit(solution)/shard_map/ppermute | solution.py:97
  252.2 25.2 %collective-permute-start.34 = (bf16[24,7168]{1,0:T(8,128)(2,1)S(1)}, bf16[24,7168]{1,0:T(8,128)(2,1)S(1)}, u32[]{:S(2)}, u32[]{:S(2)}) collective-permute-start(bf16[24,7168]{1,0:T(8,128)(2,1)S(1)} %get-tuple-element.20), channel_id=1, source_target_pairs={{0,8},{4,12},{8,0},{12,4},{1,9},{5,13},{9,1},{13,5},{2,10},{6,14},... | collective-permute-start | bytes 1032200 | tf_op jit(solution)/shard_map/ppermute | solution.py:97
  254.1 29.3 %collective-permute-start.35 = (bf16[24,7168]{1,0:T(8,128)(2,1)S(1)}, bf16[24,7168]{1,0:T(8,128)(2,1)S(1)}, u32[]{:S(2)}, u32[]{:S(2)}) collective-permute-start(bf16[24,7168]{1,0:T(8,128)(2,1)S(1)} %get-tuple-element.21), channel_id=1, source_target_pairs={{0,12},{4,8},{8,4},{12,0},{1,13},{5,9},{9,5},{13,1},{2,14},{6,10},... | collective-permute-start | bytes 1032200 | tf_op jit(solution)/shard_map/ppermute | solution.py:97
  256.3 29.6 %collective-permute-start.32 = (bf16[1,32,7168]{2,1,0:T(8,128)(2,1)S(1)}, bf16[1,32,7168]{2,1,0:T(8,128)(2,1)S(1)}, u32[]{:S(2)}, u32[]{:S(2)}) collective-permute-start(bf16[1,32,7168]{2,1,0:T(8,128)(2,1)S(1)} %fusion.3), channel_id=1, source_target_pairs={{0,16},{16,0},{1,17},{17,1},{2,18},{18,2},{3,19},{19,3},{4,20},{20... | collective-permute-start | bytes 1376264 | tf_op jit(solution)/shard_map/ppermute | solution.py:19
  284.3 9.4 %collective-permute-start.36 = (bf16[1,32,7168]{2,1,0:T(8,128)(2,1)S(1)}, bf16[1,32,7168]{2,1,0:T(8,128)(2,1)S(1)}, u32[]{:S(2)}, u32[]{:S(2)}) collective-permute-start(bf16[1,32,7168]{2,1,0:T(8,128)(2,1)S(1)} %fusion.2), channel_id=1, source_target_pairs={{0,16},{16,0},{1,17},{17,1},{2,18},{18,2},{3,19},{19,3},{4,20},{20... | collective-permute-start | bytes 1376264 | tf_op jit(solution)/shard_map/ppermute | solution.py:19
